TPU v7x, 32 devices: a whole 2x2x4 slice. The times are simulated.
32 devices in a mesh: group: 2 (over x), mp: 16 (over z, y, core).
Axes of the slice: x: 2, y: 2, z: 4, core: 2. Of those that a mesh axis runs over, the one named last changes fastest.
Arguments:
- velocity: float32 [256, 32, 128], P(('group', 'mp')), parts along dimension 0, may hold values from 0.2 to 0.4
- buoyancy: float32 [256, 32, 128], P(('group', 'mp')), parts along dimension 0, may hold values from 0.6 to 1.5
- wave_prev: float32 [2, 128, 32, 128], P('group', 'mp'), parts along dimension 0, may hold values from -6 to 6
- wave_now: float32 [2, 128, 32, 128], P('group', 'mp'), parts along dimension 0, may hold values from -6 to 6
- adjoint_next: float32 [2, 128, 32, 128], P('group', 'mp'), parts along dimension 0, may hold values from -6 to 6
- adjoint_after: float32 [2, 128, 32, 128], P('group', 'mp'), parts along dimension 0, may hold values from -6 to 6
- source_cell: int32 [2], P('group'), parts along dimension 0, may hold values from 0 to 524287
- wavelet: float32 [2, 4], P('group'), parts along dimension 0, may hold values from -16 to 16
- receiver_cell: int32 [2, 2048], P('group'), parts along dimension 0, may hold values from 0 to 524287
- observed: float32 [2, 4, 2048], P('group'), parts along dimension 0, may hold values from -6 to 6
Outputs:
- velocity_gradient: float32 [256, 32, 128], P(('group', 'mp')), parts along dimension 0
- adjoint_first: float32 [2, 128, 32, 128], P('group', 'mp'), parts along dimension 0
- adjoint_second: float32 [2, 128, 32, 128], P('group', 'mp'), parts along dimension 0
- misfit: float32 [2], P('group'), parts along dimension 0
There are 2 independent parts, one for each index of `group`. A program takes and returns all parts, laid end to end along the dimension named above; each array names one. Nothing has to cross between parts.
Inputs may be any that keep to these rules, and one draw needn't show every extreme that they name: source_cell is a flat grid index x * 32 * 128 + y * 128 + z. receiver_cell holds flat grid indices like source_cell; cells may repeat.
All inputs are finite; a program needn't handle non-finite values.
Results may differ from a plain program's by a relative error of at most 0.00002.
Values sent between devices are 32-bit elements; how exact they have to be, the bound alone decides.
No kernel may reach another device: no remote copies, remote signals or barrier semaphores. Data moves between devices by JAX's collectives and lax.ppermute only.
A program may use at most 64 MiB of HBM per device.

v0:
```python
import jax
import jax.numpy as jnp
from jax import lax
from jax.sharding import PartitionSpec as P

STEPS = 4


COEFFS = (1225.0 / 1024.0, -245.0 / 3072.0, 49.0 / 5120.0, -5.0 / 7168.0)


def extended(array, sides, width):
    for axis, dim in sides:
        devices, length = (lax.axis_size(axis), array.shape[dim])
        up = [(i, (i + 1) % devices) for i in range(devices - 1)]
        down = [(j, i) for i, j in up]
        last = lax.slice_in_dim(array, length - width, length, axis=dim)
        first = lax.slice_in_dim(array, 0, width, axis=dim)
        before = lax.ppermute(last, axis, up)
        after = lax.ppermute(first, axis, down)
        array = jnp.concatenate([before, array, after], axis=dim)
    return array


def pad_axis(values, axis):
    widths = [(0, 0)] * values.ndim
    widths[axis] = (4, 4)
    return jnp.pad(values, widths)


def forward_diff(padded, axis, length):
    total = jnp.zeros((), jnp.float32)
    for order in range(4):
        shift = order + 1
        upper = lax.slice_in_dim(padded, 4 + shift, 4 + shift + length, axis=axis)
        lower = lax.slice_in_dim(padded, 5 - shift, 5 - shift + length, axis=axis)
        total = total + COEFFS[order] * (upper - lower)
    return total


def backward_diff(padded, axis, length):
    total = jnp.zeros((), jnp.float32)
    for order in range(4):
        shift = order + 1
        upper = lax.slice_in_dim(padded, 3 + shift, 3 + shift + length, axis=axis)
        lower = lax.slice_in_dim(padded, 4 - shift, 4 - shift + length, axis=axis)
        total = total + COEFFS[order] * (upper - lower)
    return total


def cross_terms(values, buoyancy):
    total = jnp.zeros_like(values)
    for axis in (2, 3):
        length = values.shape[axis]
        flux = buoyancy * forward_diff(pad_axis(values, axis), axis, length)
        total = total + backward_diff(pad_axis(flux, axis), axis, length)
    return total


def local(
    velocity,
    buoyancy,
    wave_prev,
    wave_now,
    adjoint_next,
    adjoint_after,
    source_cell,
    wavelet,
    receiver_cell,
    observed,
):
    planes = velocity.shape[0]
    shots = wave_now.shape[0]
    shape = wave_now.shape
    cells = planes * velocity.shape[1] * velocity.shape[2]
    kappa = velocity * velocity / buoyancy
    offset = lax.axis_index("mp") * cells

    def operator(values):
        wide = extended(values, (("mp", 1),), 4)
        flux = buoyancy * forward_diff(wide, 1, planes)
        flux_wide = extended(flux, (("mp", 1),), 4)
        return backward_diff(flux_wide, 1, planes) + cross_terms(values, buoyancy)

    shot_rows = jnp.arange(shots)
    source_local = source_cell - offset
    source_owned = (source_local >= 0) & (source_local < cells)
    source_index = jnp.clip(source_local, 0, cells - 1)
    receiver_local = receiver_cell - offset
    receiver_owned = (receiver_local >= 0) & (receiver_local < cells)
    receiver_index = jnp.clip(receiver_local, 0, cells - 1)
    before, current = (wave_prev, wave_now)
    laps = []
    resids = []
    for step in range(STEPS):
        lap = operator(current)
        laps.append(lap)
        following = 2.0 * current - before + kappa * lap
        amount = jnp.where(source_owned, wavelet[:, step], 0.0)
        flat = following.reshape(shots, cells).at[shot_rows, source_index].add(amount)
        sampled = flat[shot_rows[:, None], receiver_index]
        resids.append(jnp.where(receiver_owned, sampled - observed[:, step, :], 0.0))
        before, current = (current, flat.reshape(shape))
    local_misfit = 0.5 * sum((jnp.sum(item * item, axis=1) for item in resids))
    misfit = lax.psum(local_misfit, "mp")
    mu_near, mu_far = (adjoint_next, adjoint_after)
    gradient = jnp.zeros(shape, jnp.float32)
    for level in range(STEPS, 0, -1):
        state = 2.0 * mu_near + operator(kappa * mu_near) - mu_far
        state = (
            state.reshape(shots, cells)
            .at[shot_rows[:, None], receiver_index]
            .add(resids[level - 1])
            .reshape(shape)
        )
        gradient = gradient + state * laps[level - 1]
        mu_far, mu_near = (mu_near, state)
    velocity_gradient = 2.0 * velocity / buoyancy * jnp.sum(gradient, axis=0)
    return (velocity_gradient, mu_near, mu_far, misfit)


def solution(mesh):
    placed = (
        P(("group", "mp"), None, None),
        P(("group", "mp"), None, None),
        P("group", "mp", None, None),
        P("group", "mp", None, None),
        P("group", "mp", None, None),
        P("group", "mp", None, None),
        P("group"),
        P("group", None),
        P("group", None),
        P("group", None, None),
    )
    return jax.shard_map(
        local,
        mesh=mesh,
        in_specs=placed,
        out_specs=(
            P(("group", "mp"), None, None),
            P("group", "mp", None, None),
            P("group", "mp", None, None),
            P("group"),
        ),
        check_vma=False,
    )
```

profile of v0, /device:TPU:1, one launch (start us, length us, event | category | flops | bytes accessed | tf_op | source)
XLA Modules:
  0.0 287.2 jit_solution(2906392293569151690)
XLA Ops:
  0.6 0.9 fusion.683
  1.5 4.7 %collective-permute-start.5 = (f32[1,4,32,128]{3,2,1,0:T(8,128)S(1)}, f32[1,4,32,128]{3,2,1,0:T(8,128)S(1)}, u32[]{:S(2)}, u32[]{:S(2)}) collective-permute-start(f32[1,4,32,128]{3,2,1,0:T(8,128)S(1)} %get-tuple-element.125), channel_id=1, source_target_pairs={{0,1},{1,2},{2,3},{3,4},{4,5},{5,6},{6,7},{7,8},{8,9},{9,10},{10,1... | collective-permute-start | bytes 196616 | tf_op jit(solution)/shard_map/ppermute | solution.py:19
  6.2 1.9 collective-permute-start.4
  8.9 2.9 %collective-permute-done.4 = f32[1,4,32,128]{3,2,1,0:T(8,128)S(1)} collective-permute-done((f32[1,4,32,128]{3,2,1,0:T(8,128)S(1)}, f32[1,4,32,128]{3,2,1,0:T(8,128)S(1)}, u32[]{:S(2)}, u32[]{:S(2)}) %collective-permute-start.4) | collective-permute-done | bytes 65568 | tf_op jit(solution)/shard_map/ppermute | solution.py:20
  12.2 2.1 collective-permute-start.7
  14.2 3.6 %collective-permute-start.6 = (f32[1,4,32,128]{3,2,1,0:T(8,128)S(1)}, f32[1,4,32,128]{3,2,1,0:T(8,128)S(1)}, u32[]{:S(2)}, u32[]{:S(2)}) collective-permute-start(f32[1,4,32,128]{3,2,1,0:T(8,128)S(1)} %get-tuple-element.123), channel_id=1, source_target_pairs={{0,1},{1,2},{2,3},{3,4},{4,5},{5,6},{6,7},{7,8},{8,9},{9,10},{10,1... | collective-permute-start | bytes 196616 | tf_op jit(solution)/shard_map/ppermute | solution.py:19
  17.9 0.7 fusion.684
  19.2 0.7 and_reduce_fusion.1
  20.2 0.6 fusion.685
  22.8 1.9 collective-permute-start.8
  24.8 4.2 %collective-permute-start.9 = (f32[1,4,32,128]{3,2,1,0:T(8,128)S(1)}, f32[1,4,32,128]{3,2,1,0:T(8,128)S(1)}, u32[]{:S(2)}, u32[]{:S(2)}) collective-permute-start(f32[1,4,32,128]{3,2,1,0:T(8,128)S(1)} %get-tuple-element.117), channel_id=1, source_target_pairs={{0,1},{1,2},{2,3},{3,4},{4,5},{5,6},{6,7},{7,8},{8,9},{9,10},{10,1... | collective-permute-start | bytes 196616 | tf_op jit(solution)/shard_map/ppermute | solution.py:19
  29.0 1.9 collective-permute-done.9
  31.2 1.9 collective-permute-start.11
  33.1 4.4 %collective-permute-start.10 = (f32[1,4,32,128]{3,2,1,0:T(8,128)S(1)}, f32[1,4,32,128]{3,2,1,0:T(8,128)S(1)}, u32[]{:S(2)}, u32[]{:S(2)}) collective-permute-start(f32[1,4,32,128]{3,2,1,0:T(8,128)S(1)} %get-tuple-element.115), channel_id=1, source_target_pairs={{0,1},{1,2},{2,3},{3,4},{4,5},{5,6},{6,7},{7,8},{8,9},{9,10},{10,1... | collective-permute-start | bytes 196616 | tf_op jit(solution)/shard_map/ppermute | solution.py:19
  38.0 0.8 collective-permute-done.10
  39.1 0.6 fusion.686
  41.6 1.9 collective-permute-start.12
  43.5 5.0 %collective-permute-start.13 = (f32[1,4,32,128]{3,2,1,0:T(8,128)S(1)}, f32[1,4,32,128]{3,2,1,0:T(8,128)S(1)}, u32[]{:S(2)}, u32[]{:S(2)}) collective-permute-start(f32[1,4,32,128]{3,2,1,0:T(8,128)S(1)} %get-tuple-element.113), channel_id=1, source_target_pairs={{0,1},{1,2},{2,3},{3,4},{4,5},{5,6},{6,7},{7,8},{8,9},{9,10},{10,1... | collective-permute-start | bytes 196616 | tf_op jit(solution)/shard_map/ppermute | solution.py:19
  48.5 1.3 collective-permute-done.13
  50.1 1.9 collective-permute-start.15
  52.1 4.3 %collective-permute-start.14 = (f32[1,4,32,128]{3,2,1,0:T(8,128)S(1)}, f32[1,4,32,128]{3,2,1,0:T(8,128)S(1)}, u32[]{:S(2)}, u32[]{:S(2)}) collective-permute-start(f32[1,4,32,128]{3,2,1,0:T(8,128)S(1)} %get-tuple-element.111), channel_id=1, source_target_pairs={{0,1},{1,2},{2,3},{3,4},{4,5},{5,6},{6,7},{7,8},{8,9},{9,10},{10,1... | collective-permute-start | bytes 196616 | tf_op jit(solution)/shard_map/ppermute | solution.py:19
  57.1 0.5 collective-permute-done.14
  58.0 0.7 fusion.687
  60.7 1.9 collective-permute-start.16
  62.6 4.3 %collective-permute-start.17 = (f32[1,4,32,128]{3,2,1,0:T(8,128)S(1)}, f32[1,4,32,128]{3,2,1,0:T(8,128)S(1)}, u32[]{:S(2)}, u32[]{:S(2)}) collective-permute-start(f32[1,4,32,128]{3,2,1,0:T(8,128)S(1)} %get-tuple-element.109), channel_id=1, source_target_pairs={{0,1},{1,2},{2,3},{3,4},{4,5},{5,6},{6,7},{7,8},{8,9},{9,10},{10,1... | collective-permute-start | bytes 196616 | tf_op jit(solution)/shard_map/ppermute | solution.py:19
  67.0 1.3 collective-permute-done.17
  68.6 2.1 collective-permute-start.19
  70.6 4.3 %collective-permute-start.18 = (f32[1,4,32,128]{3,2,1,0:T(8,128)S(1)}, f32[1,4,32,128]{3,2,1,0:T(8,128)S(1)}, u32[]{:S(2)}, u32[]{:S(2)}) collective-permute-start(f32[1,4,32,128]{3,2,1,0:T(8,128)S(1)} %get-tuple-element.107), channel_id=1, source_target_pairs={{0,1},{1,2},{2,3},{3,4},{4,5},{5,6},{6,7},{7,8},{8,9},{9,10},{10,1... | collective-permute-start | bytes 196616 | tf_op jit(solution)/shard_map/ppermute | solution.py:19
  75.0 1.2 collective-permute-done.18
  76.2 0.3 fusion.650
  76.6 1.9 collective-permute-start
  78.5 5.1 %collective-permute-start.1 = (f32[1,4,32,128]{3,2,1,0:T(8,128)S(1)}, f32[1,4,32,128]{3,2,1,0:T(8,128)S(1)}, u32[]{:S(2)}, u32[]{:S(2)}) collective-permute-start(f32[1,4,32,128]{3,2,1,0:T(8,128)S(1)} %get-tuple-element.121), channel_id=1, source_target_pairs={{0,1},{1,2},{2,3},{3,4},{4,5},{5,6},{6,7},{7,8},{8,9},{9,10},{10,1... | collective-permute-start | bytes 196616 | tf_op jit(solution)/shard_map/ppermute | solution.py:19
  84.3 12.4 %gather_fusion.3 = f32[2048]{0:T(1024)S(1)} fusion(f32[1,32768]{1,0:T(1,128)S(1)} %scatter-add.48, s32[2048]{0:T(1024)S(1)} %bitcast.110), kind=kCustom, calls=%fused_computation.3 | custom fusion | bytes 32768 | tf_op jit(solution)/shard_map/gather | solution.py:101
  96.7 12.4 %gather_fusion.2 = f32[2048]{0:T(1024)S(1)} fusion(f32[1,32768]{1,0:T(1,128)S(1)} %scatter-add.49, s32[2048]{0:T(1024)S(1)} %bitcast.111), kind=kCustom, calls=%fused_computation.2 | custom fusion | bytes 32768 | tf_op jit(solution)/shard_map/gather | solution.py:101
  109.1 12.4 %gather_fusion.1 = f32[2048]{0:T(1024)S(1)} fusion(f32[1,32768]{1,0:T(1,128)S(1)} %scatter-add.50, s32[2048]{0:T(1024)S(1)} %bitcast.112), kind=kCustom, calls=%fused_computation.1 | custom fusion | bytes 32768 | tf_op jit(solution)/shard_map/gather | solution.py:101
  121.5 0.7 fusion.688
  124.2 12.4 %gather_fusion = f32[2048]{0:T(1024)S(1)} fusion(f32[1,32768]{1,0:T(1,128)S(1)} %scatter-add.51, s32[2048]{0:T(1024)S(1)} %bitcast.113), kind=kCustom, calls=%fused_computation | custom fusion | bytes 32768 | tf_op jit(solution)/shard_map/gather | solution.py:101
  137.0 5.7 %collective-permute-start.2 = (f32[1,4,32,128]{3,2,1,0:T(8,128)S(1)}, f32[1,4,32,128]{3,2,1,0:T(8,128)S(1)}, u32[]{:S(2)}, u32[]{:S(2)}) collective-permute-start(f32[1,4,32,128]{3,2,1,0:T(8,128)S(1)} %get-tuple-element.118), channel_id=1, source_target_pairs={{0,1},{1,2},{2,3},{3,4},{4,5},{5,6},{6,7},{7,8},{8,9},{9,10},{10,1... | collective-permute-start | bytes 196616 | tf_op jit(solution)/shard_map/ppermute | solution.py:19
  142.7 1.9 collective-permute-start.3
  144.6 0.7 multiply_reduce_fusion.3
  145.4 4.4 %collective-permute-done.3 = f32[1,4,32,128]{3,2,1,0:T(8,128)S(1)} collective-permute-done((f32[1,4,32,128]{3,2,1,0:T(8,128)S(1)}, f32[1,4,32,128]{3,2,1,0:T(8,128)S(1)}, u32[]{:S(2)}, u32[]{:S(2)}) %collective-permute-start.3) | collective-permute-done | bytes 65568 | tf_op jit(solution)/shard_map/ppermute | solution.py:20
  150.1 13.3 %scatter_fusion = f32[32768]{0:T(1024)S(1)} fusion(f32[32768]{0:T(1024)S(1)} %bitcast.126, s32[2048]{0:T(1024)S(1)} %broadcast_select_fusion, f32[2048]{0:T(1024)S(1)} %bitcast.154), kind=kCustom, calls=%fused_computation.4 | custom fusion | flops 2048 | bytes 32768
  163.5 1.9 collective-permute-start.20
  165.5 3.6 %collective-permute-start.21 = (f32[1,4,32,128]{3,2,1,0:T(8,128)S(1)}, f32[1,4,32,128]{3,2,1,0:T(8,128)S(1)}, u32[]{:S(2)}, u32[]{:S(2)}) collective-permute-start(f32[1,4,32,128]{3,2,1,0:T(8,128)S(1)} %get-tuple-element.104), channel_id=1, source_target_pairs={{0,1},{1,2},{2,3},{3,4},{4,5},{5,6},{6,7},{7,8},{8,9},{9,10},{10,1... | collective-permute-start | bytes 196616 | tf_op jit(solution)/shard_map/ppermute | solution.py:19
  169.1 1.3 collective-permute-done.21
  170.7 4.4 %collective-permute-start.22 = (f32[1,4,32,128]{3,2,1,0:T(8,128)S(1)}, f32[1,4,32,128]{3,2,1,0:T(8,128)S(1)}, u32[]{:S(2)}, u32[]{:S(2)}) collective-permute-start(f32[1,4,32,128]{3,2,1,0:T(8,128)S(1)} %get-tuple-element.101), channel_id=1, source_target_pairs={{0,1},{1,2},{2,3},{3,4},{4,5},{5,6},{6,7},{7,8},{8,9},{9,10},{10,1... | collective-permute-start | bytes 196616 | tf_op jit(solution)/shard_map/ppermute | solution.py:19
  175.1 1.9 collective-permute-start.23
  177.1 3.6 %collective-permute-done.23 = f32[1,4,32,128]{3,2,1,0:T(8,128)S(1)} collective-permute-done((f32[1,4,32,128]{3,2,1,0:T(8,128)S(1)}, f32[1,4,32,128]{3,2,1,0:T(8,128)S(1)}, u32[]{:S(2)}, u32[]{:S(2)}) %collective-permute-start.23) | collective-permute-done | bytes 65568 | tf_op jit(solution)/shard_map/ppermute | solution.py:20
  181.0 13.3 %scatter_fusion.1 = f32[32768]{0:T(1024)S(1)} fusion(f32[32768]{0:T(1024)S(1)} %bitcast.131, s32[2048]{0:T(1024)S(1)} %broadcast_select_fusion, f32[2048]{0:T(1024)S(1)} %bitcast.153), kind=kCustom, calls=%fused_computation.5 | custom fusion | flops 2048 | bytes 32768
  194.4 1.9 collective-permute-start.24
  196.3 3.6 %collective-permute-start.25 = (f32[1,4,32,128]{3,2,1,0:T(8,128)S(1)}, f32[1,4,32,128]{3,2,1,0:T(8,128)S(1)}, u32[]{:S(2)}, u32[]{:S(2)}) collective-permute-start(f32[1,4,32,128]{3,2,1,0:T(8,128)S(1)} %get-tuple-element.100), channel_id=1, source_target_pairs={{0,1},{1,2},{2,3},{3,4},{4,5},{5,6},{6,7},{7,8},{8,9},{9,10},{10,1... | collective-permute-start | bytes 196616 | tf_op jit(solution)/shard_map/ppermute | solution.py:19
  200.0 1.3 collective-permute-done.25
  201.6 4.3 %collective-permute-start.26 = (f32[1,4,32,128]{3,2,1,0:T(8,128)S(1)}, f32[1,4,32,128]{3,2,1,0:T(8,128)S(1)}, u32[]{:S(2)}, u32[]{:S(2)}) collective-permute-start(f32[1,4,32,128]{3,2,1,0:T(8,128)S(1)} %get-tuple-element.97), channel_id=1, source_target_pairs={{0,1},{1,2},{2,3},{3,4},{4,5},{5,6},{6,7},{7,8},{8,9},{9,10},{10,1... | collective-permute-start | bytes 196616 | tf_op jit(solution)/shard_map/ppermute | solution.py:19
  205.9 1.9 collective-permute-start.27
  207.9 3.9 %collective-permute-done.27 = f32[1,4,32,128]{3,2,1,0:T(8,128)S(1)} collective-permute-done((f32[1,4,32,128]{3,2,1,0:T(8,128)S(1)}, f32[1,4,32,128]{3,2,1,0:T(8,128)S(1)}, u32[]{:S(2)}, u32[]{:S(2)}) %collective-permute-start.27) | collective-permute-done | bytes 65568 | tf_op jit(solution)/shard_map/ppermute | solution.py:20
  212.1 13.5 %scatter_fusion.2 = f32[32768]{0:T(1024)S(1)} fusion(f32[32768]{0:T(1024)S(1)} %bitcast.141, s32[2048]{0:T(1024)S(1)} %broadcast_select_fusion, f32[2048]{0:T(1024)S(1)} %bitcast.152), kind=kCustom, calls=%fused_computation.6 | custom fusion | flops 2048 | bytes 32768
  225.6 1.9 collective-permute-start.28
  227.6 3.6 %collective-permute-start.29 = (f32[1,4,32,128]{3,2,1,0:T(8,128)S(1)}, f32[1,4,32,128]{3,2,1,0:T(8,128)S(1)}, u32[]{:S(2)}, u32[]{:S(2)}) collective-permute-start(f32[1,4,32,128]{3,2,1,0:T(8,128)S(1)} %get-tuple-element.96), channel_id=1, source_target_pairs={{0,1},{1,2},{2,3},{3,4},{4,5},{5,6},{6,7},{7,8},{8,9},{9,10},{10,1... | collective-permute-start | bytes 196616 | tf_op jit(solution)/shard_map/ppermute | solution.py:19
  231.2 1.3 collective-permute-done.29
  232.9 4.5 %collective-permute-start.30 = (f32[1,4,32,128]{3,2,1,0:T(8,128)S(1)}, f32[1,4,32,128]{3,2,1,0:T(8,128)S(1)}, u32[]{:S(2)}, u32[]{:S(2)}) collective-permute-start(f32[1,4,32,128]{3,2,1,0:T(8,128)S(1)} %get-tuple-element.93), channel_id=1, source_target_pairs={{0,1},{1,2},{2,3},{3,4},{4,5},{5,6},{6,7},{7,8},{8,9},{9,10},{10,1... | collective-permute-start | bytes 196616 | tf_op jit(solution)/shard_map/ppermute | solution.py:19
  237.4 1.9 collective-permute-start.31
  241.8 30.9 %psum.7 = f32[1]{0:T(128)} all-reduce(f32[1]{0:T(128)} %bitcast.50), channel_id=1, replica_groups=mesh['group'=2,'mp'=16] {'mp'}, use_global_device_ids=true, to_apply=%region_9.10 | all-reduce | flops 1 | bytes 8 | tf_op jit(solution)/shard_map/psum | solution.py:105
  273.0 13.3 %scatter_fusion.3 = f32[32768]{0:T(1024)S(1)} fusion(f32[32768]{0:T(1024)S(1)} %bitcast.146, s32[2048]{0:T(1024)S(1)} %broadcast_select_fusion, f32[2048]{0:T(1024)S(1)} %bitcast.151), kind=kCustom, calls=%fused_computation.7 | custom fusion | flops 2048 | bytes 32768
  286.4 0.8 bitcast_multiply_fusion
  (90 shorter events, 5.8 us)
Async XLA Ops:
  1.5 7.3 %copy-start.3 = (f32[1,8,32,128]{3,2,1,0:T(8,128)S(1)}, f32[1,8,32,128]{3,2,1,0:T(8,128)}, u32[]{:S(2)}) copy-start(f32[1,8,32,128]{3,2,1,0:T(8,128)} %param.21) | copy-start | bytes 393220
  1.5 7.3 %collective-permute-start.5 = (f32[1,4,32,128]{3,2,1,0:T(8,128)S(1)}, f32[1,4,32,128]{3,2,1,0:T(8,128)S(1)}, u32[]{:S(2)}, u32[]{:S(2)}) collective-permute-start(f32[1,4,32,128]{3,2,1,0:T(8,128)S(1)} %get-tuple-element.125), channel_id=1, source_target_pairs={{0,1},{1,2},{2,3},{3,4},{4,5},{5,6},{6,7},{7,8},{8,9},{9,10},{10,1... | collective-permute-start | bytes 196616 | tf_op jit(solution)/shard_map/ppermute | solution.py:19
  6.2 5.6 %collective-permute-start.4 = (f32[1,4,32,128]{3,2,1,0:T(8,128)S(1)}, f32[1,4,32,128]{3,2,1,0:T(8,128)S(1)}, u32[]{:S(2)}, u32[]{:S(2)}) collective-permute-start(f32[1,4,32,128]{3,2,1,0:T(8,128)S(1)} %get-tuple-element.124), channel_id=1, source_target_pairs={{1,0},{2,1},{3,2},{4,3},{5,4},{6,5},{7,6},{8,7},{9,8},{10,9},{11,1... | collective-permute-start | bytes 196616 | tf_op jit(solution)/shard_map/ppermute | solution.py:20
  8.9 2.9 %copy-start.2 = (f32[8,32,128]{2,1,0:T(8,128)S(1)}, f32[8,32,128]{2,1,0:T(8,128)}, u32[]{:S(2)}) copy-start(f32[8,32,128]{2,1,0:T(8,128)} %param.19) | copy-start | bytes 393220
  12.1 7.8 %copy-start.5 = (f32[8,32,128]{2,1,0:T(8,128)S(1)}, f32[8,32,128]{2,1,0:T(8,128)}, u32[]{:S(2)}) copy-start(f32[8,32,128]{2,1,0:T(8,128)} %param.18) | copy-start | bytes 393220
  12.1 7.8 %copy-start.7 = (f32[1,8,32,128]{3,2,1,0:T(8,128)S(1)}, f32[1,8,32,128]{3,2,1,0:T(8,128)}, u32[]{:S(2)}) copy-start(f32[1,8,32,128]{3,2,1,0:T(8,128)} %param.20) | copy-start | bytes 393220
  12.2 5.7 %copy-start.10 = (f32[1,4]{1,0:T(1,128)S(1)}, f32[1,4]{1,0:T(1,128)}, u32[]{:S(2)}) copy-start(f32[1,4]{1,0:T(1,128)} %param.25) | copy-start | bytes 52
  12.2 7.7 %collective-permute-start.7 = (f32[1,4,32,128]{3,2,1,0:T(8,128)S(1)}, f32[1,4,32,128]{3,2,1,0:T(8,128)S(1)}, u32[]{:S(2)}, u32[]{:S(2)}) collective-permute-start(f32[1,4,32,128]{3,2,1,0:T(8,128)S(1)} %get-tuple-element.122), channel_id=1, source_target_pairs={{1,0},{2,1},{3,2},{4,3},{5,4},{6,5},{7,6},{8,7},{9,8},{10,9},{11,1... | collective-permute-start | bytes 196616 | tf_op jit(solution)/shard_map/ppermute | solution.py:20
  14.2 5.7 %collective-permute-start.6 = (f32[1,4,32,128]{3,2,1,0:T(8,128)S(1)}, f32[1,4,32,128]{3,2,1,0:T(8,128)S(1)}, u32[]{:S(2)}, u32[]{:S(2)}) collective-permute-start(f32[1,4,32,128]{3,2,1,0:T(8,128)S(1)} %get-tuple-element.123), channel_id=1, source_target_pairs={{0,1},{1,2},{2,3},{3,4},{4,5},{5,6},{6,7},{7,8},{8,9},{9,10},{10,1... | collective-permute-start | bytes 196616 | tf_op jit(solution)/shard_map/ppermute | solution.py:19
  22.8 6.1 %collective-permute-start.8 = (f32[1,4,32,128]{3,2,1,0:T(8,128)S(1)}, f32[1,4,32,128]{3,2,1,0:T(8,128)S(1)}, u32[]{:S(2)}, u32[]{:S(2)}) collective-permute-start(f32[1,4,32,128]{3,2,1,0:T(8,128)S(1)} %get-tuple-element.116), channel_id=1, source_target_pairs={{1,0},{2,1},{3,2},{4,3},{5,4},{6,5},{7,6},{8,7},{9,8},{10,9},{11,1... | collective-permute-start | bytes 196616 | tf_op jit(solution)/shard_map/ppermute | solution.py:20
  24.8 6.1 %collective-permute-start.9 = (f32[1,4,32,128]{3,2,1,0:T(8,128)S(1)}, f32[1,4,32,128]{3,2,1,0:T(8,128)S(1)}, u32[]{:S(2)}, u32[]{:S(2)}) collective-permute-start(f32[1,4,32,128]{3,2,1,0:T(8,128)S(1)} %get-tuple-element.117), channel_id=1, source_target_pairs={{0,1},{1,2},{2,3},{3,4},{4,5},{5,6},{6,7},{7,8},{8,9},{9,10},{10,1... | collective-permute-start | bytes 196616 | tf_op jit(solution)/shard_map/ppermute | solution.py:19
  31.2 6.9 %collective-permute-start.11 = (f32[1,4,32,128]{3,2,1,0:T(8,128)S(1)}, f32[1,4,32,128]{3,2,1,0:T(8,128)S(1)}, u32[]{:S(2)}, u32[]{:S(2)}) collective-permute-start(f32[1,4,32,128]{3,2,1,0:T(8,128)S(1)} %get-tuple-element.114), channel_id=1, source_target_pairs={{1,0},{2,1},{3,2},{4,3},{5,4},{6,5},{7,6},{8,7},{9,8},{10,9},{11,1... | collective-permute-start | bytes 196616 | tf_op jit(solution)/shard_map/ppermute | solution.py:20
  33.1 5.7 %collective-permute-start.10 = (f32[1,4,32,128]{3,2,1,0:T(8,128)S(1)}, f32[1,4,32,128]{3,2,1,0:T(8,128)S(1)}, u32[]{:S(2)}, u32[]{:S(2)}) collective-permute-start(f32[1,4,32,128]{3,2,1,0:T(8,128)S(1)} %get-tuple-element.115), channel_id=1, source_target_pairs={{0,1},{1,2},{2,3},{3,4},{4,5},{5,6},{6,7},{7,8},{8,9},{9,10},{10,1... | collective-permute-start | bytes 196616 | tf_op jit(solution)/shard_map/ppermute | solution.py:19
  41.5 6.9 %copy-start.9 = (s32[1,2048]{1,0:T(1,128)S(1)}, s32[1,2048]{1,0:T(1,128)}, u32[]{:S(2)}) copy-start(s32[1,2048]{1,0:T(1,128)} %param.26) | copy-start | bytes 24580
  41.6 6.9 %collective-permute-start.12 = (f32[1,4,32,128]{3,2,1,0:T(8,128)S(1)}, f32[1,4,32,128]{3,2,1,0:T(8,128)S(1)}, u32[]{:S(2)}, u32[]{:S(2)}) collective-permute-start(f32[1,4,32,128]{3,2,1,0:T(8,128)S(1)} %get-tuple-element.112), channel_id=1, source_target_pairs={{1,0},{2,1},{3,2},{4,3},{5,4},{6,5},{7,6},{8,7},{9,8},{10,9},{11,1... | collective-permute-start | bytes 196616 | tf_op jit(solution)/shard_map/ppermute | solution.py:20
  43.5 6.3 %collective-permute-start.13 = (f32[1,4,32,128]{3,2,1,0:T(8,128)S(1)}, f32[1,4,32,128]{3,2,1,0:T(8,128)S(1)}, u32[]{:S(2)}, u32[]{:S(2)}) collective-permute-start(f32[1,4,32,128]{3,2,1,0:T(8,128)S(1)} %get-tuple-element.113), channel_id=1, source_target_pairs={{0,1},{1,2},{2,3},{3,4},{4,5},{5,6},{6,7},{7,8},{8,9},{9,10},{10,1... | collective-permute-start | bytes 196616 | tf_op jit(solution)/shard_map/ppermute | solution.py:19
  50.1 6.2 %copy-start.11 = (s32[2]{0:T(128)S(1)}, s32[2]{0:T(128)}, u32[]{:S(2)}) copy-start(s32[2]{0:T(128)} %constant.200) | copy-start | bytes 28
  50.1 7.0 %collective-permute-start.15 = (f32[1,4,32,128]{3,2,1,0:T(8,128)S(1)}, f32[1,4,32,128]{3,2,1,0:T(8,128)S(1)}, u32[]{:S(2)}, u32[]{:S(2)}) collective-permute-start(f32[1,4,32,128]{3,2,1,0:T(8,128)S(1)} %get-tuple-element.110), channel_id=1, source_target_pairs={{1,0},{2,1},{3,2},{4,3},{5,4},{6,5},{7,6},{8,7},{9,8},{10,9},{11,1... | collective-permute-start | bytes 196616 | tf_op jit(solution)/shard_map/ppermute | solution.py:20
  52.1 5.6 %collective-permute-start.14 = (f32[1,4,32,128]{3,2,1,0:T(8,128)S(1)}, f32[1,4,32,128]{3,2,1,0:T(8,128)S(1)}, u32[]{:S(2)}, u32[]{:S(2)}) collective-permute-start(f32[1,4,32,128]{3,2,1,0:T(8,128)S(1)} %get-tuple-element.111), channel_id=1, source_target_pairs={{0,1},{1,2},{2,3},{3,4},{4,5},{5,6},{6,7},{7,8},{8,9},{9,10},{10,1... | collective-permute-start | bytes 196616 | tf_op jit(solution)/shard_map/ppermute | solution.py:19
  60.7 6.2 %collective-permute-start.16 = (f32[1,4,32,128]{3,2,1,0:T(8,128)S(1)}, f32[1,4,32,128]{3,2,1,0:T(8,128)S(1)}, u32[]{:S(2)}, u32[]{:S(2)}) collective-permute-start(f32[1,4,32,128]{3,2,1,0:T(8,128)S(1)} %get-tuple-element.108), channel_id=1, source_target_pairs={{1,0},{2,1},{3,2},{4,3},{5,4},{6,5},{7,6},{8,7},{9,8},{10,9},{11,1... | collective-permute-start | bytes 196616 | tf_op jit(solution)/shard_map/ppermute | solution.py:20
  62.6 5.6 %collective-permute-start.17 = (f32[1,4,32,128]{3,2,1,0:T(8,128)S(1)}, f32[1,4,32,128]{3,2,1,0:T(8,128)S(1)}, u32[]{:S(2)}, u32[]{:S(2)}) collective-permute-start(f32[1,4,32,128]{3,2,1,0:T(8,128)S(1)} %get-tuple-element.109), channel_id=1, source_target_pairs={{0,1},{1,2},{2,3},{3,4},{4,5},{5,6},{6,7},{7,8},{8,9},{9,10},{10,1... | collective-permute-start | bytes 196616 | tf_op jit(solution)/shard_map/ppermute | solution.py:19
  68.5 7.7 %copy-start.4 = (f32[1,8,32,128]{3,2,1,0:T(8,128)S(1)}, f32[1,8,32,128]{3,2,1,0:T(8,128)}, u32[]{:S(2)}) copy-start(f32[1,8,32,128]{3,2,1,0:T(8,128)} %param.22) | copy-start | bytes 393220
  68.6 6.3 %copy-start.12 = (s32[2]{0:T(128)S(1)}, s32[2]{0:T(128)}, u32[]{:S(2)}) copy-start(s32[2]{0:T(128)} %constant.203) | copy-start | bytes 28
  68.6 6.5 %collective-permute-start.19 = (f32[1,4,32,128]{3,2,1,0:T(8,128)S(1)}, f32[1,4,32,128]{3,2,1,0:T(8,128)S(1)}, u32[]{:S(2)}, u32[]{:S(2)}) collective-permute-start(f32[1,4,32,128]{3,2,1,0:T(8,128)S(1)} %get-tuple-element.106), channel_id=1, source_target_pairs={{1,0},{2,1},{3,2},{4,3},{5,4},{6,5},{7,6},{8,7},{9,8},{10,9},{11,1... | collective-permute-start | bytes 196616 | tf_op jit(solution)/shard_map/ppermute | solution.py:20
  70.6 5.6 %collective-permute-start.18 = (f32[1,4,32,128]{3,2,1,0:T(8,128)S(1)}, f32[1,4,32,128]{3,2,1,0:T(8,128)S(1)}, u32[]{:S(2)}, u32[]{:S(2)}) collective-permute-start(f32[1,4,32,128]{3,2,1,0:T(8,128)S(1)} %get-tuple-element.107), channel_id=1, source_target_pairs={{0,1},{1,2},{2,3},{3,4},{4,5},{5,6},{6,7},{7,8},{8,9},{9,10},{10,1... | collective-permute-start | bytes 196616 | tf_op jit(solution)/shard_map/ppermute | solution.py:19
  76.6 60.0 %collective-permute-start = (f32[1,4,32,128]{3,2,1,0:T(8,128)S(1)}, f32[1,4,32,128]{3,2,1,0:T(8,128)S(1)}, u32[]{:S(2)}, u32[]{:S(2)}) collective-permute-start(f32[1,4,32,128]{3,2,1,0:T(8,128)S(1)} %get-tuple-element.120), channel_id=1, source_target_pairs={{1,0},{2,1},{3,2},{4,3},{5,4},{6,5},{7,6},{8,7},{9,8},{10,9},{11,1... | collective-permute-start | bytes 196616 | tf_op jit(solution)/shard_map/ppermute | solution.py:20
  78.5 58.1 %collective-permute-start.1 = (f32[1,4,32,128]{3,2,1,0:T(8,128)S(1)}, f32[1,4,32,128]{3,2,1,0:T(8,128)S(1)}, u32[]{:S(2)}, u32[]{:S(2)}) collective-permute-start(f32[1,4,32,128]{3,2,1,0:T(8,128)S(1)} %get-tuple-element.121), channel_id=1, source_target_pairs={{0,1},{1,2},{2,3},{3,4},{4,5},{5,6},{6,7},{7,8},{8,9},{9,10},{10,1... | collective-permute-start | bytes 196616 | tf_op jit(solution)/shard_map/ppermute | solution.py:19
  136.6 8.0 %copy-start.8 = (f32[1,4,2048]{2,1,0:T(4,128)S(1)}, f32[1,4,2048]{2,1,0:T(4,128)}, u32[]{:S(2)}) copy-start(f32[1,4,2048]{2,1,0:T(4,128)} %param.27) | copy-start | bytes 98308
  136.9 12.9 %copy-start.6 = (f32[1,8,32,128]{3,2,1,0:T(8,128)S(1)}, f32[1,8,32,128]{3,2,1,0:T(8,128)}, u32[]{:S(2)}) copy-start(f32[1,8,32,128]{3,2,1,0:T(8,128)} %param.23) | copy-start | bytes 393220
  137.0 8.4 %collective-permute-start.2 = (f32[1,4,32,128]{3,2,1,0:T(8,128)S(1)}, f32[1,4,32,128]{3,2,1,0:T(8,128)S(1)}, u32[]{:S(2)}, u32[]{:S(2)}) collective-permute-start(f32[1,4,32,128]{3,2,1,0:T(8,128)S(1)} %get-tuple-element.118), channel_id=1, source_target_pairs={{0,1},{1,2},{2,3},{3,4},{4,5},{5,6},{6,7},{7,8},{8,9},{9,10},{10,1... | collective-permute-start | bytes 196616 | tf_op jit(solution)/shard_map/ppermute | solution.py:19
  142.7 7.1 %collective-permute-start.3 = (f32[1,4,32,128]{3,2,1,0:T(8,128)S(1)}, f32[1,4,32,128]{3,2,1,0:T(8,128)S(1)}, u32[]{:S(2)}, u32[]{:S(2)}) collective-permute-start(f32[1,4,32,128]{3,2,1,0:T(8,128)S(1)} %get-tuple-element.119), channel_id=1, source_target_pairs={{1,0},{2,1},{3,2},{4,3},{5,4},{6,5},{7,6},{8,7},{9,8},{10,9},{11,1... | collective-permute-start | bytes 196616 | tf_op jit(solution)/shard_map/ppermute | solution.py:20
  163.5 5.6 %collective-permute-start.20 = (f32[1,4,32,128]{3,2,1,0:T(8,128)S(1)}, f32[1,4,32,128]{3,2,1,0:T(8,128)S(1)}, u32[]{:S(2)}, u32[]{:S(2)}) collective-permute-start(f32[1,4,32,128]{3,2,1,0:T(8,128)S(1)} %get-tuple-element.103), channel_id=1, source_target_pairs={{1,0},{2,1},{3,2},{4,3},{5,4},{6,5},{7,6},{8,7},{9,8},{10,9},{11,1... | collective-permute-start | bytes 196616 | tf_op jit(solution)/shard_map/ppermute | solution.py:20
  165.5 5.0 %collective-permute-start.21 = (f32[1,4,32,128]{3,2,1,0:T(8,128)S(1)}, f32[1,4,32,128]{3,2,1,0:T(8,128)S(1)}, u32[]{:S(2)}, u32[]{:S(2)}) collective-permute-start(f32[1,4,32,128]{3,2,1,0:T(8,128)S(1)} %get-tuple-element.104), channel_id=1, source_target_pairs={{0,1},{1,2},{2,3},{3,4},{4,5},{5,6},{6,7},{7,8},{8,9},{9,10},{10,1... | collective-permute-start | bytes 196616 | tf_op jit(solution)/shard_map/ppermute | solution.py:19
  170.7 6.3 %collective-permute-start.22 = (f32[1,4,32,128]{3,2,1,0:T(8,128)S(1)}, f32[1,4,32,128]{3,2,1,0:T(8,128)S(1)}, u32[]{:S(2)}, u32[]{:S(2)}) collective-permute-start(f32[1,4,32,128]{3,2,1,0:T(8,128)S(1)} %get-tuple-element.101), channel_id=1, source_target_pairs={{0,1},{1,2},{2,3},{3,4},{4,5},{5,6},{6,7},{7,8},{8,9},{9,10},{10,1... | collective-permute-start | bytes 196616 | tf_op jit(solution)/shard_map/ppermute | solution.py:19
  175.1 5.6 %collective-permute-start.23 = (f32[1,4,32,128]{3,2,1,0:T(8,128)S(1)}, f32[1,4,32,128]{3,2,1,0:T(8,128)S(1)}, u32[]{:S(2)}, u32[]{:S(2)}) collective-permute-start(f32[1,4,32,128]{3,2,1,0:T(8,128)S(1)} %get-tuple-element.102), channel_id=1, source_target_pairs={{1,0},{2,1},{3,2},{4,3},{5,4},{6,5},{7,6},{8,7},{9,8},{10,9},{11,1... | collective-permute-start | bytes 196616 | tf_op jit(solution)/shard_map/ppermute | solution.py:20
  194.4 5.6 %collective-permute-start.24 = (f32[1,4,32,128]{3,2,1,0:T(8,128)S(1)}, f32[1,4,32,128]{3,2,1,0:T(8,128)S(1)}, u32[]{:S(2)}, u32[]{:S(2)}) collective-permute-start(f32[1,4,32,128]{3,2,1,0:T(8,128)S(1)} %get-tuple-element.99), channel_id=1, source_target_pairs={{1,0},{2,1},{3,2},{4,3},{5,4},{6,5},{7,6},{8,7},{9,8},{10,9},{11,1... | collective-permute-start | bytes 196616 | tf_op jit(solution)/shard_map/ppermute | solution.py:20
  196.3 5.0 %collective-permute-start.25 = (f32[1,4,32,128]{3,2,1,0:T(8,128)S(1)}, f32[1,4,32,128]{3,2,1,0:T(8,128)S(1)}, u32[]{:S(2)}, u32[]{:S(2)}) collective-permute-start(f32[1,4,32,128]{3,2,1,0:T(8,128)S(1)} %get-tuple-element.100), channel_id=1, source_target_pairs={{0,1},{1,2},{2,3},{3,4},{4,5},{5,6},{6,7},{7,8},{8,9},{9,10},{10,1... | collective-permute-start | bytes 196616 | tf_op jit(solution)/shard_map/ppermute | solution.py:19
  201.6 6.2 %collective-permute-start.26 = (f32[1,4,32,128]{3,2,1,0:T(8,128)S(1)}, f32[1,4,32,128]{3,2,1,0:T(8,128)S(1)}, u32[]{:S(2)}, u32[]{:S(2)}) collective-permute-start(f32[1,4,32,128]{3,2,1,0:T(8,128)S(1)} %get-tuple-element.97), channel_id=1, source_target_pairs={{0,1},{1,2},{2,3},{3,4},{4,5},{5,6},{6,7},{7,8},{8,9},{9,10},{10,1... | collective-permute-start | bytes 196616 | tf_op jit(solution)/shard_map/ppermute | solution.py:19
  205.9 5.8 %collective-permute-start.27 = (f32[1,4,32,128]{3,2,1,0:T(8,128)S(1)}, f32[1,4,32,128]{3,2,1,0:T(8,128)S(1)}, u32[]{:S(2)}, u32[]{:S(2)}) collective-permute-start(f32[1,4,32,128]{3,2,1,0:T(8,128)S(1)} %get-tuple-element.98), channel_id=1, source_target_pairs={{1,0},{2,1},{3,2},{4,3},{5,4},{6,5},{7,6},{8,7},{9,8},{10,9},{11,1... | collective-permute-start | bytes 196616 | tf_op jit(solution)/shard_map/ppermute | solution.py:20
  225.6 60.8 %copy-start = (f32[32768]{0:T(1024)}, f32[32768]{0:T(1024)S(1)}, u32[]{:S(2)}) copy-start(f32[32768]{0:T(1024)S(1)} %scatter_fusion.2) | copy-start | bytes 393220
  225.6 5.6 %collective-permute-start.28 = (f32[1,4,32,128]{3,2,1,0:T(8,128)S(1)}, f32[1,4,32,128]{3,2,1,0:T(8,128)S(1)}, u32[]{:S(2)}, u32[]{:S(2)}) collective-permute-start(f32[1,4,32,128]{3,2,1,0:T(8,128)S(1)} %get-tuple-element.95), channel_id=1, source_target_pairs={{1,0},{2,1},{3,2},{4,3},{5,4},{6,5},{7,6},{8,7},{9,8},{10,9},{11,1... | collective-permute-start | bytes 196616 | tf_op jit(solution)/shard_map/ppermute | solution.py:20
  227.6 5.0 %collective-permute-start.29 = (f32[1,4,32,128]{3,2,1,0:T(8,128)S(1)}, f32[1,4,32,128]{3,2,1,0:T(8,128)S(1)}, u32[]{:S(2)}, u32[]{:S(2)}) collective-permute-start(f32[1,4,32,128]{3,2,1,0:T(8,128)S(1)} %get-tuple-element.96), channel_id=1, source_target_pairs={{0,1},{1,2},{2,3},{3,4},{4,5},{5,6},{6,7},{7,8},{8,9},{9,10},{10,1... | collective-permute-start | bytes 196616 | tf_op jit(solution)/shard_map/ppermute | solution.py:19
  232.9 39.9 %collective-permute-start.30 = (f32[1,4,32,128]{3,2,1,0:T(8,128)S(1)}, f32[1,4,32,128]{3,2,1,0:T(8,128)S(1)}, u32[]{:S(2)}, u32[]{:S(2)}) collective-permute-start(f32[1,4,32,128]{3,2,1,0:T(8,128)S(1)} %get-tuple-element.93), channel_id=1, source_target_pairs={{0,1},{1,2},{2,3},{3,4},{4,5},{5,6},{6,7},{7,8},{8,9},{9,10},{10,1... | collective-permute-start | bytes 196616 | tf_op jit(solution)/shard_map/ppermute | solution.py:19
  237.4 35.4 %collective-permute-start.31 = (f32[1,4,32,128]{3,2,1,0:T(8,128)S(1)}, f32[1,4,32,128]{3,2,1,0:T(8,128)S(1)}, u32[]{:S(2)}, u32[]{:S(2)}) collective-permute-start(f32[1,4,32,128]{3,2,1,0:T(8,128)S(1)} %get-tuple-element.94), channel_id=1, source_target_pairs={{1,0},{2,1},{3,2},{4,3},{5,4},{6,5},{7,6},{8,7},{9,8},{10,9},{11,1... | collective-permute-start | bytes 196616 | tf_op jit(solution)/shard_map/ppermute | solution.py:20
  286.4 0.8 copy-start.1
where the time goes:
time: 292 us; the launch traced here: 287 us
  starting transfers between devices  101 us (35%)
  other arithmetic  63.6 us (22%)
  local copies, waits for them, and re-layouts  51.8 us (18%)
  blocking collectives  30.9 us (11%)
  waiting for transfers between devices  25.7 us (9%)
  between operations  14.6 us (5%)
    ppermute x16, starting transfers between devices, extended(): before = lax.ppermute(last, axis, up)  69.6 us
    unnamed x6, other arithmetic  53.6 us
    gather x4, local copies, waits for them, and re-layouts, local(): sampled = flat[shot_rows[:, None], receiver_index]  49.6 us
    ppermute x16, starting transfers between devices, extended(): after = lax.ppermute(first, axis, down)  31 us
    psum x1, blocking collectives, local(): misfit = lax.psum(local_misfit, 'mp')  30.9 us
    ppermute x16, waiting for transfers between devices, extended(): after = lax.ppermute(first, axis, down)  14.9 us
    ppermute x16, waiting for transfers between devices, extended(): before = lax.ppermute(last, axis, up)  10.8 us
  transfers between devices with their start and end apart: 32, of which 13 were waited for; matrix products, arithmetic and copies ran while one was open for 18% of the time, Pallas kernels for 0%

commit v1 on v0

v1 whole, which is shorter than its diff:
```python
import jax
import jax.numpy as jnp
from jax import lax
from jax.sharding import PartitionSpec as P

STEPS = 4
HALO = 7

COEFFS = (1225.0 / 1024.0, -245.0 / 3072.0, 49.0 / 5120.0, -5.0 / 7168.0)


def extended(array, dim, width):
    devices, length = (lax.axis_size("mp"), array.shape[dim])
    up = [(i, i + 1) for i in range(devices - 1)]
    down = [(j, i) for i, j in up]
    last = lax.slice_in_dim(array, length - width, length, axis=dim)
    first = lax.slice_in_dim(array, 0, width, axis=dim)
    before = lax.ppermute(last, "mp", up)
    after = lax.ppermute(first, "mp", down)
    return jnp.concatenate([before, array, after], axis=dim)


def pad_axis(values, axis):
    widths = [(0, 0)] * values.ndim
    widths[axis] = (4, 4)
    return jnp.pad(values, widths)


def forward_diff(padded, axis, length, start=4):
    total = jnp.zeros((), jnp.float32)
    for order in range(4):
        shift = order + 1
        upper = lax.slice_in_dim(padded, start + shift, start + shift + length, axis=axis)
        lower = lax.slice_in_dim(padded, start + 1 - shift, start + 1 - shift + length, axis=axis)
        total = total + COEFFS[order] * (upper - lower)
    return total


def backward_diff(padded, axis, length):
    total = jnp.zeros((), jnp.float32)
    for order in range(4):
        shift = order + 1
        upper = lax.slice_in_dim(padded, 3 + shift, 3 + shift + length, axis=axis)
        lower = lax.slice_in_dim(padded, 4 - shift, 4 - shift + length, axis=axis)
        total = total + COEFFS[order] * (upper - lower)
    return total


def cross_terms(values, buoyancy):
    total = jnp.zeros_like(values)
    for axis in (2, 3):
        length = values.shape[axis]
        flux = buoyancy * forward_diff(pad_axis(values, axis), axis, length)
        total = total + backward_diff(pad_axis(flux, axis), axis, length)
    return total


def local(
    velocity,
    buoyancy,
    wave_prev,
    wave_now,
    adjoint_next,
    adjoint_after,
    source_cell,
    wavelet,
    receiver_cell,
    observed,
):
    planes, cy, cz = velocity.shape
    assert planes >= HALO
    shots = wave_now.shape[0]
    shape = wave_now.shape
    rows = planes * cy
    cells = rows * cz
    kappa = velocity * velocity / buoyancy
    offset = lax.axis_index("mp") * cells
    buoyancy_wide = extended(buoyancy, 0, HALO)
    flux_buoyancy = buoyancy_wide[HALO - 4 : HALO + planes + 3]

    def operator(values):
        wide = extended(values, 1, HALO)
        flux = flux_buoyancy * forward_diff(wide, 1, planes + 7, start=HALO - 4)
        return backward_diff(flux, 1, planes) + cross_terms(values, buoyancy)

    source_local = source_cell - offset
    source_owned = (source_local >= 0) & (source_local < cells)
    source_index = jnp.clip(source_local, 0, cells - 1)
    shot_rows = jnp.arange(shots)

    receiver_local = receiver_cell - offset
    receiver_owned = (receiver_local >= 0) & (receiver_local < cells)
    receiver_row = jnp.where(receiver_owned, receiver_local // cz, -1)
    receiver_col = receiver_local % cz
    row_pick = (receiver_row[:, :, None] == jnp.arange(rows)[None, None, :]).astype(jnp.float32)
    col_pick = receiver_col[:, :, None] == jnp.arange(cz)[None, None, :]

    def sample(field):
        picked = jnp.einsum(
            "srk,skz->srz", row_pick, field.reshape(shots, rows, cz), precision=lax.Precision.HIGHEST
        )
        return jnp.sum(jnp.where(col_pick, picked, 0.0), axis=2)

    def inject(field, amounts):
        spread = jnp.where(col_pick, amounts[:, :, None], 0.0)
        added = jnp.einsum("srk,srz->skz", row_pick, spread, precision=lax.Precision.HIGHEST)
        return field + added.reshape(shape)

    before, current = (wave_prev, wave_now)
    laps = []
    resids = []
    for step in range(STEPS):
        lap = operator(current)
        laps.append(lap)
        following = 2.0 * current - before + kappa * lap
        amount = jnp.where(source_owned, wavelet[:, step], 0.0)
        flat = following.reshape(shots, cells).at[shot_rows, source_index].add(amount)
        following = flat.reshape(shape)
        sampled = sample(following)
        resids.append(jnp.where(receiver_owned, sampled - observed[:, step, :], 0.0))
        before, current = (current, following)
    local_misfit = 0.5 * sum((jnp.sum(item * item, axis=1) for item in resids))
    misfit = jnp.sum(lax.all_gather(local_misfit, "mp"), axis=0)
    mu_near, mu_far = (adjoint_next, adjoint_after)
    gradient = jnp.zeros(shape, jnp.float32)
    for level in range(STEPS, 0, -1):
        state = 2.0 * mu_near + operator(kappa * mu_near) - mu_far
        state = inject(state, resids[level - 1])
        gradient = gradient + state * laps[level - 1]
        mu_far, mu_near = (mu_near, state)
    velocity_gradient = 2.0 * velocity / buoyancy * jnp.sum(gradient, axis=0)
    return (velocity_gradient, mu_near, mu_far, misfit)


def solution(mesh):
    placed = (
        P(("group", "mp"), None, None),
        P(("group", "mp"), None, None),
        P("group", "mp", None, None),
        P("group", "mp", None, None),
        P("group", "mp", None, None),
        P("group", "mp", None, None),
        P("group"),
        P("group", None),
        P("group", None),
        P("group", None, None),
    )
    return jax.shard_map(
        local,
        mesh=mesh,
        in_specs=placed,
        out_specs=(
            P(("group", "mp"), None, None),
            P("group", "mp", None, None),
            P("group", "mp", None, None),
            P("group"),
        ),
        check_vma=False,
    )
```

time: 292 us -> 135 us (0.46); the launches traced: 287 us -> 134 us
  starting transfers between devices: 101 us -> 45 us
  other arithmetic: 63.6 us -> 11.2 us
  local copies, waits for them, and re-layouts: 51.8 us -> 3.45 us
  matrix products: 0 us -> 11.7 us
  waiting for transfers between devices: 25.7 us -> 19.7 us
    ppermute x32 -> x18, starting transfers between devices: 101 us -> 45 us  [the longest x9 23.5 us: extended(): before = lax.ppermute(last, 'mp', up)]
    unnamed x6 -> x0, other arithmetic: 53.6 us -> none
    gather x4 -> x0, local copies, waits for them, and re-layouts: 49.6 us -> none  [local(): sampled = flat[shot_rows[:, None], receiver_index]]
    psum x1 -> x0, blocking collectives: 30.9 us -> none  [local(): misfit = lax.psum(local_misfit, 'mp')]
    unnamed x0 -> x1, blocking collectives: none -> 28.4 us
    dot_general x0 -> x8, matrix products: none -> 11.7 us  [the longest x4 6.43 us: sample(): jnp.einsum('srk,skz->srz', row_pick, field.reshape(shots, rows, cz), prec...]
    ppermute x32 -> x18, waiting for transfers between devices: 25.7 us -> 19.7 us  [the longest x9 19.6 us: extended(): after = lax.ppermute(first, 'mp', down)]
  transfers between devices with their start and end apart: 32 -> 18, of which waited for: 13 -> 6; matrix products, arithmetic and copies ran while one was open for 18% -> 7% of each run, Pallas kernels for 0% -> 0%
where the time goes in v1:
time: 135 us; the launch traced here: 134 us
  starting transfers between devices  45 us (33%)
  blocking collectives  28.4 us (21%)
  waiting for transfers between devices  19.7 us (15%)
  between operations  14.8 us (11%)
  matrix products  11.7 us (9%)
  other arithmetic  11.2 us (8%)
  local copies, waits for them, and re-layouts  3.45 us (3%)
    unnamed x1, blocking collectives  28.4 us
    ppermute x9, starting transfers between devices, extended(): before = lax.ppermute(last, 'mp', up)  23.5 us
    ppermute x9, starting transfers between devices, extended(): after = lax.ppermute(first, 'mp', down)  21.5 us
    ppermute x9, waiting for transfers between devices, extended(): after = lax.ppermute(first, 'mp', down)  19.6 us
    dot_general x4, matrix products, sample(): jnp.einsum('srk,skz->srz', row_pick, field.reshape(shots, rows, cz), prec...  6.43 us
    dot_general x4, matrix products, inject(): jnp.einsum('srk,srz->skz', row_pick, spread, precision=lax.Precision.HIGH...  5.23 us
  transfers between devices with their start and end apart: 18, of which 6 were waited for; matrix products, arithmetic and copies ran while one was open for 7% of the time, Pallas kernels for 0%

profile of v1, /device:TPU:1, one launch (start us, length us, event | category | flops | bytes accessed | tf_op | source)
XLA Modules:
  0.0 134.2 jit_solution(16343857586338125852)
XLA Ops:
  0.6 1.1 bitcast_multiply_fusion.8
  1.7 4.7 %collective-permute-start.2 = (f32[1,7,32,128]{3,2,1,0:T(8,128)S(1)}, f32[1,7,32,128]{3,2,1,0:T(8,128)S(1)}, u32[]{:S(2)}, u32[]{:S(2)}) collective-permute-start(f32[1,7,32,128]{3,2,1,0:T(8,128)S(1)} %get-tuple-element.109), channel_id=1, source_target_pairs={{0,1},{1,2},{2,3},{3,4},{4,5},{5,6},{6,7},{7,8},{8,9},{9,10},{10,1... | collective-permute-start | bytes 344072 | tf_op jit(solution)/shard_map/ppermute | solution.py:18
  6.4 1.9 %collective-permute-start.3 = (f32[1,7,32,128]{3,2,1,0:T(8,128)S(1)}, f32[1,7,32,128]{3,2,1,0:T(8,128)S(1)}, u32[]{:S(2)}, u32[]{:S(2)}) collective-permute-start(f32[1,7,32,128]{3,2,1,0:T(8,128)S(1)} %get-tuple-element.110), channel_id=1, source_target_pairs={{1,0},{2,1},{3,2},{4,3},{5,4},{6,5},{7,6},{8,7},{9,8},{10,9},{11,1... | collective-permute-start | bytes 344072 | tf_op jit(solution)/shard_map/ppermute | solution.py:19
  8.4 3.6 %collective-permute-start = (f32[7,32,128]{2,1,0:T(8,128)S(1)}, f32[7,32,128]{2,1,0:T(8,128)S(1)}, u32[]{:S(2)}, u32[]{:S(2)}) collective-permute-start(f32[7,32,128]{2,1,0:T(8,128)S(1)} %get-tuple-element.107), channel_id=1, source_target_pairs={{0,1},{1,2},{2,3},{3,4},{4,5},{5,6},{6,7},{7,8},{8,9},{9,10},{10,1... | collective-permute-start | bytes 344072 | tf_op jit(solution)/shard_map/ppermute | solution.py:18
  12.1 1.9 %collective-permute-start.1 = (f32[7,32,128]{2,1,0:T(8,128)S(1)}, f32[7,32,128]{2,1,0:T(8,128)S(1)}, u32[]{:S(2)}, u32[]{:S(2)}) collective-permute-start(f32[7,32,128]{2,1,0:T(8,128)S(1)} %get-tuple-element.108), channel_id=1, source_target_pairs={{1,0},{2,1},{3,2},{4,3},{5,4},{6,5},{7,6},{8,7},{9,8},{10,9},{11,1... | collective-permute-start | bytes 344072 | tf_op jit(solution)/shard_map/ppermute | solution.py:19
  14.0 3.6 %collective-permute-start.4 = (f32[1,7,32,128]{3,2,1,0:T(8,128)S(1)}, f32[1,7,32,128]{3,2,1,0:T(8,128)S(1)}, u32[]{:S(2)}, u32[]{:S(2)}) collective-permute-start(f32[1,7,32,128]{3,2,1,0:T(8,128)S(1)} %get-tuple-element.106), channel_id=1, source_target_pairs={{0,1},{1,2},{2,3},{3,4},{4,5},{5,6},{6,7},{7,8},{8,9},{9,10},{10,1... | collective-permute-start | bytes 344072 | tf_op jit(solution)/shard_map/ppermute | solution.py:18
  17.8 0.6 fusion.625
  21.7 0.6 dynamic-slice.40
  22.3 0.7 and_reduce_fusion
  23.0 1.9 %collective-permute-start.5 = (f32[1,7,32,128]{3,2,1,0:T(8,128)S(1)}, f32[1,7,32,128]{3,2,1,0:T(8,128)S(1)}, u32[]{:S(2)}, u32[]{:S(2)}) collective-permute-start(f32[1,7,32,128]{3,2,1,0:T(8,128)S(1)} %get-tuple-element.105), channel_id=1, source_target_pairs={{1,0},{2,1},{3,2},{4,3},{5,4},{6,5},{7,6},{8,7},{9,8},{10,9},{11,1... | collective-permute-start | bytes 344072 | tf_op jit(solution)/shard_map/ppermute | solution.py:19
  24.9 0.5 fusion.359
  25.5 3.6 %collective-permute-done.5 = f32[1,7,32,128]{3,2,1,0:T(8,128)S(1)} collective-permute-done((f32[1,7,32,128]{3,2,1,0:T(8,128)S(1)}, f32[1,7,32,128]{3,2,1,0:T(8,128)S(1)}, u32[]{:S(2)}, u32[]{:S(2)}) %collective-permute-start.5) | collective-permute-done | bytes 114720 | tf_op jit(solution)/shard_map/ppermute | solution.py:19
  29.1 0.1 fusion.133
  29.3 0.1 fusion.126
  29.4 0.8 copy-done.6
  30.2 0.3 fusion.594
  30.5 0.7 fusion.626
  33.1 0.1 scatter-add.14
  33.2 0.3 fusion.203
  33.5 2.0 %collective-permute-start.6 = (f32[1,7,32,128]{3,2,1,0:T(8,128)S(1)}, f32[1,7,32,128]{3,2,1,0:T(8,128)S(1)}, u32[]{:S(2)}, u32[]{:S(2)}) collective-permute-start(f32[1,7,32,128]{3,2,1,0:T(8,128)S(1)} %get-tuple-element.103), channel_id=1, source_target_pairs={{0,1},{1,2},{2,3},{3,4},{4,5},{5,6},{6,7},{7,8},{8,9},{9,10},{10,1... | collective-permute-start | bytes 344072 | tf_op jit(solution)/shard_map/ppermute | solution.py:18
  35.5 2.4 %collective-permute-start.7 = (f32[1,7,32,128]{3,2,1,0:T(8,128)S(1)}, f32[1,7,32,128]{3,2,1,0:T(8,128)S(1)}, u32[]{:S(2)}, u32[]{:S(2)}) collective-permute-start(f32[1,7,32,128]{3,2,1,0:T(8,128)S(1)} %get-tuple-element.104), channel_id=1, source_target_pairs={{1,0},{2,1},{3,2},{4,3},{5,4},{6,5},{7,6},{8,7},{9,8},{10,9},{11,1... | collective-permute-start | bytes 344072 | tf_op jit(solution)/shard_map/ppermute | solution.py:19
  37.9 1.6 %fusion.22 = f32[2048]{0:T(1024)S(1)} fusion(f32[256,128]{1,0:T(8,128)S(1)} %bitcast.150, s32[2048]{0:T(1024)S(1)} %bitcast.183, s32[2048]{0:T(1024)S(1)} %bitcast.175), kind=kOutput, calls=%fused_computation.17 | convolution fusion | flops 806615040 | bytes 155648 | tf_op jit(solution)/shard_map/srk,skz->srz/dot_general | solution.py:99
  39.5 4.7 %collective-permute-done.7 = f32[1,7,32,128]{3,2,1,0:T(8,128)S(1)} collective-permute-done((f32[1,7,32,128]{3,2,1,0:T(8,128)S(1)}, f32[1,7,32,128]{3,2,1,0:T(8,128)S(1)}, u32[]{:S(2)}, u32[]{:S(2)}) %collective-permute-start.7) | collective-permute-done | bytes 114720 | tf_op jit(solution)/shard_map/ppermute | solution.py:19
  44.2 0.1 fusion.119
  44.3 0.3 fusion.595
  44.6 0.7 fusion.627
  47.2 0.1 scatter-add.15
  47.3 0.3 fusion.228
  47.7 1.9 %collective-permute-start.8 = (f32[1,7,32,128]{3,2,1,0:T(8,128)S(1)}, f32[1,7,32,128]{3,2,1,0:T(8,128)S(1)}, u32[]{:S(2)}, u32[]{:S(2)}) collective-permute-start(f32[1,7,32,128]{3,2,1,0:T(8,128)S(1)} %get-tuple-element.101), channel_id=1, source_target_pairs={{0,1},{1,2},{2,3},{3,4},{4,5},{5,6},{6,7},{7,8},{8,9},{9,10},{10,1... | collective-permute-start | bytes 344072 | tf_op jit(solution)/shard_map/ppermute | solution.py:18
  49.6 2.4 %collective-permute-start.9 = (f32[1,7,32,128]{3,2,1,0:T(8,128)S(1)}, f32[1,7,32,128]{3,2,1,0:T(8,128)S(1)}, u32[]{:S(2)}, u32[]{:S(2)}) collective-permute-start(f32[1,7,32,128]{3,2,1,0:T(8,128)S(1)} %get-tuple-element.102), channel_id=1, source_target_pairs={{1,0},{2,1},{3,2},{4,3},{5,4},{6,5},{7,6},{8,7},{9,8},{10,9},{11,1... | collective-permute-start | bytes 344072 | tf_op jit(solution)/shard_map/ppermute | solution.py:19
  52.0 1.6 %fusion.19 = f32[2048]{0:T(1024)S(1)} fusion(f32[256,128]{1,0:T(8,128)S(1)} %bitcast.159, s32[2048]{0:T(1024)S(1)} %bitcast.184, s32[2048]{0:T(1024)S(1)} %bitcast.176), kind=kOutput, calls=%fused_computation.16 | convolution fusion | flops 806615040 | bytes 155648 | tf_op jit(solution)/shard_map/srk,skz->srz/dot_general | solution.py:99
  53.6 3.0 %collective-permute-done.9 = f32[1,7,32,128]{3,2,1,0:T(8,128)S(1)} collective-permute-done((f32[1,7,32,128]{3,2,1,0:T(8,128)S(1)}, f32[1,7,32,128]{3,2,1,0:T(8,128)S(1)}, u32[]{:S(2)}, u32[]{:S(2)}) %collective-permute-start.9) | collective-permute-done | bytes 114720 | tf_op jit(solution)/shard_map/ppermute | solution.py:19
  56.7 0.3 fusion.596
  57.0 0.6 fusion.628
  59.5 0.1 scatter-add.16
  59.7 0.3 fusion.253
  60.0 1.9 %collective-permute-start.10 = (f32[1,7,32,128]{3,2,1,0:T(8,128)S(1)}, f32[1,7,32,128]{3,2,1,0:T(8,128)S(1)}, u32[]{:S(2)}, u32[]{:S(2)}) collective-permute-start(f32[1,7,32,128]{3,2,1,0:T(8,128)S(1)} %get-tuple-element.99), channel_id=1, source_target_pairs={{0,1},{1,2},{2,3},{3,4},{4,5},{5,6},{6,7},{7,8},{8,9},{9,10},{10,1... | collective-permute-start | bytes 344072 | tf_op jit(solution)/shard_map/ppermute | solution.py:18
  61.9 2.4 %collective-permute-start.11 = (f32[1,7,32,128]{3,2,1,0:T(8,128)S(1)}, f32[1,7,32,128]{3,2,1,0:T(8,128)S(1)}, u32[]{:S(2)}, u32[]{:S(2)}) collective-permute-start(f32[1,7,32,128]{3,2,1,0:T(8,128)S(1)} %get-tuple-element.100), channel_id=1, source_target_pairs={{1,0},{2,1},{3,2},{4,3},{5,4},{6,5},{7,6},{8,7},{9,8},{10,9},{11,1... | collective-permute-start | bytes 344072 | tf_op jit(solution)/shard_map/ppermute | solution.py:19
  64.3 1.6 %fusion.16 = f32[2048]{0:T(1024)S(1)} fusion(f32[256,128]{1,0:T(8,128)S(1)} %bitcast.168, s32[2048]{0:T(1024)S(1)} %bitcast.185, s32[2048]{0:T(1024)S(1)} %bitcast.177), kind=kOutput, calls=%fused_computation.15 | convolution fusion | flops 806615040 | bytes 155648 | tf_op jit(solution)/shard_map/srk,skz->srz/dot_general | solution.py:99
  65.9 3.0 %collective-permute-done.11 = f32[1,7,32,128]{3,2,1,0:T(8,128)S(1)} collective-permute-done((f32[1,7,32,128]{3,2,1,0:T(8,128)S(1)}, f32[1,7,32,128]{3,2,1,0:T(8,128)S(1)}, u32[]{:S(2)}, u32[]{:S(2)}) %collective-permute-start.11) | collective-permute-done | bytes 114720 | tf_op jit(solution)/shard_map/ppermute | solution.py:19
  69.0 0.3 fusion.597
  69.4 0.7 fusion.629
  72.0 0.1 scatter-add.19
  72.2 1.6 %fusion.13 = f32[2048]{0:T(1024)S(1)} fusion(f32[256,128]{1,0:T(8,128)S(1)} %bitcast.174, s32[2048]{0:T(1024)S(1)} %bitcast.186, s32[2048]{0:T(1024)S(1)} %bitcast.178), kind=kOutput, calls=%fused_computation.14 | convolution fusion | flops 806615040 | bytes 155648 | tf_op jit(solution)/shard_map/srk,skz->srz/dot_general | solution.py:99
  73.8 0.7 multiply_reduce_fusion.2
  74.5 1.3 bitcast_multiply_fusion.3
  75.8 1.9 %collective-permute-start.12 = (f32[1,7,32,128]{3,2,1,0:T(8,128)S(1)}, f32[1,7,32,128]{3,2,1,0:T(8,128)S(1)}, u32[]{:S(2)}, u32[]{:S(2)}) collective-permute-start(f32[1,7,32,128]{3,2,1,0:T(8,128)S(1)} %get-tuple-element.94), channel_id=1, source_target_pairs={{0,1},{1,2},{2,3},{3,4},{4,5},{5,6},{6,7},{7,8},{8,9},{9,10},{10,1... | collective-permute-start | bytes 344072 | tf_op jit(solution)/shard_map/ppermute | solution.py:18
  77.8 2.4 %collective-permute-start.13 = (f32[1,7,32,128]{3,2,1,0:T(8,128)S(1)}, f32[1,7,32,128]{3,2,1,0:T(8,128)S(1)}, u32[]{:S(2)}, u32[]{:S(2)}) collective-permute-start(f32[1,7,32,128]{3,2,1,0:T(8,128)S(1)} %get-tuple-element.95), channel_id=1, source_target_pairs={{1,0},{2,1},{3,2},{4,3},{5,4},{6,5},{7,6},{8,7},{9,8},{10,9},{11,1... | collective-permute-start | bytes 344072 | tf_op jit(solution)/shard_map/ppermute | solution.py:19
  82.7 0.7 dynamic-update-slice.12
  83.5 0.3 fusion.474
  83.8 28.4 %all-reduce.32 = f32[16]{0:T(128)S(1)} all-reduce(f32[16]{0:T(128)S(1)} %dynamic-update-slice.12), channel_id=1, replica_groups=mesh['group'=2,'mp'=16] {'mp'}, use_global_device_ids=true, to_apply=%add.32 | all-reduce | flops 16 | bytes 128
  112.2 0.6 reduce.26
  113.0 1.3 bitcast_multiply_fusion.2
  114.3 1.9 %collective-permute-start.14 = (f32[1,7,32,128]{3,2,1,0:T(8,128)S(1)}, f32[1,7,32,128]{3,2,1,0:T(8,128)S(1)}, u32[]{:S(2)}, u32[]{:S(2)}) collective-permute-start(f32[1,7,32,128]{3,2,1,0:T(8,128)S(1)} %get-tuple-element.92), channel_id=1, source_target_pairs={{0,1},{1,2},{2,3},{3,4},{4,5},{5,6},{6,7},{7,8},{8,9},{9,10},{10,1... | collective-permute-start | bytes 344072 | tf_op jit(solution)/shard_map/ppermute | solution.py:18
  116.2 3.7 %collective-permute-start.15 = (f32[1,7,32,128]{3,2,1,0:T(8,128)S(1)}, f32[1,7,32,128]{3,2,1,0:T(8,128)S(1)}, u32[]{:S(2)}, u32[]{:S(2)}) collective-permute-start(f32[1,7,32,128]{3,2,1,0:T(8,128)S(1)} %get-tuple-element.93), channel_id=1, source_target_pairs={{1,0},{2,1},{3,2},{4,3},{5,4},{6,5},{7,6},{8,7},{9,8},{10,9},{11,1... | collective-permute-start | bytes 344072 | tf_op jit(solution)/shard_map/ppermute | solution.py:19
  119.9 0.3 fusion.497
  120.2 2.1 %collective-permute-done.15 = f32[1,7,32,128]{3,2,1,0:T(8,128)S(1)} collective-permute-done((f32[1,7,32,128]{3,2,1,0:T(8,128)S(1)}, f32[1,7,32,128]{3,2,1,0:T(8,128)S(1)}, u32[]{:S(2)}, u32[]{:S(2)}) %collective-permute-start.15) | collective-permute-done | bytes 114720 | tf_op jit(solution)/shard_map/ppermute | solution.py:19
  122.5 1.3 bitcast_multiply_fusion.1
  123.8 1.9 %collective-permute-start.16 = (f32[1,7,32,128]{3,2,1,0:T(8,128)S(1)}, f32[1,7,32,128]{3,2,1,0:T(8,128)S(1)}, u32[]{:S(2)}, u32[]{:S(2)}) collective-permute-start(f32[1,7,32,128]{3,2,1,0:T(8,128)S(1)} %get-tuple-element.90), channel_id=1, source_target_pairs={{0,1},{1,2},{2,3},{3,4},{4,5},{5,6},{6,7},{7,8},{8,9},{9,10},{10,1... | collective-permute-start | bytes 344072 | tf_op jit(solution)/shard_map/ppermute | solution.py:18
  125.8 2.4 %collective-permute-start.17 = (f32[1,7,32,128]{3,2,1,0:T(8,128)S(1)}, f32[1,7,32,128]{3,2,1,0:T(8,128)S(1)}, u32[]{:S(2)}, u32[]{:S(2)}) collective-permute-start(f32[1,7,32,128]{3,2,1,0:T(8,128)S(1)} %get-tuple-element.91), channel_id=1, source_target_pairs={{1,0},{2,1},{3,2},{4,3},{5,4},{6,5},{7,6},{8,7},{9,8},{10,9},{11,1... | collective-permute-start | bytes 344072 | tf_op jit(solution)/shard_map/ppermute | solution.py:19
  128.2 0.3 fusion.520
  128.5 3.4 %collective-permute-done.17 = f32[1,7,32,128]{3,2,1,0:T(8,128)S(1)} collective-permute-done((f32[1,7,32,128]{3,2,1,0:T(8,128)S(1)}, f32[1,7,32,128]{3,2,1,0:T(8,128)S(1)}, u32[]{:S(2)}, u32[]{:S(2)}) %collective-permute-start.17) | collective-permute-done | bytes 114720 | tf_op jit(solution)/shard_map/ppermute | solution.py:19
  132.0 1.3 fusion.37
  133.4 0.8 bitcast_multiply_fusion
  (62 shorter events, 1.1 us)
Async XLA Ops:
  1.7 6.7 %copy-start = (f32[8,32,128]{2,1,0:T(8,128)S(1)}, f32[8,32,128]{2,1,0:T(8,128)}, u32[]{:S(2)}) copy-start(f32[8,32,128]{2,1,0:T(8,128)} %param.19) | copy-start | bytes 393220
  1.7 12.3 %copy-start.1 = (f32[1,8,32,128]{3,2,1,0:T(8,128)S(1)}, f32[1,8,32,128]{3,2,1,0:T(8,128)}, u32[]{:S(2)}) copy-start(f32[1,8,32,128]{3,2,1,0:T(8,128)} %param.21) | copy-start | bytes 393220
  1.7 23.7 %collective-permute-start.2 = (f32[1,7,32,128]{3,2,1,0:T(8,128)S(1)}, f32[1,7,32,128]{3,2,1,0:T(8,128)S(1)}, u32[]{:S(2)}, u32[]{:S(2)}) collective-permute-start(f32[1,7,32,128]{3,2,1,0:T(8,128)S(1)} %get-tuple-element.109), channel_id=1, source_target_pairs={{0,1},{1,2},{2,3},{3,4},{4,5},{5,6},{6,7},{7,8},{8,9},{9,10},{10,1... | collective-permute-start | bytes 344072 | tf_op jit(solution)/shard_map/ppermute | solution.py:18
  6.4 11.3 %copy-start.7 = (s32[1,2048]{1,0:T(1,128)S(1)}, s32[1,2048]{1,0:T(1,128)}, u32[]{:S(2)}) copy-start(s32[1,2048]{1,0:T(1,128)} %param.26) | copy-start | bytes 24580
  6.4 19.1 %collective-permute-start.3 = (f32[1,7,32,128]{3,2,1,0:T(8,128)S(1)}, f32[1,7,32,128]{3,2,1,0:T(8,128)S(1)}, u32[]{:S(2)}, u32[]{:S(2)}) collective-permute-start(f32[1,7,32,128]{3,2,1,0:T(8,128)S(1)} %get-tuple-element.110), channel_id=1, source_target_pairs={{1,0},{2,1},{3,2},{4,3},{5,4},{6,5},{7,6},{8,7},{9,8},{10,9},{11,1... | collective-permute-start | bytes 344072 | tf_op jit(solution)/shard_map/ppermute | solution.py:19
  8.4 9.4 %copy-start.9 = (f32[1,4]{1,0:T(1,128)S(1)}, f32[1,4]{1,0:T(1,128)}, u32[]{:S(2)}) copy-start(f32[1,4]{1,0:T(1,128)} %param.25) | copy-start | bytes 52
  8.4 13.3 %copy-start.11 = (u32[32]{0:T(128)S(1)}, u32[32]{0:T(128)}, u32[]{:S(2)}) copy-start(u32[32]{0:T(128)} %constant.233) | copy-start | bytes 388
  8.4 20.7 %collective-permute-start = (f32[7,32,128]{2,1,0:T(8,128)S(1)}, f32[7,32,128]{2,1,0:T(8,128)S(1)}, u32[]{:S(2)}, u32[]{:S(2)}) collective-permute-start(f32[7,32,128]{2,1,0:T(8,128)S(1)} %get-tuple-element.107), channel_id=1, source_target_pairs={{0,1},{1,2},{2,3},{3,4},{4,5},{5,6},{6,7},{7,8},{8,9},{9,10},{10,1... | collective-permute-start | bytes 344072 | tf_op jit(solution)/shard_map/ppermute | solution.py:18
  12.1 17.0 %collective-permute-start.1 = (f32[7,32,128]{2,1,0:T(8,128)S(1)}, f32[7,32,128]{2,1,0:T(8,128)S(1)}, u32[]{:S(2)}, u32[]{:S(2)}) collective-permute-start(f32[7,32,128]{2,1,0:T(8,128)S(1)} %get-tuple-element.108), channel_id=1, source_target_pairs={{1,0},{2,1},{3,2},{4,3},{5,4},{6,5},{7,6},{8,7},{9,8},{10,9},{11,1... | collective-permute-start | bytes 344072 | tf_op jit(solution)/shard_map/ppermute | solution.py:19
  14.0 9.0 %collective-permute-start.4 = (f32[1,7,32,128]{3,2,1,0:T(8,128)S(1)}, f32[1,7,32,128]{3,2,1,0:T(8,128)S(1)}, u32[]{:S(2)}, u32[]{:S(2)}) collective-permute-start(f32[1,7,32,128]{3,2,1,0:T(8,128)S(1)} %get-tuple-element.106), channel_id=1, source_target_pairs={{0,1},{1,2},{2,3},{3,4},{4,5},{5,6},{6,7},{7,8},{8,9},{9,10},{10,1... | collective-permute-start | bytes 344072 | tf_op jit(solution)/shard_map/ppermute | solution.py:18
  23.0 6.1 %collective-permute-start.5 = (f32[1,7,32,128]{3,2,1,0:T(8,128)S(1)}, f32[1,7,32,128]{3,2,1,0:T(8,128)S(1)}, u32[]{:S(2)}, u32[]{:S(2)}) collective-permute-start(f32[1,7,32,128]{3,2,1,0:T(8,128)S(1)} %get-tuple-element.105), channel_id=1, source_target_pairs={{1,0},{2,1},{3,2},{4,3},{5,4},{6,5},{7,6},{8,7},{9,8},{10,9},{11,1... | collective-permute-start | bytes 344072 | tf_op jit(solution)/shard_map/ppermute | solution.py:19
  29.3 0.9 copy-start.6
  33.5 6.0 %collective-permute-start.6 = (f32[1,7,32,128]{3,2,1,0:T(8,128)S(1)}, f32[1,7,32,128]{3,2,1,0:T(8,128)S(1)}, u32[]{:S(2)}, u32[]{:S(2)}) collective-permute-start(f32[1,7,32,128]{3,2,1,0:T(8,128)S(1)} %get-tuple-element.103), channel_id=1, source_target_pairs={{0,1},{1,2},{2,3},{3,4},{4,5},{5,6},{6,7},{7,8},{8,9},{9,10},{10,1... | collective-permute-start | bytes 344072 | tf_op jit(solution)/shard_map/ppermute | solution.py:18
  35.5 8.7 %collective-permute-start.7 = (f32[1,7,32,128]{3,2,1,0:T(8,128)S(1)}, f32[1,7,32,128]{3,2,1,0:T(8,128)S(1)}, u32[]{:S(2)}, u32[]{:S(2)}) collective-permute-start(f32[1,7,32,128]{3,2,1,0:T(8,128)S(1)} %get-tuple-element.104), channel_id=1, source_target_pairs={{1,0},{2,1},{3,2},{4,3},{5,4},{6,5},{7,6},{8,7},{9,8},{10,9},{11,1... | collective-permute-start | bytes 344072 | tf_op jit(solution)/shard_map/ppermute | solution.py:19
  47.7 6.0 %collective-permute-start.8 = (f32[1,7,32,128]{3,2,1,0:T(8,128)S(1)}, f32[1,7,32,128]{3,2,1,0:T(8,128)S(1)}, u32[]{:S(2)}, u32[]{:S(2)}) collective-permute-start(f32[1,7,32,128]{3,2,1,0:T(8,128)S(1)} %get-tuple-element.101), channel_id=1, source_target_pairs={{0,1},{1,2},{2,3},{3,4},{4,5},{5,6},{6,7},{7,8},{8,9},{9,10},{10,1... | collective-permute-start | bytes 344072 | tf_op jit(solution)/shard_map/ppermute | solution.py:18
  49.6 7.0 %collective-permute-start.9 = (f32[1,7,32,128]{3,2,1,0:T(8,128)S(1)}, f32[1,7,32,128]{3,2,1,0:T(8,128)S(1)}, u32[]{:S(2)}, u32[]{:S(2)}) collective-permute-start(f32[1,7,32,128]{3,2,1,0:T(8,128)S(1)} %get-tuple-element.102), channel_id=1, source_target_pairs={{1,0},{2,1},{3,2},{4,3},{5,4},{6,5},{7,6},{8,7},{9,8},{10,9},{11,1... | collective-permute-start | bytes 344072 | tf_op jit(solution)/shard_map/ppermute | solution.py:19
  60.0 6.0 %collective-permute-start.10 = (f32[1,7,32,128]{3,2,1,0:T(8,128)S(1)}, f32[1,7,32,128]{3,2,1,0:T(8,128)S(1)}, u32[]{:S(2)}, u32[]{:S(2)}) collective-permute-start(f32[1,7,32,128]{3,2,1,0:T(8,128)S(1)} %get-tuple-element.99), channel_id=1, source_target_pairs={{0,1},{1,2},{2,3},{3,4},{4,5},{5,6},{6,7},{7,8},{8,9},{9,10},{10,1... | collective-permute-start | bytes 344072 | tf_op jit(solution)/shard_map/ppermute | solution.py:18
  61.9 7.0 %collective-permute-start.11 = (f32[1,7,32,128]{3,2,1,0:T(8,128)S(1)}, f32[1,7,32,128]{3,2,1,0:T(8,128)S(1)}, u32[]{:S(2)}, u32[]{:S(2)}) collective-permute-start(f32[1,7,32,128]{3,2,1,0:T(8,128)S(1)} %get-tuple-element.100), channel_id=1, source_target_pairs={{1,0},{2,1},{3,2},{4,3},{5,4},{6,5},{7,6},{8,7},{9,8},{10,9},{11,1... | collective-permute-start | bytes 344072 | tf_op jit(solution)/shard_map/ppermute | solution.py:19
  72.1 1.6 %copy-start.8 = (f32[1,4,2048]{2,1,0:T(4,128)S(1)}, f32[1,4,2048]{2,1,0:T(4,128)}, u32[]{:S(2)}) copy-start(f32[1,4,2048]{2,1,0:T(4,128)} %param.27) | copy-start | bytes 98308
  72.1 2.4 %copy-start.3 = (f32[1,8,32,128]{3,2,1,0:T(8,128)S(1)}, f32[1,8,32,128]{3,2,1,0:T(8,128)}, u32[]{:S(2)}) copy-start(f32[1,8,32,128]{3,2,1,0:T(8,128)} %param.22) | copy-start | bytes 393220
  72.2 2.4 %copy-start.10 = (f32[1,8,32,128]{3,2,1,0:T(8,128)S(1)}, f32[1,8,32,128]{3,2,1,0:T(8,128)}, u32[]{:S(2)}) copy-start(f32[1,8,32,128]{3,2,1,0:T(8,128)} %param.23) | copy-start | bytes 393220
  75.8 37.0 %collective-permute-start.12 = (f32[1,7,32,128]{3,2,1,0:T(8,128)S(1)}, f32[1,7,32,128]{3,2,1,0:T(8,128)S(1)}, u32[]{:S(2)}, u32[]{:S(2)}) collective-permute-start(f32[1,7,32,128]{3,2,1,0:T(8,128)S(1)} %get-tuple-element.94), channel_id=1, source_target_pairs={{0,1},{1,2},{2,3},{3,4},{4,5},{5,6},{6,7},{7,8},{8,9},{9,10},{10,1... | collective-permute-start | bytes 344072 | tf_op jit(solution)/shard_map/ppermute | solution.py:18
  77.8 35.1 %collective-permute-start.13 = (f32[1,7,32,128]{3,2,1,0:T(8,128)S(1)}, f32[1,7,32,128]{3,2,1,0:T(8,128)S(1)}, u32[]{:S(2)}, u32[]{:S(2)}) collective-permute-start(f32[1,7,32,128]{3,2,1,0:T(8,128)S(1)} %get-tuple-element.95), channel_id=1, source_target_pairs={{1,0},{2,1},{3,2},{4,3},{5,4},{6,5},{7,6},{8,7},{9,8},{10,9},{11,1... | collective-permute-start | bytes 344072 | tf_op jit(solution)/shard_map/ppermute | solution.py:19
  114.3 5.9 %collective-permute-start.14 = (f32[1,7,32,128]{3,2,1,0:T(8,128)S(1)}, f32[1,7,32,128]{3,2,1,0:T(8,128)S(1)}, u32[]{:S(2)}, u32[]{:S(2)}) collective-permute-start(f32[1,7,32,128]{3,2,1,0:T(8,128)S(1)} %get-tuple-element.92), channel_id=1, source_target_pairs={{0,1},{1,2},{2,3},{3,4},{4,5},{5,6},{6,7},{7,8},{8,9},{9,10},{10,1... | collective-permute-start | bytes 344072 | tf_op jit(solution)/shard_map/ppermute | solution.py:18
  116.2 6.1 %collective-permute-start.15 = (f32[1,7,32,128]{3,2,1,0:T(8,128)S(1)}, f32[1,7,32,128]{3,2,1,0:T(8,128)S(1)}, u32[]{:S(2)}, u32[]{:S(2)}) collective-permute-start(f32[1,7,32,128]{3,2,1,0:T(8,128)S(1)} %get-tuple-element.93), channel_id=1, source_target_pairs={{1,0},{2,1},{3,2},{4,3},{5,4},{6,5},{7,6},{8,7},{9,8},{10,9},{11,1... | collective-permute-start | bytes 344072 | tf_op jit(solution)/shard_map/ppermute | solution.py:19
  123.8 9.6 %copy-start.4 = (f32[1,8,32,128]{3,2,1,0:T(8,128)}, f32[1,8,32,128]{3,2,1,0:T(8,128)S(1)}, u32[]{:S(2)}) copy-start(f32[1,8,32,128]{3,2,1,0:T(8,128)S(1)} %get-tuple-element.134) | copy-start | bytes 393220
  123.8 4.7 %collective-permute-start.16 = (f32[1,7,32,128]{3,2,1,0:T(8,128)S(1)}, f32[1,7,32,128]{3,2,1,0:T(8,128)S(1)}, u32[]{:S(2)}, u32[]{:S(2)}) collective-permute-start(f32[1,7,32,128]{3,2,1,0:T(8,128)S(1)} %get-tuple-element.90), channel_id=1, source_target_pairs={{0,1},{1,2},{2,3},{3,4},{4,5},{5,6},{6,7},{7,8},{8,9},{9,10},{10,1... | collective-permute-start | bytes 344072 | tf_op jit(solution)/shard_map/ppermute | solution.py:18
  125.8 6.1 %collective-permute-start.17 = (f32[1,7,32,128]{3,2,1,0:T(8,128)S(1)}, f32[1,7,32,128]{3,2,1,0:T(8,128)S(1)}, u32[]{:S(2)}, u32[]{:S(2)}) collective-permute-start(f32[1,7,32,128]{3,2,1,0:T(8,128)S(1)} %get-tuple-element.91), channel_id=1, source_target_pairs={{1,0},{2,1},{3,2},{4,3},{5,4},{6,5},{7,6},{8,7},{9,8},{10,9},{11,1... | collective-permute-start | bytes 344072 | tf_op jit(solution)/shard_map/ppermute | solution.py:19
  132.0 1.4 %copy-start.2 = (f32[8,32,128]{2,1,0:T(8,128)S(1)}, f32[8,32,128]{2,1,0:T(8,128)}, u32[]{:S(2)}) copy-start(f32[8,32,128]{2,1,0:T(8,128)} %param.18) | copy-start | bytes 393220
  133.4 0.8 copy-start.5

commit v2 on v1

--- a/solution.py
+++ b/solution.py
@@ -18,6 +18,17 @@
     before = lax.ppermute(last, "mp", up)
     after = lax.ppermute(first, "mp", down)
     return jnp.concatenate([before, array, after], axis=dim)
+
+
+def all_sum(values, axis):
+    devices = lax.axis_size(axis)
+    assert devices & (devices - 1) == 0
+    distance = 1
+    while distance < devices:
+        pairs = [(i, i ^ distance) for i in range(devices)]
+        values = values + lax.ppermute(values, axis, pairs)
+        distance *= 2
+    return values
 
 
 def pad_axis(values, axis):
@@ -120,7 +131,7 @@
         resids.append(jnp.where(receiver_owned, sampled - observed[:, step, :], 0.0))
         before, current = (current, following)
     local_misfit = 0.5 * sum((jnp.sum(item * item, axis=1) for item in resids))
-    misfit = jnp.sum(lax.all_gather(local_misfit, "mp"), axis=0)
+    misfit = all_sum(local_misfit, "mp")
     mu_near, mu_far = (adjoint_next, adjoint_after)
     gradient = jnp.zeros(shape, jnp.float32)
     for level in range(STEPS, 0, -1):

time: 135 us -> 125 us (0.926)
  blocking collectives: 28.4 us -> 0 us
  starting transfers between devices: 45 us -> 58.1 us
  waiting for transfers between devices: 19.7 us -> 23.9 us
  between operations: 14.8 us -> 18.1 us
  local copies, waits for them, and re-layouts: 3.45 us -> 2.08 us
    unnamed x1 -> x0, blocking collectives: 28.4 us -> none
    ppermute x0 -> x4, starting transfers between devices: none -> 10.1 us  [all_sum(): values = values + lax.ppermute(values, axis, pairs)]
    ppermute x9, starting transfers between devices: 23.5 us -> 28.2 us  [extended(): before = lax.ppermute(last, 'mp', up)]
    ppermute x9, waiting for transfers between devices: 19.6 us -> 23 us  [extended(): after = lax.ppermute(first, 'mp', down)]
    ppermute x9, starting transfers between devices: 21.5 us -> 19.9 us  [extended(): after = lax.ppermute(first, 'mp', down)]
    unnamed x28 -> x23, local copies, waits for them, and re-layouts: 2.21 us -> 0.85 us
  transfers between devices with their start and end apart: 18 -> 22, of which waited for: 6 -> 10; matrix products, arithmetic and copies ran while one was open for 7% -> 6% of each run, Pallas kernels for 0% -> 0%
where the time goes in v2:
time: 125 us; the launch traced here: 124 us
  starting transfers between devices  58.1 us (46%)
  waiting for transfers between devices  23.9 us (19%)
  between operations  18.1 us (14%)
  matrix products  11.7 us (9%)
  other arithmetic  10.5 us (8%)
  local copies, waits for them, and re-layouts  2.08 us (2%)
    ppermute x9, starting transfers between devices, extended(): before = lax.ppermute(last, 'mp', up)  28.2 us
    ppermute x9, waiting for transfers between devices, extended(): after = lax.ppermute(first, 'mp', down)  23 us
    ppermute x9, starting transfers between devices, extended(): after = lax.ppermute(first, 'mp', down)  19.9 us
    ppermute x4, starting transfers between devices, all_sum(): values = values + lax.ppermute(values, axis, pairs)  10.1 us
    dot_general x4, matrix products, sample(): jnp.einsum('srk,skz->srz', row_pick, field.reshape(shots, rows, cz), prec...  6.43 us
    dot_general x4, matrix products, inject(): jnp.einsum('srk,srz->skz', row_pick, spread, precision=lax.Precision.HIGH...  5.23 us
  transfers between devices with their start and end apart: 22, of which 10 were waited for; matrix products, arithmetic and copies ran while one was open for 6% of the time, Pallas kernels for 0%

profile of v2, /device:TPU:1, one launch (start us, length us, event | category | flops | bytes accessed | tf_op | source)
XLA Modules:
  0.0 124.4 jit_solution(9413435591198381855)
XLA Ops:
  0.6 1.1 bitcast_multiply_fusion.8
  1.7 4.7 %collective-permute-start.2 = (f32[1,7,32,128]{3,2,1,0:T(8,128)S(1)}, f32[1,7,32,128]{3,2,1,0:T(8,128)S(1)}, u32[]{:S(2)}, u32[]{:S(2)}) collective-permute-start(f32[1,7,32,128]{3,2,1,0:T(8,128)S(1)} %get-tuple-element.109), channel_id=1, source_target_pairs={{0,1},{1,2},{2,3},{3,4},{4,5},{5,6},{6,7},{7,8},{8,9},{9,10},{10,1... | collective-permute-start | bytes 344072 | tf_op jit(solution)/shard_map/ppermute | solution.py:18
  6.4 1.9 %collective-permute-start.3 = (f32[1,7,32,128]{3,2,1,0:T(8,128)S(1)}, f32[1,7,32,128]{3,2,1,0:T(8,128)S(1)}, u32[]{:S(2)}, u32[]{:S(2)}) collective-permute-start(f32[1,7,32,128]{3,2,1,0:T(8,128)S(1)} %get-tuple-element.110), channel_id=1, source_target_pairs={{1,0},{2,1},{3,2},{4,3},{5,4},{6,5},{7,6},{8,7},{9,8},{10,9},{11,1... | collective-permute-start | bytes 344072 | tf_op jit(solution)/shard_map/ppermute | solution.py:19
  8.4 3.6 %collective-permute-start = (f32[7,32,128]{2,1,0:T(8,128)S(1)}, f32[7,32,128]{2,1,0:T(8,128)S(1)}, u32[]{:S(2)}, u32[]{:S(2)}) collective-permute-start(f32[7,32,128]{2,1,0:T(8,128)S(1)} %get-tuple-element.107), channel_id=1, source_target_pairs={{0,1},{1,2},{2,3},{3,4},{4,5},{5,6},{6,7},{7,8},{8,9},{9,10},{10,1... | collective-permute-start | bytes 344072 | tf_op jit(solution)/shard_map/ppermute | solution.py:18
  12.1 1.9 %collective-permute-start.1 = (f32[7,32,128]{2,1,0:T(8,128)S(1)}, f32[7,32,128]{2,1,0:T(8,128)S(1)}, u32[]{:S(2)}, u32[]{:S(2)}) collective-permute-start(f32[7,32,128]{2,1,0:T(8,128)S(1)} %get-tuple-element.108), channel_id=1, source_target_pairs={{1,0},{2,1},{3,2},{4,3},{5,4},{6,5},{7,6},{8,7},{9,8},{10,9},{11,1... | collective-permute-start | bytes 344072 | tf_op jit(solution)/shard_map/ppermute | solution.py:19
  14.0 3.6 %collective-permute-start.4 = (f32[1,7,32,128]{3,2,1,0:T(8,128)S(1)}, f32[1,7,32,128]{3,2,1,0:T(8,128)S(1)}, u32[]{:S(2)}, u32[]{:S(2)}) collective-permute-start(f32[1,7,32,128]{3,2,1,0:T(8,128)S(1)} %get-tuple-element.106), channel_id=1, source_target_pairs={{0,1},{1,2},{2,3},{3,4},{4,5},{5,6},{6,7},{7,8},{8,9},{9,10},{10,1... | collective-permute-start | bytes 344072 | tf_op jit(solution)/shard_map/ppermute | solution.py:18
  17.8 0.6 fusion.625
  21.6 0.7 and_reduce_fusion
  22.3 1.9 %collective-permute-start.5 = (f32[1,7,32,128]{3,2,1,0:T(8,128)S(1)}, f32[1,7,32,128]{3,2,1,0:T(8,128)S(1)}, u32[]{:S(2)}, u32[]{:S(2)}) collective-permute-start(f32[1,7,32,128]{3,2,1,0:T(8,128)S(1)} %get-tuple-element.105), channel_id=1, source_target_pairs={{1,0},{2,1},{3,2},{4,3},{5,4},{6,5},{7,6},{8,7},{9,8},{10,9},{11,1... | collective-permute-start | bytes 344072 | tf_op jit(solution)/shard_map/ppermute | solution.py:19
  24.2 0.5 fusion.359
  24.8 3.6 %collective-permute-done.5 = f32[1,7,32,128]{3,2,1,0:T(8,128)S(1)} collective-permute-done((f32[1,7,32,128]{3,2,1,0:T(8,128)S(1)}, f32[1,7,32,128]{3,2,1,0:T(8,128)S(1)}, u32[]{:S(2)}, u32[]{:S(2)}) %collective-permute-start.5) | collective-permute-done | bytes 114720 | tf_op jit(solution)/shard_map/ppermute | solution.py:19
  28.4 0.1 fusion.133
  28.7 0.8 copy-done.6
  29.4 0.3 fusion.594
  29.8 0.6 fusion.626
  32.3 0.1 scatter-add.14
  32.5 0.3 fusion.203
  32.8 2.0 %collective-permute-start.6 = (f32[1,7,32,128]{3,2,1,0:T(8,128)S(1)}, f32[1,7,32,128]{3,2,1,0:T(8,128)S(1)}, u32[]{:S(2)}, u32[]{:S(2)}) collective-permute-start(f32[1,7,32,128]{3,2,1,0:T(8,128)S(1)} %get-tuple-element.103), channel_id=1, source_target_pairs={{0,1},{1,2},{2,3},{3,4},{4,5},{5,6},{6,7},{7,8},{8,9},{9,10},{10,1... | collective-permute-start | bytes 344072 | tf_op jit(solution)/shard_map/ppermute | solution.py:18
  34.7 2.4 %collective-permute-start.7 = (f32[1,7,32,128]{3,2,1,0:T(8,128)S(1)}, f32[1,7,32,128]{3,2,1,0:T(8,128)S(1)}, u32[]{:S(2)}, u32[]{:S(2)}) collective-permute-start(f32[1,7,32,128]{3,2,1,0:T(8,128)S(1)} %get-tuple-element.104), channel_id=1, source_target_pairs={{1,0},{2,1},{3,2},{4,3},{5,4},{6,5},{7,6},{8,7},{9,8},{10,9},{11,1... | collective-permute-start | bytes 344072 | tf_op jit(solution)/shard_map/ppermute | solution.py:19
  37.1 1.6 %fusion.22 = f32[2048]{0:T(1024)S(1)} fusion(f32[256,128]{1,0:T(8,128)S(1)} %bitcast.148, s32[2048]{0:T(1024)S(1)} %bitcast.181, s32[2048]{0:T(1024)S(1)} %bitcast.173), kind=kOutput, calls=%fused_computation.17 | convolution fusion | flops 806615040 | bytes 155648 | tf_op jit(solution)/shard_map/srk,skz->srz/dot_general | solution.py:110
  38.7 4.7 %collective-permute-done.7 = f32[1,7,32,128]{3,2,1,0:T(8,128)S(1)} collective-permute-done((f32[1,7,32,128]{3,2,1,0:T(8,128)S(1)}, f32[1,7,32,128]{3,2,1,0:T(8,128)S(1)}, u32[]{:S(2)}, u32[]{:S(2)}) %collective-permute-start.7) | collective-permute-done | bytes 114720 | tf_op jit(solution)/shard_map/ppermute | solution.py:19
  43.5 0.3 fusion.595
  43.8 0.6 fusion.627
  46.5 0.3 fusion.228
  46.9 1.9 %collective-permute-start.8 = (f32[1,7,32,128]{3,2,1,0:T(8,128)S(1)}, f32[1,7,32,128]{3,2,1,0:T(8,128)S(1)}, u32[]{:S(2)}, u32[]{:S(2)}) collective-permute-start(f32[1,7,32,128]{3,2,1,0:T(8,128)S(1)} %get-tuple-element.101), channel_id=1, source_target_pairs={{0,1},{1,2},{2,3},{3,4},{4,5},{5,6},{6,7},{7,8},{8,9},{9,10},{10,1... | collective-permute-start | bytes 344072 | tf_op jit(solution)/shard_map/ppermute | solution.py:18
  48.8 2.4 %collective-permute-start.9 = (f32[1,7,32,128]{3,2,1,0:T(8,128)S(1)}, f32[1,7,32,128]{3,2,1,0:T(8,128)S(1)}, u32[]{:S(2)}, u32[]{:S(2)}) collective-permute-start(f32[1,7,32,128]{3,2,1,0:T(8,128)S(1)} %get-tuple-element.102), channel_id=1, source_target_pairs={{1,0},{2,1},{3,2},{4,3},{5,4},{6,5},{7,6},{8,7},{9,8},{10,9},{11,1... | collective-permute-start | bytes 344072 | tf_op jit(solution)/shard_map/ppermute | solution.py:19
  51.2 1.6 %fusion.19 = f32[2048]{0:T(1024)S(1)} fusion(f32[256,128]{1,0:T(8,128)S(1)} %bitcast.157, s32[2048]{0:T(1024)S(1)} %bitcast.182, s32[2048]{0:T(1024)S(1)} %bitcast.174), kind=kOutput, calls=%fused_computation.16 | convolution fusion | flops 806615040 | bytes 155648 | tf_op jit(solution)/shard_map/srk,skz->srz/dot_general | solution.py:110
  52.8 3.0 %collective-permute-done.9 = f32[1,7,32,128]{3,2,1,0:T(8,128)S(1)} collective-permute-done((f32[1,7,32,128]{3,2,1,0:T(8,128)S(1)}, f32[1,7,32,128]{3,2,1,0:T(8,128)S(1)}, u32[]{:S(2)}, u32[]{:S(2)}) %collective-permute-start.9) | collective-permute-done | bytes 114720 | tf_op jit(solution)/shard_map/ppermute | solution.py:19
  55.9 0.3 fusion.596
  56.2 0.6 fusion.628
  58.8 0.1 scatter-add.16
  59.0 0.3 fusion.253
  59.3 1.9 %collective-permute-start.10 = (f32[1,7,32,128]{3,2,1,0:T(8,128)S(1)}, f32[1,7,32,128]{3,2,1,0:T(8,128)S(1)}, u32[]{:S(2)}, u32[]{:S(2)}) collective-permute-start(f32[1,7,32,128]{3,2,1,0:T(8,128)S(1)} %get-tuple-element.99), channel_id=1, source_target_pairs={{0,1},{1,2},{2,3},{3,4},{4,5},{5,6},{6,7},{7,8},{8,9},{9,10},{10,1... | collective-permute-start | bytes 344072 | tf_op jit(solution)/shard_map/ppermute | solution.py:18
  61.2 2.4 %collective-permute-start.11 = (f32[1,7,32,128]{3,2,1,0:T(8,128)S(1)}, f32[1,7,32,128]{3,2,1,0:T(8,128)S(1)}, u32[]{:S(2)}, u32[]{:S(2)}) collective-permute-start(f32[1,7,32,128]{3,2,1,0:T(8,128)S(1)} %get-tuple-element.100), channel_id=1, source_target_pairs={{1,0},{2,1},{3,2},{4,3},{5,4},{6,5},{7,6},{8,7},{9,8},{10,9},{11,1... | collective-permute-start | bytes 344072 | tf_op jit(solution)/shard_map/ppermute | solution.py:19
  63.6 1.6 %fusion.16 = f32[2048]{0:T(1024)S(1)} fusion(f32[256,128]{1,0:T(8,128)S(1)} %bitcast.166, s32[2048]{0:T(1024)S(1)} %bitcast.183, s32[2048]{0:T(1024)S(1)} %bitcast.175), kind=kOutput, calls=%fused_computation.15 | convolution fusion | flops 806615040 | bytes 155648 | tf_op jit(solution)/shard_map/srk,skz->srz/dot_general | solution.py:110
  65.2 3.0 %collective-permute-done.11 = f32[1,7,32,128]{3,2,1,0:T(8,128)S(1)} collective-permute-done((f32[1,7,32,128]{3,2,1,0:T(8,128)S(1)}, f32[1,7,32,128]{3,2,1,0:T(8,128)S(1)}, u32[]{:S(2)}, u32[]{:S(2)}) %collective-permute-start.11) | collective-permute-done | bytes 114720 | tf_op jit(solution)/shard_map/ppermute | solution.py:19
  68.3 0.3 fusion.597
  68.7 0.6 fusion.629
  71.3 1.6 %fusion.13 = f32[2048]{0:T(1024)S(1)} fusion(f32[256,128]{1,0:T(8,128)S(1)} %bitcast.172, s32[2048]{0:T(1024)S(1)} %bitcast.184, s32[2048]{0:T(1024)S(1)} %bitcast.176), kind=kOutput, calls=%fused_computation.14 | convolution fusion | flops 806615040 | bytes 155648 | tf_op jit(solution)/shard_map/srk,skz->srz/dot_general | solution.py:110
  73.0 0.7 multiply_reduce_fusion.2
  73.6 1.3 %bitcast_multiply_fusion.3 = (f32[1,8,32,128]{3,2,1,0:T(8,128)S(1)}, f32[1,8,32,128]{3,2,1,0:T(8,128)S(1)}) fusion(f32[8,32,128]{2,1,0:T(8,128)S(1)} %get-tuple-element.63, f32[2048]{0:T(1024)S(1)} %bitcast.195, s32[2048]{0:T(1024)S(1)} %bitcast.177, s32[8,32]{1,0:T(8,128)S(1)} %multiply_add_fusion, s32[2048]{0:T(1024)S(1)} %bitcast.185, ...), kind=kOutput, calls=%fused_computation.872 | convolution fusion | flops 807665664 | bytes 1991680 | tf_op jit(solution)/shard_map/srk,srz->skz/dot_general | solution.py:117
  75.0 1.9 %collective-permute-start.12 = (f32[1,7,32,128]{3,2,1,0:T(8,128)S(1)}, f32[1,7,32,128]{3,2,1,0:T(8,128)S(1)}, u32[]{:S(2)}, u32[]{:S(2)}) collective-permute-start(f32[1,7,32,128]{3,2,1,0:T(8,128)S(1)} %get-tuple-element.94), channel_id=1, source_target_pairs={{0,1},{1,2},{2,3},{3,4},{4,5},{5,6},{6,7},{7,8},{8,9},{9,10},{10,1... | collective-permute-start | bytes 344072 | tf_op jit(solution)/shard_map/ppermute | solution.py:18
  76.9 2.6 %collective-permute-start.13 = (f32[1,7,32,128]{3,2,1,0:T(8,128)S(1)}, f32[1,7,32,128]{3,2,1,0:T(8,128)S(1)}, u32[]{:S(2)}, u32[]{:S(2)}) collective-permute-start(f32[1,7,32,128]{3,2,1,0:T(8,128)S(1)} %get-tuple-element.95), channel_id=1, source_target_pairs={{1,0},{2,1},{3,2},{4,3},{5,4},{6,5},{7,6},{8,7},{9,8},{10,9},{11,1... | collective-permute-start | bytes 344072 | tf_op jit(solution)/shard_map/ppermute | solution.py:19
  79.5 0.3 fusion.474
  82.3 1.0 collective-permute-start.18
  83.3 0.3 collective-permute-done.18
  84.2 3.0 %collective-permute-start.19 = (f32[1]{0:T(128)}, f32[1]{0:T(128)}, u32[]{:S(2)}, u32[]{:S(2)}) collective-permute-start(f32[1]{0:T(128)} %add.839), channel_id=1, source_target_pairs={{0,2},{1,3},{2,0},{3,1},{4,6},{5,7},{6,4},{7,5},{8,10},{9,11},{10,... | collective-permute-start | bytes 20 | tf_op jit(solution)/shard_map/ppermute | solution.py:29
  87.2 0.2 collective-permute-done.19
  88.0 3.0 %collective-permute-start.20 = (f32[1]{0:T(128)}, f32[1]{0:T(128)}, u32[]{:S(2)}, u32[]{:S(2)}) collective-permute-start(f32[1]{0:T(128)} %add.840), channel_id=1, source_target_pairs={{0,4},{1,5},{2,6},{3,7},{4,0},{5,1},{6,2},{7,3},{8,12},{9,13},{10,... | collective-permute-start | bytes 20 | tf_op jit(solution)/shard_map/ppermute | solution.py:29
  91.0 0.2 collective-permute-done.20
  91.7 3.0 %collective-permute-start.21 = (f32[1]{0:T(128)}, f32[1]{0:T(128)}, u32[]{:S(2)}, u32[]{:S(2)}) collective-permute-start(f32[1]{0:T(128)} %add.841), channel_id=1, source_target_pairs={{0,8},{1,9},{2,10},{3,11},{4,12},{5,13},{6,14},{7,15},{8,0},{9,1},... | collective-permute-start | bytes 20 | tf_op jit(solution)/shard_map/ppermute | solution.py:29
  94.7 0.3 collective-permute-done.21
  95.8 1.3 %bitcast_multiply_fusion.2 = (f32[1,8,32,128]{3,2,1,0:T(8,128)S(1)}, f32[1,8,32,128]{3,2,1,0:T(8,128)S(1)}) fusion(f32[8,32,128]{2,1,0:T(8,128)S(1)} %get-tuple-element.63, f32[2048]{0:T(1024)S(1)} %bitcast.192, s32[2048]{0:T(1024)S(1)} %bitcast.178, s32[8,32]{1,0:T(8,128)S(1)} %multiply_add_fusion, s32[2048]{0:T(1024)S(1)} %bitcast.186, ...), kind=kOutput, calls=%fused_computation.871 | convolution fusion | flops 807665664 | bytes 1991680 | tf_op jit(solution)/shard_map/srk,srz->skz/dot_general | solution.py:117
  97.1 6.6 %collective-permute-start.14 = (f32[1,7,32,128]{3,2,1,0:T(8,128)S(1)}, f32[1,7,32,128]{3,2,1,0:T(8,128)S(1)}, u32[]{:S(2)}, u32[]{:S(2)}) collective-permute-start(f32[1,7,32,128]{3,2,1,0:T(8,128)S(1)} %get-tuple-element.92), channel_id=1, source_target_pairs={{0,1},{1,2},{2,3},{3,4},{4,5},{5,6},{6,7},{7,8},{8,9},{9,10},{10,1... | collective-permute-start | bytes 344072 | tf_op jit(solution)/shard_map/ppermute | solution.py:18
  103.7 1.9 %collective-permute-start.15 = (f32[1,7,32,128]{3,2,1,0:T(8,128)S(1)}, f32[1,7,32,128]{3,2,1,0:T(8,128)S(1)}, u32[]{:S(2)}, u32[]{:S(2)}) collective-permute-start(f32[1,7,32,128]{3,2,1,0:T(8,128)S(1)} %get-tuple-element.93), channel_id=1, source_target_pairs={{1,0},{2,1},{3,2},{4,3},{5,4},{6,5},{7,6},{8,7},{9,8},{10,9},{11,1... | collective-permute-start | bytes 344072 | tf_op jit(solution)/shard_map/ppermute | solution.py:19
  105.6 0.3 fusion.497
  106.0 3.9 %collective-permute-done.15 = f32[1,7,32,128]{3,2,1,0:T(8,128)S(1)} collective-permute-done((f32[1,7,32,128]{3,2,1,0:T(8,128)S(1)}, f32[1,7,32,128]{3,2,1,0:T(8,128)S(1)}, u32[]{:S(2)}, u32[]{:S(2)}) %collective-permute-start.15) | collective-permute-done | bytes 114720 | tf_op jit(solution)/shard_map/ppermute | solution.py:19
  110.0 1.3 %bitcast_multiply_fusion.1 = (f32[1,8,32,128]{3,2,1,0:T(8,128)S(1)}, f32[1,8,32,128]{3,2,1,0:T(8,128)S(1)}) fusion(f32[8,32,128]{2,1,0:T(8,128)S(1)} %get-tuple-element.63, f32[2048]{0:T(1024)S(1)} %bitcast.191, s32[2048]{0:T(1024)S(1)} %bitcast.179, s32[8,32]{1,0:T(8,128)S(1)} %multiply_add_fusion, s32[2048]{0:T(1024)S(1)} %bitcast.187, ...), kind=kOutput, calls=%fused_computation.870 | convolution fusion | flops 807665664 | bytes 1991680 | tf_op jit(solution)/shard_map/srk,srz->skz/dot_general | solution.py:117
  111.3 1.9 %collective-permute-start.16 = (f32[1,7,32,128]{3,2,1,0:T(8,128)S(1)}, f32[1,7,32,128]{3,2,1,0:T(8,128)S(1)}, u32[]{:S(2)}, u32[]{:S(2)}) collective-permute-start(f32[1,7,32,128]{3,2,1,0:T(8,128)S(1)} %get-tuple-element.90), channel_id=1, source_target_pairs={{0,1},{1,2},{2,3},{3,4},{4,5},{5,6},{6,7},{7,8},{8,9},{9,10},{10,1... | collective-permute-start | bytes 344072 | tf_op jit(solution)/shard_map/ppermute | solution.py:18
  113.3 2.4 %collective-permute-start.17 = (f32[1,7,32,128]{3,2,1,0:T(8,128)S(1)}, f32[1,7,32,128]{3,2,1,0:T(8,128)S(1)}, u32[]{:S(2)}, u32[]{:S(2)}) collective-permute-start(f32[1,7,32,128]{3,2,1,0:T(8,128)S(1)} %get-tuple-element.91), channel_id=1, source_target_pairs={{1,0},{2,1},{3,2},{4,3},{5,4},{6,5},{7,6},{8,7},{9,8},{10,9},{11,1... | collective-permute-start | bytes 344072 | tf_op jit(solution)/shard_map/ppermute | solution.py:19
  115.7 0.3 fusion.520
  116.0 5.0 %collective-permute-done.17 = f32[1,7,32,128]{3,2,1,0:T(8,128)S(1)} collective-permute-done((f32[1,7,32,128]{3,2,1,0:T(8,128)S(1)}, f32[1,7,32,128]{3,2,1,0:T(8,128)S(1)}, u32[]{:S(2)}, u32[]{:S(2)}) %collective-permute-start.17) | collective-permute-done | bytes 114720 | tf_op jit(solution)/shard_map/ppermute | solution.py:19
  121.1 1.3 %fusion.37 = f32[1,8,32,128]{3,2,1,0:T(8,128)S(1)} fusion(s32[8,32]{1,0:T(8,128)S(1)} %multiply_add_fusion, s32[2048]{0:T(1024)S(1)} %bitcast.188, f32[2048]{0:T(1024)S(1)} %bitcast.189, s32[2048]{0:T(1024)S(1)} %bitcast.180, f32[1,8,32,128]{3,2,1,0:T(8,128)S(1)} %get-tuple-element.132, f32[1,8,32,128]{3,2,1,0:T(8,128)S(1)} %get-tuple-element.75, ...), kind=kOutput, calls=%fused_computation.22 | convolution fusion | flops 807632896 | bytes 1729536 | tf_op jit(solution)/shard_map/srk,srz->skz/dot_general | solution.py:117
  122.5 0.8 bitcast_multiply_fusion
  (63 shorter events, 1.5 us)
Async XLA Ops:
  1.7 6.7 %copy-start = (f32[8,32,128]{2,1,0:T(8,128)S(1)}, f32[8,32,128]{2,1,0:T(8,128)}, u32[]{:S(2)}) copy-start(f32[8,32,128]{2,1,0:T(8,128)} %param.19) | copy-start | bytes 393220
  1.7 12.3 %copy-start.1 = (f32[1,8,32,128]{3,2,1,0:T(8,128)S(1)}, f32[1,8,32,128]{3,2,1,0:T(8,128)}, u32[]{:S(2)}) copy-start(f32[1,8,32,128]{3,2,1,0:T(8,128)} %param.21) | copy-start | bytes 393220
  1.7 23.0 %collective-permute-start.2 = (f32[1,7,32,128]{3,2,1,0:T(8,128)S(1)}, f32[1,7,32,128]{3,2,1,0:T(8,128)S(1)}, u32[]{:S(2)}, u32[]{:S(2)}) collective-permute-start(f32[1,7,32,128]{3,2,1,0:T(8,128)S(1)} %get-tuple-element.109), channel_id=1, source_target_pairs={{0,1},{1,2},{2,3},{3,4},{4,5},{5,6},{6,7},{7,8},{8,9},{9,10},{10,1... | collective-permute-start | bytes 344072 | tf_op jit(solution)/shard_map/ppermute | solution.py:18
  6.4 11.3 %copy-start.7 = (s32[1,2048]{1,0:T(1,128)S(1)}, s32[1,2048]{1,0:T(1,128)}, u32[]{:S(2)}) copy-start(s32[1,2048]{1,0:T(1,128)} %param.26) | copy-start | bytes 24580
  6.4 18.3 %collective-permute-start.3 = (f32[1,7,32,128]{3,2,1,0:T(8,128)S(1)}, f32[1,7,32,128]{3,2,1,0:T(8,128)S(1)}, u32[]{:S(2)}, u32[]{:S(2)}) collective-permute-start(f32[1,7,32,128]{3,2,1,0:T(8,128)S(1)} %get-tuple-element.110), channel_id=1, source_target_pairs={{1,0},{2,1},{3,2},{4,3},{5,4},{6,5},{7,6},{8,7},{9,8},{10,9},{11,1... | collective-permute-start | bytes 344072 | tf_op jit(solution)/shard_map/ppermute | solution.py:19
  8.4 9.4 %copy-start.9 = (f32[1,4]{1,0:T(1,128)S(1)}, f32[1,4]{1,0:T(1,128)}, u32[]{:S(2)}) copy-start(f32[1,4]{1,0:T(1,128)} %param.25) | copy-start | bytes 52
  8.4 20.0 %collective-permute-start = (f32[7,32,128]{2,1,0:T(8,128)S(1)}, f32[7,32,128]{2,1,0:T(8,128)S(1)}, u32[]{:S(2)}, u32[]{:S(2)}) collective-permute-start(f32[7,32,128]{2,1,0:T(8,128)S(1)} %get-tuple-element.107), channel_id=1, source_target_pairs={{0,1},{1,2},{2,3},{3,4},{4,5},{5,6},{6,7},{7,8},{8,9},{9,10},{10,1... | collective-permute-start | bytes 344072 | tf_op jit(solution)/shard_map/ppermute | solution.py:18
  12.1 16.3 %collective-permute-start.1 = (f32[7,32,128]{2,1,0:T(8,128)S(1)}, f32[7,32,128]{2,1,0:T(8,128)S(1)}, u32[]{:S(2)}, u32[]{:S(2)}) collective-permute-start(f32[7,32,128]{2,1,0:T(8,128)S(1)} %get-tuple-element.108), channel_id=1, source_target_pairs={{1,0},{2,1},{3,2},{4,3},{5,4},{6,5},{7,6},{8,7},{9,8},{10,9},{11,1... | collective-permute-start | bytes 344072 | tf_op jit(solution)/shard_map/ppermute | solution.py:19
  14.0 8.3 %collective-permute-start.4 = (f32[1,7,32,128]{3,2,1,0:T(8,128)S(1)}, f32[1,7,32,128]{3,2,1,0:T(8,128)S(1)}, u32[]{:S(2)}, u32[]{:S(2)}) collective-permute-start(f32[1,7,32,128]{3,2,1,0:T(8,128)S(1)} %get-tuple-element.106), channel_id=1, source_target_pairs={{0,1},{1,2},{2,3},{3,4},{4,5},{5,6},{6,7},{7,8},{8,9},{9,10},{10,1... | collective-permute-start | bytes 344072 | tf_op jit(solution)/shard_map/ppermute | solution.py:18
  22.3 6.1 %collective-permute-start.5 = (f32[1,7,32,128]{3,2,1,0:T(8,128)S(1)}, f32[1,7,32,128]{3,2,1,0:T(8,128)S(1)}, u32[]{:S(2)}, u32[]{:S(2)}) collective-permute-start(f32[1,7,32,128]{3,2,1,0:T(8,128)S(1)} %get-tuple-element.105), channel_id=1, source_target_pairs={{1,0},{2,1},{3,2},{4,3},{5,4},{6,5},{7,6},{8,7},{9,8},{10,9},{11,1... | collective-permute-start | bytes 344072 | tf_op jit(solution)/shard_map/ppermute | solution.py:19
  28.5 0.9 copy-start.6
  32.8 6.0 %collective-permute-start.6 = (f32[1,7,32,128]{3,2,1,0:T(8,128)S(1)}, f32[1,7,32,128]{3,2,1,0:T(8,128)S(1)}, u32[]{:S(2)}, u32[]{:S(2)}) collective-permute-start(f32[1,7,32,128]{3,2,1,0:T(8,128)S(1)} %get-tuple-element.103), channel_id=1, source_target_pairs={{0,1},{1,2},{2,3},{3,4},{4,5},{5,6},{6,7},{7,8},{8,9},{9,10},{10,1... | collective-permute-start | bytes 344072 | tf_op jit(solution)/shard_map/ppermute | solution.py:18
  34.7 8.7 %collective-permute-start.7 = (f32[1,7,32,128]{3,2,1,0:T(8,128)S(1)}, f32[1,7,32,128]{3,2,1,0:T(8,128)S(1)}, u32[]{:S(2)}, u32[]{:S(2)}) collective-permute-start(f32[1,7,32,128]{3,2,1,0:T(8,128)S(1)} %get-tuple-element.104), channel_id=1, source_target_pairs={{1,0},{2,1},{3,2},{4,3},{5,4},{6,5},{7,6},{8,7},{9,8},{10,9},{11,1... | collective-permute-start | bytes 344072 | tf_op jit(solution)/shard_map/ppermute | solution.py:19
  46.9 6.0 %collective-permute-start.8 = (f32[1,7,32,128]{3,2,1,0:T(8,128)S(1)}, f32[1,7,32,128]{3,2,1,0:T(8,128)S(1)}, u32[]{:S(2)}, u32[]{:S(2)}) collective-permute-start(f32[1,7,32,128]{3,2,1,0:T(8,128)S(1)} %get-tuple-element.101), channel_id=1, source_target_pairs={{0,1},{1,2},{2,3},{3,4},{4,5},{5,6},{6,7},{7,8},{8,9},{9,10},{10,1... | collective-permute-start | bytes 344072 | tf_op jit(solution)/shard_map/ppermute | solution.py:18
  48.8 7.0 %collective-permute-start.9 = (f32[1,7,32,128]{3,2,1,0:T(8,128)S(1)}, f32[1,7,32,128]{3,2,1,0:T(8,128)S(1)}, u32[]{:S(2)}, u32[]{:S(2)}) collective-permute-start(f32[1,7,32,128]{3,2,1,0:T(8,128)S(1)} %get-tuple-element.102), channel_id=1, source_target_pairs={{1,0},{2,1},{3,2},{4,3},{5,4},{6,5},{7,6},{8,7},{9,8},{10,9},{11,1... | collective-permute-start | bytes 344072 | tf_op jit(solution)/shard_map/ppermute | solution.py:19
  59.3 6.0 %collective-permute-start.10 = (f32[1,7,32,128]{3,2,1,0:T(8,128)S(1)}, f32[1,7,32,128]{3,2,1,0:T(8,128)S(1)}, u32[]{:S(2)}, u32[]{:S(2)}) collective-permute-start(f32[1,7,32,128]{3,2,1,0:T(8,128)S(1)} %get-tuple-element.99), channel_id=1, source_target_pairs={{0,1},{1,2},{2,3},{3,4},{4,5},{5,6},{6,7},{7,8},{8,9},{9,10},{10,1... | collective-permute-start | bytes 344072 | tf_op jit(solution)/shard_map/ppermute | solution.py:18
  61.2 7.0 %collective-permute-start.11 = (f32[1,7,32,128]{3,2,1,0:T(8,128)S(1)}, f32[1,7,32,128]{3,2,1,0:T(8,128)S(1)}, u32[]{:S(2)}, u32[]{:S(2)}) collective-permute-start(f32[1,7,32,128]{3,2,1,0:T(8,128)S(1)} %get-tuple-element.100), channel_id=1, source_target_pairs={{1,0},{2,1},{3,2},{4,3},{5,4},{6,5},{7,6},{8,7},{9,8},{10,9},{11,1... | collective-permute-start | bytes 344072 | tf_op jit(solution)/shard_map/ppermute | solution.py:19
  71.3 1.6 %copy-start.8 = (f32[1,4,2048]{2,1,0:T(4,128)S(1)}, f32[1,4,2048]{2,1,0:T(4,128)}, u32[]{:S(2)}) copy-start(f32[1,4,2048]{2,1,0:T(4,128)} %param.27) | copy-start | bytes 98308
  71.3 2.3 %copy-start.3 = (f32[1,8,32,128]{3,2,1,0:T(8,128)S(1)}, f32[1,8,32,128]{3,2,1,0:T(8,128)}, u32[]{:S(2)}) copy-start(f32[1,8,32,128]{3,2,1,0:T(8,128)} %param.22) | copy-start | bytes 393220
  71.3 2.3 %copy-start.10 = (f32[1,8,32,128]{3,2,1,0:T(8,128)S(1)}, f32[1,8,32,128]{3,2,1,0:T(8,128)}, u32[]{:S(2)}) copy-start(f32[1,8,32,128]{3,2,1,0:T(8,128)} %param.23) | copy-start | bytes 393220
  75.0 20.7 %collective-permute-start.12 = (f32[1,7,32,128]{3,2,1,0:T(8,128)S(1)}, f32[1,7,32,128]{3,2,1,0:T(8,128)S(1)}, u32[]{:S(2)}, u32[]{:S(2)}) collective-permute-start(f32[1,7,32,128]{3,2,1,0:T(8,128)S(1)} %get-tuple-element.94), channel_id=1, source_target_pairs={{0,1},{1,2},{2,3},{3,4},{4,5},{5,6},{6,7},{7,8},{8,9},{9,10},{10,1... | collective-permute-start | bytes 344072 | tf_op jit(solution)/shard_map/ppermute | solution.py:18
  76.9 18.7 %collective-permute-start.13 = (f32[1,7,32,128]{3,2,1,0:T(8,128)S(1)}, f32[1,7,32,128]{3,2,1,0:T(8,128)S(1)}, u32[]{:S(2)}, u32[]{:S(2)}) collective-permute-start(f32[1,7,32,128]{3,2,1,0:T(8,128)S(1)} %get-tuple-element.95), channel_id=1, source_target_pairs={{1,0},{2,1},{3,2},{4,3},{5,4},{6,5},{7,6},{8,7},{9,8},{10,9},{11,1... | collective-permute-start | bytes 344072 | tf_op jit(solution)/shard_map/ppermute | solution.py:19
  82.3 1.3 %collective-permute-start.18 = (f32[1]{0:T(128)}, f32[1]{0:T(128)}, u32[]{:S(2)}, u32[]{:S(2)}) collective-permute-start(f32[1]{0:T(128)} %bitcast.49), channel_id=1, source_target_pairs={{0,1},{1,0},{2,3},{3,2},{4,5},{5,4},{6,7},{7,6},{8,9},{9,8},{10,11... | collective-permute-start | bytes 20 | tf_op jit(solution)/shard_map/ppermute | solution.py:29
  84.2 3.2 %collective-permute-start.19 = (f32[1]{0:T(128)}, f32[1]{0:T(128)}, u32[]{:S(2)}, u32[]{:S(2)}) collective-permute-start(f32[1]{0:T(128)} %add.839), channel_id=1, source_target_pairs={{0,2},{1,3},{2,0},{3,1},{4,6},{5,7},{6,4},{7,5},{8,10},{9,11},{10,... | collective-permute-start | bytes 20 | tf_op jit(solution)/shard_map/ppermute | solution.py:29
  88.0 3.2 %collective-permute-start.20 = (f32[1]{0:T(128)}, f32[1]{0:T(128)}, u32[]{:S(2)}, u32[]{:S(2)}) collective-permute-start(f32[1]{0:T(128)} %add.840), channel_id=1, source_target_pairs={{0,4},{1,5},{2,6},{3,7},{4,0},{5,1},{6,2},{7,3},{8,12},{9,13},{10,... | collective-permute-start | bytes 20 | tf_op jit(solution)/shard_map/ppermute | solution.py:29
  91.7 3.3 %collective-permute-start.21 = (f32[1]{0:T(128)}, f32[1]{0:T(128)}, u32[]{:S(2)}, u32[]{:S(2)}) collective-permute-start(f32[1]{0:T(128)} %add.841), channel_id=1, source_target_pairs={{0,8},{1,9},{2,10},{3,11},{4,12},{5,13},{6,14},{7,15},{8,0},{9,1},... | collective-permute-start | bytes 20 | tf_op jit(solution)/shard_map/ppermute | solution.py:29
  97.1 8.8 %collective-permute-start.14 = (f32[1,7,32,128]{3,2,1,0:T(8,128)S(1)}, f32[1,7,32,128]{3,2,1,0:T(8,128)S(1)}, u32[]{:S(2)}, u32[]{:S(2)}) collective-permute-start(f32[1,7,32,128]{3,2,1,0:T(8,128)S(1)} %get-tuple-element.92), channel_id=1, source_target_pairs={{0,1},{1,2},{2,3},{3,4},{4,5},{5,6},{6,7},{7,8},{8,9},{9,10},{10,1... | collective-permute-start | bytes 344072 | tf_op jit(solution)/shard_map/ppermute | solution.py:18
  103.7 6.1 %collective-permute-start.15 = (f32[1,7,32,128]{3,2,1,0:T(8,128)S(1)}, f32[1,7,32,128]{3,2,1,0:T(8,128)S(1)}, u32[]{:S(2)}, u32[]{:S(2)}) collective-permute-start(f32[1,7,32,128]{3,2,1,0:T(8,128)S(1)} %get-tuple-element.93), channel_id=1, source_target_pairs={{1,0},{2,1},{3,2},{4,3},{5,4},{6,5},{7,6},{8,7},{9,8},{10,9},{11,1... | collective-permute-start | bytes 344072 | tf_op jit(solution)/shard_map/ppermute | solution.py:19
  111.3 11.2 %copy-start.4 = (f32[1,8,32,128]{3,2,1,0:T(8,128)}, f32[1,8,32,128]{3,2,1,0:T(8,128)S(1)}, u32[]{:S(2)}) copy-start(f32[1,8,32,128]{3,2,1,0:T(8,128)S(1)} %get-tuple-element.134) | copy-start | bytes 393220
  111.3 4.7 %collective-permute-start.16 = (f32[1,7,32,128]{3,2,1,0:T(8,128)S(1)}, f32[1,7,32,128]{3,2,1,0:T(8,128)S(1)}, u32[]{:S(2)}, u32[]{:S(2)}) collective-permute-start(f32[1,7,32,128]{3,2,1,0:T(8,128)S(1)} %get-tuple-element.90), channel_id=1, source_target_pairs={{0,1},{1,2},{2,3},{3,4},{4,5},{5,6},{6,7},{7,8},{8,9},{9,10},{10,1... | collective-permute-start | bytes 344072 | tf_op jit(solution)/shard_map/ppermute | solution.py:18
  113.3 7.7 %collective-permute-start.17 = (f32[1,7,32,128]{3,2,1,0:T(8,128)S(1)}, f32[1,7,32,128]{3,2,1,0:T(8,128)S(1)}, u32[]{:S(2)}, u32[]{:S(2)}) collective-permute-start(f32[1,7,32,128]{3,2,1,0:T(8,128)S(1)} %get-tuple-element.91), channel_id=1, source_target_pairs={{1,0},{2,1},{3,2},{4,3},{5,4},{6,5},{7,6},{8,7},{9,8},{10,9},{11,1... | collective-permute-start | bytes 344072 | tf_op jit(solution)/shard_map/ppermute | solution.py:19
  121.1 1.4 %copy-start.2 = (f32[8,32,128]{2,1,0:T(8,128)S(1)}, f32[8,32,128]{2,1,0:T(8,128)}, u32[]{:S(2)}) copy-start(f32[8,32,128]{2,1,0:T(8,128)} %param.18) | copy-start | bytes 393220
  122.4 0.8 copy-start.5

commit v3 on v1

--- a/solution.py
+++ b/solution.py
@@ -18,6 +18,22 @@
     before = lax.ppermute(last, "mp", up)
     after = lax.ppermute(first, "mp", down)
     return jnp.concatenate([before, array, after], axis=dim)
+
+
+def butterfly_distances(axis):
+    devices = lax.axis_size(axis)
+    assert devices & (devices - 1) == 0
+    far = []
+    distance = 2
+    while distance < devices:
+        far.append(distance)
+        distance *= 2
+    return far + [1] if devices > 1 else []
+
+
+def butterfly_round(values, axis, distance):
+    pairs = [(i, i ^ distance) for i in range(lax.axis_size(axis))]
+    return values + lax.ppermute(values, axis, pairs)
 
 
 def pad_axis(values, axis):
@@ -75,13 +91,19 @@
     cells = rows * cz
     kappa = velocity * velocity / buoyancy
     offset = lax.axis_index("mp") * cells
-    buoyancy_wide = extended(buoyancy, 0, HALO)
-    flux_buoyancy = buoyancy_wide[HALO - 4 : HALO + planes + 3]
+
+    def wide_operator(wide, values, flux_buoyancy):
+        flux = flux_buoyancy * forward_diff(wide, 1, planes + 7, start=HALO - 4)
+        return backward_diff(flux, 1, planes) + cross_terms(values, buoyancy)
+
+    adjoint_operand = kappa * adjoint_next
+    first = extended(jnp.concatenate([buoyancy[None], wave_now, adjoint_operand], axis=0), 1, HALO)
+    flux_buoyancy = first[0, HALO - 4 : HALO + planes + 3]
+    first_lap = wide_operator(first[1 : 1 + shots], wave_now, flux_buoyancy)
+    adjoint_lap = wide_operator(first[1 + shots :], adjoint_operand, flux_buoyancy)
 
     def operator(values):
-        wide = extended(values, 1, HALO)
-        flux = flux_buoyancy * forward_diff(wide, 1, planes + 7, start=HALO - 4)
-        return backward_diff(flux, 1, planes) + cross_terms(values, buoyancy)
+        return wide_operator(extended(values, 1, HALO), values, flux_buoyancy)
 
     source_local = source_cell - offset
     source_owned = (source_local >= 0) & (source_local < cells)
@@ -110,7 +132,7 @@
     laps = []
     resids = []
     for step in range(STEPS):
-        lap = operator(current)
+        lap = first_lap if step == 0 else operator(current)
         laps.append(lap)
         following = 2.0 * current - before + kappa * lap
         amount = jnp.where(source_owned, wavelet[:, step], 0.0)
@@ -119,15 +141,25 @@
         sampled = sample(following)
         resids.append(jnp.where(receiver_owned, sampled - observed[:, step, :], 0.0))
         before, current = (current, following)
-    local_misfit = 0.5 * sum((jnp.sum(item * item, axis=1) for item in resids))
-    misfit = jnp.sum(lax.all_gather(local_misfit, "mp"), axis=0)
+    misfit = 0.5 * sum((jnp.sum(item * item, axis=1) for item in resids))
+    distances = butterfly_distances("mp")
     mu_near, mu_far = (adjoint_next, adjoint_after)
     gradient = jnp.zeros(shape, jnp.float32)
     for level in range(STEPS, 0, -1):
-        state = 2.0 * mu_near + operator(kappa * mu_near) - mu_far
+        if level == STEPS:
+            lap = adjoint_lap
+        else:
+            if distances:
+                mu_near, misfit = lax.optimization_barrier((mu_near, misfit))
+                misfit = butterfly_round(misfit, "mp", distances.pop(0))
+            lap = operator(kappa * mu_near)
+        state = 2.0 * mu_near + lap - mu_far
         state = inject(state, resids[level - 1])
         gradient = gradient + state * laps[level - 1]
         mu_far, mu_near = (mu_near, state)
+        mu_near, misfit = lax.optimization_barrier((mu_near, misfit))
+    for distance in distances:
+        misfit = butterfly_round(misfit, "mp", distance)
     velocity_gradient = 2.0 * velocity / buoyancy * jnp.sum(gradient, axis=0)
     return (velocity_gradient, mu_near, mu_far, misfit)
 

time: 135 us -> 108 us (0.80)
  blocking collectives: 28.4 us -> 0 us
  waiting for transfers between devices: 19.7 us -> 10.7 us
  starting transfers between devices: 45 us -> 52.3 us
  between operations: 14.8 us -> 18.8 us
  local copies, waits for them, and re-layouts: 3.45 us -> 1.88 us
    unnamed x1 -> x0, blocking collectives: 28.4 us -> none
    ppermute x0 -> x4, starting transfers between devices: none -> 13.9 us  [butterfly_round(): return values + lax.ppermute(values, axis, pairs)]
    ppermute x9 -> x7, waiting for transfers between devices: 19.6 us -> 8.1 us  [extended(): after = lax.ppermute(first, 'mp', down)]
    ppermute x9 -> x7, starting transfers between devices: 21.5 us -> 15.5 us  [extended(): after = lax.ppermute(first, 'mp', down)]
    ppermute x9 -> x7, waiting for transfers between devices: 0.02 us -> 1.54 us  [extended(): before = lax.ppermute(last, 'mp', up)]
    unnamed x28 -> x22, local copies, waits for them, and re-layouts: 2.21 us -> 0.85 us
    ppermute x9 -> x7, starting transfers between devices: 23.5 us -> 22.9 us  [extended(): before = lax.ppermute(last, 'mp', up)]
  transfers between devices with their start and end apart: 18 -> 18, of which waited for: 6 -> 9; matrix products, arithmetic and copies ran while one was open for 7% -> 8% of each run, Pallas kernels for 0% -> 0%
where the time goes in v3:
time: 108 us; the launch traced here: 107 us
  starting transfers between devices  52.3 us (48%)
  between operations  18.8 us (17%)
  other arithmetic  11.8 us (11%)
  matrix products  11.6 us (11%)
  waiting for transfers between devices  10.7 us (10%)
  local copies, waits for them, and re-layouts  1.88 us (2%)
    ppermute x7, starting transfers between devices, extended(): before = lax.ppermute(last, 'mp', up)  22.9 us
    ppermute x7, starting transfers between devices, extended(): after = lax.ppermute(first, 'mp', down)  15.5 us
    ppermute x4, starting transfers between devices, butterfly_round(): return values + lax.ppermute(values, axis, pairs)  13.9 us
    ppermute x7, waiting for transfers between devices, extended(): after = lax.ppermute(first, 'mp', down)  8.1 us
    dot_general x4, matrix products, sample(): jnp.einsum('srk,skz->srz', row_pick, field.reshape(shots, rows, cz), prec...  6.43 us
    dot_general x4, matrix products, inject(): jnp.einsum('srk,srz->skz', row_pick, spread, precision=lax.Precision.HIGH...  5.21 us
    add x4, other arithmetic, local(): following.reshape(shots, cells).at[shot_rows, source_index].add(amount)  2.56 us
    mul x7, other arithmetic, cross_terms(): flux = buoyancy * forward_diff(pad_axis(values, axis), axis, length)  2.4 us
  transfers between devices with their start and end apart: 18, of which 9 were waited for; matrix products, arithmetic and copies ran while one was open for 8% of the time, Pallas kernels for 0%

profile of v3, /device:TPU:1, one launch (start us, length us, event | category | flops | bytes accessed | tf_op | source)
XLA Modules:
  0.0 107.1 jit_solution(13237355740902814871)
XLA Ops:
  0.6 1.1 bitcast_multiply_fusion.8
  1.7 1.0 pad_maximum_fusion.1
  2.9 2.0 %collective-permute-start.1 = (f32[3,7,32,128]{3,2,1,0:T(8,128)S(1)}, f32[3,7,32,128]{3,2,1,0:T(8,128)S(1)}, u32[]{:S(2)}, u32[]{:S(2)}) collective-permute-start(f32[3,7,32,128]{3,2,1,0:T(8,128)S(1)} %get-tuple-element.88), channel_id=1, source_target_pairs={{1,0},{2,1},{3,2},{4,3},{5,4},{6,5},{7,6},{8,7},{9,8},{10,9},{11,1... | collective-permute-start | bytes 1032200 | tf_op jit(solution)/shard_map/ppermute | solution.py:19
  4.8 4.5 %collective-permute-start = (f32[3,7,32,128]{3,2,1,0:T(8,128)S(1)}, f32[3,7,32,128]{3,2,1,0:T(8,128)S(1)}, u32[]{:S(2)}, u32[]{:S(2)}) collective-permute-start(f32[3,7,32,128]{3,2,1,0:T(8,128)S(1)} %get-tuple-element.89), channel_id=1, source_target_pairs={{0,1},{1,2},{2,3},{3,4},{4,5},{5,6},{6,7},{7,8},{8,9},{9,10},{10,1... | collective-permute-start | bytes 1032200 | tf_op jit(solution)/shard_map/ppermute | solution.py:18
  10.0 0.7 and_reduce_fusion
  10.7 0.7 fusion.622
  14.1 0.5 fusion.359
  14.7 1.5 %collective-permute-done = f32[3,7,32,128]{3,2,1,0:T(8,128)S(1)} collective-permute-done((f32[3,7,32,128]{3,2,1,0:T(8,128)S(1)}, f32[3,7,32,128]{3,2,1,0:T(8,128)S(1)}, u32[]{:S(2)}, u32[]{:S(2)}) %collective-permute-start) | collective-permute-done | bytes 344096 | tf_op jit(solution)/shard_map/ppermute | solution.py:18
  16.3 0.1 fusion.126
  16.4 0.8 copy-done.6
  17.2 0.3 fusion.594
  17.5 0.6 fusion.623
  20.0 0.3 fusion.203
  20.3 4.4 %collective-permute-start.2 = (f32[1,7,32,128]{3,2,1,0:T(8,128)S(1)}, f32[1,7,32,128]{3,2,1,0:T(8,128)S(1)}, u32[]{:S(2)}, u32[]{:S(2)}) collective-permute-start(f32[1,7,32,128]{3,2,1,0:T(8,128)S(1)} %get-tuple-element.118), channel_id=1, source_target_pairs={{0,1},{1,2},{2,3},{3,4},{4,5},{5,6},{6,7},{7,8},{8,9},{9,10},{10,1... | collective-permute-start | bytes 344072 | tf_op jit(solution)/shard_map/ppermute | solution.py:18
  24.7 1.9 %collective-permute-start.3 = (f32[1,7,32,128]{3,2,1,0:T(8,128)S(1)}, f32[1,7,32,128]{3,2,1,0:T(8,128)S(1)}, u32[]{:S(2)}, u32[]{:S(2)}) collective-permute-start(f32[1,7,32,128]{3,2,1,0:T(8,128)S(1)} %get-tuple-element.119), channel_id=1, source_target_pairs={{1,0},{2,1},{3,2},{4,3},{5,4},{6,5},{7,6},{8,7},{9,8},{10,9},{11,1... | collective-permute-start | bytes 344072 | tf_op jit(solution)/shard_map/ppermute | solution.py:19
  26.7 0.1 fusion.134
  26.8 1.6 %fusion.16 = f32[2048]{0:T(1024)S(1)} fusion(f32[256,128]{1,0:T(8,128)S(1)} %bitcast.143, s32[2048]{0:T(1024)S(1)} %bitcast.176, s32[2048]{0:T(1024)S(1)} %bitcast.168), kind=kOutput, calls=%fused_computation.15 | convolution fusion | flops 806615040 | bytes 155648 | tf_op jit(solution)/shard_map/srk,skz->srz/dot_general | solution.py:121
  28.4 2.4 %collective-permute-done.3 = f32[1,7,32,128]{3,2,1,0:T(8,128)S(1)} collective-permute-done((f32[1,7,32,128]{3,2,1,0:T(8,128)S(1)}, f32[1,7,32,128]{3,2,1,0:T(8,128)S(1)}, u32[]{:S(2)}, u32[]{:S(2)}) %collective-permute-start.3) | collective-permute-done | bytes 114720 | tf_op jit(solution)/shard_map/ppermute | solution.py:19
  30.9 0.1 fusion.119
  31.0 0.3 fusion.595
  31.3 0.7 fusion.624
  34.0 0.3 fusion.228
  34.3 1.9 %collective-permute-start.4 = (f32[1,7,32,128]{3,2,1,0:T(8,128)S(1)}, f32[1,7,32,128]{3,2,1,0:T(8,128)S(1)}, u32[]{:S(2)}, u32[]{:S(2)}) collective-permute-start(f32[1,7,32,128]{3,2,1,0:T(8,128)S(1)} %get-tuple-element.116), channel_id=1, source_target_pairs={{0,1},{1,2},{2,3},{3,4},{4,5},{5,6},{6,7},{7,8},{8,9},{9,10},{10,1... | collective-permute-start | bytes 344072 | tf_op jit(solution)/shard_map/ppermute | solution.py:18
  36.3 2.4 %collective-permute-start.5 = (f32[1,7,32,128]{3,2,1,0:T(8,128)S(1)}, f32[1,7,32,128]{3,2,1,0:T(8,128)S(1)}, u32[]{:S(2)}, u32[]{:S(2)}) collective-permute-start(f32[1,7,32,128]{3,2,1,0:T(8,128)S(1)} %get-tuple-element.117), channel_id=1, source_target_pairs={{1,0},{2,1},{3,2},{4,3},{5,4},{6,5},{7,6},{8,7},{9,8},{10,9},{11,1... | collective-permute-start | bytes 344072 | tf_op jit(solution)/shard_map/ppermute | solution.py:19
  38.7 1.6 %fusion.19 = f32[2048]{0:T(1024)S(1)} fusion(f32[256,128]{1,0:T(8,128)S(1)} %bitcast.152, s32[2048]{0:T(1024)S(1)} %bitcast.177, s32[2048]{0:T(1024)S(1)} %bitcast.169), kind=kOutput, calls=%fused_computation.16 | convolution fusion | flops 806615040 | bytes 155648 | tf_op jit(solution)/shard_map/srk,skz->srz/dot_general | solution.py:121
  40.3 2.1 %collective-permute-done.5 = f32[1,7,32,128]{3,2,1,0:T(8,128)S(1)} collective-permute-done((f32[1,7,32,128]{3,2,1,0:T(8,128)S(1)}, f32[1,7,32,128]{3,2,1,0:T(8,128)S(1)}, u32[]{:S(2)}, u32[]{:S(2)}) %collective-permute-start.5) | collective-permute-done | bytes 114720 | tf_op jit(solution)/shard_map/ppermute | solution.py:19
  42.4 0.1 fusion.112
  42.5 0.3 fusion.596
  42.8 0.6 fusion.625
  45.5 0.3 fusion.253
  45.8 1.9 %collective-permute-start.6 = (f32[1,7,32,128]{3,2,1,0:T(8,128)S(1)}, f32[1,7,32,128]{3,2,1,0:T(8,128)S(1)}, u32[]{:S(2)}, u32[]{:S(2)}) collective-permute-start(f32[1,7,32,128]{3,2,1,0:T(8,128)S(1)} %get-tuple-element.114), channel_id=1, source_target_pairs={{0,1},{1,2},{2,3},{3,4},{4,5},{5,6},{6,7},{7,8},{8,9},{9,10},{10,1... | collective-permute-start | bytes 344072 | tf_op jit(solution)/shard_map/ppermute | solution.py:18
  47.7 2.4 %collective-permute-start.7 = (f32[1,7,32,128]{3,2,1,0:T(8,128)S(1)}, f32[1,7,32,128]{3,2,1,0:T(8,128)S(1)}, u32[]{:S(2)}, u32[]{:S(2)}) collective-permute-start(f32[1,7,32,128]{3,2,1,0:T(8,128)S(1)} %get-tuple-element.115), channel_id=1, source_target_pairs={{1,0},{2,1},{3,2},{4,3},{5,4},{6,5},{7,6},{8,7},{9,8},{10,9},{11,1... | collective-permute-start | bytes 344072 | tf_op jit(solution)/shard_map/ppermute | solution.py:19
  50.1 1.6 %fusion.22 = f32[2048]{0:T(1024)S(1)} fusion(f32[256,128]{1,0:T(8,128)S(1)} %bitcast.161, s32[2048]{0:T(1024)S(1)} %bitcast.178, s32[2048]{0:T(1024)S(1)} %bitcast.170), kind=kOutput, calls=%fused_computation.17 | convolution fusion | flops 806615040 | bytes 155648 | tf_op jit(solution)/shard_map/srk,skz->srz/dot_general | solution.py:121
  51.7 2.9 %collective-permute-done.7 = f32[1,7,32,128]{3,2,1,0:T(8,128)S(1)} collective-permute-done((f32[1,7,32,128]{3,2,1,0:T(8,128)S(1)}, f32[1,7,32,128]{3,2,1,0:T(8,128)S(1)}, u32[]{:S(2)}, u32[]{:S(2)}) %collective-permute-start.7) | collective-permute-done | bytes 114720 | tf_op jit(solution)/shard_map/ppermute | solution.py:19
  54.7 0.1 fusion.105
  54.8 0.3 fusion.597
  55.2 0.7 fusion.626
  57.9 1.6 %fusion.13 = f32[2048]{0:T(1024)S(1)} fusion(f32[256,128]{1,0:T(8,128)S(1)} %bitcast.167, s32[2048]{0:T(1024)S(1)} %bitcast.179, s32[2048]{0:T(1024)S(1)} %bitcast.171), kind=kOutput, calls=%fused_computation.14 | convolution fusion | flops 806615040 | bytes 155648 | tf_op jit(solution)/shard_map/srk,skz->srz/dot_general | solution.py:121
  59.5 0.8 multiply_reduce_fusion.2
  62.9 1.3 %fusion.46 = f32[1,8,32,128]{3,2,1,0:T(8,128)S(1)} fusion(s32[8,32]{1,0:T(8,128)S(1)} %multiply_add_fusion, s32[2048]{0:T(1024)S(1)} %bitcast.180, f32[2048]{0:T(1024)S(1)} %bitcast.190, s32[2048]{0:T(1024)S(1)} %bitcast.172, f32[1,8,32,128]{3,2,1,0:T(8,128)S(1)} %copy-done.10, f32[1,8,32,128]{3,2,1,0:T(8,128)S(1)} %get-tuple-element.97, ...), kind=kOutput, calls=%fused_computation.25 | convolution fusion | flops 807632896 | bytes 1729536 | tf_op jit(solution)/shard_map/srk,srz->skz/dot_general | solution.py:128
  64.3 1.9 %collective-permute-start.8 = (f32[1,7,32,128]{3,2,1,0:T(8,128)S(1)}, f32[1,7,32,128]{3,2,1,0:T(8,128)S(1)}, u32[]{:S(2)}, u32[]{:S(2)}) collective-permute-start(f32[1,7,32,128]{3,2,1,0:T(8,128)S(1)} %get-tuple-element.110), channel_id=1, source_target_pairs={{0,1},{1,2},{2,3},{3,4},{4,5},{5,6},{6,7},{7,8},{8,9},{9,10},{10,1... | collective-permute-start | bytes 344072 | tf_op jit(solution)/shard_map/ppermute | solution.py:18
  66.2 2.4 %collective-permute-start.9 = (f32[1,7,32,128]{3,2,1,0:T(8,128)S(1)}, f32[1,7,32,128]{3,2,1,0:T(8,128)S(1)}, u32[]{:S(2)}, u32[]{:S(2)}) collective-permute-start(f32[1,7,32,128]{3,2,1,0:T(8,128)S(1)} %get-tuple-element.111), channel_id=1, source_target_pairs={{1,0},{2,1},{3,2},{4,3},{5,4},{6,5},{7,6},{8,7},{9,8},{10,9},{11,1... | collective-permute-start | bytes 344072 | tf_op jit(solution)/shard_map/ppermute | solution.py:19
  68.6 0.3 fusion.474
  68.9 3.0 %collective-permute-start.10 = (f32[1]{0:T(128)}, f32[1]{0:T(128)}, u32[]{:S(2)}, u32[]{:S(2)}) collective-permute-start(f32[1]{0:T(128)} %bitcast.38), channel_id=1, source_target_pairs={{0,2},{1,3},{2,0},{3,1},{4,6},{5,7},{6,4},{7,5},{8,10},{9,11},{10,... | collective-permute-start | bytes 20 | tf_op jit(solution)/shard_map/ppermute | solution.py:36
  72.0 0.3 collective-permute-done.10
  73.0 0.2 collective-permute-done.9
  73.2 0.1 fusion.98
  73.4 1.3 %fusion.43 = f32[1,8,32,128]{3,2,1,0:T(8,128)S(1)} fusion(s32[8,32]{1,0:T(8,128)S(1)} %multiply_add_fusion, s32[2048]{0:T(1024)S(1)} %bitcast.181, f32[2048]{0:T(1024)S(1)} %bitcast.188, s32[2048]{0:T(1024)S(1)} %bitcast.173, f32[1,8,32,128]{3,2,1,0:T(8,128)S(1)} %copy-done.4, f32[1,8,32,128]{3,2,1,0:T(8,128)S(1)} %get-tuple-element.95, ...), kind=kOutput, calls=%fused_computation.24 | convolution fusion | flops 807632896 | bytes 1729536 | tf_op jit(solution)/shard_map/srk,srz->skz/dot_general | solution.py:128
  74.7 4.0 %collective-permute-start.11 = (f32[1,7,32,128]{3,2,1,0:T(8,128)S(1)}, f32[1,7,32,128]{3,2,1,0:T(8,128)S(1)}, u32[]{:S(2)}, u32[]{:S(2)}) collective-permute-start(f32[1,7,32,128]{3,2,1,0:T(8,128)S(1)} %get-tuple-element.108), channel_id=1, source_target_pairs={{0,1},{1,2},{2,3},{3,4},{4,5},{5,6},{6,7},{7,8},{8,9},{9,10},{10,1... | collective-permute-start | bytes 344072 | tf_op jit(solution)/shard_map/ppermute | solution.py:18
  78.8 2.1 %collective-permute-start.12 = (f32[1,7,32,128]{3,2,1,0:T(8,128)S(1)}, f32[1,7,32,128]{3,2,1,0:T(8,128)S(1)}, u32[]{:S(2)}, u32[]{:S(2)}) collective-permute-start(f32[1,7,32,128]{3,2,1,0:T(8,128)S(1)} %get-tuple-element.109), channel_id=1, source_target_pairs={{1,0},{2,1},{3,2},{4,3},{5,4},{6,5},{7,6},{8,7},{9,8},{10,9},{11,1... | collective-permute-start | bytes 344072 | tf_op jit(solution)/shard_map/ppermute | solution.py:19
  80.9 0.3 fusion.497
  81.2 2.1 %collective-permute-start.13 = (f32[1]{0:T(128)}, f32[1]{0:T(128)}, u32[]{:S(2)}, u32[]{:S(2)}) collective-permute-start(f32[1]{0:T(128)} %add.793), channel_id=1, source_target_pairs={{0,4},{1,5},{2,6},{3,7},{4,0},{5,1},{6,2},{7,3},{8,12},{9,13},{10,... | collective-permute-start | bytes 20 | tf_op jit(solution)/shard_map/ppermute | solution.py:36
  83.3 0.5 collective-permute-done.13
  84.5 0.4 collective-permute-done.12
  84.9 0.1 fusion.91
  85.0 1.3 %fusion.40 = f32[1,8,32,128]{3,2,1,0:T(8,128)S(1)} fusion(s32[8,32]{1,0:T(8,128)S(1)} %multiply_add_fusion, s32[2048]{0:T(1024)S(1)} %bitcast.182, f32[2048]{0:T(1024)S(1)} %bitcast.186, s32[2048]{0:T(1024)S(1)} %bitcast.174, f32[1,8,32,128]{3,2,1,0:T(8,128)S(1)} %fusion.46, f32[1,8,32,128]{3,2,1,0:T(8,128)S(1)} %get-tuple-element.93, ...), kind=kOutput, calls=%fused_computation.23 | convolution fusion | flops 807632896 | bytes 1729536 | tf_op jit(solution)/shard_map/srk,srz->skz/dot_general | solution.py:128
  86.4 4.2 %collective-permute-start.14 = (f32[1,7,32,128]{3,2,1,0:T(8,128)S(1)}, f32[1,7,32,128]{3,2,1,0:T(8,128)S(1)}, u32[]{:S(2)}, u32[]{:S(2)}) collective-permute-start(f32[1,7,32,128]{3,2,1,0:T(8,128)S(1)} %get-tuple-element.106), channel_id=1, source_target_pairs={{0,1},{1,2},{2,3},{3,4},{4,5},{5,6},{6,7},{7,8},{8,9},{9,10},{10,1... | collective-permute-start | bytes 344072 | tf_op jit(solution)/shard_map/ppermute | solution.py:18
  90.6 2.3 %collective-permute-start.15 = (f32[1,7,32,128]{3,2,1,0:T(8,128)S(1)}, f32[1,7,32,128]{3,2,1,0:T(8,128)S(1)}, u32[]{:S(2)}, u32[]{:S(2)}) collective-permute-start(f32[1,7,32,128]{3,2,1,0:T(8,128)S(1)} %get-tuple-element.107), channel_id=1, source_target_pairs={{1,0},{2,1},{3,2},{4,3},{5,4},{6,5},{7,6},{8,7},{9,8},{10,9},{11,1... | collective-permute-start | bytes 344072 | tf_op jit(solution)/shard_map/ppermute | solution.py:19
  92.9 0.3 fusion.520
  93.2 3.7 %collective-permute-start.16 = (f32[1]{0:T(128)}, f32[1]{0:T(128)}, u32[]{:S(2)}, u32[]{:S(2)}) collective-permute-start(f32[1]{0:T(128)} %add.817), channel_id=1, source_target_pairs={{0,8},{1,9},{2,10},{3,11},{4,12},{5,13},{6,14},{7,15},{8,0},{9,1},... | collective-permute-start | bytes 20 | tf_op jit(solution)/shard_map/ppermute | solution.py:36
  97.0 0.3 collective-permute-done.16
  98.1 1.3 %fusion.37 = f32[1,8,32,128]{3,2,1,0:T(8,128)S(1)} fusion(s32[8,32]{1,0:T(8,128)S(1)} %multiply_add_fusion, s32[2048]{0:T(1024)S(1)} %bitcast.183, f32[2048]{0:T(1024)S(1)} %bitcast.184, s32[2048]{0:T(1024)S(1)} %bitcast.175, f32[1,8,32,128]{3,2,1,0:T(8,128)S(1)} %fusion.43, f32[1,8,32,128]{3,2,1,0:T(8,128)S(1)} %get-tuple-element.91, ...), kind=kOutput, calls=%fused_computation.22 | convolution fusion | flops 807632896 | bytes 1729536 | tf_op jit(solution)/shard_map/srk,srz->skz/dot_general | solution.py:128
  99.5 5.1 %collective-permute-start.17 = (f32[1]{0:T(128)}, f32[1]{0:T(128)}, u32[]{:S(2)}, u32[]{:S(2)}) collective-permute-start(f32[1]{0:T(128)} %add.841), channel_id=1, source_target_pairs={{0,1},{1,0},{2,3},{3,2},{4,5},{5,4},{6,7},{7,6},{8,9},{9,8},{10,11... | collective-permute-start | bytes 20 | tf_op jit(solution)/shard_map/ppermute | solution.py:36
  104.5 0.8 bitcast_multiply_fusion
  (55 shorter events, 0.9 us)
Async XLA Ops:
  1.7 9.0 %copy-start.9 = (f32[1,4]{1,0:T(1,128)S(1)}, f32[1,4]{1,0:T(1,128)}, u32[]{:S(2)}) copy-start(f32[1,4]{1,0:T(1,128)} %param.25) | copy-start | bytes 52
  1.7 12.3 %copy-start.7 = (s32[1,2048]{1,0:T(1,128)S(1)}, s32[1,2048]{1,0:T(1,128)}, u32[]{:S(2)}) copy-start(s32[1,2048]{1,0:T(1,128)} %param.26) | copy-start | bytes 24580
  1.7 12.4 %copy-start = (f32[8,32,128]{2,1,0:T(8,128)S(1)}, f32[8,32,128]{2,1,0:T(8,128)}, u32[]{:S(2)}) copy-start(f32[8,32,128]{2,1,0:T(8,128)} %param.19) | copy-start | bytes 393220
  1.7 12.4 %copy-start.1 = (f32[1,8,32,128]{3,2,1,0:T(8,128)S(1)}, f32[1,8,32,128]{3,2,1,0:T(8,128)}, u32[]{:S(2)}) copy-start(f32[1,8,32,128]{3,2,1,0:T(8,128)} %param.21) | copy-start | bytes 393220
  2.9 11.8 %collective-permute-start.1 = (f32[3,7,32,128]{3,2,1,0:T(8,128)S(1)}, f32[3,7,32,128]{3,2,1,0:T(8,128)S(1)}, u32[]{:S(2)}, u32[]{:S(2)}) collective-permute-start(f32[3,7,32,128]{3,2,1,0:T(8,128)S(1)} %get-tuple-element.88), channel_id=1, source_target_pairs={{1,0},{2,1},{3,2},{4,3},{5,4},{6,5},{7,6},{8,7},{9,8},{10,9},{11,1... | collective-permute-start | bytes 1032200 | tf_op jit(solution)/shard_map/ppermute | solution.py:19
  4.8 11.3 %collective-permute-start = (f32[3,7,32,128]{3,2,1,0:T(8,128)S(1)}, f32[3,7,32,128]{3,2,1,0:T(8,128)S(1)}, u32[]{:S(2)}, u32[]{:S(2)}) collective-permute-start(f32[3,7,32,128]{3,2,1,0:T(8,128)S(1)} %get-tuple-element.89), channel_id=1, source_target_pairs={{0,1},{1,2},{2,3},{3,4},{4,5},{5,6},{6,7},{7,8},{8,9},{9,10},{10,1... | collective-permute-start | bytes 1032200 | tf_op jit(solution)/shard_map/ppermute | solution.py:18
  16.3 0.9 copy-start.6
  20.3 8.1 %collective-permute-start.2 = (f32[1,7,32,128]{3,2,1,0:T(8,128)S(1)}, f32[1,7,32,128]{3,2,1,0:T(8,128)S(1)}, u32[]{:S(2)}, u32[]{:S(2)}) collective-permute-start(f32[1,7,32,128]{3,2,1,0:T(8,128)S(1)} %get-tuple-element.118), channel_id=1, source_target_pairs={{0,1},{1,2},{2,3},{3,4},{4,5},{5,6},{6,7},{7,8},{8,9},{9,10},{10,1... | collective-permute-start | bytes 344072 | tf_op jit(solution)/shard_map/ppermute | solution.py:18
  24.7 6.1 %collective-permute-start.3 = (f32[1,7,32,128]{3,2,1,0:T(8,128)S(1)}, f32[1,7,32,128]{3,2,1,0:T(8,128)S(1)}, u32[]{:S(2)}, u32[]{:S(2)}) collective-permute-start(f32[1,7,32,128]{3,2,1,0:T(8,128)S(1)} %get-tuple-element.119), channel_id=1, source_target_pairs={{1,0},{2,1},{3,2},{4,3},{5,4},{6,5},{7,6},{8,7},{9,8},{10,9},{11,1... | collective-permute-start | bytes 344072 | tf_op jit(solution)/shard_map/ppermute | solution.py:19
  34.3 6.0 %collective-permute-start.4 = (f32[1,7,32,128]{3,2,1,0:T(8,128)S(1)}, f32[1,7,32,128]{3,2,1,0:T(8,128)S(1)}, u32[]{:S(2)}, u32[]{:S(2)}) collective-permute-start(f32[1,7,32,128]{3,2,1,0:T(8,128)S(1)} %get-tuple-element.116), channel_id=1, source_target_pairs={{0,1},{1,2},{2,3},{3,4},{4,5},{5,6},{6,7},{7,8},{8,9},{9,10},{10,1... | collective-permute-start | bytes 344072 | tf_op jit(solution)/shard_map/ppermute | solution.py:18
  36.3 6.1 %collective-permute-start.5 = (f32[1,7,32,128]{3,2,1,0:T(8,128)S(1)}, f32[1,7,32,128]{3,2,1,0:T(8,128)S(1)}, u32[]{:S(2)}, u32[]{:S(2)}) collective-permute-start(f32[1,7,32,128]{3,2,1,0:T(8,128)S(1)} %get-tuple-element.117), channel_id=1, source_target_pairs={{1,0},{2,1},{3,2},{4,3},{5,4},{6,5},{7,6},{8,7},{9,8},{10,9},{11,1... | collective-permute-start | bytes 344072 | tf_op jit(solution)/shard_map/ppermute | solution.py:19
  45.8 6.0 %collective-permute-start.6 = (f32[1,7,32,128]{3,2,1,0:T(8,128)S(1)}, f32[1,7,32,128]{3,2,1,0:T(8,128)S(1)}, u32[]{:S(2)}, u32[]{:S(2)}) collective-permute-start(f32[1,7,32,128]{3,2,1,0:T(8,128)S(1)} %get-tuple-element.114), channel_id=1, source_target_pairs={{0,1},{1,2},{2,3},{3,4},{4,5},{5,6},{6,7},{7,8},{8,9},{9,10},{10,1... | collective-permute-start | bytes 344072 | tf_op jit(solution)/shard_map/ppermute | solution.py:18
  47.7 7.0 %collective-permute-start.7 = (f32[1,7,32,128]{3,2,1,0:T(8,128)S(1)}, f32[1,7,32,128]{3,2,1,0:T(8,128)S(1)}, u32[]{:S(2)}, u32[]{:S(2)}) collective-permute-start(f32[1,7,32,128]{3,2,1,0:T(8,128)S(1)} %get-tuple-element.115), channel_id=1, source_target_pairs={{1,0},{2,1},{3,2},{4,3},{5,4},{6,5},{7,6},{8,7},{9,8},{10,9},{11,1... | collective-permute-start | bytes 344072 | tf_op jit(solution)/shard_map/ppermute | solution.py:19
  55.1 4.4 %copy-start.8 = (f32[1,4,2048]{2,1,0:T(4,128)S(1)}, f32[1,4,2048]{2,1,0:T(4,128)}, u32[]{:S(2)}) copy-start(f32[1,4,2048]{2,1,0:T(4,128)} %param.27) | copy-start | bytes 98308
  55.1 7.8 %copy-start.4 = (f32[1,8,32,128]{3,2,1,0:T(8,128)S(1)}, f32[1,8,32,128]{3,2,1,0:T(8,128)}, u32[]{:S(2)}) copy-start(f32[1,8,32,128]{3,2,1,0:T(8,128)} %param.22) | copy-start | bytes 393220
  55.1 7.8 %copy-start.10 = (f32[1,8,32,128]{3,2,1,0:T(8,128)S(1)}, f32[1,8,32,128]{3,2,1,0:T(8,128)}, u32[]{:S(2)}) copy-start(f32[1,8,32,128]{3,2,1,0:T(8,128)} %param.23) | copy-start | bytes 393220
  64.3 8.7 %collective-permute-start.8 = (f32[1,7,32,128]{3,2,1,0:T(8,128)S(1)}, f32[1,7,32,128]{3,2,1,0:T(8,128)S(1)}, u32[]{:S(2)}, u32[]{:S(2)}) collective-permute-start(f32[1,7,32,128]{3,2,1,0:T(8,128)S(1)} %get-tuple-element.110), channel_id=1, source_target_pairs={{0,1},{1,2},{2,3},{3,4},{4,5},{5,6},{6,7},{7,8},{8,9},{9,10},{10,1... | collective-permute-start | bytes 344072 | tf_op jit(solution)/shard_map/ppermute | solution.py:18
  66.2 7.0 %collective-permute-start.9 = (f32[1,7,32,128]{3,2,1,0:T(8,128)S(1)}, f32[1,7,32,128]{3,2,1,0:T(8,128)S(1)}, u32[]{:S(2)}, u32[]{:S(2)}) collective-permute-start(f32[1,7,32,128]{3,2,1,0:T(8,128)S(1)} %get-tuple-element.111), channel_id=1, source_target_pairs={{1,0},{2,1},{3,2},{4,3},{5,4},{6,5},{7,6},{8,7},{9,8},{10,9},{11,1... | collective-permute-start | bytes 344072 | tf_op jit(solution)/shard_map/ppermute | solution.py:19
  68.9 3.4 %collective-permute-start.10 = (f32[1]{0:T(128)}, f32[1]{0:T(128)}, u32[]{:S(2)}, u32[]{:S(2)}) collective-permute-start(f32[1]{0:T(128)} %bitcast.38), channel_id=1, source_target_pairs={{0,2},{1,3},{2,0},{3,1},{4,6},{5,7},{6,4},{7,5},{8,10},{9,11},{10,... | collective-permute-start | bytes 20 | tf_op jit(solution)/shard_map/ppermute | solution.py:36
  74.7 9.7 %collective-permute-start.11 = (f32[1,7,32,128]{3,2,1,0:T(8,128)S(1)}, f32[1,7,32,128]{3,2,1,0:T(8,128)S(1)}, u32[]{:S(2)}, u32[]{:S(2)}) collective-permute-start(f32[1,7,32,128]{3,2,1,0:T(8,128)S(1)} %get-tuple-element.108), channel_id=1, source_target_pairs={{0,1},{1,2},{2,3},{3,4},{4,5},{5,6},{6,7},{7,8},{8,9},{9,10},{10,1... | collective-permute-start | bytes 344072 | tf_op jit(solution)/shard_map/ppermute | solution.py:18
  78.8 6.1 %collective-permute-start.12 = (f32[1,7,32,128]{3,2,1,0:T(8,128)S(1)}, f32[1,7,32,128]{3,2,1,0:T(8,128)S(1)}, u32[]{:S(2)}, u32[]{:S(2)}) collective-permute-start(f32[1,7,32,128]{3,2,1,0:T(8,128)S(1)} %get-tuple-element.109), channel_id=1, source_target_pairs={{1,0},{2,1},{3,2},{4,3},{5,4},{6,5},{7,6},{8,7},{9,8},{10,9},{11,1... | collective-permute-start | bytes 344072 | tf_op jit(solution)/shard_map/ppermute | solution.py:19
  81.2 2.6 %collective-permute-start.13 = (f32[1]{0:T(128)}, f32[1]{0:T(128)}, u32[]{:S(2)}, u32[]{:S(2)}) collective-permute-start(f32[1]{0:T(128)} %add.793), channel_id=1, source_target_pairs={{0,4},{1,5},{2,6},{3,7},{4,0},{5,1},{6,2},{7,3},{8,12},{9,13},{10,... | collective-permute-start | bytes 20 | tf_op jit(solution)/shard_map/ppermute | solution.py:36
  86.3 18.2 %copy-start.3 = (f32[1,8,32,128]{3,2,1,0:T(8,128)}, f32[1,8,32,128]{3,2,1,0:T(8,128)S(1)}, u32[]{:S(2)}) copy-start(f32[1,8,32,128]{3,2,1,0:T(8,128)S(1)} %fusion.40) | copy-start | bytes 393220
  86.4 11.6 %collective-permute-start.14 = (f32[1,7,32,128]{3,2,1,0:T(8,128)S(1)}, f32[1,7,32,128]{3,2,1,0:T(8,128)S(1)}, u32[]{:S(2)}, u32[]{:S(2)}) collective-permute-start(f32[1,7,32,128]{3,2,1,0:T(8,128)S(1)} %get-tuple-element.106), channel_id=1, source_target_pairs={{0,1},{1,2},{2,3},{3,4},{4,5},{5,6},{6,7},{7,8},{8,9},{9,10},{10,1... | collective-permute-start | bytes 344072 | tf_op jit(solution)/shard_map/ppermute | solution.py:18
  90.6 7.3 %collective-permute-start.15 = (f32[1,7,32,128]{3,2,1,0:T(8,128)S(1)}, f32[1,7,32,128]{3,2,1,0:T(8,128)S(1)}, u32[]{:S(2)}, u32[]{:S(2)}) collective-permute-start(f32[1,7,32,128]{3,2,1,0:T(8,128)S(1)} %get-tuple-element.107), channel_id=1, source_target_pairs={{1,0},{2,1},{3,2},{4,3},{5,4},{6,5},{7,6},{8,7},{9,8},{10,9},{11,1... | collective-permute-start | bytes 344072 | tf_op jit(solution)/shard_map/ppermute | solution.py:19
  93.2 4.0 %collective-permute-start.16 = (f32[1]{0:T(128)}, f32[1]{0:T(128)}, u32[]{:S(2)}, u32[]{:S(2)}) collective-permute-start(f32[1]{0:T(128)} %add.817), channel_id=1, source_target_pairs={{0,8},{1,9},{2,10},{3,11},{4,12},{5,13},{6,14},{7,15},{8,0},{9,1},... | collective-permute-start | bytes 20 | tf_op jit(solution)/shard_map/ppermute | solution.py:36
  98.1 6.4 %copy-start.2 = (f32[8,32,128]{2,1,0:T(8,128)S(1)}, f32[8,32,128]{2,1,0:T(8,128)}, u32[]{:S(2)}) copy-start(f32[8,32,128]{2,1,0:T(8,128)} %param.18) | copy-start | bytes 393220
  99.4 6.6 %copy-start.5 = (f32[1,8,32,128]{3,2,1,0:T(8,128)}, f32[1,8,32,128]{3,2,1,0:T(8,128)S(1)}, u32[]{:S(2)}) copy-start(f32[1,8,32,128]{3,2,1,0:T(8,128)S(1)} %fusion.37) | copy-start | bytes 393220
  99.5 5.9 %collective-permute-start.17 = (f32[1]{0:T(128)}, f32[1]{0:T(128)}, u32[]{:S(2)}, u32[]{:S(2)}) collective-permute-start(f32[1]{0:T(128)} %add.841), channel_id=1, source_target_pairs={{0,1},{1,0},{2,3},{3,2},{4,5},{5,4},{6,7},{7,6},{8,9},{9,8},{10,11... | collective-permute-start | bytes 20 | tf_op jit(solution)/shard_map/ppermute | solution.py:36

commit v4 on v3

--- a/solution.py
+++ b/solution.py
@@ -107,8 +107,10 @@
 
     source_local = source_cell - offset
     source_owned = (source_local >= 0) & (source_local < cells)
-    source_index = jnp.clip(source_local, 0, cells - 1)
-    shot_rows = jnp.arange(shots)
+    cell_index = lax.broadcasted_iota(jnp.int32, shape, 1) * (cy * cz)
+    cell_index = cell_index + lax.broadcasted_iota(jnp.int32, shape, 2) * cz
+    cell_index = cell_index + lax.broadcasted_iota(jnp.int32, shape, 3)
+    source_hit = cell_index == source_local.reshape(shots, 1, 1, 1)
 
     receiver_local = receiver_cell - offset
     receiver_owned = (receiver_local >= 0) & (receiver_local < cells)
@@ -135,9 +137,8 @@
         lap = first_lap if step == 0 else operator(current)
         laps.append(lap)
         following = 2.0 * current - before + kappa * lap
-        amount = jnp.where(source_owned, wavelet[:, step], 0.0)
-        flat = following.reshape(shots, cells).at[shot_rows, source_index].add(amount)
-        following = flat.reshape(shape)
+        amount = wavelet[:, step].reshape(shots, 1, 1, 1)
+        following = following + jnp.where(source_hit, amount, 0.0)
         sampled = sample(following)
         resids.append(jnp.where(receiver_owned, sampled - observed[:, step, :], 0.0))
         before, current = (current, following)

time: 108 us -> 99.9 us (0.925)
  between operations: 18.8 us -> 8.34 us
  waiting for transfers between devices: 10.7 us -> 14.1 us
    ppermute x7, waiting for transfers between devices: 1.54 us -> 3.87 us  [extended(): before = lax.ppermute(last, 'mp', up)]
    add x8 -> x4, other arithmetic: 3.82 us -> 3.93 us  [local(): following = following + jnp.where(source_hit, amount, 0.0)]
  transfers between devices with their start and end apart: 18 -> 18, of which waited for: 9 -> 10; matrix products, arithmetic and copies ran while one was open for 8% -> 8% of each run, Pallas kernels for 0% -> 0%
where the time goes in v4:
time: 99.9 us; the launch traced here: 99.2 us
  starting transfers between devices  52.3 us (52%)
  waiting for transfers between devices  14.1 us (14%)
  matrix products  11.7 us (12%)
  other arithmetic  11.2 us (11%)
  between operations  8.34 us (8%)
  local copies, waits for them, and re-layouts  1.68 us (2%)
    ppermute x7, starting transfers between devices, extended(): before = lax.ppermute(last, 'mp', up)  22.9 us
    ppermute x7, starting transfers between devices, extended(): after = lax.ppermute(first, 'mp', down)  15.5 us
    ppermute x4, starting transfers between devices, butterfly_round(): return values + lax.ppermute(values, axis, pairs)  13.9 us
    ppermute x7, waiting for transfers between devices, extended(): after = lax.ppermute(first, 'mp', down)  9.1 us
    dot_general x4, matrix products, sample(): jnp.einsum('srk,skz->srz', row_pick, field.reshape(shots, rows, cz), prec...  6.43 us
    dot_general x4, matrix products, inject(): jnp.einsum('srk,srz->skz', row_pick, spread, precision=lax.Precision.HIGH...  5.22 us
    add x4, other arithmetic, local(): following = following + jnp.where(source_hit, amount, 0.0)  3.93 us
    ppermute x7, waiting for transfers between devices, extended(): before = lax.ppermute(last, 'mp', up)  3.87 us
  transfers between devices with their start and end apart: 18, of which 10 were waited for; matrix products, arithmetic and copies ran while one was open for 8% of the time, Pallas kernels for 0%

profile of v4, /device:TPU:1, one launch (start us, length us, event | category | flops | bytes accessed | tf_op | source)
XLA Modules:
  0.0 99.2 jit_solution(7191718213192960267)
XLA Ops:
  0.6 1.1 %bitcast_multiply_fusion.8 = (f32[1,8,32,128]{3,2,1,0:T(8,128)S(1)}, f32[8,32,128]{2,1,0:T(8,128)S(1)}) fusion(f32[1,8,32,128]{3,2,1,0:T(8,128)} %param.14, f32[8,32,128]{2,1,0:T(8,128)} %param.11, f32[8,32,128]{2,1,0:T(8,128)} %param.10), kind=kLoop, calls=%fused_computation.881 | loop fusion | flops 98304 | bytes 655360 | tf_op jit(solution)/shard_map/mul | solution.py:99
  1.7 0.0 copy-start
  1.7 1.0 %pad_maximum_fusion.1 = f32[3,8,32,128]{3,2,1,0:T(8,128)S(1)} fusion(f32[1,8,32,128]{3,2,1,0:T(8,128)S(1)} %get-tuple-element.38, f32[1,8,32,128]{3,2,1,0:T(8,128)} %param.13, f32[1,8,32,128]{3,2,1,0:T(8,128)} %bitcast.131), kind=kLoop, calls=%fused_computation.172 | loop fusion | flops 196608 | bytes 786432 | tf_op jit(solution)/shard_map/concatenate | solution.py:100
  2.8 0.1 fusion.619
  2.9 2.0 %collective-permute-start.1 = (f32[3,7,32,128]{3,2,1,0:T(8,128)S(1)}, f32[3,7,32,128]{3,2,1,0:T(8,128)S(1)}, u32[]{:S(2)}, u32[]{:S(2)}) collective-permute-start(f32[3,7,32,128]{3,2,1,0:T(8,128)S(1)} %get-tuple-element.40), channel_id=1, source_target_pairs={{1,0},{2,1},{3,2},{4,3},{5,4},{6,5},{7,6},{8,7},{9,8},{10,9},{11,1... | collective-permute-start | bytes 1032200 | tf_op jit(solution)/shard_map/ppermute | solution.py:19
  4.8 4.5 %collective-permute-start = (f32[3,7,32,128]{3,2,1,0:T(8,128)S(1)}, f32[3,7,32,128]{3,2,1,0:T(8,128)S(1)}, u32[]{:S(2)}, u32[]{:S(2)}) collective-permute-start(f32[3,7,32,128]{3,2,1,0:T(8,128)S(1)} %get-tuple-element.41), channel_id=1, source_target_pairs={{0,1},{1,2},{2,3},{3,4},{4,5},{5,6},{6,7},{7,8},{8,9},{9,10},{10,1... | collective-permute-start | bytes 1032200 | tf_op jit(solution)/shard_map/ppermute | solution.py:18
  10.0 0.7 fusion.626
  10.8 0.5 fusion.359
  11.3 1.0 collective-permute-done.1
  12.3 3.9 %collective-permute-done = f32[3,7,32,128]{3,2,1,0:T(8,128)S(1)} collective-permute-done((f32[3,7,32,128]{3,2,1,0:T(8,128)S(1)}, f32[3,7,32,128]{3,2,1,0:T(8,128)S(1)}, u32[]{:S(2)}, u32[]{:S(2)}) %collective-permute-start) | collective-permute-done | bytes 344096 | tf_op jit(solution)/shard_map/ppermute | solution.py:18
  16.2 0.1 pad_maximum_fusion
  16.3 0.1 fusion.126
  16.4 0.8 copy-done.4
  17.2 1.0 fusion.595
  18.2 0.3 fusion.203
  18.5 4.4 %collective-permute-start.2 = (f32[1,7,32,128]{3,2,1,0:T(8,128)S(1)}, f32[1,7,32,128]{3,2,1,0:T(8,128)S(1)}, u32[]{:S(2)}, u32[]{:S(2)}) collective-permute-start(f32[1,7,32,128]{3,2,1,0:T(8,128)S(1)} %get-tuple-element.70), channel_id=1, source_target_pairs={{0,1},{1,2},{2,3},{3,4},{4,5},{5,6},{6,7},{7,8},{8,9},{9,10},{10,1... | collective-permute-start | bytes 344072 | tf_op jit(solution)/shard_map/ppermute | solution.py:18
  22.9 1.9 %collective-permute-start.3 = (f32[1,7,32,128]{3,2,1,0:T(8,128)S(1)}, f32[1,7,32,128]{3,2,1,0:T(8,128)S(1)}, u32[]{:S(2)}, u32[]{:S(2)}) collective-permute-start(f32[1,7,32,128]{3,2,1,0:T(8,128)S(1)} %get-tuple-element.71), channel_id=1, source_target_pairs={{1,0},{2,1},{3,2},{4,3},{5,4},{6,5},{7,6},{8,7},{9,8},{10,9},{11,1... | collective-permute-start | bytes 344072 | tf_op jit(solution)/shard_map/ppermute | solution.py:19
  24.8 0.1 fusion.134
  24.9 1.6 %fusion.16 = f32[2048]{0:T(1024)S(1)} fusion(f32[256,128]{1,0:T(8,128)S(1)} %bitcast.135, s32[2048]{0:T(1024)S(1)} %bitcast.147, s32[2048]{0:T(1024)S(1)} %bitcast.139), kind=kOutput, calls=%fused_computation.15 | convolution fusion | flops 806615040 | bytes 155648 | tf_op jit(solution)/shard_map/srk,skz->srz/dot_general | solution.py:123
  26.6 2.4 %collective-permute-done.3 = f32[1,7,32,128]{3,2,1,0:T(8,128)S(1)} collective-permute-done((f32[1,7,32,128]{3,2,1,0:T(8,128)S(1)}, f32[1,7,32,128]{3,2,1,0:T(8,128)S(1)}, u32[]{:S(2)}, u32[]{:S(2)}) %collective-permute-start.3) | collective-permute-done | bytes 114720 | tf_op jit(solution)/shard_map/ppermute | solution.py:19
  29.0 0.1 fusion.119
  29.1 1.0 fusion.597
  30.1 0.3 fusion.228
  30.5 1.9 %collective-permute-start.4 = (f32[1,7,32,128]{3,2,1,0:T(8,128)S(1)}, f32[1,7,32,128]{3,2,1,0:T(8,128)S(1)}, u32[]{:S(2)}, u32[]{:S(2)}) collective-permute-start(f32[1,7,32,128]{3,2,1,0:T(8,128)S(1)} %get-tuple-element.68), channel_id=1, source_target_pairs={{0,1},{1,2},{2,3},{3,4},{4,5},{5,6},{6,7},{7,8},{8,9},{9,10},{10,1... | collective-permute-start | bytes 344072 | tf_op jit(solution)/shard_map/ppermute | solution.py:18
  32.4 2.4 %collective-permute-start.5 = (f32[1,7,32,128]{3,2,1,0:T(8,128)S(1)}, f32[1,7,32,128]{3,2,1,0:T(8,128)S(1)}, u32[]{:S(2)}, u32[]{:S(2)}) collective-permute-start(f32[1,7,32,128]{3,2,1,0:T(8,128)S(1)} %get-tuple-element.69), channel_id=1, source_target_pairs={{1,0},{2,1},{3,2},{4,3},{5,4},{6,5},{7,6},{8,7},{9,8},{10,9},{11,1... | collective-permute-start | bytes 344072 | tf_op jit(solution)/shard_map/ppermute | solution.py:19
  34.8 1.6 %fusion.19 = f32[2048]{0:T(1024)S(1)} fusion(f32[256,128]{1,0:T(8,128)S(1)} %bitcast.136, s32[2048]{0:T(1024)S(1)} %bitcast.148, s32[2048]{0:T(1024)S(1)} %bitcast.140), kind=kOutput, calls=%fused_computation.16 | convolution fusion | flops 806615040 | bytes 155648 | tf_op jit(solution)/shard_map/srk,skz->srz/dot_general | solution.py:123
  36.4 2.1 %collective-permute-done.5 = f32[1,7,32,128]{3,2,1,0:T(8,128)S(1)} collective-permute-done((f32[1,7,32,128]{3,2,1,0:T(8,128)S(1)}, f32[1,7,32,128]{3,2,1,0:T(8,128)S(1)}, u32[]{:S(2)}, u32[]{:S(2)}) %collective-permute-start.5) | collective-permute-done | bytes 114720 | tf_op jit(solution)/shard_map/ppermute | solution.py:19
  38.5 0.1 fusion.112
  38.6 1.0 %fusion.599 = (f32[1,8,32,128]{3,2,1,0:T(8,128)S(1)}, f32[1,8,32,128]{3,2,1,0:T(8,128)S(1)}) fusion(f32[8,32,128]{2,1,0:T(8,128)S(1)} %get-tuple-element.39, f32[1,8,32,128]{3,2,1,0:T(8,128)S(1)} %get-tuple-element.36, f32[1,8,32,128]{3,2,1,0:T(8,128)S(1)} %get-tuple-element.32, f32[]{:T(128)} %bitcast.9, s32[]{:T(128)} %bitcast.6, ...), kind=kLoop, calls=%fused_computation.887 | loop fusion | flops 1441792 | bytes 1966248 | tf_op jit(solution)/shard_map/add | solution.py:141
  39.7 0.3 fusion.253
  40.0 1.9 %collective-permute-start.6 = (f32[1,7,32,128]{3,2,1,0:T(8,128)S(1)}, f32[1,7,32,128]{3,2,1,0:T(8,128)S(1)}, u32[]{:S(2)}, u32[]{:S(2)}) collective-permute-start(f32[1,7,32,128]{3,2,1,0:T(8,128)S(1)} %get-tuple-element.66), channel_id=1, source_target_pairs={{0,1},{1,2},{2,3},{3,4},{4,5},{5,6},{6,7},{7,8},{8,9},{9,10},{10,1... | collective-permute-start | bytes 344072 | tf_op jit(solution)/shard_map/ppermute | solution.py:18
  41.9 2.4 %collective-permute-start.7 = (f32[1,7,32,128]{3,2,1,0:T(8,128)S(1)}, f32[1,7,32,128]{3,2,1,0:T(8,128)S(1)}, u32[]{:S(2)}, u32[]{:S(2)}) collective-permute-start(f32[1,7,32,128]{3,2,1,0:T(8,128)S(1)} %get-tuple-element.67), channel_id=1, source_target_pairs={{1,0},{2,1},{3,2},{4,3},{5,4},{6,5},{7,6},{8,7},{9,8},{10,9},{11,1... | collective-permute-start | bytes 344072 | tf_op jit(solution)/shard_map/ppermute | solution.py:19
  44.3 1.6 %fusion.22 = f32[2048]{0:T(1024)S(1)} fusion(f32[256,128]{1,0:T(8,128)S(1)} %bitcast.137, s32[2048]{0:T(1024)S(1)} %bitcast.149, s32[2048]{0:T(1024)S(1)} %bitcast.141), kind=kOutput, calls=%fused_computation.17 | convolution fusion | flops 806615040 | bytes 155648 | tf_op jit(solution)/shard_map/srk,skz->srz/dot_general | solution.py:123
  46.0 2.9 %collective-permute-done.7 = f32[1,7,32,128]{3,2,1,0:T(8,128)S(1)} collective-permute-done((f32[1,7,32,128]{3,2,1,0:T(8,128)S(1)}, f32[1,7,32,128]{3,2,1,0:T(8,128)S(1)}, u32[]{:S(2)}, u32[]{:S(2)}) %collective-permute-start.7) | collective-permute-done | bytes 114720 | tf_op jit(solution)/shard_map/ppermute | solution.py:19
  48.9 0.1 fusion.105
  49.0 1.0 fusion.601
  50.0 1.6 %fusion.13 = f32[2048]{0:T(1024)S(1)} fusion(f32[256,128]{1,0:T(8,128)S(1)} %bitcast.138, s32[2048]{0:T(1024)S(1)} %bitcast.150, s32[2048]{0:T(1024)S(1)} %bitcast.142), kind=kOutput, calls=%fused_computation.14 | convolution fusion | flops 806615040 | bytes 155648 | tf_op jit(solution)/shard_map/srk,skz->srz/dot_general | solution.py:123
  51.7 0.7 multiply_reduce_fusion.2
  55.1 1.3 %fusion.46 = f32[1,8,32,128]{3,2,1,0:T(8,128)S(1)} fusion(s32[8,32]{1,0:T(8,128)S(1)} %multiply_add_fusion, s32[2048]{0:T(1024)S(1)} %bitcast.151, f32[2048]{0:T(1024)S(1)} %bitcast.161, s32[2048]{0:T(1024)S(1)} %bitcast.143, f32[1,8,32,128]{3,2,1,0:T(8,128)S(1)} %copy-done.10, f32[1,8,32,128]{3,2,1,0:T(8,128)S(1)} %get-tuple-element.49, ...), kind=kOutput, calls=%fused_computation.25 | convolution fusion | flops 807632896 | bytes 1729536 | tf_op jit(solution)/shard_map/srk,srz->skz/dot_general | solution.py:130
  56.4 1.9 %collective-permute-start.8 = (f32[1,7,32,128]{3,2,1,0:T(8,128)S(1)}, f32[1,7,32,128]{3,2,1,0:T(8,128)S(1)}, u32[]{:S(2)}, u32[]{:S(2)}) collective-permute-start(f32[1,7,32,128]{3,2,1,0:T(8,128)S(1)} %get-tuple-element.62), channel_id=1, source_target_pairs={{0,1},{1,2},{2,3},{3,4},{4,5},{5,6},{6,7},{7,8},{8,9},{9,10},{10,1... | collective-permute-start | bytes 344072 | tf_op jit(solution)/shard_map/ppermute | solution.py:18
  58.3 2.4 %collective-permute-start.9 = (f32[1,7,32,128]{3,2,1,0:T(8,128)S(1)}, f32[1,7,32,128]{3,2,1,0:T(8,128)S(1)}, u32[]{:S(2)}, u32[]{:S(2)}) collective-permute-start(f32[1,7,32,128]{3,2,1,0:T(8,128)S(1)} %get-tuple-element.63), channel_id=1, source_target_pairs={{1,0},{2,1},{3,2},{4,3},{5,4},{6,5},{7,6},{8,7},{9,8},{10,9},{11,1... | collective-permute-start | bytes 344072 | tf_op jit(solution)/shard_map/ppermute | solution.py:19
  60.7 0.3 fusion.474
  61.1 3.0 %collective-permute-start.10 = (f32[1]{0:T(128)}, f32[1]{0:T(128)}, u32[]{:S(2)}, u32[]{:S(2)}) collective-permute-start(f32[1]{0:T(128)} %bitcast.26), channel_id=1, source_target_pairs={{0,2},{1,3},{2,0},{3,1},{4,6},{5,7},{6,4},{7,5},{8,10},{9,11},{10,... | collective-permute-start | bytes 20 | tf_op jit(solution)/shard_map/ppermute | solution.py:36
  64.1 0.3 collective-permute-done.10
  65.1 0.2 collective-permute-done.9
  65.4 0.1 fusion.98
  65.5 1.3 %fusion.43 = f32[1,8,32,128]{3,2,1,0:T(8,128)S(1)} fusion(s32[8,32]{1,0:T(8,128)S(1)} %multiply_add_fusion, s32[2048]{0:T(1024)S(1)} %bitcast.152, f32[2048]{0:T(1024)S(1)} %bitcast.159, s32[2048]{0:T(1024)S(1)} %bitcast.144, f32[1,8,32,128]{3,2,1,0:T(8,128)S(1)} %copy-done.5, f32[1,8,32,128]{3,2,1,0:T(8,128)S(1)} %get-tuple-element.47, ...), kind=kOutput, calls=%fused_computation.24 | convolution fusion | flops 807632896 | bytes 1729536 | tf_op jit(solution)/shard_map/srk,srz->skz/dot_general | solution.py:130
  66.9 4.0 %collective-permute-start.11 = (f32[1,7,32,128]{3,2,1,0:T(8,128)S(1)}, f32[1,7,32,128]{3,2,1,0:T(8,128)S(1)}, u32[]{:S(2)}, u32[]{:S(2)}) collective-permute-start(f32[1,7,32,128]{3,2,1,0:T(8,128)S(1)} %get-tuple-element.60), channel_id=1, source_target_pairs={{0,1},{1,2},{2,3},{3,4},{4,5},{5,6},{6,7},{7,8},{8,9},{9,10},{10,1... | collective-permute-start | bytes 344072 | tf_op jit(solution)/shard_map/ppermute | solution.py:18
  70.9 2.1 %collective-permute-start.12 = (f32[1,7,32,128]{3,2,1,0:T(8,128)S(1)}, f32[1,7,32,128]{3,2,1,0:T(8,128)S(1)}, u32[]{:S(2)}, u32[]{:S(2)}) collective-permute-start(f32[1,7,32,128]{3,2,1,0:T(8,128)S(1)} %get-tuple-element.61), channel_id=1, source_target_pairs={{1,0},{2,1},{3,2},{4,3},{5,4},{6,5},{7,6},{8,7},{9,8},{10,9},{11,1... | collective-permute-start | bytes 344072 | tf_op jit(solution)/shard_map/ppermute | solution.py:19
  73.0 0.3 fusion.497
  73.3 2.1 %collective-permute-start.13 = (f32[1]{0:T(128)}, f32[1]{0:T(128)}, u32[]{:S(2)}, u32[]{:S(2)}) collective-permute-start(f32[1]{0:T(128)} %add.821), channel_id=1, source_target_pairs={{0,4},{1,5},{2,6},{3,7},{4,0},{5,1},{6,2},{7,3},{8,12},{9,13},{10,... | collective-permute-start | bytes 20 | tf_op jit(solution)/shard_map/ppermute | solution.py:36
  75.4 0.5 collective-permute-done.13
  76.6 0.4 collective-permute-done.12
  77.0 0.1 fusion.91
  77.1 1.3 %fusion.40 = f32[1,8,32,128]{3,2,1,0:T(8,128)S(1)} fusion(s32[8,32]{1,0:T(8,128)S(1)} %multiply_add_fusion, s32[2048]{0:T(1024)S(1)} %bitcast.153, f32[2048]{0:T(1024)S(1)} %bitcast.157, s32[2048]{0:T(1024)S(1)} %bitcast.145, f32[1,8,32,128]{3,2,1,0:T(8,128)S(1)} %fusion.46, f32[1,8,32,128]{3,2,1,0:T(8,128)S(1)} %get-tuple-element.45, ...), kind=kOutput, calls=%fused_computation.23 | convolution fusion | flops 807632896 | bytes 1729536 | tf_op jit(solution)/shard_map/srk,srz->skz/dot_general | solution.py:130
  78.5 4.2 %collective-permute-start.14 = (f32[1,7,32,128]{3,2,1,0:T(8,128)S(1)}, f32[1,7,32,128]{3,2,1,0:T(8,128)S(1)}, u32[]{:S(2)}, u32[]{:S(2)}) collective-permute-start(f32[1,7,32,128]{3,2,1,0:T(8,128)S(1)} %get-tuple-element.58), channel_id=1, source_target_pairs={{0,1},{1,2},{2,3},{3,4},{4,5},{5,6},{6,7},{7,8},{8,9},{9,10},{10,1... | collective-permute-start | bytes 344072 | tf_op jit(solution)/shard_map/ppermute | solution.py:18
  82.7 2.3 %collective-permute-start.15 = (f32[1,7,32,128]{3,2,1,0:T(8,128)S(1)}, f32[1,7,32,128]{3,2,1,0:T(8,128)S(1)}, u32[]{:S(2)}, u32[]{:S(2)}) collective-permute-start(f32[1,7,32,128]{3,2,1,0:T(8,128)S(1)} %get-tuple-element.59), channel_id=1, source_target_pairs={{1,0},{2,1},{3,2},{4,3},{5,4},{6,5},{7,6},{8,7},{9,8},{10,9},{11,1... | collective-permute-start | bytes 344072 | tf_op jit(solution)/shard_map/ppermute | solution.py:19
  85.0 0.3 fusion.520
  85.3 3.7 %collective-permute-start.16 = (f32[1]{0:T(128)}, f32[1]{0:T(128)}, u32[]{:S(2)}, u32[]{:S(2)}) collective-permute-start(f32[1]{0:T(128)} %add.845), channel_id=1, source_target_pairs={{0,8},{1,9},{2,10},{3,11},{4,12},{5,13},{6,14},{7,15},{8,0},{9,1},... | collective-permute-start | bytes 20 | tf_op jit(solution)/shard_map/ppermute | solution.py:36
  89.1 0.3 collective-permute-done.16
  90.1 0.1 fusion.84
  90.2 1.3 %fusion.37 = f32[1,8,32,128]{3,2,1,0:T(8,128)S(1)} fusion(s32[8,32]{1,0:T(8,128)S(1)} %multiply_add_fusion, s32[2048]{0:T(1024)S(1)} %bitcast.154, f32[2048]{0:T(1024)S(1)} %bitcast.155, s32[2048]{0:T(1024)S(1)} %bitcast.146, f32[1,8,32,128]{3,2,1,0:T(8,128)S(1)} %fusion.43, f32[1,8,32,128]{3,2,1,0:T(8,128)S(1)} %get-tuple-element.43, ...), kind=kOutput, calls=%fused_computation.22 | convolution fusion | flops 807632896 | bytes 1729536 | tf_op jit(solution)/shard_map/srk,srz->skz/dot_general | solution.py:130
  91.6 5.1 %collective-permute-start.17 = (f32[1]{0:T(128)}, f32[1]{0:T(128)}, u32[]{:S(2)}, u32[]{:S(2)}) collective-permute-start(f32[1]{0:T(128)} %add.869), channel_id=1, source_target_pairs={{0,1},{1,0},{2,3},{3,2},{4,5},{5,4},{6,7},{7,6},{8,9},{9,8},{10,11... | collective-permute-start | bytes 20 | tf_op jit(solution)/shard_map/ppermute | solution.py:36
  96.6 0.8 bitcast_multiply_fusion
  (48 shorter events, 0.5 us)
Async XLA Ops:
  1.7 8.3 %copy-start.9 = (f32[1,4]{1,0:T(1,128)S(1)}, f32[1,4]{1,0:T(1,128)}, u32[]{:S(2)}) copy-start(f32[1,4]{1,0:T(1,128)} %param.17) | copy-start | bytes 52
  1.7 9.0 %copy-start.7 = (s32[1,2048]{1,0:T(1,128)S(1)}, s32[1,2048]{1,0:T(1,128)}, u32[]{:S(2)}) copy-start(s32[1,2048]{1,0:T(1,128)} %param.18) | copy-start | bytes 24580
  1.7 9.1 %copy-start = (f32[8,32,128]{2,1,0:T(8,128)S(1)}, f32[8,32,128]{2,1,0:T(8,128)}, u32[]{:S(2)}) copy-start(f32[8,32,128]{2,1,0:T(8,128)} %param.11) | copy-start | bytes 393220
  1.7 9.1 %copy-start.1 = (f32[1,8,32,128]{3,2,1,0:T(8,128)S(1)}, f32[1,8,32,128]{3,2,1,0:T(8,128)}, u32[]{:S(2)}) copy-start(f32[1,8,32,128]{3,2,1,0:T(8,128)} %param.13) | copy-start | bytes 393220
  2.9 9.5 %collective-permute-start.1 = (f32[3,7,32,128]{3,2,1,0:T(8,128)S(1)}, f32[3,7,32,128]{3,2,1,0:T(8,128)S(1)}, u32[]{:S(2)}, u32[]{:S(2)}) collective-permute-start(f32[3,7,32,128]{3,2,1,0:T(8,128)S(1)} %get-tuple-element.40), channel_id=1, source_target_pairs={{1,0},{2,1},{3,2},{4,3},{5,4},{6,5},{7,6},{8,7},{9,8},{10,9},{11,1... | collective-permute-start | bytes 1032200 | tf_op jit(solution)/shard_map/ppermute | solution.py:19
  4.8 11.3 %collective-permute-start = (f32[3,7,32,128]{3,2,1,0:T(8,128)S(1)}, f32[3,7,32,128]{3,2,1,0:T(8,128)S(1)}, u32[]{:S(2)}, u32[]{:S(2)}) collective-permute-start(f32[3,7,32,128]{3,2,1,0:T(8,128)S(1)} %get-tuple-element.41), channel_id=1, source_target_pairs={{0,1},{1,2},{2,3},{3,4},{4,5},{5,6},{6,7},{7,8},{8,9},{9,10},{10,1... | collective-permute-start | bytes 1032200 | tf_op jit(solution)/shard_map/ppermute | solution.py:18
  16.3 0.9 copy-start.4
  18.5 8.1 %collective-permute-start.2 = (f32[1,7,32,128]{3,2,1,0:T(8,128)S(1)}, f32[1,7,32,128]{3,2,1,0:T(8,128)S(1)}, u32[]{:S(2)}, u32[]{:S(2)}) collective-permute-start(f32[1,7,32,128]{3,2,1,0:T(8,128)S(1)} %get-tuple-element.70), channel_id=1, source_target_pairs={{0,1},{1,2},{2,3},{3,4},{4,5},{5,6},{6,7},{7,8},{8,9},{9,10},{10,1... | collective-permute-start | bytes 344072 | tf_op jit(solution)/shard_map/ppermute | solution.py:18
  22.9 6.1 %collective-permute-start.3 = (f32[1,7,32,128]{3,2,1,0:T(8,128)S(1)}, f32[1,7,32,128]{3,2,1,0:T(8,128)S(1)}, u32[]{:S(2)}, u32[]{:S(2)}) collective-permute-start(f32[1,7,32,128]{3,2,1,0:T(8,128)S(1)} %get-tuple-element.71), channel_id=1, source_target_pairs={{1,0},{2,1},{3,2},{4,3},{5,4},{6,5},{7,6},{8,7},{9,8},{10,9},{11,1... | collective-permute-start | bytes 344072 | tf_op jit(solution)/shard_map/ppermute | solution.py:19
  30.5 6.0 %collective-permute-start.4 = (f32[1,7,32,128]{3,2,1,0:T(8,128)S(1)}, f32[1,7,32,128]{3,2,1,0:T(8,128)S(1)}, u32[]{:S(2)}, u32[]{:S(2)}) collective-permute-start(f32[1,7,32,128]{3,2,1,0:T(8,128)S(1)} %get-tuple-element.68), channel_id=1, source_target_pairs={{0,1},{1,2},{2,3},{3,4},{4,5},{5,6},{6,7},{7,8},{8,9},{9,10},{10,1... | collective-permute-start | bytes 344072 | tf_op jit(solution)/shard_map/ppermute | solution.py:18
  32.4 6.1 %collective-permute-start.5 = (f32[1,7,32,128]{3,2,1,0:T(8,128)S(1)}, f32[1,7,32,128]{3,2,1,0:T(8,128)S(1)}, u32[]{:S(2)}, u32[]{:S(2)}) collective-permute-start(f32[1,7,32,128]{3,2,1,0:T(8,128)S(1)} %get-tuple-element.69), channel_id=1, source_target_pairs={{1,0},{2,1},{3,2},{4,3},{5,4},{6,5},{7,6},{8,7},{9,8},{10,9},{11,1... | collective-permute-start | bytes 344072 | tf_op jit(solution)/shard_map/ppermute | solution.py:19
  40.0 6.0 %collective-permute-start.6 = (f32[1,7,32,128]{3,2,1,0:T(8,128)S(1)}, f32[1,7,32,128]{3,2,1,0:T(8,128)S(1)}, u32[]{:S(2)}, u32[]{:S(2)}) collective-permute-start(f32[1,7,32,128]{3,2,1,0:T(8,128)S(1)} %get-tuple-element.66), channel_id=1, source_target_pairs={{0,1},{1,2},{2,3},{3,4},{4,5},{5,6},{6,7},{7,8},{8,9},{9,10},{10,1... | collective-permute-start | bytes 344072 | tf_op jit(solution)/shard_map/ppermute | solution.py:18
  41.9 7.0 %collective-permute-start.7 = (f32[1,7,32,128]{3,2,1,0:T(8,128)S(1)}, f32[1,7,32,128]{3,2,1,0:T(8,128)S(1)}, u32[]{:S(2)}, u32[]{:S(2)}) collective-permute-start(f32[1,7,32,128]{3,2,1,0:T(8,128)S(1)} %get-tuple-element.67), channel_id=1, source_target_pairs={{1,0},{2,1},{3,2},{4,3},{5,4},{6,5},{7,6},{8,7},{9,8},{10,9},{11,1... | collective-permute-start | bytes 344072 | tf_op jit(solution)/shard_map/ppermute | solution.py:19
  50.0 1.7 %copy-start.8 = (f32[1,4,2048]{2,1,0:T(4,128)S(1)}, f32[1,4,2048]{2,1,0:T(4,128)}, u32[]{:S(2)}) copy-start(f32[1,4,2048]{2,1,0:T(4,128)} %param.19) | copy-start | bytes 98308
  50.0 5.0 %copy-start.5 = (f32[1,8,32,128]{3,2,1,0:T(8,128)S(1)}, f32[1,8,32,128]{3,2,1,0:T(8,128)}, u32[]{:S(2)}) copy-start(f32[1,8,32,128]{3,2,1,0:T(8,128)} %param.14) | copy-start | bytes 393220
  50.0 5.0 %copy-start.10 = (f32[1,8,32,128]{3,2,1,0:T(8,128)S(1)}, f32[1,8,32,128]{3,2,1,0:T(8,128)}, u32[]{:S(2)}) copy-start(f32[1,8,32,128]{3,2,1,0:T(8,128)} %param.15) | copy-start | bytes 393220
  56.4 8.7 %collective-permute-start.8 = (f32[1,7,32,128]{3,2,1,0:T(8,128)S(1)}, f32[1,7,32,128]{3,2,1,0:T(8,128)S(1)}, u32[]{:S(2)}, u32[]{:S(2)}) collective-permute-start(f32[1,7,32,128]{3,2,1,0:T(8,128)S(1)} %get-tuple-element.62), channel_id=1, source_target_pairs={{0,1},{1,2},{2,3},{3,4},{4,5},{5,6},{6,7},{7,8},{8,9},{9,10},{10,1... | collective-permute-start | bytes 344072 | tf_op jit(solution)/shard_map/ppermute | solution.py:18
  58.3 7.0 %collective-permute-start.9 = (f32[1,7,32,128]{3,2,1,0:T(8,128)S(1)}, f32[1,7,32,128]{3,2,1,0:T(8,128)S(1)}, u32[]{:S(2)}, u32[]{:S(2)}) collective-permute-start(f32[1,7,32,128]{3,2,1,0:T(8,128)S(1)} %get-tuple-element.63), channel_id=1, source_target_pairs={{1,0},{2,1},{3,2},{4,3},{5,4},{6,5},{7,6},{8,7},{9,8},{10,9},{11,1... | collective-permute-start | bytes 344072 | tf_op jit(solution)/shard_map/ppermute | solution.py:19
  61.1 3.3 %collective-permute-start.10 = (f32[1]{0:T(128)}, f32[1]{0:T(128)}, u32[]{:S(2)}, u32[]{:S(2)}) collective-permute-start(f32[1]{0:T(128)} %bitcast.26), channel_id=1, source_target_pairs={{0,2},{1,3},{2,0},{3,1},{4,6},{5,7},{6,4},{7,5},{8,10},{9,11},{10,... | collective-permute-start | bytes 20 | tf_op jit(solution)/shard_map/ppermute | solution.py:36
  66.9 9.7 %collective-permute-start.11 = (f32[1,7,32,128]{3,2,1,0:T(8,128)S(1)}, f32[1,7,32,128]{3,2,1,0:T(8,128)S(1)}, u32[]{:S(2)}, u32[]{:S(2)}) collective-permute-start(f32[1,7,32,128]{3,2,1,0:T(8,128)S(1)} %get-tuple-element.60), channel_id=1, source_target_pairs={{0,1},{1,2},{2,3},{3,4},{4,5},{5,6},{6,7},{7,8},{8,9},{9,10},{10,1... | collective-permute-start | bytes 344072 | tf_op jit(solution)/shard_map/ppermute | solution.py:18
  70.9 6.1 %collective-permute-start.12 = (f32[1,7,32,128]{3,2,1,0:T(8,128)S(1)}, f32[1,7,32,128]{3,2,1,0:T(8,128)S(1)}, u32[]{:S(2)}, u32[]{:S(2)}) collective-permute-start(f32[1,7,32,128]{3,2,1,0:T(8,128)S(1)} %get-tuple-element.61), channel_id=1, source_target_pairs={{1,0},{2,1},{3,2},{4,3},{5,4},{6,5},{7,6},{8,7},{9,8},{10,9},{11,1... | collective-permute-start | bytes 344072 | tf_op jit(solution)/shard_map/ppermute | solution.py:19
  73.3 2.6 %collective-permute-start.13 = (f32[1]{0:T(128)}, f32[1]{0:T(128)}, u32[]{:S(2)}, u32[]{:S(2)}) collective-permute-start(f32[1]{0:T(128)} %add.821), channel_id=1, source_target_pairs={{0,4},{1,5},{2,6},{3,7},{4,0},{5,1},{6,2},{7,3},{8,12},{9,13},{10,... | collective-permute-start | bytes 20 | tf_op jit(solution)/shard_map/ppermute | solution.py:36
  78.5 18.2 %copy-start.3 = (f32[1,8,32,128]{3,2,1,0:T(8,128)}, f32[1,8,32,128]{3,2,1,0:T(8,128)S(1)}, u32[]{:S(2)}) copy-start(f32[1,8,32,128]{3,2,1,0:T(8,128)S(1)} %fusion.40) | copy-start | bytes 393220
  78.5 11.5 %collective-permute-start.14 = (f32[1,7,32,128]{3,2,1,0:T(8,128)S(1)}, f32[1,7,32,128]{3,2,1,0:T(8,128)S(1)}, u32[]{:S(2)}, u32[]{:S(2)}) collective-permute-start(f32[1,7,32,128]{3,2,1,0:T(8,128)S(1)} %get-tuple-element.58), channel_id=1, source_target_pairs={{0,1},{1,2},{2,3},{3,4},{4,5},{5,6},{6,7},{7,8},{8,9},{9,10},{10,1... | collective-permute-start | bytes 344072 | tf_op jit(solution)/shard_map/ppermute | solution.py:18
  82.7 7.3 %collective-permute-start.15 = (f32[1,7,32,128]{3,2,1,0:T(8,128)S(1)}, f32[1,7,32,128]{3,2,1,0:T(8,128)S(1)}, u32[]{:S(2)}, u32[]{:S(2)}) collective-permute-start(f32[1,7,32,128]{3,2,1,0:T(8,128)S(1)} %get-tuple-element.59), channel_id=1, source_target_pairs={{1,0},{2,1},{3,2},{4,3},{5,4},{6,5},{7,6},{8,7},{9,8},{10,9},{11,1... | collective-permute-start | bytes 344072 | tf_op jit(solution)/shard_map/ppermute | solution.py:19
  85.3 4.0 %collective-permute-start.16 = (f32[1]{0:T(128)}, f32[1]{0:T(128)}, u32[]{:S(2)}, u32[]{:S(2)}) collective-permute-start(f32[1]{0:T(128)} %add.845), channel_id=1, source_target_pairs={{0,8},{1,9},{2,10},{3,11},{4,12},{5,13},{6,14},{7,15},{8,0},{9,1},... | collective-permute-start | bytes 20 | tf_op jit(solution)/shard_map/ppermute | solution.py:36
  90.2 6.4 %copy-start.2 = (f32[8,32,128]{2,1,0:T(8,128)S(1)}, f32[8,32,128]{2,1,0:T(8,128)}, u32[]{:S(2)}) copy-start(f32[8,32,128]{2,1,0:T(8,128)} %param.10) | copy-start | bytes 393220
  91.6 6.5 %copy-start.6 = (f32[1,8,32,128]{3,2,1,0:T(8,128)}, f32[1,8,32,128]{3,2,1,0:T(8,128)S(1)}, u32[]{:S(2)}) copy-start(f32[1,8,32,128]{3,2,1,0:T(8,128)S(1)} %fusion.37) | copy-start | bytes 393220
  91.6 5.8 %collective-permute-start.17 = (f32[1]{0:T(128)}, f32[1]{0:T(128)}, u32[]{:S(2)}, u32[]{:S(2)}) collective-permute-start(f32[1]{0:T(128)} %add.869), channel_id=1, source_target_pairs={{0,1},{1,0},{2,3},{3,2},{4,5},{5,4},{6,7},{7,6},{8,9},{9,8},{10,11... | collective-permute-start | bytes 20 | tf_op jit(solution)/shard_map/ppermute | solution.py:36

commit v5 on v4

--- a/solution.py
+++ b/solution.py
@@ -116,19 +116,28 @@
     receiver_owned = (receiver_local >= 0) & (receiver_local < cells)
     receiver_row = jnp.where(receiver_owned, receiver_local // cz, -1)
     receiver_col = receiver_local % cz
-    row_pick = (receiver_row[:, :, None] == jnp.arange(rows)[None, None, :]).astype(jnp.float32)
+    row_pick = (receiver_row[:, :, None] == jnp.arange(rows)[None, None, :]).astype(jnp.bfloat16)
     col_pick = receiver_col[:, :, None] == jnp.arange(cz)[None, None, :]
 
+    def split3(values):
+        high = lax.reduce_precision(values, exponent_bits=8, mantissa_bits=7)
+        rest = values - high
+        middle = lax.reduce_precision(rest, exponent_bits=8, mantissa_bits=7)
+        low = lax.reduce_precision(rest - middle, exponent_bits=8, mantissa_bits=7)
+        return jnp.concatenate([high, middle, low], axis=-1).astype(jnp.bfloat16)
+
+    def join3(values):
+        return (values[..., :cz] + values[..., cz : 2 * cz]) + values[..., 2 * cz :]
+
     def sample(field):
-        picked = jnp.einsum(
-            "srk,skz->srz", row_pick, field.reshape(shots, rows, cz), precision=lax.Precision.HIGHEST
-        )
-        return jnp.sum(jnp.where(col_pick, picked, 0.0), axis=2)
+        pieces = split3(field.reshape(shots, rows, cz))
+        picked = jnp.einsum("srk,skz->srz", row_pick, pieces, preferred_element_type=jnp.float32)
+        return jnp.sum(jnp.where(col_pick, join3(picked), 0.0), axis=2)
 
     def inject(field, amounts):
         spread = jnp.where(col_pick, amounts[:, :, None], 0.0)
-        added = jnp.einsum("srk,srz->skz", row_pick, spread, precision=lax.Precision.HIGHEST)
-        return field + added.reshape(shape)
+        added = jnp.einsum("srk,srz->skz", row_pick, split3(spread), preferred_element_type=jnp.float32)
+        return field + join3(added).reshape(shape)
 
     before, current = (wave_prev, wave_now)
     laps = []

time: 99.9 us -> 107 us (1.071)
  other arithmetic: 11.2 us -> 19.8 us
  matrix products: 11.7 us -> 7.51 us
  waiting for transfers between devices: 14.1 us -> 16.1 us
  starting transfers between devices: 52.3 us -> 53.4 us
    dot_general x8, matrix products: 11.7 us -> 7.51 us  [the longest x4 4.42 us: inject(): jnp.einsum('srk,srz->skz', row_pick, split3(spread), preferred_element_ty...]
    another operation x0 -> x5, other arithmetic: none -> 3.4 us
    ppermute x7, waiting for transfers between devices: 9.1 us -> 11.6 us  [extended(): after = lax.ppermute(first, 'mp', down)]
    add x0 -> x7, other arithmetic: none -> 2.04 us  [the longest x3 1.96 us: inject(): return field + join3(added).reshape(shape)]
    reduce_sum x0 -> x1, other arithmetic: none -> 1.57 us  [sample(): return jnp.sum(jnp.where(col_pick, join3(picked), 0.0), axis=2)]
    add x4, other arithmetic: 3.93 us -> 5.22 us  [local(): following = following + jnp.where(source_hit, amount, 0.0)]
  transfers between devices with their start and end apart: 18 -> 18, of which waited for: 10 -> 9; matrix products, arithmetic and copies ran while one was open for 8% -> 5% of each run, Pallas kernels for 0% -> 0%
where the time goes in v5:
time: 107 us; the launch traced here: 106 us
  starting transfers between devices  53.4 us (50%)
  other arithmetic  19.8 us (19%)
  waiting for transfers between devices  16.1 us (15%)
  between operations  8.25 us (8%)
  matrix products  7.51 us (7%)
    ppermute x7, starting transfers between devices, extended(): before = lax.ppermute(last, 'mp', up)  23.5 us
    ppermute x7, starting transfers between devices, extended(): after = lax.ppermute(first, 'mp', down)  15.7 us
    ppermute x4, starting transfers between devices, butterfly_round(): return values + lax.ppermute(values, axis, pairs)  14.3 us
    ppermute x7, waiting for transfers between devices, extended(): after = lax.ppermute(first, 'mp', down)  11.6 us
    add x4, other arithmetic, local(): following = following + jnp.where(source_hit, amount, 0.0)  5.22 us
    dot_general x4, matrix products, inject(): jnp.einsum('srk,srz->skz', row_pick, split3(spread), preferred_element_ty...  4.42 us
    ppermute x7, waiting for transfers between devices, extended(): before = lax.ppermute(last, 'mp', up)  3.87 us
    another operation x5, other arithmetic  3.4 us
  transfers between devices with their start and end apart: 18, of which 9 were waited for; matrix products, arithmetic and copies ran while one was open for 5% of the time, Pallas kernels for 0%

profile of v5, /device:TPU:1, one launch (start us, length us, event | category | flops | bytes accessed | tf_op | source)
XLA Modules:
  0.0 106.2 jit_solution(9984646117242607172)
XLA Ops:
  0.7 1.2 %bitcast_multiply_fusion.8 = (f32[1,8,32,128]{3,2,1,0:T(8,128)S(1)}, f32[8,32,128]{2,1,0:T(8,128)S(1)}) fusion(f32[1,8,32,128]{3,2,1,0:T(8,128)} %param.14, f32[8,32,128]{2,1,0:T(8,128)} %param.11, f32[8,32,128]{2,1,0:T(8,128)} %param.10), kind=kLoop, calls=%fused_computation.961 | loop fusion | flops 98304 | bytes 655360 | tf_op jit(solution)/shard_map/mul | solution.py:99
  1.8 1.0 pad_maximum_fusion.1
  2.9 2.0 %collective-permute-start.1 = (f32[3,7,32,128]{3,2,1,0:T(8,128)S(1)}, f32[3,7,32,128]{3,2,1,0:T(8,128)S(1)}, u32[]{:S(2)}, u32[]{:S(2)}) collective-permute-start(f32[3,7,32,128]{3,2,1,0:T(8,128)S(1)} %get-tuple-element.46), channel_id=1, source_target_pairs={{1,0},{2,1},{3,2},{4,3},{5,4},{6,5},{7,6},{8,7},{9,8},{10,9},{11,1... | collective-permute-start | bytes 1032200 | tf_op jit(solution)/shard_map/ppermute | solution.py:19
  4.9 4.5 %collective-permute-start = (f32[3,7,32,128]{3,2,1,0:T(8,128)S(1)}, f32[3,7,32,128]{3,2,1,0:T(8,128)S(1)}, u32[]{:S(2)}, u32[]{:S(2)}) collective-permute-start(f32[3,7,32,128]{3,2,1,0:T(8,128)S(1)} %get-tuple-element.47), channel_id=1, source_target_pairs={{0,1},{1,2},{2,3},{3,4},{4,5},{5,6},{6,7},{7,8},{8,9},{9,10},{10,1... | collective-permute-start | bytes 1032200 | tf_op jit(solution)/shard_map/ppermute | solution.py:18
  10.1 0.6 fusion.642
  10.8 0.5 fusion.370
  11.3 1.0 collective-permute-done.1
  12.4 3.9 %collective-permute-done = f32[3,7,32,128]{3,2,1,0:T(8,128)S(1)} collective-permute-done((f32[3,7,32,128]{3,2,1,0:T(8,128)S(1)}, f32[3,7,32,128]{3,2,1,0:T(8,128)S(1)}, u32[]{:S(2)}, u32[]{:S(2)}) %collective-permute-start) | collective-permute-done | bytes 344096 | tf_op jit(solution)/shard_map/ppermute | solution.py:18
  16.3 0.1 fusion.105
  16.4 1.0 fusion.606
  17.5 0.3 fusion.211
  17.8 4.4 %collective-permute-start.2 = (f32[1,7,32,128]{3,2,1,0:T(8,128)S(1)}, f32[1,7,32,128]{3,2,1,0:T(8,128)S(1)}, u32[]{:S(2)}, u32[]{:S(2)}) collective-permute-start(f32[1,7,32,128]{3,2,1,0:T(8,128)S(1)} %get-tuple-element.88), channel_id=1, source_target_pairs={{0,1},{1,2},{2,3},{3,4},{4,5},{5,6},{6,7},{7,8},{8,9},{9,10},{10,1... | collective-permute-start | bytes 344072 | tf_op jit(solution)/shard_map/ppermute | solution.py:18
  22.2 1.9 %collective-permute-start.3 = (f32[1,7,32,128]{3,2,1,0:T(8,128)S(1)}, f32[1,7,32,128]{3,2,1,0:T(8,128)S(1)}, u32[]{:S(2)}, u32[]{:S(2)}) collective-permute-start(f32[1,7,32,128]{3,2,1,0:T(8,128)S(1)} %get-tuple-element.89), channel_id=1, source_target_pairs={{1,0},{2,1},{3,2},{4,3},{5,4},{6,5},{7,6},{8,7},{9,8},{10,9},{11,1... | collective-permute-start | bytes 344072 | tf_op jit(solution)/shard_map/ppermute | solution.py:19
  24.1 0.1 fusion.113
  24.2 0.8 convolution_bitcast_fusion.2
  25.0 3.3 %collective-permute-done.3 = f32[1,7,32,128]{3,2,1,0:T(8,128)S(1)} collective-permute-done((f32[1,7,32,128]{3,2,1,0:T(8,128)S(1)}, f32[1,7,32,128]{3,2,1,0:T(8,128)S(1)}, u32[]{:S(2)}, u32[]{:S(2)}) %collective-permute-start.3) | collective-permute-done | bytes 114720 | tf_op jit(solution)/shard_map/ppermute | solution.py:19
  28.3 0.1 fusion.98
  28.5 1.0 fusion.608
  29.5 0.3 fusion.236
  29.8 1.9 %collective-permute-start.4 = (f32[1,7,32,128]{3,2,1,0:T(8,128)S(1)}, f32[1,7,32,128]{3,2,1,0:T(8,128)S(1)}, u32[]{:S(2)}, u32[]{:S(2)}) collective-permute-start(f32[1,7,32,128]{3,2,1,0:T(8,128)S(1)} %get-tuple-element.83), channel_id=1, source_target_pairs={{0,1},{1,2},{2,3},{3,4},{4,5},{5,6},{6,7},{7,8},{8,9},{9,10},{10,1... | collective-permute-start | bytes 344072 | tf_op jit(solution)/shard_map/ppermute | solution.py:18
  31.8 2.4 %collective-permute-start.5 = (f32[1,7,32,128]{3,2,1,0:T(8,128)S(1)}, f32[1,7,32,128]{3,2,1,0:T(8,128)S(1)}, u32[]{:S(2)}, u32[]{:S(2)}) collective-permute-start(f32[1,7,32,128]{3,2,1,0:T(8,128)S(1)} %get-tuple-element.84), channel_id=1, source_target_pairs={{1,0},{2,1},{3,2},{4,3},{5,4},{6,5},{7,6},{8,7},{9,8},{10,9},{11,1... | collective-permute-start | bytes 344072 | tf_op jit(solution)/shard_map/ppermute | solution.py:19
  34.2 0.8 convolution_bitcast_fusion.1
  35.0 2.9 %collective-permute-done.5 = f32[1,7,32,128]{3,2,1,0:T(8,128)S(1)} collective-permute-done((f32[1,7,32,128]{3,2,1,0:T(8,128)S(1)}, f32[1,7,32,128]{3,2,1,0:T(8,128)S(1)}, u32[]{:S(2)}, u32[]{:S(2)}) %collective-permute-start.5) | collective-permute-done | bytes 114720 | tf_op jit(solution)/shard_map/ppermute | solution.py:19
  37.9 0.1 fusion.91
  38.0 1.6 %fusion.610 = (f32[1,8,32,128]{3,2,1,0:T(8,128)S(1)}, f32[1,8,32,128]{3,2,1,0:T(8,128)}) fusion(f32[8,32,128]{2,1,0:T(8,128)S(1)} %get-tuple-element.45, f32[1,8,32,128]{3,2,1,0:T(8,128)S(1)} %get-tuple-element.42, f32[1,8,32,128]{3,2,1,0:T(8,128)S(1)} %get-tuple-element.40, f32[]{:T(128)} %bitcast.8, s32[]{:T(128)} %bitcast.5, ...), kind=kLoop, calls=%fused_computation.967 | loop fusion | flops 1441792 | bytes 1966248 | tf_op jit(solution)/shard_map/add | solution.py:150
  39.7 0.3 fusion.261
  40.0 1.9 %collective-permute-start.6 = (f32[1,7,32,128]{3,2,1,0:T(8,128)S(1)}, f32[1,7,32,128]{3,2,1,0:T(8,128)S(1)}, u32[]{:S(2)}, u32[]{:S(2)}) collective-permute-start(f32[1,7,32,128]{3,2,1,0:T(8,128)S(1)} %get-tuple-element.75), channel_id=1, source_target_pairs={{0,1},{1,2},{2,3},{3,4},{4,5},{5,6},{6,7},{7,8},{8,9},{9,10},{10,1... | collective-permute-start | bytes 344072 | tf_op jit(solution)/shard_map/ppermute | solution.py:18
  42.0 2.6 %collective-permute-start.7 = (f32[1,7,32,128]{3,2,1,0:T(8,128)S(1)}, f32[1,7,32,128]{3,2,1,0:T(8,128)S(1)}, u32[]{:S(2)}, u32[]{:S(2)}) collective-permute-start(f32[1,7,32,128]{3,2,1,0:T(8,128)S(1)} %get-tuple-element.76), channel_id=1, source_target_pairs={{1,0},{2,1},{3,2},{4,3},{5,4},{6,5},{7,6},{8,7},{9,8},{10,9},{11,1... | collective-permute-start | bytes 344072 | tf_op jit(solution)/shard_map/ppermute | solution.py:19
  44.6 0.8 convolution_bitcast_fusion
  45.3 3.6 %collective-permute-done.7 = f32[1,7,32,128]{3,2,1,0:T(8,128)S(1)} collective-permute-done((f32[1,7,32,128]{3,2,1,0:T(8,128)S(1)}, f32[1,7,32,128]{3,2,1,0:T(8,128)S(1)}, u32[]{:S(2)}, u32[]{:S(2)}) %collective-permute-start.7) | collective-permute-done | bytes 114720 | tf_op jit(solution)/shard_map/ppermute | solution.py:19
  48.9 0.1 fusion.84
  49.1 1.6 %fusion.612 = (f32[1,8,32,128]{3,2,1,0:T(8,128)S(1)}, f32[1,8,32,128]{3,2,1,0:T(8,128)}) fusion(f32[8,32,128]{2,1,0:T(8,128)S(1)} %get-tuple-element.45, f32[1,8,32,128]{3,2,1,0:T(8,128)S(1)} %get-tuple-element.40, f32[1,8,32,128]{3,2,1,0:T(8,128)S(1)} %get-tuple-element.36, f32[]{:T(128)} %bitcast.9, s32[]{:T(128)} %bitcast.5, ...), kind=kLoop, calls=%fused_computation.969 | loop fusion | flops 1441792 | bytes 1966248 | tf_op jit(solution)/shard_map/add | solution.py:150
  50.7 0.8 convolution_bitcast_fusion.3
  51.5 1.6 %fusion.47 = (f32[2048]{0:T(1024)S(1)}, f32[2048]{0:T(1024)S(1)}, f32[2048]{0:T(1024)S(1)}, f32[2048]{0:T(1024)S(1)}) fusion(f32[1,2048,384]{1,2,0:T(8,128)S(1)} %convolution_bitcast_fusion.1, s32[2048]{0:T(1024)S(1)} %bitcast.145, f32[1,2048,384]{1,2,0:T(8,128)S(1)} %convolution_bitcast_fusion, f32[1,2048,384]{1,2,0:T(8,128)S(1)} %convolution_bitcast_fusion.2, ...), kind=kLoop, calls=%fused_computation.64 | loop fusion | flops 4448256 | bytes 12623872 | tf_op jit(solution)/shard_map/reduce_sum | solution.py:135
  53.1 0.7 multiply_reduce_fusion.1
  53.9 3.2 %reduce-precision_convert_fusion.1 = (bf16[2048,128]{1,0:T(8,128)(2,1)}, bf16[2048,128]{1,0:T(8,128)(2,1)}, bf16[2048,128]{1,0:T(8,128)(2,1)}, bf16[2048,128]{1,...) fusion(f32[2048]{0:T(1024)S(1)} %bitcast.148, ...), kind=kLoop, calls=%fused_computation.32 | loop fusion | flops 9699328 | bytes 6332416 | tf_op jit(solution)/shard_map/convert
  57.1 1.1 %fusion.24 = f32[1,256,384]{2,1,0:T(8,128)S(1)} fusion(bf16[2048,128]{1,0:T(8,128)(2,1)S(1)} %get-tuple-element.114, bf16[2048,128]{1,0:T(8,128)(2,1)S(1)} %get-tuple-element.115, bf16[2048,128]{1,0:T(8,128)(2,1)S(1)} %get-tuple-element.116, s32[2048]{0:T(1024)S(1)} %bitcast.141), kind=kOutput, calls=%fused_computation.45 | convolution fusion | flops 407896064 | bytes 1974272 | tf_op jit(solution)/shard_map/srk,srz->skz/dot_general | solution.py:139
  60.8 1.3 %fusion.174 = f32[1,8,32,128]{3,2,1,0:T(8,128)S(1)} fusion(f32[1,8,32,128]{3,2,1,0:T(8,128)S(1)} %bitcast.135, f32[1,8,32,128]{3,2,1,0:T(8,128)} %param.15, f32[1,8,32,128]{3,2,1,0:T(8,128)S(1)} %get-tuple-element.55, f32[1,8,32,128]{3,2,1,0:T(8,128)S(1)} %get-tuple-element.54, f32[1,15,32,128]{3,2,1,0:T(8,128)S(1)} %fusion.113, ...), kind=kLoop, calls=%fused_computation.482 | loop fusion | flops 1277952 | bytes 1835008 | tf_op jit(solution)/shard_map/add | solution.py:140
  62.2 0.3 fusion.485
  62.6 1.1 %fusion.33 = f32[1,256,384]{2,1,0:T(8,128)S(1)} fusion(bf16[2048,128]{1,0:T(8,128)(2,1)S(1)} %copy-done.10, bf16[2048,128]{1,0:T(8,128)(2,1)S(1)} %copy-done.9, bf16[2048,128]{1,0:T(8,128)(2,1)S(1)} %copy-done.8, s32[2048]{0:T(1024)S(1)} %bitcast.142), kind=kOutput, calls=%fused_computation.48 | convolution fusion | flops 407896064 | bytes 1974272 | tf_op jit(solution)/shard_map/srk,srz->skz/dot_general | solution.py:139
  63.7 0.2 copy-done.7
  63.9 1.1 %fusion.30 = f32[1,256,384]{2,1,0:T(8,128)S(1)} fusion(bf16[2048,128]{1,0:T(8,128)(2,1)S(1)} %copy-done.5, bf16[2048,128]{1,0:T(8,128)(2,1)S(1)} %copy-done.6, bf16[2048,128]{1,0:T(8,128)(2,1)S(1)} %copy-done.7, s32[2048]{0:T(1024)S(1)} %bitcast.143), kind=kOutput, calls=%fused_computation.47 | convolution fusion | flops 407896064 | bytes 1974272 | tf_op jit(solution)/shard_map/srk,srz->skz/dot_general | solution.py:139
  65.0 1.9 %collective-permute-start.8 = (f32[1,7,32,128]{3,2,1,0:T(8,128)S(1)}, f32[1,7,32,128]{3,2,1,0:T(8,128)S(1)}, u32[]{:S(2)}, u32[]{:S(2)}) collective-permute-start(f32[1,7,32,128]{3,2,1,0:T(8,128)S(1)} %get-tuple-element.68), channel_id=1, source_target_pairs={{0,1},{1,2},{2,3},{3,4},{4,5},{5,6},{6,7},{7,8},{8,9},{9,10},{10,1... | collective-permute-start | bytes 344072 | tf_op jit(solution)/shard_map/ppermute | solution.py:18
  67.0 2.4 %collective-permute-start.9 = (f32[1,7,32,128]{3,2,1,0:T(8,128)S(1)}, f32[1,7,32,128]{3,2,1,0:T(8,128)S(1)}, u32[]{:S(2)}, u32[]{:S(2)}) collective-permute-start(f32[1,7,32,128]{3,2,1,0:T(8,128)S(1)} %get-tuple-element.69), channel_id=1, source_target_pairs={{1,0},{2,1},{3,2},{4,3},{5,4},{6,5},{7,6},{8,7},{9,8},{10,9},{11,1... | collective-permute-start | bytes 344072 | tf_op jit(solution)/shard_map/ppermute | solution.py:19
  69.4 1.1 %fusion.27 = f32[1,256,384]{2,1,0:T(8,128)S(1)} fusion(bf16[2048,128]{1,0:T(8,128)(2,1)S(1)} %get-tuple-element.111, bf16[2048,128]{1,0:T(8,128)(2,1)S(1)} %get-tuple-element.112, bf16[2048,128]{1,0:T(8,128)(2,1)S(1)} %copy-done.4, s32[2048]{0:T(1024)S(1)} %bitcast.144), kind=kOutput, calls=%fused_computation.46 | convolution fusion | flops 407896064 | bytes 1974272 | tf_op jit(solution)/shard_map/srk,srz->skz/dot_general | solution.py:139
  70.5 3.0 %collective-permute-start.10 = (f32[1]{0:T(128)}, f32[1]{0:T(128)}, u32[]{:S(2)}, u32[]{:S(2)}) collective-permute-start(f32[1]{0:T(128)} %bitcast.29), channel_id=1, source_target_pairs={{0,2},{1,3},{2,0},{3,1},{4,6},{5,7},{6,4},{7,5},{8,10},{9,11},{10,... | collective-permute-start | bytes 20 | tf_op jit(solution)/shard_map/ppermute | solution.py:36
  73.6 0.2 collective-permute-done.10
  74.4 0.1 fusion.77
  74.6 0.3 fusion.302
  74.9 4.6 %collective-permute-start.11 = (f32[1,7,32,128]{3,2,1,0:T(8,128)S(1)}, f32[1,7,32,128]{3,2,1,0:T(8,128)S(1)}, u32[]{:S(2)}, u32[]{:S(2)}) collective-permute-start(f32[1,7,32,128]{3,2,1,0:T(8,128)S(1)} %get-tuple-element.66), channel_id=1, source_target_pairs={{0,1},{1,2},{2,3},{3,4},{4,5},{5,6},{6,7},{7,8},{8,9},{9,10},{10,1... | collective-permute-start | bytes 344072 | tf_op jit(solution)/shard_map/ppermute | solution.py:18
  79.5 1.9 %collective-permute-start.12 = (f32[1,7,32,128]{3,2,1,0:T(8,128)S(1)}, f32[1,7,32,128]{3,2,1,0:T(8,128)S(1)}, u32[]{:S(2)}, u32[]{:S(2)}) collective-permute-start(f32[1,7,32,128]{3,2,1,0:T(8,128)S(1)} %get-tuple-element.67), channel_id=1, source_target_pairs={{1,0},{2,1},{3,2},{4,3},{5,4},{6,5},{7,6},{8,7},{9,8},{10,9},{11,1... | collective-permute-start | bytes 344072 | tf_op jit(solution)/shard_map/ppermute | solution.py:19
  81.4 0.3 fusion.508
  81.7 2.1 %collective-permute-start.13 = (f32[1]{0:T(128)}, f32[1]{0:T(128)}, u32[]{:S(2)}, u32[]{:S(2)}) collective-permute-start(f32[1]{0:T(128)} %add.877), channel_id=1, source_target_pairs={{0,4},{1,5},{2,6},{3,7},{4,0},{5,1},{6,2},{7,3},{8,12},{9,13},{10,... | collective-permute-start | bytes 20 | tf_op jit(solution)/shard_map/ppermute | solution.py:36
  83.8 0.3 collective-permute-done.13
  84.8 0.8 collective-permute-done.12
  85.6 0.1 fusion.70
  85.8 0.3 fusion.330
  86.2 4.3 %collective-permute-start.14 = (f32[1,7,32,128]{3,2,1,0:T(8,128)S(1)}, f32[1,7,32,128]{3,2,1,0:T(8,128)S(1)}, u32[]{:S(2)}, u32[]{:S(2)}) collective-permute-start(f32[1,7,32,128]{3,2,1,0:T(8,128)S(1)} %get-tuple-element.64), channel_id=1, source_target_pairs={{0,1},{1,2},{2,3},{3,4},{4,5},{5,6},{6,7},{7,8},{8,9},{9,10},{10,1... | collective-permute-start | bytes 344072 | tf_op jit(solution)/shard_map/ppermute | solution.py:18
  90.5 2.5 %collective-permute-start.15 = (f32[1,7,32,128]{3,2,1,0:T(8,128)S(1)}, f32[1,7,32,128]{3,2,1,0:T(8,128)S(1)}, u32[]{:S(2)}, u32[]{:S(2)}) collective-permute-start(f32[1,7,32,128]{3,2,1,0:T(8,128)S(1)} %get-tuple-element.65), channel_id=1, source_target_pairs={{1,0},{2,1},{3,2},{4,3},{5,4},{6,5},{7,6},{8,7},{9,8},{10,9},{11,1... | collective-permute-start | bytes 344072 | tf_op jit(solution)/shard_map/ppermute | solution.py:19
  92.9 0.3 fusion.342
  93.2 3.7 %collective-permute-start.16 = (f32[1]{0:T(128)}, f32[1]{0:T(128)}, u32[]{:S(2)}, u32[]{:S(2)}) collective-permute-start(f32[1]{0:T(128)} %add.903), channel_id=1, source_target_pairs={{0,8},{1,9},{2,10},{3,11},{4,12},{5,13},{6,14},{7,15},{8,0},{9,1},... | collective-permute-start | bytes 20 | tf_op jit(solution)/shard_map/ppermute | solution.py:36
  96.9 0.2 collective-permute-done.16
  98.0 1.0 bitcast_multiply_fusion
  99.0 5.4 %collective-permute-start.17 = (f32[1]{0:T(128)}, f32[1]{0:T(128)}, u32[]{:S(2)}, u32[]{:S(2)}) collective-permute-start(f32[1]{0:T(128)} %add.929), channel_id=1, source_target_pairs={{0,1},{1,0},{2,3},{3,2},{4,5},{5,4},{6,7},{7,6},{8,9},{9,8},{10,11... | collective-permute-start | bytes 20 | tf_op jit(solution)/shard_map/ppermute | solution.py:36
  (74 shorter events, 1.0 us)
Async XLA Ops:
  0.6 10.1 %copy-start = (f32[8,32,128]{2,1,0:T(8,128)S(1)}, f32[8,32,128]{2,1,0:T(8,128)}, u32[]{:S(2)}) copy-start(f32[8,32,128]{2,1,0:T(8,128)} %param.11) | copy-start | bytes 393220
  0.6 10.1 %copy-start.1 = (f32[1,8,32,128]{3,2,1,0:T(8,128)S(1)}, f32[1,8,32,128]{3,2,1,0:T(8,128)}, u32[]{:S(2)}) copy-start(f32[1,8,32,128]{3,2,1,0:T(8,128)} %param.13) | copy-start | bytes 393220
  0.7 9.4 %copy-start.17 = (f32[1,4]{1,0:T(1,128)S(1)}, f32[1,4]{1,0:T(1,128)}, u32[]{:S(2)}) copy-start(f32[1,4]{1,0:T(1,128)} %param.17) | copy-start | bytes 52
  0.7 10.0 %copy-start.15 = (s32[1,2048]{1,0:T(1,128)S(1)}, s32[1,2048]{1,0:T(1,128)}, u32[]{:S(2)}) copy-start(s32[1,2048]{1,0:T(1,128)} %param.18) | copy-start | bytes 24580
  2.9 9.5 %collective-permute-start.1 = (f32[3,7,32,128]{3,2,1,0:T(8,128)S(1)}, f32[3,7,32,128]{3,2,1,0:T(8,128)S(1)}, u32[]{:S(2)}, u32[]{:S(2)}) collective-permute-start(f32[3,7,32,128]{3,2,1,0:T(8,128)S(1)} %get-tuple-element.46), channel_id=1, source_target_pairs={{1,0},{2,1},{3,2},{4,3},{5,4},{6,5},{7,6},{8,7},{9,8},{10,9},{11,1... | collective-permute-start | bytes 1032200 | tf_op jit(solution)/shard_map/ppermute | solution.py:19
  4.9 11.3 %collective-permute-start = (f32[3,7,32,128]{3,2,1,0:T(8,128)S(1)}, f32[3,7,32,128]{3,2,1,0:T(8,128)S(1)}, u32[]{:S(2)}, u32[]{:S(2)}) collective-permute-start(f32[3,7,32,128]{3,2,1,0:T(8,128)S(1)} %get-tuple-element.47), channel_id=1, source_target_pairs={{0,1},{1,2},{2,3},{3,4},{4,5},{5,6},{6,7},{7,8},{8,9},{9,10},{10,1... | collective-permute-start | bytes 1032200 | tf_op jit(solution)/shard_map/ppermute | solution.py:18
  11.3 5.1 %copy-start.14 = (f32[1,8,32,128]{3,2,1,0:T(8,128)S(1)}, f32[1,8,32,128]{3,2,1,0:T(8,128)}, u32[]{:S(2)}) copy-start(f32[1,8,32,128]{3,2,1,0:T(8,128)} %param.12) | copy-start | bytes 393220
  17.8 7.2 %collective-permute-start.2 = (f32[1,7,32,128]{3,2,1,0:T(8,128)S(1)}, f32[1,7,32,128]{3,2,1,0:T(8,128)S(1)}, u32[]{:S(2)}, u32[]{:S(2)}) collective-permute-start(f32[1,7,32,128]{3,2,1,0:T(8,128)S(1)} %get-tuple-element.88), channel_id=1, source_target_pairs={{0,1},{1,2},{2,3},{3,4},{4,5},{5,6},{6,7},{7,8},{8,9},{9,10},{10,1... | collective-permute-start | bytes 344072 | tf_op jit(solution)/shard_map/ppermute | solution.py:18
  22.2 6.1 %collective-permute-start.3 = (f32[1,7,32,128]{3,2,1,0:T(8,128)S(1)}, f32[1,7,32,128]{3,2,1,0:T(8,128)S(1)}, u32[]{:S(2)}, u32[]{:S(2)}) collective-permute-start(f32[1,7,32,128]{3,2,1,0:T(8,128)S(1)} %get-tuple-element.89), channel_id=1, source_target_pairs={{1,0},{2,1},{3,2},{4,3},{5,4},{6,5},{7,6},{8,7},{9,8},{10,9},{11,1... | collective-permute-start | bytes 344072 | tf_op jit(solution)/shard_map/ppermute | solution.py:19
  29.8 5.1 %collective-permute-start.4 = (f32[1,7,32,128]{3,2,1,0:T(8,128)S(1)}, f32[1,7,32,128]{3,2,1,0:T(8,128)S(1)}, u32[]{:S(2)}, u32[]{:S(2)}) collective-permute-start(f32[1,7,32,128]{3,2,1,0:T(8,128)S(1)} %get-tuple-element.83), channel_id=1, source_target_pairs={{0,1},{1,2},{2,3},{3,4},{4,5},{5,6},{6,7},{7,8},{8,9},{9,10},{10,1... | collective-permute-start | bytes 344072 | tf_op jit(solution)/shard_map/ppermute | solution.py:18
  31.8 6.1 %collective-permute-start.5 = (f32[1,7,32,128]{3,2,1,0:T(8,128)S(1)}, f32[1,7,32,128]{3,2,1,0:T(8,128)S(1)}, u32[]{:S(2)}, u32[]{:S(2)}) collective-permute-start(f32[1,7,32,128]{3,2,1,0:T(8,128)S(1)} %get-tuple-element.84), channel_id=1, source_target_pairs={{1,0},{2,1},{3,2},{4,3},{5,4},{6,5},{7,6},{8,7},{9,8},{10,9},{11,1... | collective-permute-start | bytes 344072 | tf_op jit(solution)/shard_map/ppermute | solution.py:19
  40.0 5.3 %collective-permute-start.6 = (f32[1,7,32,128]{3,2,1,0:T(8,128)S(1)}, f32[1,7,32,128]{3,2,1,0:T(8,128)S(1)}, u32[]{:S(2)}, u32[]{:S(2)}) collective-permute-start(f32[1,7,32,128]{3,2,1,0:T(8,128)S(1)} %get-tuple-element.75), channel_id=1, source_target_pairs={{0,1},{1,2},{2,3},{3,4},{4,5},{5,6},{6,7},{7,8},{8,9},{9,10},{10,1... | collective-permute-start | bytes 344072 | tf_op jit(solution)/shard_map/ppermute | solution.py:18
  42.0 7.0 %collective-permute-start.7 = (f32[1,7,32,128]{3,2,1,0:T(8,128)S(1)}, f32[1,7,32,128]{3,2,1,0:T(8,128)S(1)}, u32[]{:S(2)}, u32[]{:S(2)}) collective-permute-start(f32[1,7,32,128]{3,2,1,0:T(8,128)S(1)} %get-tuple-element.76), channel_id=1, source_target_pairs={{1,0},{2,1},{3,2},{4,3},{5,4},{6,5},{7,6},{8,7},{9,8},{10,9},{11,1... | collective-permute-start | bytes 344072 | tf_op jit(solution)/shard_map/ppermute | solution.py:19
  51.5 1.6 %copy-start.16 = (f32[1,4,2048]{2,1,0:T(4,128)S(1)}, f32[1,4,2048]{2,1,0:T(4,128)}, u32[]{:S(2)}) copy-start(f32[1,4,2048]{2,1,0:T(4,128)} %param.19) | copy-start | bytes 98308
  57.1 3.7 %copy-start.2 = (f32[1,8,32,128]{3,2,1,0:T(8,128)S(1)}, f32[1,8,32,128]{3,2,1,0:T(8,128)}, u32[]{:S(2)}) copy-start(f32[1,8,32,128]{3,2,1,0:T(8,128)} %param.14) | copy-start | bytes 393220
  60.8 1.7 %copy-start.8 = (bf16[2048,128]{1,0:T(8,128)(2,1)S(1)}, bf16[2048,128]{1,0:T(8,128)(2,1)}, u32[]{:S(2)}) copy-start(bf16[2048,128]{1,0:T(8,128)(2,1)} %get-tuple-element.96) | copy-start | bytes 1572868
  60.8 1.7 %copy-start.9 = (bf16[2048,128]{1,0:T(8,128)(2,1)S(1)}, bf16[2048,128]{1,0:T(8,128)(2,1)}, u32[]{:S(2)}) copy-start(bf16[2048,128]{1,0:T(8,128)(2,1)} %get-tuple-element.97) | copy-start | bytes 1572868
  60.8 1.7 %copy-start.10 = (bf16[2048,128]{1,0:T(8,128)(2,1)S(1)}, bf16[2048,128]{1,0:T(8,128)(2,1)}, u32[]{:S(2)}) copy-start(bf16[2048,128]{1,0:T(8,128)(2,1)} %get-tuple-element.98) | copy-start | bytes 1572868
  62.5 1.2 %copy-start.5 = (bf16[2048,128]{1,0:T(8,128)(2,1)S(1)}, bf16[2048,128]{1,0:T(8,128)(2,1)}, u32[]{:S(2)}) copy-start(bf16[2048,128]{1,0:T(8,128)(2,1)} %get-tuple-element.108) | copy-start | bytes 1572868
  62.6 1.2 %copy-start.6 = (bf16[2048,128]{1,0:T(8,128)(2,1)S(1)}, bf16[2048,128]{1,0:T(8,128)(2,1)}, u32[]{:S(2)}) copy-start(bf16[2048,128]{1,0:T(8,128)(2,1)} %get-tuple-element.109) | copy-start | bytes 1572868
  62.6 1.3 %copy-start.7 = (bf16[2048,128]{1,0:T(8,128)(2,1)S(1)}, bf16[2048,128]{1,0:T(8,128)(2,1)}, u32[]{:S(2)}) copy-start(bf16[2048,128]{1,0:T(8,128)(2,1)} %get-tuple-element.110) | copy-start | bytes 1572868
  63.9 5.5 %copy-start.4 = (bf16[2048,128]{1,0:T(8,128)(2,1)S(1)}, bf16[2048,128]{1,0:T(8,128)(2,1)}, u32[]{:S(2)}) copy-start(bf16[2048,128]{1,0:T(8,128)(2,1)} %get-tuple-element.113) | copy-start | bytes 1572868
  65.0 9.3 %collective-permute-start.8 = (f32[1,7,32,128]{3,2,1,0:T(8,128)S(1)}, f32[1,7,32,128]{3,2,1,0:T(8,128)S(1)}, u32[]{:S(2)}, u32[]{:S(2)}) collective-permute-start(f32[1,7,32,128]{3,2,1,0:T(8,128)S(1)} %get-tuple-element.68), channel_id=1, source_target_pairs={{0,1},{1,2},{2,3},{3,4},{4,5},{5,6},{6,7},{7,8},{8,9},{9,10},{10,1... | collective-permute-start | bytes 344072 | tf_op jit(solution)/shard_map/ppermute | solution.py:18
  67.0 7.4 %collective-permute-start.9 = (f32[1,7,32,128]{3,2,1,0:T(8,128)S(1)}, f32[1,7,32,128]{3,2,1,0:T(8,128)S(1)}, u32[]{:S(2)}, u32[]{:S(2)}) collective-permute-start(f32[1,7,32,128]{3,2,1,0:T(8,128)S(1)} %get-tuple-element.69), channel_id=1, source_target_pairs={{1,0},{2,1},{3,2},{4,3},{5,4},{6,5},{7,6},{8,7},{9,8},{10,9},{11,1... | collective-permute-start | bytes 344072 | tf_op jit(solution)/shard_map/ppermute | solution.py:19
  70.5 3.2 %collective-permute-start.10 = (f32[1]{0:T(128)}, f32[1]{0:T(128)}, u32[]{:S(2)}, u32[]{:S(2)}) collective-permute-start(f32[1]{0:T(128)} %bitcast.29), channel_id=1, source_target_pairs={{0,2},{1,3},{2,0},{3,1},{4,6},{5,7},{6,4},{7,5},{8,10},{9,11},{10,... | collective-permute-start | bytes 20 | tf_op jit(solution)/shard_map/ppermute | solution.py:36
  74.9 9.9 %collective-permute-start.11 = (f32[1,7,32,128]{3,2,1,0:T(8,128)S(1)}, f32[1,7,32,128]{3,2,1,0:T(8,128)S(1)}, u32[]{:S(2)}, u32[]{:S(2)}) collective-permute-start(f32[1,7,32,128]{3,2,1,0:T(8,128)S(1)} %get-tuple-element.66), channel_id=1, source_target_pairs={{0,1},{1,2},{2,3},{3,4},{4,5},{5,6},{6,7},{7,8},{8,9},{9,10},{10,1... | collective-permute-start | bytes 344072 | tf_op jit(solution)/shard_map/ppermute | solution.py:18
  79.5 6.1 %collective-permute-start.12 = (f32[1,7,32,128]{3,2,1,0:T(8,128)S(1)}, f32[1,7,32,128]{3,2,1,0:T(8,128)S(1)}, u32[]{:S(2)}, u32[]{:S(2)}) collective-permute-start(f32[1,7,32,128]{3,2,1,0:T(8,128)S(1)} %get-tuple-element.67), channel_id=1, source_target_pairs={{1,0},{2,1},{3,2},{4,3},{5,4},{6,5},{7,6},{8,7},{9,8},{10,9},{11,1... | collective-permute-start | bytes 344072 | tf_op jit(solution)/shard_map/ppermute | solution.py:19
  81.7 2.4 %collective-permute-start.13 = (f32[1]{0:T(128)}, f32[1]{0:T(128)}, u32[]{:S(2)}, u32[]{:S(2)}) collective-permute-start(f32[1]{0:T(128)} %add.877), channel_id=1, source_target_pairs={{0,4},{1,5},{2,6},{3,7},{4,0},{5,1},{6,2},{7,3},{8,12},{9,13},{10,... | collective-permute-start | bytes 20 | tf_op jit(solution)/shard_map/ppermute | solution.py:36
  86.1 11.8 %copy-start.3 = (f32[1,8,32,128]{3,2,1,0:T(8,128)}, f32[1,8,32,128]{3,2,1,0:T(8,128)S(1)}, u32[]{:S(2)}) copy-start(f32[1,8,32,128]{3,2,1,0:T(8,128)S(1)} %fusion.330) | copy-start | bytes 393220
  86.1 11.8 %copy-start.11 = (f32[8,32,128]{2,1,0:T(8,128)S(1)}, f32[8,32,128]{2,1,0:T(8,128)}, u32[]{:S(2)}) copy-start(f32[8,32,128]{2,1,0:T(8,128)} %param.10) | copy-start | bytes 393220
  86.1 11.8 %copy-start.12 = (f32[1,8,32,128]{3,2,1,0:T(8,128)S(1)}, f32[1,8,32,128]{3,2,1,0:T(8,128)}, u32[]{:S(2)}) copy-start(f32[1,8,32,128]{3,2,1,0:T(8,128)} %get-tuple-element.37) | copy-start | bytes 393220
  86.1 11.8 %copy-start.13 = (f32[1,8,32,128]{3,2,1,0:T(8,128)S(1)}, f32[1,8,32,128]{3,2,1,0:T(8,128)}, u32[]{:S(2)}) copy-start(f32[1,8,32,128]{3,2,1,0:T(8,128)} %get-tuple-element.35) | copy-start | bytes 393220
  86.2 11.6 %collective-permute-start.14 = (f32[1,7,32,128]{3,2,1,0:T(8,128)S(1)}, f32[1,7,32,128]{3,2,1,0:T(8,128)S(1)}, u32[]{:S(2)}, u32[]{:S(2)}) collective-permute-start(f32[1,7,32,128]{3,2,1,0:T(8,128)S(1)} %get-tuple-element.64), channel_id=1, source_target_pairs={{0,1},{1,2},{2,3},{3,4},{4,5},{5,6},{6,7},{7,8},{8,9},{9,10},{10,1... | collective-permute-start | bytes 344072 | tf_op jit(solution)/shard_map/ppermute | solution.py:18
  90.5 7.3 %collective-permute-start.15 = (f32[1,7,32,128]{3,2,1,0:T(8,128)S(1)}, f32[1,7,32,128]{3,2,1,0:T(8,128)S(1)}, u32[]{:S(2)}, u32[]{:S(2)}) collective-permute-start(f32[1,7,32,128]{3,2,1,0:T(8,128)S(1)} %get-tuple-element.65), channel_id=1, source_target_pairs={{1,0},{2,1},{3,2},{4,3},{5,4},{6,5},{7,6},{8,7},{9,8},{10,9},{11,1... | collective-permute-start | bytes 344072 | tf_op jit(solution)/shard_map/ppermute | solution.py:19
  93.2 3.9 %collective-permute-start.16 = (f32[1]{0:T(128)}, f32[1]{0:T(128)}, u32[]{:S(2)}, u32[]{:S(2)}) collective-permute-start(f32[1]{0:T(128)} %add.903), channel_id=1, source_target_pairs={{0,8},{1,9},{2,10},{3,11},{4,12},{5,13},{6,14},{7,15},{8,0},{9,1},... | collective-permute-start | bytes 20 | tf_op jit(solution)/shard_map/ppermute | solution.py:36
  99.0 5.4 %collective-permute-start.17 = (f32[1]{0:T(128)}, f32[1]{0:T(128)}, u32[]{:S(2)}, u32[]{:S(2)}) collective-permute-start(f32[1]{0:T(128)} %add.929), channel_id=1, source_target_pairs={{0,1},{1,0},{2,3},{3,2},{4,5},{5,4},{6,7},{7,6},{8,9},{9,8},{10,11... | collective-permute-start | bytes 20 | tf_op jit(solution)/shard_map/ppermute | solution.py:36

commit v6 on v5

--- a/solution.py
+++ b/solution.py
@@ -135,8 +135,14 @@
         return jnp.sum(jnp.where(col_pick, join3(picked), 0.0), axis=2)
 
     def inject(field, amounts):
-        spread = jnp.where(col_pick, amounts[:, :, None], 0.0)
-        added = jnp.einsum("srk,srz->skz", row_pick, split3(spread), preferred_element_type=jnp.float32)
+        high = lax.reduce_precision(amounts, exponent_bits=8, mantissa_bits=7)
+        rest = amounts - high
+        middle = lax.reduce_precision(rest, exponent_bits=8, mantissa_bits=7)
+        low = lax.reduce_precision(rest - middle, exponent_bits=8, mantissa_bits=7)
+        pieces = jnp.stack([high, middle, low], axis=2)
+        spread = jnp.where(col_pick[:, :, None, :], pieces[:, :, :, None], 0.0).astype(jnp.bfloat16)
+        spread = spread.reshape(shots, spread.shape[1], 3 * cz)
+        added = jnp.einsum("srk,srz->skz", row_pick, spread, preferred_element_type=jnp.float32)
         return field + join3(added).reshape(shape)
 
     before, current = (wave_prev, wave_now)

time: 107 us -> 110 us (1.028)
  other arithmetic: 19.8 us -> 22.2 us
  starting transfers between devices: 53.4 us -> 51.9 us
    another operation x5 -> x8, other arithmetic: 3.4 us -> 0.26 us
    convert_element_type x0 -> x1, other arithmetic: none -> 2.58 us  [inject(): jnp.where(col_pick[:, :, None, :], pieces[:, :, :, None], 0.0)]
    add x4, other arithmetic: 5.22 us -> 6.55 us  [local(): following = following + jnp.where(source_hit, amount, 0.0)]
  transfers between devices with their start and end apart: 18 -> 18, of which waited for: 9 -> 10; matrix products, arithmetic and copies ran while one was open for 5% -> 4% of each run, Pallas kernels for 0% -> 0%
where the time goes in v6:
time: 110 us; the launch traced here: 109 us
  starting transfers between devices  51.9 us (47%)
  other arithmetic  22.2 us (20%)
  waiting for transfers between devices  16.7 us (15%)
  between operations  8.33 us (8%)
  matrix products  7.61 us (7%)
  local copies, waits for them, and re-layouts  1.92 us (2%)
    ppermute x7, starting transfers between devices, extended(): before = lax.ppermute(last, 'mp', up)  22.4 us
    ppermute x7, starting transfers between devices, extended(): after = lax.ppermute(first, 'mp', down)  15.7 us
    ppermute x4, starting transfers between devices, butterfly_round(): return values + lax.ppermute(values, axis, pairs)  13.8 us
    ppermute x7, waiting for transfers between devices, extended(): after = lax.ppermute(first, 'mp', down)  11.7 us
    add x4, other arithmetic, local(): following = following + jnp.where(source_hit, amount, 0.0)  6.55 us
    dot_general x4, matrix products, inject(): jnp.einsum('srk,srz->skz', row_pick, spread, preferred_element_type=jnp.f...  4.52 us
    ppermute x7, waiting for transfers between devices, extended(): before = lax.ppermute(last, 'mp', up)  3.87 us
    dot_general x4, matrix products, sample(): jnp.einsum('srk,skz->srz', row_pick, pieces, preferred_element_type=jnp.f...  3.09 us
  transfers between devices with their start and end apart: 18, of which 10 were waited for; matrix products, arithmetic and copies ran while one was open for 4% of the time, Pallas kernels for 0%

profile of v6, /device:TPU:1, one launch (start us, length us, event | category | flops | bytes accessed | tf_op | source)
XLA Modules:
  0.0 108.7 jit_solution(1015399108437313058)
XLA Ops:
  0.7 1.2 %bitcast_multiply_fusion.8 = (f32[1,8,32,128]{3,2,1,0:T(8,128)S(1)}, f32[8,32,128]{2,1,0:T(8,128)S(1)}) fusion(f32[1,8,32,128]{3,2,1,0:T(8,128)} %param.14, f32[8,32,128]{2,1,0:T(8,128)} %param.11, f32[8,32,128]{2,1,0:T(8,128)} %param.10), kind=kLoop, calls=%fused_computation.924 | loop fusion | flops 98304 | bytes 655360 | tf_op jit(solution)/shard_map/mul | solution.py:99
  1.8 1.0 pad_maximum_fusion.1
  2.9 2.0 %collective-permute-start.1 = (f32[3,7,32,128]{3,2,1,0:T(8,128)S(1)}, f32[3,7,32,128]{3,2,1,0:T(8,128)S(1)}, u32[]{:S(2)}, u32[]{:S(2)}) collective-permute-start(f32[3,7,32,128]{3,2,1,0:T(8,128)S(1)} %get-tuple-element.46), channel_id=1, source_target_pairs={{1,0},{2,1},{3,2},{4,3},{5,4},{6,5},{7,6},{8,7},{9,8},{10,9},{11,1... | collective-permute-start | bytes 1032200 | tf_op jit(solution)/shard_map/ppermute | solution.py:19
  4.9 4.5 %collective-permute-start = (f32[3,7,32,128]{3,2,1,0:T(8,128)S(1)}, f32[3,7,32,128]{3,2,1,0:T(8,128)S(1)}, u32[]{:S(2)}, u32[]{:S(2)}) collective-permute-start(f32[3,7,32,128]{3,2,1,0:T(8,128)S(1)} %get-tuple-element.47), channel_id=1, source_target_pairs={{0,1},{1,2},{2,3},{3,4},{4,5},{5,6},{6,7},{7,8},{8,9},{9,10},{10,1... | collective-permute-start | bytes 1032200 | tf_op jit(solution)/shard_map/ppermute | solution.py:18
  10.1 0.7 fusion.624
  10.8 0.1 iota_compare_fusion.7
  11.0 0.5 fusion.348
  11.6 0.8 collective-permute-done.1
  12.4 3.9 %collective-permute-done = f32[3,7,32,128]{3,2,1,0:T(8,128)S(1)} collective-permute-done((f32[3,7,32,128]{3,2,1,0:T(8,128)S(1)}, f32[3,7,32,128]{3,2,1,0:T(8,128)S(1)}, u32[]{:S(2)}, u32[]{:S(2)}) %collective-permute-start) | collective-permute-done | bytes 344096 | tf_op jit(solution)/shard_map/ppermute | solution.py:18
  16.5 0.8 copy-done.13
  17.2 1.6 %fusion.584 = (f32[1,8,32,128]{3,2,1,0:T(8,128)S(1)}, f32[1,8,32,128]{3,2,1,0:T(8,128)}) fusion(f32[8,32,128]{2,1,0:T(8,128)S(1)} %get-tuple-element.45, f32[1,8,32,128]{3,2,1,0:T(8,128)S(1)} %copy-done.13, f32[1,8,32,128]{3,2,1,0:T(8,128)S(1)} %copy-done.1, f32[]{:T(128)} %bitcast.7, s32[]{:T(128)} %bitcast.6, s32[32]{0:T(128)S(1)} %iota_multiply_fusion, ...), kind=kLoop, calls=%fused_computation.926 | loop fusion | flops 1441792 | bytes 1966248 | tf_op jit(solution)/shard_map/add | solution.py:156
  18.9 0.3 fusion.189
  19.2 4.4 %collective-permute-start.2 = (f32[1,7,32,128]{3,2,1,0:T(8,128)S(1)}, f32[1,7,32,128]{3,2,1,0:T(8,128)S(1)}, u32[]{:S(2)}, u32[]{:S(2)}) collective-permute-start(f32[1,7,32,128]{3,2,1,0:T(8,128)S(1)} %get-tuple-element.92), channel_id=1, source_target_pairs={{0,1},{1,2},{2,3},{3,4},{4,5},{5,6},{6,7},{7,8},{8,9},{9,10},{10,1... | collective-permute-start | bytes 344072 | tf_op jit(solution)/shard_map/ppermute | solution.py:18
  23.6 1.9 %collective-permute-start.3 = (f32[1,7,32,128]{3,2,1,0:T(8,128)S(1)}, f32[1,7,32,128]{3,2,1,0:T(8,128)S(1)}, u32[]{:S(2)}, u32[]{:S(2)}) collective-permute-start(f32[1,7,32,128]{3,2,1,0:T(8,128)S(1)} %get-tuple-element.93), channel_id=1, source_target_pairs={{1,0},{2,1},{3,2},{4,3},{5,4},{6,5},{7,6},{8,7},{9,8},{10,9},{11,1... | collective-permute-start | bytes 344072 | tf_op jit(solution)/shard_map/ppermute | solution.py:19
  25.7 0.8 convolution_bitcast_fusion.2
  26.5 3.3 %collective-permute-done.3 = f32[1,7,32,128]{3,2,1,0:T(8,128)S(1)} collective-permute-done((f32[1,7,32,128]{3,2,1,0:T(8,128)S(1)}, f32[1,7,32,128]{3,2,1,0:T(8,128)S(1)}, u32[]{:S(2)}, u32[]{:S(2)}) %collective-permute-start.3) | collective-permute-done | bytes 114720 | tf_op jit(solution)/shard_map/ppermute | solution.py:19
  29.8 0.1 fusion.76
  29.9 1.6 %fusion.586 = (f32[1,8,32,128]{3,2,1,0:T(8,128)S(1)}, f32[1,8,32,128]{3,2,1,0:T(8,128)}) fusion(f32[8,32,128]{2,1,0:T(8,128)S(1)} %get-tuple-element.45, f32[1,8,32,128]{3,2,1,0:T(8,128)S(1)} %copy-done.1, f32[1,8,32,128]{3,2,1,0:T(8,128)S(1)} %get-tuple-element.42, f32[]{:T(128)} %bitcast.8, s32[]{:T(128)} %bitcast.6, s32[32]{0:T(128)S(1)} %iota_multiply_fusion, ...), kind=kLoop, calls=%fused_computation.928 | loop fusion | flops 1441792 | bytes 1966248 | tf_op jit(solution)/shard_map/add | solution.py:156
  31.6 0.3 fusion.214
  31.9 1.9 %collective-permute-start.4 = (f32[1,7,32,128]{3,2,1,0:T(8,128)S(1)}, f32[1,7,32,128]{3,2,1,0:T(8,128)S(1)}, u32[]{:S(2)}, u32[]{:S(2)}) collective-permute-start(f32[1,7,32,128]{3,2,1,0:T(8,128)S(1)} %get-tuple-element.87), channel_id=1, source_target_pairs={{0,1},{1,2},{2,3},{3,4},{4,5},{5,6},{6,7},{7,8},{8,9},{9,10},{10,1... | collective-permute-start | bytes 344072 | tf_op jit(solution)/shard_map/ppermute | solution.py:18
  33.8 2.4 %collective-permute-start.5 = (f32[1,7,32,128]{3,2,1,0:T(8,128)S(1)}, f32[1,7,32,128]{3,2,1,0:T(8,128)S(1)}, u32[]{:S(2)}, u32[]{:S(2)}) collective-permute-start(f32[1,7,32,128]{3,2,1,0:T(8,128)S(1)} %get-tuple-element.88), channel_id=1, source_target_pairs={{1,0},{2,1},{3,2},{4,3},{5,4},{6,5},{7,6},{8,7},{9,8},{10,9},{11,1... | collective-permute-start | bytes 344072 | tf_op jit(solution)/shard_map/ppermute | solution.py:19
  36.3 0.8 convolution_bitcast_fusion.1
  37.0 2.9 %collective-permute-done.5 = f32[1,7,32,128]{3,2,1,0:T(8,128)S(1)} collective-permute-done((f32[1,7,32,128]{3,2,1,0:T(8,128)S(1)}, f32[1,7,32,128]{3,2,1,0:T(8,128)S(1)}, u32[]{:S(2)}, u32[]{:S(2)}) %collective-permute-start.5) | collective-permute-done | bytes 114720 | tf_op jit(solution)/shard_map/ppermute | solution.py:19
  40.0 0.1 fusion.69
  40.1 1.7 %fusion.588 = (f32[1,8,32,128]{3,2,1,0:T(8,128)S(1)}, f32[1,8,32,128]{3,2,1,0:T(8,128)}) fusion(f32[8,32,128]{2,1,0:T(8,128)S(1)} %get-tuple-element.45, f32[1,8,32,128]{3,2,1,0:T(8,128)S(1)} %get-tuple-element.42, f32[1,8,32,128]{3,2,1,0:T(8,128)S(1)} %get-tuple-element.40, f32[]{:T(128)} %bitcast.9, s32[]{:T(128)} %bitcast.6, ...), kind=kLoop, calls=%fused_computation.930 | loop fusion | flops 1441792 | bytes 1966248 | tf_op jit(solution)/shard_map/add | solution.py:156
  41.8 0.3 fusion.239
  42.1 1.9 %collective-permute-start.6 = (f32[1,7,32,128]{3,2,1,0:T(8,128)S(1)}, f32[1,7,32,128]{3,2,1,0:T(8,128)S(1)}, u32[]{:S(2)}, u32[]{:S(2)}) collective-permute-start(f32[1,7,32,128]{3,2,1,0:T(8,128)S(1)} %get-tuple-element.79), channel_id=1, source_target_pairs={{0,1},{1,2},{2,3},{3,4},{4,5},{5,6},{6,7},{7,8},{8,9},{9,10},{10,1... | collective-permute-start | bytes 344072 | tf_op jit(solution)/shard_map/ppermute | solution.py:18
  44.1 2.6 %collective-permute-start.7 = (f32[1,7,32,128]{3,2,1,0:T(8,128)S(1)}, f32[1,7,32,128]{3,2,1,0:T(8,128)S(1)}, u32[]{:S(2)}, u32[]{:S(2)}) collective-permute-start(f32[1,7,32,128]{3,2,1,0:T(8,128)S(1)} %get-tuple-element.80), channel_id=1, source_target_pairs={{1,0},{2,1},{3,2},{4,3},{5,4},{6,5},{7,6},{8,7},{9,8},{10,9},{11,1... | collective-permute-start | bytes 344072 | tf_op jit(solution)/shard_map/ppermute | solution.py:19
  46.7 0.8 convolution_bitcast_fusion
  47.4 3.6 %collective-permute-done.7 = f32[1,7,32,128]{3,2,1,0:T(8,128)S(1)} collective-permute-done((f32[1,7,32,128]{3,2,1,0:T(8,128)S(1)}, f32[1,7,32,128]{3,2,1,0:T(8,128)S(1)}, u32[]{:S(2)}, u32[]{:S(2)}) %collective-permute-start.7) | collective-permute-done | bytes 114720 | tf_op jit(solution)/shard_map/ppermute | solution.py:19
  51.2 1.6 %fusion.590 = (f32[1,8,32,128]{3,2,1,0:T(8,128)S(1)}, f32[1,8,32,128]{3,2,1,0:T(8,128)}) fusion(f32[8,32,128]{2,1,0:T(8,128)S(1)} %get-tuple-element.45, f32[1,8,32,128]{3,2,1,0:T(8,128)S(1)} %get-tuple-element.40, f32[1,8,32,128]{3,2,1,0:T(8,128)S(1)} %get-tuple-element.36, f32[]{:T(128)} %bitcast.10, s32[]{:T(128)} %bitcast.6, ...), kind=kLoop, calls=%fused_computation.932 | loop fusion | flops 1441792 | bytes 1966248 | tf_op jit(solution)/shard_map/add | solution.py:156
  52.9 0.8 convolution_bitcast_fusion.3
  53.6 1.6 %fusion.25 = (f32[2048]{0:T(1024)S(1)}, f32[2048]{0:T(1024)S(1)}, f32[2048]{0:T(1024)S(1)}, f32[2048]{0:T(1024)S(1)}) fusion(f32[1,2048,384]{1,2,0:T(8,128)S(1)} %convolution_bitcast_fusion.1, s32[2048]{0:T(1024)S(1)} %bitcast.202, f32[1,2048,384]{1,2,0:T(8,128)S(1)} %convolution_bitcast_fusion, f32[1,2048,384]{1,2,0:T(8,128)S(1)} %convolution_bitcast_fusion.2, ...), kind=kLoop, calls=%fused_computation.27 | loop fusion | flops 4448256 | bytes 12623872 | tf_op jit(solution)/shard_map/reduce_sum | solution.py:135
  55.3 0.6 multiply_reduce_fusion.2
  55.9 0.7 multiply_reduce_fusion.1
  56.8 2.6 %select_convert_fusion = (bf16[2048,3,128]{0,2,1:T(8,128)(2,1)}, bf16[2048,3,128]{0,2,1:T(8,128)(2,1)}, bf16[2048,3,128]{0,2,1:T(8,128)(2,1)S(1)}, bf16[2048,3,128]{0,2,1:T(8,128)(2,1)S(1)}) fusion(bf16[2048,3]{0,1:T(4,128)(2,1)S(1)} %maximum_bitcast_fusion.3, pred[2048,128]{0,1:T(8,128)(4,1)S(1)} %iota_compare_fusion.7, ...), kind=kLoop, calls=%fused_computation | loop fusion | flops 3145728 | bytes 6602752 | tf_op jit(solution)/shard_map/convert_element_type | solution.py:143
  59.4 1.1 %fusion.10 = f32[1,256,384]{2,1,0:T(8,128)S(1)} fusion(bf16[2048,384]{0,1:T(8,128)(2,1)S(1)} %bitcast.188, s32[2048]{0:T(1024)S(1)} %bitcast.197), kind=kOutput, calls=%fused_computation.16 | convolution fusion | flops 403701760 | bytes 1974272 | tf_op jit(solution)/shard_map/srk,srz->skz/dot_general | solution.py:145
  60.6 0.7 slice_add_fusion.14
  63.7 1.4 %fusion.152 = f32[1,8,32,128]{3,2,1,0:T(8,128)S(1)} fusion(f32[1,8,32,128]{3,2,1,0:T(8,128)} %bitcast.191, f32[1,8,32,128]{3,2,1,0:T(8,128)} %param.15, f32[1,8,32,128]{3,2,1,0:T(8,128)S(1)} %get-tuple-element.59, f32[1,8,32,128]{3,2,1,0:T(8,128)S(1)} %get-tuple-element.58, f32[1,15,32,128]{3,2,1,0:T(8,128)S(1)} %fusion.91, f32[1,8,32,128]{3,2,1,0:T(8,128)S(1)} %copy-done.4), kind=kLoop, calls=%fused_computation.445 | loop fusion | flops 1277952 | bytes 1835008 | tf_op jit(solution)/shard_map/add | solution.py:146
  65.2 0.3 fusion.463
  65.5 1.1 %fusion.19 = f32[1,256,384]{2,1,0:T(8,128)S(1)} fusion(bf16[2048,384]{0,1:T(8,128)(2,1)S(1)} %bitcast.187, s32[2048]{0:T(1024)S(1)} %bitcast.198), kind=kOutput, calls=%fused_computation.19 | convolution fusion | flops 403701760 | bytes 1974272 | tf_op jit(solution)/shard_map/srk,srz->skz/dot_general | solution.py:145
  66.7 0.2 copy-done.2
  66.9 1.1 %fusion.13 = f32[1,256,384]{2,1,0:T(8,128)S(1)} fusion(bf16[2048,384]{0,1:T(8,128)(2,1)S(1)} %bitcast.186, s32[2048]{0:T(1024)S(1)} %bitcast.199), kind=kOutput, calls=%fused_computation.17 | convolution fusion | flops 403701760 | bytes 1974272 | tf_op jit(solution)/shard_map/srk,srz->skz/dot_general | solution.py:145
  68.1 1.1 %fusion.16 = f32[1,256,384]{2,1,0:T(8,128)S(1)} fusion(bf16[2048,384]{0,1:T(8,128)(2,1)S(1)} %bitcast.185, s32[2048]{0:T(1024)S(1)} %bitcast.200), kind=kOutput, calls=%fused_computation.18 | convolution fusion | flops 403701760 | bytes 1974272 | tf_op jit(solution)/shard_map/srk,srz->skz/dot_general | solution.py:145
  69.2 1.9 %collective-permute-start.8 = (f32[1,7,32,128]{3,2,1,0:T(8,128)S(1)}, f32[1,7,32,128]{3,2,1,0:T(8,128)S(1)}, u32[]{:S(2)}, u32[]{:S(2)}) collective-permute-start(f32[1,7,32,128]{3,2,1,0:T(8,128)S(1)} %get-tuple-element.72), channel_id=1, source_target_pairs={{0,1},{1,2},{2,3},{3,4},{4,5},{5,6},{6,7},{7,8},{8,9},{9,10},{10,1... | collective-permute-start | bytes 344072 | tf_op jit(solution)/shard_map/ppermute | solution.py:18
  71.1 2.4 %collective-permute-start.9 = (f32[1,7,32,128]{3,2,1,0:T(8,128)S(1)}, f32[1,7,32,128]{3,2,1,0:T(8,128)S(1)}, u32[]{:S(2)}, u32[]{:S(2)}) collective-permute-start(f32[1,7,32,128]{3,2,1,0:T(8,128)S(1)} %get-tuple-element.73), channel_id=1, source_target_pairs={{1,0},{2,1},{3,2},{4,3},{5,4},{6,5},{7,6},{8,7},{9,8},{10,9},{11,1... | collective-permute-start | bytes 344072 | tf_op jit(solution)/shard_map/ppermute | solution.py:19
  73.6 3.0 %collective-permute-start.10 = (f32[1]{0:T(128)}, f32[1]{0:T(128)}, u32[]{:S(2)}, u32[]{:S(2)}) collective-permute-start(f32[1]{0:T(128)} %bitcast.34), channel_id=1, source_target_pairs={{0,2},{1,3},{2,0},{3,1},{4,6},{5,7},{6,4},{7,5},{8,10},{9,11},{10,... | collective-permute-start | bytes 20 | tf_op jit(solution)/shard_map/ppermute | solution.py:36
  76.6 0.3 collective-permute-done.10
  77.6 0.5 collective-permute-done.9
  78.3 0.3 fusion.280
  78.6 3.8 %collective-permute-start.11 = (f32[1,7,32,128]{3,2,1,0:T(8,128)S(1)}, f32[1,7,32,128]{3,2,1,0:T(8,128)S(1)}, u32[]{:S(2)}, u32[]{:S(2)}) collective-permute-start(f32[1,7,32,128]{3,2,1,0:T(8,128)S(1)} %get-tuple-element.70), channel_id=1, source_target_pairs={{0,1},{1,2},{2,3},{3,4},{4,5},{5,6},{6,7},{7,8},{8,9},{9,10},{10,1... | collective-permute-start | bytes 344072 | tf_op jit(solution)/shard_map/ppermute | solution.py:18
  82.4 1.9 %collective-permute-start.12 = (f32[1,7,32,128]{3,2,1,0:T(8,128)S(1)}, f32[1,7,32,128]{3,2,1,0:T(8,128)S(1)}, u32[]{:S(2)}, u32[]{:S(2)}) collective-permute-start(f32[1,7,32,128]{3,2,1,0:T(8,128)S(1)} %get-tuple-element.71), channel_id=1, source_target_pairs={{1,0},{2,1},{3,2},{4,3},{5,4},{6,5},{7,6},{8,7},{9,8},{10,9},{11,1... | collective-permute-start | bytes 344072 | tf_op jit(solution)/shard_map/ppermute | solution.py:19
  84.3 0.3 fusion.486
  84.6 2.1 %collective-permute-start.13 = (f32[1]{0:T(128)}, f32[1]{0:T(128)}, u32[]{:S(2)}, u32[]{:S(2)}) collective-permute-start(f32[1]{0:T(128)} %add.877), channel_id=1, source_target_pairs={{0,4},{1,5},{2,6},{3,7},{4,0},{5,1},{6,2},{7,3},{8,12},{9,13},{10,... | collective-permute-start | bytes 20 | tf_op jit(solution)/shard_map/ppermute | solution.py:36
  86.7 0.5 collective-permute-done.13
  87.9 0.6 collective-permute-done.12
  88.7 0.3 fusion.308
  89.0 4.0 %collective-permute-start.14 = (f32[1,7,32,128]{3,2,1,0:T(8,128)S(1)}, f32[1,7,32,128]{3,2,1,0:T(8,128)S(1)}, u32[]{:S(2)}, u32[]{:S(2)}) collective-permute-start(f32[1,7,32,128]{3,2,1,0:T(8,128)S(1)} %get-tuple-element.68), channel_id=1, source_target_pairs={{0,1},{1,2},{2,3},{3,4},{4,5},{5,6},{6,7},{7,8},{8,9},{9,10},{10,1... | collective-permute-start | bytes 344072 | tf_op jit(solution)/shard_map/ppermute | solution.py:18
  93.1 2.5 %collective-permute-start.15 = (f32[1,7,32,128]{3,2,1,0:T(8,128)S(1)}, f32[1,7,32,128]{3,2,1,0:T(8,128)S(1)}, u32[]{:S(2)}, u32[]{:S(2)}) collective-permute-start(f32[1,7,32,128]{3,2,1,0:T(8,128)S(1)} %get-tuple-element.69), channel_id=1, source_target_pairs={{1,0},{2,1},{3,2},{4,3},{5,4},{6,5},{7,6},{8,7},{9,8},{10,9},{11,1... | collective-permute-start | bytes 344072 | tf_op jit(solution)/shard_map/ppermute | solution.py:19
  95.6 0.3 fusion.320
  95.9 3.7 %collective-permute-start.16 = (f32[1]{0:T(128)}, f32[1]{0:T(128)}, u32[]{:S(2)}, u32[]{:S(2)}) collective-permute-start(f32[1]{0:T(128)} %add.903), channel_id=1, source_target_pairs={{0,8},{1,9},{2,10},{3,11},{4,12},{5,13},{6,14},{7,15},{8,0},{9,1},... | collective-permute-start | bytes 20 | tf_op jit(solution)/shard_map/ppermute | solution.py:36
  99.6 0.3 collective-permute-done.16
  100.9 1.0 bitcast_multiply_fusion
  101.9 4.9 %collective-permute-start.17 = (f32[1]{0:T(128)}, f32[1]{0:T(128)}, u32[]{:S(2)}, u32[]{:S(2)}) collective-permute-start(f32[1]{0:T(128)} %add.929), channel_id=1, source_target_pairs={{0,1},{1,0},{2,3},{3,2},{4,5},{5,4},{6,7},{7,6},{8,9},{9,8},{10,11... | collective-permute-start | bytes 20 | tf_op jit(solution)/shard_map/ppermute | solution.py:36
  (81 shorter events, 1.8 us)
Async XLA Ops:
  0.6 10.4 %copy-start = (f32[8,32,128]{2,1,0:T(8,128)S(1)}, f32[8,32,128]{2,1,0:T(8,128)}, u32[]{:S(2)}) copy-start(f32[8,32,128]{2,1,0:T(8,128)} %param.11) | copy-start | bytes 393220
  0.6 10.4 %copy-start.1 = (f32[1,8,32,128]{3,2,1,0:T(8,128)S(1)}, f32[1,8,32,128]{3,2,1,0:T(8,128)}, u32[]{:S(2)}) copy-start(f32[1,8,32,128]{3,2,1,0:T(8,128)} %param.13) | copy-start | bytes 393220
  0.7 9.4 %copy-start.16 = (f32[1,4]{1,0:T(1,128)S(1)}, f32[1,4]{1,0:T(1,128)}, u32[]{:S(2)}) copy-start(f32[1,4]{1,0:T(1,128)} %param.17) | copy-start | bytes 52
  0.7 10.1 %copy-start.14 = (s32[1,2048]{1,0:T(1,128)S(1)}, s32[1,2048]{1,0:T(1,128)}, u32[]{:S(2)}) copy-start(s32[1,2048]{1,0:T(1,128)} %param.18) | copy-start | bytes 24580
  2.9 9.5 %collective-permute-start.1 = (f32[3,7,32,128]{3,2,1,0:T(8,128)S(1)}, f32[3,7,32,128]{3,2,1,0:T(8,128)S(1)}, u32[]{:S(2)}, u32[]{:S(2)}) collective-permute-start(f32[3,7,32,128]{3,2,1,0:T(8,128)S(1)} %get-tuple-element.46), channel_id=1, source_target_pairs={{1,0},{2,1},{3,2},{4,3},{5,4},{6,5},{7,6},{8,7},{9,8},{10,9},{11,1... | collective-permute-start | bytes 1032200 | tf_op jit(solution)/shard_map/ppermute | solution.py:19
  4.9 11.3 %collective-permute-start = (f32[3,7,32,128]{3,2,1,0:T(8,128)S(1)}, f32[3,7,32,128]{3,2,1,0:T(8,128)S(1)}, u32[]{:S(2)}, u32[]{:S(2)}) collective-permute-start(f32[3,7,32,128]{3,2,1,0:T(8,128)S(1)} %get-tuple-element.47), channel_id=1, source_target_pairs={{0,1},{1,2},{2,3},{3,4},{4,5},{5,6},{6,7},{7,8},{8,9},{9,10},{10,1... | collective-permute-start | bytes 1032200 | tf_op jit(solution)/shard_map/ppermute | solution.py:18
  10.8 48.6 %copy-start.11 = (s32[1,2048]{1,0:T(1,128)}, s32[1,2048]{1,0:T(1,128)S(1)}, u32[]{:S(2)}) copy-start(s32[1,2048]{1,0:T(1,128)S(1)} %fusion.603) | copy-start | bytes 24580
  16.3 0.9 copy-start.13
  19.2 7.2 %collective-permute-start.2 = (f32[1,7,32,128]{3,2,1,0:T(8,128)S(1)}, f32[1,7,32,128]{3,2,1,0:T(8,128)S(1)}, u32[]{:S(2)}, u32[]{:S(2)}) collective-permute-start(f32[1,7,32,128]{3,2,1,0:T(8,128)S(1)} %get-tuple-element.92), channel_id=1, source_target_pairs={{0,1},{1,2},{2,3},{3,4},{4,5},{5,6},{6,7},{7,8},{8,9},{9,10},{10,1... | collective-permute-start | bytes 344072 | tf_op jit(solution)/shard_map/ppermute | solution.py:18
  23.6 6.1 %collective-permute-start.3 = (f32[1,7,32,128]{3,2,1,0:T(8,128)S(1)}, f32[1,7,32,128]{3,2,1,0:T(8,128)S(1)}, u32[]{:S(2)}, u32[]{:S(2)}) collective-permute-start(f32[1,7,32,128]{3,2,1,0:T(8,128)S(1)} %get-tuple-element.93), channel_id=1, source_target_pairs={{1,0},{2,1},{3,2},{4,3},{5,4},{6,5},{7,6},{8,7},{9,8},{10,9},{11,1... | collective-permute-start | bytes 344072 | tf_op jit(solution)/shard_map/ppermute | solution.py:19
  31.9 5.1 %collective-permute-start.4 = (f32[1,7,32,128]{3,2,1,0:T(8,128)S(1)}, f32[1,7,32,128]{3,2,1,0:T(8,128)S(1)}, u32[]{:S(2)}, u32[]{:S(2)}) collective-permute-start(f32[1,7,32,128]{3,2,1,0:T(8,128)S(1)} %get-tuple-element.87), channel_id=1, source_target_pairs={{0,1},{1,2},{2,3},{3,4},{4,5},{5,6},{6,7},{7,8},{8,9},{9,10},{10,1... | collective-permute-start | bytes 344072 | tf_op jit(solution)/shard_map/ppermute | solution.py:18
  33.8 6.1 %collective-permute-start.5 = (f32[1,7,32,128]{3,2,1,0:T(8,128)S(1)}, f32[1,7,32,128]{3,2,1,0:T(8,128)S(1)}, u32[]{:S(2)}, u32[]{:S(2)}) collective-permute-start(f32[1,7,32,128]{3,2,1,0:T(8,128)S(1)} %get-tuple-element.88), channel_id=1, source_target_pairs={{1,0},{2,1},{3,2},{4,3},{5,4},{6,5},{7,6},{8,7},{9,8},{10,9},{11,1... | collective-permute-start | bytes 344072 | tf_op jit(solution)/shard_map/ppermute | solution.py:19
  42.1 5.3 %collective-permute-start.6 = (f32[1,7,32,128]{3,2,1,0:T(8,128)S(1)}, f32[1,7,32,128]{3,2,1,0:T(8,128)S(1)}, u32[]{:S(2)}, u32[]{:S(2)}) collective-permute-start(f32[1,7,32,128]{3,2,1,0:T(8,128)S(1)} %get-tuple-element.79), channel_id=1, source_target_pairs={{0,1},{1,2},{2,3},{3,4},{4,5},{5,6},{6,7},{7,8},{8,9},{9,10},{10,1... | collective-permute-start | bytes 344072 | tf_op jit(solution)/shard_map/ppermute | solution.py:18
  44.1 7.0 %collective-permute-start.7 = (f32[1,7,32,128]{3,2,1,0:T(8,128)S(1)}, f32[1,7,32,128]{3,2,1,0:T(8,128)S(1)}, u32[]{:S(2)}, u32[]{:S(2)}) collective-permute-start(f32[1,7,32,128]{3,2,1,0:T(8,128)S(1)} %get-tuple-element.80), channel_id=1, source_target_pairs={{1,0},{2,1},{3,2},{4,3},{5,4},{6,5},{7,6},{8,7},{9,8},{10,9},{11,1... | collective-permute-start | bytes 344072 | tf_op jit(solution)/shard_map/ppermute | solution.py:19
  53.6 1.6 %copy-start.15 = (f32[1,4,2048]{2,1,0:T(4,128)S(1)}, f32[1,4,2048]{2,1,0:T(4,128)}, u32[]{:S(2)}) copy-start(f32[1,4,2048]{2,1,0:T(4,128)} %param.19) | copy-start | bytes 98308
  59.4 4.3 %copy-start.4 = (f32[1,8,32,128]{3,2,1,0:T(8,128)S(1)}, f32[1,8,32,128]{3,2,1,0:T(8,128)}, u32[]{:S(2)}) copy-start(f32[1,8,32,128]{3,2,1,0:T(8,128)} %param.14) | copy-start | bytes 393220
  63.7 1.8 %copy-start.3 = (bf16[2048,3,128]{0,2,1:T(8,128)(2,1)S(1)}, bf16[2048,3,128]{0,2,1:T(8,128)(2,1)}, u32[]{:S(2)}) copy-start(bf16[2048,3,128]{0,2,1:T(8,128)(2,1)} %get-tuple-element.50) | copy-start | bytes 4718596
  63.7 1.8 %copy-start.12 = (s32[1,2048]{1,0:T(1,128)S(1)}, s32[1,2048]{1,0:T(1,128)}, u32[]{:S(2)}) copy-start(s32[1,2048]{1,0:T(1,128)} %copy-done.11) | copy-start | bytes 24580
  65.5 1.4 %copy-start.2 = (bf16[2048,3,128]{0,2,1:T(8,128)(2,1)S(1)}, bf16[2048,3,128]{0,2,1:T(8,128)(2,1)}, u32[]{:S(2)}) copy-start(bf16[2048,3,128]{0,2,1:T(8,128)(2,1)} %get-tuple-element.51) | copy-start | bytes 4718596
  69.2 8.4 %collective-permute-start.8 = (f32[1,7,32,128]{3,2,1,0:T(8,128)S(1)}, f32[1,7,32,128]{3,2,1,0:T(8,128)S(1)}, u32[]{:S(2)}, u32[]{:S(2)}) collective-permute-start(f32[1,7,32,128]{3,2,1,0:T(8,128)S(1)} %get-tuple-element.72), channel_id=1, source_target_pairs={{0,1},{1,2},{2,3},{3,4},{4,5},{5,6},{6,7},{7,8},{8,9},{9,10},{10,1... | collective-permute-start | bytes 344072 | tf_op jit(solution)/shard_map/ppermute | solution.py:18
  71.1 7.0 %collective-permute-start.9 = (f32[1,7,32,128]{3,2,1,0:T(8,128)S(1)}, f32[1,7,32,128]{3,2,1,0:T(8,128)S(1)}, u32[]{:S(2)}, u32[]{:S(2)}) collective-permute-start(f32[1,7,32,128]{3,2,1,0:T(8,128)S(1)} %get-tuple-element.73), channel_id=1, source_target_pairs={{1,0},{2,1},{3,2},{4,3},{5,4},{6,5},{7,6},{8,7},{9,8},{10,9},{11,1... | collective-permute-start | bytes 344072 | tf_op jit(solution)/shard_map/ppermute | solution.py:19
  73.6 3.3 %collective-permute-start.10 = (f32[1]{0:T(128)}, f32[1]{0:T(128)}, u32[]{:S(2)}, u32[]{:S(2)}) collective-permute-start(f32[1]{0:T(128)} %bitcast.34), channel_id=1, source_target_pairs={{0,2},{1,3},{2,0},{3,1},{4,6},{5,7},{6,4},{7,5},{8,10},{9,11},{10,... | collective-permute-start | bytes 20 | tf_op jit(solution)/shard_map/ppermute | solution.py:36
  78.6 9.2 %collective-permute-start.11 = (f32[1,7,32,128]{3,2,1,0:T(8,128)S(1)}, f32[1,7,32,128]{3,2,1,0:T(8,128)S(1)}, u32[]{:S(2)}, u32[]{:S(2)}) collective-permute-start(f32[1,7,32,128]{3,2,1,0:T(8,128)S(1)} %get-tuple-element.70), channel_id=1, source_target_pairs={{0,1},{1,2},{2,3},{3,4},{4,5},{5,6},{6,7},{7,8},{8,9},{9,10},{10,1... | collective-permute-start | bytes 344072 | tf_op jit(solution)/shard_map/ppermute | solution.py:18
  82.4 6.1 %collective-permute-start.12 = (f32[1,7,32,128]{3,2,1,0:T(8,128)S(1)}, f32[1,7,32,128]{3,2,1,0:T(8,128)S(1)}, u32[]{:S(2)}, u32[]{:S(2)}) collective-permute-start(f32[1,7,32,128]{3,2,1,0:T(8,128)S(1)} %get-tuple-element.71), channel_id=1, source_target_pairs={{1,0},{2,1},{3,2},{4,3},{5,4},{6,5},{7,6},{8,7},{9,8},{10,9},{11,1... | collective-permute-start | bytes 344072 | tf_op jit(solution)/shard_map/ppermute | solution.py:19
  84.6 2.6 %collective-permute-start.13 = (f32[1]{0:T(128)}, f32[1]{0:T(128)}, u32[]{:S(2)}, u32[]{:S(2)}) collective-permute-start(f32[1]{0:T(128)} %add.877), channel_id=1, source_target_pairs={{0,4},{1,5},{2,6},{3,7},{4,0},{5,1},{6,2},{7,3},{8,12},{9,13},{10,... | collective-permute-start | bytes 20 | tf_op jit(solution)/shard_map/ppermute | solution.py:36
  89.0 11.8 %copy-start.5 = (f32[1,8,32,128]{3,2,1,0:T(8,128)}, f32[1,8,32,128]{3,2,1,0:T(8,128)S(1)}, u32[]{:S(2)}) copy-start(f32[1,8,32,128]{3,2,1,0:T(8,128)S(1)} %fusion.308) | copy-start | bytes 393220
  89.0 11.6 %collective-permute-start.14 = (f32[1,7,32,128]{3,2,1,0:T(8,128)S(1)}, f32[1,7,32,128]{3,2,1,0:T(8,128)S(1)}, u32[]{:S(2)}, u32[]{:S(2)}) collective-permute-start(f32[1,7,32,128]{3,2,1,0:T(8,128)S(1)} %get-tuple-element.68), channel_id=1, source_target_pairs={{0,1},{1,2},{2,3},{3,4},{4,5},{5,6},{6,7},{7,8},{8,9},{9,10},{10,1... | collective-permute-start | bytes 344072 | tf_op jit(solution)/shard_map/ppermute | solution.py:18
  93.1 7.6 %collective-permute-start.15 = (f32[1,7,32,128]{3,2,1,0:T(8,128)S(1)}, f32[1,7,32,128]{3,2,1,0:T(8,128)S(1)}, u32[]{:S(2)}, u32[]{:S(2)}) collective-permute-start(f32[1,7,32,128]{3,2,1,0:T(8,128)S(1)} %get-tuple-element.69), channel_id=1, source_target_pairs={{1,0},{2,1},{3,2},{4,3},{5,4},{6,5},{7,6},{8,7},{9,8},{10,9},{11,1... | collective-permute-start | bytes 344072 | tf_op jit(solution)/shard_map/ppermute | solution.py:19
  95.9 4.9 %copy-start.6 = (f32[8,32,128]{2,1,0:T(8,128)S(1)}, f32[8,32,128]{2,1,0:T(8,128)}, u32[]{:S(2)}) copy-start(f32[8,32,128]{2,1,0:T(8,128)} %param.10) | copy-start | bytes 393220
  95.9 4.9 %copy-start.7 = (f32[1,8,32,128]{3,2,1,0:T(8,128)S(1)}, f32[1,8,32,128]{3,2,1,0:T(8,128)}, u32[]{:S(2)}) copy-start(f32[1,8,32,128]{3,2,1,0:T(8,128)} %get-tuple-element.43) | copy-start | bytes 393220
  95.9 4.9 %copy-start.8 = (f32[1,8,32,128]{3,2,1,0:T(8,128)S(1)}, f32[1,8,32,128]{3,2,1,0:T(8,128)}, u32[]{:S(2)}) copy-start(f32[1,8,32,128]{3,2,1,0:T(8,128)} %get-tuple-element.41) | copy-start | bytes 393220
  95.9 4.9 %copy-start.9 = (f32[1,8,32,128]{3,2,1,0:T(8,128)S(1)}, f32[1,8,32,128]{3,2,1,0:T(8,128)}, u32[]{:S(2)}) copy-start(f32[1,8,32,128]{3,2,1,0:T(8,128)} %get-tuple-element.37) | copy-start | bytes 393220
  95.9 4.9 %copy-start.10 = (f32[1,8,32,128]{3,2,1,0:T(8,128)S(1)}, f32[1,8,32,128]{3,2,1,0:T(8,128)}, u32[]{:S(2)}) copy-start(f32[1,8,32,128]{3,2,1,0:T(8,128)} %get-tuple-element.35) | copy-start | bytes 393220
  95.9 4.0 %collective-permute-start.16 = (f32[1]{0:T(128)}, f32[1]{0:T(128)}, u32[]{:S(2)}, u32[]{:S(2)}) collective-permute-start(f32[1]{0:T(128)} %add.903), channel_id=1, source_target_pairs={{0,8},{1,9},{2,10},{3,11},{4,12},{5,13},{6,14},{7,15},{8,0},{9,1},... | collective-permute-start | bytes 20 | tf_op jit(solution)/shard_map/ppermute | solution.py:36
  101.9 4.9 %collective-permute-start.17 = (f32[1]{0:T(128)}, f32[1]{0:T(128)}, u32[]{:S(2)}, u32[]{:S(2)}) collective-permute-start(f32[1]{0:T(128)} %add.929), channel_id=1, source_target_pairs={{0,1},{1,0},{2,3},{3,2},{4,5},{5,4},{6,7},{7,6},{8,9},{9,8},{10,11... | collective-permute-start | bytes 20 | tf_op jit(solution)/shard_map/ppermute | solution.py:36

commit v7 on v3

--- a/solution.py
+++ b/solution.py
@@ -18,6 +18,21 @@
     before = lax.ppermute(last, "mp", up)
     after = lax.ppermute(first, "mp", down)
     return jnp.concatenate([before, array, after], axis=dim)
+
+
+def wide_extended(array, dim, width):
+    devices, length = (lax.axis_size("mp"), array.shape[dim])
+    extra = width - length
+    assert 0 < extra <= length
+    up_near = [(i, i + 1) for i in range(devices - 1)]
+    up_far = [(i, i + 2) for i in range(devices - 2)]
+    down_near = [(j, i) for i, j in up_near]
+    down_far = [(j, i) for i, j in up_far]
+    below_far = lax.ppermute(lax.slice_in_dim(array, length - extra, length, axis=dim), "mp", up_far)
+    below_near = lax.ppermute(array, "mp", up_near)
+    above_near = lax.ppermute(array, "mp", down_near)
+    above_far = lax.ppermute(lax.slice_in_dim(array, 0, extra, axis=dim), "mp", down_far)
+    return jnp.concatenate([below_far, below_near, array, above_near, above_far], axis=dim)
 
 
 def butterfly_distances(axis):
@@ -91,24 +106,37 @@
     cells = rows * cz
     kappa = velocity * velocity / buoyancy
     offset = lax.axis_index("mp") * cells
-
-    def wide_operator(wide, values, flux_buoyancy):
-        flux = flux_buoyancy * forward_diff(wide, 1, planes + 7, start=HALO - 4)
-        return backward_diff(flux, 1, planes) + cross_terms(values, buoyancy)
+    wide = 2 * HALO
+
+    def wide_operator(values, reach):
+        margin = reach - HALO
+        length = planes + 2 * margin
+        flux_planes = buoyancy_wide[:, wide - margin - 4 : wide - margin + length + 3]
+        flux = flux_planes * forward_diff(values, 1, length + 7, start=HALO - 4)
+        center = lax.slice_in_dim(values, reach - margin, reach - margin + length, axis=1)
+        center_buoyancy = buoyancy_wide[:, wide - margin : wide - margin + length]
+        return backward_diff(flux, 1, length) + cross_terms(center, center_buoyancy)
 
     adjoint_operand = kappa * adjoint_next
-    first = extended(jnp.concatenate([buoyancy[None], wave_now, adjoint_operand], axis=0), 1, HALO)
-    flux_buoyancy = first[0, HALO - 4 : HALO + planes + 3]
-    first_lap = wide_operator(first[1 : 1 + shots], wave_now, flux_buoyancy)
-    adjoint_lap = wide_operator(first[1 + shots :], adjoint_operand, flux_buoyancy)
+    first = wide_extended(
+        jnp.concatenate([buoyancy[None], kappa[None], wave_prev, wave_now, adjoint_operand], axis=0), 1, wide
+    )
+    buoyancy_wide = first[0:1]
+    kappa_near = first[1:2, HALO : wide + planes + HALO]
+    prev_near = first[2 : 2 + shots, HALO : wide + planes + HALO]
+    now_wide = first[2 + shots : 2 + 2 * shots]
+    adjoint_lap = wide_operator(first[2 + 2 * shots :, HALO : wide + planes + HALO], HALO)
 
     def operator(values):
-        return wide_operator(extended(values, 1, HALO), values, flux_buoyancy)
+        return wide_operator(extended(values, 1, HALO), HALO)
 
     source_local = source_cell - offset
-    source_owned = (source_local >= 0) & (source_local < cells)
-    source_index = jnp.clip(source_local, 0, cells - 1)
-    shot_rows = jnp.arange(shots)
+    near_shape = (shots, planes + 2 * HALO, cy, cz)
+    cell_index = (lax.broadcasted_iota(jnp.int32, near_shape, 1) - HALO) * (cy * cz)
+    cell_index = cell_index + lax.broadcasted_iota(jnp.int32, near_shape, 2) * cz
+    cell_index = cell_index + lax.broadcasted_iota(jnp.int32, near_shape, 3)
+    source_hit_near = cell_index == source_local.reshape(shots, 1, 1, 1)
+    source_hit = source_hit_near[:, HALO : HALO + planes]
 
     receiver_local = receiver_cell - offset
     receiver_owned = (receiver_local >= 0) & (receiver_local < cells)
@@ -128,19 +156,37 @@
         added = jnp.einsum("srk,srz->skz", row_pick, spread, precision=lax.Precision.HIGHEST)
         return field + added.reshape(shape)
 
-    before, current = (wave_prev, wave_now)
     laps = []
     resids = []
-    for step in range(STEPS):
-        lap = first_lap if step == 0 else operator(current)
-        laps.append(lap)
-        following = 2.0 * current - before + kappa * lap
-        amount = jnp.where(source_owned, wavelet[:, step], 0.0)
-        flat = following.reshape(shots, cells).at[shot_rows, source_index].add(amount)
-        following = flat.reshape(shape)
+
+    def record(following):
         sampled = sample(following)
-        resids.append(jnp.where(receiver_owned, sampled - observed[:, step, :], 0.0))
+        resids.append(jnp.where(receiver_owned, sampled - observed[:, len(resids), :], 0.0))
+
+    def source(step, hit):
+        return jnp.where(hit, wavelet[:, step].reshape(shots, 1, 1, 1), 0.0)
+
+    before, current = (wave_prev, wave_now)
+    current_wide = now_wide
+    before_near = prev_near
+    for step in range(0, STEPS, 2):
+        if step > 0:
+            current_wide = wide_extended(current, 1, wide)
+        lap_near = wide_operator(current_wide, wide)
+        current_near = current_wide[:, HALO : wide + planes + HALO]
+        following_near = 2.0 * current_near - before_near + kappa_near * lap_near
+        following_near = following_near + source(step, source_hit_near)
+        laps.append(lap_near[:, HALO : HALO + planes])
+        following = following_near[:, HALO : HALO + planes]
+        record(following)
         before, current = (current, following)
+        before_near = following_near
+        if step + 1 < STEPS:
+            lap = wide_operator(following_near, HALO)
+            laps.append(lap)
+            following = 2.0 * current - before + kappa * lap + source(step + 1, source_hit)
+            record(following)
+            before, current = (current, following)
     misfit = 0.5 * sum((jnp.sum(item * item, axis=1) for item in resids))
     distances = butterfly_distances("mp")
     mu_near, mu_far = (adjoint_next, adjoint_after)

time: 108 us -> 134 us (1.24)
  waiting for transfers between devices: 10.7 us -> 26.5 us
  between operations: 18.8 us -> 8.14 us
  other arithmetic: 11.8 us -> 21.5 us
  local copies, waits for them, and re-layouts: 1.88 us -> 7.57 us
  starting transfers between devices: 52.3 us -> 56.7 us
    ppermute x0 -> x8, waiting for transfers between devices: none -> 26 us  [the longest x2 26 us: wide_extended(): lax.ppermute(lax.slice_in_dim(array, length - extra, length, axis=dim), '...]
    ppermute x0 -> x8, starting transfers between devices: none -> 20.6 us  [the longest x2 7.11 us: wide_extended(): lax.ppermute(lax.slice_in_dim(array, length - extra, length, axis=dim), '...]
    ppermute x7 -> x3, starting transfers between devices: 22.9 us -> 13 us  [extended(): before = lax.ppermute(last, 'mp', up)]
    ppermute x7 -> x3, starting transfers between devices: 15.5 us -> 7.25 us  [extended(): after = lax.ppermute(first, 'mp', down)]
    ppermute x7 -> x3, waiting for transfers between devices: 8.1 us -> 0.01 us  [extended(): after = lax.ppermute(first, 'mp', down)]
    unnamed x22 -> x67, local copies, waits for them, and re-layouts: 0.85 us -> 4.82 us
    add x8 -> x4, other arithmetic: 3.82 us -> 6.21 us  [the longest x2 3.69 us: local(): following_near = following_near + source(step, source_hit_near)]
    concatenate x1 -> x4, other arithmetic: 1.04 us -> 3.08 us  [the longest x1 1.58 us: local(): jnp.concatenate([buoyancy[None], kappa[None], wave_prev, wave_now, adjoin...]
  transfers between devices with their start and end apart: 18 -> 18, of which waited for: 9 -> 4; matrix products, arithmetic and copies ran while one was open for 8% -> 11% of each run, Pallas kernels for 0% -> 0%
where the time goes in v7:
time: 134 us; the launch traced here: 133 us
  starting transfers between devices  56.7 us (42%)
  waiting for transfers between devices  26.5 us (20%)
  other arithmetic  21.5 us (16%)
  matrix products  12.4 us (9%)
  between operations  8.14 us (6%)
  local copies, waits for them, and re-layouts  7.57 us (6%)
    ppermute x2, waiting for transfers between devices, wide_extended(): lax.ppermute(lax.slice_in_dim(array, length - extra, length, axis=dim), '...  26 us
    ppermute x4, starting transfers between devices, butterfly_round(): return values + lax.ppermute(values, axis, pairs)  15.9 us
    ppermute x3, starting transfers between devices, extended(): before = lax.ppermute(last, 'mp', up)  13 us
    ppermute x3, starting transfers between devices, extended(): after = lax.ppermute(first, 'mp', down)  7.25 us
    ppermute x2, starting transfers between devices, wide_extended(): lax.ppermute(lax.slice_in_dim(array, length - extra, length, axis=dim), '...  7.11 us
    ppermute x2, starting transfers between devices, wide_extended(): below_near = lax.ppermute(array, 'mp', up_near)  6.81 us
    dot_general x4, matrix products, sample(): jnp.einsum('srk,skz->srz', row_pick, field.reshape(shots, rows, cz), prec...  6.42 us
    dot_general x4, matrix products, inject(): jnp.einsum('srk,srz->skz', row_pick, spread, precision=lax.Precision.HIGH...  5.95 us
  transfers between devices with their start and end apart: 18, of which 4 were waited for; matrix products, arithmetic and copies ran while one was open for 11% of the time, Pallas kernels for 0%

profile of v7, /device:TPU:1, one launch (start us, length us, event | category | flops | bytes accessed | tf_op | source)
XLA Modules:
  0.0 132.8 jit_solution(10462267575560956851)
XLA Ops:
  0.7 0.9 bitcast_dynamic-update-slice_fusion.3
  1.6 1.0 bitcast_dynamic-update-slice_fusion.1
  2.6 0.9 constant_dynamic-update-slice_fusion.2
  3.5 0.9 constant_dynamic-update-slice_fusion.1
  4.4 1.6 %constant_dynamic-update-slice_fusion = (f32[5,8,32,128]{3,2,1,0:T(8,128)S(1)}, f32[1,8,32,128]{3,2,1,0:T(8,128)}) fusion(f32[5,8,32,128]{3,2,1,0:T(8,128)S(1)} %constant_dynamic-update-slice_fusion.1, f32[1,8,32,128]{3,2,1,0:T(8,128)} %param.14, f32[8,32,128]{2,1,0:T(8,128)S(1)} %get-tuple-element.41), kind=kLoop, calls=%fused_computation.902 | loop fusion | flops 32768 | bytes 524288 | tf_op jit(solution)/shard_map/concatenate | solution.py:122
  6.0 4.7 %collective-permute-start = (f32[5,8,32,128]{3,2,1,0:T(8,128)S(1)}, f32[5,8,32,128]{3,2,1,0:T(8,128)S(1)}, u32[]{:S(2)}, u32[]{:S(2)}) collective-permute-start(f32[5,8,32,128]{3,2,1,0:T(8,128)S(1)} %get-tuple-element.38), channel_id=1, source_target_pairs={{0,1},{1,2},{2,3},{3,4},{4,5},{5,6},{6,7},{7,8},{8,9},{9,10},{10,1... | collective-permute-start | bytes 1966088 | tf_op jit(solution)/shard_map/ppermute | solution.py:32
  10.7 1.9 %collective-permute-start.1 = (f32[5,8,32,128]{3,2,1,0:T(8,128)S(1)}, f32[5,8,32,128]{3,2,1,0:T(8,128)}, u32[]{:S(2)}, u32[]{:S(2)}) collective-permute-start(f32[5,8,32,128]{3,2,1,0:T(8,128)S(1)} %get-tuple-element.38), channel_id=1, source_target_pairs={{1,0},{2,1},{3,2},{4,3},{5,4},{6,5},{7,6},{8,7},{9,8},{10,9},{11,1... | collective-permute-start | bytes 1966088 | tf_op jit(solution)/shard_map/ppermute | solution.py:33
  12.6 0.9 fusion.623
  13.5 3.3 %collective-permute-start.2 = (f32[5,6,32,128]{3,2,1,0:T(8,128)S(1)}, f32[5,6,32,128]{3,2,1,0:T(8,128)S(1)}, u32[]{:S(2)}, u32[]{:S(2)}) collective-permute-start(f32[5,6,32,128]{3,2,1,0:T(8,128)S(1)} %get-tuple-element.47), channel_id=1, source_target_pairs={{0,2},{1,3},{2,4},{3,5},{4,6},{5,7},{6,8},{7,9},{8,10},{9,11},{10,... | collective-permute-start | bytes 1474568 | tf_op jit(solution)/shard_map/ppermute | solution.py:31
  16.8 1.3 collective-permute-start.3
  18.8 0.7 fusion.628
  19.5 0.1 add_compare_fusion
  19.7 0.6 multiply_add_fusion
  20.3 26.0 %collective-permute-done.2 = f32[5,6,32,128]{3,2,1,0:T(8,128)S(1)} collective-permute-done((f32[5,6,32,128]{3,2,1,0:T(8,128)S(1)}, f32[5,6,32,128]{3,2,1,0:T(8,128)S(1)}, u32[]{:S(2)}, u32[]{:S(2)}) %collective-permute-start.2) | collective-permute-done | bytes 491552 | tf_op jit(solution)/shard_map/ppermute | solution.py:31
  46.5 0.6 copy-done.1
  47.1 1.4 %pad_maximum_fusion = f32[5,24,32,128]{3,2,1,0:T(8,128)S(1)} fusion(f32[5,8,32,128]{3,2,1,0:T(8,128)} %collective-permute-done.1, f32[5,8,32,128]{3,2,1,0:T(8,128)S(1)} %get-tuple-element.38, f32[5,8,32,128]{3,2,1,0:T(8,128)S(1)} %collective-permute-done), kind=kLoop, calls=%fused_computation.14 | loop fusion | flops 983040 | bytes 3932160 | tf_op jit(solution)/shard_map/concatenate | solution.py:35
  48.5 1.2 constant_dynamic-update-slice_fusion.4
  49.7 0.7 fusion.103
  50.5 1.1 constant_dynamic-update-slice_fusion.3
  51.6 1.4 %fusion.92 = f32[1,29,32,128]{3,2,1,0:T(8,128)S(1)} fusion(f32[5,8,32,128]{3,2,1,0:T(8,128)} %collective-permute-done.1, f32[5,8,32,128]{3,2,1,0:T(8,128)S(1)} %get-tuple-element.38, f32[5,8,32,128]{3,2,1,0:T(8,128)S(1)} %collective-permute-done, f32[5,6,32,128]{3,2,1,0:T(8,128)S(1)} %copy-done.2, f32[5,6,32,128]{3,2,1,0:T(8,128)} %collective-permute-done.3, ...), kind=kLoop, calls=%fused_computation.218 | loop fusion | flops 2850816 | bytes 5799936 | tf_op jit(solution)/shard_map/mul | solution.py:115
  53.0 2.2 %fusion.209 = (f32[1,22,32,128]{3,2,1,0:T(8,128)S(1)}, f32[1,22,32,128]{3,2,1,0:T(8,128)}) fusion(f32[5,24,32,128]{3,2,1,0:T(8,128)S(1)} %pad_maximum_fusion, f32[]{:T(128)} %bitcast.7, s32[]{:T(128)} %bitcast.6, s32[32]{0:T(128)S(1)} %copy-done.23, s32[22]{0:T(128)S(1)} %copy-done.21, f32[1,22,32,128]{3,2,1,0:T(8,128)S(1)} %get-tuple-element.45, ...), kind=kLoop, calls=%fused_computation.354 | loop fusion | flops 3964928 | bytes 5406944 | tf_op jit(solution)/shard_map/add | solution.py:178
  55.4 1.2 fusion.422
  56.6 1.6 %fusion.603 = (f32[1,8,32,128]{3,2,1,0:T(8,128)S(1)}, f32[1,8,32,128]{3,2,1,0:T(8,128)}) fusion(f32[8,32,128]{2,1,0:T(8,128)S(1)} %get-tuple-element.41, f32[1,8,32,128]{3,2,1,0:T(8,128)S(1)} %copy-done.4, pred[1,22,32,128]{3,2,1,0:T(8,128)(4,1)S(1)} %add_compare_fusion, f32[]{:T(128)} %bitcast.8, f32[1,22,32,128]{3,2,1,0:T(8,128)S(1)} %get-tuple-element.36, ...), kind=kLoop, calls=%fused_computation.896 | loop fusion | flops 1343488 | bytes 1998852 | tf_op jit(solution)/shard_map/add | solution.py:187
  58.2 2.2 %collective-permute-start.4 = (f32[1,8,32,128]{3,2,1,0:T(8,128)S(1)}, f32[1,8,32,128]{3,2,1,0:T(8,128)S(1)}, u32[]{:S(2)}, u32[]{:S(2)}) collective-permute-start(f32[1,8,32,128]{3,2,1,0:T(8,128)S(1)} %get-tuple-element.32), channel_id=1, source_target_pairs={{0,1},{1,2},{2,3},{3,4},{4,5},{5,6},{6,7},{7,8},{8,9},{9,10},{10,1... | collective-permute-start | bytes 393224 | tf_op jit(solution)/shard_map/ppermute | solution.py:32
  60.3 2.2 %collective-permute-start.5 = (f32[1,8,32,128]{3,2,1,0:T(8,128)S(1)}, f32[1,8,32,128]{3,2,1,0:T(8,128)S(1)}, u32[]{:S(2)}, u32[]{:S(2)}) collective-permute-start(f32[1,8,32,128]{3,2,1,0:T(8,128)S(1)} %get-tuple-element.32), channel_id=1, source_target_pairs={{1,0},{2,1},{3,2},{4,3},{5,4},{6,5},{7,6},{8,7},{9,8},{10,9},{11,1... | collective-permute-start | bytes 393224 | tf_op jit(solution)/shard_map/ppermute | solution.py:33
  62.5 3.8 %collective-permute-start.6 = (f32[1,6,32,128]{3,2,1,0:T(8,128)S(1)}, f32[1,6,32,128]{3,2,1,0:T(8,128)S(1)}, u32[]{:S(2)}, u32[]{:S(2)}) collective-permute-start(f32[1,6,32,128]{3,2,1,0:T(8,128)S(1)} %get-tuple-element.71), channel_id=1, source_target_pairs={{0,2},{1,3},{2,4},{3,5},{4,6},{5,7},{6,8},{7,9},{8,10},{9,11},{10,... | collective-permute-start | bytes 294920 | tf_op jit(solution)/shard_map/ppermute | solution.py:31
  66.3 1.3 collective-permute-start.7
  67.6 1.6 %fusion.19 = f32[2048]{0:T(1024)S(1)} fusion(f32[256,128]{1,0:T(8,128)S(1)} %bitcast.124, s32[2048]{0:T(1024)S(1)} %bitcast.136, s32[2048]{0:T(1024)S(1)} %bitcast.128), kind=kOutput, calls=%fused_computation.45 | convolution fusion | flops 806615040 | bytes 155648 | tf_op jit(solution)/shard_map/srk,skz->srz/dot_general | solution.py:149
  69.3 1.7 %fusion.250 = f32[1,15,32,128]{3,2,1,0:T(8,128)} fusion(f32[5,8,32,128]{3,2,1,0:T(8,128)S(1)} %get-tuple-element.38, f32[5,8,32,128]{3,2,1,0:T(8,128)S(1)} %collective-permute-done, f32[5,8,32,128]{3,2,1,0:T(8,128)} %collective-permute-done.1, f32[5,24,32,128]{3,2,1,0:T(8,128)S(1)} %pad_maximum_fusion), kind=kLoop, calls=%fused_computation.418 | loop fusion | flops 860160 | bytes 3932160 | tf_op jit(solution)/shard_map/mul | solution.py:115
  71.0 1.6 %fusion.16 = f32[2048]{0:T(1024)S(1)} fusion(f32[256,128]{1,0:T(8,128)S(1)} %bitcast.125, s32[2048]{0:T(1024)S(1)} %bitcast.137, s32[2048]{0:T(1024)S(1)} %bitcast.129), kind=kOutput, calls=%fused_computation.44 | convolution fusion | flops 806615040 | bytes 155648 | tf_op jit(solution)/shard_map/srk,skz->srz/dot_general | solution.py:149
  72.7 0.7 fusion.128
  73.4 0.1 pad_maximum_fusion.1
  73.6 0.2 fusion.83
  73.8 1.5 %select_add_fusion = (f32[1,22,32,128]{3,2,1,0:T(8,128)S(1)}, f32[1,22,32,128]{3,2,1,0:T(8,128)S(1)}) fusion(f32[1,22,32,128]{3,2,1,0:T(8,128)S(1)} %get-tuple-element.36, f32[1,22,32,128]{3,2,1,0:T(8,128)S(1)} %pad_maximum_fusion.9, f32[5,24,32,128]{3,2,1,0:T(8,128)S(1)} %pad_maximum_fusion, f32[]{:T(128)} %bitcast.9, s32[]{:T(128)} %bitcast.6, ...), kind=kLoop, calls=%fused_computation.358 | loop fusion | flops 3964928 | bytes 5406944 | tf_op jit(solution)/shard_map/add | solution.py:178
  75.3 0.1 fusion.233
  75.4 0.3 fusion.316
  75.7 0.9 fusion.605
  76.7 1.6 %fusion.13 = f32[2048]{0:T(1024)S(1)} fusion(f32[256,128]{1,0:T(8,128)S(1)} %bitcast.127, s32[2048]{0:T(1024)S(1)} %bitcast.138, s32[2048]{0:T(1024)S(1)} %bitcast.130), kind=kOutput, calls=%fused_computation.43 | convolution fusion | flops 806615040 | bytes 155648 | tf_op jit(solution)/shard_map/srk,skz->srz/dot_general | solution.py:149
  78.4 1.6 %fusion.22 = f32[2048]{0:T(1024)S(1)} fusion(f32[256,128]{1,0:T(8,128)S(1)} %bitcast.126, s32[2048]{0:T(1024)S(1)} %bitcast.139, s32[2048]{0:T(1024)S(1)} %bitcast.131), kind=kOutput, calls=%fused_computation.46 | convolution fusion | flops 806615040 | bytes 155648 | tf_op jit(solution)/shard_map/srk,skz->srz/dot_general | solution.py:149
  80.0 0.7 multiply_reduce_fusion.2
  83.3 2.0 %fusion.46 = f32[1,8,32,128]{3,2,1,0:T(8,128)S(1)} fusion(s32[8,32]{1,0:T(8,128)S(1)} %copy-done.24, s32[2048]{0:T(1024)} %bitcast.140, f32[2048]{0:T(1024)S(1)} %bitcast.149, s32[2048]{0:T(1024)S(1)} %bitcast.132, f32[1,8,32,128]{3,2,1,0:T(8,128)S(1)} %copy-done.25, f32[1,8,32,128]{3,2,1,0:T(8,128)S(1)} %copy-done.12, ...), kind=kOutput, calls=%fused_computation.54 | convolution fusion | flops 807632896 | bytes 1729536 | tf_op jit(solution)/shard_map/srk,srz->skz/dot_general | solution.py:156
  85.4 5.0 %collective-permute-start.8 = (f32[1,7,32,128]{3,2,1,0:T(8,128)S(1)}, f32[1,7,32,128]{3,2,1,0:T(8,128)S(1)}, u32[]{:S(2)}, u32[]{:S(2)}) collective-permute-start(f32[1,7,32,128]{3,2,1,0:T(8,128)S(1)} %get-tuple-element.66), channel_id=1, source_target_pairs={{0,1},{1,2},{2,3},{3,4},{4,5},{5,6},{6,7},{7,8},{8,9},{9,10},{10,1... | collective-permute-start | bytes 344072 | tf_op jit(solution)/shard_map/ppermute | solution.py:18
  90.3 1.9 %collective-permute-start.9 = (f32[1,7,32,128]{3,2,1,0:T(8,128)S(1)}, f32[1,7,32,128]{3,2,1,0:T(8,128)S(1)}, u32[]{:S(2)}, u32[]{:S(2)}) collective-permute-start(f32[1,7,32,128]{3,2,1,0:T(8,128)S(1)} %get-tuple-element.67), channel_id=1, source_target_pairs={{1,0},{2,1},{3,2},{4,3},{5,4},{6,5},{7,6},{8,7},{9,8},{10,9},{11,1... | collective-permute-start | bytes 344072 | tf_op jit(solution)/shard_map/ppermute | solution.py:19
  92.3 0.3 fusion.491
  92.6 3.4 %collective-permute-start.10 = (f32[1]{0:T(128)}, f32[1]{0:T(128)}, u32[]{:S(2)}, u32[]{:S(2)}) collective-permute-start(f32[1]{0:T(128)} %bitcast.26), channel_id=1, source_target_pairs={{0,2},{1,3},{2,0},{3,1},{4,6},{5,7},{6,4},{7,5},{8,10},{9,11},{10,... | collective-permute-start | bytes 20 | tf_op jit(solution)/shard_map/ppermute | solution.py:51
  96.0 0.2 collective-permute-done.10
  96.8 0.1 fusion.227
  96.9 1.3 fusion.43
  98.3 3.8 %collective-permute-start.11 = (f32[1,7,32,128]{3,2,1,0:T(8,128)S(1)}, f32[1,7,32,128]{3,2,1,0:T(8,128)S(1)}, u32[]{:S(2)}, u32[]{:S(2)}) collective-permute-start(f32[1,7,32,128]{3,2,1,0:T(8,128)S(1)} %get-tuple-element.64), channel_id=1, source_target_pairs={{0,1},{1,2},{2,3},{3,4},{4,5},{5,6},{6,7},{7,8},{8,9},{9,10},{10,1... | collective-permute-start | bytes 344072 | tf_op jit(solution)/shard_map/ppermute | solution.py:18
  102.1 1.9 %collective-permute-start.12 = (f32[1,7,32,128]{3,2,1,0:T(8,128)S(1)}, f32[1,7,32,128]{3,2,1,0:T(8,128)S(1)}, u32[]{:S(2)}, u32[]{:S(2)}) collective-permute-start(f32[1,7,32,128]{3,2,1,0:T(8,128)S(1)} %get-tuple-element.65), channel_id=1, source_target_pairs={{1,0},{2,1},{3,2},{4,3},{5,4},{6,5},{7,6},{8,7},{9,8},{10,9},{11,1... | collective-permute-start | bytes 344072 | tf_op jit(solution)/shard_map/ppermute | solution.py:19
  104.0 0.3 fusion.514
  104.3 3.3 %collective-permute-start.13 = (f32[1]{0:T(128)}, f32[1]{0:T(128)}, u32[]{:S(2)}, u32[]{:S(2)}) collective-permute-start(f32[1]{0:T(128)} %add.815), channel_id=1, source_target_pairs={{0,4},{1,5},{2,6},{3,7},{4,0},{5,1},{6,2},{7,3},{8,12},{9,13},{10,... | collective-permute-start | bytes 20 | tf_op jit(solution)/shard_map/ppermute | solution.py:51
  107.6 0.2 collective-permute-done.13
  108.4 0.1 fusion.220
  108.5 1.3 fusion.40
  109.9 4.3 %collective-permute-start.14 = (f32[1,7,32,128]{3,2,1,0:T(8,128)S(1)}, f32[1,7,32,128]{3,2,1,0:T(8,128)S(1)}, u32[]{:S(2)}, u32[]{:S(2)}) collective-permute-start(f32[1,7,32,128]{3,2,1,0:T(8,128)S(1)} %get-tuple-element.62), channel_id=1, source_target_pairs={{0,1},{1,2},{2,3},{3,4},{4,5},{5,6},{6,7},{7,8},{8,9},{9,10},{10,1... | collective-permute-start | bytes 344072 | tf_op jit(solution)/shard_map/ppermute | solution.py:18
  114.2 3.4 %collective-permute-start.15 = (f32[1,7,32,128]{3,2,1,0:T(8,128)S(1)}, f32[1,7,32,128]{3,2,1,0:T(8,128)S(1)}, u32[]{:S(2)}, u32[]{:S(2)}) collective-permute-start(f32[1,7,32,128]{3,2,1,0:T(8,128)S(1)} %get-tuple-element.63), channel_id=1, source_target_pairs={{1,0},{2,1},{3,2},{4,3},{5,4},{6,5},{7,6},{8,7},{9,8},{10,9},{11,1... | collective-permute-start | bytes 344072 | tf_op jit(solution)/shard_map/ppermute | solution.py:19
  117.6 0.3 fusion.537
  117.9 3.7 %collective-permute-start.16 = (f32[1]{0:T(128)}, f32[1]{0:T(128)}, u32[]{:S(2)}, u32[]{:S(2)}) collective-permute-start(f32[1]{0:T(128)} %add.839), channel_id=1, source_target_pairs={{0,8},{1,9},{2,10},{3,11},{4,12},{5,13},{6,14},{7,15},{8,0},{9,1},... | collective-permute-start | bytes 20 | tf_op jit(solution)/shard_map/ppermute | solution.py:51
  121.6 0.2 collective-permute-done.16
  122.4 0.1 fusion.213
  122.5 1.3 fusion.37
  123.9 5.5 %collective-permute-start.17 = (f32[1]{0:T(128)}, f32[1]{0:T(128)}, u32[]{:S(2)}, u32[]{:S(2)}) collective-permute-start(f32[1]{0:T(128)} %add.863), channel_id=1, source_target_pairs={{0,1},{1,0},{2,3},{3,2},{4,5},{5,4},{6,7},{7,6},{8,9},{9,8},{10,11... | collective-permute-start | bytes 20 | tf_op jit(solution)/shard_map/ppermute | solution.py:51
  129.4 1.7 %fusion.557 = f32[8,32,128]{2,1,0:T(8,128)} fusion(f32[1,8,32,128]{3,2,1,0:T(8,128)S(1)} %fusion.37, f32[1,22,32,128]{3,2,1,0:T(8,128)} %get-tuple-element.37, f32[1,8,32,128]{3,2,1,0:T(8,128)S(1)} %fusion.43, f32[1,22,32,128]{3,2,1,0:T(8,128)S(1)} %get-tuple-element.31, f32[1,8,32,128]{3,2,1,0:T(8,128)S(1)} %fusion.40, f32[1,8,32,128]{3,2,1,0:T(8,128)S(1)} %copy-done.7, ...), kind=kLoop, calls=%fused_computation.817 | loop fusion | flops 327680 | bytes 1441792 | tf_op jit(solution)/shard_map/mul | solution.py:209
  (96 shorter events, 0.8 us)
Async XLA Ops:
  0.6 18.2 %copy-start.19 = (f32[1,4]{1,0:T(1,128)S(1)}, f32[1,4]{1,0:T(1,128)}, u32[]{:S(2)}) copy-start(f32[1,4]{1,0:T(1,128)} %param.17) | copy-start | bytes 52
  0.6 18.8 %copy-start.15 = (s32[1,2048]{1,0:T(1,128)S(1)}, s32[1,2048]{1,0:T(1,128)}, u32[]{:S(2)}) copy-start(s32[1,2048]{1,0:T(1,128)} %param.18) | copy-start | bytes 24580
  6.0 40.4 %copy-start = (f32[8,32,128]{2,1,0:T(8,128)S(1)}, f32[8,32,128]{2,1,0:T(8,128)}, u32[]{:S(2)}) copy-start(f32[8,32,128]{2,1,0:T(8,128)} %param.11) | copy-start | bytes 393220
  6.0 40.4 %copy-start.6 = (f32[1,8,32,128]{3,2,1,0:T(8,128)S(1)}, f32[1,8,32,128]{3,2,1,0:T(8,128)}, u32[]{:S(2)}) copy-start(f32[1,8,32,128]{3,2,1,0:T(8,128)} %param.12) | copy-start | bytes 393220
  6.0 40.3 %collective-permute-start = (f32[5,8,32,128]{3,2,1,0:T(8,128)S(1)}, f32[5,8,32,128]{3,2,1,0:T(8,128)S(1)}, u32[]{:S(2)}, u32[]{:S(2)}) collective-permute-start(f32[5,8,32,128]{3,2,1,0:T(8,128)S(1)} %get-tuple-element.38), channel_id=1, source_target_pairs={{0,1},{1,2},{2,3},{3,4},{4,5},{5,6},{6,7},{7,8},{8,9},{9,10},{10,1... | collective-permute-start | bytes 1966088 | tf_op jit(solution)/shard_map/ppermute | solution.py:32
  10.7 36.4 %collective-permute-start.1 = (f32[5,8,32,128]{3,2,1,0:T(8,128)S(1)}, f32[5,8,32,128]{3,2,1,0:T(8,128)}, u32[]{:S(2)}, u32[]{:S(2)}) collective-permute-start(f32[5,8,32,128]{3,2,1,0:T(8,128)S(1)} %get-tuple-element.38), channel_id=1, source_target_pairs={{1,0},{2,1},{3,2},{4,3},{5,4},{6,5},{7,6},{8,7},{9,8},{10,9},{11,1... | collective-permute-start | bytes 1966088 | tf_op jit(solution)/shard_map/ppermute | solution.py:33
  13.5 32.9 %copy-start.3 = (f32[1,8,32,128]{3,2,1,0:T(8,128)S(1)}, f32[1,8,32,128]{3,2,1,0:T(8,128)}, u32[]{:S(2)}) copy-start(f32[1,8,32,128]{3,2,1,0:T(8,128)} %param.13) | copy-start | bytes 393220
  13.5 32.8 %collective-permute-start.2 = (f32[5,6,32,128]{3,2,1,0:T(8,128)S(1)}, f32[5,6,32,128]{3,2,1,0:T(8,128)S(1)}, u32[]{:S(2)}, u32[]{:S(2)}) collective-permute-start(f32[5,6,32,128]{3,2,1,0:T(8,128)S(1)} %get-tuple-element.47), channel_id=1, source_target_pairs={{0,2},{1,3},{2,4},{3,5},{4,6},{5,7},{6,8},{7,9},{8,10},{9,11},{10,... | collective-permute-start | bytes 1474568 | tf_op jit(solution)/shard_map/ppermute | solution.py:31
  16.8 33.6 %collective-permute-start.3 = (f32[5,6,32,128]{3,2,1,0:T(8,128)}, f32[5,6,32,128]{3,2,1,0:T(8,128)}, u32[]{:S(2)}, u32[]{:S(2)}) collective-permute-start(f32[5,6,32,128]{3,2,1,0:T(8,128)} %get-tuple-element.46), channel_id=1, source_target_pairs={{2,0},{3,1},{4,2},{5,3},{6,4},{7,5},{8,6},{9,7},{10,8},{11,9},{12,... | collective-permute-start | bytes 1474568 | tf_op jit(solution)/shard_map/ppermute | solution.py:34
  18.1 28.4 %copy-start.20 = (s32[22]{0:T(128)}, s32[22]{0:T(128)S(1)}, u32[]{:S(2)}) copy-start(s32[22]{0:T(128)S(1)} %add_multiply_fusion) | copy-start | bytes 268
  18.1 28.3 %copy-start.22 = (s32[32]{0:T(128)}, s32[32]{0:T(128)S(1)}, u32[]{:S(2)}) copy-start(s32[32]{0:T(128)S(1)} %iota_multiply_fusion) | copy-start | bytes 388
  20.3 58.1 %copy-start.17 = (s32[1,2048]{1,0:T(1,128)}, s32[1,2048]{1,0:T(1,128)S(1)}, u32[]{:S(2)}) copy-start(s32[1,2048]{1,0:T(1,128)S(1)} %fusion.610) | copy-start | bytes 24580
  46.3 0.8 copy-start.1
  47.1 1.4 %copy-start.5 = (f32[1,8,32,128]{3,2,1,0:T(8,128)S(1)}, f32[1,8,32,128]{3,2,1,0:T(8,128)}, u32[]{:S(2)}) copy-start(f32[1,8,32,128]{3,2,1,0:T(8,128)} %get-tuple-element.39) | copy-start | bytes 393220
  48.5 3.1 %copy-start.2 = (f32[5,6,32,128]{3,2,1,0:T(8,128)S(1)}, f32[5,6,32,128]{3,2,1,0:T(8,128)}, u32[]{:S(2)}) copy-start(f32[5,6,32,128]{3,2,1,0:T(8,128)} %copy-done.1) | copy-start | bytes 1474564
  51.5 1.5 %copy-start.21 = (s32[22]{0:T(128)S(1)}, s32[22]{0:T(128)}, u32[]{:S(2)}) copy-start(s32[22]{0:T(128)} %copy-done.20) | copy-start | bytes 268
  51.6 1.5 %copy-start.23 = (s32[32]{0:T(128)S(1)}, s32[32]{0:T(128)}, u32[]{:S(2)}) copy-start(s32[32]{0:T(128)} %copy-done.22) | copy-start | bytes 388
  55.2 1.3 copy-start.4
  58.2 14.4 %collective-permute-start.4 = (f32[1,8,32,128]{3,2,1,0:T(8,128)S(1)}, f32[1,8,32,128]{3,2,1,0:T(8,128)S(1)}, u32[]{:S(2)}, u32[]{:S(2)}) collective-permute-start(f32[1,8,32,128]{3,2,1,0:T(8,128)S(1)} %get-tuple-element.32), channel_id=1, source_target_pairs={{0,1},{1,2},{2,3},{3,4},{4,5},{5,6},{6,7},{7,8},{8,9},{9,10},{10,1... | collective-permute-start | bytes 393224 | tf_op jit(solution)/shard_map/ppermute | solution.py:32
  60.3 12.3 %collective-permute-start.5 = (f32[1,8,32,128]{3,2,1,0:T(8,128)S(1)}, f32[1,8,32,128]{3,2,1,0:T(8,128)S(1)}, u32[]{:S(2)}, u32[]{:S(2)}) collective-permute-start(f32[1,8,32,128]{3,2,1,0:T(8,128)S(1)} %get-tuple-element.32), channel_id=1, source_target_pairs={{1,0},{2,1},{3,2},{4,3},{5,4},{6,5},{7,6},{8,7},{9,8},{10,9},{11,1... | collective-permute-start | bytes 393224 | tf_op jit(solution)/shard_map/ppermute | solution.py:33
  62.5 10.0 %collective-permute-start.6 = (f32[1,6,32,128]{3,2,1,0:T(8,128)S(1)}, f32[1,6,32,128]{3,2,1,0:T(8,128)S(1)}, u32[]{:S(2)}, u32[]{:S(2)}) collective-permute-start(f32[1,6,32,128]{3,2,1,0:T(8,128)S(1)} %get-tuple-element.71), channel_id=1, source_target_pairs={{0,2},{1,3},{2,4},{3,5},{4,6},{5,7},{6,8},{7,9},{8,10},{9,11},{10,... | collective-permute-start | bytes 294920 | tf_op jit(solution)/shard_map/ppermute | solution.py:31
  66.3 7.1 %collective-permute-start.7 = (f32[1,6,32,128]{3,2,1,0:T(8,128)S(1)}, f32[1,6,32,128]{3,2,1,0:T(8,128)S(1)}, u32[]{:S(2)}, u32[]{:S(2)}) collective-permute-start(f32[1,6,32,128]{3,2,1,0:T(8,128)S(1)} %get-tuple-element.70), channel_id=1, source_target_pairs={{2,0},{3,1},{4,2},{5,3},{6,4},{7,5},{8,6},{9,7},{10,8},{11,9},{12,... | collective-permute-start | bytes 294920 | tf_op jit(solution)/shard_map/ppermute | solution.py:34
  76.7 3.3 %copy-start.16 = (f32[1,4,2048]{2,1,0:T(4,128)S(1)}, f32[1,4,2048]{2,1,0:T(4,128)}, u32[]{:S(2)}) copy-start(f32[1,4,2048]{2,1,0:T(4,128)} %param.19) | copy-start | bytes 98308
  76.7 6.6 %copy-start.10 = (f32[1,15,32,128]{3,2,1,0:T(8,128)S(1)}, f32[1,15,32,128]{3,2,1,0:T(8,128)}, u32[]{:S(2)}) copy-start(f32[1,15,32,128]{3,2,1,0:T(8,128)} %fusion.250) | copy-start | bytes 737284
  76.7 6.6 %copy-start.11 = (f32[1,8,32,128]{3,2,1,0:T(8,128)S(1)}, f32[1,8,32,128]{3,2,1,0:T(8,128)}, u32[]{:S(2)}) copy-start(f32[1,8,32,128]{3,2,1,0:T(8,128)} %get-tuple-element.56) | copy-start | bytes 393220
  76.7 6.6 %copy-start.12 = (f32[1,8,32,128]{3,2,1,0:T(8,128)S(1)}, f32[1,8,32,128]{3,2,1,0:T(8,128)}, u32[]{:S(2)}) copy-start(f32[1,8,32,128]{3,2,1,0:T(8,128)} %get-tuple-element.57) | copy-start | bytes 393220
  76.7 6.6 %copy-start.13 = (f32[1,8,32,128]{3,2,1,0:T(8,128)S(1)}, f32[1,8,32,128]{3,2,1,0:T(8,128)}, u32[]{:S(2)}) copy-start(f32[1,8,32,128]{3,2,1,0:T(8,128)} %param.14) | copy-start | bytes 393220
  76.7 6.6 %copy-start.24 = (s32[8,32]{1,0:T(8,128)S(1)}, s32[8,32]{1,0:T(8,128)}, u32[]{:S(2)}) copy-start(s32[8,32]{1,0:T(8,128)} %multiply_add_fusion) | copy-start | bytes 3076
  76.7 6.6 %copy-start.25 = (f32[1,8,32,128]{3,2,1,0:T(8,128)S(1)}, f32[1,8,32,128]{3,2,1,0:T(8,128)}, u32[]{:S(2)}) copy-start(f32[1,8,32,128]{3,2,1,0:T(8,128)} %param.15) | copy-start | bytes 393220
  85.3 11.6 %copy-start.18 = (s32[1,2048]{1,0:T(1,128)S(1)}, s32[1,2048]{1,0:T(1,128)}, u32[]{:S(2)}) copy-start(s32[1,2048]{1,0:T(1,128)} %copy-done.17) | copy-start | bytes 24580
  85.4 11.4 %collective-permute-start.8 = (f32[1,7,32,128]{3,2,1,0:T(8,128)S(1)}, f32[1,7,32,128]{3,2,1,0:T(8,128)S(1)}, u32[]{:S(2)}, u32[]{:S(2)}) collective-permute-start(f32[1,7,32,128]{3,2,1,0:T(8,128)S(1)} %get-tuple-element.66), channel_id=1, source_target_pairs={{0,1},{1,2},{2,3},{3,4},{4,5},{5,6},{6,7},{7,8},{8,9},{9,10},{10,1... | collective-permute-start | bytes 344072 | tf_op jit(solution)/shard_map/ppermute | solution.py:18
  90.3 6.4 %collective-permute-start.9 = (f32[1,7,32,128]{3,2,1,0:T(8,128)S(1)}, f32[1,7,32,128]{3,2,1,0:T(8,128)S(1)}, u32[]{:S(2)}, u32[]{:S(2)}) collective-permute-start(f32[1,7,32,128]{3,2,1,0:T(8,128)S(1)} %get-tuple-element.67), channel_id=1, source_target_pairs={{1,0},{2,1},{3,2},{4,3},{5,4},{6,5},{7,6},{8,7},{9,8},{10,9},{11,1... | collective-permute-start | bytes 344072 | tf_op jit(solution)/shard_map/ppermute | solution.py:19
  92.6 3.6 %collective-permute-start.10 = (f32[1]{0:T(128)}, f32[1]{0:T(128)}, u32[]{:S(2)}, u32[]{:S(2)}) collective-permute-start(f32[1]{0:T(128)} %bitcast.26), channel_id=1, source_target_pairs={{0,2},{1,3},{2,0},{3,1},{4,6},{5,7},{6,4},{7,5},{8,10},{9,11},{10,... | collective-permute-start | bytes 20 | tf_op jit(solution)/shard_map/ppermute | solution.py:51
  98.3 10.0 %collective-permute-start.11 = (f32[1,7,32,128]{3,2,1,0:T(8,128)S(1)}, f32[1,7,32,128]{3,2,1,0:T(8,128)S(1)}, u32[]{:S(2)}, u32[]{:S(2)}) collective-permute-start(f32[1,7,32,128]{3,2,1,0:T(8,128)S(1)} %get-tuple-element.64), channel_id=1, source_target_pairs={{0,1},{1,2},{2,3},{3,4},{4,5},{5,6},{6,7},{7,8},{8,9},{9,10},{10,1... | collective-permute-start | bytes 344072 | tf_op jit(solution)/shard_map/ppermute | solution.py:18
  102.1 6.2 %collective-permute-start.12 = (f32[1,7,32,128]{3,2,1,0:T(8,128)S(1)}, f32[1,7,32,128]{3,2,1,0:T(8,128)S(1)}, u32[]{:S(2)}, u32[]{:S(2)}) collective-permute-start(f32[1,7,32,128]{3,2,1,0:T(8,128)S(1)} %get-tuple-element.65), channel_id=1, source_target_pairs={{1,0},{2,1},{3,2},{4,3},{5,4},{6,5},{7,6},{8,7},{9,8},{10,9},{11,1... | collective-permute-start | bytes 344072 | tf_op jit(solution)/shard_map/ppermute | solution.py:19
  104.3 3.4 %collective-permute-start.13 = (f32[1]{0:T(128)}, f32[1]{0:T(128)}, u32[]{:S(2)}, u32[]{:S(2)}) collective-permute-start(f32[1]{0:T(128)} %add.815), channel_id=1, source_target_pairs={{0,4},{1,5},{2,6},{3,7},{4,0},{5,1},{6,2},{7,3},{8,12},{9,13},{10,... | collective-permute-start | bytes 20 | tf_op jit(solution)/shard_map/ppermute | solution.py:51
  109.8 19.6 %copy-start.8 = (f32[1,8,32,128]{3,2,1,0:T(8,128)}, f32[1,8,32,128]{3,2,1,0:T(8,128)S(1)}, u32[]{:S(2)}) copy-start(f32[1,8,32,128]{3,2,1,0:T(8,128)S(1)} %fusion.40) | copy-start | bytes 393220
  109.9 12.5 %collective-permute-start.14 = (f32[1,7,32,128]{3,2,1,0:T(8,128)S(1)}, f32[1,7,32,128]{3,2,1,0:T(8,128)S(1)}, u32[]{:S(2)}, u32[]{:S(2)}) collective-permute-start(f32[1,7,32,128]{3,2,1,0:T(8,128)S(1)} %get-tuple-element.62), channel_id=1, source_target_pairs={{0,1},{1,2},{2,3},{3,4},{4,5},{5,6},{6,7},{7,8},{8,9},{9,10},{10,1... | collective-permute-start | bytes 344072 | tf_op jit(solution)/shard_map/ppermute | solution.py:18
  114.2 8.2 %collective-permute-start.15 = (f32[1,7,32,128]{3,2,1,0:T(8,128)S(1)}, f32[1,7,32,128]{3,2,1,0:T(8,128)S(1)}, u32[]{:S(2)}, u32[]{:S(2)}) collective-permute-start(f32[1,7,32,128]{3,2,1,0:T(8,128)S(1)} %get-tuple-element.63), channel_id=1, source_target_pairs={{1,0},{2,1},{3,2},{4,3},{5,4},{6,5},{7,6},{8,7},{9,8},{10,9},{11,1... | collective-permute-start | bytes 344072 | tf_op jit(solution)/shard_map/ppermute | solution.py:19
  117.9 3.9 %collective-permute-start.16 = (f32[1]{0:T(128)}, f32[1]{0:T(128)}, u32[]{:S(2)}, u32[]{:S(2)}) collective-permute-start(f32[1]{0:T(128)} %add.839), channel_id=1, source_target_pairs={{0,8},{1,9},{2,10},{3,11},{4,12},{5,13},{6,14},{7,15},{8,0},{9,1},... | collective-permute-start | bytes 20 | tf_op jit(solution)/shard_map/ppermute | solution.py:51
  122.5 6.9 %copy-start.7 = (f32[1,8,32,128]{3,2,1,0:T(8,128)S(1)}, f32[1,8,32,128]{3,2,1,0:T(8,128)}, u32[]{:S(2)}) copy-start(f32[1,8,32,128]{3,2,1,0:T(8,128)} %get-tuple-element.33) | copy-start | bytes 393220
  122.5 6.8 %copy-start.9 = (f32[8,32,128]{2,1,0:T(8,128)S(1)}, f32[8,32,128]{2,1,0:T(8,128)}, u32[]{:S(2)}) copy-start(f32[8,32,128]{2,1,0:T(8,128)} %param.10) | copy-start | bytes 393220
  123.9 7.8 %copy-start.14 = (f32[1,8,32,128]{3,2,1,0:T(8,128)}, f32[1,8,32,128]{3,2,1,0:T(8,128)S(1)}, u32[]{:S(2)}) copy-start(f32[1,8,32,128]{3,2,1,0:T(8,128)S(1)} %fusion.37) | copy-start | bytes 393220
  123.9 7.2 %collective-permute-start.17 = (f32[1]{0:T(128)}, f32[1]{0:T(128)}, u32[]{:S(2)}, u32[]{:S(2)}) collective-permute-start(f32[1]{0:T(128)} %add.863), channel_id=1, source_target_pairs={{0,1},{1,0},{2,3},{3,2},{4,5},{5,4},{6,7},{7,6},{8,9},{9,8},{10,11... | collective-permute-start | bytes 20 | tf_op jit(solution)/shard_map/ppermute | solution.py:51

commit v8 on v4

--- a/solution.py
+++ b/solution.py
@@ -103,7 +103,10 @@
     adjoint_lap = wide_operator(first[1 + shots :], adjoint_operand, flux_buoyancy)
 
     def operator(values):
-        return wide_operator(extended(values, 1, HALO), values, flux_buoyancy)
+        wide = extended(values, 1, HALO)
+        cross = lax.optimization_barrier(cross_terms(values, buoyancy))
+        flux = flux_buoyancy * forward_diff(wide, 1, planes + 7, start=HALO - 4)
+        return backward_diff(flux, 1, planes) + cross
 
     source_local = source_cell - offset
     source_owned = (source_local >= 0) & (source_local < cells)
@@ -125,10 +128,10 @@
         )
         return jnp.sum(jnp.where(col_pick, picked, 0.0), axis=2)
 
-    def inject(field, amounts):
+    def injected(amounts):
         spread = jnp.where(col_pick, amounts[:, :, None], 0.0)
         added = jnp.einsum("srk,srz->skz", row_pick, spread, precision=lax.Precision.HIGHEST)
-        return field + added.reshape(shape)
+        return lax.optimization_barrier(added.reshape(shape))
 
     before, current = (wave_prev, wave_now)
     laps = []
@@ -155,7 +158,7 @@
                 misfit = butterfly_round(misfit, "mp", distances.pop(0))
             lap = operator(kappa * mu_near)
         state = 2.0 * mu_near + lap - mu_far
-        state = inject(state, resids[level - 1])
+        state = state + injected(resids[level - 1])
         gradient = gradient + state * laps[level - 1]
         mu_far, mu_near = (mu_near, state)
         mu_near, misfit = lax.optimization_barrier((mu_near, misfit))

time: 99.9 us -> 99.5 us (level)
  starting transfers between devices: 52.3 us -> 43.8 us
  waiting for transfers between devices: 14.1 us -> 19.3 us
  other arithmetic: 11.2 us -> 12.8 us
    ppermute x7, waiting for transfers between devices: 9.1 us -> 15.2 us  [extended(): after = lax.ppermute(first, 'mp', down)]
    ppermute x4, starting transfers between devices: 13.9 us -> 8.77 us  [butterfly_round(): return values + lax.ppermute(values, axis, pairs)]
    ppermute x7, starting transfers between devices: 22.9 us -> 19.9 us  [extended(): before = lax.ppermute(last, 'mp', up)]
    add x0 -> x9, other arithmetic: none -> 2.31 us  [the longest x6 1.84 us: cross_terms(): total = total + backward_diff(pad_axis(flux, axis), axis, length)]
  transfers between devices with their start and end apart: 18 -> 18, of which waited for: 10 -> 9; matrix products, arithmetic and copies ran while one was open for 8% -> 9% of each run, Pallas kernels for 0% -> 0%
where the time goes in v8:
time: 99.5 us; the launch traced here: 98.1 us
  starting transfers between devices  43.8 us (44%)
  waiting for transfers between devices  19.3 us (19%)
  other arithmetic  12.8 us (13%)
  matrix products  11.4 us (11%)
  between operations  8.36 us (8%)
  local copies, waits for them, and re-layouts  2.38 us (2%)
    ppermute x7, starting transfers between devices, extended(): before = lax.ppermute(last, 'mp', up)  19.9 us
    ppermute x7, waiting for transfers between devices, extended(): after = lax.ppermute(first, 'mp', down)  15.2 us
    ppermute x7, starting transfers between devices, extended(): after = lax.ppermute(first, 'mp', down)  15.1 us
    ppermute x4, starting transfers between devices, butterfly_round(): return values + lax.ppermute(values, axis, pairs)  8.77 us
    dot_general x4, matrix products, sample(): jnp.einsum('srk,skz->srz', row_pick, field.reshape(shots, rows, cz), prec...  6.43 us
    dot_general x4, matrix products, injected(): jnp.einsum('srk,srz->skz', row_pick, spread, precision=lax.Precision.HIGH...  4.93 us
    ppermute x7, waiting for transfers between devices, extended(): before = lax.ppermute(last, 'mp', up)  3.87 us
    add x4, other arithmetic, local(): following = following + jnp.where(source_hit, amount, 0.0)  3.22 us
  transfers between devices with their start and end apart: 18, of which 9 were waited for; matrix products, arithmetic and copies ran while one was open for 9% of the time, Pallas kernels for 0%

profile of v8, /device:TPU:1, one launch (start us, length us, event | category | flops | bytes accessed | tf_op | source)
XLA Modules:
  0.0 98.1 jit_solution(8460907531088279884)
XLA Ops:
  0.6 1.1 %bitcast_multiply_fusion.8 = (f32[1,8,32,128]{3,2,1,0:T(8,128)S(1)}, f32[8,32,128]{2,1,0:T(8,128)S(1)}) fusion(f32[1,8,32,128]{3,2,1,0:T(8,128)} %param.14, f32[8,32,128]{2,1,0:T(8,128)} %param.11, f32[8,32,128]{2,1,0:T(8,128)} %param.10), kind=kLoop, calls=%fused_computation.881 | loop fusion | flops 98304 | bytes 655360 | tf_op jit(solution)/shard_map/mul | solution.py:99
  1.7 1.0 %pad_maximum_fusion.1 = f32[3,8,32,128]{3,2,1,0:T(8,128)S(1)} fusion(f32[1,8,32,128]{3,2,1,0:T(8,128)S(1)} %get-tuple-element.40, f32[1,8,32,128]{3,2,1,0:T(8,128)} %param.13, f32[1,8,32,128]{3,2,1,0:T(8,128)} %bitcast.123), kind=kLoop, calls=%fused_computation.168 | loop fusion | flops 196608 | bytes 786432 | tf_op jit(solution)/shard_map/concatenate | solution.py:100
  2.9 2.0 %collective-permute-start.1 = (f32[3,7,32,128]{3,2,1,0:T(8,128)S(1)}, f32[3,7,32,128]{3,2,1,0:T(8,128)S(1)}, u32[]{:S(2)}, u32[]{:S(2)}) collective-permute-start(f32[3,7,32,128]{3,2,1,0:T(8,128)S(1)} %get-tuple-element.42), channel_id=1, source_target_pairs={{1,0},{2,1},{3,2},{4,3},{5,4},{6,5},{7,6},{8,7},{9,8},{10,9},{11,1... | collective-permute-start | bytes 1032200 | tf_op jit(solution)/shard_map/ppermute | solution.py:19
  4.8 4.5 %collective-permute-start = (f32[3,7,32,128]{3,2,1,0:T(8,128)S(1)}, f32[3,7,32,128]{3,2,1,0:T(8,128)S(1)}, u32[]{:S(2)}, u32[]{:S(2)}) collective-permute-start(f32[3,7,32,128]{3,2,1,0:T(8,128)S(1)} %get-tuple-element.43), channel_id=1, source_target_pairs={{0,1},{1,2},{2,3},{3,4},{4,5},{5,6},{6,7},{7,8},{8,9},{9,10},{10,1... | collective-permute-start | bytes 1032200 | tf_op jit(solution)/shard_map/ppermute | solution.py:18
  10.0 0.6 fusion.619
  10.7 0.5 fusion.336
  11.3 1.0 %collective-permute-done.1 = f32[3,7,32,128]{3,2,1,0:T(8,128)S(1)} collective-permute-done((f32[3,7,32,128]{3,2,1,0:T(8,128)S(1)}, f32[3,7,32,128]{3,2,1,0:T(8,128)S(1)}, u32[]{:S(2)}, u32[]{:S(2)}) %collective-permute-start.1) | collective-permute-done | bytes 344096 | tf_op jit(solution)/shard_map/ppermute | solution.py:19
  12.3 3.9 %collective-permute-done = f32[3,7,32,128]{3,2,1,0:T(8,128)S(1)} collective-permute-done((f32[3,7,32,128]{3,2,1,0:T(8,128)S(1)}, f32[3,7,32,128]{3,2,1,0:T(8,128)S(1)}, u32[]{:S(2)}, u32[]{:S(2)}) %collective-permute-start) | collective-permute-done | bytes 344096 | tf_op jit(solution)/shard_map/ppermute | solution.py:18
  16.3 0.1 fusion.114
  16.4 0.8 copy-done.6
  17.2 1.0 fusion.587
  18.2 0.3 fusion.382
  18.5 4.4 %collective-permute-start.2 = (f32[1,7,32,128]{3,2,1,0:T(8,128)S(1)}, f32[1,7,32,128]{3,2,1,0:T(8,128)S(1)}, u32[]{:S(2)}, u32[]{:S(2)}) collective-permute-start(f32[1,7,32,128]{3,2,1,0:T(8,128)S(1)} %get-tuple-element.72), channel_id=1, source_target_pairs={{0,1},{1,2},{2,3},{3,4},{4,5},{5,6},{6,7},{7,8},{8,9},{9,10},{10,1... | collective-permute-start | bytes 344072 | tf_op jit(solution)/shard_map/ppermute | solution.py:18
  22.9 1.9 %collective-permute-start.3 = (f32[1,7,32,128]{3,2,1,0:T(8,128)S(1)}, f32[1,7,32,128]{3,2,1,0:T(8,128)S(1)}, u32[]{:S(2)}, u32[]{:S(2)}) collective-permute-start(f32[1,7,32,128]{3,2,1,0:T(8,128)S(1)} %get-tuple-element.73), channel_id=1, source_target_pairs={{1,0},{2,1},{3,2},{4,3},{5,4},{6,5},{7,6},{8,7},{9,8},{10,9},{11,1... | collective-permute-start | bytes 344072 | tf_op jit(solution)/shard_map/ppermute | solution.py:19
  24.8 0.3 fusion.204
  25.1 0.1 fusion.122
  25.2 1.6 %fusion.16 = f32[2048]{0:T(1024)S(1)} fusion(f32[256,128]{1,0:T(8,128)S(1)} %bitcast.127, s32[2048]{0:T(1024)S(1)} %bitcast.139, s32[2048]{0:T(1024)S(1)} %bitcast.131), kind=kOutput, calls=%fused_computation.15 | convolution fusion | flops 806615040 | bytes 155648 | tf_op jit(solution)/shard_map/srk,skz->srz/dot_general | solution.py:126
  26.9 2.1 %collective-permute-done.3 = f32[1,7,32,128]{3,2,1,0:T(8,128)S(1)} collective-permute-done((f32[1,7,32,128]{3,2,1,0:T(8,128)S(1)}, f32[1,7,32,128]{3,2,1,0:T(8,128)S(1)}, u32[]{:S(2)}, u32[]{:S(2)}) %collective-permute-start.3) | collective-permute-done | bytes 114720 | tf_op jit(solution)/shard_map/ppermute | solution.py:19
  29.0 0.1 fusion.107
  29.1 0.8 fusion.589
  29.9 0.3 fusion.405
  30.2 1.9 %collective-permute-start.4 = (f32[1,7,32,128]{3,2,1,0:T(8,128)S(1)}, f32[1,7,32,128]{3,2,1,0:T(8,128)S(1)}, u32[]{:S(2)}, u32[]{:S(2)}) collective-permute-start(f32[1,7,32,128]{3,2,1,0:T(8,128)S(1)} %get-tuple-element.70), channel_id=1, source_target_pairs={{0,1},{1,2},{2,3},{3,4},{4,5},{5,6},{6,7},{7,8},{8,9},{9,10},{10,1... | collective-permute-start | bytes 344072 | tf_op jit(solution)/shard_map/ppermute | solution.py:18
  32.2 2.4 %collective-permute-start.5 = (f32[1,7,32,128]{3,2,1,0:T(8,128)S(1)}, f32[1,7,32,128]{3,2,1,0:T(8,128)S(1)}, u32[]{:S(2)}, u32[]{:S(2)}) collective-permute-start(f32[1,7,32,128]{3,2,1,0:T(8,128)S(1)} %get-tuple-element.71), channel_id=1, source_target_pairs={{1,0},{2,1},{3,2},{4,3},{5,4},{6,5},{7,6},{8,7},{9,8},{10,9},{11,1... | collective-permute-start | bytes 344072 | tf_op jit(solution)/shard_map/ppermute | solution.py:19
  34.6 0.3 fusion.228
  34.9 1.6 %fusion.19 = f32[2048]{0:T(1024)S(1)} fusion(f32[256,128]{1,0:T(8,128)S(1)} %bitcast.128, s32[2048]{0:T(1024)S(1)} %bitcast.140, s32[2048]{0:T(1024)S(1)} %bitcast.132), kind=kOutput, calls=%fused_computation.16 | convolution fusion | flops 806615040 | bytes 155648 | tf_op jit(solution)/shard_map/srk,skz->srz/dot_general | solution.py:126
  36.5 1.8 %collective-permute-done.5 = f32[1,7,32,128]{3,2,1,0:T(8,128)S(1)} collective-permute-done((f32[1,7,32,128]{3,2,1,0:T(8,128)S(1)}, f32[1,7,32,128]{3,2,1,0:T(8,128)S(1)}, u32[]{:S(2)}, u32[]{:S(2)}) %collective-permute-start.5) | collective-permute-done | bytes 114720 | tf_op jit(solution)/shard_map/ppermute | solution.py:19
  38.4 0.7 fusion.591
  39.2 0.3 fusion.428
  39.5 1.9 %collective-permute-start.6 = (f32[1,7,32,128]{3,2,1,0:T(8,128)S(1)}, f32[1,7,32,128]{3,2,1,0:T(8,128)S(1)}, u32[]{:S(2)}, u32[]{:S(2)}) collective-permute-start(f32[1,7,32,128]{3,2,1,0:T(8,128)S(1)} %get-tuple-element.68), channel_id=1, source_target_pairs={{0,1},{1,2},{2,3},{3,4},{4,5},{5,6},{6,7},{7,8},{8,9},{9,10},{10,1... | collective-permute-start | bytes 344072 | tf_op jit(solution)/shard_map/ppermute | solution.py:18
  41.4 2.6 %collective-permute-start.7 = (f32[1,7,32,128]{3,2,1,0:T(8,128)S(1)}, f32[1,7,32,128]{3,2,1,0:T(8,128)S(1)}, u32[]{:S(2)}, u32[]{:S(2)}) collective-permute-start(f32[1,7,32,128]{3,2,1,0:T(8,128)S(1)} %get-tuple-element.69), channel_id=1, source_target_pairs={{1,0},{2,1},{3,2},{4,3},{5,4},{6,5},{7,6},{8,7},{9,8},{10,9},{11,1... | collective-permute-start | bytes 344072 | tf_op jit(solution)/shard_map/ppermute | solution.py:19
  44.0 0.3 fusion.252
  44.4 1.6 %fusion.22 = f32[2048]{0:T(1024)S(1)} fusion(f32[256,128]{1,0:T(8,128)S(1)} %bitcast.129, s32[2048]{0:T(1024)S(1)} %bitcast.141, s32[2048]{0:T(1024)S(1)} %bitcast.133), kind=kOutput, calls=%fused_computation.17 | convolution fusion | flops 806615040 | bytes 155648 | tf_op jit(solution)/shard_map/srk,skz->srz/dot_general | solution.py:126
  46.0 2.4 %collective-permute-done.7 = f32[1,7,32,128]{3,2,1,0:T(8,128)S(1)} collective-permute-done((f32[1,7,32,128]{3,2,1,0:T(8,128)S(1)}, f32[1,7,32,128]{3,2,1,0:T(8,128)S(1)}, u32[]{:S(2)}, u32[]{:S(2)}) %collective-permute-start.7) | collective-permute-done | bytes 114720 | tf_op jit(solution)/shard_map/ppermute | solution.py:19
  48.6 0.7 fusion.593
  49.3 1.6 %fusion.13 = f32[2048]{0:T(1024)S(1)} fusion(f32[256,128]{1,0:T(8,128)S(1)} %bitcast.130, s32[2048]{0:T(1024)S(1)} %bitcast.142, s32[2048]{0:T(1024)S(1)} %bitcast.134), kind=kOutput, calls=%fused_computation.14 | convolution fusion | flops 806615040 | bytes 155648 | tf_op jit(solution)/shard_map/srk,skz->srz/dot_general | solution.py:126
  51.0 0.7 multiply_reduce_fusion.1
  51.6 1.2 %fusion.25 = f32[1,8,32,128]{3,2,1,0:T(8,128)S(1)} fusion(s32[8,32]{1,0:T(8,128)S(1)} %multiply_add_fusion, s32[2048]{0:T(1024)S(1)} %bitcast.143, f32[2048]{0:T(1024)S(1)} %bitcast.154, s32[2048]{0:T(1024)S(1)} %bitcast.135), kind=kOutput, calls=%fused_computation.18 | convolution fusion | flops 806354944 | bytes 156672 | tf_op jit(solution)/shard_map/srk,srz->skz/dot_general | solution.py:133
  55.5 0.3 fusion.155
  55.9 0.3 fusion.451
  56.2 1.2 %fusion.34 = f32[1,8,32,128]{3,2,1,0:T(8,128)S(1)} fusion(s32[8,32]{1,0:T(8,128)S(1)} %multiply_add_fusion, s32[2048]{0:T(1024)S(1)} %bitcast.144, f32[2048]{0:T(1024)S(1)} %bitcast.152, s32[2048]{0:T(1024)S(1)} %bitcast.136), kind=kOutput, calls=%fused_computation.21 | convolution fusion | flops 806354944 | bytes 156672 | tf_op jit(solution)/shard_map/srk,srz->skz/dot_general | solution.py:133
  57.4 1.2 %fusion.28 = f32[1,8,32,128]{3,2,1,0:T(8,128)S(1)} fusion(s32[8,32]{1,0:T(8,128)S(1)} %multiply_add_fusion, s32[2048]{0:T(1024)S(1)} %bitcast.145, f32[2048]{0:T(1024)S(1)} %bitcast.151, s32[2048]{0:T(1024)S(1)} %bitcast.137), kind=kOutput, calls=%fused_computation.19 | convolution fusion | flops 806354944 | bytes 156672 | tf_op jit(solution)/shard_map/srk,srz->skz/dot_general | solution.py:133
  58.7 3.0 %collective-permute-start.10 = (f32[1]{0:T(128)}, f32[1]{0:T(128)}, u32[]{:S(2)}, u32[]{:S(2)}) collective-permute-start(f32[1]{0:T(128)} %bitcast.26), channel_id=1, source_target_pairs={{0,2},{1,3},{2,0},{3,1},{4,6},{5,7},{6,4},{7,5},{8,10},{9,11},{10,... | collective-permute-start | bytes 20 | tf_op jit(solution)/shard_map/ppermute | solution.py:36
  61.7 1.9 %collective-permute-start.8 = (f32[1,7,32,128]{3,2,1,0:T(8,128)S(1)}, f32[1,7,32,128]{3,2,1,0:T(8,128)S(1)}, u32[]{:S(2)}, u32[]{:S(2)}) collective-permute-start(f32[1,7,32,128]{3,2,1,0:T(8,128)S(1)} %get-tuple-element.64), channel_id=1, source_target_pairs={{0,1},{1,2},{2,3},{3,4},{4,5},{5,6},{6,7},{7,8},{8,9},{9,10},{10,1... | collective-permute-start | bytes 344072 | tf_op jit(solution)/shard_map/ppermute | solution.py:18
  63.6 2.4 %collective-permute-start.9 = (f32[1,7,32,128]{3,2,1,0:T(8,128)S(1)}, f32[1,7,32,128]{3,2,1,0:T(8,128)S(1)}, u32[]{:S(2)}, u32[]{:S(2)}) collective-permute-start(f32[1,7,32,128]{3,2,1,0:T(8,128)S(1)} %get-tuple-element.65), channel_id=1, source_target_pairs={{1,0},{2,1},{3,2},{4,3},{5,4},{6,5},{7,6},{8,7},{9,8},{10,9},{11,1... | collective-permute-start | bytes 344072 | tf_op jit(solution)/shard_map/ppermute | solution.py:19
  66.0 0.3 fusion.276
  66.3 1.2 %fusion.31 = f32[1,8,32,128]{3,2,1,0:T(8,128)S(1)} fusion(s32[8,32]{1,0:T(8,128)S(1)} %multiply_add_fusion, s32[2048]{0:T(1024)S(1)} %bitcast.146, f32[2048]{0:T(1024)S(1)} %bitcast.149, s32[2048]{0:T(1024)S(1)} %bitcast.138), kind=kOutput, calls=%fused_computation.20 | convolution fusion | flops 806354944 | bytes 156672 | tf_op jit(solution)/shard_map/srk,srz->skz/dot_general | solution.py:133
  68.3 1.5 %collective-permute-done.9 = f32[1,7,32,128]{3,2,1,0:T(8,128)S(1)} collective-permute-done((f32[1,7,32,128]{3,2,1,0:T(8,128)S(1)}, f32[1,7,32,128]{3,2,1,0:T(8,128)S(1)}, u32[]{:S(2)}, u32[]{:S(2)}) %collective-permute-start.9) | collective-permute-done | bytes 114720 | tf_op jit(solution)/shard_map/ppermute | solution.py:19
  69.8 0.1 fusion.86
  70.0 0.3 fusion.474
  70.3 2.1 %collective-permute-start.13 = (f32[1]{0:T(128)}, f32[1]{0:T(128)}, u32[]{:S(2)}, u32[]{:S(2)}) collective-permute-start(f32[1]{0:T(128)} %add.821), channel_id=1, source_target_pairs={{0,4},{1,5},{2,6},{3,7},{4,0},{5,1},{6,2},{7,3},{8,12},{9,13},{10,... | collective-permute-start | bytes 20 | tf_op jit(solution)/shard_map/ppermute | solution.py:36
  72.4 2.6 %collective-permute-start.11 = (f32[1,7,32,128]{3,2,1,0:T(8,128)S(1)}, f32[1,7,32,128]{3,2,1,0:T(8,128)S(1)}, u32[]{:S(2)}, u32[]{:S(2)}) collective-permute-start(f32[1,7,32,128]{3,2,1,0:T(8,128)S(1)} %get-tuple-element.62), channel_id=1, source_target_pairs={{0,1},{1,2},{2,3},{3,4},{4,5},{5,6},{6,7},{7,8},{8,9},{9,10},{10,1... | collective-permute-start | bytes 344072 | tf_op jit(solution)/shard_map/ppermute | solution.py:18
  75.1 1.9 %collective-permute-start.12 = (f32[1,7,32,128]{3,2,1,0:T(8,128)S(1)}, f32[1,7,32,128]{3,2,1,0:T(8,128)S(1)}, u32[]{:S(2)}, u32[]{:S(2)}) collective-permute-start(f32[1,7,32,128]{3,2,1,0:T(8,128)S(1)} %get-tuple-element.63), channel_id=1, source_target_pairs={{1,0},{2,1},{3,2},{4,3},{5,4},{6,5},{7,6},{8,7},{9,8},{10,9},{11,1... | collective-permute-start | bytes 344072 | tf_op jit(solution)/shard_map/ppermute | solution.py:19
  77.0 0.3 fusion.300
  78.0 3.2 %collective-permute-done.12 = f32[1,7,32,128]{3,2,1,0:T(8,128)S(1)} collective-permute-done((f32[1,7,32,128]{3,2,1,0:T(8,128)S(1)}, f32[1,7,32,128]{3,2,1,0:T(8,128)S(1)}, u32[]{:S(2)}, u32[]{:S(2)}) %collective-permute-start.12) | collective-permute-done | bytes 114720 | tf_op jit(solution)/shard_map/ppermute | solution.py:19
  81.5 0.3 fusion.497
  81.8 2.8 %collective-permute-start.16 = (f32[1]{0:T(128)}, f32[1]{0:T(128)}, u32[]{:S(2)}, u32[]{:S(2)}) collective-permute-start(f32[1]{0:T(128)} %add.845), channel_id=1, source_target_pairs={{0,8},{1,9},{2,10},{3,11},{4,12},{5,13},{6,14},{7,15},{8,0},{9,1},... | collective-permute-start | bytes 20 | tf_op jit(solution)/shard_map/ppermute | solution.py:36
  84.6 2.6 %collective-permute-start.14 = (f32[1,7,32,128]{3,2,1,0:T(8,128)S(1)}, f32[1,7,32,128]{3,2,1,0:T(8,128)S(1)}, u32[]{:S(2)}, u32[]{:S(2)}) collective-permute-start(f32[1,7,32,128]{3,2,1,0:T(8,128)S(1)} %get-tuple-element.60), channel_id=1, source_target_pairs={{0,1},{1,2},{2,3},{3,4},{4,5},{5,6},{6,7},{7,8},{8,9},{9,10},{10,1... | collective-permute-start | bytes 344072 | tf_op jit(solution)/shard_map/ppermute | solution.py:18
  87.2 1.9 %collective-permute-start.15 = (f32[1,7,32,128]{3,2,1,0:T(8,128)S(1)}, f32[1,7,32,128]{3,2,1,0:T(8,128)S(1)}, u32[]{:S(2)}, u32[]{:S(2)}) collective-permute-start(f32[1,7,32,128]{3,2,1,0:T(8,128)S(1)} %get-tuple-element.61), channel_id=1, source_target_pairs={{1,0},{2,1},{3,2},{4,3},{5,4},{6,5},{7,6},{8,7},{9,8},{10,9},{11,1... | collective-permute-start | bytes 344072 | tf_op jit(solution)/shard_map/ppermute | solution.py:19
  89.2 0.3 fusion.324
  90.2 3.2 %collective-permute-done.15 = f32[1,7,32,128]{3,2,1,0:T(8,128)S(1)} collective-permute-done((f32[1,7,32,128]{3,2,1,0:T(8,128)S(1)}, f32[1,7,32,128]{3,2,1,0:T(8,128)S(1)}, u32[]{:S(2)}, u32[]{:S(2)}) %collective-permute-start.15) | collective-permute-done | bytes 114720 | tf_op jit(solution)/shard_map/ppermute | solution.py:19
  93.5 0.8 copy-done.4
  94.3 0.9 bitcast_multiply_fusion
  95.2 0.8 collective-permute-start.17
  96.0 0.3 collective-permute-done.17
  (55 shorter events, 1.2 us)
Async XLA Ops:
  1.7 8.3 %copy-start.9 = (f32[1,4]{1,0:T(1,128)S(1)}, f32[1,4]{1,0:T(1,128)}, u32[]{:S(2)}) copy-start(f32[1,4]{1,0:T(1,128)} %param.17) | copy-start | bytes 52
  1.7 8.9 %copy-start.7 = (s32[1,2048]{1,0:T(1,128)S(1)}, s32[1,2048]{1,0:T(1,128)}, u32[]{:S(2)}) copy-start(s32[1,2048]{1,0:T(1,128)} %param.18) | copy-start | bytes 24580
  1.7 9.0 %copy-start = (f32[8,32,128]{2,1,0:T(8,128)S(1)}, f32[8,32,128]{2,1,0:T(8,128)}, u32[]{:S(2)}) copy-start(f32[8,32,128]{2,1,0:T(8,128)} %param.11) | copy-start | bytes 393220
  1.7 9.0 %copy-start.1 = (f32[1,8,32,128]{3,2,1,0:T(8,128)S(1)}, f32[1,8,32,128]{3,2,1,0:T(8,128)}, u32[]{:S(2)}) copy-start(f32[1,8,32,128]{3,2,1,0:T(8,128)} %param.13) | copy-start | bytes 393220
  2.9 9.5 %collective-permute-start.1 = (f32[3,7,32,128]{3,2,1,0:T(8,128)S(1)}, f32[3,7,32,128]{3,2,1,0:T(8,128)S(1)}, u32[]{:S(2)}, u32[]{:S(2)}) collective-permute-start(f32[3,7,32,128]{3,2,1,0:T(8,128)S(1)} %get-tuple-element.42), channel_id=1, source_target_pairs={{1,0},{2,1},{3,2},{4,3},{5,4},{6,5},{7,6},{8,7},{9,8},{10,9},{11,1... | collective-permute-start | bytes 1032200 | tf_op jit(solution)/shard_map/ppermute | solution.py:19
  4.8 11.3 %collective-permute-start = (f32[3,7,32,128]{3,2,1,0:T(8,128)S(1)}, f32[3,7,32,128]{3,2,1,0:T(8,128)S(1)}, u32[]{:S(2)}, u32[]{:S(2)}) collective-permute-start(f32[3,7,32,128]{3,2,1,0:T(8,128)S(1)} %get-tuple-element.43), channel_id=1, source_target_pairs={{0,1},{1,2},{2,3},{3,4},{4,5},{5,6},{6,7},{7,8},{8,9},{9,10},{10,1... | collective-permute-start | bytes 1032200 | tf_op jit(solution)/shard_map/ppermute | solution.py:18
  16.3 0.9 copy-start.6
  18.5 8.4 %collective-permute-start.2 = (f32[1,7,32,128]{3,2,1,0:T(8,128)S(1)}, f32[1,7,32,128]{3,2,1,0:T(8,128)S(1)}, u32[]{:S(2)}, u32[]{:S(2)}) collective-permute-start(f32[1,7,32,128]{3,2,1,0:T(8,128)S(1)} %get-tuple-element.72), channel_id=1, source_target_pairs={{0,1},{1,2},{2,3},{3,4},{4,5},{5,6},{6,7},{7,8},{8,9},{9,10},{10,1... | collective-permute-start | bytes 344072 | tf_op jit(solution)/shard_map/ppermute | solution.py:18
  22.9 6.1 %collective-permute-start.3 = (f32[1,7,32,128]{3,2,1,0:T(8,128)S(1)}, f32[1,7,32,128]{3,2,1,0:T(8,128)S(1)}, u32[]{:S(2)}, u32[]{:S(2)}) collective-permute-start(f32[1,7,32,128]{3,2,1,0:T(8,128)S(1)} %get-tuple-element.73), channel_id=1, source_target_pairs={{1,0},{2,1},{3,2},{4,3},{5,4},{6,5},{7,6},{8,7},{9,8},{10,9},{11,1... | collective-permute-start | bytes 344072 | tf_op jit(solution)/shard_map/ppermute | solution.py:19
  30.2 6.3 %collective-permute-start.4 = (f32[1,7,32,128]{3,2,1,0:T(8,128)S(1)}, f32[1,7,32,128]{3,2,1,0:T(8,128)S(1)}, u32[]{:S(2)}, u32[]{:S(2)}) collective-permute-start(f32[1,7,32,128]{3,2,1,0:T(8,128)S(1)} %get-tuple-element.70), channel_id=1, source_target_pairs={{0,1},{1,2},{2,3},{3,4},{4,5},{5,6},{6,7},{7,8},{8,9},{9,10},{10,1... | collective-permute-start | bytes 344072 | tf_op jit(solution)/shard_map/ppermute | solution.py:18
  32.2 6.1 %collective-permute-start.5 = (f32[1,7,32,128]{3,2,1,0:T(8,128)S(1)}, f32[1,7,32,128]{3,2,1,0:T(8,128)S(1)}, u32[]{:S(2)}, u32[]{:S(2)}) collective-permute-start(f32[1,7,32,128]{3,2,1,0:T(8,128)S(1)} %get-tuple-element.71), channel_id=1, source_target_pairs={{1,0},{2,1},{3,2},{4,3},{5,4},{6,5},{7,6},{8,7},{9,8},{10,9},{11,1... | collective-permute-start | bytes 344072 | tf_op jit(solution)/shard_map/ppermute | solution.py:19
  39.5 6.5 %collective-permute-start.6 = (f32[1,7,32,128]{3,2,1,0:T(8,128)S(1)}, f32[1,7,32,128]{3,2,1,0:T(8,128)S(1)}, u32[]{:S(2)}, u32[]{:S(2)}) collective-permute-start(f32[1,7,32,128]{3,2,1,0:T(8,128)S(1)} %get-tuple-element.68), channel_id=1, source_target_pairs={{0,1},{1,2},{2,3},{3,4},{4,5},{5,6},{6,7},{7,8},{8,9},{9,10},{10,1... | collective-permute-start | bytes 344072 | tf_op jit(solution)/shard_map/ppermute | solution.py:18
  41.4 7.0 %collective-permute-start.7 = (f32[1,7,32,128]{3,2,1,0:T(8,128)S(1)}, f32[1,7,32,128]{3,2,1,0:T(8,128)S(1)}, u32[]{:S(2)}, u32[]{:S(2)}) collective-permute-start(f32[1,7,32,128]{3,2,1,0:T(8,128)S(1)} %get-tuple-element.69), channel_id=1, source_target_pairs={{1,0},{2,1},{3,2},{4,3},{5,4},{6,5},{7,6},{8,7},{9,8},{10,9},{11,1... | collective-permute-start | bytes 344072 | tf_op jit(solution)/shard_map/ppermute | solution.py:19
  49.3 1.7 %copy-start.8 = (f32[1,4,2048]{2,1,0:T(4,128)S(1)}, f32[1,4,2048]{2,1,0:T(4,128)}, u32[]{:S(2)}) copy-start(f32[1,4,2048]{2,1,0:T(4,128)} %param.19) | copy-start | bytes 98308
  50.9 4.6 %copy-start.2 = (f32[1,8,32,128]{3,2,1,0:T(8,128)S(1)}, f32[1,8,32,128]{3,2,1,0:T(8,128)}, u32[]{:S(2)}) copy-start(f32[1,8,32,128]{3,2,1,0:T(8,128)} %param.14) | copy-start | bytes 393220
  50.9 4.5 %copy-start.5 = (f32[1,8,32,128]{3,2,1,0:T(8,128)S(1)}, f32[1,8,32,128]{3,2,1,0:T(8,128)}, u32[]{:S(2)}) copy-start(f32[1,8,32,128]{3,2,1,0:T(8,128)} %param.15) | copy-start | bytes 393220
  58.7 8.9 %collective-permute-start.10 = (f32[1]{0:T(128)}, f32[1]{0:T(128)}, u32[]{:S(2)}, u32[]{:S(2)}) collective-permute-start(f32[1]{0:T(128)} %bitcast.26), channel_id=1, source_target_pairs={{0,2},{1,3},{2,0},{3,1},{4,6},{5,7},{6,4},{7,5},{8,10},{9,11},{10,... | collective-permute-start | bytes 20 | tf_op jit(solution)/shard_map/ppermute | solution.py:36
  61.7 6.6 %collective-permute-start.8 = (f32[1,7,32,128]{3,2,1,0:T(8,128)S(1)}, f32[1,7,32,128]{3,2,1,0:T(8,128)S(1)}, u32[]{:S(2)}, u32[]{:S(2)}) collective-permute-start(f32[1,7,32,128]{3,2,1,0:T(8,128)S(1)} %get-tuple-element.64), channel_id=1, source_target_pairs={{0,1},{1,2},{2,3},{3,4},{4,5},{5,6},{6,7},{7,8},{8,9},{9,10},{10,1... | collective-permute-start | bytes 344072 | tf_op jit(solution)/shard_map/ppermute | solution.py:18
  63.6 6.1 %collective-permute-start.9 = (f32[1,7,32,128]{3,2,1,0:T(8,128)S(1)}, f32[1,7,32,128]{3,2,1,0:T(8,128)S(1)}, u32[]{:S(2)}, u32[]{:S(2)}) collective-permute-start(f32[1,7,32,128]{3,2,1,0:T(8,128)S(1)} %get-tuple-element.65), channel_id=1, source_target_pairs={{1,0},{2,1},{3,2},{4,3},{5,4},{6,5},{7,6},{8,7},{9,8},{10,9},{11,1... | collective-permute-start | bytes 344072 | tf_op jit(solution)/shard_map/ppermute | solution.py:19
  70.3 7.0 %collective-permute-start.13 = (f32[1]{0:T(128)}, f32[1]{0:T(128)}, u32[]{:S(2)}, u32[]{:S(2)}) collective-permute-start(f32[1]{0:T(128)} %add.821), channel_id=1, source_target_pairs={{0,4},{1,5},{2,6},{3,7},{4,0},{5,1},{6,2},{7,3},{8,12},{9,13},{10,... | collective-permute-start | bytes 20 | tf_op jit(solution)/shard_map/ppermute | solution.py:36
  72.4 5.6 %collective-permute-start.11 = (f32[1,7,32,128]{3,2,1,0:T(8,128)S(1)}, f32[1,7,32,128]{3,2,1,0:T(8,128)S(1)}, u32[]{:S(2)}, u32[]{:S(2)}) collective-permute-start(f32[1,7,32,128]{3,2,1,0:T(8,128)S(1)} %get-tuple-element.62), channel_id=1, source_target_pairs={{0,1},{1,2},{2,3},{3,4},{4,5},{5,6},{6,7},{7,8},{8,9},{9,10},{10,1... | collective-permute-start | bytes 344072 | tf_op jit(solution)/shard_map/ppermute | solution.py:18
  75.1 6.1 %collective-permute-start.12 = (f32[1,7,32,128]{3,2,1,0:T(8,128)S(1)}, f32[1,7,32,128]{3,2,1,0:T(8,128)S(1)}, u32[]{:S(2)}, u32[]{:S(2)}) collective-permute-start(f32[1,7,32,128]{3,2,1,0:T(8,128)S(1)} %get-tuple-element.63), channel_id=1, source_target_pairs={{1,0},{2,1},{3,2},{4,3},{5,4},{6,5},{7,6},{8,7},{9,8},{10,9},{11,1... | collective-permute-start | bytes 344072 | tf_op jit(solution)/shard_map/ppermute | solution.py:19
  81.4 12.1 %copy-start.3 = (f32[1,8,32,128]{3,2,1,0:T(8,128)}, f32[1,8,32,128]{3,2,1,0:T(8,128)S(1)}, u32[]{:S(2)}) copy-start(f32[1,8,32,128]{3,2,1,0:T(8,128)S(1)} %fusion.531) | copy-start | bytes 393220
  81.8 7.7 %collective-permute-start.16 = (f32[1]{0:T(128)}, f32[1]{0:T(128)}, u32[]{:S(2)}, u32[]{:S(2)}) collective-permute-start(f32[1]{0:T(128)} %add.845), channel_id=1, source_target_pairs={{0,8},{1,9},{2,10},{3,11},{4,12},{5,13},{6,14},{7,15},{8,0},{9,1},... | collective-permute-start | bytes 20 | tf_op jit(solution)/shard_map/ppermute | solution.py:36
  84.6 5.6 %collective-permute-start.14 = (f32[1,7,32,128]{3,2,1,0:T(8,128)S(1)}, f32[1,7,32,128]{3,2,1,0:T(8,128)S(1)}, u32[]{:S(2)}, u32[]{:S(2)}) collective-permute-start(f32[1,7,32,128]{3,2,1,0:T(8,128)S(1)} %get-tuple-element.60), channel_id=1, source_target_pairs={{0,1},{1,2},{2,3},{3,4},{4,5},{5,6},{6,7},{7,8},{8,9},{9,10},{10,1... | collective-permute-start | bytes 344072 | tf_op jit(solution)/shard_map/ppermute | solution.py:18
  87.2 6.1 %collective-permute-start.15 = (f32[1,7,32,128]{3,2,1,0:T(8,128)S(1)}, f32[1,7,32,128]{3,2,1,0:T(8,128)S(1)}, u32[]{:S(2)}, u32[]{:S(2)}) collective-permute-start(f32[1,7,32,128]{3,2,1,0:T(8,128)S(1)} %get-tuple-element.61), channel_id=1, source_target_pairs={{1,0},{2,1},{3,2},{4,3},{5,4},{6,5},{7,6},{8,7},{9,8},{10,9},{11,1... | collective-permute-start | bytes 344072 | tf_op jit(solution)/shard_map/ppermute | solution.py:19
  93.4 0.9 copy-start.4
  95.2 1.1 %collective-permute-start.17 = (f32[1]{0:T(128)}, f32[1]{0:T(128)}, u32[]{:S(2)}, u32[]{:S(2)}) collective-permute-start(f32[1]{0:T(128)} %add.869), channel_id=1, source_target_pairs={{0,1},{1,0},{2,3},{3,2},{4,5},{5,4},{6,7},{7,6},{8,9},{9,8},{10,11... | collective-permute-start | bytes 20 | tf_op jit(solution)/shard_map/ppermute | solution.py:36

commit v9 on v8

--- a/solution.py
+++ b/solution.py
@@ -131,11 +131,15 @@
     def injected(amounts):
         spread = jnp.where(col_pick, amounts[:, :, None], 0.0)
         added = jnp.einsum("srk,srz->skz", row_pick, spread, precision=lax.Precision.HIGHEST)
-        return lax.optimization_barrier(added.reshape(shape))
+        return added.reshape(shape)
+
+    receiver_count = injected(jnp.ones_like(observed[:, 0, :]))
+    recorded_sum = [injected(observed[:, step, :]) for step in range(STEPS)]
 
     before, current = (wave_prev, wave_now)
     laps = []
     resids = []
+    fields = []
     for step in range(STEPS):
         lap = first_lap if step == 0 else operator(current)
         laps.append(lap)
@@ -144,6 +148,7 @@
         following = following + jnp.where(source_hit, amount, 0.0)
         sampled = sample(following)
         resids.append(jnp.where(receiver_owned, sampled - observed[:, step, :], 0.0))
+        fields.append(following)
         before, current = (current, following)
     misfit = 0.5 * sum((jnp.sum(item * item, axis=1) for item in resids))
     distances = butterfly_distances("mp")
@@ -158,7 +163,7 @@
                 misfit = butterfly_round(misfit, "mp", distances.pop(0))
             lap = operator(kappa * mu_near)
         state = 2.0 * mu_near + lap - mu_far
-        state = state + injected(resids[level - 1])
+        state = state + (receiver_count * fields[level - 1] - recorded_sum[level - 1])
         gradient = gradient + state * laps[level - 1]
         mu_far, mu_near = (mu_near, state)
         mu_near, misfit = lax.optimization_barrier((mu_near, misfit))

time: 99.5 us -> 101 us (1.015)
  matrix products: 11.4 us -> 12.7 us
    mul x7, other arithmetic: 2.4 us -> 5.41 us  [cross_terms(): flux = buoyancy * forward_diff(pad_axis(values, axis), axis, length)]
    dot_general x4 -> x5, matrix products: 4.93 us -> 6.25 us  [injected(): jnp.einsum('srk,srz->skz', row_pick, spread, precision=lax.Precision.HIGH...]
    mul x1 -> x0, other arithmetic: 1.06 us -> none  [local(): adjoint_operand = kappa * adjoint_next]
  transfers between devices with their start and end apart: 18 -> 18, of which waited for: 9 -> 8; matrix products, arithmetic and copies ran while one was open for 9% -> 10% of each run, Pallas kernels for 0% -> 0%
where the time goes in v9:
time: 101 us; the launch traced here: 99.4 us
  starting transfers between devices  43.9 us (43%)
  waiting for transfers between devices  19.5 us (19%)
  other arithmetic  13.3 us (13%)
  matrix products  12.7 us (13%)
  between operations  8.4 us (8%)
  local copies, waits for them, and re-layouts  1.7 us (2%)
    ppermute x7, starting transfers between devices, extended(): before = lax.ppermute(last, 'mp', up)  19.9 us
    ppermute x7, waiting for transfers between devices, extended(): after = lax.ppermute(first, 'mp', down)  15.6 us
    ppermute x7, starting transfers between devices, extended(): after = lax.ppermute(first, 'mp', down)  15.1 us
    ppermute x4, starting transfers between devices, butterfly_round(): return values + lax.ppermute(values, axis, pairs)  8.83 us
    dot_general x4, matrix products, sample(): jnp.einsum('srk,skz->srz', row_pick, field.reshape(shots, rows, cz), prec...  6.43 us
    dot_general x5, matrix products, injected(): jnp.einsum('srk,srz->skz', row_pick, spread, precision=lax.Precision.HIGH...  6.25 us
    mul x7, other arithmetic, cross_terms(): flux = buoyancy * forward_diff(pad_axis(values, axis), axis, length)  5.41 us
    ppermute x7, waiting for transfers between devices, extended(): before = lax.ppermute(last, 'mp', up)  3.87 us
  transfers between devices with their start and end apart: 18, of which 8 were waited for; matrix products, arithmetic and copies ran while one was open for 10% of the time, Pallas kernels for 0%

profile of v9, /device:TPU:1, one launch (start us, length us, event | category | flops | bytes accessed | tf_op | source)
XLA Modules:
  0.0 99.4 jit_solution(12088502927427411132)
XLA Ops:
  0.7 3.3 %fusion.202 = (f32[1,8,32,128]{3,2,1,0:T(8,128)S(1)}, f32[1,8,32,128]{3,2,1,0:T(8,128)S(1)}, f32[1,8,32,128]{3,2,1,0:T(8,128)S(1)}, f32[8,32,128]{2,1,0:T(8,128)S(1)}) fusion(f32[1,8,32,128]{3,2,1,0:T(8,128)} %param.13, f32[8,32,128]{2,1,0:T(8,128)} %param.11, f32[1,8,32,128]{3,2,1,0:T(8,128)} %param.14, f32[8,32,128]{2,1,0:T(8,128)} %param.10), kind=kLoop, calls=%fused_computation.439 | loop fusion | flops 884736 | bytes 1048576 | tf_op jit(solution)/shard_map/mul | solution.py:69
  4.1 2.0 %collective-permute-start.1 = (f32[3,7,32,128]{3,2,1,0:T(8,128)S(1)}, f32[3,7,32,128]{3,2,1,0:T(8,128)S(1)}, u32[]{:S(2)}, u32[]{:S(2)}) collective-permute-start(f32[3,7,32,128]{3,2,1,0:T(8,128)S(1)} %get-tuple-element.36), channel_id=1, source_target_pairs={{1,0},{2,1},{3,2},{4,3},{5,4},{6,5},{7,6},{8,7},{9,8},{10,9},{11,1... | collective-permute-start | bytes 1032200 | tf_op jit(solution)/shard_map/ppermute | solution.py:19
  6.1 4.5 %collective-permute-start = (f32[3,7,32,128]{3,2,1,0:T(8,128)S(1)}, f32[3,7,32,128]{3,2,1,0:T(8,128)S(1)}, u32[]{:S(2)}, u32[]{:S(2)}) collective-permute-start(f32[3,7,32,128]{3,2,1,0:T(8,128)S(1)} %get-tuple-element.37), channel_id=1, source_target_pairs={{0,1},{1,2},{2,3},{3,4},{4,5},{5,6},{6,7},{7,8},{8,9},{9,10},{10,1... | collective-permute-start | bytes 1032200 | tf_op jit(solution)/shard_map/ppermute | solution.py:18
  11.3 0.7 fusion.657
  12.1 1.3 %fusion.27 = f32[1,8,32,128]{3,2,1,0:T(8,128)S(1)} fusion(s32[8,32]{1,0:T(8,128)S(1)} %multiply_add_fusion, s32[2048]{0:T(1024)S(1)} %bitcast.173, s32[2048]{0:T(1024)S(1)} %bitcast.164), kind=kOutput, calls=%fused_computation.20 | convolution fusion | flops 806354944 | bytes 148480 | tf_op jit(solution)/shard_map/srk,srz->skz/dot_general | solution.py:133
  13.4 0.2 collective-permute-done.1
  13.6 3.9 %collective-permute-done = f32[3,7,32,128]{3,2,1,0:T(8,128)S(1)} collective-permute-done((f32[3,7,32,128]{3,2,1,0:T(8,128)S(1)}, f32[3,7,32,128]{3,2,1,0:T(8,128)S(1)}, u32[]{:S(2)}, u32[]{:S(2)}) %collective-permute-start) | collective-permute-done | bytes 344096 | tf_op jit(solution)/shard_map/ppermute | solution.py:18
  17.5 0.1 fusion.150
  17.7 0.8 copy-done.4
  18.4 1.0 fusion.619
  19.4 0.3 fusion.417
  19.8 4.4 %collective-permute-start.2 = (f32[1,7,32,128]{3,2,1,0:T(8,128)S(1)}, f32[1,7,32,128]{3,2,1,0:T(8,128)S(1)}, u32[]{:S(2)}, u32[]{:S(2)}) collective-permute-start(f32[1,7,32,128]{3,2,1,0:T(8,128)S(1)} %get-tuple-element.66), channel_id=1, source_target_pairs={{0,1},{1,2},{2,3},{3,4},{4,5},{5,6},{6,7},{7,8},{8,9},{9,10},{10,1... | collective-permute-start | bytes 344072 | tf_op jit(solution)/shard_map/ppermute | solution.py:18
  24.2 1.9 %collective-permute-start.3 = (f32[1,7,32,128]{3,2,1,0:T(8,128)S(1)}, f32[1,7,32,128]{3,2,1,0:T(8,128)S(1)}, u32[]{:S(2)}, u32[]{:S(2)}) collective-permute-start(f32[1,7,32,128]{3,2,1,0:T(8,128)S(1)} %get-tuple-element.67), channel_id=1, source_target_pairs={{1,0},{2,1},{3,2},{4,3},{5,4},{6,5},{7,6},{8,7},{9,8},{10,9},{11,1... | collective-permute-start | bytes 344072 | tf_op jit(solution)/shard_map/ppermute | solution.py:19
  26.1 0.3 fusion.239
  26.4 0.1 fusion.158
  26.5 1.6 %fusion.15 = f32[2048]{0:T(1024)S(1)} fusion(f32[256,128]{1,0:T(8,128)S(1)} %bitcast.160, s32[2048]{0:T(1024)S(1)} %bitcast.174, s32[2048]{0:T(1024)S(1)} %bitcast.165), kind=kOutput, calls=%fused_computation.16 | convolution fusion | flops 806615040 | bytes 155648 | tf_op jit(solution)/shard_map/srk,skz->srz/dot_general | solution.py:126
  28.1 2.1 %collective-permute-done.3 = f32[1,7,32,128]{3,2,1,0:T(8,128)S(1)} collective-permute-done((f32[1,7,32,128]{3,2,1,0:T(8,128)S(1)}, f32[1,7,32,128]{3,2,1,0:T(8,128)S(1)}, u32[]{:S(2)}, u32[]{:S(2)}) %collective-permute-start.3) | collective-permute-done | bytes 114720 | tf_op jit(solution)/shard_map/ppermute | solution.py:19
  30.3 0.1 fusion.143
  30.4 0.8 fusion.621
  31.2 0.3 fusion.440
  31.5 1.9 %collective-permute-start.4 = (f32[1,7,32,128]{3,2,1,0:T(8,128)S(1)}, f32[1,7,32,128]{3,2,1,0:T(8,128)S(1)}, u32[]{:S(2)}, u32[]{:S(2)}) collective-permute-start(f32[1,7,32,128]{3,2,1,0:T(8,128)S(1)} %get-tuple-element.64), channel_id=1, source_target_pairs={{0,1},{1,2},{2,3},{3,4},{4,5},{5,6},{6,7},{7,8},{8,9},{9,10},{10,1... | collective-permute-start | bytes 344072 | tf_op jit(solution)/shard_map/ppermute | solution.py:18
  33.4 2.4 %collective-permute-start.5 = (f32[1,7,32,128]{3,2,1,0:T(8,128)S(1)}, f32[1,7,32,128]{3,2,1,0:T(8,128)S(1)}, u32[]{:S(2)}, u32[]{:S(2)}) collective-permute-start(f32[1,7,32,128]{3,2,1,0:T(8,128)S(1)} %get-tuple-element.65), channel_id=1, source_target_pairs={{1,0},{2,1},{3,2},{4,3},{5,4},{6,5},{7,6},{8,7},{9,8},{10,9},{11,1... | collective-permute-start | bytes 344072 | tf_op jit(solution)/shard_map/ppermute | solution.py:19
  35.8 0.3 fusion.263
  36.2 1.6 %fusion.18 = f32[2048]{0:T(1024)S(1)} fusion(f32[256,128]{1,0:T(8,128)S(1)} %bitcast.161, s32[2048]{0:T(1024)S(1)} %bitcast.175, s32[2048]{0:T(1024)S(1)} %bitcast.166), kind=kOutput, calls=%fused_computation.17 | convolution fusion | flops 806615040 | bytes 155648 | tf_op jit(solution)/shard_map/srk,skz->srz/dot_general | solution.py:126
  37.8 1.8 %collective-permute-done.5 = f32[1,7,32,128]{3,2,1,0:T(8,128)S(1)} collective-permute-done((f32[1,7,32,128]{3,2,1,0:T(8,128)S(1)}, f32[1,7,32,128]{3,2,1,0:T(8,128)S(1)}, u32[]{:S(2)}, u32[]{:S(2)}) %collective-permute-start.5) | collective-permute-done | bytes 114720 | tf_op jit(solution)/shard_map/ppermute | solution.py:19
  39.6 0.1 fusion.136
  39.7 0.8 fusion.623
  40.5 0.5 fusion.463
  41.0 1.9 %collective-permute-start.6 = (f32[1,7,32,128]{3,2,1,0:T(8,128)S(1)}, f32[1,7,32,128]{3,2,1,0:T(8,128)S(1)}, u32[]{:S(2)}, u32[]{:S(2)}) collective-permute-start(f32[1,7,32,128]{3,2,1,0:T(8,128)S(1)} %get-tuple-element.60), channel_id=1, source_target_pairs={{0,1},{1,2},{2,3},{3,4},{4,5},{5,6},{6,7},{7,8},{8,9},{9,10},{10,1... | collective-permute-start | bytes 344072 | tf_op jit(solution)/shard_map/ppermute | solution.py:18
  43.0 2.4 %collective-permute-start.7 = (f32[1,7,32,128]{3,2,1,0:T(8,128)S(1)}, f32[1,7,32,128]{3,2,1,0:T(8,128)S(1)}, u32[]{:S(2)}, u32[]{:S(2)}) collective-permute-start(f32[1,7,32,128]{3,2,1,0:T(8,128)S(1)} %get-tuple-element.61), channel_id=1, source_target_pairs={{1,0},{2,1},{3,2},{4,3},{5,4},{6,5},{7,6},{8,7},{9,8},{10,9},{11,1... | collective-permute-start | bytes 344072 | tf_op jit(solution)/shard_map/ppermute | solution.py:19
  45.4 0.3 fusion.287
  45.7 1.6 %fusion.21 = f32[2048]{0:T(1024)S(1)} fusion(f32[256,128]{1,0:T(8,128)S(1)} %bitcast.162, s32[2048]{0:T(1024)S(1)} %bitcast.176, s32[2048]{0:T(1024)S(1)} %bitcast.167), kind=kOutput, calls=%fused_computation.18 | convolution fusion | flops 806615040 | bytes 155648 | tf_op jit(solution)/shard_map/srk,skz->srz/dot_general | solution.py:126
  47.3 2.6 %collective-permute-done.7 = f32[1,7,32,128]{3,2,1,0:T(8,128)S(1)} collective-permute-done((f32[1,7,32,128]{3,2,1,0:T(8,128)S(1)}, f32[1,7,32,128]{3,2,1,0:T(8,128)S(1)}, u32[]{:S(2)}, u32[]{:S(2)}) %collective-permute-start.7) | collective-permute-done | bytes 114720 | tf_op jit(solution)/shard_map/ppermute | solution.py:19
  50.0 0.1 fusion.129
  50.1 0.7 fusion.625
  50.8 1.6 %fusion.24 = f32[2048]{0:T(1024)S(1)} fusion(f32[256,128]{1,0:T(8,128)S(1)} %bitcast.163, s32[2048]{0:T(1024)S(1)} %bitcast.177, s32[2048]{0:T(1024)S(1)} %bitcast.168), kind=kOutput, calls=%fused_computation.19 | convolution fusion | flops 806615040 | bytes 155648 | tf_op jit(solution)/shard_map/srk,skz->srz/dot_general | solution.py:126
  52.5 0.7 fusion.638
  55.8 1.3 %fusion.63 = f32[1,8,32,128]{3,2,1,0:T(8,128)S(1)} fusion(s32[8,32]{1,0:T(8,128)S(1)} %multiply_add_fusion, s32[2048]{0:T(1024)S(1)} %bitcast.178, f32[2048]{0:T(1024)S(1)} %bitcast.189, s32[2048]{0:T(1024)S(1)} %bitcast.169, f32[1,8,32,128]{3,2,1,0:T(8,128)S(1)} %copy-done.10, f32[1,8,32,128]{3,2,1,0:T(8,128)S(1)} %get-tuple-element.62, ...), kind=kOutput, calls=%fused_computation.32 | convolution fusion | flops 807698432 | bytes 1991680 | tf_op jit(solution)/shard_map/srk,srz->skz/dot_general | solution.py:133
  57.2 0.3 fusion.486
  57.5 3.0 %collective-permute-start.10 = (f32[1]{0:T(128)}, f32[1]{0:T(128)}, u32[]{:S(2)}, u32[]{:S(2)}) collective-permute-start(f32[1]{0:T(128)} %bitcast.28), channel_id=1, source_target_pairs={{0,2},{1,3},{2,0},{3,1},{4,6},{5,7},{6,4},{7,5},{8,10},{9,11},{10,... | collective-permute-start | bytes 20 | tf_op jit(solution)/shard_map/ppermute | solution.py:36
  60.5 1.9 %collective-permute-start.8 = (f32[1,7,32,128]{3,2,1,0:T(8,128)S(1)}, f32[1,7,32,128]{3,2,1,0:T(8,128)S(1)}, u32[]{:S(2)}, u32[]{:S(2)}) collective-permute-start(f32[1,7,32,128]{3,2,1,0:T(8,128)S(1)} %get-tuple-element.58), channel_id=1, source_target_pairs={{0,1},{1,2},{2,3},{3,4},{4,5},{5,6},{6,7},{7,8},{8,9},{9,10},{10,1... | collective-permute-start | bytes 344072 | tf_op jit(solution)/shard_map/ppermute | solution.py:18
  62.4 2.6 %collective-permute-start.9 = (f32[1,7,32,128]{3,2,1,0:T(8,128)S(1)}, f32[1,7,32,128]{3,2,1,0:T(8,128)S(1)}, u32[]{:S(2)}, u32[]{:S(2)}) collective-permute-start(f32[1,7,32,128]{3,2,1,0:T(8,128)S(1)} %get-tuple-element.59), channel_id=1, source_target_pairs={{1,0},{2,1},{3,2},{4,3},{5,4},{6,5},{7,6},{8,7},{9,8},{10,9},{11,1... | collective-permute-start | bytes 344072 | tf_op jit(solution)/shard_map/ppermute | solution.py:19
  65.0 0.3 fusion.311
  66.0 2.5 %collective-permute-done.9 = f32[1,7,32,128]{3,2,1,0:T(8,128)S(1)} collective-permute-done((f32[1,7,32,128]{3,2,1,0:T(8,128)S(1)}, f32[1,7,32,128]{3,2,1,0:T(8,128)S(1)}, u32[]{:S(2)}, u32[]{:S(2)}) %collective-permute-start.9) | collective-permute-done | bytes 114720 | tf_op jit(solution)/shard_map/ppermute | solution.py:19
  68.6 0.1 fusion.122
  68.7 1.2 %fusion.57 = f32[1,8,32,128]{3,2,1,0:T(8,128)S(1)} fusion(s32[8,32]{1,0:T(8,128)S(1)} %multiply_add_fusion, s32[2048]{0:T(1024)S(1)} %bitcast.179, f32[2048]{0:T(1024)S(1)} %bitcast.188, s32[2048]{0:T(1024)S(1)} %bitcast.170, f32[1,8,32,128]{3,2,1,0:T(8,128)S(1)} %copy-done.6, f32[1,8,32,128]{3,2,1,0:T(8,128)S(1)} %fusion.311, ...), kind=kOutput, calls=%fused_computation.30 | convolution fusion | flops 806944768 | bytes 1860608 | tf_op jit(solution)/shard_map/srk,srz->skz/dot_general | solution.py:133
  70.0 0.3 fusion.509
  70.3 2.1 %collective-permute-start.13 = (f32[1]{0:T(128)}, f32[1]{0:T(128)}, u32[]{:S(2)}, u32[]{:S(2)}) collective-permute-start(f32[1]{0:T(128)} %add.821), channel_id=1, source_target_pairs={{0,4},{1,5},{2,6},{3,7},{4,0},{5,1},{6,2},{7,3},{8,12},{9,13},{10,... | collective-permute-start | bytes 20 | tf_op jit(solution)/shard_map/ppermute | solution.py:36
  72.4 2.6 %collective-permute-start.11 = (f32[1,7,32,128]{3,2,1,0:T(8,128)S(1)}, f32[1,7,32,128]{3,2,1,0:T(8,128)S(1)}, u32[]{:S(2)}, u32[]{:S(2)}) collective-permute-start(f32[1,7,32,128]{3,2,1,0:T(8,128)S(1)} %get-tuple-element.56), channel_id=1, source_target_pairs={{0,1},{1,2},{2,3},{3,4},{4,5},{5,6},{6,7},{7,8},{8,9},{9,10},{10,1... | collective-permute-start | bytes 344072 | tf_op jit(solution)/shard_map/ppermute | solution.py:18
  75.0 1.9 %collective-permute-start.12 = (f32[1,7,32,128]{3,2,1,0:T(8,128)S(1)}, f32[1,7,32,128]{3,2,1,0:T(8,128)S(1)}, u32[]{:S(2)}, u32[]{:S(2)}) collective-permute-start(f32[1,7,32,128]{3,2,1,0:T(8,128)S(1)} %get-tuple-element.57), channel_id=1, source_target_pairs={{1,0},{2,1},{3,2},{4,3},{5,4},{6,5},{7,6},{8,7},{9,8},{10,9},{11,1... | collective-permute-start | bytes 344072 | tf_op jit(solution)/shard_map/ppermute | solution.py:19
  76.9 0.3 fusion.335
  78.0 3.2 %collective-permute-done.12 = f32[1,7,32,128]{3,2,1,0:T(8,128)S(1)} collective-permute-done((f32[1,7,32,128]{3,2,1,0:T(8,128)S(1)}, f32[1,7,32,128]{3,2,1,0:T(8,128)S(1)}, u32[]{:S(2)}, u32[]{:S(2)}) %collective-permute-start.12) | collective-permute-done | bytes 114720 | tf_op jit(solution)/shard_map/ppermute | solution.py:19
  81.2 0.1 fusion.115
  81.3 1.2 %fusion.51 = f32[1,8,32,128]{3,2,1,0:T(8,128)S(1)} fusion(s32[8,32]{1,0:T(8,128)S(1)} %multiply_add_fusion, s32[2048]{0:T(1024)S(1)} %bitcast.180, f32[2048]{0:T(1024)S(1)} %bitcast.187, s32[2048]{0:T(1024)S(1)} %bitcast.171, f32[1,8,32,128]{3,2,1,0:T(8,128)S(1)} %fusion.63, f32[1,8,32,128]{3,2,1,0:T(8,128)S(1)} %fusion.335, ...), kind=kOutput, calls=%fused_computation.28 | convolution fusion | flops 806944768 | bytes 1860608 | tf_op jit(solution)/shard_map/srk,srz->skz/dot_general | solution.py:133
  82.6 0.3 fusion.532
  82.9 2.8 %collective-permute-start.16 = (f32[1]{0:T(128)}, f32[1]{0:T(128)}, u32[]{:S(2)}, u32[]{:S(2)}) collective-permute-start(f32[1]{0:T(128)} %add.845), channel_id=1, source_target_pairs={{0,8},{1,9},{2,10},{3,11},{4,12},{5,13},{6,14},{7,15},{8,0},{9,1},... | collective-permute-start | bytes 20 | tf_op jit(solution)/shard_map/ppermute | solution.py:36
  85.7 2.6 %collective-permute-start.14 = (f32[1,7,32,128]{3,2,1,0:T(8,128)S(1)}, f32[1,7,32,128]{3,2,1,0:T(8,128)S(1)}, u32[]{:S(2)}, u32[]{:S(2)}) collective-permute-start(f32[1,7,32,128]{3,2,1,0:T(8,128)S(1)} %get-tuple-element.54), channel_id=1, source_target_pairs={{0,1},{1,2},{2,3},{3,4},{4,5},{5,6},{6,7},{7,8},{8,9},{9,10},{10,1... | collective-permute-start | bytes 344072 | tf_op jit(solution)/shard_map/ppermute | solution.py:18
  88.4 1.9 %collective-permute-start.15 = (f32[1,7,32,128]{3,2,1,0:T(8,128)S(1)}, f32[1,7,32,128]{3,2,1,0:T(8,128)S(1)}, u32[]{:S(2)}, u32[]{:S(2)}) collective-permute-start(f32[1,7,32,128]{3,2,1,0:T(8,128)S(1)} %get-tuple-element.55), channel_id=1, source_target_pairs={{1,0},{2,1},{3,2},{4,3},{5,4},{6,5},{7,6},{8,7},{9,8},{10,9},{11,1... | collective-permute-start | bytes 344072 | tf_op jit(solution)/shard_map/ppermute | solution.py:19
  90.3 0.3 fusion.359
  91.3 3.2 %collective-permute-done.15 = f32[1,7,32,128]{3,2,1,0:T(8,128)S(1)} collective-permute-done((f32[1,7,32,128]{3,2,1,0:T(8,128)S(1)}, f32[1,7,32,128]{3,2,1,0:T(8,128)S(1)}, u32[]{:S(2)}, u32[]{:S(2)}) %collective-permute-start.15) | collective-permute-done | bytes 114720 | tf_op jit(solution)/shard_map/ppermute | solution.py:19
  94.5 0.1 fusion.108
  94.6 1.2 %fusion.45 = f32[1,8,32,128]{3,2,1,0:T(8,128)S(1)} fusion(s32[8,32]{1,0:T(8,128)S(1)} %multiply_add_fusion, s32[2048]{0:T(1024)S(1)} %bitcast.181, f32[2048]{0:T(1024)S(1)} %bitcast.186, s32[2048]{0:T(1024)S(1)} %bitcast.172, f32[1,8,32,128]{3,2,1,0:T(8,128)S(1)} %fusion.57, f32[1,8,32,128]{3,2,1,0:T(8,128)S(1)} %fusion.359, ...), kind=kOutput, calls=%fused_computation.26 | convolution fusion | flops 806944768 | bytes 1860608 | tf_op jit(solution)/shard_map/srk,srz->skz/dot_general | solution.py:133
  95.9 0.9 collective-permute-start.17
  96.8 0.8 bitcast_multiply_fusion
  (55 shorter events, 0.7 us)
Async XLA Ops:
  0.6 3.3 %copy-start = (f32[8,32,128]{2,1,0:T(8,128)S(1)}, f32[8,32,128]{2,1,0:T(8,128)}, u32[]{:S(2)}) copy-start(f32[8,32,128]{2,1,0:T(8,128)} %param.11) | copy-start | bytes 393220
  0.6 3.3 %copy-start.1 = (f32[1,8,32,128]{3,2,1,0:T(8,128)S(1)}, f32[1,8,32,128]{3,2,1,0:T(8,128)}, u32[]{:S(2)}) copy-start(f32[1,8,32,128]{3,2,1,0:T(8,128)} %param.13) | copy-start | bytes 393220
  4.0 7.3 %copy-start.9 = (f32[1,4]{1,0:T(1,128)S(1)}, f32[1,4]{1,0:T(1,128)}, u32[]{:S(2)}) copy-start(f32[1,4]{1,0:T(1,128)} %param.17) | copy-start | bytes 52
  4.0 8.0 %copy-start.8 = (s32[1,2048]{1,0:T(1,128)S(1)}, s32[1,2048]{1,0:T(1,128)}, u32[]{:S(2)}) copy-start(s32[1,2048]{1,0:T(1,128)} %param.18) | copy-start | bytes 24580
  4.1 9.2 %copy-start.5 = (f32[1,4,2048]{2,1,0:T(4,128)S(1)}, f32[1,4,2048]{2,1,0:T(4,128)}, u32[]{:S(2)}) copy-start(f32[1,4,2048]{2,1,0:T(4,128)} %param.19) | copy-start | bytes 98308
  4.1 9.5 %collective-permute-start.1 = (f32[3,7,32,128]{3,2,1,0:T(8,128)S(1)}, f32[3,7,32,128]{3,2,1,0:T(8,128)S(1)}, u32[]{:S(2)}, u32[]{:S(2)}) collective-permute-start(f32[3,7,32,128]{3,2,1,0:T(8,128)S(1)} %get-tuple-element.36), channel_id=1, source_target_pairs={{1,0},{2,1},{3,2},{4,3},{5,4},{6,5},{7,6},{8,7},{9,8},{10,9},{11,1... | collective-permute-start | bytes 1032200 | tf_op jit(solution)/shard_map/ppermute | solution.py:19
  6.1 11.3 %collective-permute-start = (f32[3,7,32,128]{3,2,1,0:T(8,128)S(1)}, f32[3,7,32,128]{3,2,1,0:T(8,128)S(1)}, u32[]{:S(2)}, u32[]{:S(2)}) collective-permute-start(f32[3,7,32,128]{3,2,1,0:T(8,128)S(1)} %get-tuple-element.37), channel_id=1, source_target_pairs={{0,1},{1,2},{2,3},{3,4},{4,5},{5,6},{6,7},{7,8},{8,9},{9,10},{10,1... | collective-permute-start | bytes 1032200 | tf_op jit(solution)/shard_map/ppermute | solution.py:18
  17.5 0.9 copy-start.4
  19.8 8.4 %collective-permute-start.2 = (f32[1,7,32,128]{3,2,1,0:T(8,128)S(1)}, f32[1,7,32,128]{3,2,1,0:T(8,128)S(1)}, u32[]{:S(2)}, u32[]{:S(2)}) collective-permute-start(f32[1,7,32,128]{3,2,1,0:T(8,128)S(1)} %get-tuple-element.66), channel_id=1, source_target_pairs={{0,1},{1,2},{2,3},{3,4},{4,5},{5,6},{6,7},{7,8},{8,9},{9,10},{10,1... | collective-permute-start | bytes 344072 | tf_op jit(solution)/shard_map/ppermute | solution.py:18
  24.2 6.1 %collective-permute-start.3 = (f32[1,7,32,128]{3,2,1,0:T(8,128)S(1)}, f32[1,7,32,128]{3,2,1,0:T(8,128)S(1)}, u32[]{:S(2)}, u32[]{:S(2)}) collective-permute-start(f32[1,7,32,128]{3,2,1,0:T(8,128)S(1)} %get-tuple-element.67), channel_id=1, source_target_pairs={{1,0},{2,1},{3,2},{4,3},{5,4},{6,5},{7,6},{8,7},{9,8},{10,9},{11,1... | collective-permute-start | bytes 344072 | tf_op jit(solution)/shard_map/ppermute | solution.py:19
  31.5 6.3 %collective-permute-start.4 = (f32[1,7,32,128]{3,2,1,0:T(8,128)S(1)}, f32[1,7,32,128]{3,2,1,0:T(8,128)S(1)}, u32[]{:S(2)}, u32[]{:S(2)}) collective-permute-start(f32[1,7,32,128]{3,2,1,0:T(8,128)S(1)} %get-tuple-element.64), channel_id=1, source_target_pairs={{0,1},{1,2},{2,3},{3,4},{4,5},{5,6},{6,7},{7,8},{8,9},{9,10},{10,1... | collective-permute-start | bytes 344072 | tf_op jit(solution)/shard_map/ppermute | solution.py:18
  33.4 6.1 %collective-permute-start.5 = (f32[1,7,32,128]{3,2,1,0:T(8,128)S(1)}, f32[1,7,32,128]{3,2,1,0:T(8,128)S(1)}, u32[]{:S(2)}, u32[]{:S(2)}) collective-permute-start(f32[1,7,32,128]{3,2,1,0:T(8,128)S(1)} %get-tuple-element.65), channel_id=1, source_target_pairs={{1,0},{2,1},{3,2},{4,3},{5,4},{6,5},{7,6},{8,7},{9,8},{10,9},{11,1... | collective-permute-start | bytes 344072 | tf_op jit(solution)/shard_map/ppermute | solution.py:19
  41.0 6.3 %collective-permute-start.6 = (f32[1,7,32,128]{3,2,1,0:T(8,128)S(1)}, f32[1,7,32,128]{3,2,1,0:T(8,128)S(1)}, u32[]{:S(2)}, u32[]{:S(2)}) collective-permute-start(f32[1,7,32,128]{3,2,1,0:T(8,128)S(1)} %get-tuple-element.60), channel_id=1, source_target_pairs={{0,1},{1,2},{2,3},{3,4},{4,5},{5,6},{6,7},{7,8},{8,9},{9,10},{10,1... | collective-permute-start | bytes 344072 | tf_op jit(solution)/shard_map/ppermute | solution.py:18
  43.0 7.0 %collective-permute-start.7 = (f32[1,7,32,128]{3,2,1,0:T(8,128)S(1)}, f32[1,7,32,128]{3,2,1,0:T(8,128)S(1)}, u32[]{:S(2)}, u32[]{:S(2)}) collective-permute-start(f32[1,7,32,128]{3,2,1,0:T(8,128)S(1)} %get-tuple-element.61), channel_id=1, source_target_pairs={{1,0},{2,1},{3,2},{4,3},{5,4},{6,5},{7,6},{8,7},{9,8},{10,9},{11,1... | collective-permute-start | bytes 344072 | tf_op jit(solution)/shard_map/ppermute | solution.py:19
  50.8 5.0 %copy-start.6 = (f32[1,8,32,128]{3,2,1,0:T(8,128)S(1)}, f32[1,8,32,128]{3,2,1,0:T(8,128)}, u32[]{:S(2)}) copy-start(f32[1,8,32,128]{3,2,1,0:T(8,128)} %param.14) | copy-start | bytes 393220
  50.8 5.0 %copy-start.10 = (f32[1,8,32,128]{3,2,1,0:T(8,128)S(1)}, f32[1,8,32,128]{3,2,1,0:T(8,128)}, u32[]{:S(2)}) copy-start(f32[1,8,32,128]{3,2,1,0:T(8,128)} %param.15) | copy-start | bytes 393220
  57.5 7.9 %collective-permute-start.10 = (f32[1]{0:T(128)}, f32[1]{0:T(128)}, u32[]{:S(2)}, u32[]{:S(2)}) collective-permute-start(f32[1]{0:T(128)} %bitcast.28), channel_id=1, source_target_pairs={{0,2},{1,3},{2,0},{3,1},{4,6},{5,7},{6,4},{7,5},{8,10},{9,11},{10,... | collective-permute-start | bytes 20 | tf_op jit(solution)/shard_map/ppermute | solution.py:36
  60.5 5.5 %collective-permute-start.8 = (f32[1,7,32,128]{3,2,1,0:T(8,128)S(1)}, f32[1,7,32,128]{3,2,1,0:T(8,128)S(1)}, u32[]{:S(2)}, u32[]{:S(2)}) collective-permute-start(f32[1,7,32,128]{3,2,1,0:T(8,128)S(1)} %get-tuple-element.58), channel_id=1, source_target_pairs={{0,1},{1,2},{2,3},{3,4},{4,5},{5,6},{6,7},{7,8},{8,9},{9,10},{10,1... | collective-permute-start | bytes 344072 | tf_op jit(solution)/shard_map/ppermute | solution.py:18
  62.4 6.1 %collective-permute-start.9 = (f32[1,7,32,128]{3,2,1,0:T(8,128)S(1)}, f32[1,7,32,128]{3,2,1,0:T(8,128)S(1)}, u32[]{:S(2)}, u32[]{:S(2)}) collective-permute-start(f32[1,7,32,128]{3,2,1,0:T(8,128)S(1)} %get-tuple-element.59), channel_id=1, source_target_pairs={{1,0},{2,1},{3,2},{4,3},{5,4},{6,5},{7,6},{8,7},{9,8},{10,9},{11,1... | collective-permute-start | bytes 344072 | tf_op jit(solution)/shard_map/ppermute | solution.py:19
  70.3 7.0 %collective-permute-start.13 = (f32[1]{0:T(128)}, f32[1]{0:T(128)}, u32[]{:S(2)}, u32[]{:S(2)}) collective-permute-start(f32[1]{0:T(128)} %add.821), channel_id=1, source_target_pairs={{0,4},{1,5},{2,6},{3,7},{4,0},{5,1},{6,2},{7,3},{8,12},{9,13},{10,... | collective-permute-start | bytes 20 | tf_op jit(solution)/shard_map/ppermute | solution.py:36
  72.4 5.6 %collective-permute-start.11 = (f32[1,7,32,128]{3,2,1,0:T(8,128)S(1)}, f32[1,7,32,128]{3,2,1,0:T(8,128)S(1)}, u32[]{:S(2)}, u32[]{:S(2)}) collective-permute-start(f32[1,7,32,128]{3,2,1,0:T(8,128)S(1)} %get-tuple-element.56), channel_id=1, source_target_pairs={{0,1},{1,2},{2,3},{3,4},{4,5},{5,6},{6,7},{7,8},{8,9},{9,10},{10,1... | collective-permute-start | bytes 344072 | tf_op jit(solution)/shard_map/ppermute | solution.py:18
  75.0 6.1 %collective-permute-start.12 = (f32[1,7,32,128]{3,2,1,0:T(8,128)S(1)}, f32[1,7,32,128]{3,2,1,0:T(8,128)S(1)}, u32[]{:S(2)}, u32[]{:S(2)}) collective-permute-start(f32[1,7,32,128]{3,2,1,0:T(8,128)S(1)} %get-tuple-element.57), channel_id=1, source_target_pairs={{1,0},{2,1},{3,2},{4,3},{5,4},{6,5},{7,6},{8,7},{9,8},{10,9},{11,1... | collective-permute-start | bytes 344072 | tf_op jit(solution)/shard_map/ppermute | solution.py:19
  82.5 14.3 %copy-start.2 = (f32[1,8,32,128]{3,2,1,0:T(8,128)}, f32[1,8,32,128]{3,2,1,0:T(8,128)S(1)}, u32[]{:S(2)}) copy-start(f32[1,8,32,128]{3,2,1,0:T(8,128)S(1)} %fusion.51) | copy-start | bytes 393220
  82.9 7.7 %collective-permute-start.16 = (f32[1]{0:T(128)}, f32[1]{0:T(128)}, u32[]{:S(2)}, u32[]{:S(2)}) collective-permute-start(f32[1]{0:T(128)} %add.845), channel_id=1, source_target_pairs={{0,8},{1,9},{2,10},{3,11},{4,12},{5,13},{6,14},{7,15},{8,0},{9,1},... | collective-permute-start | bytes 20 | tf_op jit(solution)/shard_map/ppermute | solution.py:36
  85.7 5.6 %collective-permute-start.14 = (f32[1,7,32,128]{3,2,1,0:T(8,128)S(1)}, f32[1,7,32,128]{3,2,1,0:T(8,128)S(1)}, u32[]{:S(2)}, u32[]{:S(2)}) collective-permute-start(f32[1,7,32,128]{3,2,1,0:T(8,128)S(1)} %get-tuple-element.54), channel_id=1, source_target_pairs={{0,1},{1,2},{2,3},{3,4},{4,5},{5,6},{6,7},{7,8},{8,9},{9,10},{10,1... | collective-permute-start | bytes 344072 | tf_op jit(solution)/shard_map/ppermute | solution.py:18
  88.4 6.1 %collective-permute-start.15 = (f32[1,7,32,128]{3,2,1,0:T(8,128)S(1)}, f32[1,7,32,128]{3,2,1,0:T(8,128)S(1)}, u32[]{:S(2)}, u32[]{:S(2)}) collective-permute-start(f32[1,7,32,128]{3,2,1,0:T(8,128)S(1)} %get-tuple-element.55), channel_id=1, source_target_pairs={{1,0},{2,1},{3,2},{4,3},{5,4},{6,5},{7,6},{8,7},{9,8},{10,9},{11,1... | collective-permute-start | bytes 344072 | tf_op jit(solution)/shard_map/ppermute | solution.py:19
  94.6 2.2 %copy-start.3 = (f32[8,32,128]{2,1,0:T(8,128)S(1)}, f32[8,32,128]{2,1,0:T(8,128)}, u32[]{:S(2)}) copy-start(f32[8,32,128]{2,1,0:T(8,128)} %param.10) | copy-start | bytes 393220
  95.9 2.4 %copy-start.7 = (f32[1,8,32,128]{3,2,1,0:T(8,128)}, f32[1,8,32,128]{3,2,1,0:T(8,128)S(1)}, u32[]{:S(2)}) copy-start(f32[1,8,32,128]{3,2,1,0:T(8,128)S(1)} %fusion.45) | copy-start | bytes 393220
  95.9 1.7 %collective-permute-start.17 = (f32[1]{0:T(128)}, f32[1]{0:T(128)}, u32[]{:S(2)}, u32[]{:S(2)}) collective-permute-start(f32[1]{0:T(128)} %add.869), channel_id=1, source_target_pairs={{0,1},{1,0},{2,3},{3,2},{4,5},{5,4},{6,7},{7,6},{8,9},{9,8},{10,11... | collective-permute-start | bytes 20 | tf_op jit(solution)/shard_map/ppermute | solution.py:36

commit v10 on v9

--- a/solution.py
+++ b/solution.py
@@ -22,13 +22,33 @@
 
 def butterfly_distances(axis):
     devices = lax.axis_size(axis)
-    assert devices & (devices - 1) == 0
+    assert devices & (devices - 1) == 0 and devices > 1
     far = []
     distance = 2
     while distance < devices:
         far.append(distance)
         distance *= 2
-    return far + [1] if devices > 1 else []
+    return far
+
+
+def extended_with(array, dim, width, extra):
+    devices, length = (lax.axis_size("mp"), array.shape[dim])
+    up = [(i, i + 1) for i in range(devices - 1)]
+    down = [(j, i) for i, j in up]
+    plane_shape = list(array.shape)
+    plane_shape[dim] = 1
+    carried = jnp.broadcast_to(extra.reshape([-1] + [1] * (array.ndim - 1)), plane_shape)
+    last = jnp.concatenate([lax.slice_in_dim(array, length - width, length, axis=dim), carried], axis=dim)
+    first = jnp.concatenate([lax.slice_in_dim(array, 0, width, axis=dim), carried], axis=dim)
+    before = lax.ppermute(last, "mp", up)
+    after = lax.ppermute(first, "mp", down)
+    from_below = lax.index_in_dim(before, width, axis=dim, keepdims=False).reshape(extra.shape[0], -1)[:, 0]
+    from_above = lax.index_in_dim(after, width, axis=dim, keepdims=False).reshape(extra.shape[0], -1)[:, 0]
+    paired = jnp.where(lax.axis_index("mp") % 2 == 0, from_above, from_below)
+    wide = jnp.concatenate(
+        [lax.slice_in_dim(before, 0, width, axis=dim), array, lax.slice_in_dim(after, 0, width, axis=dim)], axis=dim
+    )
+    return wide, paired
 
 
 def butterfly_round(values, axis, distance):
@@ -102,11 +122,15 @@
     first_lap = wide_operator(first[1 : 1 + shots], wave_now, flux_buoyancy)
     adjoint_lap = wide_operator(first[1 + shots :], adjoint_operand, flux_buoyancy)
 
-    def operator(values):
-        wide = extended(values, 1, HALO)
+    def operator(values, carried=None):
+        if carried is None:
+            wide = extended(values, 1, HALO)
+        else:
+            wide, paired = extended_with(values, 1, HALO, carried)
         cross = lax.optimization_barrier(cross_terms(values, buoyancy))
         flux = flux_buoyancy * forward_diff(wide, 1, planes + 7, start=HALO - 4)
-        return backward_diff(flux, 1, planes) + cross
+        lap = backward_diff(flux, 1, planes) + cross
+        return lap if carried is None else (lap, paired)
 
     source_local = source_cell - offset
     source_owned = (source_local >= 0) & (source_local < cells)
@@ -158,10 +182,14 @@
         if level == STEPS:
             lap = adjoint_lap
         else:
-            if distances:
-                mu_near, misfit = lax.optimization_barrier((mu_near, misfit))
-                misfit = butterfly_round(misfit, "mp", distances.pop(0))
-            lap = operator(kappa * mu_near)
+            if level == STEPS - 1:
+                lap, paired = operator(kappa * mu_near, misfit)
+                misfit = misfit + paired
+            else:
+                if distances:
+                    mu_near, misfit = lax.optimization_barrier((mu_near, misfit))
+                    misfit = butterfly_round(misfit, "mp", distances.pop(0))
+                lap = operator(kappa * mu_near)
         state = 2.0 * mu_near + lap - mu_far
         state = state + (receiver_count * fields[level - 1] - recorded_sum[level - 1])
         gradient = gradient + state * laps[level - 1]

time: 101 us -> 102 us (level)
  starting transfers between devices: 43.9 us -> 42.7 us
  local copies, waits for them, and re-layouts: 1.7 us -> 2.77 us
    ppermute x0 -> x2, starting transfers between devices: none -> 4.51 us  [the longest x1 2.59 us: extended_with(): after = lax.ppermute(first, 'mp', down)]
    ppermute x0 -> x2, waiting for transfers between devices: none -> 3.75 us  [the longest x1 3.74 us: extended_with(): after = lax.ppermute(first, 'mp', down)]
    ppermute x7 -> x6, waiting for transfers between devices: 15.6 us -> 12.6 us  [extended(): after = lax.ppermute(first, 'mp', down)]
    ppermute x7 -> x6, starting transfers between devices: 19.9 us -> 17.3 us  [extended(): before = lax.ppermute(last, 'mp', up)]
    ppermute x7 -> x6, starting transfers between devices: 15.1 us -> 13 us  [extended(): after = lax.ppermute(first, 'mp', down)]
    slice x0 -> x7, local copies, waits for them, and re-layouts: none -> 1.06 us  [the longest x2 0.52 us: extended_with(): lax.index_in_dim(before, width, axis=dim, keepdims=False)]
    ppermute x4 -> x3, starting transfers between devices: 8.83 us -> 7.92 us  [butterfly_round(): return values + lax.ppermute(values, axis, pairs)]
    ppermute x7 -> x6, waiting for transfers between devices: 3.87 us -> 3.87 us  [extended(): before = lax.ppermute(last, 'mp', up)]
  transfers between devices with their start and end apart: 18 -> 17, of which waited for: 8 -> 8; matrix products, arithmetic and copies ran while one was open for 10% -> 10% of each run, Pallas kernels for 0% -> 0%
where the time goes in v10:
time: 102 us; the launch traced here: 101 us
  starting transfers between devices  42.7 us (42%)
  waiting for transfers between devices  20.2 us (20%)
  other arithmetic  13.3 us (13%)
  matrix products  12.7 us (12%)
  between operations  9.1 us (9%)
  local copies, waits for them, and re-layouts  2.77 us (3%)
    ppermute x6, starting transfers between devices, extended(): before = lax.ppermute(last, 'mp', up)  17.3 us
    ppermute x6, starting transfers between devices, extended(): after = lax.ppermute(first, 'mp', down)  13 us
    ppermute x6, waiting for transfers between devices, extended(): after = lax.ppermute(first, 'mp', down)  12.6 us
    ppermute x3, starting transfers between devices, butterfly_round(): return values + lax.ppermute(values, axis, pairs)  7.92 us
    dot_general x4, matrix products, sample(): jnp.einsum('srk,skz->srz', row_pick, field.reshape(shots, rows, cz), prec...  6.43 us
    dot_general x5, matrix products, injected(): jnp.einsum('srk,srz->skz', row_pick, spread, precision=lax.Precision.HIGH...  6.25 us
    mul x7, other arithmetic, cross_terms(): flux = buoyancy * forward_diff(pad_axis(values, axis), axis, length)  5.34 us
    ppermute x6, waiting for transfers between devices, extended(): before = lax.ppermute(last, 'mp', up)  3.87 us
  transfers between devices with their start and end apart: 17, of which 8 were waited for; matrix products, arithmetic and copies ran while one was open for 10% of the time, Pallas kernels for 0%

profile of v10, /device:TPU:1, one launch (start us, length us, event | category | flops | bytes accessed | tf_op | source)
XLA Modules:
  0.0 100.8 jit_solution(4722235352884222022)
XLA Ops:
  0.7 3.2 %fusion.202 = (f32[1,8,32,128]{3,2,1,0:T(8,128)S(1)}, f32[1,8,32,128]{3,2,1,0:T(8,128)S(1)}, f32[1,8,32,128]{3,2,1,0:T(8,128)S(1)}, f32[8,32,128]{2,1,0:T(8,128)S(1)}) fusion(f32[1,8,32,128]{3,2,1,0:T(8,128)} %param.13, f32[8,32,128]{2,1,0:T(8,128)} %param.11, f32[1,8,32,128]{3,2,1,0:T(8,128)} %param.14, f32[8,32,128]{2,1,0:T(8,128)} %param.10), kind=kLoop, calls=%fused_computation.439 | loop fusion | flops 884736 | bytes 1048576 | tf_op jit(solution)/shard_map/mul | solution.py:89
  4.1 2.0 %collective-permute-start.1 = (f32[3,7,32,128]{3,2,1,0:T(8,128)S(1)}, f32[3,7,32,128]{3,2,1,0:T(8,128)S(1)}, u32[]{:S(2)}, u32[]{:S(2)}) collective-permute-start(f32[3,7,32,128]{3,2,1,0:T(8,128)S(1)} %get-tuple-element.38), channel_id=1, source_target_pairs={{1,0},{2,1},{3,2},{4,3},{5,4},{6,5},{7,6},{8,7},{9,8},{10,9},{11,1... | collective-permute-start | bytes 1032200 | tf_op jit(solution)/shard_map/ppermute | solution.py:19
  6.0 4.5 %collective-permute-start = (f32[3,7,32,128]{3,2,1,0:T(8,128)S(1)}, f32[3,7,32,128]{3,2,1,0:T(8,128)S(1)}, u32[]{:S(2)}, u32[]{:S(2)}) collective-permute-start(f32[3,7,32,128]{3,2,1,0:T(8,128)S(1)} %get-tuple-element.39), channel_id=1, source_target_pairs={{0,1},{1,2},{2,3},{3,4},{4,5},{5,6},{6,7},{7,8},{8,9},{9,10},{10,1... | collective-permute-start | bytes 1032200 | tf_op jit(solution)/shard_map/ppermute | solution.py:18
  11.3 0.7 fusion.656
  12.0 1.3 %fusion.27 = f32[1,8,32,128]{3,2,1,0:T(8,128)S(1)} fusion(s32[8,32]{1,0:T(8,128)S(1)} %multiply_add_fusion, s32[2048]{0:T(1024)S(1)} %bitcast.182, s32[2048]{0:T(1024)S(1)} %bitcast.173), kind=kOutput, calls=%fused_computation.20 | convolution fusion | flops 806354944 | bytes 148480 | tf_op jit(solution)/shard_map/srk,srz->skz/dot_general | solution.py:157
  13.3 0.2 collective-permute-done.1
  13.5 3.9 %collective-permute-done = f32[3,7,32,128]{3,2,1,0:T(8,128)S(1)} collective-permute-done((f32[3,7,32,128]{3,2,1,0:T(8,128)S(1)}, f32[3,7,32,128]{3,2,1,0:T(8,128)S(1)}, u32[]{:S(2)}, u32[]{:S(2)}) %collective-permute-start) | collective-permute-done | bytes 344096 | tf_op jit(solution)/shard_map/ppermute | solution.py:18
  17.5 0.1 fusion.150
  17.6 0.8 copy-done.4
  18.4 1.0 fusion.619
  19.4 0.3 fusion.417
  19.7 4.4 %collective-permute-start.2 = (f32[1,7,32,128]{3,2,1,0:T(8,128)S(1)}, f32[1,7,32,128]{3,2,1,0:T(8,128)S(1)}, u32[]{:S(2)}, u32[]{:S(2)}) collective-permute-start(f32[1,7,32,128]{3,2,1,0:T(8,128)S(1)} %get-tuple-element.66), channel_id=1, source_target_pairs={{0,1},{1,2},{2,3},{3,4},{4,5},{5,6},{6,7},{7,8},{8,9},{9,10},{10,1... | collective-permute-start | bytes 344072 | tf_op jit(solution)/shard_map/ppermute | solution.py:18
  24.1 1.9 %collective-permute-start.3 = (f32[1,7,32,128]{3,2,1,0:T(8,128)S(1)}, f32[1,7,32,128]{3,2,1,0:T(8,128)S(1)}, u32[]{:S(2)}, u32[]{:S(2)}) collective-permute-start(f32[1,7,32,128]{3,2,1,0:T(8,128)S(1)} %get-tuple-element.67), channel_id=1, source_target_pairs={{1,0},{2,1},{3,2},{4,3},{5,4},{6,5},{7,6},{8,7},{9,8},{10,9},{11,1... | collective-permute-start | bytes 344072 | tf_op jit(solution)/shard_map/ppermute | solution.py:19
  26.0 0.3 fusion.239
  26.3 0.1 fusion.158
  26.4 1.6 %fusion.15 = f32[2048]{0:T(1024)S(1)} fusion(f32[256,128]{1,0:T(8,128)S(1)} %bitcast.167, s32[2048]{0:T(1024)S(1)} %bitcast.183, s32[2048]{0:T(1024)S(1)} %bitcast.174), kind=kOutput, calls=%fused_computation.16 | convolution fusion | flops 806615040 | bytes 155648 | tf_op jit(solution)/shard_map/srk,skz->srz/dot_general | solution.py:150
  28.1 2.1 %collective-permute-done.3 = f32[1,7,32,128]{3,2,1,0:T(8,128)S(1)} collective-permute-done((f32[1,7,32,128]{3,2,1,0:T(8,128)S(1)}, f32[1,7,32,128]{3,2,1,0:T(8,128)S(1)}, u32[]{:S(2)}, u32[]{:S(2)}) %collective-permute-start.3) | collective-permute-done | bytes 114720 | tf_op jit(solution)/shard_map/ppermute | solution.py:19
  30.2 0.1 fusion.143
  30.3 0.8 fusion.621
  31.1 0.3 fusion.440
  31.4 1.9 %collective-permute-start.4 = (f32[1,7,32,128]{3,2,1,0:T(8,128)S(1)}, f32[1,7,32,128]{3,2,1,0:T(8,128)S(1)}, u32[]{:S(2)}, u32[]{:S(2)}) collective-permute-start(f32[1,7,32,128]{3,2,1,0:T(8,128)S(1)} %get-tuple-element.64), channel_id=1, source_target_pairs={{0,1},{1,2},{2,3},{3,4},{4,5},{5,6},{6,7},{7,8},{8,9},{9,10},{10,1... | collective-permute-start | bytes 344072 | tf_op jit(solution)/shard_map/ppermute | solution.py:18
  33.4 2.4 %collective-permute-start.5 = (f32[1,7,32,128]{3,2,1,0:T(8,128)S(1)}, f32[1,7,32,128]{3,2,1,0:T(8,128)S(1)}, u32[]{:S(2)}, u32[]{:S(2)}) collective-permute-start(f32[1,7,32,128]{3,2,1,0:T(8,128)S(1)} %get-tuple-element.65), channel_id=1, source_target_pairs={{1,0},{2,1},{3,2},{4,3},{5,4},{6,5},{7,6},{8,7},{9,8},{10,9},{11,1... | collective-permute-start | bytes 344072 | tf_op jit(solution)/shard_map/ppermute | solution.py:19
  35.8 0.3 fusion.263
  36.1 1.6 %fusion.18 = f32[2048]{0:T(1024)S(1)} fusion(f32[256,128]{1,0:T(8,128)S(1)} %bitcast.168, s32[2048]{0:T(1024)S(1)} %bitcast.184, s32[2048]{0:T(1024)S(1)} %bitcast.175), kind=kOutput, calls=%fused_computation.17 | convolution fusion | flops 806615040 | bytes 155648 | tf_op jit(solution)/shard_map/srk,skz->srz/dot_general | solution.py:150
  37.7 1.8 %collective-permute-done.5 = f32[1,7,32,128]{3,2,1,0:T(8,128)S(1)} collective-permute-done((f32[1,7,32,128]{3,2,1,0:T(8,128)S(1)}, f32[1,7,32,128]{3,2,1,0:T(8,128)S(1)}, u32[]{:S(2)}, u32[]{:S(2)}) %collective-permute-start.5) | collective-permute-done | bytes 114720 | tf_op jit(solution)/shard_map/ppermute | solution.py:19
  39.5 0.1 fusion.136
  39.6 0.8 fusion.623
  40.4 0.5 fusion.463
  41.0 1.9 %collective-permute-start.6 = (f32[1,7,32,128]{3,2,1,0:T(8,128)S(1)}, f32[1,7,32,128]{3,2,1,0:T(8,128)S(1)}, u32[]{:S(2)}, u32[]{:S(2)}) collective-permute-start(f32[1,7,32,128]{3,2,1,0:T(8,128)S(1)} %get-tuple-element.60), channel_id=1, source_target_pairs={{0,1},{1,2},{2,3},{3,4},{4,5},{5,6},{6,7},{7,8},{8,9},{9,10},{10,1... | collective-permute-start | bytes 344072 | tf_op jit(solution)/shard_map/ppermute | solution.py:18
  42.9 2.4 %collective-permute-start.7 = (f32[1,7,32,128]{3,2,1,0:T(8,128)S(1)}, f32[1,7,32,128]{3,2,1,0:T(8,128)S(1)}, u32[]{:S(2)}, u32[]{:S(2)}) collective-permute-start(f32[1,7,32,128]{3,2,1,0:T(8,128)S(1)} %get-tuple-element.61), channel_id=1, source_target_pairs={{1,0},{2,1},{3,2},{4,3},{5,4},{6,5},{7,6},{8,7},{9,8},{10,9},{11,1... | collective-permute-start | bytes 344072 | tf_op jit(solution)/shard_map/ppermute | solution.py:19
  45.3 0.3 fusion.287
  45.6 1.6 %fusion.21 = f32[2048]{0:T(1024)S(1)} fusion(f32[256,128]{1,0:T(8,128)S(1)} %bitcast.169, s32[2048]{0:T(1024)S(1)} %bitcast.185, s32[2048]{0:T(1024)S(1)} %bitcast.176), kind=kOutput, calls=%fused_computation.18 | convolution fusion | flops 806615040 | bytes 155648 | tf_op jit(solution)/shard_map/srk,skz->srz/dot_general | solution.py:150
  47.3 2.6 %collective-permute-done.7 = f32[1,7,32,128]{3,2,1,0:T(8,128)S(1)} collective-permute-done((f32[1,7,32,128]{3,2,1,0:T(8,128)S(1)}, f32[1,7,32,128]{3,2,1,0:T(8,128)S(1)}, u32[]{:S(2)}, u32[]{:S(2)}) %collective-permute-start.7) | collective-permute-done | bytes 114720 | tf_op jit(solution)/shard_map/ppermute | solution.py:19
  50.0 0.7 fusion.625
  50.8 1.6 %fusion.24 = f32[2048]{0:T(1024)S(1)} fusion(f32[256,128]{1,0:T(8,128)S(1)} %bitcast.170, s32[2048]{0:T(1024)S(1)} %bitcast.186, s32[2048]{0:T(1024)S(1)} %bitcast.177), kind=kOutput, calls=%fused_computation.19 | convolution fusion | flops 806615040 | bytes 155648 | tf_op jit(solution)/shard_map/srk,skz->srz/dot_general | solution.py:150
  52.4 0.8 fusion.638
  55.8 1.3 %fusion.63 = f32[1,8,32,128]{3,2,1,0:T(8,128)S(1)} fusion(s32[8,32]{1,0:T(8,128)S(1)} %multiply_add_fusion, s32[2048]{0:T(1024)S(1)} %bitcast.187, f32[2048]{0:T(1024)S(1)} %bitcast.198, s32[2048]{0:T(1024)S(1)} %bitcast.178, f32[1,8,32,128]{3,2,1,0:T(8,128)S(1)} %copy-done.11, f32[1,8,32,128]{3,2,1,0:T(8,128)S(1)} %get-tuple-element.62, ...), kind=kOutput, calls=%fused_computation.32 | convolution fusion | flops 807698432 | bytes 1991680 | tf_op jit(solution)/shard_map/srk,srz->skz/dot_general | solution.py:157
  57.2 0.3 fusion.486
  57.5 1.9 %collective-permute-start.8 = (f32[1,8,32,128]{3,2,1,0:T(8,128)S(1)}, f32[1,8,32,128]{3,2,1,0:T(8,128)S(1)}, u32[]{:S(2)}, u32[]{:S(2)}) collective-permute-start(f32[1,8,32,128]{3,2,1,0:T(8,128)S(1)} %concatenate.159), channel_id=1, source_target_pairs={{0,1},{1,2},{2,3},{3,4},{4,5},{5,6},{6,7},{7,8},{8,9},{9,10},{10,1... | collective-permute-start | bytes 393224 | tf_op jit(solution)/shard_map/ppermute | solution.py:43
  59.5 2.6 %collective-permute-start.9 = (f32[1,8,32,128]{3,2,1,0:T(8,128)S(1)}, f32[1,8,32,128]{3,2,1,0:T(8,128)S(1)}, u32[]{:S(2)}, u32[]{:S(2)}) collective-permute-start(f32[1,8,32,128]{3,2,1,0:T(8,128)S(1)} %get-tuple-element.24), channel_id=1, source_target_pairs={{1,0},{2,1},{3,2},{4,3},{5,4},{6,5},{7,6},{8,7},{9,8},{10,9},{11,1... | collective-permute-start | bytes 393224 | tf_op jit(solution)/shard_map/ppermute | solution.py:44
  62.1 0.3 fusion.311
  62.4 0.5 slice.1655
  62.9 3.7 %collective-permute-done.9 = f32[1,8,32,128]{3,2,1,0:T(8,128)S(1)} collective-permute-done((f32[1,8,32,128]{3,2,1,0:T(8,128)S(1)}, f32[1,8,32,128]{3,2,1,0:T(8,128)S(1)}, u32[]{:S(2)}, u32[]{:S(2)}) %collective-permute-start.9) | collective-permute-done | bytes 131104 | tf_op jit(solution)/shard_map/ppermute | solution.py:44
  66.6 0.5 slice.1653
  68.5 0.1 fusion.122
  68.6 1.2 %fusion.57 = f32[1,8,32,128]{3,2,1,0:T(8,128)S(1)} fusion(s32[8,32]{1,0:T(8,128)S(1)} %multiply_add_fusion, s32[2048]{0:T(1024)S(1)} %bitcast.188, f32[2048]{0:T(1024)S(1)} %bitcast.197, s32[2048]{0:T(1024)S(1)} %bitcast.179, f32[1,8,32,128]{3,2,1,0:T(8,128)S(1)} %copy-done.6, f32[1,8,32,128]{3,2,1,0:T(8,128)S(1)} %fusion.311, ...), kind=kOutput, calls=%fused_computation.30 | convolution fusion | flops 806944768 | bytes 1860608 | tf_op jit(solution)/shard_map/srk,srz->skz/dot_general | solution.py:157
  70.0 0.3 fusion.509
  70.3 3.0 %collective-permute-start.12 = (f32[1]{0:T(128)}, f32[1]{0:T(128)}, u32[]{:S(2)}, u32[]{:S(2)}) collective-permute-start(f32[1]{0:T(128)} %add.828), channel_id=1, source_target_pairs={{0,2},{1,3},{2,0},{3,1},{4,6},{5,7},{6,4},{7,5},{8,10},{9,11},{10,... | collective-permute-start | bytes 20 | tf_op jit(solution)/shard_map/ppermute | solution.py:56
  73.3 1.9 %collective-permute-start.10 = (f32[1,7,32,128]{3,2,1,0:T(8,128)S(1)}, f32[1,7,32,128]{3,2,1,0:T(8,128)S(1)}, u32[]{:S(2)}, u32[]{:S(2)}) collective-permute-start(f32[1,7,32,128]{3,2,1,0:T(8,128)S(1)} %get-tuple-element.58), channel_id=1, source_target_pairs={{0,1},{1,2},{2,3},{3,4},{4,5},{5,6},{6,7},{7,8},{8,9},{9,10},{10,1... | collective-permute-start | bytes 344072 | tf_op jit(solution)/shard_map/ppermute | solution.py:18
  75.2 2.4 %collective-permute-start.11 = (f32[1,7,32,128]{3,2,1,0:T(8,128)S(1)}, f32[1,7,32,128]{3,2,1,0:T(8,128)S(1)}, u32[]{:S(2)}, u32[]{:S(2)}) collective-permute-start(f32[1,7,32,128]{3,2,1,0:T(8,128)S(1)} %get-tuple-element.59), channel_id=1, source_target_pairs={{1,0},{2,1},{3,2},{4,3},{5,4},{6,5},{7,6},{8,7},{9,8},{10,9},{11,1... | collective-permute-start | bytes 344072 | tf_op jit(solution)/shard_map/ppermute | solution.py:19
  77.6 0.3 fusion.335
  78.6 2.7 %collective-permute-done.11 = f32[1,7,32,128]{3,2,1,0:T(8,128)S(1)} collective-permute-done((f32[1,7,32,128]{3,2,1,0:T(8,128)S(1)}, f32[1,7,32,128]{3,2,1,0:T(8,128)S(1)}, u32[]{:S(2)}, u32[]{:S(2)}) %collective-permute-start.11) | collective-permute-done | bytes 114720 | tf_op jit(solution)/shard_map/ppermute | solution.py:19
  81.4 0.1 fusion.115
  81.5 1.2 %fusion.51 = f32[1,8,32,128]{3,2,1,0:T(8,128)S(1)} fusion(s32[8,32]{1,0:T(8,128)S(1)} %multiply_add_fusion, s32[2048]{0:T(1024)S(1)} %bitcast.189, f32[2048]{0:T(1024)S(1)} %bitcast.196, s32[2048]{0:T(1024)S(1)} %bitcast.180, f32[1,8,32,128]{3,2,1,0:T(8,128)S(1)} %fusion.63, f32[1,8,32,128]{3,2,1,0:T(8,128)S(1)} %fusion.335, ...), kind=kOutput, calls=%fused_computation.28 | convolution fusion | flops 806944768 | bytes 1860608 | tf_op jit(solution)/shard_map/srk,srz->skz/dot_general | solution.py:157
  82.8 0.3 fusion.532
  83.1 2.1 %collective-permute-start.15 = (f32[1]{0:T(128)}, f32[1]{0:T(128)}, u32[]{:S(2)}, u32[]{:S(2)}) collective-permute-start(f32[1]{0:T(128)} %add.852), channel_id=1, source_target_pairs={{0,4},{1,5},{2,6},{3,7},{4,0},{5,1},{6,2},{7,3},{8,12},{9,13},{10,... | collective-permute-start | bytes 20 | tf_op jit(solution)/shard_map/ppermute | solution.py:56
  85.2 2.6 %collective-permute-start.13 = (f32[1,7,32,128]{3,2,1,0:T(8,128)S(1)}, f32[1,7,32,128]{3,2,1,0:T(8,128)S(1)}, u32[]{:S(2)}, u32[]{:S(2)}) collective-permute-start(f32[1,7,32,128]{3,2,1,0:T(8,128)S(1)} %get-tuple-element.56), channel_id=1, source_target_pairs={{0,1},{1,2},{2,3},{3,4},{4,5},{5,6},{6,7},{7,8},{8,9},{9,10},{10,1... | collective-permute-start | bytes 344072 | tf_op jit(solution)/shard_map/ppermute | solution.py:18
  87.8 1.9 %collective-permute-start.14 = (f32[1,7,32,128]{3,2,1,0:T(8,128)S(1)}, f32[1,7,32,128]{3,2,1,0:T(8,128)S(1)}, u32[]{:S(2)}, u32[]{:S(2)}) collective-permute-start(f32[1,7,32,128]{3,2,1,0:T(8,128)S(1)} %get-tuple-element.57), channel_id=1, source_target_pairs={{1,0},{2,1},{3,2},{4,3},{5,4},{6,5},{7,6},{8,7},{9,8},{10,9},{11,1... | collective-permute-start | bytes 344072 | tf_op jit(solution)/shard_map/ppermute | solution.py:19
  89.8 0.3 fusion.359
  90.8 3.2 %collective-permute-done.14 = f32[1,7,32,128]{3,2,1,0:T(8,128)S(1)} collective-permute-done((f32[1,7,32,128]{3,2,1,0:T(8,128)S(1)}, f32[1,7,32,128]{3,2,1,0:T(8,128)S(1)}, u32[]{:S(2)}, u32[]{:S(2)}) %collective-permute-start.14) | collective-permute-done | bytes 114720 | tf_op jit(solution)/shard_map/ppermute | solution.py:19
  94.0 0.1 fusion.108
  94.1 1.2 %fusion.45 = f32[1,8,32,128]{3,2,1,0:T(8,128)S(1)} fusion(s32[8,32]{1,0:T(8,128)S(1)} %multiply_add_fusion, s32[2048]{0:T(1024)S(1)} %bitcast.190, f32[2048]{0:T(1024)S(1)} %bitcast.195, s32[2048]{0:T(1024)S(1)} %bitcast.181, f32[1,8,32,128]{3,2,1,0:T(8,128)S(1)} %fusion.57, f32[1,8,32,128]{3,2,1,0:T(8,128)S(1)} %fusion.359, ...), kind=kOutput, calls=%fused_computation.26 | convolution fusion | flops 806944768 | bytes 1860608 | tf_op jit(solution)/shard_map/srk,srz->skz/dot_general | solution.py:157
  95.4 2.8 %collective-permute-start.16 = (f32[1]{0:T(128)}, f32[1]{0:T(128)}, u32[]{:S(2)}, u32[]{:S(2)}) collective-permute-start(f32[1]{0:T(128)} %add.876), channel_id=1, source_target_pairs={{0,8},{1,9},{2,10},{3,11},{4,12},{5,13},{6,14},{7,15},{8,0},{9,1},... | collective-permute-start | bytes 20 | tf_op jit(solution)/shard_map/ppermute | solution.py:56
  98.2 0.8 bitcast_multiply_fusion
  (62 shorter events, 0.9 us)
Async XLA Ops:
  0.6 3.3 %copy-start = (f32[8,32,128]{2,1,0:T(8,128)S(1)}, f32[8,32,128]{2,1,0:T(8,128)}, u32[]{:S(2)}) copy-start(f32[8,32,128]{2,1,0:T(8,128)} %param.11) | copy-start | bytes 393220
  0.6 3.3 %copy-start.1 = (f32[1,8,32,128]{3,2,1,0:T(8,128)S(1)}, f32[1,8,32,128]{3,2,1,0:T(8,128)}, u32[]{:S(2)}) copy-start(f32[1,8,32,128]{3,2,1,0:T(8,128)} %param.13) | copy-start | bytes 393220
  3.9 7.3 %copy-start.9 = (f32[1,4]{1,0:T(1,128)S(1)}, f32[1,4]{1,0:T(1,128)}, u32[]{:S(2)}) copy-start(f32[1,4]{1,0:T(1,128)} %param.17) | copy-start | bytes 52
  3.9 8.0 %copy-start.8 = (s32[1,2048]{1,0:T(1,128)S(1)}, s32[1,2048]{1,0:T(1,128)}, u32[]{:S(2)}) copy-start(s32[1,2048]{1,0:T(1,128)} %param.18) | copy-start | bytes 24580
  4.1 9.2 %copy-start.5 = (f32[1,4,2048]{2,1,0:T(4,128)S(1)}, f32[1,4,2048]{2,1,0:T(4,128)}, u32[]{:S(2)}) copy-start(f32[1,4,2048]{2,1,0:T(4,128)} %param.19) | copy-start | bytes 98308
  4.1 9.5 %collective-permute-start.1 = (f32[3,7,32,128]{3,2,1,0:T(8,128)S(1)}, f32[3,7,32,128]{3,2,1,0:T(8,128)S(1)}, u32[]{:S(2)}, u32[]{:S(2)}) collective-permute-start(f32[3,7,32,128]{3,2,1,0:T(8,128)S(1)} %get-tuple-element.38), channel_id=1, source_target_pairs={{1,0},{2,1},{3,2},{4,3},{5,4},{6,5},{7,6},{8,7},{9,8},{10,9},{11,1... | collective-permute-start | bytes 1032200 | tf_op jit(solution)/shard_map/ppermute | solution.py:19
  6.0 11.3 %collective-permute-start = (f32[3,7,32,128]{3,2,1,0:T(8,128)S(1)}, f32[3,7,32,128]{3,2,1,0:T(8,128)S(1)}, u32[]{:S(2)}, u32[]{:S(2)}) collective-permute-start(f32[3,7,32,128]{3,2,1,0:T(8,128)S(1)} %get-tuple-element.39), channel_id=1, source_target_pairs={{0,1},{1,2},{2,3},{3,4},{4,5},{5,6},{6,7},{7,8},{8,9},{9,10},{10,1... | collective-permute-start | bytes 1032200 | tf_op jit(solution)/shard_map/ppermute | solution.py:18
  17.5 0.9 copy-start.4
  19.7 8.4 %collective-permute-start.2 = (f32[1,7,32,128]{3,2,1,0:T(8,128)S(1)}, f32[1,7,32,128]{3,2,1,0:T(8,128)S(1)}, u32[]{:S(2)}, u32[]{:S(2)}) collective-permute-start(f32[1,7,32,128]{3,2,1,0:T(8,128)S(1)} %get-tuple-element.66), channel_id=1, source_target_pairs={{0,1},{1,2},{2,3},{3,4},{4,5},{5,6},{6,7},{7,8},{8,9},{9,10},{10,1... | collective-permute-start | bytes 344072 | tf_op jit(solution)/shard_map/ppermute | solution.py:18
  24.1 6.1 %collective-permute-start.3 = (f32[1,7,32,128]{3,2,1,0:T(8,128)S(1)}, f32[1,7,32,128]{3,2,1,0:T(8,128)S(1)}, u32[]{:S(2)}, u32[]{:S(2)}) collective-permute-start(f32[1,7,32,128]{3,2,1,0:T(8,128)S(1)} %get-tuple-element.67), channel_id=1, source_target_pairs={{1,0},{2,1},{3,2},{4,3},{5,4},{6,5},{7,6},{8,7},{9,8},{10,9},{11,1... | collective-permute-start | bytes 344072 | tf_op jit(solution)/shard_map/ppermute | solution.py:19
  31.4 6.3 %collective-permute-start.4 = (f32[1,7,32,128]{3,2,1,0:T(8,128)S(1)}, f32[1,7,32,128]{3,2,1,0:T(8,128)S(1)}, u32[]{:S(2)}, u32[]{:S(2)}) collective-permute-start(f32[1,7,32,128]{3,2,1,0:T(8,128)S(1)} %get-tuple-element.64), channel_id=1, source_target_pairs={{0,1},{1,2},{2,3},{3,4},{4,5},{5,6},{6,7},{7,8},{8,9},{9,10},{10,1... | collective-permute-start | bytes 344072 | tf_op jit(solution)/shard_map/ppermute | solution.py:18
  33.4 6.1 %collective-permute-start.5 = (f32[1,7,32,128]{3,2,1,0:T(8,128)S(1)}, f32[1,7,32,128]{3,2,1,0:T(8,128)S(1)}, u32[]{:S(2)}, u32[]{:S(2)}) collective-permute-start(f32[1,7,32,128]{3,2,1,0:T(8,128)S(1)} %get-tuple-element.65), channel_id=1, source_target_pairs={{1,0},{2,1},{3,2},{4,3},{5,4},{6,5},{7,6},{8,7},{9,8},{10,9},{11,1... | collective-permute-start | bytes 344072 | tf_op jit(solution)/shard_map/ppermute | solution.py:19
  41.0 6.3 %collective-permute-start.6 = (f32[1,7,32,128]{3,2,1,0:T(8,128)S(1)}, f32[1,7,32,128]{3,2,1,0:T(8,128)S(1)}, u32[]{:S(2)}, u32[]{:S(2)}) collective-permute-start(f32[1,7,32,128]{3,2,1,0:T(8,128)S(1)} %get-tuple-element.60), channel_id=1, source_target_pairs={{0,1},{1,2},{2,3},{3,4},{4,5},{5,6},{6,7},{7,8},{8,9},{9,10},{10,1... | collective-permute-start | bytes 344072 | tf_op jit(solution)/shard_map/ppermute | solution.py:18
  42.9 7.0 %collective-permute-start.7 = (f32[1,7,32,128]{3,2,1,0:T(8,128)S(1)}, f32[1,7,32,128]{3,2,1,0:T(8,128)S(1)}, u32[]{:S(2)}, u32[]{:S(2)}) collective-permute-start(f32[1,7,32,128]{3,2,1,0:T(8,128)S(1)} %get-tuple-element.61), channel_id=1, source_target_pairs={{1,0},{2,1},{3,2},{4,3},{5,4},{6,5},{7,6},{8,7},{9,8},{10,9},{11,1... | collective-permute-start | bytes 344072 | tf_op jit(solution)/shard_map/ppermute | solution.py:19
  50.8 5.0 %copy-start.6 = (f32[1,8,32,128]{3,2,1,0:T(8,128)S(1)}, f32[1,8,32,128]{3,2,1,0:T(8,128)}, u32[]{:S(2)}) copy-start(f32[1,8,32,128]{3,2,1,0:T(8,128)} %param.14) | copy-start | bytes 393220
  50.8 5.0 %copy-start.11 = (f32[1,8,32,128]{3,2,1,0:T(8,128)S(1)}, f32[1,8,32,128]{3,2,1,0:T(8,128)}, u32[]{:S(2)}) copy-start(f32[1,8,32,128]{3,2,1,0:T(8,128)} %param.15) | copy-start | bytes 393220
  55.8 1.3 %copy-start.10 = (pred[8]{0:T(512)(128)(4,1)S(1)}, pred[8]{0:T(512)(128)(4,1)}, u32[]{:S(2)}) copy-start(pred[8]{0:T(512)(128)(4,1)} %constant.77.clone.1) | copy-start | bytes 28
  57.5 4.8 %collective-permute-start.8 = (f32[1,8,32,128]{3,2,1,0:T(8,128)S(1)}, f32[1,8,32,128]{3,2,1,0:T(8,128)S(1)}, u32[]{:S(2)}, u32[]{:S(2)}) collective-permute-start(f32[1,8,32,128]{3,2,1,0:T(8,128)S(1)} %concatenate.159), channel_id=1, source_target_pairs={{0,1},{1,2},{2,3},{3,4},{4,5},{5,6},{6,7},{7,8},{8,9},{9,10},{10,1... | collective-permute-start | bytes 393224 | tf_op jit(solution)/shard_map/ppermute | solution.py:43
  59.5 7.2 %collective-permute-start.9 = (f32[1,8,32,128]{3,2,1,0:T(8,128)S(1)}, f32[1,8,32,128]{3,2,1,0:T(8,128)S(1)}, u32[]{:S(2)}, u32[]{:S(2)}) collective-permute-start(f32[1,8,32,128]{3,2,1,0:T(8,128)S(1)} %get-tuple-element.24), channel_id=1, source_target_pairs={{1,0},{2,1},{3,2},{4,3},{5,4},{6,5},{7,6},{8,7},{9,8},{10,9},{11,1... | collective-permute-start | bytes 393224 | tf_op jit(solution)/shard_map/ppermute | solution.py:44
  70.3 7.7 %collective-permute-start.12 = (f32[1]{0:T(128)}, f32[1]{0:T(128)}, u32[]{:S(2)}, u32[]{:S(2)}) collective-permute-start(f32[1]{0:T(128)} %add.828), channel_id=1, source_target_pairs={{0,2},{1,3},{2,0},{3,1},{4,6},{5,7},{6,4},{7,5},{8,10},{9,11},{10,... | collective-permute-start | bytes 20 | tf_op jit(solution)/shard_map/ppermute | solution.py:56
  73.3 5.3 %collective-permute-start.10 = (f32[1,7,32,128]{3,2,1,0:T(8,128)S(1)}, f32[1,7,32,128]{3,2,1,0:T(8,128)S(1)}, u32[]{:S(2)}, u32[]{:S(2)}) collective-permute-start(f32[1,7,32,128]{3,2,1,0:T(8,128)S(1)} %get-tuple-element.58), channel_id=1, source_target_pairs={{0,1},{1,2},{2,3},{3,4},{4,5},{5,6},{6,7},{7,8},{8,9},{9,10},{10,1... | collective-permute-start | bytes 344072 | tf_op jit(solution)/shard_map/ppermute | solution.py:18
  75.2 6.1 %collective-permute-start.11 = (f32[1,7,32,128]{3,2,1,0:T(8,128)S(1)}, f32[1,7,32,128]{3,2,1,0:T(8,128)S(1)}, u32[]{:S(2)}, u32[]{:S(2)}) collective-permute-start(f32[1,7,32,128]{3,2,1,0:T(8,128)S(1)} %get-tuple-element.59), channel_id=1, source_target_pairs={{1,0},{2,1},{3,2},{4,3},{5,4},{6,5},{7,6},{8,7},{9,8},{10,9},{11,1... | collective-permute-start | bytes 344072 | tf_op jit(solution)/shard_map/ppermute | solution.py:19
  82.7 15.4 %copy-start.2 = (f32[1,8,32,128]{3,2,1,0:T(8,128)}, f32[1,8,32,128]{3,2,1,0:T(8,128)S(1)}, u32[]{:S(2)}) copy-start(f32[1,8,32,128]{3,2,1,0:T(8,128)S(1)} %fusion.51) | copy-start | bytes 393220
  83.1 7.0 %collective-permute-start.15 = (f32[1]{0:T(128)}, f32[1]{0:T(128)}, u32[]{:S(2)}, u32[]{:S(2)}) collective-permute-start(f32[1]{0:T(128)} %add.852), channel_id=1, source_target_pairs={{0,4},{1,5},{2,6},{3,7},{4,0},{5,1},{6,2},{7,3},{8,12},{9,13},{10,... | collective-permute-start | bytes 20 | tf_op jit(solution)/shard_map/ppermute | solution.py:56
  85.2 5.6 %collective-permute-start.13 = (f32[1,7,32,128]{3,2,1,0:T(8,128)S(1)}, f32[1,7,32,128]{3,2,1,0:T(8,128)S(1)}, u32[]{:S(2)}, u32[]{:S(2)}) collective-permute-start(f32[1,7,32,128]{3,2,1,0:T(8,128)S(1)} %get-tuple-element.56), channel_id=1, source_target_pairs={{0,1},{1,2},{2,3},{3,4},{4,5},{5,6},{6,7},{7,8},{8,9},{9,10},{10,1... | collective-permute-start | bytes 344072 | tf_op jit(solution)/shard_map/ppermute | solution.py:18
  87.8 6.1 %collective-permute-start.14 = (f32[1,7,32,128]{3,2,1,0:T(8,128)S(1)}, f32[1,7,32,128]{3,2,1,0:T(8,128)S(1)}, u32[]{:S(2)}, u32[]{:S(2)}) collective-permute-start(f32[1,7,32,128]{3,2,1,0:T(8,128)S(1)} %get-tuple-element.57), channel_id=1, source_target_pairs={{1,0},{2,1},{3,2},{4,3},{5,4},{6,5},{7,6},{8,7},{9,8},{10,9},{11,1... | collective-permute-start | bytes 344072 | tf_op jit(solution)/shard_map/ppermute | solution.py:19
  94.1 4.1 %copy-start.3 = (f32[8,32,128]{2,1,0:T(8,128)S(1)}, f32[8,32,128]{2,1,0:T(8,128)}, u32[]{:S(2)}) copy-start(f32[8,32,128]{2,1,0:T(8,128)} %param.10) | copy-start | bytes 393220
  95.3 4.3 %copy-start.7 = (f32[1,8,32,128]{3,2,1,0:T(8,128)}, f32[1,8,32,128]{3,2,1,0:T(8,128)S(1)}, u32[]{:S(2)}) copy-start(f32[1,8,32,128]{3,2,1,0:T(8,128)S(1)} %fusion.45) | copy-start | bytes 393220
  95.4 3.6 %collective-permute-start.16 = (f32[1]{0:T(128)}, f32[1]{0:T(128)}, u32[]{:S(2)}, u32[]{:S(2)}) collective-permute-start(f32[1]{0:T(128)} %add.876), channel_id=1, source_target_pairs={{0,8},{1,9},{2,10},{3,11},{4,12},{5,13},{6,14},{7,15},{8,0},{9,1},... | collective-permute-start | bytes 20 | tf_op jit(solution)/shard_map/ppermute | solution.py:56

commit v11 on v9

--- a/solution.py
+++ b/solution.py
@@ -102,11 +102,14 @@
     first_lap = wide_operator(first[1 : 1 + shots], wave_now, flux_buoyancy)
     adjoint_lap = wide_operator(first[1 + shots :], adjoint_operand, flux_buoyancy)
 
-    def operator(values):
+    def operator(values, later=None):
         wide = extended(values, 1, HALO)
         cross = lax.optimization_barrier(cross_terms(values, buoyancy))
+        if later is not None:
+            cross, later = lax.optimization_barrier((cross, later))
         flux = flux_buoyancy * forward_diff(wide, 1, planes + 7, start=HALO - 4)
-        return backward_diff(flux, 1, planes) + cross
+        lap = backward_diff(flux, 1, planes) + cross
+        return lap if later is None else (lap, later)
 
     source_local = source_cell - offset
     source_owned = (source_local >= 0) & (source_local < cells)
@@ -146,11 +149,12 @@
         following = 2.0 * current - before + kappa * lap
         amount = wavelet[:, step].reshape(shots, 1, 1, 1)
         following = following + jnp.where(source_hit, amount, 0.0)
-        sampled = sample(following)
-        resids.append(jnp.where(receiver_owned, sampled - observed[:, step, :], 0.0))
+        if step < STEPS - 1:
+            sampled = sample(following)
+            resids.append(jnp.where(receiver_owned, sampled - observed[:, step, :], 0.0))
         fields.append(following)
         before, current = (current, following)
-    misfit = 0.5 * sum((jnp.sum(item * item, axis=1) for item in resids))
+    squares = sum((jnp.sum(item * item, axis=1) for item in resids))
     distances = butterfly_distances("mp")
     mu_near, mu_far = (adjoint_next, adjoint_after)
     gradient = jnp.zeros(shape, jnp.float32)
@@ -158,15 +162,24 @@
         if level == STEPS:
             lap = adjoint_lap
         else:
-            if distances:
-                mu_near, misfit = lax.optimization_barrier((mu_near, misfit))
-                misfit = butterfly_round(misfit, "mp", distances.pop(0))
-            lap = operator(kappa * mu_near)
+            if level == STEPS - 1:
+                lap, last = operator(kappa * mu_near, fields[-1])
+                sampled = sample(last)
+                resid = jnp.where(receiver_owned, sampled - observed[:, STEPS - 1, :], 0.0)
+                misfit = 0.5 * (squares + jnp.sum(resid * resid, axis=1))
+                if distances:
+                    misfit = butterfly_round(misfit, "mp", distances.pop(0))
+            else:
+                if distances:
+                    mu_near, misfit = lax.optimization_barrier((mu_near, misfit))
+                    misfit = butterfly_round(misfit, "mp", distances.pop(0))
+                lap = operator(kappa * mu_near)
         state = 2.0 * mu_near + lap - mu_far
         state = state + (receiver_count * fields[level - 1] - recorded_sum[level - 1])
         gradient = gradient + state * laps[level - 1]
         mu_far, mu_near = (mu_near, state)
-        mu_near, misfit = lax.optimization_barrier((mu_near, misfit))
+        if level < STEPS:
+            mu_near, misfit = lax.optimization_barrier((mu_near, misfit))
     for distance in distances:
         misfit = butterfly_round(misfit, "mp", distance)
     velocity_gradient = 2.0 * velocity / buoyancy * jnp.sum(gradient, axis=0)

time: 101 us -> 102 us (level)
  starting transfers between devices: 43.9 us -> 46.8 us
  waiting for transfers between devices: 19.5 us -> 17 us
    ppermute x7, waiting for transfers between devices: 15.6 us -> 12.8 us  [extended(): after = lax.ppermute(first, 'mp', down)]
    ppermute x7, starting transfers between devices: 19.9 us -> 22.4 us  [extended(): before = lax.ppermute(last, 'mp', up)]
  transfers between devices with their start and end apart: 18 -> 18, of which waited for: 8 -> 8; matrix products, arithmetic and copies ran while one was open for 10% -> 12% of each run, Pallas kernels for 0% -> 0%
where the time goes in v11:
time: 102 us; the launch traced here: 100 us
  starting transfers between devices  46.8 us (46%)
  waiting for transfers between devices  17 us (17%)
  other arithmetic  13.3 us (13%)
  matrix products  12.7 us (12%)
  between operations  8.45 us (8%)
  local copies, waits for them, and re-layouts  1.88 us (2%)
    ppermute x7, starting transfers between devices, extended(): before = lax.ppermute(last, 'mp', up)  22.4 us
    ppermute x7, starting transfers between devices, extended(): after = lax.ppermute(first, 'mp', down)  15.8 us
    ppermute x7, waiting for transfers between devices, extended(): after = lax.ppermute(first, 'mp', down)  12.8 us
    ppermute x4, starting transfers between devices, butterfly_round(): return values + lax.ppermute(values, axis, pairs)  8.6 us
    dot_general x4, matrix products, sample(): jnp.einsum('srk,skz->srz', row_pick, field.reshape(shots, rows, cz), prec...  6.43 us
    dot_general x5, matrix products, injected(): jnp.einsum('srk,srz->skz', row_pick, spread, precision=lax.Precision.HIGH...  6.26 us
    mul x7, other arithmetic, cross_terms(): flux = buoyancy * forward_diff(pad_axis(values, axis), axis, length)  5.41 us
    ppermute x7, waiting for transfers between devices, extended(): before = lax.ppermute(last, 'mp', up)  3.87 us
  transfers between devices with their start and end apart: 18, of which 8 were waited for; matrix products, arithmetic and copies ran while one was open for 12% of the time, Pallas kernels for 0%

profile of v11, /device:TPU:1, one launch (start us, length us, event | category | flops | bytes accessed | tf_op | source)
XLA Modules:
  0.0 100.1 jit_solution(14051852399158898629)
XLA Ops:
  0.7 3.3 %fusion.202 = (f32[1,8,32,128]{3,2,1,0:T(8,128)S(1)}, f32[1,8,32,128]{3,2,1,0:T(8,128)S(1)}, f32[1,8,32,128]{3,2,1,0:T(8,128)S(1)}, f32[8,32,128]{2,1,0:T(8,128)S(1)}) fusion(f32[1,8,32,128]{3,2,1,0:T(8,128)} %param.13, f32[8,32,128]{2,1,0:T(8,128)} %param.11, f32[1,8,32,128]{3,2,1,0:T(8,128)} %param.14, f32[8,32,128]{2,1,0:T(8,128)} %param.10), kind=kLoop, calls=%fused_computation.439 | loop fusion | flops 884736 | bytes 1048576 | tf_op jit(solution)/shard_map/mul | solution.py:69
  4.1 2.0 %collective-permute-start.1 = (f32[3,7,32,128]{3,2,1,0:T(8,128)S(1)}, f32[3,7,32,128]{3,2,1,0:T(8,128)S(1)}, u32[]{:S(2)}, u32[]{:S(2)}) collective-permute-start(f32[3,7,32,128]{3,2,1,0:T(8,128)S(1)} %get-tuple-element.36), channel_id=1, source_target_pairs={{1,0},{2,1},{3,2},{4,3},{5,4},{6,5},{7,6},{8,7},{9,8},{10,9},{11,1... | collective-permute-start | bytes 1032200 | tf_op jit(solution)/shard_map/ppermute | solution.py:19
  6.1 4.5 %collective-permute-start = (f32[3,7,32,128]{3,2,1,0:T(8,128)S(1)}, f32[3,7,32,128]{3,2,1,0:T(8,128)S(1)}, u32[]{:S(2)}, u32[]{:S(2)}) collective-permute-start(f32[3,7,32,128]{3,2,1,0:T(8,128)S(1)} %get-tuple-element.37), channel_id=1, source_target_pairs={{0,1},{1,2},{2,3},{3,4},{4,5},{5,6},{6,7},{7,8},{8,9},{9,10},{10,1... | collective-permute-start | bytes 1032200 | tf_op jit(solution)/shard_map/ppermute | solution.py:18
  11.3 0.7 fusion.657
  12.1 1.3 %fusion.27 = f32[1,8,32,128]{3,2,1,0:T(8,128)S(1)} fusion(s32[8,32]{1,0:T(8,128)S(1)} %multiply_add_fusion, s32[2048]{0:T(1024)S(1)} %bitcast.175, s32[2048]{0:T(1024)S(1)} %bitcast.166), kind=kOutput, calls=%fused_computation.20 | convolution fusion | flops 806354944 | bytes 148480 | tf_op jit(solution)/shard_map/srk,srz->skz/dot_general | solution.py:136
  13.4 0.2 collective-permute-done.1
  13.6 3.9 %collective-permute-done = f32[3,7,32,128]{3,2,1,0:T(8,128)S(1)} collective-permute-done((f32[3,7,32,128]{3,2,1,0:T(8,128)S(1)}, f32[3,7,32,128]{3,2,1,0:T(8,128)S(1)}, u32[]{:S(2)}, u32[]{:S(2)}) %collective-permute-start) | collective-permute-done | bytes 344096 | tf_op jit(solution)/shard_map/ppermute | solution.py:18
  17.5 0.1 fusion.150
  17.7 0.8 copy-done.4
  18.4 1.0 fusion.619
  19.4 0.3 fusion.417
  19.8 4.4 %collective-permute-start.2 = (f32[1,7,32,128]{3,2,1,0:T(8,128)S(1)}, f32[1,7,32,128]{3,2,1,0:T(8,128)S(1)}, u32[]{:S(2)}, u32[]{:S(2)}) collective-permute-start(f32[1,7,32,128]{3,2,1,0:T(8,128)S(1)} %get-tuple-element.66), channel_id=1, source_target_pairs={{0,1},{1,2},{2,3},{3,4},{4,5},{5,6},{6,7},{7,8},{8,9},{9,10},{10,1... | collective-permute-start | bytes 344072 | tf_op jit(solution)/shard_map/ppermute | solution.py:18
  24.2 1.9 %collective-permute-start.3 = (f32[1,7,32,128]{3,2,1,0:T(8,128)S(1)}, f32[1,7,32,128]{3,2,1,0:T(8,128)S(1)}, u32[]{:S(2)}, u32[]{:S(2)}) collective-permute-start(f32[1,7,32,128]{3,2,1,0:T(8,128)S(1)} %get-tuple-element.67), channel_id=1, source_target_pairs={{1,0},{2,1},{3,2},{4,3},{5,4},{6,5},{7,6},{8,7},{9,8},{10,9},{11,1... | collective-permute-start | bytes 344072 | tf_op jit(solution)/shard_map/ppermute | solution.py:19
  26.1 0.3 fusion.239
  26.4 0.1 fusion.158
  26.5 1.6 %fusion.15 = f32[2048]{0:T(1024)S(1)} fusion(f32[256,128]{1,0:T(8,128)S(1)} %bitcast.162, s32[2048]{0:T(1024)S(1)} %bitcast.176, s32[2048]{0:T(1024)S(1)} %bitcast.167), kind=kOutput, calls=%fused_computation.16 | convolution fusion | flops 806615040 | bytes 155648 | tf_op jit(solution)/shard_map/srk,skz->srz/dot_general | solution.py:129
  28.1 2.1 %collective-permute-done.3 = f32[1,7,32,128]{3,2,1,0:T(8,128)S(1)} collective-permute-done((f32[1,7,32,128]{3,2,1,0:T(8,128)S(1)}, f32[1,7,32,128]{3,2,1,0:T(8,128)S(1)}, u32[]{:S(2)}, u32[]{:S(2)}) %collective-permute-start.3) | collective-permute-done | bytes 114720 | tf_op jit(solution)/shard_map/ppermute | solution.py:19
  30.3 0.1 fusion.143
  30.4 0.8 fusion.621
  31.2 0.3 fusion.440
  31.5 1.9 %collective-permute-start.4 = (f32[1,7,32,128]{3,2,1,0:T(8,128)S(1)}, f32[1,7,32,128]{3,2,1,0:T(8,128)S(1)}, u32[]{:S(2)}, u32[]{:S(2)}) collective-permute-start(f32[1,7,32,128]{3,2,1,0:T(8,128)S(1)} %get-tuple-element.64), channel_id=1, source_target_pairs={{0,1},{1,2},{2,3},{3,4},{4,5},{5,6},{6,7},{7,8},{8,9},{9,10},{10,1... | collective-permute-start | bytes 344072 | tf_op jit(solution)/shard_map/ppermute | solution.py:18
  33.4 2.4 %collective-permute-start.5 = (f32[1,7,32,128]{3,2,1,0:T(8,128)S(1)}, f32[1,7,32,128]{3,2,1,0:T(8,128)S(1)}, u32[]{:S(2)}, u32[]{:S(2)}) collective-permute-start(f32[1,7,32,128]{3,2,1,0:T(8,128)S(1)} %get-tuple-element.65), channel_id=1, source_target_pairs={{1,0},{2,1},{3,2},{4,3},{5,4},{6,5},{7,6},{8,7},{9,8},{10,9},{11,1... | collective-permute-start | bytes 344072 | tf_op jit(solution)/shard_map/ppermute | solution.py:19
  35.8 0.3 fusion.263
  36.2 1.6 %fusion.18 = f32[2048]{0:T(1024)S(1)} fusion(f32[256,128]{1,0:T(8,128)S(1)} %bitcast.163, s32[2048]{0:T(1024)S(1)} %bitcast.177, s32[2048]{0:T(1024)S(1)} %bitcast.168), kind=kOutput, calls=%fused_computation.17 | convolution fusion | flops 806615040 | bytes 155648 | tf_op jit(solution)/shard_map/srk,skz->srz/dot_general | solution.py:129
  37.8 1.8 %collective-permute-done.5 = f32[1,7,32,128]{3,2,1,0:T(8,128)S(1)} collective-permute-done((f32[1,7,32,128]{3,2,1,0:T(8,128)S(1)}, f32[1,7,32,128]{3,2,1,0:T(8,128)S(1)}, u32[]{:S(2)}, u32[]{:S(2)}) %collective-permute-start.5) | collective-permute-done | bytes 114720 | tf_op jit(solution)/shard_map/ppermute | solution.py:19
  39.6 0.1 fusion.136
  39.7 0.8 fusion.623
  40.5 0.5 fusion.463
  41.0 1.9 %collective-permute-start.6 = (f32[1,7,32,128]{3,2,1,0:T(8,128)S(1)}, f32[1,7,32,128]{3,2,1,0:T(8,128)S(1)}, u32[]{:S(2)}, u32[]{:S(2)}) collective-permute-start(f32[1,7,32,128]{3,2,1,0:T(8,128)S(1)} %get-tuple-element.60), channel_id=1, source_target_pairs={{0,1},{1,2},{2,3},{3,4},{4,5},{5,6},{6,7},{7,8},{8,9},{9,10},{10,1... | collective-permute-start | bytes 344072 | tf_op jit(solution)/shard_map/ppermute | solution.py:18
  43.0 2.4 %collective-permute-start.7 = (f32[1,7,32,128]{3,2,1,0:T(8,128)S(1)}, f32[1,7,32,128]{3,2,1,0:T(8,128)S(1)}, u32[]{:S(2)}, u32[]{:S(2)}) collective-permute-start(f32[1,7,32,128]{3,2,1,0:T(8,128)S(1)} %get-tuple-element.61), channel_id=1, source_target_pairs={{1,0},{2,1},{3,2},{4,3},{5,4},{6,5},{7,6},{8,7},{9,8},{10,9},{11,1... | collective-permute-start | bytes 344072 | tf_op jit(solution)/shard_map/ppermute | solution.py:19
  45.4 0.3 fusion.287
  45.7 1.6 %fusion.21 = f32[2048]{0:T(1024)S(1)} fusion(f32[256,128]{1,0:T(8,128)S(1)} %bitcast.164, s32[2048]{0:T(1024)S(1)} %bitcast.178, s32[2048]{0:T(1024)S(1)} %bitcast.169), kind=kOutput, calls=%fused_computation.18 | convolution fusion | flops 806615040 | bytes 155648 | tf_op jit(solution)/shard_map/srk,skz->srz/dot_general | solution.py:129
  47.3 2.6 %collective-permute-done.7 = f32[1,7,32,128]{3,2,1,0:T(8,128)S(1)} collective-permute-done((f32[1,7,32,128]{3,2,1,0:T(8,128)S(1)}, f32[1,7,32,128]{3,2,1,0:T(8,128)S(1)}, u32[]{:S(2)}, u32[]{:S(2)}) %collective-permute-start.7) | collective-permute-done | bytes 114720 | tf_op jit(solution)/shard_map/ppermute | solution.py:19
  50.0 0.1 fusion.129
  50.1 0.8 fusion.625
  51.1 1.3 %bitcast_multiply_fusion.3 = (f32[1,8,32,128]{3,2,1,0:T(8,128)S(1)}, f32[1,8,32,128]{3,2,1,0:T(8,128)S(1)}) fusion(f32[8,32,128]{2,1,0:T(8,128)S(1)} %get-tuple-element.69, f32[2048]{0:T(1024)S(1)} %bitcast.191, s32[2048]{0:T(1024)S(1)} %bitcast.170, s32[8,32]{1,0:T(8,128)S(1)} %multiply_add_fusion, s32[2048]{0:T(1024)S(1)} %bitcast.179, ...), kind=kOutput, calls=%fused_computation.890 | convolution fusion | flops 807731200 | bytes 2253824 | tf_op jit(solution)/shard_map/srk,srz->skz/dot_general | solution.py:136
  52.4 0.3 fusion.486
  52.7 1.9 %collective-permute-start.8 = (f32[1,7,32,128]{3,2,1,0:T(8,128)S(1)}, f32[1,7,32,128]{3,2,1,0:T(8,128)S(1)}, u32[]{:S(2)}, u32[]{:S(2)}) collective-permute-start(f32[1,7,32,128]{3,2,1,0:T(8,128)S(1)} %get-tuple-element.58), channel_id=1, source_target_pairs={{0,1},{1,2},{2,3},{3,4},{4,5},{5,6},{6,7},{7,8},{8,9},{9,10},{10,1... | collective-permute-start | bytes 344072 | tf_op jit(solution)/shard_map/ppermute | solution.py:18
  54.6 2.6 %collective-permute-start.9 = (f32[1,7,32,128]{3,2,1,0:T(8,128)S(1)}, f32[1,7,32,128]{3,2,1,0:T(8,128)S(1)}, u32[]{:S(2)}, u32[]{:S(2)}) collective-permute-start(f32[1,7,32,128]{3,2,1,0:T(8,128)S(1)} %get-tuple-element.59), channel_id=1, source_target_pairs={{1,0},{2,1},{3,2},{4,3},{5,4},{6,5},{7,6},{8,7},{9,8},{10,9},{11,1... | collective-permute-start | bytes 344072 | tf_op jit(solution)/shard_map/ppermute | solution.py:19
  57.2 0.3 fusion.311
  57.5 1.6 %fusion.24 = f32[2048]{0:T(1024)S(1)} fusion(f32[256,128]{1,0:T(8,128)S(1)} %bitcast.165, s32[2048]{0:T(1024)S(1)} %bitcast.180, s32[2048]{0:T(1024)S(1)} %bitcast.171), kind=kOutput, calls=%fused_computation.19 | convolution fusion | flops 806615040 | bytes 155648 | tf_op jit(solution)/shard_map/srk,skz->srz/dot_general | solution.py:129
  59.1 0.8 fusion.638
  62.5 3.0 %collective-permute-start.10 = (f32[1]{0:T(128)}, f32[1]{0:T(128)}, u32[]{:S(2)}, u32[]{:S(2)}) collective-permute-start(f32[1]{0:T(128)} %bitcast.31), channel_id=1, source_target_pairs={{0,2},{1,3},{2,0},{3,1},{4,6},{5,7},{6,4},{7,5},{8,10},{9,11},{10,... | collective-permute-start | bytes 20 | tf_op jit(solution)/shard_map/ppermute | solution.py:36
  65.6 0.3 collective-permute-done.10
  66.6 0.1 fusion.122
  66.7 1.2 %fusion.57 = f32[1,8,32,128]{3,2,1,0:T(8,128)S(1)} fusion(s32[8,32]{1,0:T(8,128)S(1)} %multiply_add_fusion, s32[2048]{0:T(1024)S(1)} %bitcast.181, f32[2048]{0:T(1024)S(1)} %bitcast.190, s32[2048]{0:T(1024)S(1)} %bitcast.172, f32[1,8,32,128]{3,2,1,0:T(8,128)S(1)} %copy-done.6, f32[1,8,32,128]{3,2,1,0:T(8,128)S(1)} %fusion.311, ...), kind=kOutput, calls=%fused_computation.30 | convolution fusion | flops 806944768 | bytes 1860608 | tf_op jit(solution)/shard_map/srk,srz->skz/dot_general | solution.py:136
  68.0 0.3 fusion.509
  68.3 2.1 %collective-permute-start.13 = (f32[1]{0:T(128)}, f32[1]{0:T(128)}, u32[]{:S(2)}, u32[]{:S(2)}) collective-permute-start(f32[1]{0:T(128)} %add.821), channel_id=1, source_target_pairs={{0,4},{1,5},{2,6},{3,7},{4,0},{5,1},{6,2},{7,3},{8,12},{9,13},{10,... | collective-permute-start | bytes 20 | tf_op jit(solution)/shard_map/ppermute | solution.py:36
  70.4 5.1 %collective-permute-start.11 = (f32[1,7,32,128]{3,2,1,0:T(8,128)S(1)}, f32[1,7,32,128]{3,2,1,0:T(8,128)S(1)}, u32[]{:S(2)}, u32[]{:S(2)}) collective-permute-start(f32[1,7,32,128]{3,2,1,0:T(8,128)S(1)} %get-tuple-element.56), channel_id=1, source_target_pairs={{0,1},{1,2},{2,3},{3,4},{4,5},{5,6},{6,7},{7,8},{8,9},{9,10},{10,1... | collective-permute-start | bytes 344072 | tf_op jit(solution)/shard_map/ppermute | solution.py:18
  75.5 1.9 %collective-permute-start.12 = (f32[1,7,32,128]{3,2,1,0:T(8,128)S(1)}, f32[1,7,32,128]{3,2,1,0:T(8,128)S(1)}, u32[]{:S(2)}, u32[]{:S(2)}) collective-permute-start(f32[1,7,32,128]{3,2,1,0:T(8,128)S(1)} %get-tuple-element.57), channel_id=1, source_target_pairs={{1,0},{2,1},{3,2},{4,3},{5,4},{6,5},{7,6},{8,7},{9,8},{10,9},{11,1... | collective-permute-start | bytes 344072 | tf_op jit(solution)/shard_map/ppermute | solution.py:19
  77.5 0.3 fusion.335
  78.5 3.2 %collective-permute-done.12 = f32[1,7,32,128]{3,2,1,0:T(8,128)S(1)} collective-permute-done((f32[1,7,32,128]{3,2,1,0:T(8,128)S(1)}, f32[1,7,32,128]{3,2,1,0:T(8,128)S(1)}, u32[]{:S(2)}, u32[]{:S(2)}) %collective-permute-start.12) | collective-permute-done | bytes 114720 | tf_op jit(solution)/shard_map/ppermute | solution.py:19
  81.7 0.1 fusion.115
  81.8 1.2 %fusion.51 = f32[1,8,32,128]{3,2,1,0:T(8,128)S(1)} fusion(s32[8,32]{1,0:T(8,128)S(1)} %multiply_add_fusion, s32[2048]{0:T(1024)S(1)} %bitcast.182, f32[2048]{0:T(1024)S(1)} %bitcast.189, s32[2048]{0:T(1024)S(1)} %bitcast.173, f32[1,8,32,128]{3,2,1,0:T(8,128)S(1)} %get-tuple-element.79, f32[1,8,32,128]{3,2,1,0:T(8,128)S(1)} %fusion.335, ...), kind=kOutput, calls=%fused_computation.28 | convolution fusion | flops 806944768 | bytes 1860608 | tf_op jit(solution)/shard_map/srk,srz->skz/dot_general | solution.py:136
  83.1 0.3 fusion.532
  83.4 2.6 %collective-permute-start.16 = (f32[1]{0:T(128)}, f32[1]{0:T(128)}, u32[]{:S(2)}, u32[]{:S(2)}) collective-permute-start(f32[1]{0:T(128)} %add.845), channel_id=1, source_target_pairs={{0,8},{1,9},{2,10},{3,11},{4,12},{5,13},{6,14},{7,15},{8,0},{9,1},... | collective-permute-start | bytes 20 | tf_op jit(solution)/shard_map/ppermute | solution.py:36
  86.0 2.6 %collective-permute-start.14 = (f32[1,7,32,128]{3,2,1,0:T(8,128)S(1)}, f32[1,7,32,128]{3,2,1,0:T(8,128)S(1)}, u32[]{:S(2)}, u32[]{:S(2)}) collective-permute-start(f32[1,7,32,128]{3,2,1,0:T(8,128)S(1)} %get-tuple-element.54), channel_id=1, source_target_pairs={{0,1},{1,2},{2,3},{3,4},{4,5},{5,6},{6,7},{7,8},{8,9},{9,10},{10,1... | collective-permute-start | bytes 344072 | tf_op jit(solution)/shard_map/ppermute | solution.py:18
  88.7 2.6 %collective-permute-start.15 = (f32[1,7,32,128]{3,2,1,0:T(8,128)S(1)}, f32[1,7,32,128]{3,2,1,0:T(8,128)S(1)}, u32[]{:S(2)}, u32[]{:S(2)}) collective-permute-start(f32[1,7,32,128]{3,2,1,0:T(8,128)S(1)} %get-tuple-element.55), channel_id=1, source_target_pairs={{1,0},{2,1},{3,2},{4,3},{5,4},{6,5},{7,6},{8,7},{9,8},{10,9},{11,1... | collective-permute-start | bytes 344072 | tf_op jit(solution)/shard_map/ppermute | solution.py:19
  91.3 0.3 fusion.359
  92.3 2.9 %collective-permute-done.15 = f32[1,7,32,128]{3,2,1,0:T(8,128)S(1)} collective-permute-done((f32[1,7,32,128]{3,2,1,0:T(8,128)S(1)}, f32[1,7,32,128]{3,2,1,0:T(8,128)S(1)}, u32[]{:S(2)}, u32[]{:S(2)}) %collective-permute-start.15) | collective-permute-done | bytes 114720 | tf_op jit(solution)/shard_map/ppermute | solution.py:19
  95.2 0.1 fusion.108
  95.4 1.2 %fusion.45 = f32[1,8,32,128]{3,2,1,0:T(8,128)S(1)} fusion(s32[8,32]{1,0:T(8,128)S(1)} %multiply_add_fusion, s32[2048]{0:T(1024)S(1)} %bitcast.183, f32[2048]{0:T(1024)S(1)} %bitcast.188, s32[2048]{0:T(1024)S(1)} %bitcast.174, f32[1,8,32,128]{3,2,1,0:T(8,128)S(1)} %fusion.57, f32[1,8,32,128]{3,2,1,0:T(8,128)S(1)} %fusion.359, ...), kind=kOutput, calls=%fused_computation.26 | convolution fusion | flops 806944768 | bytes 1860608 | tf_op jit(solution)/shard_map/srk,srz->skz/dot_general | solution.py:136
  96.6 0.9 collective-permute-start.17
  97.5 0.8 bitcast_multiply_fusion
  (54 shorter events, 0.8 us)
Async XLA Ops:
  0.6 3.3 %copy-start = (f32[8,32,128]{2,1,0:T(8,128)S(1)}, f32[8,32,128]{2,1,0:T(8,128)}, u32[]{:S(2)}) copy-start(f32[8,32,128]{2,1,0:T(8,128)} %param.11) | copy-start | bytes 393220
  0.6 3.3 %copy-start.1 = (f32[1,8,32,128]{3,2,1,0:T(8,128)S(1)}, f32[1,8,32,128]{3,2,1,0:T(8,128)}, u32[]{:S(2)}) copy-start(f32[1,8,32,128]{3,2,1,0:T(8,128)} %param.13) | copy-start | bytes 393220
  4.0 7.3 %copy-start.9 = (f32[1,4]{1,0:T(1,128)S(1)}, f32[1,4]{1,0:T(1,128)}, u32[]{:S(2)}) copy-start(f32[1,4]{1,0:T(1,128)} %param.17) | copy-start | bytes 52
  4.0 8.0 %copy-start.8 = (s32[1,2048]{1,0:T(1,128)S(1)}, s32[1,2048]{1,0:T(1,128)}, u32[]{:S(2)}) copy-start(s32[1,2048]{1,0:T(1,128)} %param.18) | copy-start | bytes 24580
  4.1 9.2 %copy-start.5 = (f32[1,4,2048]{2,1,0:T(4,128)S(1)}, f32[1,4,2048]{2,1,0:T(4,128)}, u32[]{:S(2)}) copy-start(f32[1,4,2048]{2,1,0:T(4,128)} %param.19) | copy-start | bytes 98308
  4.1 9.5 %collective-permute-start.1 = (f32[3,7,32,128]{3,2,1,0:T(8,128)S(1)}, f32[3,7,32,128]{3,2,1,0:T(8,128)S(1)}, u32[]{:S(2)}, u32[]{:S(2)}) collective-permute-start(f32[3,7,32,128]{3,2,1,0:T(8,128)S(1)} %get-tuple-element.36), channel_id=1, source_target_pairs={{1,0},{2,1},{3,2},{4,3},{5,4},{6,5},{7,6},{8,7},{9,8},{10,9},{11,1... | collective-permute-start | bytes 1032200 | tf_op jit(solution)/shard_map/ppermute | solution.py:19
  6.1 11.3 %collective-permute-start = (f32[3,7,32,128]{3,2,1,0:T(8,128)S(1)}, f32[3,7,32,128]{3,2,1,0:T(8,128)S(1)}, u32[]{:S(2)}, u32[]{:S(2)}) collective-permute-start(f32[3,7,32,128]{3,2,1,0:T(8,128)S(1)} %get-tuple-element.37), channel_id=1, source_target_pairs={{0,1},{1,2},{2,3},{3,4},{4,5},{5,6},{6,7},{7,8},{8,9},{9,10},{10,1... | collective-permute-start | bytes 1032200 | tf_op jit(solution)/shard_map/ppermute | solution.py:18
  17.5 0.9 copy-start.4
  19.8 8.4 %collective-permute-start.2 = (f32[1,7,32,128]{3,2,1,0:T(8,128)S(1)}, f32[1,7,32,128]{3,2,1,0:T(8,128)S(1)}, u32[]{:S(2)}, u32[]{:S(2)}) collective-permute-start(f32[1,7,32,128]{3,2,1,0:T(8,128)S(1)} %get-tuple-element.66), channel_id=1, source_target_pairs={{0,1},{1,2},{2,3},{3,4},{4,5},{5,6},{6,7},{7,8},{8,9},{9,10},{10,1... | collective-permute-start | bytes 344072 | tf_op jit(solution)/shard_map/ppermute | solution.py:18
  24.2 6.1 %collective-permute-start.3 = (f32[1,7,32,128]{3,2,1,0:T(8,128)S(1)}, f32[1,7,32,128]{3,2,1,0:T(8,128)S(1)}, u32[]{:S(2)}, u32[]{:S(2)}) collective-permute-start(f32[1,7,32,128]{3,2,1,0:T(8,128)S(1)} %get-tuple-element.67), channel_id=1, source_target_pairs={{1,0},{2,1},{3,2},{4,3},{5,4},{6,5},{7,6},{8,7},{9,8},{10,9},{11,1... | collective-permute-start | bytes 344072 | tf_op jit(solution)/shard_map/ppermute | solution.py:19
  31.5 6.3 %collective-permute-start.4 = (f32[1,7,32,128]{3,2,1,0:T(8,128)S(1)}, f32[1,7,32,128]{3,2,1,0:T(8,128)S(1)}, u32[]{:S(2)}, u32[]{:S(2)}) collective-permute-start(f32[1,7,32,128]{3,2,1,0:T(8,128)S(1)} %get-tuple-element.64), channel_id=1, source_target_pairs={{0,1},{1,2},{2,3},{3,4},{4,5},{5,6},{6,7},{7,8},{8,9},{9,10},{10,1... | collective-permute-start | bytes 344072 | tf_op jit(solution)/shard_map/ppermute | solution.py:18
  33.4 6.1 %collective-permute-start.5 = (f32[1,7,32,128]{3,2,1,0:T(8,128)S(1)}, f32[1,7,32,128]{3,2,1,0:T(8,128)S(1)}, u32[]{:S(2)}, u32[]{:S(2)}) collective-permute-start(f32[1,7,32,128]{3,2,1,0:T(8,128)S(1)} %get-tuple-element.65), channel_id=1, source_target_pairs={{1,0},{2,1},{3,2},{4,3},{5,4},{6,5},{7,6},{8,7},{9,8},{10,9},{11,1... | collective-permute-start | bytes 344072 | tf_op jit(solution)/shard_map/ppermute | solution.py:19
  41.0 6.3 %collective-permute-start.6 = (f32[1,7,32,128]{3,2,1,0:T(8,128)S(1)}, f32[1,7,32,128]{3,2,1,0:T(8,128)S(1)}, u32[]{:S(2)}, u32[]{:S(2)}) collective-permute-start(f32[1,7,32,128]{3,2,1,0:T(8,128)S(1)} %get-tuple-element.60), channel_id=1, source_target_pairs={{0,1},{1,2},{2,3},{3,4},{4,5},{5,6},{6,7},{7,8},{8,9},{9,10},{10,1... | collective-permute-start | bytes 344072 | tf_op jit(solution)/shard_map/ppermute | solution.py:18
  43.0 7.0 %collective-permute-start.7 = (f32[1,7,32,128]{3,2,1,0:T(8,128)S(1)}, f32[1,7,32,128]{3,2,1,0:T(8,128)S(1)}, u32[]{:S(2)}, u32[]{:S(2)}) collective-permute-start(f32[1,7,32,128]{3,2,1,0:T(8,128)S(1)} %get-tuple-element.61), channel_id=1, source_target_pairs={{1,0},{2,1},{3,2},{4,3},{5,4},{6,5},{7,6},{8,7},{9,8},{10,9},{11,1... | collective-permute-start | bytes 344072 | tf_op jit(solution)/shard_map/ppermute | solution.py:19
  50.1 0.9 copy-start.6
  50.1 1.0 copy-start.10
  52.7 13.9 %collective-permute-start.8 = (f32[1,7,32,128]{3,2,1,0:T(8,128)S(1)}, f32[1,7,32,128]{3,2,1,0:T(8,128)S(1)}, u32[]{:S(2)}, u32[]{:S(2)}) collective-permute-start(f32[1,7,32,128]{3,2,1,0:T(8,128)S(1)} %get-tuple-element.58), channel_id=1, source_target_pairs={{0,1},{1,2},{2,3},{3,4},{4,5},{5,6},{6,7},{7,8},{8,9},{9,10},{10,1... | collective-permute-start | bytes 344072 | tf_op jit(solution)/shard_map/ppermute | solution.py:18
  54.6 12.0 %collective-permute-start.9 = (f32[1,7,32,128]{3,2,1,0:T(8,128)S(1)}, f32[1,7,32,128]{3,2,1,0:T(8,128)S(1)}, u32[]{:S(2)}, u32[]{:S(2)}) collective-permute-start(f32[1,7,32,128]{3,2,1,0:T(8,128)S(1)} %get-tuple-element.59), channel_id=1, source_target_pairs={{1,0},{2,1},{3,2},{4,3},{5,4},{6,5},{7,6},{8,7},{9,8},{10,9},{11,1... | collective-permute-start | bytes 344072 | tf_op jit(solution)/shard_map/ppermute | solution.py:19
  62.5 3.3 %collective-permute-start.10 = (f32[1]{0:T(128)}, f32[1]{0:T(128)}, u32[]{:S(2)}, u32[]{:S(2)}) collective-permute-start(f32[1]{0:T(128)} %bitcast.31), channel_id=1, source_target_pairs={{0,2},{1,3},{2,0},{3,1},{4,6},{5,7},{6,4},{7,5},{8,10},{9,11},{10,... | collective-permute-start | bytes 20 | tf_op jit(solution)/shard_map/ppermute | solution.py:36
  68.3 9.4 %collective-permute-start.13 = (f32[1]{0:T(128)}, f32[1]{0:T(128)}, u32[]{:S(2)}, u32[]{:S(2)}) collective-permute-start(f32[1]{0:T(128)} %add.821), channel_id=1, source_target_pairs={{0,4},{1,5},{2,6},{3,7},{4,0},{5,1},{6,2},{7,3},{8,12},{9,13},{10,... | collective-permute-start | bytes 20 | tf_op jit(solution)/shard_map/ppermute | solution.py:36
  70.4 8.0 %collective-permute-start.11 = (f32[1,7,32,128]{3,2,1,0:T(8,128)S(1)}, f32[1,7,32,128]{3,2,1,0:T(8,128)S(1)}, u32[]{:S(2)}, u32[]{:S(2)}) collective-permute-start(f32[1,7,32,128]{3,2,1,0:T(8,128)S(1)} %get-tuple-element.56), channel_id=1, source_target_pairs={{0,1},{1,2},{2,3},{3,4},{4,5},{5,6},{6,7},{7,8},{8,9},{9,10},{10,1... | collective-permute-start | bytes 344072 | tf_op jit(solution)/shard_map/ppermute | solution.py:18
  75.5 6.1 %collective-permute-start.12 = (f32[1,7,32,128]{3,2,1,0:T(8,128)S(1)}, f32[1,7,32,128]{3,2,1,0:T(8,128)S(1)}, u32[]{:S(2)}, u32[]{:S(2)}) collective-permute-start(f32[1,7,32,128]{3,2,1,0:T(8,128)S(1)} %get-tuple-element.57), channel_id=1, source_target_pairs={{1,0},{2,1},{3,2},{4,3},{5,4},{6,5},{7,6},{8,7},{9,8},{10,9},{11,1... | collective-permute-start | bytes 344072 | tf_op jit(solution)/shard_map/ppermute | solution.py:19
  83.0 14.5 %copy-start.2 = (f32[1,8,32,128]{3,2,1,0:T(8,128)}, f32[1,8,32,128]{3,2,1,0:T(8,128)S(1)}, u32[]{:S(2)}) copy-start(f32[1,8,32,128]{3,2,1,0:T(8,128)S(1)} %fusion.51) | copy-start | bytes 393220
  83.4 8.2 %collective-permute-start.16 = (f32[1]{0:T(128)}, f32[1]{0:T(128)}, u32[]{:S(2)}, u32[]{:S(2)}) collective-permute-start(f32[1]{0:T(128)} %add.845), channel_id=1, source_target_pairs={{0,8},{1,9},{2,10},{3,11},{4,12},{5,13},{6,14},{7,15},{8,0},{9,1},... | collective-permute-start | bytes 20 | tf_op jit(solution)/shard_map/ppermute | solution.py:36
  86.0 6.3 %collective-permute-start.14 = (f32[1,7,32,128]{3,2,1,0:T(8,128)S(1)}, f32[1,7,32,128]{3,2,1,0:T(8,128)S(1)}, u32[]{:S(2)}, u32[]{:S(2)}) collective-permute-start(f32[1,7,32,128]{3,2,1,0:T(8,128)S(1)} %get-tuple-element.54), channel_id=1, source_target_pairs={{0,1},{1,2},{2,3},{3,4},{4,5},{5,6},{6,7},{7,8},{8,9},{9,10},{10,1... | collective-permute-start | bytes 344072 | tf_op jit(solution)/shard_map/ppermute | solution.py:18
  88.7 6.5 %collective-permute-start.15 = (f32[1,7,32,128]{3,2,1,0:T(8,128)S(1)}, f32[1,7,32,128]{3,2,1,0:T(8,128)S(1)}, u32[]{:S(2)}, u32[]{:S(2)}) collective-permute-start(f32[1,7,32,128]{3,2,1,0:T(8,128)S(1)} %get-tuple-element.55), channel_id=1, source_target_pairs={{1,0},{2,1},{3,2},{4,3},{5,4},{6,5},{7,6},{8,7},{9,8},{10,9},{11,1... | collective-permute-start | bytes 344072 | tf_op jit(solution)/shard_map/ppermute | solution.py:19
  95.4 2.2 %copy-start.3 = (f32[8,32,128]{2,1,0:T(8,128)S(1)}, f32[8,32,128]{2,1,0:T(8,128)}, u32[]{:S(2)}) copy-start(f32[8,32,128]{2,1,0:T(8,128)} %param.10) | copy-start | bytes 393220
  96.6 2.4 %copy-start.7 = (f32[1,8,32,128]{3,2,1,0:T(8,128)}, f32[1,8,32,128]{3,2,1,0:T(8,128)S(1)}, u32[]{:S(2)}) copy-start(f32[1,8,32,128]{3,2,1,0:T(8,128)S(1)} %fusion.45) | copy-start | bytes 393220
  96.6 1.7 %collective-permute-start.17 = (f32[1]{0:T(128)}, f32[1]{0:T(128)}, u32[]{:S(2)}, u32[]{:S(2)}) collective-permute-start(f32[1]{0:T(128)} %add.869), channel_id=1, source_target_pairs={{0,1},{1,0},{2,3},{3,2},{4,5},{5,4},{6,7},{7,6},{8,9},{9,8},{10,11... | collective-permute-start | bytes 20 | tf_op jit(solution)/shard_map/ppermute | solution.py:36

commit v12 on v8

--- a/solution.py
+++ b/solution.py
@@ -145,7 +145,8 @@
         sampled = sample(following)
         resids.append(jnp.where(receiver_owned, sampled - observed[:, step, :], 0.0))
         before, current = (current, following)
-    misfit = 0.5 * sum((jnp.sum(item * item, axis=1) for item in resids))
+    stacked = jnp.stack(resids, axis=1)
+    misfit = 0.5 * jnp.sum(stacked * stacked, axis=(1, 2))
     distances = butterfly_distances("mp")
     mu_near, mu_far = (adjoint_next, adjoint_after)
     gradient = jnp.zeros(shape, jnp.float32)

time: 99.5 us -> 97.5 us (0.980)
  between operations: 8.36 us -> 6.42 us
  transfers between devices with their start and end apart: 18 -> 18, of which waited for: 9 -> 9; matrix products, arithmetic and copies ran while one was open for 9% -> 10% of each run, Pallas kernels for 0% -> 0%
where the time goes in v12:
time: 97.5 us; the launch traced here: 96.2 us
  starting transfers between devices  43.8 us (45%)
  waiting for transfers between devices  19.3 us (20%)
  other arithmetic  12.9 us (13%)
  matrix products  11.4 us (12%)
  between operations  6.42 us (7%)
  local copies, waits for them, and re-layouts  2.38 us (2%)
    ppermute x7, starting transfers between devices, extended(): before = lax.ppermute(last, 'mp', up)  19.9 us
    ppermute x7, waiting for transfers between devices, extended(): after = lax.ppermute(first, 'mp', down)  15.2 us
    ppermute x7, starting transfers between devices, extended(): after = lax.ppermute(first, 'mp', down)  15.1 us
    ppermute x4, starting transfers between devices, butterfly_round(): return values + lax.ppermute(values, axis, pairs)  8.77 us
    dot_general x4, matrix products, sample(): jnp.einsum('srk,skz->srz', row_pick, field.reshape(shots, rows, cz), prec...  6.43 us
    dot_general x4, matrix products, injected(): jnp.einsum('srk,srz->skz', row_pick, spread, precision=lax.Precision.HIGH...  4.93 us
    ppermute x7, waiting for transfers between devices, extended(): before = lax.ppermute(last, 'mp', up)  3.87 us
    add x4, other arithmetic, local(): following = following + jnp.where(source_hit, amount, 0.0)  3.22 us
  transfers between devices with their start and end apart: 18, of which 9 were waited for; matrix products, arithmetic and copies ran while one was open for 10% of the time, Pallas kernels for 0%

profile of v12, /device:TPU:1, one launch (start us, length us, event | category | flops | bytes accessed | tf_op | source)
XLA Modules:
  0.0 96.2 jit_solution(13770907570243937330)
XLA Ops:
  0.6 1.1 %bitcast_multiply_fusion.8 = (f32[1,8,32,128]{3,2,1,0:T(8,128)S(1)}, f32[8,32,128]{2,1,0:T(8,128)S(1)}) fusion(f32[1,8,32,128]{3,2,1,0:T(8,128)} %param.14, f32[8,32,128]{2,1,0:T(8,128)} %param.11, f32[8,32,128]{2,1,0:T(8,128)} %param.10), kind=kLoop, calls=%fused_computation.881 | loop fusion | flops 98304 | bytes 655360 | tf_op jit(solution)/shard_map/mul | solution.py:99
  1.7 1.0 %pad_maximum_fusion.1 = f32[3,8,32,128]{3,2,1,0:T(8,128)S(1)} fusion(f32[1,8,32,128]{3,2,1,0:T(8,128)S(1)} %get-tuple-element.32, f32[1,8,32,128]{3,2,1,0:T(8,128)} %param.13, f32[1,8,32,128]{3,2,1,0:T(8,128)} %bitcast.123), kind=kLoop, calls=%fused_computation.168 | loop fusion | flops 196608 | bytes 786432 | tf_op jit(solution)/shard_map/concatenate | solution.py:100
  2.9 2.0 %collective-permute-start.1 = (f32[3,7,32,128]{3,2,1,0:T(8,128)S(1)}, f32[3,7,32,128]{3,2,1,0:T(8,128)S(1)}, u32[]{:S(2)}, u32[]{:S(2)}) collective-permute-start(f32[3,7,32,128]{3,2,1,0:T(8,128)S(1)} %get-tuple-element.34), channel_id=1, source_target_pairs={{1,0},{2,1},{3,2},{4,3},{5,4},{6,5},{7,6},{8,7},{9,8},{10,9},{11,1... | collective-permute-start | bytes 1032200 | tf_op jit(solution)/shard_map/ppermute | solution.py:19
  4.8 4.5 %collective-permute-start = (f32[3,7,32,128]{3,2,1,0:T(8,128)S(1)}, f32[3,7,32,128]{3,2,1,0:T(8,128)S(1)}, u32[]{:S(2)}, u32[]{:S(2)}) collective-permute-start(f32[3,7,32,128]{3,2,1,0:T(8,128)S(1)} %get-tuple-element.35), channel_id=1, source_target_pairs={{0,1},{1,2},{2,3},{3,4},{4,5},{5,6},{6,7},{7,8},{8,9},{9,10},{10,1... | collective-permute-start | bytes 1032200 | tf_op jit(solution)/shard_map/ppermute | solution.py:18
  10.0 0.6 fusion.616
  10.7 0.5 fusion.336
  11.3 1.0 %collective-permute-done.1 = f32[3,7,32,128]{3,2,1,0:T(8,128)S(1)} collective-permute-done((f32[3,7,32,128]{3,2,1,0:T(8,128)S(1)}, f32[3,7,32,128]{3,2,1,0:T(8,128)S(1)}, u32[]{:S(2)}, u32[]{:S(2)}) %collective-permute-start.1) | collective-permute-done | bytes 344096 | tf_op jit(solution)/shard_map/ppermute | solution.py:19
  12.3 3.9 %collective-permute-done = f32[3,7,32,128]{3,2,1,0:T(8,128)S(1)} collective-permute-done((f32[3,7,32,128]{3,2,1,0:T(8,128)S(1)}, f32[3,7,32,128]{3,2,1,0:T(8,128)S(1)}, u32[]{:S(2)}, u32[]{:S(2)}) %collective-permute-start) | collective-permute-done | bytes 344096 | tf_op jit(solution)/shard_map/ppermute | solution.py:18
  16.3 0.1 fusion.114
  16.4 0.8 copy-done.6
  17.2 1.0 %fusion.587 = (f32[1,8,32,128]{3,2,1,0:T(8,128)S(1)}, f32[1,8,32,128]{3,2,1,0:T(8,128)S(1)}) fusion(f32[8,32,128]{2,1,0:T(8,128)S(1)} %get-tuple-element.33, f32[1,8,32,128]{3,2,1,0:T(8,128)S(1)} %copy-done.6, f32[1,8,32,128]{3,2,1,0:T(8,128)S(1)} %copy-done.1, f32[]{:T(128)} %bitcast.7, s32[]{:T(128)} %bitcast.6, s32[32]{0:T(128)S(1)} %iota_multiply_fusion, ...), kind=kLoop, calls=%fused_computation.883 | loop fusion | flops 1441792 | bytes 1966248 | tf_op jit(solution)/shard_map/add | solution.py:144
  18.2 0.3 fusion.382
  18.5 4.4 %collective-permute-start.2 = (f32[1,7,32,128]{3,2,1,0:T(8,128)S(1)}, f32[1,7,32,128]{3,2,1,0:T(8,128)S(1)}, u32[]{:S(2)}, u32[]{:S(2)}) collective-permute-start(f32[1,7,32,128]{3,2,1,0:T(8,128)S(1)} %get-tuple-element.64), channel_id=1, source_target_pairs={{0,1},{1,2},{2,3},{3,4},{4,5},{5,6},{6,7},{7,8},{8,9},{9,10},{10,1... | collective-permute-start | bytes 344072 | tf_op jit(solution)/shard_map/ppermute | solution.py:18
  22.9 1.9 %collective-permute-start.3 = (f32[1,7,32,128]{3,2,1,0:T(8,128)S(1)}, f32[1,7,32,128]{3,2,1,0:T(8,128)S(1)}, u32[]{:S(2)}, u32[]{:S(2)}) collective-permute-start(f32[1,7,32,128]{3,2,1,0:T(8,128)S(1)} %get-tuple-element.65), channel_id=1, source_target_pairs={{1,0},{2,1},{3,2},{4,3},{5,4},{6,5},{7,6},{8,7},{9,8},{10,9},{11,1... | collective-permute-start | bytes 344072 | tf_op jit(solution)/shard_map/ppermute | solution.py:19
  24.8 0.3 fusion.204
  25.1 0.1 fusion.122
  25.2 1.6 %fusion.16 = f32[2048]{0:T(1024)S(1)} fusion(f32[256,128]{1,0:T(8,128)S(1)} %bitcast.127, s32[2048]{0:T(1024)S(1)} %bitcast.147, s32[2048]{0:T(1024)S(1)} %bitcast.139), kind=kOutput, calls=%fused_computation.15 | convolution fusion | flops 806615040 | bytes 155648 | tf_op jit(solution)/shard_map/srk,skz->srz/dot_general | solution.py:126
  26.9 2.1 %collective-permute-done.3 = f32[1,7,32,128]{3,2,1,0:T(8,128)S(1)} collective-permute-done((f32[1,7,32,128]{3,2,1,0:T(8,128)S(1)}, f32[1,7,32,128]{3,2,1,0:T(8,128)S(1)}, u32[]{:S(2)}, u32[]{:S(2)}) %collective-permute-start.3) | collective-permute-done | bytes 114720 | tf_op jit(solution)/shard_map/ppermute | solution.py:19
  29.0 0.1 fusion.107
  29.1 0.8 fusion.589
  29.9 0.3 fusion.405
  30.2 1.9 %collective-permute-start.4 = (f32[1,7,32,128]{3,2,1,0:T(8,128)S(1)}, f32[1,7,32,128]{3,2,1,0:T(8,128)S(1)}, u32[]{:S(2)}, u32[]{:S(2)}) collective-permute-start(f32[1,7,32,128]{3,2,1,0:T(8,128)S(1)} %get-tuple-element.62), channel_id=1, source_target_pairs={{0,1},{1,2},{2,3},{3,4},{4,5},{5,6},{6,7},{7,8},{8,9},{9,10},{10,1... | collective-permute-start | bytes 344072 | tf_op jit(solution)/shard_map/ppermute | solution.py:18
  32.2 2.4 %collective-permute-start.5 = (f32[1,7,32,128]{3,2,1,0:T(8,128)S(1)}, f32[1,7,32,128]{3,2,1,0:T(8,128)S(1)}, u32[]{:S(2)}, u32[]{:S(2)}) collective-permute-start(f32[1,7,32,128]{3,2,1,0:T(8,128)S(1)} %get-tuple-element.63), channel_id=1, source_target_pairs={{1,0},{2,1},{3,2},{4,3},{5,4},{6,5},{7,6},{8,7},{9,8},{10,9},{11,1... | collective-permute-start | bytes 344072 | tf_op jit(solution)/shard_map/ppermute | solution.py:19
  34.6 0.3 fusion.228
  34.9 1.6 %fusion.19 = f32[2048]{0:T(1024)S(1)} fusion(f32[256,128]{1,0:T(8,128)S(1)} %bitcast.128, s32[2048]{0:T(1024)S(1)} %bitcast.148, s32[2048]{0:T(1024)S(1)} %bitcast.140), kind=kOutput, calls=%fused_computation.16 | convolution fusion | flops 806615040 | bytes 155648 | tf_op jit(solution)/shard_map/srk,skz->srz/dot_general | solution.py:126
  36.5 1.8 %collective-permute-done.5 = f32[1,7,32,128]{3,2,1,0:T(8,128)S(1)} collective-permute-done((f32[1,7,32,128]{3,2,1,0:T(8,128)S(1)}, f32[1,7,32,128]{3,2,1,0:T(8,128)S(1)}, u32[]{:S(2)}, u32[]{:S(2)}) %collective-permute-start.5) | collective-permute-done | bytes 114720 | tf_op jit(solution)/shard_map/ppermute | solution.py:19
  38.4 0.7 fusion.591
  39.2 0.3 fusion.428
  39.5 1.9 %collective-permute-start.6 = (f32[1,7,32,128]{3,2,1,0:T(8,128)S(1)}, f32[1,7,32,128]{3,2,1,0:T(8,128)S(1)}, u32[]{:S(2)}, u32[]{:S(2)}) collective-permute-start(f32[1,7,32,128]{3,2,1,0:T(8,128)S(1)} %get-tuple-element.60), channel_id=1, source_target_pairs={{0,1},{1,2},{2,3},{3,4},{4,5},{5,6},{6,7},{7,8},{8,9},{9,10},{10,1... | collective-permute-start | bytes 344072 | tf_op jit(solution)/shard_map/ppermute | solution.py:18
  41.4 2.6 %collective-permute-start.7 = (f32[1,7,32,128]{3,2,1,0:T(8,128)S(1)}, f32[1,7,32,128]{3,2,1,0:T(8,128)S(1)}, u32[]{:S(2)}, u32[]{:S(2)}) collective-permute-start(f32[1,7,32,128]{3,2,1,0:T(8,128)S(1)} %get-tuple-element.61), channel_id=1, source_target_pairs={{1,0},{2,1},{3,2},{4,3},{5,4},{6,5},{7,6},{8,7},{9,8},{10,9},{11,1... | collective-permute-start | bytes 344072 | tf_op jit(solution)/shard_map/ppermute | solution.py:19
  44.0 0.3 fusion.252
  44.4 1.6 %fusion.22 = f32[2048]{0:T(1024)S(1)} fusion(f32[256,128]{1,0:T(8,128)S(1)} %bitcast.129, s32[2048]{0:T(1024)S(1)} %bitcast.149, s32[2048]{0:T(1024)S(1)} %bitcast.141), kind=kOutput, calls=%fused_computation.17 | convolution fusion | flops 806615040 | bytes 155648 | tf_op jit(solution)/shard_map/srk,skz->srz/dot_general | solution.py:126
  46.0 2.4 %collective-permute-done.7 = f32[1,7,32,128]{3,2,1,0:T(8,128)S(1)} collective-permute-done((f32[1,7,32,128]{3,2,1,0:T(8,128)S(1)}, f32[1,7,32,128]{3,2,1,0:T(8,128)S(1)}, u32[]{:S(2)}, u32[]{:S(2)}) %collective-permute-start.7) | collective-permute-done | bytes 114720 | tf_op jit(solution)/shard_map/ppermute | solution.py:19
  48.4 0.1 fusion.93
  48.6 0.7 fusion.593
  49.3 1.6 %fusion.13 = f32[2048]{0:T(1024)S(1)} fusion(f32[256,128]{1,0:T(8,128)S(1)} %bitcast.130, s32[2048]{0:T(1024)S(1)} %bitcast.150, s32[2048]{0:T(1024)S(1)} %bitcast.142), kind=kOutput, calls=%fused_computation.14 | convolution fusion | flops 806615040 | bytes 155648 | tf_op jit(solution)/shard_map/srk,skz->srz/dot_general | solution.py:126
  51.0 1.2 %fusion.25 = f32[1,8,32,128]{3,2,1,0:T(8,128)S(1)} fusion(s32[8,32]{1,0:T(8,128)S(1)} %multiply_add_fusion, s32[2048]{0:T(1024)S(1)} %bitcast.151, f32[2048]{0:T(1024)S(1)} %bitcast.137, s32[2048]{0:T(1024)S(1)} %bitcast.143), kind=kOutput, calls=%fused_computation.18 | convolution fusion | flops 806354944 | bytes 156672 | tf_op jit(solution)/shard_map/srk,srz->skz/dot_general | solution.py:133
  52.3 0.6 fusion.594
  53.6 0.3 fusion.155
  53.9 0.3 fusion.451
  54.3 1.2 %fusion.31 = f32[1,8,32,128]{3,2,1,0:T(8,128)S(1)} fusion(s32[8,32]{1,0:T(8,128)S(1)} %multiply_add_fusion, s32[2048]{0:T(1024)S(1)} %bitcast.152, f32[2048]{0:T(1024)S(1)} %bitcast.136, s32[2048]{0:T(1024)S(1)} %bitcast.144), kind=kOutput, calls=%fused_computation.20 | convolution fusion | flops 806354944 | bytes 156672 | tf_op jit(solution)/shard_map/srk,srz->skz/dot_general | solution.py:133
  55.5 1.2 %fusion.28 = f32[1,8,32,128]{3,2,1,0:T(8,128)S(1)} fusion(s32[8,32]{1,0:T(8,128)S(1)} %multiply_add_fusion, s32[2048]{0:T(1024)S(1)} %bitcast.153, f32[2048]{0:T(1024)S(1)} %bitcast.134, s32[2048]{0:T(1024)S(1)} %bitcast.145), kind=kOutput, calls=%fused_computation.19 | convolution fusion | flops 806354944 | bytes 156672 | tf_op jit(solution)/shard_map/srk,srz->skz/dot_general | solution.py:133
  56.7 3.0 %collective-permute-start.10 = (f32[1]{0:T(128)}, f32[1]{0:T(128)}, u32[]{:S(2)}, u32[]{:S(2)}) collective-permute-start(f32[1]{0:T(128)} %bitcast.30), channel_id=1, source_target_pairs={{0,2},{1,3},{2,0},{3,1},{4,6},{5,7},{6,4},{7,5},{8,10},{9,11},{10,... | collective-permute-start | bytes 20 | tf_op jit(solution)/shard_map/ppermute | solution.py:36
  59.8 1.9 %collective-permute-start.8 = (f32[1,7,32,128]{3,2,1,0:T(8,128)S(1)}, f32[1,7,32,128]{3,2,1,0:T(8,128)S(1)}, u32[]{:S(2)}, u32[]{:S(2)}) collective-permute-start(f32[1,7,32,128]{3,2,1,0:T(8,128)S(1)} %get-tuple-element.56), channel_id=1, source_target_pairs={{0,1},{1,2},{2,3},{3,4},{4,5},{5,6},{6,7},{7,8},{8,9},{9,10},{10,1... | collective-permute-start | bytes 344072 | tf_op jit(solution)/shard_map/ppermute | solution.py:18
  61.7 2.4 %collective-permute-start.9 = (f32[1,7,32,128]{3,2,1,0:T(8,128)S(1)}, f32[1,7,32,128]{3,2,1,0:T(8,128)S(1)}, u32[]{:S(2)}, u32[]{:S(2)}) collective-permute-start(f32[1,7,32,128]{3,2,1,0:T(8,128)S(1)} %get-tuple-element.57), channel_id=1, source_target_pairs={{1,0},{2,1},{3,2},{4,3},{5,4},{6,5},{7,6},{8,7},{9,8},{10,9},{11,1... | collective-permute-start | bytes 344072 | tf_op jit(solution)/shard_map/ppermute | solution.py:19
  64.1 0.3 fusion.276
  64.4 1.2 %fusion.34 = f32[1,8,32,128]{3,2,1,0:T(8,128)S(1)} fusion(s32[8,32]{1,0:T(8,128)S(1)} %multiply_add_fusion, s32[2048]{0:T(1024)S(1)} %bitcast.154, f32[2048]{0:T(1024)S(1)} %bitcast.132, s32[2048]{0:T(1024)S(1)} %bitcast.146), kind=kOutput, calls=%fused_computation.21 | convolution fusion | flops 806354944 | bytes 156672 | tf_op jit(solution)/shard_map/srk,srz->skz/dot_general | solution.py:133
  66.4 1.5 %collective-permute-done.9 = f32[1,7,32,128]{3,2,1,0:T(8,128)S(1)} collective-permute-done((f32[1,7,32,128]{3,2,1,0:T(8,128)S(1)}, f32[1,7,32,128]{3,2,1,0:T(8,128)S(1)}, u32[]{:S(2)}, u32[]{:S(2)}) %collective-permute-start.9) | collective-permute-done | bytes 114720 | tf_op jit(solution)/shard_map/ppermute | solution.py:19
  68.1 0.3 fusion.474
  68.4 2.1 %collective-permute-start.13 = (f32[1]{0:T(128)}, f32[1]{0:T(128)}, u32[]{:S(2)}, u32[]{:S(2)}) collective-permute-start(f32[1]{0:T(128)} %add.806), channel_id=1, source_target_pairs={{0,4},{1,5},{2,6},{3,7},{4,0},{5,1},{6,2},{7,3},{8,12},{9,13},{10,... | collective-permute-start | bytes 20 | tf_op jit(solution)/shard_map/ppermute | solution.py:36
  70.5 2.6 %collective-permute-start.11 = (f32[1,7,32,128]{3,2,1,0:T(8,128)S(1)}, f32[1,7,32,128]{3,2,1,0:T(8,128)S(1)}, u32[]{:S(2)}, u32[]{:S(2)}) collective-permute-start(f32[1,7,32,128]{3,2,1,0:T(8,128)S(1)} %get-tuple-element.54), channel_id=1, source_target_pairs={{0,1},{1,2},{2,3},{3,4},{4,5},{5,6},{6,7},{7,8},{8,9},{9,10},{10,1... | collective-permute-start | bytes 344072 | tf_op jit(solution)/shard_map/ppermute | solution.py:18
  73.1 1.9 %collective-permute-start.12 = (f32[1,7,32,128]{3,2,1,0:T(8,128)S(1)}, f32[1,7,32,128]{3,2,1,0:T(8,128)S(1)}, u32[]{:S(2)}, u32[]{:S(2)}) collective-permute-start(f32[1,7,32,128]{3,2,1,0:T(8,128)S(1)} %get-tuple-element.55), channel_id=1, source_target_pairs={{1,0},{2,1},{3,2},{4,3},{5,4},{6,5},{7,6},{8,7},{9,8},{10,9},{11,1... | collective-permute-start | bytes 344072 | tf_op jit(solution)/shard_map/ppermute | solution.py:19
  75.1 0.3 fusion.300
  76.1 3.2 %collective-permute-done.12 = f32[1,7,32,128]{3,2,1,0:T(8,128)S(1)} collective-permute-done((f32[1,7,32,128]{3,2,1,0:T(8,128)S(1)}, f32[1,7,32,128]{3,2,1,0:T(8,128)S(1)}, u32[]{:S(2)}, u32[]{:S(2)}) %collective-permute-start.12) | collective-permute-done | bytes 114720 | tf_op jit(solution)/shard_map/ppermute | solution.py:19
  79.5 0.3 fusion.497
  79.8 2.8 %collective-permute-start.16 = (f32[1]{0:T(128)}, f32[1]{0:T(128)}, u32[]{:S(2)}, u32[]{:S(2)}) collective-permute-start(f32[1]{0:T(128)} %add.830), channel_id=1, source_target_pairs={{0,8},{1,9},{2,10},{3,11},{4,12},{5,13},{6,14},{7,15},{8,0},{9,1},... | collective-permute-start | bytes 20 | tf_op jit(solution)/shard_map/ppermute | solution.py:36
  82.7 2.6 %collective-permute-start.14 = (f32[1,7,32,128]{3,2,1,0:T(8,128)S(1)}, f32[1,7,32,128]{3,2,1,0:T(8,128)S(1)}, u32[]{:S(2)}, u32[]{:S(2)}) collective-permute-start(f32[1,7,32,128]{3,2,1,0:T(8,128)S(1)} %get-tuple-element.52), channel_id=1, source_target_pairs={{0,1},{1,2},{2,3},{3,4},{4,5},{5,6},{6,7},{7,8},{8,9},{9,10},{10,1... | collective-permute-start | bytes 344072 | tf_op jit(solution)/shard_map/ppermute | solution.py:18
  85.3 1.9 %collective-permute-start.15 = (f32[1,7,32,128]{3,2,1,0:T(8,128)S(1)}, f32[1,7,32,128]{3,2,1,0:T(8,128)S(1)}, u32[]{:S(2)}, u32[]{:S(2)}) collective-permute-start(f32[1,7,32,128]{3,2,1,0:T(8,128)S(1)} %get-tuple-element.53), channel_id=1, source_target_pairs={{1,0},{2,1},{3,2},{4,3},{5,4},{6,5},{7,6},{8,7},{9,8},{10,9},{11,1... | collective-permute-start | bytes 344072 | tf_op jit(solution)/shard_map/ppermute | solution.py:19
  87.3 0.3 fusion.324
  88.3 3.2 %collective-permute-done.15 = f32[1,7,32,128]{3,2,1,0:T(8,128)S(1)} collective-permute-done((f32[1,7,32,128]{3,2,1,0:T(8,128)S(1)}, f32[1,7,32,128]{3,2,1,0:T(8,128)S(1)}, u32[]{:S(2)}, u32[]{:S(2)}) %collective-permute-start.15) | collective-permute-done | bytes 114720 | tf_op jit(solution)/shard_map/ppermute | solution.py:19
  91.6 0.8 copy-done.4
  92.4 0.9 bitcast_multiply_fusion
  93.3 0.8 collective-permute-start.17
  94.1 0.3 collective-permute-done.17
  (56 shorter events, 1.3 us)
Async XLA Ops:
  1.7 8.3 %copy-start.9 = (f32[1,4]{1,0:T(1,128)S(1)}, f32[1,4]{1,0:T(1,128)}, u32[]{:S(2)}) copy-start(f32[1,4]{1,0:T(1,128)} %param.17) | copy-start | bytes 52
  1.7 8.9 %copy-start.7 = (s32[1,2048]{1,0:T(1,128)S(1)}, s32[1,2048]{1,0:T(1,128)}, u32[]{:S(2)}) copy-start(s32[1,2048]{1,0:T(1,128)} %param.18) | copy-start | bytes 24580
  1.7 9.0 %copy-start = (f32[8,32,128]{2,1,0:T(8,128)S(1)}, f32[8,32,128]{2,1,0:T(8,128)}, u32[]{:S(2)}) copy-start(f32[8,32,128]{2,1,0:T(8,128)} %param.11) | copy-start | bytes 393220
  1.7 9.0 %copy-start.1 = (f32[1,8,32,128]{3,2,1,0:T(8,128)S(1)}, f32[1,8,32,128]{3,2,1,0:T(8,128)}, u32[]{:S(2)}) copy-start(f32[1,8,32,128]{3,2,1,0:T(8,128)} %param.13) | copy-start | bytes 393220
  2.9 9.5 %collective-permute-start.1 = (f32[3,7,32,128]{3,2,1,0:T(8,128)S(1)}, f32[3,7,32,128]{3,2,1,0:T(8,128)S(1)}, u32[]{:S(2)}, u32[]{:S(2)}) collective-permute-start(f32[3,7,32,128]{3,2,1,0:T(8,128)S(1)} %get-tuple-element.34), channel_id=1, source_target_pairs={{1,0},{2,1},{3,2},{4,3},{5,4},{6,5},{7,6},{8,7},{9,8},{10,9},{11,1... | collective-permute-start | bytes 1032200 | tf_op jit(solution)/shard_map/ppermute | solution.py:19
  4.8 11.3 %collective-permute-start = (f32[3,7,32,128]{3,2,1,0:T(8,128)S(1)}, f32[3,7,32,128]{3,2,1,0:T(8,128)S(1)}, u32[]{:S(2)}, u32[]{:S(2)}) collective-permute-start(f32[3,7,32,128]{3,2,1,0:T(8,128)S(1)} %get-tuple-element.35), channel_id=1, source_target_pairs={{0,1},{1,2},{2,3},{3,4},{4,5},{5,6},{6,7},{7,8},{8,9},{9,10},{10,1... | collective-permute-start | bytes 1032200 | tf_op jit(solution)/shard_map/ppermute | solution.py:18
  16.3 0.9 copy-start.6
  18.5 8.4 %collective-permute-start.2 = (f32[1,7,32,128]{3,2,1,0:T(8,128)S(1)}, f32[1,7,32,128]{3,2,1,0:T(8,128)S(1)}, u32[]{:S(2)}, u32[]{:S(2)}) collective-permute-start(f32[1,7,32,128]{3,2,1,0:T(8,128)S(1)} %get-tuple-element.64), channel_id=1, source_target_pairs={{0,1},{1,2},{2,3},{3,4},{4,5},{5,6},{6,7},{7,8},{8,9},{9,10},{10,1... | collective-permute-start | bytes 344072 | tf_op jit(solution)/shard_map/ppermute | solution.py:18
  22.9 6.1 %collective-permute-start.3 = (f32[1,7,32,128]{3,2,1,0:T(8,128)S(1)}, f32[1,7,32,128]{3,2,1,0:T(8,128)S(1)}, u32[]{:S(2)}, u32[]{:S(2)}) collective-permute-start(f32[1,7,32,128]{3,2,1,0:T(8,128)S(1)} %get-tuple-element.65), channel_id=1, source_target_pairs={{1,0},{2,1},{3,2},{4,3},{5,4},{6,5},{7,6},{8,7},{9,8},{10,9},{11,1... | collective-permute-start | bytes 344072 | tf_op jit(solution)/shard_map/ppermute | solution.py:19
  30.2 6.3 %collective-permute-start.4 = (f32[1,7,32,128]{3,2,1,0:T(8,128)S(1)}, f32[1,7,32,128]{3,2,1,0:T(8,128)S(1)}, u32[]{:S(2)}, u32[]{:S(2)}) collective-permute-start(f32[1,7,32,128]{3,2,1,0:T(8,128)S(1)} %get-tuple-element.62), channel_id=1, source_target_pairs={{0,1},{1,2},{2,3},{3,4},{4,5},{5,6},{6,7},{7,8},{8,9},{9,10},{10,1... | collective-permute-start | bytes 344072 | tf_op jit(solution)/shard_map/ppermute | solution.py:18
  32.2 6.1 %collective-permute-start.5 = (f32[1,7,32,128]{3,2,1,0:T(8,128)S(1)}, f32[1,7,32,128]{3,2,1,0:T(8,128)S(1)}, u32[]{:S(2)}, u32[]{:S(2)}) collective-permute-start(f32[1,7,32,128]{3,2,1,0:T(8,128)S(1)} %get-tuple-element.63), channel_id=1, source_target_pairs={{1,0},{2,1},{3,2},{4,3},{5,4},{6,5},{7,6},{8,7},{9,8},{10,9},{11,1... | collective-permute-start | bytes 344072 | tf_op jit(solution)/shard_map/ppermute | solution.py:19
  39.5 6.5 %collective-permute-start.6 = (f32[1,7,32,128]{3,2,1,0:T(8,128)S(1)}, f32[1,7,32,128]{3,2,1,0:T(8,128)S(1)}, u32[]{:S(2)}, u32[]{:S(2)}) collective-permute-start(f32[1,7,32,128]{3,2,1,0:T(8,128)S(1)} %get-tuple-element.60), channel_id=1, source_target_pairs={{0,1},{1,2},{2,3},{3,4},{4,5},{5,6},{6,7},{7,8},{8,9},{9,10},{10,1... | collective-permute-start | bytes 344072 | tf_op jit(solution)/shard_map/ppermute | solution.py:18
  41.4 7.0 %collective-permute-start.7 = (f32[1,7,32,128]{3,2,1,0:T(8,128)S(1)}, f32[1,7,32,128]{3,2,1,0:T(8,128)S(1)}, u32[]{:S(2)}, u32[]{:S(2)}) collective-permute-start(f32[1,7,32,128]{3,2,1,0:T(8,128)S(1)} %get-tuple-element.61), channel_id=1, source_target_pairs={{1,0},{2,1},{3,2},{4,3},{5,4},{6,5},{7,6},{8,7},{9,8},{10,9},{11,1... | collective-permute-start | bytes 344072 | tf_op jit(solution)/shard_map/ppermute | solution.py:19
  49.3 1.7 %copy-start.8 = (f32[1,4,2048]{2,1,0:T(4,128)S(1)}, f32[1,4,2048]{2,1,0:T(4,128)}, u32[]{:S(2)}) copy-start(f32[1,4,2048]{2,1,0:T(4,128)} %param.19) | copy-start | bytes 98308
  50.9 2.6 %copy-start.2 = (f32[1,8,32,128]{3,2,1,0:T(8,128)S(1)}, f32[1,8,32,128]{3,2,1,0:T(8,128)}, u32[]{:S(2)}) copy-start(f32[1,8,32,128]{3,2,1,0:T(8,128)} %param.14) | copy-start | bytes 393220
  50.9 2.6 %copy-start.5 = (f32[1,8,32,128]{3,2,1,0:T(8,128)S(1)}, f32[1,8,32,128]{3,2,1,0:T(8,128)}, u32[]{:S(2)}) copy-start(f32[1,8,32,128]{3,2,1,0:T(8,128)} %param.15) | copy-start | bytes 393220
  56.7 8.9 %collective-permute-start.10 = (f32[1]{0:T(128)}, f32[1]{0:T(128)}, u32[]{:S(2)}, u32[]{:S(2)}) collective-permute-start(f32[1]{0:T(128)} %bitcast.30), channel_id=1, source_target_pairs={{0,2},{1,3},{2,0},{3,1},{4,6},{5,7},{6,4},{7,5},{8,10},{9,11},{10,... | collective-permute-start | bytes 20 | tf_op jit(solution)/shard_map/ppermute | solution.py:36
  59.8 6.6 %collective-permute-start.8 = (f32[1,7,32,128]{3,2,1,0:T(8,128)S(1)}, f32[1,7,32,128]{3,2,1,0:T(8,128)S(1)}, u32[]{:S(2)}, u32[]{:S(2)}) collective-permute-start(f32[1,7,32,128]{3,2,1,0:T(8,128)S(1)} %get-tuple-element.56), channel_id=1, source_target_pairs={{0,1},{1,2},{2,3},{3,4},{4,5},{5,6},{6,7},{7,8},{8,9},{9,10},{10,1... | collective-permute-start | bytes 344072 | tf_op jit(solution)/shard_map/ppermute | solution.py:18
  61.7 6.1 %collective-permute-start.9 = (f32[1,7,32,128]{3,2,1,0:T(8,128)S(1)}, f32[1,7,32,128]{3,2,1,0:T(8,128)S(1)}, u32[]{:S(2)}, u32[]{:S(2)}) collective-permute-start(f32[1,7,32,128]{3,2,1,0:T(8,128)S(1)} %get-tuple-element.57), channel_id=1, source_target_pairs={{1,0},{2,1},{3,2},{4,3},{5,4},{6,5},{7,6},{8,7},{9,8},{10,9},{11,1... | collective-permute-start | bytes 344072 | tf_op jit(solution)/shard_map/ppermute | solution.py:19
  68.4 7.0 %collective-permute-start.13 = (f32[1]{0:T(128)}, f32[1]{0:T(128)}, u32[]{:S(2)}, u32[]{:S(2)}) collective-permute-start(f32[1]{0:T(128)} %add.806), channel_id=1, source_target_pairs={{0,4},{1,5},{2,6},{3,7},{4,0},{5,1},{6,2},{7,3},{8,12},{9,13},{10,... | collective-permute-start | bytes 20 | tf_op jit(solution)/shard_map/ppermute | solution.py:36
  70.5 5.6 %collective-permute-start.11 = (f32[1,7,32,128]{3,2,1,0:T(8,128)S(1)}, f32[1,7,32,128]{3,2,1,0:T(8,128)S(1)}, u32[]{:S(2)}, u32[]{:S(2)}) collective-permute-start(f32[1,7,32,128]{3,2,1,0:T(8,128)S(1)} %get-tuple-element.54), channel_id=1, source_target_pairs={{0,1},{1,2},{2,3},{3,4},{4,5},{5,6},{6,7},{7,8},{8,9},{9,10},{10,1... | collective-permute-start | bytes 344072 | tf_op jit(solution)/shard_map/ppermute | solution.py:18
  73.1 6.1 %collective-permute-start.12 = (f32[1,7,32,128]{3,2,1,0:T(8,128)S(1)}, f32[1,7,32,128]{3,2,1,0:T(8,128)S(1)}, u32[]{:S(2)}, u32[]{:S(2)}) collective-permute-start(f32[1,7,32,128]{3,2,1,0:T(8,128)S(1)} %get-tuple-element.55), channel_id=1, source_target_pairs={{1,0},{2,1},{3,2},{4,3},{5,4},{6,5},{7,6},{8,7},{9,8},{10,9},{11,1... | collective-permute-start | bytes 344072 | tf_op jit(solution)/shard_map/ppermute | solution.py:19
  79.5 12.1 %copy-start.3 = (f32[1,8,32,128]{3,2,1,0:T(8,128)}, f32[1,8,32,128]{3,2,1,0:T(8,128)S(1)}, u32[]{:S(2)}) copy-start(f32[1,8,32,128]{3,2,1,0:T(8,128)S(1)} %fusion.531) | copy-start | bytes 393220
  79.8 7.7 %collective-permute-start.16 = (f32[1]{0:T(128)}, f32[1]{0:T(128)}, u32[]{:S(2)}, u32[]{:S(2)}) collective-permute-start(f32[1]{0:T(128)} %add.830), channel_id=1, source_target_pairs={{0,8},{1,9},{2,10},{3,11},{4,12},{5,13},{6,14},{7,15},{8,0},{9,1},... | collective-permute-start | bytes 20 | tf_op jit(solution)/shard_map/ppermute | solution.py:36
  82.7 5.6 %collective-permute-start.14 = (f32[1,7,32,128]{3,2,1,0:T(8,128)S(1)}, f32[1,7,32,128]{3,2,1,0:T(8,128)S(1)}, u32[]{:S(2)}, u32[]{:S(2)}) collective-permute-start(f32[1,7,32,128]{3,2,1,0:T(8,128)S(1)} %get-tuple-element.52), channel_id=1, source_target_pairs={{0,1},{1,2},{2,3},{3,4},{4,5},{5,6},{6,7},{7,8},{8,9},{9,10},{10,1... | collective-permute-start | bytes 344072 | tf_op jit(solution)/shard_map/ppermute | solution.py:18
  85.3 6.1 %collective-permute-start.15 = (f32[1,7,32,128]{3,2,1,0:T(8,128)S(1)}, f32[1,7,32,128]{3,2,1,0:T(8,128)S(1)}, u32[]{:S(2)}, u32[]{:S(2)}) collective-permute-start(f32[1,7,32,128]{3,2,1,0:T(8,128)S(1)} %get-tuple-element.53), channel_id=1, source_target_pairs={{1,0},{2,1},{3,2},{4,3},{5,4},{6,5},{7,6},{8,7},{9,8},{10,9},{11,1... | collective-permute-start | bytes 344072 | tf_op jit(solution)/shard_map/ppermute | solution.py:19
  91.5 0.9 copy-start.4
  93.3 1.1 %collective-permute-start.17 = (f32[1]{0:T(128)}, f32[1]{0:T(128)}, u32[]{:S(2)}, u32[]{:S(2)}) collective-permute-start(f32[1]{0:T(128)} %add.854), channel_id=1, source_target_pairs={{0,1},{1,0},{2,3},{3,2},{4,5},{5,4},{6,7},{7,6},{8,9},{9,8},{10,11... | collective-permute-start | bytes 20 | tf_op jit(solution)/shard_map/ppermute | solution.py:36

commit v13 on v12

--- a/solution.py
+++ b/solution.py
@@ -102,11 +102,14 @@
     first_lap = wide_operator(first[1 : 1 + shots], wave_now, flux_buoyancy)
     adjoint_lap = wide_operator(first[1 + shots :], adjoint_operand, flux_buoyancy)
 
-    def operator(values):
+    def operator(values, later=None):
         wide = extended(values, 1, HALO)
         cross = lax.optimization_barrier(cross_terms(values, buoyancy))
+        if later is not None:
+            cross, later = lax.optimization_barrier((cross, later))
         flux = flux_buoyancy * forward_diff(wide, 1, planes + 7, start=HALO - 4)
-        return backward_diff(flux, 1, planes) + cross
+        lap = backward_diff(flux, 1, planes) + cross
+        return lap if later is None else (lap, later)
 
     source_local = source_cell - offset
     source_owned = (source_local >= 0) & (source_local < cells)
@@ -153,13 +156,14 @@
     for level in range(STEPS, 0, -1):
         if level == STEPS:
             lap = adjoint_lap
+            resid = resids[level - 1]
         else:
             if distances:
                 mu_near, misfit = lax.optimization_barrier((mu_near, misfit))
                 misfit = butterfly_round(misfit, "mp", distances.pop(0))
-            lap = operator(kappa * mu_near)
+            lap, resid = operator(kappa * mu_near, resids[level - 1])
         state = 2.0 * mu_near + lap - mu_far
-        state = state + injected(resids[level - 1])
+        state = state + injected(resid)
         gradient = gradient + state * laps[level - 1]
         mu_far, mu_near = (mu_near, state)
         mu_near, misfit = lax.optimization_barrier((mu_near, misfit))

time: 97.5 us -> 95.2 us (0.976)
  waiting for transfers between devices: 19.3 us -> 17 us
    ppermute x7, waiting for transfers between devices: 15.2 us -> 12.9 us  [extended(): after = lax.ppermute(first, 'mp', down)]
  transfers between devices with their start and end apart: 18 -> 18, of which waited for: 9 -> 9; matrix products, arithmetic and copies ran while one was open for 10% -> 12% of each run, Pallas kernels for 0% -> 0%
where the time goes in v13:
time: 95.2 us; the launch traced here: 93.9 us
  starting transfers between devices  43.8 us (46%)
  waiting for transfers between devices  17 us (18%)
  other arithmetic  12.9 us (14%)
  matrix products  11.4 us (12%)
  between operations  6.42 us (7%)
  local copies, waits for them, and re-layouts  2.38 us (2%)
    ppermute x7, starting transfers between devices, extended(): before = lax.ppermute(last, 'mp', up)  20.1 us
    ppermute x7, starting transfers between devices, extended(): after = lax.ppermute(first, 'mp', down)  15 us
    ppermute x7, waiting for transfers between devices, extended(): after = lax.ppermute(first, 'mp', down)  12.9 us
    ppermute x4, starting transfers between devices, butterfly_round(): return values + lax.ppermute(values, axis, pairs)  8.77 us
    dot_general x4, matrix products, sample(): jnp.einsum('srk,skz->srz', row_pick, field.reshape(shots, rows, cz), prec...  6.43 us
    dot_general x4, matrix products, injected(): jnp.einsum('srk,srz->skz', row_pick, spread, precision=lax.Precision.HIGH...  4.93 us
    ppermute x7, waiting for transfers between devices, extended(): before = lax.ppermute(last, 'mp', up)  3.87 us
    add x4, other arithmetic, local(): following = following + jnp.where(source_hit, amount, 0.0)  3.22 us
  transfers between devices with their start and end apart: 18, of which 9 were waited for; matrix products, arithmetic and copies ran while one was open for 12% of the time, Pallas kernels for 0%

profile of v13, /device:TPU:1, one launch (start us, length us, event | category | flops | bytes accessed | tf_op | source)
XLA Modules:
  0.0 93.9 jit_solution(1515732876607443894)
XLA Ops:
  0.6 1.1 %bitcast_multiply_fusion.8 = (f32[1,8,32,128]{3,2,1,0:T(8,128)S(1)}, f32[8,32,128]{2,1,0:T(8,128)S(1)}) fusion(f32[1,8,32,128]{3,2,1,0:T(8,128)} %param.14, f32[8,32,128]{2,1,0:T(8,128)} %param.11, f32[8,32,128]{2,1,0:T(8,128)} %param.10), kind=kLoop, calls=%fused_computation.881 | loop fusion | flops 98304 | bytes 655360 | tf_op jit(solution)/shard_map/mul | solution.py:99
  1.7 1.0 %pad_maximum_fusion.1 = f32[3,8,32,128]{3,2,1,0:T(8,128)S(1)} fusion(f32[1,8,32,128]{3,2,1,0:T(8,128)S(1)} %get-tuple-element.44, f32[1,8,32,128]{3,2,1,0:T(8,128)} %param.13, f32[1,8,32,128]{3,2,1,0:T(8,128)} %bitcast.123), kind=kLoop, calls=%fused_computation.168 | loop fusion | flops 196608 | bytes 786432 | tf_op jit(solution)/shard_map/concatenate | solution.py:100
  2.9 2.0 %collective-permute-start.1 = (f32[3,7,32,128]{3,2,1,0:T(8,128)S(1)}, f32[3,7,32,128]{3,2,1,0:T(8,128)S(1)}, u32[]{:S(2)}, u32[]{:S(2)}) collective-permute-start(f32[3,7,32,128]{3,2,1,0:T(8,128)S(1)} %get-tuple-element.46), channel_id=1, source_target_pairs={{1,0},{2,1},{3,2},{4,3},{5,4},{6,5},{7,6},{8,7},{9,8},{10,9},{11,1... | collective-permute-start | bytes 1032200 | tf_op jit(solution)/shard_map/ppermute | solution.py:19
  4.8 4.5 %collective-permute-start = (f32[3,7,32,128]{3,2,1,0:T(8,128)S(1)}, f32[3,7,32,128]{3,2,1,0:T(8,128)S(1)}, u32[]{:S(2)}, u32[]{:S(2)}) collective-permute-start(f32[3,7,32,128]{3,2,1,0:T(8,128)S(1)} %get-tuple-element.47), channel_id=1, source_target_pairs={{0,1},{1,2},{2,3},{3,4},{4,5},{5,6},{6,7},{7,8},{8,9},{9,10},{10,1... | collective-permute-start | bytes 1032200 | tf_op jit(solution)/shard_map/ppermute | solution.py:18
  10.0 0.6 fusion.616
  10.7 0.5 fusion.336
  11.3 1.0 %collective-permute-done.1 = f32[3,7,32,128]{3,2,1,0:T(8,128)S(1)} collective-permute-done((f32[3,7,32,128]{3,2,1,0:T(8,128)S(1)}, f32[3,7,32,128]{3,2,1,0:T(8,128)S(1)}, u32[]{:S(2)}, u32[]{:S(2)}) %collective-permute-start.1) | collective-permute-done | bytes 344096 | tf_op jit(solution)/shard_map/ppermute | solution.py:19
  12.3 3.9 %collective-permute-done = f32[3,7,32,128]{3,2,1,0:T(8,128)S(1)} collective-permute-done((f32[3,7,32,128]{3,2,1,0:T(8,128)S(1)}, f32[3,7,32,128]{3,2,1,0:T(8,128)S(1)}, u32[]{:S(2)}, u32[]{:S(2)}) %collective-permute-start) | collective-permute-done | bytes 344096 | tf_op jit(solution)/shard_map/ppermute | solution.py:18
  16.3 0.1 fusion.114
  16.4 0.8 copy-done.6
  17.2 1.0 %fusion.587 = (f32[1,8,32,128]{3,2,1,0:T(8,128)S(1)}, f32[1,8,32,128]{3,2,1,0:T(8,128)S(1)}) fusion(f32[8,32,128]{2,1,0:T(8,128)S(1)} %get-tuple-element.45, f32[1,8,32,128]{3,2,1,0:T(8,128)S(1)} %copy-done.6, f32[1,8,32,128]{3,2,1,0:T(8,128)S(1)} %copy-done.1, f32[]{:T(128)} %bitcast.7, s32[]{:T(128)} %bitcast.6, s32[32]{0:T(128)S(1)} %iota_multiply_fusion, ...), kind=kLoop, calls=%fused_computation.883 | loop fusion | flops 1441792 | bytes 1966248 | tf_op jit(solution)/shard_map/add | solution.py:147
  18.2 0.3 fusion.382
  18.5 4.4 %collective-permute-start.2 = (f32[1,7,32,128]{3,2,1,0:T(8,128)S(1)}, f32[1,7,32,128]{3,2,1,0:T(8,128)S(1)}, u32[]{:S(2)}, u32[]{:S(2)}) collective-permute-start(f32[1,7,32,128]{3,2,1,0:T(8,128)S(1)} %get-tuple-element.76), channel_id=1, source_target_pairs={{0,1},{1,2},{2,3},{3,4},{4,5},{5,6},{6,7},{7,8},{8,9},{9,10},{10,1... | collective-permute-start | bytes 344072 | tf_op jit(solution)/shard_map/ppermute | solution.py:18
  22.9 1.9 %collective-permute-start.3 = (f32[1,7,32,128]{3,2,1,0:T(8,128)S(1)}, f32[1,7,32,128]{3,2,1,0:T(8,128)S(1)}, u32[]{:S(2)}, u32[]{:S(2)}) collective-permute-start(f32[1,7,32,128]{3,2,1,0:T(8,128)S(1)} %get-tuple-element.77), channel_id=1, source_target_pairs={{1,0},{2,1},{3,2},{4,3},{5,4},{6,5},{7,6},{8,7},{9,8},{10,9},{11,1... | collective-permute-start | bytes 344072 | tf_op jit(solution)/shard_map/ppermute | solution.py:19
  24.8 0.3 fusion.204
  25.1 0.1 fusion.122
  25.2 1.6 %fusion.16 = f32[2048]{0:T(1024)S(1)} fusion(f32[256,128]{1,0:T(8,128)S(1)} %bitcast.127, s32[2048]{0:T(1024)S(1)} %bitcast.147, s32[2048]{0:T(1024)S(1)} %bitcast.139), kind=kOutput, calls=%fused_computation.15 | convolution fusion | flops 806615040 | bytes 155648 | tf_op jit(solution)/shard_map/srk,skz->srz/dot_general | solution.py:129
  26.9 2.1 %collective-permute-done.3 = f32[1,7,32,128]{3,2,1,0:T(8,128)S(1)} collective-permute-done((f32[1,7,32,128]{3,2,1,0:T(8,128)S(1)}, f32[1,7,32,128]{3,2,1,0:T(8,128)S(1)}, u32[]{:S(2)}, u32[]{:S(2)}) %collective-permute-start.3) | collective-permute-done | bytes 114720 | tf_op jit(solution)/shard_map/ppermute | solution.py:19
  29.0 0.1 fusion.107
  29.1 0.8 fusion.589
  29.9 0.3 fusion.405
  30.2 1.9 %collective-permute-start.4 = (f32[1,7,32,128]{3,2,1,0:T(8,128)S(1)}, f32[1,7,32,128]{3,2,1,0:T(8,128)S(1)}, u32[]{:S(2)}, u32[]{:S(2)}) collective-permute-start(f32[1,7,32,128]{3,2,1,0:T(8,128)S(1)} %get-tuple-element.74), channel_id=1, source_target_pairs={{0,1},{1,2},{2,3},{3,4},{4,5},{5,6},{6,7},{7,8},{8,9},{9,10},{10,1... | collective-permute-start | bytes 344072 | tf_op jit(solution)/shard_map/ppermute | solution.py:18
  32.2 2.4 %collective-permute-start.5 = (f32[1,7,32,128]{3,2,1,0:T(8,128)S(1)}, f32[1,7,32,128]{3,2,1,0:T(8,128)S(1)}, u32[]{:S(2)}, u32[]{:S(2)}) collective-permute-start(f32[1,7,32,128]{3,2,1,0:T(8,128)S(1)} %get-tuple-element.75), channel_id=1, source_target_pairs={{1,0},{2,1},{3,2},{4,3},{5,4},{6,5},{7,6},{8,7},{9,8},{10,9},{11,1... | collective-permute-start | bytes 344072 | tf_op jit(solution)/shard_map/ppermute | solution.py:19
  34.6 0.3 fusion.228
  34.9 1.6 %fusion.19 = f32[2048]{0:T(1024)S(1)} fusion(f32[256,128]{1,0:T(8,128)S(1)} %bitcast.128, s32[2048]{0:T(1024)S(1)} %bitcast.148, s32[2048]{0:T(1024)S(1)} %bitcast.140), kind=kOutput, calls=%fused_computation.16 | convolution fusion | flops 806615040 | bytes 155648 | tf_op jit(solution)/shard_map/srk,skz->srz/dot_general | solution.py:129
  36.5 1.8 %collective-permute-done.5 = f32[1,7,32,128]{3,2,1,0:T(8,128)S(1)} collective-permute-done((f32[1,7,32,128]{3,2,1,0:T(8,128)S(1)}, f32[1,7,32,128]{3,2,1,0:T(8,128)S(1)}, u32[]{:S(2)}, u32[]{:S(2)}) %collective-permute-start.5) | collective-permute-done | bytes 114720 | tf_op jit(solution)/shard_map/ppermute | solution.py:19
  38.4 0.7 fusion.591
  39.2 0.3 fusion.428
  39.5 1.9 %collective-permute-start.6 = (f32[1,7,32,128]{3,2,1,0:T(8,128)S(1)}, f32[1,7,32,128]{3,2,1,0:T(8,128)S(1)}, u32[]{:S(2)}, u32[]{:S(2)}) collective-permute-start(f32[1,7,32,128]{3,2,1,0:T(8,128)S(1)} %get-tuple-element.72), channel_id=1, source_target_pairs={{0,1},{1,2},{2,3},{3,4},{4,5},{5,6},{6,7},{7,8},{8,9},{9,10},{10,1... | collective-permute-start | bytes 344072 | tf_op jit(solution)/shard_map/ppermute | solution.py:18
  41.4 2.4 %collective-permute-start.7 = (f32[1,7,32,128]{3,2,1,0:T(8,128)S(1)}, f32[1,7,32,128]{3,2,1,0:T(8,128)S(1)}, u32[]{:S(2)}, u32[]{:S(2)}) collective-permute-start(f32[1,7,32,128]{3,2,1,0:T(8,128)S(1)} %get-tuple-element.73), channel_id=1, source_target_pairs={{1,0},{2,1},{3,2},{4,3},{5,4},{6,5},{7,6},{8,7},{9,8},{10,9},{11,1... | collective-permute-start | bytes 344072 | tf_op jit(solution)/shard_map/ppermute | solution.py:19
  43.9 0.3 fusion.252
  44.2 1.6 %fusion.22 = f32[2048]{0:T(1024)S(1)} fusion(f32[256,128]{1,0:T(8,128)S(1)} %bitcast.129, s32[2048]{0:T(1024)S(1)} %bitcast.149, s32[2048]{0:T(1024)S(1)} %bitcast.141), kind=kOutput, calls=%fused_computation.17 | convolution fusion | flops 806615040 | bytes 155648 | tf_op jit(solution)/shard_map/srk,skz->srz/dot_general | solution.py:129
  45.8 2.6 %collective-permute-done.7 = f32[1,7,32,128]{3,2,1,0:T(8,128)S(1)} collective-permute-done((f32[1,7,32,128]{3,2,1,0:T(8,128)S(1)}, f32[1,7,32,128]{3,2,1,0:T(8,128)S(1)}, u32[]{:S(2)}, u32[]{:S(2)}) %collective-permute-start.7) | collective-permute-done | bytes 114720 | tf_op jit(solution)/shard_map/ppermute | solution.py:19
  48.6 0.7 fusion.593
  49.3 1.6 %fusion.13 = f32[2048]{0:T(1024)S(1)} fusion(f32[256,128]{1,0:T(8,128)S(1)} %bitcast.130, s32[2048]{0:T(1024)S(1)} %bitcast.150, s32[2048]{0:T(1024)S(1)} %bitcast.142), kind=kOutput, calls=%fused_computation.14 | convolution fusion | flops 806615040 | bytes 155648 | tf_op jit(solution)/shard_map/srk,skz->srz/dot_general | solution.py:129
  51.0 1.2 %fusion.25 = f32[1,8,32,128]{3,2,1,0:T(8,128)S(1)} fusion(s32[8,32]{1,0:T(8,128)S(1)} %multiply_add_fusion, s32[2048]{0:T(1024)S(1)} %bitcast.151, f32[2048]{0:T(1024)S(1)} %bitcast.137, s32[2048]{0:T(1024)S(1)} %bitcast.143), kind=kOutput, calls=%fused_computation.18 | convolution fusion | flops 806354944 | bytes 156672 | tf_op jit(solution)/shard_map/srk,srz->skz/dot_general | solution.py:136
  52.3 0.6 fusion.594
  53.6 0.3 fusion.155
  53.9 0.3 fusion.451
  54.3 3.0 %collective-permute-start.10 = (f32[1]{0:T(128)}, f32[1]{0:T(128)}, u32[]{:S(2)}, u32[]{:S(2)}) collective-permute-start(f32[1]{0:T(128)} %bitcast.30), channel_id=1, source_target_pairs={{0,2},{1,3},{2,0},{3,1},{4,6},{5,7},{6,4},{7,5},{8,10},{9,11},{10,... | collective-permute-start | bytes 20 | tf_op jit(solution)/shard_map/ppermute | solution.py:36
  57.3 1.9 %collective-permute-start.8 = (f32[1,7,32,128]{3,2,1,0:T(8,128)S(1)}, f32[1,7,32,128]{3,2,1,0:T(8,128)S(1)}, u32[]{:S(2)}, u32[]{:S(2)}) collective-permute-start(f32[1,7,32,128]{3,2,1,0:T(8,128)S(1)} %get-tuple-element.68), channel_id=1, source_target_pairs={{0,1},{1,2},{2,3},{3,4},{4,5},{5,6},{6,7},{7,8},{8,9},{9,10},{10,1... | collective-permute-start | bytes 344072 | tf_op jit(solution)/shard_map/ppermute | solution.py:18
  59.2 2.4 %collective-permute-start.9 = (f32[1,7,32,128]{3,2,1,0:T(8,128)S(1)}, f32[1,7,32,128]{3,2,1,0:T(8,128)S(1)}, u32[]{:S(2)}, u32[]{:S(2)}) collective-permute-start(f32[1,7,32,128]{3,2,1,0:T(8,128)S(1)} %get-tuple-element.69), channel_id=1, source_target_pairs={{1,0},{2,1},{3,2},{4,3},{5,4},{6,5},{7,6},{8,7},{9,8},{10,9},{11,1... | collective-permute-start | bytes 344072 | tf_op jit(solution)/shard_map/ppermute | solution.py:19
  61.6 0.3 fusion.276
  61.9 1.2 %fusion.28 = f32[1,8,32,128]{3,2,1,0:T(8,128)S(1)} fusion(s32[8,32]{1,0:T(8,128)S(1)} %multiply_add_fusion, s32[2048]{0:T(1024)S(1)} %bitcast.152, f32[2048]{0:T(1024)S(1)} %bitcast.136, s32[2048]{0:T(1024)S(1)} %bitcast.144), kind=kOutput, calls=%fused_computation.19 | convolution fusion | flops 806354944 | bytes 156672 | tf_op jit(solution)/shard_map/srk,srz->skz/dot_general | solution.py:136
  63.9 1.5 %collective-permute-done.9 = f32[1,7,32,128]{3,2,1,0:T(8,128)S(1)} collective-permute-done((f32[1,7,32,128]{3,2,1,0:T(8,128)S(1)}, f32[1,7,32,128]{3,2,1,0:T(8,128)S(1)}, u32[]{:S(2)}, u32[]{:S(2)}) %collective-permute-start.9) | collective-permute-done | bytes 114720 | tf_op jit(solution)/shard_map/ppermute | solution.py:19
  65.3 0.1 fusion.86
  65.6 0.3 fusion.474
  65.9 2.1 %collective-permute-start.13 = (f32[1]{0:T(128)}, f32[1]{0:T(128)}, u32[]{:S(2)}, u32[]{:S(2)}) collective-permute-start(f32[1]{0:T(128)} %add.806), channel_id=1, source_target_pairs={{0,4},{1,5},{2,6},{3,7},{4,0},{5,1},{6,2},{7,3},{8,12},{9,13},{10,... | collective-permute-start | bytes 20 | tf_op jit(solution)/shard_map/ppermute | solution.py:36
  68.0 2.8 %collective-permute-start.11 = (f32[1,7,32,128]{3,2,1,0:T(8,128)S(1)}, f32[1,7,32,128]{3,2,1,0:T(8,128)S(1)}, u32[]{:S(2)}, u32[]{:S(2)}) collective-permute-start(f32[1,7,32,128]{3,2,1,0:T(8,128)S(1)} %get-tuple-element.66), channel_id=1, source_target_pairs={{0,1},{1,2},{2,3},{3,4},{4,5},{5,6},{6,7},{7,8},{8,9},{9,10},{10,1... | collective-permute-start | bytes 344072 | tf_op jit(solution)/shard_map/ppermute | solution.py:18
  70.8 1.9 %collective-permute-start.12 = (f32[1,7,32,128]{3,2,1,0:T(8,128)S(1)}, f32[1,7,32,128]{3,2,1,0:T(8,128)S(1)}, u32[]{:S(2)}, u32[]{:S(2)}) collective-permute-start(f32[1,7,32,128]{3,2,1,0:T(8,128)S(1)} %get-tuple-element.67), channel_id=1, source_target_pairs={{1,0},{2,1},{3,2},{4,3},{5,4},{6,5},{7,6},{8,7},{9,8},{10,9},{11,1... | collective-permute-start | bytes 344072 | tf_op jit(solution)/shard_map/ppermute | solution.py:19
  72.8 0.3 fusion.300
  73.1 1.2 %fusion.31 = f32[1,8,32,128]{3,2,1,0:T(8,128)S(1)} fusion(s32[8,32]{1,0:T(8,128)S(1)} %multiply_add_fusion, s32[2048]{0:T(1024)S(1)} %bitcast.153, f32[2048]{0:T(1024)S(1)} %bitcast.134, s32[2048]{0:T(1024)S(1)} %bitcast.145), kind=kOutput, calls=%fused_computation.20 | convolution fusion | flops 806354944 | bytes 156672 | tf_op jit(solution)/shard_map/srk,srz->skz/dot_general | solution.py:136
  75.0 1.9 %collective-permute-done.12 = f32[1,7,32,128]{3,2,1,0:T(8,128)S(1)} collective-permute-done((f32[1,7,32,128]{3,2,1,0:T(8,128)S(1)}, f32[1,7,32,128]{3,2,1,0:T(8,128)S(1)}, u32[]{:S(2)}, u32[]{:S(2)}) %collective-permute-start.12) | collective-permute-done | bytes 114720 | tf_op jit(solution)/shard_map/ppermute | solution.py:19
  77.2 0.3 fusion.497
  77.5 2.8 %collective-permute-start.16 = (f32[1]{0:T(128)}, f32[1]{0:T(128)}, u32[]{:S(2)}, u32[]{:S(2)}) collective-permute-start(f32[1]{0:T(128)} %add.830), channel_id=1, source_target_pairs={{0,8},{1,9},{2,10},{3,11},{4,12},{5,13},{6,14},{7,15},{8,0},{9,1},... | collective-permute-start | bytes 20 | tf_op jit(solution)/shard_map/ppermute | solution.py:36
  80.4 2.6 %collective-permute-start.14 = (f32[1,7,32,128]{3,2,1,0:T(8,128)S(1)}, f32[1,7,32,128]{3,2,1,0:T(8,128)S(1)}, u32[]{:S(2)}, u32[]{:S(2)}) collective-permute-start(f32[1,7,32,128]{3,2,1,0:T(8,128)S(1)} %get-tuple-element.64), channel_id=1, source_target_pairs={{0,1},{1,2},{2,3},{3,4},{4,5},{5,6},{6,7},{7,8},{8,9},{9,10},{10,1... | collective-permute-start | bytes 344072 | tf_op jit(solution)/shard_map/ppermute | solution.py:18
  83.0 1.9 %collective-permute-start.15 = (f32[1,7,32,128]{3,2,1,0:T(8,128)S(1)}, f32[1,7,32,128]{3,2,1,0:T(8,128)S(1)}, u32[]{:S(2)}, u32[]{:S(2)}) collective-permute-start(f32[1,7,32,128]{3,2,1,0:T(8,128)S(1)} %get-tuple-element.65), channel_id=1, source_target_pairs={{1,0},{2,1},{3,2},{4,3},{5,4},{6,5},{7,6},{8,7},{9,8},{10,9},{11,1... | collective-permute-start | bytes 344072 | tf_op jit(solution)/shard_map/ppermute | solution.py:19
  85.0 0.3 fusion.324
  85.3 1.2 %fusion.34 = f32[1,8,32,128]{3,2,1,0:T(8,128)S(1)} fusion(s32[8,32]{1,0:T(8,128)S(1)} %multiply_add_fusion, s32[2048]{0:T(1024)S(1)} %bitcast.154, f32[2048]{0:T(1024)S(1)} %bitcast.132, s32[2048]{0:T(1024)S(1)} %bitcast.146), kind=kOutput, calls=%fused_computation.21 | convolution fusion | flops 806354944 | bytes 156672 | tf_op jit(solution)/shard_map/srk,srz->skz/dot_general | solution.py:136
  87.2 1.9 %collective-permute-done.15 = f32[1,7,32,128]{3,2,1,0:T(8,128)S(1)} collective-permute-done((f32[1,7,32,128]{3,2,1,0:T(8,128)S(1)}, f32[1,7,32,128]{3,2,1,0:T(8,128)S(1)}, u32[]{:S(2)}, u32[]{:S(2)}) %collective-permute-start.15) | collective-permute-done | bytes 114720 | tf_op jit(solution)/shard_map/ppermute | solution.py:19
  89.3 0.8 copy-done.4
  90.1 0.9 bitcast_multiply_fusion
  91.0 0.8 collective-permute-start.17
  91.8 0.3 collective-permute-done.17
  (56 shorter events, 1.3 us)
Async XLA Ops:
  1.7 8.3 %copy-start.9 = (f32[1,4]{1,0:T(1,128)S(1)}, f32[1,4]{1,0:T(1,128)}, u32[]{:S(2)}) copy-start(f32[1,4]{1,0:T(1,128)} %param.17) | copy-start | bytes 52
  1.7 8.9 %copy-start.7 = (s32[1,2048]{1,0:T(1,128)S(1)}, s32[1,2048]{1,0:T(1,128)}, u32[]{:S(2)}) copy-start(s32[1,2048]{1,0:T(1,128)} %param.18) | copy-start | bytes 24580
  1.7 9.0 %copy-start = (f32[8,32,128]{2,1,0:T(8,128)S(1)}, f32[8,32,128]{2,1,0:T(8,128)}, u32[]{:S(2)}) copy-start(f32[8,32,128]{2,1,0:T(8,128)} %param.11) | copy-start | bytes 393220
  1.7 9.0 %copy-start.1 = (f32[1,8,32,128]{3,2,1,0:T(8,128)S(1)}, f32[1,8,32,128]{3,2,1,0:T(8,128)}, u32[]{:S(2)}) copy-start(f32[1,8,32,128]{3,2,1,0:T(8,128)} %param.13) | copy-start | bytes 393220
  2.9 9.5 %collective-permute-start.1 = (f32[3,7,32,128]{3,2,1,0:T(8,128)S(1)}, f32[3,7,32,128]{3,2,1,0:T(8,128)S(1)}, u32[]{:S(2)}, u32[]{:S(2)}) collective-permute-start(f32[3,7,32,128]{3,2,1,0:T(8,128)S(1)} %get-tuple-element.46), channel_id=1, source_target_pairs={{1,0},{2,1},{3,2},{4,3},{5,4},{6,5},{7,6},{8,7},{9,8},{10,9},{11,1... | collective-permute-start | bytes 1032200 | tf_op jit(solution)/shard_map/ppermute | solution.py:19
  4.8 11.3 %collective-permute-start = (f32[3,7,32,128]{3,2,1,0:T(8,128)S(1)}, f32[3,7,32,128]{3,2,1,0:T(8,128)S(1)}, u32[]{:S(2)}, u32[]{:S(2)}) collective-permute-start(f32[3,7,32,128]{3,2,1,0:T(8,128)S(1)} %get-tuple-element.47), channel_id=1, source_target_pairs={{0,1},{1,2},{2,3},{3,4},{4,5},{5,6},{6,7},{7,8},{8,9},{9,10},{10,1... | collective-permute-start | bytes 1032200 | tf_op jit(solution)/shard_map/ppermute | solution.py:18
  16.3 0.9 copy-start.6
  18.5 8.4 %collective-permute-start.2 = (f32[1,7,32,128]{3,2,1,0:T(8,128)S(1)}, f32[1,7,32,128]{3,2,1,0:T(8,128)S(1)}, u32[]{:S(2)}, u32[]{:S(2)}) collective-permute-start(f32[1,7,32,128]{3,2,1,0:T(8,128)S(1)} %get-tuple-element.76), channel_id=1, source_target_pairs={{0,1},{1,2},{2,3},{3,4},{4,5},{5,6},{6,7},{7,8},{8,9},{9,10},{10,1... | collective-permute-start | bytes 344072 | tf_op jit(solution)/shard_map/ppermute | solution.py:18
  22.9 6.1 %collective-permute-start.3 = (f32[1,7,32,128]{3,2,1,0:T(8,128)S(1)}, f32[1,7,32,128]{3,2,1,0:T(8,128)S(1)}, u32[]{:S(2)}, u32[]{:S(2)}) collective-permute-start(f32[1,7,32,128]{3,2,1,0:T(8,128)S(1)} %get-tuple-element.77), channel_id=1, source_target_pairs={{1,0},{2,1},{3,2},{4,3},{5,4},{6,5},{7,6},{8,7},{9,8},{10,9},{11,1... | collective-permute-start | bytes 344072 | tf_op jit(solution)/shard_map/ppermute | solution.py:19
  30.2 6.3 %collective-permute-start.4 = (f32[1,7,32,128]{3,2,1,0:T(8,128)S(1)}, f32[1,7,32,128]{3,2,1,0:T(8,128)S(1)}, u32[]{:S(2)}, u32[]{:S(2)}) collective-permute-start(f32[1,7,32,128]{3,2,1,0:T(8,128)S(1)} %get-tuple-element.74), channel_id=1, source_target_pairs={{0,1},{1,2},{2,3},{3,4},{4,5},{5,6},{6,7},{7,8},{8,9},{9,10},{10,1... | collective-permute-start | bytes 344072 | tf_op jit(solution)/shard_map/ppermute | solution.py:18
  32.2 6.1 %collective-permute-start.5 = (f32[1,7,32,128]{3,2,1,0:T(8,128)S(1)}, f32[1,7,32,128]{3,2,1,0:T(8,128)S(1)}, u32[]{:S(2)}, u32[]{:S(2)}) collective-permute-start(f32[1,7,32,128]{3,2,1,0:T(8,128)S(1)} %get-tuple-element.75), channel_id=1, source_target_pairs={{1,0},{2,1},{3,2},{4,3},{5,4},{6,5},{7,6},{8,7},{9,8},{10,9},{11,1... | collective-permute-start | bytes 344072 | tf_op jit(solution)/shard_map/ppermute | solution.py:19
  39.5 6.3 %collective-permute-start.6 = (f32[1,7,32,128]{3,2,1,0:T(8,128)S(1)}, f32[1,7,32,128]{3,2,1,0:T(8,128)S(1)}, u32[]{:S(2)}, u32[]{:S(2)}) collective-permute-start(f32[1,7,32,128]{3,2,1,0:T(8,128)S(1)} %get-tuple-element.72), channel_id=1, source_target_pairs={{0,1},{1,2},{2,3},{3,4},{4,5},{5,6},{6,7},{7,8},{8,9},{9,10},{10,1... | collective-permute-start | bytes 344072 | tf_op jit(solution)/shard_map/ppermute | solution.py:18
  41.4 7.0 %collective-permute-start.7 = (f32[1,7,32,128]{3,2,1,0:T(8,128)S(1)}, f32[1,7,32,128]{3,2,1,0:T(8,128)S(1)}, u32[]{:S(2)}, u32[]{:S(2)}) collective-permute-start(f32[1,7,32,128]{3,2,1,0:T(8,128)S(1)} %get-tuple-element.73), channel_id=1, source_target_pairs={{1,0},{2,1},{3,2},{4,3},{5,4},{6,5},{7,6},{8,7},{9,8},{10,9},{11,1... | collective-permute-start | bytes 344072 | tf_op jit(solution)/shard_map/ppermute | solution.py:19
  49.3 1.7 %copy-start.8 = (f32[1,4,2048]{2,1,0:T(4,128)S(1)}, f32[1,4,2048]{2,1,0:T(4,128)}, u32[]{:S(2)}) copy-start(f32[1,4,2048]{2,1,0:T(4,128)} %param.19) | copy-start | bytes 98308
  50.9 2.6 %copy-start.2 = (f32[1,8,32,128]{3,2,1,0:T(8,128)S(1)}, f32[1,8,32,128]{3,2,1,0:T(8,128)}, u32[]{:S(2)}) copy-start(f32[1,8,32,128]{3,2,1,0:T(8,128)} %param.14) | copy-start | bytes 393220
  50.9 2.6 %copy-start.5 = (f32[1,8,32,128]{3,2,1,0:T(8,128)S(1)}, f32[1,8,32,128]{3,2,1,0:T(8,128)}, u32[]{:S(2)}) copy-start(f32[1,8,32,128]{3,2,1,0:T(8,128)} %param.15) | copy-start | bytes 393220
  54.3 8.9 %collective-permute-start.10 = (f32[1]{0:T(128)}, f32[1]{0:T(128)}, u32[]{:S(2)}, u32[]{:S(2)}) collective-permute-start(f32[1]{0:T(128)} %bitcast.30), channel_id=1, source_target_pairs={{0,2},{1,3},{2,0},{3,1},{4,6},{5,7},{6,4},{7,5},{8,10},{9,11},{10,... | collective-permute-start | bytes 20 | tf_op jit(solution)/shard_map/ppermute | solution.py:36
  57.3 6.6 %collective-permute-start.8 = (f32[1,7,32,128]{3,2,1,0:T(8,128)S(1)}, f32[1,7,32,128]{3,2,1,0:T(8,128)S(1)}, u32[]{:S(2)}, u32[]{:S(2)}) collective-permute-start(f32[1,7,32,128]{3,2,1,0:T(8,128)S(1)} %get-tuple-element.68), channel_id=1, source_target_pairs={{0,1},{1,2},{2,3},{3,4},{4,5},{5,6},{6,7},{7,8},{8,9},{9,10},{10,1... | collective-permute-start | bytes 344072 | tf_op jit(solution)/shard_map/ppermute | solution.py:18
  59.2 6.1 %collective-permute-start.9 = (f32[1,7,32,128]{3,2,1,0:T(8,128)S(1)}, f32[1,7,32,128]{3,2,1,0:T(8,128)S(1)}, u32[]{:S(2)}, u32[]{:S(2)}) collective-permute-start(f32[1,7,32,128]{3,2,1,0:T(8,128)S(1)} %get-tuple-element.69), channel_id=1, source_target_pairs={{1,0},{2,1},{3,2},{4,3},{5,4},{6,5},{7,6},{8,7},{9,8},{10,9},{11,1... | collective-permute-start | bytes 344072 | tf_op jit(solution)/shard_map/ppermute | solution.py:19
  65.9 8.4 %collective-permute-start.13 = (f32[1]{0:T(128)}, f32[1]{0:T(128)}, u32[]{:S(2)}, u32[]{:S(2)}) collective-permute-start(f32[1]{0:T(128)} %add.806), channel_id=1, source_target_pairs={{0,4},{1,5},{2,6},{3,7},{4,0},{5,1},{6,2},{7,3},{8,12},{9,13},{10,... | collective-permute-start | bytes 20 | tf_op jit(solution)/shard_map/ppermute | solution.py:36
  68.0 7.0 %collective-permute-start.11 = (f32[1,7,32,128]{3,2,1,0:T(8,128)S(1)}, f32[1,7,32,128]{3,2,1,0:T(8,128)S(1)}, u32[]{:S(2)}, u32[]{:S(2)}) collective-permute-start(f32[1,7,32,128]{3,2,1,0:T(8,128)S(1)} %get-tuple-element.66), channel_id=1, source_target_pairs={{0,1},{1,2},{2,3},{3,4},{4,5},{5,6},{6,7},{7,8},{8,9},{9,10},{10,1... | collective-permute-start | bytes 344072 | tf_op jit(solution)/shard_map/ppermute | solution.py:18
  70.8 6.1 %collective-permute-start.12 = (f32[1,7,32,128]{3,2,1,0:T(8,128)S(1)}, f32[1,7,32,128]{3,2,1,0:T(8,128)S(1)}, u32[]{:S(2)}, u32[]{:S(2)}) collective-permute-start(f32[1,7,32,128]{3,2,1,0:T(8,128)S(1)} %get-tuple-element.67), channel_id=1, source_target_pairs={{1,0},{2,1},{3,2},{4,3},{5,4},{6,5},{7,6},{8,7},{9,8},{10,9},{11,1... | collective-permute-start | bytes 344072 | tf_op jit(solution)/shard_map/ppermute | solution.py:19
  77.2 12.1 %copy-start.3 = (f32[1,8,32,128]{3,2,1,0:T(8,128)}, f32[1,8,32,128]{3,2,1,0:T(8,128)S(1)}, u32[]{:S(2)}) copy-start(f32[1,8,32,128]{3,2,1,0:T(8,128)S(1)} %fusion.531) | copy-start | bytes 393220
  77.5 9.0 %collective-permute-start.16 = (f32[1]{0:T(128)}, f32[1]{0:T(128)}, u32[]{:S(2)}, u32[]{:S(2)}) collective-permute-start(f32[1]{0:T(128)} %add.830), channel_id=1, source_target_pairs={{0,8},{1,9},{2,10},{3,11},{4,12},{5,13},{6,14},{7,15},{8,0},{9,1},... | collective-permute-start | bytes 20 | tf_op jit(solution)/shard_map/ppermute | solution.py:36
  80.4 6.8 %collective-permute-start.14 = (f32[1,7,32,128]{3,2,1,0:T(8,128)S(1)}, f32[1,7,32,128]{3,2,1,0:T(8,128)S(1)}, u32[]{:S(2)}, u32[]{:S(2)}) collective-permute-start(f32[1,7,32,128]{3,2,1,0:T(8,128)S(1)} %get-tuple-element.64), channel_id=1, source_target_pairs={{0,1},{1,2},{2,3},{3,4},{4,5},{5,6},{6,7},{7,8},{8,9},{9,10},{10,1... | collective-permute-start | bytes 344072 | tf_op jit(solution)/shard_map/ppermute | solution.py:18
  83.0 6.1 %collective-permute-start.15 = (f32[1,7,32,128]{3,2,1,0:T(8,128)S(1)}, f32[1,7,32,128]{3,2,1,0:T(8,128)S(1)}, u32[]{:S(2)}, u32[]{:S(2)}) collective-permute-start(f32[1,7,32,128]{3,2,1,0:T(8,128)S(1)} %get-tuple-element.65), channel_id=1, source_target_pairs={{1,0},{2,1},{3,2},{4,3},{5,4},{6,5},{7,6},{8,7},{9,8},{10,9},{11,1... | collective-permute-start | bytes 344072 | tf_op jit(solution)/shard_map/ppermute | solution.py:19
  89.2 0.9 copy-start.4
  91.0 1.1 %collective-permute-start.17 = (f32[1]{0:T(128)}, f32[1]{0:T(128)}, u32[]{:S(2)}, u32[]{:S(2)}) collective-permute-start(f32[1]{0:T(128)} %add.854), channel_id=1, source_target_pairs={{0,1},{1,0},{2,3},{3,2},{4,5},{5,4},{6,7},{7,6},{8,9},{9,8},{10,11... | collective-permute-start | bytes 20 | tf_op jit(solution)/shard_map/ppermute | solution.py:36

commit v14 on v13

--- a/solution.py
+++ b/solution.py
@@ -136,37 +136,51 @@
         added = jnp.einsum("srk,srz->skz", row_pick, spread, precision=lax.Precision.HIGHEST)
         return lax.optimization_barrier(added.reshape(shape))
 
+    receiver_count = injected(jnp.ones_like(observed[:, 0, :]))
+    recorded_last = injected(observed[:, STEPS - 1, :])
+
     before, current = (wave_prev, wave_now)
     laps = []
     resids = []
     for step in range(STEPS):
-        lap = first_lap if step == 0 else operator(current)
+        if step == 0:
+            lap = first_lap
+        else:
+            lap, field = operator(current, current)
+            sampled = sample(field)
+            resids.append(jnp.where(receiver_owned, sampled - observed[:, step - 1, :], 0.0))
         laps.append(lap)
         following = 2.0 * current - before + kappa * lap
         amount = wavelet[:, step].reshape(shots, 1, 1, 1)
         following = following + jnp.where(source_hit, amount, 0.0)
-        sampled = sample(following)
-        resids.append(jnp.where(receiver_owned, sampled - observed[:, step, :], 0.0))
         before, current = (current, following)
-    stacked = jnp.stack(resids, axis=1)
-    misfit = 0.5 * jnp.sum(stacked * stacked, axis=(1, 2))
+    last_field = current
     distances = butterfly_distances("mp")
     mu_near, mu_far = (adjoint_next, adjoint_after)
     gradient = jnp.zeros(shape, jnp.float32)
     for level in range(STEPS, 0, -1):
         if level == STEPS:
-            lap = adjoint_lap
-            resid = resids[level - 1]
+            state = 2.0 * mu_near + adjoint_lap - mu_far
+            state = state + (receiver_count * last_field - recorded_last)
+        elif level == STEPS - 1:
+            lap, (resid, field) = operator(kappa * mu_near, (resids[level - 1], last_field))
+            sampled = sample(field)
+            resids.append(jnp.where(receiver_owned, sampled - observed[:, STEPS - 1, :], 0.0))
+            stacked = jnp.stack(resids, axis=1)
+            misfit = 0.5 * jnp.sum(stacked * stacked, axis=(1, 2))
+            if distances:
+                misfit = butterfly_round(misfit, "mp", distances.pop(0))
+            state = 2.0 * mu_near + lap - mu_far + injected(resid)
         else:
             if distances:
                 mu_near, misfit = lax.optimization_barrier((mu_near, misfit))
                 misfit = butterfly_round(misfit, "mp", distances.pop(0))
             lap, resid = operator(kappa * mu_near, resids[level - 1])
-        state = 2.0 * mu_near + lap - mu_far
-        state = state + injected(resid)
+            state = 2.0 * mu_near + lap - mu_far + injected(resid)
         gradient = gradient + state * laps[level - 1]
         mu_far, mu_near = (mu_near, state)
-        mu_near, misfit = lax.optimization_barrier((mu_near, misfit))
+        if level < STEPS:
+            mu_near, misfit = lax.optimization_barrier((mu_near, misfit))
     for distance in distances:
         misfit = butterfly_round(misfit, "mp", distance)
     velocity_gradient = 2.0 * velocity / buoyancy * jnp.sum(gradient, axis=0)

time: 95.2 us -> 96.8 us (1.017)
  waiting for transfers between devices: 17 us -> 13.8 us
  starting transfers between devices: 43.8 us -> 46.3 us
  matrix products: 11.4 us -> 12.6 us
    mul x7, other arithmetic: 2.4 us -> 5.41 us  [cross_terms(): flux = buoyancy * forward_diff(pad_axis(values, axis), axis, length)]
    ppermute x7, waiting for transfers between devices: 12.9 us -> 10.6 us  [extended(): after = lax.ppermute(first, 'mp', down)]
    ppermute x7, starting transfers between devices: 20.1 us -> 22 us  [extended(): before = lax.ppermute(last, 'mp', up)]
    dot_general x4 -> x5, matrix products: 4.93 us -> 6.19 us  [injected(): jnp.einsum('srk,srz->skz', row_pick, spread, precision=lax.Precision.HIGH...]
    concatenate x1, other arithmetic: 1.04 us -> 0.03 us  [local(): jnp.concatenate([buoyancy[None], wave_now, adjoint_operand], axis=0)]
    ppermute x7, waiting for transfers between devices: 3.87 us -> 2.9 us  [extended(): before = lax.ppermute(last, 'mp', up)]
    add x4 -> x3, other arithmetic: 3.22 us -> 2.48 us  [local(): following = following + jnp.where(source_hit, amount, 0.0)]
  transfers between devices with their start and end apart: 18 -> 18, of which waited for: 9 -> 7; matrix products, arithmetic and copies ran while one was open for 12% -> 17% of each run, Pallas kernels for 0% -> 0%
where the time goes in v14:
time: 96.8 us; the launch traced here: 95.7 us
  starting transfers between devices  46.3 us (48%)
  other arithmetic  13.8 us (14%)
  waiting for transfers between devices  13.8 us (14%)
  matrix products  12.6 us (13%)
  between operations  5.99 us (6%)
  local copies, waits for them, and re-layouts  3.22 us (3%)
    ppermute x7, starting transfers between devices, extended(): before = lax.ppermute(last, 'mp', up)  22 us
    ppermute x7, starting transfers between devices, extended(): after = lax.ppermute(first, 'mp', down)  15.1 us
    ppermute x7, waiting for transfers between devices, extended(): after = lax.ppermute(first, 'mp', down)  10.6 us
    ppermute x4, starting transfers between devices, butterfly_round(): return values + lax.ppermute(values, axis, pairs)  9.17 us
    dot_general x4, matrix products, sample(): jnp.einsum('srk,skz->srz', row_pick, field.reshape(shots, rows, cz), prec...  6.43 us
    dot_general x5, matrix products, injected(): jnp.einsum('srk,srz->skz', row_pick, spread, precision=lax.Precision.HIGH...  6.19 us
    mul x7, other arithmetic, cross_terms(): flux = buoyancy * forward_diff(pad_axis(values, axis), axis, length)  5.41 us
    ppermute x7, waiting for transfers between devices, extended(): before = lax.ppermute(last, 'mp', up)  2.9 us
  transfers between devices with their start and end apart: 18, of which 7 were waited for; matrix products, arithmetic and copies ran while one was open for 17% of the time, Pallas kernels for 0%

profile of v14, /device:TPU:1, one launch (start us, length us, event | category | flops | bytes accessed | tf_op | source)
XLA Modules:
  0.0 95.7 jit_solution(11519736001145048222)
XLA Ops:
  0.7 3.3 %fusion.179 = (f32[1,8,32,128]{3,2,1,0:T(8,128)S(1)}, f32[1,8,32,128]{3,2,1,0:T(8,128)S(1)}, f32[1,8,32,128]{3,2,1,0:T(8,128)S(1)}, f32[8,32,128]{2,1,0:T(8,128)S(1)}) fusion(f32[1,8,32,128]{3,2,1,0:T(8,128)} %param.13, f32[8,32,128]{2,1,0:T(8,128)} %param.11, f32[1,8,32,128]{3,2,1,0:T(8,128)} %param.14, f32[8,32,128]{2,1,0:T(8,128)} %param.10), kind=kLoop, calls=%fused_computation.432 | loop fusion | flops 884736 | bytes 1048576 | tf_op jit(solution)/shard_map/mul | solution.py:69
  4.1 2.0 %collective-permute-start.1 = (f32[3,7,32,128]{3,2,1,0:T(8,128)S(1)}, f32[3,7,32,128]{3,2,1,0:T(8,128)S(1)}, u32[]{:S(2)}, u32[]{:S(2)}) collective-permute-start(f32[3,7,32,128]{3,2,1,0:T(8,128)S(1)} %get-tuple-element.58), channel_id=1, source_target_pairs={{1,0},{2,1},{3,2},{4,3},{5,4},{6,5},{7,6},{8,7},{9,8},{10,9},{11,1... | collective-permute-start | bytes 1032200 | tf_op jit(solution)/shard_map/ppermute | solution.py:19
  6.1 4.5 %collective-permute-start = (f32[3,7,32,128]{3,2,1,0:T(8,128)S(1)}, f32[3,7,32,128]{3,2,1,0:T(8,128)S(1)}, u32[]{:S(2)}, u32[]{:S(2)}) collective-permute-start(f32[3,7,32,128]{3,2,1,0:T(8,128)S(1)} %get-tuple-element.59), channel_id=1, source_target_pairs={{0,1},{1,2},{2,3},{3,4},{4,5},{5,6},{6,7},{7,8},{8,9},{9,10},{10,1... | collective-permute-start | bytes 1032200 | tf_op jit(solution)/shard_map/ppermute | solution.py:18
  10.8 1.2 %fusion.30 = f32[1,8,32,128]{3,2,1,0:T(8,128)S(1)} fusion(s32[8,32]{1,0:T(8,128)S(1)} %multiply_add_fusion, s32[2048]{0:T(1024)S(1)} %bitcast.155, f32[2048]{0:T(1024)S(1)} %bitcast.167, s32[2048]{0:T(1024)S(1)} %bitcast.146), kind=kOutput, calls=%fused_computation.21 | convolution fusion | flops 806354944 | bytes 156672 | tf_op jit(solution)/shard_map/srk,srz->skz/dot_general | solution.py:136
  12.0 1.3 %fusion.27 = f32[1,8,32,128]{3,2,1,0:T(8,128)S(1)} fusion(s32[8,32]{1,0:T(8,128)S(1)} %multiply_add_fusion, s32[2048]{0:T(1024)S(1)} %bitcast.156, s32[2048]{0:T(1024)S(1)} %bitcast.147), kind=kOutput, calls=%fused_computation.20 | convolution fusion | flops 806354944 | bytes 148480 | tf_op jit(solution)/shard_map/srk,srz->skz/dot_general | solution.py:136
  14.0 0.6 fusion.633
  14.6 2.9 %collective-permute-done = f32[3,7,32,128]{3,2,1,0:T(8,128)S(1)} collective-permute-done((f32[3,7,32,128]{3,2,1,0:T(8,128)S(1)}, f32[3,7,32,128]{3,2,1,0:T(8,128)S(1)}, u32[]{:S(2)}, u32[]{:S(2)}) %collective-permute-start) | collective-permute-done | bytes 344096 | tf_op jit(solution)/shard_map/ppermute | solution.py:18
  17.5 0.1 fusion.126
  17.7 0.8 copy-done.5
  18.4 1.0 %fusion.599 = (f32[1,8,32,128]{3,2,1,0:T(8,128)S(1)}, f32[1,8,32,128]{3,2,1,0:T(8,128)S(1)}) fusion(f32[8,32,128]{2,1,0:T(8,128)S(1)} %get-tuple-element.91, f32[1,8,32,128]{3,2,1,0:T(8,128)S(1)} %copy-done.5, f32[1,8,32,128]{3,2,1,0:T(8,128)S(1)} %copy-done.1, f32[]{:T(128)} %bitcast.8, s32[]{:T(128)} %bitcast.7, s32[32]{0:T(128)S(1)} %iota_multiply_fusion, ...), kind=kLoop, calls=%fused_computation.893 | loop fusion | flops 1441792 | bytes 1966248 | tf_op jit(solution)/shard_map/add | solution.py:155
  19.4 0.3 fusion.394
  19.7 4.4 %collective-permute-start.2 = (f32[1,7,32,128]{3,2,1,0:T(8,128)S(1)}, f32[1,7,32,128]{3,2,1,0:T(8,128)S(1)}, u32[]{:S(2)}, u32[]{:S(2)}) collective-permute-start(f32[1,7,32,128]{3,2,1,0:T(8,128)S(1)} %get-tuple-element.88), channel_id=1, source_target_pairs={{0,1},{1,2},{2,3},{3,4},{4,5},{5,6},{6,7},{7,8},{8,9},{9,10},{10,1... | collective-permute-start | bytes 344072 | tf_op jit(solution)/shard_map/ppermute | solution.py:18
  24.1 1.9 %collective-permute-start.3 = (f32[1,7,32,128]{3,2,1,0:T(8,128)S(1)}, f32[1,7,32,128]{3,2,1,0:T(8,128)S(1)}, u32[]{:S(2)}, u32[]{:S(2)}) collective-permute-start(f32[1,7,32,128]{3,2,1,0:T(8,128)S(1)} %get-tuple-element.89), channel_id=1, source_target_pairs={{1,0},{2,1},{3,2},{4,3},{5,4},{6,5},{7,6},{8,7},{9,8},{10,9},{11,1... | collective-permute-start | bytes 344072 | tf_op jit(solution)/shard_map/ppermute | solution.py:19
  26.1 0.3 fusion.216
  26.4 0.1 fusion.134
  26.5 1.6 %fusion.18 = f32[2048]{0:T(1024)S(1)} fusion(f32[256,128]{1,0:T(8,128)S(1)} %bitcast.137, s32[2048]{0:T(1024)S(1)} %bitcast.157, s32[2048]{0:T(1024)S(1)} %bitcast.148), kind=kOutput, calls=%fused_computation.17 | convolution fusion | flops 806615040 | bytes 155648 | tf_op jit(solution)/shard_map/srk,skz->srz/dot_general | solution.py:129
  28.1 2.1 %collective-permute-done.3 = f32[1,7,32,128]{3,2,1,0:T(8,128)S(1)} collective-permute-done((f32[1,7,32,128]{3,2,1,0:T(8,128)S(1)}, f32[1,7,32,128]{3,2,1,0:T(8,128)S(1)}, u32[]{:S(2)}, u32[]{:S(2)}) %collective-permute-start.3) | collective-permute-done | bytes 114720 | tf_op jit(solution)/shard_map/ppermute | solution.py:19
  30.3 0.1 fusion.119
  30.4 0.8 fusion.601
  31.2 0.3 fusion.417
  31.5 1.9 %collective-permute-start.4 = (f32[1,7,32,128]{3,2,1,0:T(8,128)S(1)}, f32[1,7,32,128]{3,2,1,0:T(8,128)S(1)}, u32[]{:S(2)}, u32[]{:S(2)}) collective-permute-start(f32[1,7,32,128]{3,2,1,0:T(8,128)S(1)} %get-tuple-element.86), channel_id=1, source_target_pairs={{0,1},{1,2},{2,3},{3,4},{4,5},{5,6},{6,7},{7,8},{8,9},{9,10},{10,1... | collective-permute-start | bytes 344072 | tf_op jit(solution)/shard_map/ppermute | solution.py:18
  33.4 2.4 %collective-permute-start.5 = (f32[1,7,32,128]{3,2,1,0:T(8,128)S(1)}, f32[1,7,32,128]{3,2,1,0:T(8,128)S(1)}, u32[]{:S(2)}, u32[]{:S(2)}) collective-permute-start(f32[1,7,32,128]{3,2,1,0:T(8,128)S(1)} %get-tuple-element.87), channel_id=1, source_target_pairs={{1,0},{2,1},{3,2},{4,3},{5,4},{6,5},{7,6},{8,7},{9,8},{10,9},{11,1... | collective-permute-start | bytes 344072 | tf_op jit(solution)/shard_map/ppermute | solution.py:19
  35.8 0.3 fusion.240
  36.1 1.6 %fusion.21 = f32[2048]{0:T(1024)S(1)} fusion(f32[256,128]{1,0:T(8,128)S(1)} %bitcast.136, s32[2048]{0:T(1024)S(1)} %bitcast.158, s32[2048]{0:T(1024)S(1)} %bitcast.149), kind=kOutput, calls=%fused_computation.18 | convolution fusion | flops 806615040 | bytes 155648 | tf_op jit(solution)/shard_map/srk,skz->srz/dot_general | solution.py:129
  37.8 1.8 %collective-permute-done.5 = f32[1,7,32,128]{3,2,1,0:T(8,128)S(1)} collective-permute-done((f32[1,7,32,128]{3,2,1,0:T(8,128)S(1)}, f32[1,7,32,128]{3,2,1,0:T(8,128)S(1)}, u32[]{:S(2)}, u32[]{:S(2)}) %collective-permute-start.5) | collective-permute-done | bytes 114720 | tf_op jit(solution)/shard_map/ppermute | solution.py:19
  39.6 0.1 fusion.112
  39.7 0.8 fusion.603
  40.5 0.5 fusion.440
  41.0 1.9 %collective-permute-start.6 = (f32[1,7,32,128]{3,2,1,0:T(8,128)S(1)}, f32[1,7,32,128]{3,2,1,0:T(8,128)S(1)}, u32[]{:S(2)}, u32[]{:S(2)}) collective-permute-start(f32[1,7,32,128]{3,2,1,0:T(8,128)S(1)} %get-tuple-element.82), channel_id=1, source_target_pairs={{0,1},{1,2},{2,3},{3,4},{4,5},{5,6},{6,7},{7,8},{8,9},{9,10},{10,1... | collective-permute-start | bytes 344072 | tf_op jit(solution)/shard_map/ppermute | solution.py:18
  42.9 2.4 %collective-permute-start.7 = (f32[1,7,32,128]{3,2,1,0:T(8,128)S(1)}, f32[1,7,32,128]{3,2,1,0:T(8,128)S(1)}, u32[]{:S(2)}, u32[]{:S(2)}) collective-permute-start(f32[1,7,32,128]{3,2,1,0:T(8,128)S(1)} %get-tuple-element.83), channel_id=1, source_target_pairs={{1,0},{2,1},{3,2},{4,3},{5,4},{6,5},{7,6},{8,7},{9,8},{10,9},{11,1... | collective-permute-start | bytes 344072 | tf_op jit(solution)/shard_map/ppermute | solution.py:19
  45.3 0.3 fusion.264
  45.7 1.6 %fusion.15 = f32[2048]{0:T(1024)S(1)} fusion(f32[256,128]{1,0:T(8,128)S(1)} %bitcast.138, s32[2048]{0:T(1024)S(1)} %bitcast.159, s32[2048]{0:T(1024)S(1)} %bitcast.150), kind=kOutput, calls=%fused_computation.16 | convolution fusion | flops 806615040 | bytes 155648 | tf_op jit(solution)/shard_map/srk,skz->srz/dot_general | solution.py:129
  47.3 2.6 %collective-permute-done.7 = f32[1,7,32,128]{3,2,1,0:T(8,128)S(1)} collective-permute-done((f32[1,7,32,128]{3,2,1,0:T(8,128)S(1)}, f32[1,7,32,128]{3,2,1,0:T(8,128)S(1)}, u32[]{:S(2)}, u32[]{:S(2)}) %collective-permute-start.7) | collective-permute-done | bytes 114720 | tf_op jit(solution)/shard_map/ppermute | solution.py:19
  50.0 0.1 fusion.105
  50.1 0.8 copy-done.2
  50.9 1.0 %bitcast_multiply_fusion.3 = (f32[1,8,32,128]{3,2,1,0:T(8,128)S(1)}, f32[1,8,32,128]{3,2,1,0:T(8,128)S(1)}, f32[1,8,32,128]{3,2,1,0:T(8,128)S(1)}, f32[1,8,32,128]{3,2,1,0:T(8,128)S(1)}) fusion(f32[8,32,128]{2,1,0:T(8,128)S(1)} %get-tuple-element.91, f32[1,8,32,128]{3,2,1,0:T(8,128)S(1)} %fusion.30, f32[1,8,32,128]{3,2,1,0:T(8,128)S(1)} %fusion.27, ...), kind=kLoop, calls=%fused_computation.886 | loop fusion | flops 2064384 | bytes 3932328 | tf_op jit(solution)/shard_map/mul | solution.py:166
  52.0 0.3 fusion.463
  52.3 1.9 %collective-permute-start.8 = (f32[1,7,32,128]{3,2,1,0:T(8,128)S(1)}, f32[1,7,32,128]{3,2,1,0:T(8,128)S(1)}, u32[]{:S(2)}, u32[]{:S(2)}) collective-permute-start(f32[1,7,32,128]{3,2,1,0:T(8,128)S(1)} %get-tuple-element.80), channel_id=1, source_target_pairs={{0,1},{1,2},{2,3},{3,4},{4,5},{5,6},{6,7},{7,8},{8,9},{9,10},{10,1... | collective-permute-start | bytes 344072 | tf_op jit(solution)/shard_map/ppermute | solution.py:18
  54.2 2.6 %collective-permute-start.9 = (f32[1,7,32,128]{3,2,1,0:T(8,128)S(1)}, f32[1,7,32,128]{3,2,1,0:T(8,128)S(1)}, u32[]{:S(2)}, u32[]{:S(2)}) collective-permute-start(f32[1,7,32,128]{3,2,1,0:T(8,128)S(1)} %get-tuple-element.81), channel_id=1, source_target_pairs={{1,0},{2,1},{3,2},{4,3},{5,4},{6,5},{7,6},{8,7},{9,8},{10,9},{11,1... | collective-permute-start | bytes 344072 | tf_op jit(solution)/shard_map/ppermute | solution.py:19
  56.8 0.3 fusion.288
  57.1 1.6 %fusion.24 = f32[2048]{0:T(1024)S(1)} fusion(f32[256,128]{1,0:T(8,128)S(1)} %bitcast.139, s32[2048]{0:T(1024)S(1)} %bitcast.160, s32[2048]{0:T(1024)S(1)} %bitcast.151), kind=kOutput, calls=%fused_computation.19 | convolution fusion | flops 806615040 | bytes 155648 | tf_op jit(solution)/shard_map/srk,skz->srz/dot_general | solution.py:129
  58.8 0.6 fusion.606
  60.1 3.0 %collective-permute-start.10 = (f32[1]{0:T(128)}, f32[1]{0:T(128)}, u32[]{:S(2)}, u32[]{:S(2)}) collective-permute-start(f32[1]{0:T(128)} %bitcast.35), channel_id=1, source_target_pairs={{0,2},{1,3},{2,0},{3,1},{4,6},{5,7},{6,4},{7,5},{8,10},{9,11},{10,... | collective-permute-start | bytes 20 | tf_op jit(solution)/shard_map/ppermute | solution.py:36
  63.1 1.2 %fusion.33 = f32[1,8,32,128]{3,2,1,0:T(8,128)S(1)} fusion(s32[8,32]{1,0:T(8,128)S(1)} %multiply_add_fusion, s32[2048]{0:T(1024)S(1)} %bitcast.161, f32[2048]{0:T(1024)S(1)} %bitcast.145, s32[2048]{0:T(1024)S(1)} %bitcast.152), kind=kOutput, calls=%fused_computation.22 | convolution fusion | flops 806354944 | bytes 156672 | tf_op jit(solution)/shard_map/srk,srz->skz/dot_general | solution.py:136
  65.0 0.1 fusion.98
  65.2 0.3 fusion.486
  65.5 2.1 %collective-permute-start.13 = (f32[1]{0:T(128)}, f32[1]{0:T(128)}, u32[]{:S(2)}, u32[]{:S(2)}) collective-permute-start(f32[1]{0:T(128)} %add.806), channel_id=1, source_target_pairs={{0,4},{1,5},{2,6},{3,7},{4,0},{5,1},{6,2},{7,3},{8,12},{9,13},{10,... | collective-permute-start | bytes 20 | tf_op jit(solution)/shard_map/ppermute | solution.py:36
  67.6 4.7 %collective-permute-start.11 = (f32[1,7,32,128]{3,2,1,0:T(8,128)S(1)}, f32[1,7,32,128]{3,2,1,0:T(8,128)S(1)}, u32[]{:S(2)}, u32[]{:S(2)}) collective-permute-start(f32[1,7,32,128]{3,2,1,0:T(8,128)S(1)} %get-tuple-element.78), channel_id=1, source_target_pairs={{0,1},{1,2},{2,3},{3,4},{4,5},{5,6},{6,7},{7,8},{8,9},{9,10},{10,1... | collective-permute-start | bytes 344072 | tf_op jit(solution)/shard_map/ppermute | solution.py:18
  72.4 1.9 %collective-permute-start.12 = (f32[1,7,32,128]{3,2,1,0:T(8,128)S(1)}, f32[1,7,32,128]{3,2,1,0:T(8,128)S(1)}, u32[]{:S(2)}, u32[]{:S(2)}) collective-permute-start(f32[1,7,32,128]{3,2,1,0:T(8,128)S(1)} %get-tuple-element.79), channel_id=1, source_target_pairs={{1,0},{2,1},{3,2},{4,3},{5,4},{6,5},{7,6},{8,7},{9,8},{10,9},{11,1... | collective-permute-start | bytes 344072 | tf_op jit(solution)/shard_map/ppermute | solution.py:19
  74.3 0.3 fusion.312
  74.6 1.2 %fusion.36 = f32[1,8,32,128]{3,2,1,0:T(8,128)S(1)} fusion(s32[8,32]{1,0:T(8,128)S(1)} %multiply_add_fusion, s32[2048]{0:T(1024)S(1)} %bitcast.162, f32[2048]{0:T(1024)S(1)} %bitcast.143, s32[2048]{0:T(1024)S(1)} %bitcast.153), kind=kOutput, calls=%fused_computation.23 | convolution fusion | flops 806354944 | bytes 156672 | tf_op jit(solution)/shard_map/srk,srz->skz/dot_general | solution.py:136
  76.4 2.1 %collective-permute-done.12 = f32[1,7,32,128]{3,2,1,0:T(8,128)S(1)} collective-permute-done((f32[1,7,32,128]{3,2,1,0:T(8,128)S(1)}, f32[1,7,32,128]{3,2,1,0:T(8,128)S(1)}, u32[]{:S(2)}, u32[]{:S(2)}) %collective-permute-start.12) | collective-permute-done | bytes 114720 | tf_op jit(solution)/shard_map/ppermute | solution.py:19
  78.5 0.1 fusion.91
  78.8 0.3 fusion.509
  79.1 3.1 %collective-permute-start.16 = (f32[1]{0:T(128)}, f32[1]{0:T(128)}, u32[]{:S(2)}, u32[]{:S(2)}) collective-permute-start(f32[1]{0:T(128)} %add.830), channel_id=1, source_target_pairs={{0,8},{1,9},{2,10},{3,11},{4,12},{5,13},{6,14},{7,15},{8,0},{9,1},... | collective-permute-start | bytes 20 | tf_op jit(solution)/shard_map/ppermute | solution.py:36
  82.2 2.6 %collective-permute-start.14 = (f32[1,7,32,128]{3,2,1,0:T(8,128)S(1)}, f32[1,7,32,128]{3,2,1,0:T(8,128)S(1)}, u32[]{:S(2)}, u32[]{:S(2)}) collective-permute-start(f32[1,7,32,128]{3,2,1,0:T(8,128)S(1)} %get-tuple-element.76), channel_id=1, source_target_pairs={{0,1},{1,2},{2,3},{3,4},{4,5},{5,6},{6,7},{7,8},{8,9},{9,10},{10,1... | collective-permute-start | bytes 344072 | tf_op jit(solution)/shard_map/ppermute | solution.py:18
  84.8 1.9 %collective-permute-start.15 = (f32[1,7,32,128]{3,2,1,0:T(8,128)S(1)}, f32[1,7,32,128]{3,2,1,0:T(8,128)S(1)}, u32[]{:S(2)}, u32[]{:S(2)}) collective-permute-start(f32[1,7,32,128]{3,2,1,0:T(8,128)S(1)} %get-tuple-element.77), channel_id=1, source_target_pairs={{1,0},{2,1},{3,2},{4,3},{5,4},{6,5},{7,6},{8,7},{9,8},{10,9},{11,1... | collective-permute-start | bytes 344072 | tf_op jit(solution)/shard_map/ppermute | solution.py:19
  86.8 0.3 fusion.336
  87.1 1.2 %fusion.39 = f32[1,8,32,128]{3,2,1,0:T(8,128)S(1)} fusion(s32[8,32]{1,0:T(8,128)S(1)} %multiply_add_fusion, s32[2048]{0:T(1024)S(1)} %bitcast.163, f32[2048]{0:T(1024)S(1)} %bitcast.141, s32[2048]{0:T(1024)S(1)} %bitcast.154), kind=kOutput, calls=%fused_computation.24 | convolution fusion | flops 806354944 | bytes 156672 | tf_op jit(solution)/shard_map/srk,srz->skz/dot_general | solution.py:136
  88.9 2.1 %collective-permute-done.15 = f32[1,7,32,128]{3,2,1,0:T(8,128)S(1)} collective-permute-done((f32[1,7,32,128]{3,2,1,0:T(8,128)S(1)}, f32[1,7,32,128]{3,2,1,0:T(8,128)S(1)}, u32[]{:S(2)}, u32[]{:S(2)}) %collective-permute-start.15) | collective-permute-done | bytes 114720 | tf_op jit(solution)/shard_map/ppermute | solution.py:19
  91.1 0.8 copy-done.4
  91.9 0.9 bitcast_multiply_fusion
  92.7 1.0 collective-permute-start.17
  93.7 0.3 collective-permute-done.17
  (56 shorter events, 1.0 us)
Async XLA Ops:
  0.6 3.3 %copy-start = (f32[8,32,128]{2,1,0:T(8,128)S(1)}, f32[8,32,128]{2,1,0:T(8,128)}, u32[]{:S(2)}) copy-start(f32[8,32,128]{2,1,0:T(8,128)} %param.11) | copy-start | bytes 393220
  0.6 3.3 %copy-start.1 = (f32[1,8,32,128]{3,2,1,0:T(8,128)S(1)}, f32[1,8,32,128]{3,2,1,0:T(8,128)}, u32[]{:S(2)}) copy-start(f32[1,8,32,128]{3,2,1,0:T(8,128)} %param.13) | copy-start | bytes 393220
  4.0 6.6 %copy-start.8 = (f32[1,4,2048]{2,1,0:T(4,128)S(1)}, f32[1,4,2048]{2,1,0:T(4,128)}, u32[]{:S(2)}) copy-start(f32[1,4,2048]{2,1,0:T(4,128)} %param.19) | copy-start | bytes 98308
  4.0 6.7 %copy-start.7 = (s32[1,2048]{1,0:T(1,128)S(1)}, s32[1,2048]{1,0:T(1,128)}, u32[]{:S(2)}) copy-start(s32[1,2048]{1,0:T(1,128)} %param.18) | copy-start | bytes 24580
  4.1 10.4 %collective-permute-start.1 = (f32[3,7,32,128]{3,2,1,0:T(8,128)S(1)}, f32[3,7,32,128]{3,2,1,0:T(8,128)S(1)}, u32[]{:S(2)}, u32[]{:S(2)}) collective-permute-start(f32[3,7,32,128]{3,2,1,0:T(8,128)S(1)} %get-tuple-element.58), channel_id=1, source_target_pairs={{1,0},{2,1},{3,2},{4,3},{5,4},{6,5},{7,6},{8,7},{9,8},{10,9},{11,1... | collective-permute-start | bytes 1032200 | tf_op jit(solution)/shard_map/ppermute | solution.py:19
  6.1 11.3 %collective-permute-start = (f32[3,7,32,128]{3,2,1,0:T(8,128)S(1)}, f32[3,7,32,128]{3,2,1,0:T(8,128)S(1)}, u32[]{:S(2)}, u32[]{:S(2)}) collective-permute-start(f32[3,7,32,128]{3,2,1,0:T(8,128)S(1)} %get-tuple-element.59), channel_id=1, source_target_pairs={{0,1},{1,2},{2,3},{3,4},{4,5},{5,6},{6,7},{7,8},{8,9},{9,10},{10,1... | collective-permute-start | bytes 1032200 | tf_op jit(solution)/shard_map/ppermute | solution.py:18
  12.0 2.0 %copy-start.9 = (f32[1,4]{1,0:T(1,128)S(1)}, f32[1,4]{1,0:T(1,128)}, u32[]{:S(2)}) copy-start(f32[1,4]{1,0:T(1,128)} %param.17) | copy-start | bytes 52
  17.5 0.9 copy-start.5
  19.7 8.4 %collective-permute-start.2 = (f32[1,7,32,128]{3,2,1,0:T(8,128)S(1)}, f32[1,7,32,128]{3,2,1,0:T(8,128)S(1)}, u32[]{:S(2)}, u32[]{:S(2)}) collective-permute-start(f32[1,7,32,128]{3,2,1,0:T(8,128)S(1)} %get-tuple-element.88), channel_id=1, source_target_pairs={{0,1},{1,2},{2,3},{3,4},{4,5},{5,6},{6,7},{7,8},{8,9},{9,10},{10,1... | collective-permute-start | bytes 344072 | tf_op jit(solution)/shard_map/ppermute | solution.py:18
  24.1 6.1 %collective-permute-start.3 = (f32[1,7,32,128]{3,2,1,0:T(8,128)S(1)}, f32[1,7,32,128]{3,2,1,0:T(8,128)S(1)}, u32[]{:S(2)}, u32[]{:S(2)}) collective-permute-start(f32[1,7,32,128]{3,2,1,0:T(8,128)S(1)} %get-tuple-element.89), channel_id=1, source_target_pairs={{1,0},{2,1},{3,2},{4,3},{5,4},{6,5},{7,6},{8,7},{9,8},{10,9},{11,1... | collective-permute-start | bytes 344072 | tf_op jit(solution)/shard_map/ppermute | solution.py:19
  31.5 6.3 %collective-permute-start.4 = (f32[1,7,32,128]{3,2,1,0:T(8,128)S(1)}, f32[1,7,32,128]{3,2,1,0:T(8,128)S(1)}, u32[]{:S(2)}, u32[]{:S(2)}) collective-permute-start(f32[1,7,32,128]{3,2,1,0:T(8,128)S(1)} %get-tuple-element.86), channel_id=1, source_target_pairs={{0,1},{1,2},{2,3},{3,4},{4,5},{5,6},{6,7},{7,8},{8,9},{9,10},{10,1... | collective-permute-start | bytes 344072 | tf_op jit(solution)/shard_map/ppermute | solution.py:18
  33.4 6.1 %collective-permute-start.5 = (f32[1,7,32,128]{3,2,1,0:T(8,128)S(1)}, f32[1,7,32,128]{3,2,1,0:T(8,128)S(1)}, u32[]{:S(2)}, u32[]{:S(2)}) collective-permute-start(f32[1,7,32,128]{3,2,1,0:T(8,128)S(1)} %get-tuple-element.87), channel_id=1, source_target_pairs={{1,0},{2,1},{3,2},{4,3},{5,4},{6,5},{7,6},{8,7},{9,8},{10,9},{11,1... | collective-permute-start | bytes 344072 | tf_op jit(solution)/shard_map/ppermute | solution.py:19
  41.0 6.3 %collective-permute-start.6 = (f32[1,7,32,128]{3,2,1,0:T(8,128)S(1)}, f32[1,7,32,128]{3,2,1,0:T(8,128)S(1)}, u32[]{:S(2)}, u32[]{:S(2)}) collective-permute-start(f32[1,7,32,128]{3,2,1,0:T(8,128)S(1)} %get-tuple-element.82), channel_id=1, source_target_pairs={{0,1},{1,2},{2,3},{3,4},{4,5},{5,6},{6,7},{7,8},{8,9},{9,10},{10,1... | collective-permute-start | bytes 344072 | tf_op jit(solution)/shard_map/ppermute | solution.py:18
  42.9 7.0 %collective-permute-start.7 = (f32[1,7,32,128]{3,2,1,0:T(8,128)S(1)}, f32[1,7,32,128]{3,2,1,0:T(8,128)S(1)}, u32[]{:S(2)}, u32[]{:S(2)}) collective-permute-start(f32[1,7,32,128]{3,2,1,0:T(8,128)S(1)} %get-tuple-element.83), channel_id=1, source_target_pairs={{1,0},{2,1},{3,2},{4,3},{5,4},{6,5},{7,6},{8,7},{9,8},{10,9},{11,1... | collective-permute-start | bytes 344072 | tf_op jit(solution)/shard_map/ppermute | solution.py:19
  49.9 0.9 copy-start.2
  49.9 1.0 %copy-start.6 = (f32[1,8,32,128]{3,2,1,0:T(8,128)S(1)}, f32[1,8,32,128]{3,2,1,0:T(8,128)}, u32[]{:S(2)}) copy-start(f32[1,8,32,128]{3,2,1,0:T(8,128)} %param.15) | copy-start | bytes 393220
  52.3 12.6 %collective-permute-start.8 = (f32[1,7,32,128]{3,2,1,0:T(8,128)S(1)}, f32[1,7,32,128]{3,2,1,0:T(8,128)S(1)}, u32[]{:S(2)}, u32[]{:S(2)}) collective-permute-start(f32[1,7,32,128]{3,2,1,0:T(8,128)S(1)} %get-tuple-element.80), channel_id=1, source_target_pairs={{0,1},{1,2},{2,3},{3,4},{4,5},{5,6},{6,7},{7,8},{8,9},{9,10},{10,1... | collective-permute-start | bytes 344072 | tf_op jit(solution)/shard_map/ppermute | solution.py:18
  54.2 10.7 %collective-permute-start.9 = (f32[1,7,32,128]{3,2,1,0:T(8,128)S(1)}, f32[1,7,32,128]{3,2,1,0:T(8,128)S(1)}, u32[]{:S(2)}, u32[]{:S(2)}) collective-permute-start(f32[1,7,32,128]{3,2,1,0:T(8,128)S(1)} %get-tuple-element.81), channel_id=1, source_target_pairs={{1,0},{2,1},{3,2},{4,3},{5,4},{6,5},{7,6},{8,7},{9,8},{10,9},{11,1... | collective-permute-start | bytes 344072 | tf_op jit(solution)/shard_map/ppermute | solution.py:19
  60.1 4.3 %collective-permute-start.10 = (f32[1]{0:T(128)}, f32[1]{0:T(128)}, u32[]{:S(2)}, u32[]{:S(2)}) collective-permute-start(f32[1]{0:T(128)} %bitcast.35), channel_id=1, source_target_pairs={{0,2},{1,3},{2,0},{3,1},{4,6},{5,7},{6,4},{7,5},{8,10},{9,11},{10,... | collective-permute-start | bytes 20 | tf_op jit(solution)/shard_map/ppermute | solution.py:36
  65.5 10.3 %collective-permute-start.13 = (f32[1]{0:T(128)}, f32[1]{0:T(128)}, u32[]{:S(2)}, u32[]{:S(2)}) collective-permute-start(f32[1]{0:T(128)} %add.806), channel_id=1, source_target_pairs={{0,4},{1,5},{2,6},{3,7},{4,0},{5,1},{6,2},{7,3},{8,12},{9,13},{10,... | collective-permute-start | bytes 20 | tf_op jit(solution)/shard_map/ppermute | solution.py:36
  67.6 8.8 %collective-permute-start.11 = (f32[1,7,32,128]{3,2,1,0:T(8,128)S(1)}, f32[1,7,32,128]{3,2,1,0:T(8,128)S(1)}, u32[]{:S(2)}, u32[]{:S(2)}) collective-permute-start(f32[1,7,32,128]{3,2,1,0:T(8,128)S(1)} %get-tuple-element.78), channel_id=1, source_target_pairs={{0,1},{1,2},{2,3},{3,4},{4,5},{5,6},{6,7},{7,8},{8,9},{9,10},{10,1... | collective-permute-start | bytes 344072 | tf_op jit(solution)/shard_map/ppermute | solution.py:18
  72.4 6.1 %collective-permute-start.12 = (f32[1,7,32,128]{3,2,1,0:T(8,128)S(1)}, f32[1,7,32,128]{3,2,1,0:T(8,128)S(1)}, u32[]{:S(2)}, u32[]{:S(2)}) collective-permute-start(f32[1,7,32,128]{3,2,1,0:T(8,128)S(1)} %get-tuple-element.79), channel_id=1, source_target_pairs={{1,0},{2,1},{3,2},{4,3},{5,4},{6,5},{7,6},{8,7},{9,8},{10,9},{11,1... | collective-permute-start | bytes 344072 | tf_op jit(solution)/shard_map/ppermute | solution.py:19
  78.7 12.4 %copy-start.3 = (f32[1,8,32,128]{3,2,1,0:T(8,128)}, f32[1,8,32,128]{3,2,1,0:T(8,128)S(1)}, u32[]{:S(2)}) copy-start(f32[1,8,32,128]{3,2,1,0:T(8,128)S(1)} %fusion.543) | copy-start | bytes 393220
  79.1 9.2 %collective-permute-start.16 = (f32[1]{0:T(128)}, f32[1]{0:T(128)}, u32[]{:S(2)}, u32[]{:S(2)}) collective-permute-start(f32[1]{0:T(128)} %add.830), channel_id=1, source_target_pairs={{0,8},{1,9},{2,10},{3,11},{4,12},{5,13},{6,14},{7,15},{8,0},{9,1},... | collective-permute-start | bytes 20 | tf_op jit(solution)/shard_map/ppermute | solution.py:36
  82.2 6.7 %collective-permute-start.14 = (f32[1,7,32,128]{3,2,1,0:T(8,128)S(1)}, f32[1,7,32,128]{3,2,1,0:T(8,128)S(1)}, u32[]{:S(2)}, u32[]{:S(2)}) collective-permute-start(f32[1,7,32,128]{3,2,1,0:T(8,128)S(1)} %get-tuple-element.76), channel_id=1, source_target_pairs={{0,1},{1,2},{2,3},{3,4},{4,5},{5,6},{6,7},{7,8},{8,9},{9,10},{10,1... | collective-permute-start | bytes 344072 | tf_op jit(solution)/shard_map/ppermute | solution.py:18
  84.8 6.1 %collective-permute-start.15 = (f32[1,7,32,128]{3,2,1,0:T(8,128)S(1)}, f32[1,7,32,128]{3,2,1,0:T(8,128)S(1)}, u32[]{:S(2)}, u32[]{:S(2)}) collective-permute-start(f32[1,7,32,128]{3,2,1,0:T(8,128)S(1)} %get-tuple-element.77), channel_id=1, source_target_pairs={{1,0},{2,1},{3,2},{4,3},{5,4},{6,5},{7,6},{8,7},{9,8},{10,9},{11,1... | collective-permute-start | bytes 344072 | tf_op jit(solution)/shard_map/ppermute | solution.py:19
  91.0 0.9 copy-start.4
  92.7 1.3 %collective-permute-start.17 = (f32[1]{0:T(128)}, f32[1]{0:T(128)}, u32[]{:S(2)}, u32[]{:S(2)}) collective-permute-start(f32[1]{0:T(128)} %add.854), channel_id=1, source_target_pairs={{0,1},{1,0},{2,3},{3,2},{4,5},{5,4},{6,7},{7,6},{8,9},{9,8},{10,11... | collective-permute-start | bytes 20 | tf_op jit(solution)/shard_map/ppermute | solution.py:36

commit v15 on v14

--- a/solution.py
+++ b/solution.py
@@ -172,15 +172,12 @@
                 misfit = butterfly_round(misfit, "mp", distances.pop(0))
             state = 2.0 * mu_near + lap - mu_far + injected(resid)
         else:
+            lap, (resid, misfit) = operator(kappa * mu_near, (resids[level - 1], misfit))
             if distances:
-                mu_near, misfit = lax.optimization_barrier((mu_near, misfit))
                 misfit = butterfly_round(misfit, "mp", distances.pop(0))
-            lap, resid = operator(kappa * mu_near, resids[level - 1])
             state = 2.0 * mu_near + lap - mu_far + injected(resid)
         gradient = gradient + state * laps[level - 1]
         mu_far, mu_near = (mu_near, state)
-        if level < STEPS:
-            mu_near, misfit = lax.optimization_barrier((mu_near, misfit))
     for distance in distances:
         misfit = butterfly_round(misfit, "mp", distance)
     velocity_gradient = 2.0 * velocity / buoyancy * jnp.sum(gradient, axis=0)

time: 96.8 us -> 97.3 us (level)
  starting transfers between devices: 46.3 us -> 51 us
  waiting for transfers between devices: 13.8 us -> 9.38 us
    ppermute x4, starting transfers between devices: 9.17 us -> 13.4 us  [butterfly_round(): return values + lax.ppermute(values, axis, pairs)]
    ppermute x7, waiting for transfers between devices: 10.6 us -> 6.48 us  [extended(): after = lax.ppermute(first, 'mp', down)]
  transfers between devices with their start and end apart: 18 -> 18, of which waited for: 7 -> 4; matrix products, arithmetic and copies ran while one was open for 17% -> 17% of each run, Pallas kernels for 0% -> 0%
where the time goes in v15:
time: 97.3 us; the launch traced here: 96.3 us
  starting transfers between devices  51 us (52%)
  other arithmetic  13.7 us (14%)
  matrix products  12.6 us (13%)
  waiting for transfers between devices  9.38 us (10%)
  between operations  6.49 us (7%)
  local copies, waits for them, and re-layouts  3.22 us (3%)
    ppermute x7, starting transfers between devices, extended(): before = lax.ppermute(last, 'mp', up)  22.5 us
    ppermute x7, starting transfers between devices, extended(): after = lax.ppermute(first, 'mp', down)  15.1 us
    ppermute x4, starting transfers between devices, butterfly_round(): return values + lax.ppermute(values, axis, pairs)  13.4 us
    ppermute x7, waiting for transfers between devices, extended(): after = lax.ppermute(first, 'mp', down)  6.48 us
    dot_general x4, matrix products, sample(): jnp.einsum('srk,skz->srz', row_pick, field.reshape(shots, rows, cz), prec...  6.43 us
    dot_general x5, matrix products, injected(): jnp.einsum('srk,srz->skz', row_pick, spread, precision=lax.Precision.HIGH...  6.18 us
    mul x7, other arithmetic, cross_terms(): flux = buoyancy * forward_diff(pad_axis(values, axis), axis, length)  5.34 us
    ppermute x7, waiting for transfers between devices, extended(): before = lax.ppermute(last, 'mp', up)  2.9 us
  transfers between devices with their start and end apart: 18, of which 4 were waited for; matrix products, arithmetic and copies ran while one was open for 17% of the time, Pallas kernels for 0%

profile of v15, /device:TPU:1, one launch (start us, length us, event | category | flops | bytes accessed | tf_op | source)
XLA Modules:
  0.0 96.3 jit_solution(16128415588516195718)
XLA Ops:
  0.7 3.2 %fusion.179 = (f32[1,8,32,128]{3,2,1,0:T(8,128)S(1)}, f32[1,8,32,128]{3,2,1,0:T(8,128)S(1)}, f32[1,8,32,128]{3,2,1,0:T(8,128)S(1)}, f32[8,32,128]{2,1,0:T(8,128)S(1)}) fusion(f32[1,8,32,128]{3,2,1,0:T(8,128)} %param.13, f32[8,32,128]{2,1,0:T(8,128)} %param.11, f32[1,8,32,128]{3,2,1,0:T(8,128)} %param.14, f32[8,32,128]{2,1,0:T(8,128)} %param.10), kind=kLoop, calls=%fused_computation.432 | loop fusion | flops 884736 | bytes 1048576 | tf_op jit(solution)/shard_map/mul | solution.py:69
  4.1 2.0 %collective-permute-start.1 = (f32[3,7,32,128]{3,2,1,0:T(8,128)S(1)}, f32[3,7,32,128]{3,2,1,0:T(8,128)S(1)}, u32[]{:S(2)}, u32[]{:S(2)}) collective-permute-start(f32[3,7,32,128]{3,2,1,0:T(8,128)S(1)} %get-tuple-element.54), channel_id=1, source_target_pairs={{1,0},{2,1},{3,2},{4,3},{5,4},{6,5},{7,6},{8,7},{9,8},{10,9},{11,1... | collective-permute-start | bytes 1032200 | tf_op jit(solution)/shard_map/ppermute | solution.py:19
  6.0 4.5 %collective-permute-start = (f32[3,7,32,128]{3,2,1,0:T(8,128)S(1)}, f32[3,7,32,128]{3,2,1,0:T(8,128)S(1)}, u32[]{:S(2)}, u32[]{:S(2)}) collective-permute-start(f32[3,7,32,128]{3,2,1,0:T(8,128)S(1)} %get-tuple-element.55), channel_id=1, source_target_pairs={{0,1},{1,2},{2,3},{3,4},{4,5},{5,6},{6,7},{7,8},{8,9},{9,10},{10,1... | collective-permute-start | bytes 1032200 | tf_op jit(solution)/shard_map/ppermute | solution.py:18
  10.7 1.2 %fusion.30 = f32[1,8,32,128]{3,2,1,0:T(8,128)S(1)} fusion(s32[8,32]{1,0:T(8,128)S(1)} %multiply_add_fusion, s32[2048]{0:T(1024)S(1)} %bitcast.155, f32[2048]{0:T(1024)S(1)} %bitcast.167, s32[2048]{0:T(1024)S(1)} %bitcast.146), kind=kOutput, calls=%fused_computation.21 | convolution fusion | flops 806354944 | bytes 156672 | tf_op jit(solution)/shard_map/srk,srz->skz/dot_general | solution.py:136
  11.9 1.3 %fusion.27 = f32[1,8,32,128]{3,2,1,0:T(8,128)S(1)} fusion(s32[8,32]{1,0:T(8,128)S(1)} %multiply_add_fusion, s32[2048]{0:T(1024)S(1)} %bitcast.156, s32[2048]{0:T(1024)S(1)} %bitcast.147), kind=kOutput, calls=%fused_computation.20 | convolution fusion | flops 806354944 | bytes 148480 | tf_op jit(solution)/shard_map/srk,srz->skz/dot_general | solution.py:136
  13.9 0.6 fusion.635
  14.5 2.9 %collective-permute-done = f32[3,7,32,128]{3,2,1,0:T(8,128)S(1)} collective-permute-done((f32[3,7,32,128]{3,2,1,0:T(8,128)S(1)}, f32[3,7,32,128]{3,2,1,0:T(8,128)S(1)}, u32[]{:S(2)}, u32[]{:S(2)}) %collective-permute-start) | collective-permute-done | bytes 344096 | tf_op jit(solution)/shard_map/ppermute | solution.py:18
  17.5 0.1 fusion.126
  17.6 0.8 copy-done.5
  18.4 1.0 %fusion.599 = (f32[1,8,32,128]{3,2,1,0:T(8,128)S(1)}, f32[1,8,32,128]{3,2,1,0:T(8,128)S(1)}) fusion(f32[8,32,128]{2,1,0:T(8,128)S(1)} %get-tuple-element.87, f32[1,8,32,128]{3,2,1,0:T(8,128)S(1)} %copy-done.5, f32[1,8,32,128]{3,2,1,0:T(8,128)S(1)} %copy-done.1, f32[]{:T(128)} %bitcast.8, s32[]{:T(128)} %bitcast.7, s32[32]{0:T(128)S(1)} %iota_multiply_fusion, ...), kind=kLoop, calls=%fused_computation.893 | loop fusion | flops 1441792 | bytes 1966248 | tf_op jit(solution)/shard_map/add | solution.py:155
  19.4 0.3 fusion.394
  19.7 4.4 %collective-permute-start.2 = (f32[1,7,32,128]{3,2,1,0:T(8,128)S(1)}, f32[1,7,32,128]{3,2,1,0:T(8,128)S(1)}, u32[]{:S(2)}, u32[]{:S(2)}) collective-permute-start(f32[1,7,32,128]{3,2,1,0:T(8,128)S(1)} %get-tuple-element.84), channel_id=1, source_target_pairs={{0,1},{1,2},{2,3},{3,4},{4,5},{5,6},{6,7},{7,8},{8,9},{9,10},{10,1... | collective-permute-start | bytes 344072 | tf_op jit(solution)/shard_map/ppermute | solution.py:18
  24.1 1.9 %collective-permute-start.3 = (f32[1,7,32,128]{3,2,1,0:T(8,128)S(1)}, f32[1,7,32,128]{3,2,1,0:T(8,128)S(1)}, u32[]{:S(2)}, u32[]{:S(2)}) collective-permute-start(f32[1,7,32,128]{3,2,1,0:T(8,128)S(1)} %get-tuple-element.85), channel_id=1, source_target_pairs={{1,0},{2,1},{3,2},{4,3},{5,4},{6,5},{7,6},{8,7},{9,8},{10,9},{11,1... | collective-permute-start | bytes 344072 | tf_op jit(solution)/shard_map/ppermute | solution.py:19
  26.0 0.3 fusion.216
  26.3 0.1 fusion.134
  26.4 1.6 %fusion.21 = f32[2048]{0:T(1024)S(1)} fusion(f32[256,128]{1,0:T(8,128)S(1)} %bitcast.137, s32[2048]{0:T(1024)S(1)} %bitcast.157, s32[2048]{0:T(1024)S(1)} %bitcast.148), kind=kOutput, calls=%fused_computation.18 | convolution fusion | flops 806615040 | bytes 155648 | tf_op jit(solution)/shard_map/srk,skz->srz/dot_general | solution.py:129
  28.1 2.1 %collective-permute-done.3 = f32[1,7,32,128]{3,2,1,0:T(8,128)S(1)} collective-permute-done((f32[1,7,32,128]{3,2,1,0:T(8,128)S(1)}, f32[1,7,32,128]{3,2,1,0:T(8,128)S(1)}, u32[]{:S(2)}, u32[]{:S(2)}) %collective-permute-start.3) | collective-permute-done | bytes 114720 | tf_op jit(solution)/shard_map/ppermute | solution.py:19
  30.2 0.1 fusion.119
  30.3 0.8 fusion.601
  31.1 0.3 fusion.417
  31.4 1.9 %collective-permute-start.4 = (f32[1,7,32,128]{3,2,1,0:T(8,128)S(1)}, f32[1,7,32,128]{3,2,1,0:T(8,128)S(1)}, u32[]{:S(2)}, u32[]{:S(2)}) collective-permute-start(f32[1,7,32,128]{3,2,1,0:T(8,128)S(1)} %get-tuple-element.82), channel_id=1, source_target_pairs={{0,1},{1,2},{2,3},{3,4},{4,5},{5,6},{6,7},{7,8},{8,9},{9,10},{10,1... | collective-permute-start | bytes 344072 | tf_op jit(solution)/shard_map/ppermute | solution.py:18
  33.4 2.4 %collective-permute-start.5 = (f32[1,7,32,128]{3,2,1,0:T(8,128)S(1)}, f32[1,7,32,128]{3,2,1,0:T(8,128)S(1)}, u32[]{:S(2)}, u32[]{:S(2)}) collective-permute-start(f32[1,7,32,128]{3,2,1,0:T(8,128)S(1)} %get-tuple-element.83), channel_id=1, source_target_pairs={{1,0},{2,1},{3,2},{4,3},{5,4},{6,5},{7,6},{8,7},{9,8},{10,9},{11,1... | collective-permute-start | bytes 344072 | tf_op jit(solution)/shard_map/ppermute | solution.py:19
  35.8 0.3 fusion.240
  36.1 1.6 %fusion.18 = f32[2048]{0:T(1024)S(1)} fusion(f32[256,128]{1,0:T(8,128)S(1)} %bitcast.136, s32[2048]{0:T(1024)S(1)} %bitcast.158, s32[2048]{0:T(1024)S(1)} %bitcast.149), kind=kOutput, calls=%fused_computation.17 | convolution fusion | flops 806615040 | bytes 155648 | tf_op jit(solution)/shard_map/srk,skz->srz/dot_general | solution.py:129
  37.7 1.8 %collective-permute-done.5 = f32[1,7,32,128]{3,2,1,0:T(8,128)S(1)} collective-permute-done((f32[1,7,32,128]{3,2,1,0:T(8,128)S(1)}, f32[1,7,32,128]{3,2,1,0:T(8,128)S(1)}, u32[]{:S(2)}, u32[]{:S(2)}) %collective-permute-start.5) | collective-permute-done | bytes 114720 | tf_op jit(solution)/shard_map/ppermute | solution.py:19
  39.5 0.1 fusion.112
  39.6 0.8 fusion.603
  40.4 0.5 fusion.440
  40.9 1.9 %collective-permute-start.6 = (f32[1,7,32,128]{3,2,1,0:T(8,128)S(1)}, f32[1,7,32,128]{3,2,1,0:T(8,128)S(1)}, u32[]{:S(2)}, u32[]{:S(2)}) collective-permute-start(f32[1,7,32,128]{3,2,1,0:T(8,128)S(1)} %get-tuple-element.78), channel_id=1, source_target_pairs={{0,1},{1,2},{2,3},{3,4},{4,5},{5,6},{6,7},{7,8},{8,9},{9,10},{10,1... | collective-permute-start | bytes 344072 | tf_op jit(solution)/shard_map/ppermute | solution.py:18
  42.9 2.4 %collective-permute-start.7 = (f32[1,7,32,128]{3,2,1,0:T(8,128)S(1)}, f32[1,7,32,128]{3,2,1,0:T(8,128)S(1)}, u32[]{:S(2)}, u32[]{:S(2)}) collective-permute-start(f32[1,7,32,128]{3,2,1,0:T(8,128)S(1)} %get-tuple-element.79), channel_id=1, source_target_pairs={{1,0},{2,1},{3,2},{4,3},{5,4},{6,5},{7,6},{8,7},{9,8},{10,9},{11,1... | collective-permute-start | bytes 344072 | tf_op jit(solution)/shard_map/ppermute | solution.py:19
  45.3 0.3 fusion.264
  45.6 1.6 %fusion.15 = f32[2048]{0:T(1024)S(1)} fusion(f32[256,128]{1,0:T(8,128)S(1)} %bitcast.138, s32[2048]{0:T(1024)S(1)} %bitcast.159, s32[2048]{0:T(1024)S(1)} %bitcast.150), kind=kOutput, calls=%fused_computation.16 | convolution fusion | flops 806615040 | bytes 155648 | tf_op jit(solution)/shard_map/srk,skz->srz/dot_general | solution.py:129
  47.2 2.6 %collective-permute-done.7 = f32[1,7,32,128]{3,2,1,0:T(8,128)S(1)} collective-permute-done((f32[1,7,32,128]{3,2,1,0:T(8,128)S(1)}, f32[1,7,32,128]{3,2,1,0:T(8,128)S(1)}, u32[]{:S(2)}, u32[]{:S(2)}) %collective-permute-start.7) | collective-permute-done | bytes 114720 | tf_op jit(solution)/shard_map/ppermute | solution.py:19
  49.9 0.1 fusion.105
  50.0 0.8 copy-done.2
  50.8 1.0 %bitcast_multiply_fusion.3 = (f32[1,8,32,128]{3,2,1,0:T(8,128)S(1)}, f32[1,8,32,128]{3,2,1,0:T(8,128)S(1)}, f32[1,8,32,128]{3,2,1,0:T(8,128)S(1)}, f32[1,8,32,128]{3,2,1,0:T(8,128)S(1)}) fusion(f32[8,32,128]{2,1,0:T(8,128)S(1)} %get-tuple-element.87, f32[1,8,32,128]{3,2,1,0:T(8,128)S(1)} %fusion.30, f32[1,8,32,128]{3,2,1,0:T(8,128)S(1)} %fusion.27, ...), kind=kLoop, calls=%fused_computation.886 | loop fusion | flops 2064384 | bytes 3932328 | tf_op jit(solution)/shard_map/mul | solution.py:166
  51.9 0.3 fusion.463
  52.2 1.9 %collective-permute-start.8 = (f32[1,7,32,128]{3,2,1,0:T(8,128)S(1)}, f32[1,7,32,128]{3,2,1,0:T(8,128)S(1)}, u32[]{:S(2)}, u32[]{:S(2)}) collective-permute-start(f32[1,7,32,128]{3,2,1,0:T(8,128)S(1)} %get-tuple-element.76), channel_id=1, source_target_pairs={{0,1},{1,2},{2,3},{3,4},{4,5},{5,6},{6,7},{7,8},{8,9},{9,10},{10,1... | collective-permute-start | bytes 344072 | tf_op jit(solution)/shard_map/ppermute | solution.py:18
  54.1 2.6 %collective-permute-start.9 = (f32[1,7,32,128]{3,2,1,0:T(8,128)S(1)}, f32[1,7,32,128]{3,2,1,0:T(8,128)S(1)}, u32[]{:S(2)}, u32[]{:S(2)}) collective-permute-start(f32[1,7,32,128]{3,2,1,0:T(8,128)S(1)} %get-tuple-element.77), channel_id=1, source_target_pairs={{1,0},{2,1},{3,2},{4,3},{5,4},{6,5},{7,6},{8,7},{9,8},{10,9},{11,1... | collective-permute-start | bytes 344072 | tf_op jit(solution)/shard_map/ppermute | solution.py:19
  56.7 0.3 fusion.288
  57.0 1.6 %fusion.24 = f32[2048]{0:T(1024)S(1)} fusion(f32[256,128]{1,0:T(8,128)S(1)} %bitcast.139, s32[2048]{0:T(1024)S(1)} %bitcast.160, s32[2048]{0:T(1024)S(1)} %bitcast.151), kind=kOutput, calls=%fused_computation.19 | convolution fusion | flops 806615040 | bytes 155648 | tf_op jit(solution)/shard_map/srk,skz->srz/dot_general | solution.py:129
  58.7 0.6 fusion.606
  60.0 3.0 %collective-permute-start.12 = (f32[1]{0:T(128)}, f32[1]{0:T(128)}, u32[]{:S(2)}, u32[]{:S(2)}) collective-permute-start(f32[1]{0:T(128)} %bitcast.35), channel_id=1, source_target_pairs={{0,2},{1,3},{2,0},{3,1},{4,6},{5,7},{6,4},{7,5},{8,10},{9,11},{10,... | collective-permute-start | bytes 20 | tf_op jit(solution)/shard_map/ppermute | solution.py:36
  63.0 1.2 %fusion.33 = f32[1,8,32,128]{3,2,1,0:T(8,128)S(1)} fusion(s32[8,32]{1,0:T(8,128)S(1)} %multiply_add_fusion, s32[2048]{0:T(1024)S(1)} %bitcast.161, f32[2048]{0:T(1024)S(1)} %bitcast.145, s32[2048]{0:T(1024)S(1)} %bitcast.152), kind=kOutput, calls=%fused_computation.22 | convolution fusion | flops 806354944 | bytes 156672 | tf_op jit(solution)/shard_map/srk,srz->skz/dot_general | solution.py:136
  65.0 0.1 fusion.98
  65.1 0.1 bitcast_multiply_fusion.2
  65.2 0.3 fusion.486
  65.6 3.3 %collective-permute-start.10 = (f32[1,7,32,128]{3,2,1,0:T(8,128)S(1)}, f32[1,7,32,128]{3,2,1,0:T(8,128)S(1)}, u32[]{:S(2)}, u32[]{:S(2)}) collective-permute-start(f32[1,7,32,128]{3,2,1,0:T(8,128)S(1)} %get-tuple-element.74), channel_id=1, source_target_pairs={{0,1},{1,2},{2,3},{3,4},{4,5},{5,6},{6,7},{7,8},{8,9},{9,10},{10,1... | collective-permute-start | bytes 344072 | tf_op jit(solution)/shard_map/ppermute | solution.py:18
  68.9 1.9 %collective-permute-start.11 = (f32[1,7,32,128]{3,2,1,0:T(8,128)S(1)}, f32[1,7,32,128]{3,2,1,0:T(8,128)S(1)}, u32[]{:S(2)}, u32[]{:S(2)}) collective-permute-start(f32[1,7,32,128]{3,2,1,0:T(8,128)S(1)} %get-tuple-element.75), channel_id=1, source_target_pairs={{1,0},{2,1},{3,2},{4,3},{5,4},{6,5},{7,6},{8,7},{9,8},{10,9},{11,1... | collective-permute-start | bytes 344072 | tf_op jit(solution)/shard_map/ppermute | solution.py:19
  70.8 0.3 fusion.312
  71.1 2.6 %collective-permute-start.15 = (f32[1]{0:T(128)}, f32[1]{0:T(128)}, u32[]{:S(2)}, u32[]{:S(2)}) collective-permute-start(f32[1]{0:T(128)} %add.825), channel_id=1, source_target_pairs={{0,4},{1,5},{2,6},{3,7},{4,0},{5,1},{6,2},{7,3},{8,12},{9,13},{10,... | collective-permute-start | bytes 20 | tf_op jit(solution)/shard_map/ppermute | solution.py:36
  73.8 1.2 %fusion.36 = f32[1,8,32,128]{3,2,1,0:T(8,128)S(1)} fusion(s32[8,32]{1,0:T(8,128)S(1)} %multiply_add_fusion, s32[2048]{0:T(1024)S(1)} %bitcast.162, f32[2048]{0:T(1024)S(1)} %bitcast.143, s32[2048]{0:T(1024)S(1)} %bitcast.153), kind=kOutput, calls=%fused_computation.23 | convolution fusion | flops 806354944 | bytes 156672 | tf_op jit(solution)/shard_map/srk,srz->skz/dot_general | solution.py:136
  75.8 0.1 fusion.91
  75.9 0.1 bitcast_multiply_fusion.1
  76.0 0.3 fusion.509
  76.3 4.5 %collective-permute-start.13 = (f32[1,7,32,128]{3,2,1,0:T(8,128)S(1)}, f32[1,7,32,128]{3,2,1,0:T(8,128)S(1)}, u32[]{:S(2)}, u32[]{:S(2)}) collective-permute-start(f32[1,7,32,128]{3,2,1,0:T(8,128)S(1)} %get-tuple-element.72), channel_id=1, source_target_pairs={{0,1},{1,2},{2,3},{3,4},{4,5},{5,6},{6,7},{7,8},{8,9},{9,10},{10,1... | collective-permute-start | bytes 344072 | tf_op jit(solution)/shard_map/ppermute | solution.py:18
  80.8 1.9 %collective-permute-start.14 = (f32[1,7,32,128]{3,2,1,0:T(8,128)S(1)}, f32[1,7,32,128]{3,2,1,0:T(8,128)S(1)}, u32[]{:S(2)}, u32[]{:S(2)}) collective-permute-start(f32[1,7,32,128]{3,2,1,0:T(8,128)S(1)} %get-tuple-element.73), channel_id=1, source_target_pairs={{1,0},{2,1},{3,2},{4,3},{5,4},{6,5},{7,6},{8,7},{9,8},{10,9},{11,1... | collective-permute-start | bytes 344072 | tf_op jit(solution)/shard_map/ppermute | solution.py:19
  82.8 0.3 fusion.336
  83.1 3.3 %collective-permute-start.16 = (f32[1]{0:T(128)}, f32[1]{0:T(128)}, u32[]{:S(2)}, u32[]{:S(2)}) collective-permute-start(f32[1]{0:T(128)} %add.849), channel_id=1, source_target_pairs={{0,8},{1,9},{2,10},{3,11},{4,12},{5,13},{6,14},{7,15},{8,0},{9,1},... | collective-permute-start | bytes 20 | tf_op jit(solution)/shard_map/ppermute | solution.py:36
  86.4 1.2 %fusion.39 = f32[1,8,32,128]{3,2,1,0:T(8,128)S(1)} fusion(s32[8,32]{1,0:T(8,128)S(1)} %multiply_add_fusion, s32[2048]{0:T(1024)S(1)} %bitcast.163, f32[2048]{0:T(1024)S(1)} %bitcast.141, s32[2048]{0:T(1024)S(1)} %bitcast.154), kind=kOutput, calls=%fused_computation.24 | convolution fusion | flops 806354944 | bytes 156672 | tf_op jit(solution)/shard_map/srk,srz->skz/dot_general | solution.py:136
  88.3 4.4 %collective-permute-start.17 = (f32[1]{0:T(128)}, f32[1]{0:T(128)}, u32[]{:S(2)}, u32[]{:S(2)}) collective-permute-start(f32[1]{0:T(128)} %add.854), channel_id=1, source_target_pairs={{0,1},{1,0},{2,3},{3,2},{4,5},{5,4},{6,7},{7,6},{8,9},{9,8},{10,11... | collective-permute-start | bytes 20 | tf_op jit(solution)/shard_map/ppermute | solution.py:36
  93.4 0.1 fusion.84
  93.6 0.8 copy-done.3
  94.3 0.9 bitcast_multiply_fusion
  (54 shorter events, 0.7 us)
Async XLA Ops:
  0.6 3.3 %copy-start = (f32[8,32,128]{2,1,0:T(8,128)S(1)}, f32[8,32,128]{2,1,0:T(8,128)}, u32[]{:S(2)}) copy-start(f32[8,32,128]{2,1,0:T(8,128)} %param.11) | copy-start | bytes 393220
  0.6 3.3 %copy-start.1 = (f32[1,8,32,128]{3,2,1,0:T(8,128)S(1)}, f32[1,8,32,128]{3,2,1,0:T(8,128)}, u32[]{:S(2)}) copy-start(f32[1,8,32,128]{3,2,1,0:T(8,128)} %param.13) | copy-start | bytes 393220
  3.9 6.6 %copy-start.8 = (f32[1,4,2048]{2,1,0:T(4,128)S(1)}, f32[1,4,2048]{2,1,0:T(4,128)}, u32[]{:S(2)}) copy-start(f32[1,4,2048]{2,1,0:T(4,128)} %param.19) | copy-start | bytes 98308
  3.9 6.7 %copy-start.7 = (s32[1,2048]{1,0:T(1,128)S(1)}, s32[1,2048]{1,0:T(1,128)}, u32[]{:S(2)}) copy-start(s32[1,2048]{1,0:T(1,128)} %param.18) | copy-start | bytes 24580
  4.1 10.4 %collective-permute-start.1 = (f32[3,7,32,128]{3,2,1,0:T(8,128)S(1)}, f32[3,7,32,128]{3,2,1,0:T(8,128)S(1)}, u32[]{:S(2)}, u32[]{:S(2)}) collective-permute-start(f32[3,7,32,128]{3,2,1,0:T(8,128)S(1)} %get-tuple-element.54), channel_id=1, source_target_pairs={{1,0},{2,1},{3,2},{4,3},{5,4},{6,5},{7,6},{8,7},{9,8},{10,9},{11,1... | collective-permute-start | bytes 1032200 | tf_op jit(solution)/shard_map/ppermute | solution.py:19
  6.0 11.3 %collective-permute-start = (f32[3,7,32,128]{3,2,1,0:T(8,128)S(1)}, f32[3,7,32,128]{3,2,1,0:T(8,128)S(1)}, u32[]{:S(2)}, u32[]{:S(2)}) collective-permute-start(f32[3,7,32,128]{3,2,1,0:T(8,128)S(1)} %get-tuple-element.55), channel_id=1, source_target_pairs={{0,1},{1,2},{2,3},{3,4},{4,5},{5,6},{6,7},{7,8},{8,9},{9,10},{10,1... | collective-permute-start | bytes 1032200 | tf_op jit(solution)/shard_map/ppermute | solution.py:18
  11.9 2.0 %copy-start.9 = (f32[1,4]{1,0:T(1,128)S(1)}, f32[1,4]{1,0:T(1,128)}, u32[]{:S(2)}) copy-start(f32[1,4]{1,0:T(1,128)} %param.17) | copy-start | bytes 52
  17.5 0.9 copy-start.5
  19.7 8.4 %collective-permute-start.2 = (f32[1,7,32,128]{3,2,1,0:T(8,128)S(1)}, f32[1,7,32,128]{3,2,1,0:T(8,128)S(1)}, u32[]{:S(2)}, u32[]{:S(2)}) collective-permute-start(f32[1,7,32,128]{3,2,1,0:T(8,128)S(1)} %get-tuple-element.84), channel_id=1, source_target_pairs={{0,1},{1,2},{2,3},{3,4},{4,5},{5,6},{6,7},{7,8},{8,9},{9,10},{10,1... | collective-permute-start | bytes 344072 | tf_op jit(solution)/shard_map/ppermute | solution.py:18
  24.1 6.1 %collective-permute-start.3 = (f32[1,7,32,128]{3,2,1,0:T(8,128)S(1)}, f32[1,7,32,128]{3,2,1,0:T(8,128)S(1)}, u32[]{:S(2)}, u32[]{:S(2)}) collective-permute-start(f32[1,7,32,128]{3,2,1,0:T(8,128)S(1)} %get-tuple-element.85), channel_id=1, source_target_pairs={{1,0},{2,1},{3,2},{4,3},{5,4},{6,5},{7,6},{8,7},{9,8},{10,9},{11,1... | collective-permute-start | bytes 344072 | tf_op jit(solution)/shard_map/ppermute | solution.py:19
  31.4 6.3 %collective-permute-start.4 = (f32[1,7,32,128]{3,2,1,0:T(8,128)S(1)}, f32[1,7,32,128]{3,2,1,0:T(8,128)S(1)}, u32[]{:S(2)}, u32[]{:S(2)}) collective-permute-start(f32[1,7,32,128]{3,2,1,0:T(8,128)S(1)} %get-tuple-element.82), channel_id=1, source_target_pairs={{0,1},{1,2},{2,3},{3,4},{4,5},{5,6},{6,7},{7,8},{8,9},{9,10},{10,1... | collective-permute-start | bytes 344072 | tf_op jit(solution)/shard_map/ppermute | solution.py:18
  33.4 6.1 %collective-permute-start.5 = (f32[1,7,32,128]{3,2,1,0:T(8,128)S(1)}, f32[1,7,32,128]{3,2,1,0:T(8,128)S(1)}, u32[]{:S(2)}, u32[]{:S(2)}) collective-permute-start(f32[1,7,32,128]{3,2,1,0:T(8,128)S(1)} %get-tuple-element.83), channel_id=1, source_target_pairs={{1,0},{2,1},{3,2},{4,3},{5,4},{6,5},{7,6},{8,7},{9,8},{10,9},{11,1... | collective-permute-start | bytes 344072 | tf_op jit(solution)/shard_map/ppermute | solution.py:19
  40.9 6.3 %collective-permute-start.6 = (f32[1,7,32,128]{3,2,1,0:T(8,128)S(1)}, f32[1,7,32,128]{3,2,1,0:T(8,128)S(1)}, u32[]{:S(2)}, u32[]{:S(2)}) collective-permute-start(f32[1,7,32,128]{3,2,1,0:T(8,128)S(1)} %get-tuple-element.78), channel_id=1, source_target_pairs={{0,1},{1,2},{2,3},{3,4},{4,5},{5,6},{6,7},{7,8},{8,9},{9,10},{10,1... | collective-permute-start | bytes 344072 | tf_op jit(solution)/shard_map/ppermute | solution.py:18
  42.9 7.0 %collective-permute-start.7 = (f32[1,7,32,128]{3,2,1,0:T(8,128)S(1)}, f32[1,7,32,128]{3,2,1,0:T(8,128)S(1)}, u32[]{:S(2)}, u32[]{:S(2)}) collective-permute-start(f32[1,7,32,128]{3,2,1,0:T(8,128)S(1)} %get-tuple-element.79), channel_id=1, source_target_pairs={{1,0},{2,1},{3,2},{4,3},{5,4},{6,5},{7,6},{8,7},{9,8},{10,9},{11,1... | collective-permute-start | bytes 344072 | tf_op jit(solution)/shard_map/ppermute | solution.py:19
  49.9 0.9 copy-start.2
  49.9 1.0 copy-start.6
  52.2 12.8 %collective-permute-start.8 = (f32[1,7,32,128]{3,2,1,0:T(8,128)S(1)}, f32[1,7,32,128]{3,2,1,0:T(8,128)S(1)}, u32[]{:S(2)}, u32[]{:S(2)}) collective-permute-start(f32[1,7,32,128]{3,2,1,0:T(8,128)S(1)} %get-tuple-element.76), channel_id=1, source_target_pairs={{0,1},{1,2},{2,3},{3,4},{4,5},{5,6},{6,7},{7,8},{8,9},{9,10},{10,1... | collective-permute-start | bytes 344072 | tf_op jit(solution)/shard_map/ppermute | solution.py:18
  54.1 10.8 %collective-permute-start.9 = (f32[1,7,32,128]{3,2,1,0:T(8,128)S(1)}, f32[1,7,32,128]{3,2,1,0:T(8,128)S(1)}, u32[]{:S(2)}, u32[]{:S(2)}) collective-permute-start(f32[1,7,32,128]{3,2,1,0:T(8,128)S(1)} %get-tuple-element.77), channel_id=1, source_target_pairs={{1,0},{2,1},{3,2},{4,3},{5,4},{6,5},{7,6},{8,7},{9,8},{10,9},{11,1... | collective-permute-start | bytes 344072 | tf_op jit(solution)/shard_map/ppermute | solution.py:19
  60.0 4.3 %collective-permute-start.12 = (f32[1]{0:T(128)}, f32[1]{0:T(128)}, u32[]{:S(2)}, u32[]{:S(2)}) collective-permute-start(f32[1]{0:T(128)} %bitcast.35), channel_id=1, source_target_pairs={{0,2},{1,3},{2,0},{3,1},{4,6},{5,7},{6,4},{7,5},{8,10},{9,11},{10,... | collective-permute-start | bytes 20 | tf_op jit(solution)/shard_map/ppermute | solution.py:36
  65.6 10.2 %collective-permute-start.10 = (f32[1,7,32,128]{3,2,1,0:T(8,128)S(1)}, f32[1,7,32,128]{3,2,1,0:T(8,128)S(1)}, u32[]{:S(2)}, u32[]{:S(2)}) collective-permute-start(f32[1,7,32,128]{3,2,1,0:T(8,128)S(1)} %get-tuple-element.74), channel_id=1, source_target_pairs={{0,1},{1,2},{2,3},{3,4},{4,5},{5,6},{6,7},{7,8},{8,9},{9,10},{10,1... | collective-permute-start | bytes 344072 | tf_op jit(solution)/shard_map/ppermute | solution.py:18
  68.9 6.8 %collective-permute-start.11 = (f32[1,7,32,128]{3,2,1,0:T(8,128)S(1)}, f32[1,7,32,128]{3,2,1,0:T(8,128)S(1)}, u32[]{:S(2)}, u32[]{:S(2)}) collective-permute-start(f32[1,7,32,128]{3,2,1,0:T(8,128)S(1)} %get-tuple-element.75), channel_id=1, source_target_pairs={{1,0},{2,1},{3,2},{4,3},{5,4},{6,5},{7,6},{8,7},{9,8},{10,9},{11,1... | collective-permute-start | bytes 344072 | tf_op jit(solution)/shard_map/ppermute | solution.py:19
  71.1 3.9 %collective-permute-start.15 = (f32[1]{0:T(128)}, f32[1]{0:T(128)}, u32[]{:S(2)}, u32[]{:S(2)}) collective-permute-start(f32[1]{0:T(128)} %add.825), channel_id=1, source_target_pairs={{0,4},{1,5},{2,6},{3,7},{4,0},{5,1},{6,2},{7,3},{8,12},{9,13},{10,... | collective-permute-start | bytes 20 | tf_op jit(solution)/shard_map/ppermute | solution.py:36
  76.0 17.6 %copy-start.4 = (f32[1,8,32,128]{3,2,1,0:T(8,128)}, f32[1,8,32,128]{3,2,1,0:T(8,128)S(1)}, u32[]{:S(2)}) copy-start(f32[1,8,32,128]{3,2,1,0:T(8,128)S(1)} %get-tuple-element.37) | copy-start | bytes 393220
  76.3 17.0 %collective-permute-start.13 = (f32[1,7,32,128]{3,2,1,0:T(8,128)S(1)}, f32[1,7,32,128]{3,2,1,0:T(8,128)S(1)}, u32[]{:S(2)}, u32[]{:S(2)}) collective-permute-start(f32[1,7,32,128]{3,2,1,0:T(8,128)S(1)} %get-tuple-element.72), channel_id=1, source_target_pairs={{0,1},{1,2},{2,3},{3,4},{4,5},{5,6},{6,7},{7,8},{8,9},{9,10},{10,1... | collective-permute-start | bytes 344072 | tf_op jit(solution)/shard_map/ppermute | solution.py:18
  80.8 12.6 %collective-permute-start.14 = (f32[1,7,32,128]{3,2,1,0:T(8,128)S(1)}, f32[1,7,32,128]{3,2,1,0:T(8,128)S(1)}, u32[]{:S(2)}, u32[]{:S(2)}) collective-permute-start(f32[1,7,32,128]{3,2,1,0:T(8,128)S(1)} %get-tuple-element.73), channel_id=1, source_target_pairs={{1,0},{2,1},{3,2},{4,3},{5,4},{6,5},{7,6},{8,7},{9,8},{10,9},{11,1... | collective-permute-start | bytes 344072 | tf_op jit(solution)/shard_map/ppermute | solution.py:19
  83.1 4.6 %collective-permute-start.16 = (f32[1]{0:T(128)}, f32[1]{0:T(128)}, u32[]{:S(2)}, u32[]{:S(2)}) collective-permute-start(f32[1]{0:T(128)} %add.849), channel_id=1, source_target_pairs={{0,8},{1,9},{2,10},{3,11},{4,12},{5,13},{6,14},{7,15},{8,0},{9,1},... | collective-permute-start | bytes 20 | tf_op jit(solution)/shard_map/ppermute | solution.py:36
  88.3 4.4 %collective-permute-start.17 = (f32[1]{0:T(128)}, f32[1]{0:T(128)}, u32[]{:S(2)}, u32[]{:S(2)}) collective-permute-start(f32[1]{0:T(128)} %add.854), channel_id=1, source_target_pairs={{0,1},{1,0},{2,3},{3,2},{4,5},{5,4},{6,7},{7,6},{8,9},{9,8},{10,11... | collective-permute-start | bytes 20 | tf_op jit(solution)/shard_map/ppermute | solution.py:36
  93.4 0.9 copy-start.3

commit v16 on v13

--- a/solution.py
+++ b/solution.py
@@ -136,6 +136,9 @@
         added = jnp.einsum("srk,srz->skz", row_pick, spread, precision=lax.Precision.HIGHEST)
         return lax.optimization_barrier(added.reshape(shape))
 
+    receiver_count = injected(jnp.ones_like(observed[:, 0, :]))
+    recorded_last = injected(observed[:, STEPS - 1, :])
+
     before, current = (wave_prev, wave_now)
     laps = []
     resids = []
@@ -156,14 +159,16 @@
     for level in range(STEPS, 0, -1):
         if level == STEPS:
             lap = adjoint_lap
-            resid = resids[level - 1]
         else:
             if distances:
                 mu_near, misfit = lax.optimization_barrier((mu_near, misfit))
                 misfit = butterfly_round(misfit, "mp", distances.pop(0))
             lap, resid = operator(kappa * mu_near, resids[level - 1])
         state = 2.0 * mu_near + lap - mu_far
-        state = state + injected(resid)
+        if level == STEPS:
+            state = state + (receiver_count * current - recorded_last)
+        else:
+            state = state + injected(resid)
         gradient = gradient + state * laps[level - 1]
         mu_far, mu_near = (mu_near, state)
         mu_near, misfit = lax.optimization_barrier((mu_near, misfit))

time: 95.2 us -> 96.1 us (level)
  waiting for transfers between devices: 17 us -> 15.2 us
  matrix products: 11.4 us -> 12.6 us
    mul x7, other arithmetic: 2.4 us -> 5.41 us  [cross_terms(): flux = buoyancy * forward_diff(pad_axis(values, axis), axis, length)]
    dot_general x4 -> x5, matrix products: 4.93 us -> 6.19 us  [injected(): jnp.einsum('srk,srz->skz', row_pick, spread, precision=lax.Precision.HIGH...]
    mul x1 -> x0, other arithmetic: 1.06 us -> none  [local(): adjoint_operand = kappa * adjoint_next]
    add x0 -> x1, other arithmetic: none -> 1.03 us  [local(): state = state + (receiver_count * current - recorded_last)]
    concatenate x1, other arithmetic: 1.04 us -> 0.03 us  [local(): jnp.concatenate([buoyancy[None], wave_now, adjoint_operand], axis=0)]
    ppermute x7, waiting for transfers between devices: 3.87 us -> 2.9 us  [extended(): before = lax.ppermute(last, 'mp', up)]
    add x4 -> x3, other arithmetic: 3.22 us -> 2.48 us  [local(): following = following + jnp.where(source_hit, amount, 0.0)]
  transfers between devices with their start and end apart: 18 -> 18, of which waited for: 9 -> 8; matrix products, arithmetic and copies ran while one was open for 12% -> 14% of each run, Pallas kernels for 0% -> 0%
where the time goes in v16:
time: 96.1 us; the launch traced here: 94.7 us
  starting transfers between devices  44 us (46%)
  waiting for transfers between devices  15.2 us (16%)
  other arithmetic  13.8 us (14%)
  matrix products  12.6 us (13%)
  between operations  5.98 us (6%)
  local copies, waits for them, and re-layouts  3.22 us (3%)
    ppermute x7, starting transfers between devices, extended(): before = lax.ppermute(last, 'mp', up)  19.9 us
    ppermute x7, starting transfers between devices, extended(): after = lax.ppermute(first, 'mp', down)  15.1 us
    ppermute x7, waiting for transfers between devices, extended(): after = lax.ppermute(first, 'mp', down)  12 us
    ppermute x4, starting transfers between devices, butterfly_round(): return values + lax.ppermute(values, axis, pairs)  8.9 us
    dot_general x4, matrix products, sample(): jnp.einsum('srk,skz->srz', row_pick, field.reshape(shots, rows, cz), prec...  6.43 us
    dot_general x5, matrix products, injected(): jnp.einsum('srk,srz->skz', row_pick, spread, precision=lax.Precision.HIGH...  6.19 us
    mul x7, other arithmetic, cross_terms(): flux = buoyancy * forward_diff(pad_axis(values, axis), axis, length)  5.41 us
    ppermute x7, waiting for transfers between devices, extended(): before = lax.ppermute(last, 'mp', up)  2.9 us
  transfers between devices with their start and end apart: 18, of which 8 were waited for; matrix products, arithmetic and copies ran while one was open for 14% of the time, Pallas kernels for 0%

profile of v16, /device:TPU:1, one launch (start us, length us, event | category | flops | bytes accessed | tf_op | source)
XLA Modules:
  0.0 94.7 jit_solution(9547572790231794242)
XLA Ops:
  0.7 3.3 %fusion.179 = (f32[1,8,32,128]{3,2,1,0:T(8,128)S(1)}, f32[1,8,32,128]{3,2,1,0:T(8,128)S(1)}, f32[1,8,32,128]{3,2,1,0:T(8,128)S(1)}, f32[8,32,128]{2,1,0:T(8,128)S(1)}) fusion(f32[1,8,32,128]{3,2,1,0:T(8,128)} %param.13, f32[8,32,128]{2,1,0:T(8,128)} %param.11, f32[1,8,32,128]{3,2,1,0:T(8,128)} %param.14, f32[8,32,128]{2,1,0:T(8,128)} %param.10), kind=kLoop, calls=%fused_computation.432 | loop fusion | flops 884736 | bytes 1048576 | tf_op jit(solution)/shard_map/mul | solution.py:69
  4.1 2.0 %collective-permute-start.1 = (f32[3,7,32,128]{3,2,1,0:T(8,128)S(1)}, f32[3,7,32,128]{3,2,1,0:T(8,128)S(1)}, u32[]{:S(2)}, u32[]{:S(2)}) collective-permute-start(f32[3,7,32,128]{3,2,1,0:T(8,128)S(1)} %get-tuple-element.47), channel_id=1, source_target_pairs={{1,0},{2,1},{3,2},{4,3},{5,4},{6,5},{7,6},{8,7},{9,8},{10,9},{11,1... | collective-permute-start | bytes 1032200 | tf_op jit(solution)/shard_map/ppermute | solution.py:19
  6.1 4.5 %collective-permute-start = (f32[3,7,32,128]{3,2,1,0:T(8,128)S(1)}, f32[3,7,32,128]{3,2,1,0:T(8,128)S(1)}, u32[]{:S(2)}, u32[]{:S(2)}) collective-permute-start(f32[3,7,32,128]{3,2,1,0:T(8,128)S(1)} %get-tuple-element.48), channel_id=1, source_target_pairs={{0,1},{1,2},{2,3},{3,4},{4,5},{5,6},{6,7},{7,8},{8,9},{9,10},{10,1... | collective-permute-start | bytes 1032200 | tf_op jit(solution)/shard_map/ppermute | solution.py:18
  10.8 1.2 %fusion.30 = f32[1,8,32,128]{3,2,1,0:T(8,128)S(1)} fusion(s32[8,32]{1,0:T(8,128)S(1)} %multiply_add_fusion, s32[2048]{0:T(1024)S(1)} %bitcast.155, f32[2048]{0:T(1024)S(1)} %bitcast.164, s32[2048]{0:T(1024)S(1)} %bitcast.146), kind=kOutput, calls=%fused_computation.21 | convolution fusion | flops 806354944 | bytes 156672 | tf_op jit(solution)/shard_map/srk,srz->skz/dot_general | solution.py:136
  12.0 1.3 %fusion.27 = f32[1,8,32,128]{3,2,1,0:T(8,128)S(1)} fusion(s32[8,32]{1,0:T(8,128)S(1)} %multiply_add_fusion, s32[2048]{0:T(1024)S(1)} %bitcast.156, s32[2048]{0:T(1024)S(1)} %bitcast.147), kind=kOutput, calls=%fused_computation.20 | convolution fusion | flops 806354944 | bytes 148480 | tf_op jit(solution)/shard_map/srk,srz->skz/dot_general | solution.py:136
  14.0 0.6 fusion.632
  14.6 2.9 %collective-permute-done = f32[3,7,32,128]{3,2,1,0:T(8,128)S(1)} collective-permute-done((f32[3,7,32,128]{3,2,1,0:T(8,128)S(1)}, f32[3,7,32,128]{3,2,1,0:T(8,128)S(1)}, u32[]{:S(2)}, u32[]{:S(2)}) %collective-permute-start) | collective-permute-done | bytes 344096 | tf_op jit(solution)/shard_map/ppermute | solution.py:18
  17.5 0.1 fusion.126
  17.7 0.8 copy-done.5
  18.4 1.0 %fusion.599 = (f32[1,8,32,128]{3,2,1,0:T(8,128)S(1)}, f32[1,8,32,128]{3,2,1,0:T(8,128)S(1)}) fusion(f32[8,32,128]{2,1,0:T(8,128)S(1)} %get-tuple-element.80, f32[1,8,32,128]{3,2,1,0:T(8,128)S(1)} %copy-done.5, f32[1,8,32,128]{3,2,1,0:T(8,128)S(1)} %copy-done.1, f32[]{:T(128)} %bitcast.8, s32[]{:T(128)} %bitcast.7, s32[32]{0:T(128)S(1)} %iota_multiply_fusion, ...), kind=kLoop, calls=%fused_computation.893 | loop fusion | flops 1441792 | bytes 1966248 | tf_op jit(solution)/shard_map/add | solution.py:150
  19.4 0.3 fusion.394
  19.7 4.4 %collective-permute-start.2 = (f32[1,7,32,128]{3,2,1,0:T(8,128)S(1)}, f32[1,7,32,128]{3,2,1,0:T(8,128)S(1)}, u32[]{:S(2)}, u32[]{:S(2)}) collective-permute-start(f32[1,7,32,128]{3,2,1,0:T(8,128)S(1)} %get-tuple-element.77), channel_id=1, source_target_pairs={{0,1},{1,2},{2,3},{3,4},{4,5},{5,6},{6,7},{7,8},{8,9},{9,10},{10,1... | collective-permute-start | bytes 344072 | tf_op jit(solution)/shard_map/ppermute | solution.py:18
  24.1 1.9 %collective-permute-start.3 = (f32[1,7,32,128]{3,2,1,0:T(8,128)S(1)}, f32[1,7,32,128]{3,2,1,0:T(8,128)S(1)}, u32[]{:S(2)}, u32[]{:S(2)}) collective-permute-start(f32[1,7,32,128]{3,2,1,0:T(8,128)S(1)} %get-tuple-element.78), channel_id=1, source_target_pairs={{1,0},{2,1},{3,2},{4,3},{5,4},{6,5},{7,6},{8,7},{9,8},{10,9},{11,1... | collective-permute-start | bytes 344072 | tf_op jit(solution)/shard_map/ppermute | solution.py:19
  26.1 0.3 fusion.216
  26.4 0.1 fusion.134
  26.5 1.6 %fusion.15 = f32[2048]{0:T(1024)S(1)} fusion(f32[256,128]{1,0:T(8,128)S(1)} %bitcast.137, s32[2048]{0:T(1024)S(1)} %bitcast.157, s32[2048]{0:T(1024)S(1)} %bitcast.148), kind=kOutput, calls=%fused_computation.16 | convolution fusion | flops 806615040 | bytes 155648 | tf_op jit(solution)/shard_map/srk,skz->srz/dot_general | solution.py:129
  28.1 2.1 %collective-permute-done.3 = f32[1,7,32,128]{3,2,1,0:T(8,128)S(1)} collective-permute-done((f32[1,7,32,128]{3,2,1,0:T(8,128)S(1)}, f32[1,7,32,128]{3,2,1,0:T(8,128)S(1)}, u32[]{:S(2)}, u32[]{:S(2)}) %collective-permute-start.3) | collective-permute-done | bytes 114720 | tf_op jit(solution)/shard_map/ppermute | solution.py:19
  30.3 0.1 fusion.119
  30.4 0.8 fusion.601
  31.2 0.3 fusion.417
  31.5 1.9 %collective-permute-start.4 = (f32[1,7,32,128]{3,2,1,0:T(8,128)S(1)}, f32[1,7,32,128]{3,2,1,0:T(8,128)S(1)}, u32[]{:S(2)}, u32[]{:S(2)}) collective-permute-start(f32[1,7,32,128]{3,2,1,0:T(8,128)S(1)} %get-tuple-element.75), channel_id=1, source_target_pairs={{0,1},{1,2},{2,3},{3,4},{4,5},{5,6},{6,7},{7,8},{8,9},{9,10},{10,1... | collective-permute-start | bytes 344072 | tf_op jit(solution)/shard_map/ppermute | solution.py:18
  33.4 2.4 %collective-permute-start.5 = (f32[1,7,32,128]{3,2,1,0:T(8,128)S(1)}, f32[1,7,32,128]{3,2,1,0:T(8,128)S(1)}, u32[]{:S(2)}, u32[]{:S(2)}) collective-permute-start(f32[1,7,32,128]{3,2,1,0:T(8,128)S(1)} %get-tuple-element.76), channel_id=1, source_target_pairs={{1,0},{2,1},{3,2},{4,3},{5,4},{6,5},{7,6},{8,7},{9,8},{10,9},{11,1... | collective-permute-start | bytes 344072 | tf_op jit(solution)/shard_map/ppermute | solution.py:19
  35.8 0.3 fusion.240
  36.1 1.6 %fusion.18 = f32[2048]{0:T(1024)S(1)} fusion(f32[256,128]{1,0:T(8,128)S(1)} %bitcast.136, s32[2048]{0:T(1024)S(1)} %bitcast.158, s32[2048]{0:T(1024)S(1)} %bitcast.149), kind=kOutput, calls=%fused_computation.17 | convolution fusion | flops 806615040 | bytes 155648 | tf_op jit(solution)/shard_map/srk,skz->srz/dot_general | solution.py:129
  37.8 1.8 %collective-permute-done.5 = f32[1,7,32,128]{3,2,1,0:T(8,128)S(1)} collective-permute-done((f32[1,7,32,128]{3,2,1,0:T(8,128)S(1)}, f32[1,7,32,128]{3,2,1,0:T(8,128)S(1)}, u32[]{:S(2)}, u32[]{:S(2)}) %collective-permute-start.5) | collective-permute-done | bytes 114720 | tf_op jit(solution)/shard_map/ppermute | solution.py:19
  39.6 0.1 fusion.112
  39.7 0.8 fusion.603
  40.5 0.5 fusion.440
  41.0 1.9 %collective-permute-start.6 = (f32[1,7,32,128]{3,2,1,0:T(8,128)S(1)}, f32[1,7,32,128]{3,2,1,0:T(8,128)S(1)}, u32[]{:S(2)}, u32[]{:S(2)}) collective-permute-start(f32[1,7,32,128]{3,2,1,0:T(8,128)S(1)} %get-tuple-element.71), channel_id=1, source_target_pairs={{0,1},{1,2},{2,3},{3,4},{4,5},{5,6},{6,7},{7,8},{8,9},{9,10},{10,1... | collective-permute-start | bytes 344072 | tf_op jit(solution)/shard_map/ppermute | solution.py:18
  42.9 2.4 %collective-permute-start.7 = (f32[1,7,32,128]{3,2,1,0:T(8,128)S(1)}, f32[1,7,32,128]{3,2,1,0:T(8,128)S(1)}, u32[]{:S(2)}, u32[]{:S(2)}) collective-permute-start(f32[1,7,32,128]{3,2,1,0:T(8,128)S(1)} %get-tuple-element.72), channel_id=1, source_target_pairs={{1,0},{2,1},{3,2},{4,3},{5,4},{6,5},{7,6},{8,7},{9,8},{10,9},{11,1... | collective-permute-start | bytes 344072 | tf_op jit(solution)/shard_map/ppermute | solution.py:19
  45.3 0.3 fusion.264
  45.7 1.6 %fusion.21 = f32[2048]{0:T(1024)S(1)} fusion(f32[256,128]{1,0:T(8,128)S(1)} %bitcast.138, s32[2048]{0:T(1024)S(1)} %bitcast.159, s32[2048]{0:T(1024)S(1)} %bitcast.150), kind=kOutput, calls=%fused_computation.18 | convolution fusion | flops 806615040 | bytes 155648 | tf_op jit(solution)/shard_map/srk,skz->srz/dot_general | solution.py:129
  47.3 2.6 %collective-permute-done.7 = f32[1,7,32,128]{3,2,1,0:T(8,128)S(1)} collective-permute-done((f32[1,7,32,128]{3,2,1,0:T(8,128)S(1)}, f32[1,7,32,128]{3,2,1,0:T(8,128)S(1)}, u32[]{:S(2)}, u32[]{:S(2)}) %collective-permute-start.7) | collective-permute-done | bytes 114720 | tf_op jit(solution)/shard_map/ppermute | solution.py:19
  50.0 0.1 fusion.105
  50.1 0.8 copy-done.2
  50.9 1.0 %fusion.167 = (f32[1,8,32,128]{3,2,1,0:T(8,128)S(1)}, f32[1,8,32,128]{3,2,1,0:T(8,128)S(1)}, f32[1,8,32,128]{3,2,1,0:T(8,128)S(1)}) fusion(f32[1,8,32,128]{3,2,1,0:T(8,128)S(1)} %copy-done.6, f32[1,8,32,128]{3,2,1,0:T(8,128)S(1)} %get-tuple-element.73, f32[1,8,32,128]{3,2,1,0:T(8,128)S(1)} %get-tuple-element.74, f32[1,15,32,128]{3,2,1,0:T(8,128)S(1)} %fusion.134, ...), kind=kLoop, calls=%fused_computation.420 | loop fusion | flops 2031616 | bytes 3801256 | tf_op jit(solution)/shard_map/add | solution.py:169
  51.9 1.6 %fusion.24 = f32[2048]{0:T(1024)S(1)} fusion(f32[256,128]{1,0:T(8,128)S(1)} %bitcast.139, s32[2048]{0:T(1024)S(1)} %bitcast.160, s32[2048]{0:T(1024)S(1)} %bitcast.151), kind=kOutput, calls=%fused_computation.19 | convolution fusion | flops 806615040 | bytes 155648 | tf_op jit(solution)/shard_map/srk,skz->srz/dot_general | solution.py:129
  53.6 0.6 fusion.606
  55.0 0.3 fusion.463
  55.3 3.0 %collective-permute-start.10 = (f32[1]{0:T(128)}, f32[1]{0:T(128)}, u32[]{:S(2)}, u32[]{:S(2)}) collective-permute-start(f32[1]{0:T(128)} %bitcast.32), channel_id=1, source_target_pairs={{0,2},{1,3},{2,0},{3,1},{4,6},{5,7},{6,4},{7,5},{8,10},{9,11},{10,... | collective-permute-start | bytes 20 | tf_op jit(solution)/shard_map/ppermute | solution.py:36
  58.3 1.9 %collective-permute-start.8 = (f32[1,7,32,128]{3,2,1,0:T(8,128)S(1)}, f32[1,7,32,128]{3,2,1,0:T(8,128)S(1)}, u32[]{:S(2)}, u32[]{:S(2)}) collective-permute-start(f32[1,7,32,128]{3,2,1,0:T(8,128)S(1)} %get-tuple-element.69), channel_id=1, source_target_pairs={{0,1},{1,2},{2,3},{3,4},{4,5},{5,6},{6,7},{7,8},{8,9},{9,10},{10,1... | collective-permute-start | bytes 344072 | tf_op jit(solution)/shard_map/ppermute | solution.py:18
  60.2 2.6 %collective-permute-start.9 = (f32[1,7,32,128]{3,2,1,0:T(8,128)S(1)}, f32[1,7,32,128]{3,2,1,0:T(8,128)S(1)}, u32[]{:S(2)}, u32[]{:S(2)}) collective-permute-start(f32[1,7,32,128]{3,2,1,0:T(8,128)S(1)} %get-tuple-element.70), channel_id=1, source_target_pairs={{1,0},{2,1},{3,2},{4,3},{5,4},{6,5},{7,6},{8,7},{9,8},{10,9},{11,1... | collective-permute-start | bytes 344072 | tf_op jit(solution)/shard_map/ppermute | solution.py:19
  62.8 0.3 fusion.288
  63.1 1.2 %fusion.33 = f32[1,8,32,128]{3,2,1,0:T(8,128)S(1)} fusion(s32[8,32]{1,0:T(8,128)S(1)} %multiply_add_fusion, s32[2048]{0:T(1024)S(1)} %bitcast.161, f32[2048]{0:T(1024)S(1)} %bitcast.145, s32[2048]{0:T(1024)S(1)} %bitcast.152), kind=kOutput, calls=%fused_computation.22 | convolution fusion | flops 806354944 | bytes 156672 | tf_op jit(solution)/shard_map/srk,srz->skz/dot_general | solution.py:136
  64.9 1.4 %collective-permute-done.9 = f32[1,7,32,128]{3,2,1,0:T(8,128)S(1)} collective-permute-done((f32[1,7,32,128]{3,2,1,0:T(8,128)S(1)}, f32[1,7,32,128]{3,2,1,0:T(8,128)S(1)}, u32[]{:S(2)}, u32[]{:S(2)}) %collective-permute-start.9) | collective-permute-done | bytes 114720 | tf_op jit(solution)/shard_map/ppermute | solution.py:19
  66.4 0.1 fusion.98
  66.6 0.3 fusion.486
  66.9 2.1 %collective-permute-start.13 = (f32[1]{0:T(128)}, f32[1]{0:T(128)}, u32[]{:S(2)}, u32[]{:S(2)}) collective-permute-start(f32[1]{0:T(128)} %add.806), channel_id=1, source_target_pairs={{0,4},{1,5},{2,6},{3,7},{4,0},{5,1},{6,2},{7,3},{8,12},{9,13},{10,... | collective-permute-start | bytes 20 | tf_op jit(solution)/shard_map/ppermute | solution.py:36
  69.0 2.6 %collective-permute-start.11 = (f32[1,7,32,128]{3,2,1,0:T(8,128)S(1)}, f32[1,7,32,128]{3,2,1,0:T(8,128)S(1)}, u32[]{:S(2)}, u32[]{:S(2)}) collective-permute-start(f32[1,7,32,128]{3,2,1,0:T(8,128)S(1)} %get-tuple-element.67), channel_id=1, source_target_pairs={{0,1},{1,2},{2,3},{3,4},{4,5},{5,6},{6,7},{7,8},{8,9},{9,10},{10,1... | collective-permute-start | bytes 344072 | tf_op jit(solution)/shard_map/ppermute | solution.py:18
  71.7 1.9 %collective-permute-start.12 = (f32[1,7,32,128]{3,2,1,0:T(8,128)S(1)}, f32[1,7,32,128]{3,2,1,0:T(8,128)S(1)}, u32[]{:S(2)}, u32[]{:S(2)}) collective-permute-start(f32[1,7,32,128]{3,2,1,0:T(8,128)S(1)} %get-tuple-element.68), channel_id=1, source_target_pairs={{1,0},{2,1},{3,2},{4,3},{5,4},{6,5},{7,6},{8,7},{9,8},{10,9},{11,1... | collective-permute-start | bytes 344072 | tf_op jit(solution)/shard_map/ppermute | solution.py:19
  73.6 0.3 fusion.312
  73.9 1.2 %fusion.36 = f32[1,8,32,128]{3,2,1,0:T(8,128)S(1)} fusion(s32[8,32]{1,0:T(8,128)S(1)} %multiply_add_fusion, s32[2048]{0:T(1024)S(1)} %bitcast.162, f32[2048]{0:T(1024)S(1)} %bitcast.143, s32[2048]{0:T(1024)S(1)} %bitcast.153), kind=kOutput, calls=%fused_computation.23 | convolution fusion | flops 806354944 | bytes 156672 | tf_op jit(solution)/shard_map/srk,srz->skz/dot_general | solution.py:136
  75.7 2.1 %collective-permute-done.12 = f32[1,7,32,128]{3,2,1,0:T(8,128)S(1)} collective-permute-done((f32[1,7,32,128]{3,2,1,0:T(8,128)S(1)}, f32[1,7,32,128]{3,2,1,0:T(8,128)S(1)}, u32[]{:S(2)}, u32[]{:S(2)}) %collective-permute-start.12) | collective-permute-done | bytes 114720 | tf_op jit(solution)/shard_map/ppermute | solution.py:19
  78.1 0.3 fusion.509
  78.4 2.8 %collective-permute-start.16 = (f32[1]{0:T(128)}, f32[1]{0:T(128)}, u32[]{:S(2)}, u32[]{:S(2)}) collective-permute-start(f32[1]{0:T(128)} %add.830), channel_id=1, source_target_pairs={{0,8},{1,9},{2,10},{3,11},{4,12},{5,13},{6,14},{7,15},{8,0},{9,1},... | collective-permute-start | bytes 20 | tf_op jit(solution)/shard_map/ppermute | solution.py:36
  81.2 2.6 %collective-permute-start.14 = (f32[1,7,32,128]{3,2,1,0:T(8,128)S(1)}, f32[1,7,32,128]{3,2,1,0:T(8,128)S(1)}, u32[]{:S(2)}, u32[]{:S(2)}) collective-permute-start(f32[1,7,32,128]{3,2,1,0:T(8,128)S(1)} %get-tuple-element.65), channel_id=1, source_target_pairs={{0,1},{1,2},{2,3},{3,4},{4,5},{5,6},{6,7},{7,8},{8,9},{9,10},{10,1... | collective-permute-start | bytes 344072 | tf_op jit(solution)/shard_map/ppermute | solution.py:18
  83.9 1.9 %collective-permute-start.15 = (f32[1,7,32,128]{3,2,1,0:T(8,128)S(1)}, f32[1,7,32,128]{3,2,1,0:T(8,128)S(1)}, u32[]{:S(2)}, u32[]{:S(2)}) collective-permute-start(f32[1,7,32,128]{3,2,1,0:T(8,128)S(1)} %get-tuple-element.66), channel_id=1, source_target_pairs={{1,0},{2,1},{3,2},{4,3},{5,4},{6,5},{7,6},{8,7},{9,8},{10,9},{11,1... | collective-permute-start | bytes 344072 | tf_op jit(solution)/shard_map/ppermute | solution.py:19
  85.8 0.3 fusion.336
  86.1 1.2 %fusion.39 = f32[1,8,32,128]{3,2,1,0:T(8,128)S(1)} fusion(s32[8,32]{1,0:T(8,128)S(1)} %multiply_add_fusion, s32[2048]{0:T(1024)S(1)} %bitcast.163, f32[2048]{0:T(1024)S(1)} %bitcast.141, s32[2048]{0:T(1024)S(1)} %bitcast.154), kind=kOutput, calls=%fused_computation.24 | convolution fusion | flops 806354944 | bytes 156672 | tf_op jit(solution)/shard_map/srk,srz->skz/dot_general | solution.py:136
  87.9 2.1 %collective-permute-done.15 = f32[1,7,32,128]{3,2,1,0:T(8,128)S(1)} collective-permute-done((f32[1,7,32,128]{3,2,1,0:T(8,128)S(1)}, f32[1,7,32,128]{3,2,1,0:T(8,128)S(1)}, u32[]{:S(2)}, u32[]{:S(2)}) %collective-permute-start.15) | collective-permute-done | bytes 114720 | tf_op jit(solution)/shard_map/ppermute | solution.py:19
  90.1 0.8 copy-done.4
  90.9 0.9 bitcast_multiply_fusion
  91.8 1.0 %collective-permute-start.17 = (f32[1]{0:T(128)}, f32[1]{0:T(128)}, u32[]{:S(2)}, u32[]{:S(2)}) collective-permute-start(f32[1]{0:T(128)} %add.854), channel_id=1, source_target_pairs={{0,1},{1,0},{2,3},{3,2},{4,5},{5,4},{6,7},{7,6},{8,9},{9,8},{10,11... | collective-permute-start | bytes 20 | tf_op jit(solution)/shard_map/ppermute | solution.py:36
  92.7 0.3 collective-permute-done.17
  (56 shorter events, 1.1 us)
Async XLA Ops:
  0.6 3.3 %copy-start = (f32[8,32,128]{2,1,0:T(8,128)S(1)}, f32[8,32,128]{2,1,0:T(8,128)}, u32[]{:S(2)}) copy-start(f32[8,32,128]{2,1,0:T(8,128)} %param.11) | copy-start | bytes 393220
  0.6 3.3 %copy-start.1 = (f32[1,8,32,128]{3,2,1,0:T(8,128)S(1)}, f32[1,8,32,128]{3,2,1,0:T(8,128)}, u32[]{:S(2)}) copy-start(f32[1,8,32,128]{3,2,1,0:T(8,128)} %param.13) | copy-start | bytes 393220
  4.0 6.6 %copy-start.8 = (f32[1,4,2048]{2,1,0:T(4,128)S(1)}, f32[1,4,2048]{2,1,0:T(4,128)}, u32[]{:S(2)}) copy-start(f32[1,4,2048]{2,1,0:T(4,128)} %param.19) | copy-start | bytes 98308
  4.0 6.7 %copy-start.7 = (s32[1,2048]{1,0:T(1,128)S(1)}, s32[1,2048]{1,0:T(1,128)}, u32[]{:S(2)}) copy-start(s32[1,2048]{1,0:T(1,128)} %param.18) | copy-start | bytes 24580
  4.1 10.4 %collective-permute-start.1 = (f32[3,7,32,128]{3,2,1,0:T(8,128)S(1)}, f32[3,7,32,128]{3,2,1,0:T(8,128)S(1)}, u32[]{:S(2)}, u32[]{:S(2)}) collective-permute-start(f32[3,7,32,128]{3,2,1,0:T(8,128)S(1)} %get-tuple-element.47), channel_id=1, source_target_pairs={{1,0},{2,1},{3,2},{4,3},{5,4},{6,5},{7,6},{8,7},{9,8},{10,9},{11,1... | collective-permute-start | bytes 1032200 | tf_op jit(solution)/shard_map/ppermute | solution.py:19
  6.1 11.3 %collective-permute-start = (f32[3,7,32,128]{3,2,1,0:T(8,128)S(1)}, f32[3,7,32,128]{3,2,1,0:T(8,128)S(1)}, u32[]{:S(2)}, u32[]{:S(2)}) collective-permute-start(f32[3,7,32,128]{3,2,1,0:T(8,128)S(1)} %get-tuple-element.48), channel_id=1, source_target_pairs={{0,1},{1,2},{2,3},{3,4},{4,5},{5,6},{6,7},{7,8},{8,9},{9,10},{10,1... | collective-permute-start | bytes 1032200 | tf_op jit(solution)/shard_map/ppermute | solution.py:18
  12.0 2.0 %copy-start.9 = (f32[1,4]{1,0:T(1,128)S(1)}, f32[1,4]{1,0:T(1,128)}, u32[]{:S(2)}) copy-start(f32[1,4]{1,0:T(1,128)} %param.17) | copy-start | bytes 52
  17.5 0.9 copy-start.5
  19.7 8.4 %collective-permute-start.2 = (f32[1,7,32,128]{3,2,1,0:T(8,128)S(1)}, f32[1,7,32,128]{3,2,1,0:T(8,128)S(1)}, u32[]{:S(2)}, u32[]{:S(2)}) collective-permute-start(f32[1,7,32,128]{3,2,1,0:T(8,128)S(1)} %get-tuple-element.77), channel_id=1, source_target_pairs={{0,1},{1,2},{2,3},{3,4},{4,5},{5,6},{6,7},{7,8},{8,9},{9,10},{10,1... | collective-permute-start | bytes 344072 | tf_op jit(solution)/shard_map/ppermute | solution.py:18
  24.1 6.1 %collective-permute-start.3 = (f32[1,7,32,128]{3,2,1,0:T(8,128)S(1)}, f32[1,7,32,128]{3,2,1,0:T(8,128)S(1)}, u32[]{:S(2)}, u32[]{:S(2)}) collective-permute-start(f32[1,7,32,128]{3,2,1,0:T(8,128)S(1)} %get-tuple-element.78), channel_id=1, source_target_pairs={{1,0},{2,1},{3,2},{4,3},{5,4},{6,5},{7,6},{8,7},{9,8},{10,9},{11,1... | collective-permute-start | bytes 344072 | tf_op jit(solution)/shard_map/ppermute | solution.py:19
  31.5 6.3 %collective-permute-start.4 = (f32[1,7,32,128]{3,2,1,0:T(8,128)S(1)}, f32[1,7,32,128]{3,2,1,0:T(8,128)S(1)}, u32[]{:S(2)}, u32[]{:S(2)}) collective-permute-start(f32[1,7,32,128]{3,2,1,0:T(8,128)S(1)} %get-tuple-element.75), channel_id=1, source_target_pairs={{0,1},{1,2},{2,3},{3,4},{4,5},{5,6},{6,7},{7,8},{8,9},{9,10},{10,1... | collective-permute-start | bytes 344072 | tf_op jit(solution)/shard_map/ppermute | solution.py:18
  33.4 6.1 %collective-permute-start.5 = (f32[1,7,32,128]{3,2,1,0:T(8,128)S(1)}, f32[1,7,32,128]{3,2,1,0:T(8,128)S(1)}, u32[]{:S(2)}, u32[]{:S(2)}) collective-permute-start(f32[1,7,32,128]{3,2,1,0:T(8,128)S(1)} %get-tuple-element.76), channel_id=1, source_target_pairs={{1,0},{2,1},{3,2},{4,3},{5,4},{6,5},{7,6},{8,7},{9,8},{10,9},{11,1... | collective-permute-start | bytes 344072 | tf_op jit(solution)/shard_map/ppermute | solution.py:19
  41.0 6.3 %collective-permute-start.6 = (f32[1,7,32,128]{3,2,1,0:T(8,128)S(1)}, f32[1,7,32,128]{3,2,1,0:T(8,128)S(1)}, u32[]{:S(2)}, u32[]{:S(2)}) collective-permute-start(f32[1,7,32,128]{3,2,1,0:T(8,128)S(1)} %get-tuple-element.71), channel_id=1, source_target_pairs={{0,1},{1,2},{2,3},{3,4},{4,5},{5,6},{6,7},{7,8},{8,9},{9,10},{10,1... | collective-permute-start | bytes 344072 | tf_op jit(solution)/shard_map/ppermute | solution.py:18
  42.9 7.0 %collective-permute-start.7 = (f32[1,7,32,128]{3,2,1,0:T(8,128)S(1)}, f32[1,7,32,128]{3,2,1,0:T(8,128)S(1)}, u32[]{:S(2)}, u32[]{:S(2)}) collective-permute-start(f32[1,7,32,128]{3,2,1,0:T(8,128)S(1)} %get-tuple-element.72), channel_id=1, source_target_pairs={{1,0},{2,1},{3,2},{4,3},{5,4},{6,5},{7,6},{8,7},{9,8},{10,9},{11,1... | collective-permute-start | bytes 344072 | tf_op jit(solution)/shard_map/ppermute | solution.py:19
  49.9 0.9 copy-start.2
  49.9 1.0 %copy-start.6 = (f32[1,8,32,128]{3,2,1,0:T(8,128)S(1)}, f32[1,8,32,128]{3,2,1,0:T(8,128)}, u32[]{:S(2)}) copy-start(f32[1,8,32,128]{3,2,1,0:T(8,128)} %param.15) | copy-start | bytes 393220
  55.3 9.1 %collective-permute-start.10 = (f32[1]{0:T(128)}, f32[1]{0:T(128)}, u32[]{:S(2)}, u32[]{:S(2)}) collective-permute-start(f32[1]{0:T(128)} %bitcast.32), channel_id=1, source_target_pairs={{0,2},{1,3},{2,0},{3,1},{4,6},{5,7},{6,4},{7,5},{8,10},{9,11},{10,... | collective-permute-start | bytes 20 | tf_op jit(solution)/shard_map/ppermute | solution.py:36
  58.3 6.6 %collective-permute-start.8 = (f32[1,7,32,128]{3,2,1,0:T(8,128)S(1)}, f32[1,7,32,128]{3,2,1,0:T(8,128)S(1)}, u32[]{:S(2)}, u32[]{:S(2)}) collective-permute-start(f32[1,7,32,128]{3,2,1,0:T(8,128)S(1)} %get-tuple-element.69), channel_id=1, source_target_pairs={{0,1},{1,2},{2,3},{3,4},{4,5},{5,6},{6,7},{7,8},{8,9},{9,10},{10,1... | collective-permute-start | bytes 344072 | tf_op jit(solution)/shard_map/ppermute | solution.py:18
  60.2 6.1 %collective-permute-start.9 = (f32[1,7,32,128]{3,2,1,0:T(8,128)S(1)}, f32[1,7,32,128]{3,2,1,0:T(8,128)S(1)}, u32[]{:S(2)}, u32[]{:S(2)}) collective-permute-start(f32[1,7,32,128]{3,2,1,0:T(8,128)S(1)} %get-tuple-element.70), channel_id=1, source_target_pairs={{1,0},{2,1},{3,2},{4,3},{5,4},{6,5},{7,6},{8,7},{9,8},{10,9},{11,1... | collective-permute-start | bytes 344072 | tf_op jit(solution)/shard_map/ppermute | solution.py:19
  66.9 8.2 %collective-permute-start.13 = (f32[1]{0:T(128)}, f32[1]{0:T(128)}, u32[]{:S(2)}, u32[]{:S(2)}) collective-permute-start(f32[1]{0:T(128)} %add.806), channel_id=1, source_target_pairs={{0,4},{1,5},{2,6},{3,7},{4,0},{5,1},{6,2},{7,3},{8,12},{9,13},{10,... | collective-permute-start | bytes 20 | tf_op jit(solution)/shard_map/ppermute | solution.py:36
  69.0 6.7 %collective-permute-start.11 = (f32[1,7,32,128]{3,2,1,0:T(8,128)S(1)}, f32[1,7,32,128]{3,2,1,0:T(8,128)S(1)}, u32[]{:S(2)}, u32[]{:S(2)}) collective-permute-start(f32[1,7,32,128]{3,2,1,0:T(8,128)S(1)} %get-tuple-element.67), channel_id=1, source_target_pairs={{0,1},{1,2},{2,3},{3,4},{4,5},{5,6},{6,7},{7,8},{8,9},{9,10},{10,1... | collective-permute-start | bytes 344072 | tf_op jit(solution)/shard_map/ppermute | solution.py:18
  71.7 6.1 %collective-permute-start.12 = (f32[1,7,32,128]{3,2,1,0:T(8,128)S(1)}, f32[1,7,32,128]{3,2,1,0:T(8,128)S(1)}, u32[]{:S(2)}, u32[]{:S(2)}) collective-permute-start(f32[1,7,32,128]{3,2,1,0:T(8,128)S(1)} %get-tuple-element.68), channel_id=1, source_target_pairs={{1,0},{2,1},{3,2},{4,3},{5,4},{6,5},{7,6},{8,7},{9,8},{10,9},{11,1... | collective-permute-start | bytes 344072 | tf_op jit(solution)/shard_map/ppermute | solution.py:19
  78.0 12.1 %copy-start.3 = (f32[1,8,32,128]{3,2,1,0:T(8,128)}, f32[1,8,32,128]{3,2,1,0:T(8,128)S(1)}, u32[]{:S(2)}) copy-start(f32[1,8,32,128]{3,2,1,0:T(8,128)S(1)} %fusion.543) | copy-start | bytes 393220
  78.4 9.0 %collective-permute-start.16 = (f32[1]{0:T(128)}, f32[1]{0:T(128)}, u32[]{:S(2)}, u32[]{:S(2)}) collective-permute-start(f32[1]{0:T(128)} %add.830), channel_id=1, source_target_pairs={{0,8},{1,9},{2,10},{3,11},{4,12},{5,13},{6,14},{7,15},{8,0},{9,1},... | collective-permute-start | bytes 20 | tf_op jit(solution)/shard_map/ppermute | solution.py:36
  81.2 6.7 %collective-permute-start.14 = (f32[1,7,32,128]{3,2,1,0:T(8,128)S(1)}, f32[1,7,32,128]{3,2,1,0:T(8,128)S(1)}, u32[]{:S(2)}, u32[]{:S(2)}) collective-permute-start(f32[1,7,32,128]{3,2,1,0:T(8,128)S(1)} %get-tuple-element.65), channel_id=1, source_target_pairs={{0,1},{1,2},{2,3},{3,4},{4,5},{5,6},{6,7},{7,8},{8,9},{9,10},{10,1... | collective-permute-start | bytes 344072 | tf_op jit(solution)/shard_map/ppermute | solution.py:18
  83.9 6.1 %collective-permute-start.15 = (f32[1,7,32,128]{3,2,1,0:T(8,128)S(1)}, f32[1,7,32,128]{3,2,1,0:T(8,128)S(1)}, u32[]{:S(2)}, u32[]{:S(2)}) collective-permute-start(f32[1,7,32,128]{3,2,1,0:T(8,128)S(1)} %get-tuple-element.66), channel_id=1, source_target_pairs={{1,0},{2,1},{3,2},{4,3},{5,4},{6,5},{7,6},{8,7},{9,8},{10,9},{11,1... | collective-permute-start | bytes 344072 | tf_op jit(solution)/shard_map/ppermute | solution.py:19
  90.0 0.9 copy-start.4
  91.8 1.3 %collective-permute-start.17 = (f32[1]{0:T(128)}, f32[1]{0:T(128)}, u32[]{:S(2)}, u32[]{:S(2)}) collective-permute-start(f32[1]{0:T(128)} %add.854), channel_id=1, source_target_pairs={{0,1},{1,0},{2,3},{3,2},{4,5},{5,4},{6,7},{7,6},{8,9},{9,8},{10,11... | collective-permute-start | bytes 20 | tf_op jit(solution)/shard_map/ppermute | solution.py:36

commit v17 on v13

--- a/solution.py
+++ b/solution.py
@@ -140,7 +140,12 @@
     laps = []
     resids = []
     for step in range(STEPS):
-        lap = first_lap if step == 0 else operator(current)
+        if step == 0:
+            lap = first_lap
+        elif step == 1:
+            lap, scale = operator(current, 2.0 * velocity / buoyancy)
+        else:
+            lap = operator(current)
         laps.append(lap)
         following = 2.0 * current - before + kappa * lap
         amount = wavelet[:, step].reshape(shots, 1, 1, 1)
@@ -166,10 +171,11 @@
         state = state + injected(resid)
         gradient = gradient + state * laps[level - 1]
         mu_far, mu_near = (mu_near, state)
-        mu_near, misfit = lax.optimization_barrier((mu_near, misfit))
+        if level > 1:
+            mu_near, misfit = lax.optimization_barrier((mu_near, misfit))
     for distance in distances:
         misfit = butterfly_round(misfit, "mp", distance)
-    velocity_gradient = 2.0 * velocity / buoyancy * jnp.sum(gradient, axis=0)
+    velocity_gradient = scale * jnp.sum(gradient, axis=0)
     return (velocity_gradient, mu_near, mu_far, misfit)
 
 

time: 95.2 us -> 92.9 us (0.976)
  waiting for transfers between devices: 17 us -> 15.1 us
    ppermute x7, waiting for transfers between devices: 12.9 us -> 11 us  [extended(): after = lax.ppermute(first, 'mp', down)]
  transfers between devices with their start and end apart: 18 -> 18, of which waited for: 9 -> 9; matrix products, arithmetic and copies ran while one was open for 12% -> 13% of each run, Pallas kernels for 0% -> 0%
where the time goes in v17:
time: 92.9 us; the launch traced here: 91.3 us
  starting transfers between devices  43.9 us (47%)
  waiting for transfers between devices  15.1 us (16%)
  other arithmetic  12.9 us (14%)
  matrix products  11.4 us (12%)
  between operations  6.44 us (7%)
  local copies, waits for them, and re-layouts  1.61 us (2%)
    ppermute x7, starting transfers between devices, extended(): before = lax.ppermute(last, 'mp', up)  20.1 us
    ppermute x7, starting transfers between devices, extended(): after = lax.ppermute(first, 'mp', down)  15 us
    ppermute x7, waiting for transfers between devices, extended(): after = lax.ppermute(first, 'mp', down)  11 us
    ppermute x4, starting transfers between devices, butterfly_round(): return values + lax.ppermute(values, axis, pairs)  8.83 us
    dot_general x4, matrix products, sample(): jnp.einsum('srk,skz->srz', row_pick, field.reshape(shots, rows, cz), prec...  6.43 us
    dot_general x4, matrix products, injected(): jnp.einsum('srk,srz->skz', row_pick, spread, precision=lax.Precision.HIGH...  4.93 us
    ppermute x7, waiting for transfers between devices, extended(): before = lax.ppermute(last, 'mp', up)  3.87 us
    add x4, other arithmetic, local(): following = following + jnp.where(source_hit, amount, 0.0)  3.22 us
  transfers between devices with their start and end apart: 18, of which 9 were waited for; matrix products, arithmetic and copies ran while one was open for 13% of the time, Pallas kernels for 0%

profile of v17, /device:TPU:1, one launch (start us, length us, event | category | flops | bytes accessed | tf_op | source)
XLA Modules:
  0.0 91.3 jit_solution(2916363821475789728)
XLA Ops:
  0.6 1.1 %bitcast_multiply_fusion.8 = (f32[1,8,32,128]{3,2,1,0:T(8,128)S(1)}, f32[8,32,128]{2,1,0:T(8,128)S(1)}) fusion(f32[1,8,32,128]{3,2,1,0:T(8,128)} %param.14, f32[8,32,128]{2,1,0:T(8,128)} %param.11, f32[8,32,128]{2,1,0:T(8,128)} %param.10), kind=kLoop, calls=%fused_computation.881 | loop fusion | flops 98304 | bytes 655360 | tf_op jit(solution)/shard_map/mul | solution.py:99
  1.7 1.0 %pad_maximum_fusion.1 = f32[3,8,32,128]{3,2,1,0:T(8,128)S(1)} fusion(f32[1,8,32,128]{3,2,1,0:T(8,128)S(1)} %get-tuple-element.44, f32[1,8,32,128]{3,2,1,0:T(8,128)} %param.13, f32[1,8,32,128]{3,2,1,0:T(8,128)} %bitcast.123), kind=kLoop, calls=%fused_computation.168 | loop fusion | flops 196608 | bytes 786432 | tf_op jit(solution)/shard_map/concatenate | solution.py:100
  2.9 2.0 %collective-permute-start.1 = (f32[3,7,32,128]{3,2,1,0:T(8,128)S(1)}, f32[3,7,32,128]{3,2,1,0:T(8,128)S(1)}, u32[]{:S(2)}, u32[]{:S(2)}) collective-permute-start(f32[3,7,32,128]{3,2,1,0:T(8,128)S(1)} %get-tuple-element.46), channel_id=1, source_target_pairs={{1,0},{2,1},{3,2},{4,3},{5,4},{6,5},{7,6},{8,7},{9,8},{10,9},{11,1... | collective-permute-start | bytes 1032200 | tf_op jit(solution)/shard_map/ppermute | solution.py:19
  4.8 4.5 %collective-permute-start = (f32[3,7,32,128]{3,2,1,0:T(8,128)S(1)}, f32[3,7,32,128]{3,2,1,0:T(8,128)S(1)}, u32[]{:S(2)}, u32[]{:S(2)}) collective-permute-start(f32[3,7,32,128]{3,2,1,0:T(8,128)S(1)} %get-tuple-element.47), channel_id=1, source_target_pairs={{0,1},{1,2},{2,3},{3,4},{4,5},{5,6},{6,7},{7,8},{8,9},{9,10},{10,1... | collective-permute-start | bytes 1032200 | tf_op jit(solution)/shard_map/ppermute | solution.py:18
  10.1 0.6 fusion.616
  10.8 0.5 fusion.382
  11.3 1.0 %collective-permute-done.1 = f32[3,7,32,128]{3,2,1,0:T(8,128)S(1)} collective-permute-done((f32[3,7,32,128]{3,2,1,0:T(8,128)S(1)}, f32[3,7,32,128]{3,2,1,0:T(8,128)S(1)}, u32[]{:S(2)}, u32[]{:S(2)}) %collective-permute-start.1) | collective-permute-done | bytes 344096 | tf_op jit(solution)/shard_map/ppermute | solution.py:19
  12.3 3.9 %collective-permute-done = f32[3,7,32,128]{3,2,1,0:T(8,128)S(1)} collective-permute-done((f32[3,7,32,128]{3,2,1,0:T(8,128)S(1)}, f32[3,7,32,128]{3,2,1,0:T(8,128)S(1)}, u32[]{:S(2)}, u32[]{:S(2)}) %collective-permute-start) | collective-permute-done | bytes 344096 | tf_op jit(solution)/shard_map/ppermute | solution.py:18
  16.3 0.1 fusion.122
  16.4 0.8 copy-done.6
  17.2 1.0 %fusion.587 = (f32[1,8,32,128]{3,2,1,0:T(8,128)S(1)}, f32[1,8,32,128]{3,2,1,0:T(8,128)S(1)}) fusion(f32[8,32,128]{2,1,0:T(8,128)S(1)} %get-tuple-element.45, f32[1,8,32,128]{3,2,1,0:T(8,128)S(1)} %copy-done.6, f32[1,8,32,128]{3,2,1,0:T(8,128)S(1)} %copy-done.1, f32[]{:T(128)} %bitcast.4, s32[]{:T(128)} %bitcast.3, s32[32]{0:T(128)S(1)} %iota_multiply_fusion, ...), kind=kLoop, calls=%fused_computation.883 | loop fusion | flops 1441792 | bytes 1966248 | tf_op jit(solution)/shard_map/add | solution.py:152
  18.2 0.3 fusion.359
  18.5 4.4 %collective-permute-start.2 = (f32[1,7,32,128]{3,2,1,0:T(8,128)S(1)}, f32[1,7,32,128]{3,2,1,0:T(8,128)S(1)}, u32[]{:S(2)}, u32[]{:S(2)}) collective-permute-start(f32[1,7,32,128]{3,2,1,0:T(8,128)S(1)} %get-tuple-element.76), channel_id=1, source_target_pairs={{0,1},{1,2},{2,3},{3,4},{4,5},{5,6},{6,7},{7,8},{8,9},{9,10},{10,1... | collective-permute-start | bytes 344072 | tf_op jit(solution)/shard_map/ppermute | solution.py:18
  22.9 1.9 %collective-permute-start.3 = (f32[1,7,32,128]{3,2,1,0:T(8,128)S(1)}, f32[1,7,32,128]{3,2,1,0:T(8,128)S(1)}, u32[]{:S(2)}, u32[]{:S(2)}) collective-permute-start(f32[1,7,32,128]{3,2,1,0:T(8,128)S(1)} %get-tuple-element.77), channel_id=1, source_target_pairs={{1,0},{2,1},{3,2},{4,3},{5,4},{6,5},{7,6},{8,7},{9,8},{10,9},{11,1... | collective-permute-start | bytes 344072 | tf_op jit(solution)/shard_map/ppermute | solution.py:19
  24.8 0.3 fusion.176
  25.1 0.1 fusion.114
  25.3 1.6 %fusion.16 = f32[2048]{0:T(1024)S(1)} fusion(f32[256,128]{1,0:T(8,128)S(1)} %bitcast.128, s32[2048]{0:T(1024)S(1)} %bitcast.147, s32[2048]{0:T(1024)S(1)} %bitcast.139), kind=kOutput, calls=%fused_computation.15 | convolution fusion | flops 806615040 | bytes 155648 | tf_op jit(solution)/shard_map/srk,skz->srz/dot_general | solution.py:129
  26.9 2.1 %collective-permute-done.3 = f32[1,7,32,128]{3,2,1,0:T(8,128)S(1)} collective-permute-done((f32[1,7,32,128]{3,2,1,0:T(8,128)S(1)}, f32[1,7,32,128]{3,2,1,0:T(8,128)S(1)}, u32[]{:S(2)}, u32[]{:S(2)}) %collective-permute-start.3) | collective-permute-done | bytes 114720 | tf_op jit(solution)/shard_map/ppermute | solution.py:19
  29.0 0.1 fusion.107
  29.2 0.8 fusion.589
  29.9 0.3 fusion.405
  30.3 1.9 %collective-permute-start.4 = (f32[1,7,32,128]{3,2,1,0:T(8,128)S(1)}, f32[1,7,32,128]{3,2,1,0:T(8,128)S(1)}, u32[]{:S(2)}, u32[]{:S(2)}) collective-permute-start(f32[1,7,32,128]{3,2,1,0:T(8,128)S(1)} %get-tuple-element.74), channel_id=1, source_target_pairs={{0,1},{1,2},{2,3},{3,4},{4,5},{5,6},{6,7},{7,8},{8,9},{9,10},{10,1... | collective-permute-start | bytes 344072 | tf_op jit(solution)/shard_map/ppermute | solution.py:18
  32.2 2.4 %collective-permute-start.5 = (f32[1,7,32,128]{3,2,1,0:T(8,128)S(1)}, f32[1,7,32,128]{3,2,1,0:T(8,128)S(1)}, u32[]{:S(2)}, u32[]{:S(2)}) collective-permute-start(f32[1,7,32,128]{3,2,1,0:T(8,128)S(1)} %get-tuple-element.75), channel_id=1, source_target_pairs={{1,0},{2,1},{3,2},{4,3},{5,4},{6,5},{7,6},{8,7},{9,8},{10,9},{11,1... | collective-permute-start | bytes 344072 | tf_op jit(solution)/shard_map/ppermute | solution.py:19
  34.6 0.3 fusion.228
  34.9 1.6 %fusion.19 = f32[2048]{0:T(1024)S(1)} fusion(f32[256,128]{1,0:T(8,128)S(1)} %bitcast.127, s32[2048]{0:T(1024)S(1)} %bitcast.148, s32[2048]{0:T(1024)S(1)} %bitcast.140), kind=kOutput, calls=%fused_computation.16 | convolution fusion | flops 806615040 | bytes 155648 | tf_op jit(solution)/shard_map/srk,skz->srz/dot_general | solution.py:129
  36.5 1.8 %collective-permute-done.5 = f32[1,7,32,128]{3,2,1,0:T(8,128)S(1)} collective-permute-done((f32[1,7,32,128]{3,2,1,0:T(8,128)S(1)}, f32[1,7,32,128]{3,2,1,0:T(8,128)S(1)}, u32[]{:S(2)}, u32[]{:S(2)}) %collective-permute-start.5) | collective-permute-done | bytes 114720 | tf_op jit(solution)/shard_map/ppermute | solution.py:19
  38.3 0.1 fusion.100
  38.4 0.7 fusion.591
  39.2 0.3 fusion.428
  39.5 1.9 %collective-permute-start.6 = (f32[1,7,32,128]{3,2,1,0:T(8,128)S(1)}, f32[1,7,32,128]{3,2,1,0:T(8,128)S(1)}, u32[]{:S(2)}, u32[]{:S(2)}) collective-permute-start(f32[1,7,32,128]{3,2,1,0:T(8,128)S(1)} %get-tuple-element.72), channel_id=1, source_target_pairs={{0,1},{1,2},{2,3},{3,4},{4,5},{5,6},{6,7},{7,8},{8,9},{9,10},{10,1... | collective-permute-start | bytes 344072 | tf_op jit(solution)/shard_map/ppermute | solution.py:18
  41.5 2.4 %collective-permute-start.7 = (f32[1,7,32,128]{3,2,1,0:T(8,128)S(1)}, f32[1,7,32,128]{3,2,1,0:T(8,128)S(1)}, u32[]{:S(2)}, u32[]{:S(2)}) collective-permute-start(f32[1,7,32,128]{3,2,1,0:T(8,128)S(1)} %get-tuple-element.73), channel_id=1, source_target_pairs={{1,0},{2,1},{3,2},{4,3},{5,4},{6,5},{7,6},{8,7},{9,8},{10,9},{11,1... | collective-permute-start | bytes 344072 | tf_op jit(solution)/shard_map/ppermute | solution.py:19
  43.9 0.3 fusion.252
  44.2 1.6 %fusion.22 = f32[2048]{0:T(1024)S(1)} fusion(f32[256,128]{1,0:T(8,128)S(1)} %bitcast.129, s32[2048]{0:T(1024)S(1)} %bitcast.149, s32[2048]{0:T(1024)S(1)} %bitcast.141), kind=kOutput, calls=%fused_computation.17 | convolution fusion | flops 806615040 | bytes 155648 | tf_op jit(solution)/shard_map/srk,skz->srz/dot_general | solution.py:129
  45.8 2.6 %collective-permute-done.7 = f32[1,7,32,128]{3,2,1,0:T(8,128)S(1)} collective-permute-done((f32[1,7,32,128]{3,2,1,0:T(8,128)S(1)}, f32[1,7,32,128]{3,2,1,0:T(8,128)S(1)}, u32[]{:S(2)}, u32[]{:S(2)}) %collective-permute-start.7) | collective-permute-done | bytes 114720 | tf_op jit(solution)/shard_map/ppermute | solution.py:19
  48.5 0.1 fusion.93
  48.6 0.7 fusion.593
  49.3 1.6 %fusion.13 = f32[2048]{0:T(1024)S(1)} fusion(f32[256,128]{1,0:T(8,128)S(1)} %bitcast.130, s32[2048]{0:T(1024)S(1)} %bitcast.150, s32[2048]{0:T(1024)S(1)} %bitcast.142), kind=kOutput, calls=%fused_computation.14 | convolution fusion | flops 806615040 | bytes 155648 | tf_op jit(solution)/shard_map/srk,skz->srz/dot_general | solution.py:129
  51.0 1.2 %fusion.25 = f32[1,8,32,128]{3,2,1,0:T(8,128)S(1)} fusion(s32[8,32]{1,0:T(8,128)S(1)} %multiply_add_fusion, s32[2048]{0:T(1024)S(1)} %bitcast.151, f32[2048]{0:T(1024)S(1)} %bitcast.137, s32[2048]{0:T(1024)S(1)} %bitcast.143), kind=kOutput, calls=%fused_computation.18 | convolution fusion | flops 806354944 | bytes 156672 | tf_op jit(solution)/shard_map/srk,srz->skz/dot_general | solution.py:136
  52.3 0.6 fusion.594
  53.6 0.3 fusion.204
  54.0 0.3 fusion.451
  54.3 3.0 %collective-permute-start.10 = (f32[1]{0:T(128)}, f32[1]{0:T(128)}, u32[]{:S(2)}, u32[]{:S(2)}) collective-permute-start(f32[1]{0:T(128)} %bitcast.30), channel_id=1, source_target_pairs={{0,2},{1,3},{2,0},{3,1},{4,6},{5,7},{6,4},{7,5},{8,10},{9,11},{10,... | collective-permute-start | bytes 20 | tf_op jit(solution)/shard_map/ppermute | solution.py:36
  57.3 1.9 %collective-permute-start.8 = (f32[1,7,32,128]{3,2,1,0:T(8,128)S(1)}, f32[1,7,32,128]{3,2,1,0:T(8,128)S(1)}, u32[]{:S(2)}, u32[]{:S(2)}) collective-permute-start(f32[1,7,32,128]{3,2,1,0:T(8,128)S(1)} %get-tuple-element.68), channel_id=1, source_target_pairs={{0,1},{1,2},{2,3},{3,4},{4,5},{5,6},{6,7},{7,8},{8,9},{9,10},{10,1... | collective-permute-start | bytes 344072 | tf_op jit(solution)/shard_map/ppermute | solution.py:18
  59.2 2.4 %collective-permute-start.9 = (f32[1,7,32,128]{3,2,1,0:T(8,128)S(1)}, f32[1,7,32,128]{3,2,1,0:T(8,128)S(1)}, u32[]{:S(2)}, u32[]{:S(2)}) collective-permute-start(f32[1,7,32,128]{3,2,1,0:T(8,128)S(1)} %get-tuple-element.69), channel_id=1, source_target_pairs={{1,0},{2,1},{3,2},{4,3},{5,4},{6,5},{7,6},{8,7},{9,8},{10,9},{11,1... | collective-permute-start | bytes 344072 | tf_op jit(solution)/shard_map/ppermute | solution.py:19
  61.6 0.3 fusion.276
  61.9 1.2 %fusion.28 = f32[1,8,32,128]{3,2,1,0:T(8,128)S(1)} fusion(s32[8,32]{1,0:T(8,128)S(1)} %multiply_add_fusion, s32[2048]{0:T(1024)S(1)} %bitcast.152, f32[2048]{0:T(1024)S(1)} %bitcast.136, s32[2048]{0:T(1024)S(1)} %bitcast.144), kind=kOutput, calls=%fused_computation.19 | convolution fusion | flops 806354944 | bytes 156672 | tf_op jit(solution)/shard_map/srk,srz->skz/dot_general | solution.py:136
  63.9 1.5 %collective-permute-done.9 = f32[1,7,32,128]{3,2,1,0:T(8,128)S(1)} collective-permute-done((f32[1,7,32,128]{3,2,1,0:T(8,128)S(1)}, f32[1,7,32,128]{3,2,1,0:T(8,128)S(1)}, u32[]{:S(2)}, u32[]{:S(2)}) %collective-permute-start.9) | collective-permute-done | bytes 114720 | tf_op jit(solution)/shard_map/ppermute | solution.py:19
  65.4 0.1 fusion.86
  65.6 0.3 fusion.474
  65.9 2.1 %collective-permute-start.13 = (f32[1]{0:T(128)}, f32[1]{0:T(128)}, u32[]{:S(2)}, u32[]{:S(2)}) collective-permute-start(f32[1]{0:T(128)} %add.806), channel_id=1, source_target_pairs={{0,4},{1,5},{2,6},{3,7},{4,0},{5,1},{6,2},{7,3},{8,12},{9,13},{10,... | collective-permute-start | bytes 20 | tf_op jit(solution)/shard_map/ppermute | solution.py:36
  68.0 2.8 %collective-permute-start.11 = (f32[1,7,32,128]{3,2,1,0:T(8,128)S(1)}, f32[1,7,32,128]{3,2,1,0:T(8,128)S(1)}, u32[]{:S(2)}, u32[]{:S(2)}) collective-permute-start(f32[1,7,32,128]{3,2,1,0:T(8,128)S(1)} %get-tuple-element.66), channel_id=1, source_target_pairs={{0,1},{1,2},{2,3},{3,4},{4,5},{5,6},{6,7},{7,8},{8,9},{9,10},{10,1... | collective-permute-start | bytes 344072 | tf_op jit(solution)/shard_map/ppermute | solution.py:18
  70.8 1.9 %collective-permute-start.12 = (f32[1,7,32,128]{3,2,1,0:T(8,128)S(1)}, f32[1,7,32,128]{3,2,1,0:T(8,128)S(1)}, u32[]{:S(2)}, u32[]{:S(2)}) collective-permute-start(f32[1,7,32,128]{3,2,1,0:T(8,128)S(1)} %get-tuple-element.67), channel_id=1, source_target_pairs={{1,0},{2,1},{3,2},{4,3},{5,4},{6,5},{7,6},{8,7},{9,8},{10,9},{11,1... | collective-permute-start | bytes 344072 | tf_op jit(solution)/shard_map/ppermute | solution.py:19
  72.8 0.3 fusion.300
  73.1 1.2 %fusion.31 = f32[1,8,32,128]{3,2,1,0:T(8,128)S(1)} fusion(s32[8,32]{1,0:T(8,128)S(1)} %multiply_add_fusion, s32[2048]{0:T(1024)S(1)} %bitcast.153, f32[2048]{0:T(1024)S(1)} %bitcast.134, s32[2048]{0:T(1024)S(1)} %bitcast.145), kind=kOutput, calls=%fused_computation.20 | convolution fusion | flops 806354944 | bytes 156672 | tf_op jit(solution)/shard_map/srk,srz->skz/dot_general | solution.py:136
  75.0 1.9 %collective-permute-done.12 = f32[1,7,32,128]{3,2,1,0:T(8,128)S(1)} collective-permute-done((f32[1,7,32,128]{3,2,1,0:T(8,128)S(1)}, f32[1,7,32,128]{3,2,1,0:T(8,128)S(1)}, u32[]{:S(2)}, u32[]{:S(2)}) %collective-permute-start.12) | collective-permute-done | bytes 114720 | tf_op jit(solution)/shard_map/ppermute | solution.py:19
  77.2 0.3 fusion.497
  77.6 2.8 %collective-permute-start.16 = (f32[1]{0:T(128)}, f32[1]{0:T(128)}, u32[]{:S(2)}, u32[]{:S(2)}) collective-permute-start(f32[1]{0:T(128)} %add.830), channel_id=1, source_target_pairs={{0,8},{1,9},{2,10},{3,11},{4,12},{5,13},{6,14},{7,15},{8,0},{9,1},... | collective-permute-start | bytes 20 | tf_op jit(solution)/shard_map/ppermute | solution.py:36
  80.4 2.6 %collective-permute-start.14 = (f32[1,7,32,128]{3,2,1,0:T(8,128)S(1)}, f32[1,7,32,128]{3,2,1,0:T(8,128)S(1)}, u32[]{:S(2)}, u32[]{:S(2)}) collective-permute-start(f32[1,7,32,128]{3,2,1,0:T(8,128)S(1)} %get-tuple-element.64), channel_id=1, source_target_pairs={{0,1},{1,2},{2,3},{3,4},{4,5},{5,6},{6,7},{7,8},{8,9},{9,10},{10,1... | collective-permute-start | bytes 344072 | tf_op jit(solution)/shard_map/ppermute | solution.py:18
  83.0 1.9 %collective-permute-start.15 = (f32[1,7,32,128]{3,2,1,0:T(8,128)S(1)}, f32[1,7,32,128]{3,2,1,0:T(8,128)S(1)}, u32[]{:S(2)}, u32[]{:S(2)}) collective-permute-start(f32[1,7,32,128]{3,2,1,0:T(8,128)S(1)} %get-tuple-element.65), channel_id=1, source_target_pairs={{1,0},{2,1},{3,2},{4,3},{5,4},{6,5},{7,6},{8,7},{9,8},{10,9},{11,1... | collective-permute-start | bytes 344072 | tf_op jit(solution)/shard_map/ppermute | solution.py:19
  85.0 0.3 fusion.324
  85.3 1.2 %fusion.34 = f32[1,8,32,128]{3,2,1,0:T(8,128)S(1)} fusion(s32[8,32]{1,0:T(8,128)S(1)} %multiply_add_fusion, s32[2048]{0:T(1024)S(1)} %bitcast.154, f32[2048]{0:T(1024)S(1)} %bitcast.132, s32[2048]{0:T(1024)S(1)} %bitcast.146), kind=kOutput, calls=%fused_computation.21 | convolution fusion | flops 806354944 | bytes 156672 | tf_op jit(solution)/shard_map/srk,srz->skz/dot_general | solution.py:136
  87.2 0.9 collective-permute-start.17
  88.1 0.3 collective-permute-done.17
  89.3 0.9 bitcast_multiply_fusion
  (57 shorter events, 1.2 us)
Async XLA Ops:
  1.7 7.7 %copy-start = (f32[8,32,128]{2,1,0:T(8,128)S(1)}, f32[8,32,128]{2,1,0:T(8,128)}, u32[]{:S(2)}) copy-start(f32[8,32,128]{2,1,0:T(8,128)} %param.11) | copy-start | bytes 393220
  1.7 7.7 %copy-start.4 = (f32[8,32,128]{2,1,0:T(8,128)S(1)}, f32[8,32,128]{2,1,0:T(8,128)}, u32[]{:S(2)}) copy-start(f32[8,32,128]{2,1,0:T(8,128)} %param.10) | copy-start | bytes 393220
  2.8 7.3 %copy-start.9 = (f32[1,4]{1,0:T(1,128)S(1)}, f32[1,4]{1,0:T(1,128)}, u32[]{:S(2)}) copy-start(f32[1,4]{1,0:T(1,128)} %param.17) | copy-start | bytes 52
  2.8 7.9 %copy-start.7 = (s32[1,2048]{1,0:T(1,128)S(1)}, s32[1,2048]{1,0:T(1,128)}, u32[]{:S(2)}) copy-start(s32[1,2048]{1,0:T(1,128)} %param.18) | copy-start | bytes 24580
  2.8 8.0 %copy-start.1 = (f32[1,8,32,128]{3,2,1,0:T(8,128)S(1)}, f32[1,8,32,128]{3,2,1,0:T(8,128)}, u32[]{:S(2)}) copy-start(f32[1,8,32,128]{3,2,1,0:T(8,128)} %param.13) | copy-start | bytes 393220
  2.9 9.5 %collective-permute-start.1 = (f32[3,7,32,128]{3,2,1,0:T(8,128)S(1)}, f32[3,7,32,128]{3,2,1,0:T(8,128)S(1)}, u32[]{:S(2)}, u32[]{:S(2)}) collective-permute-start(f32[3,7,32,128]{3,2,1,0:T(8,128)S(1)} %get-tuple-element.46), channel_id=1, source_target_pairs={{1,0},{2,1},{3,2},{4,3},{5,4},{6,5},{7,6},{8,7},{9,8},{10,9},{11,1... | collective-permute-start | bytes 1032200 | tf_op jit(solution)/shard_map/ppermute | solution.py:19
  4.8 11.3 %collective-permute-start = (f32[3,7,32,128]{3,2,1,0:T(8,128)S(1)}, f32[3,7,32,128]{3,2,1,0:T(8,128)S(1)}, u32[]{:S(2)}, u32[]{:S(2)}) collective-permute-start(f32[3,7,32,128]{3,2,1,0:T(8,128)S(1)} %get-tuple-element.47), channel_id=1, source_target_pairs={{0,1},{1,2},{2,3},{3,4},{4,5},{5,6},{6,7},{7,8},{8,9},{9,10},{10,1... | collective-permute-start | bytes 1032200 | tf_op jit(solution)/shard_map/ppermute | solution.py:18
  16.3 0.9 copy-start.6
  18.5 8.4 %collective-permute-start.2 = (f32[1,7,32,128]{3,2,1,0:T(8,128)S(1)}, f32[1,7,32,128]{3,2,1,0:T(8,128)S(1)}, u32[]{:S(2)}, u32[]{:S(2)}) collective-permute-start(f32[1,7,32,128]{3,2,1,0:T(8,128)S(1)} %get-tuple-element.76), channel_id=1, source_target_pairs={{0,1},{1,2},{2,3},{3,4},{4,5},{5,6},{6,7},{7,8},{8,9},{9,10},{10,1... | collective-permute-start | bytes 344072 | tf_op jit(solution)/shard_map/ppermute | solution.py:18
  22.9 6.1 %collective-permute-start.3 = (f32[1,7,32,128]{3,2,1,0:T(8,128)S(1)}, f32[1,7,32,128]{3,2,1,0:T(8,128)S(1)}, u32[]{:S(2)}, u32[]{:S(2)}) collective-permute-start(f32[1,7,32,128]{3,2,1,0:T(8,128)S(1)} %get-tuple-element.77), channel_id=1, source_target_pairs={{1,0},{2,1},{3,2},{4,3},{5,4},{6,5},{7,6},{8,7},{9,8},{10,9},{11,1... | collective-permute-start | bytes 344072 | tf_op jit(solution)/shard_map/ppermute | solution.py:19
  30.3 6.3 %collective-permute-start.4 = (f32[1,7,32,128]{3,2,1,0:T(8,128)S(1)}, f32[1,7,32,128]{3,2,1,0:T(8,128)S(1)}, u32[]{:S(2)}, u32[]{:S(2)}) collective-permute-start(f32[1,7,32,128]{3,2,1,0:T(8,128)S(1)} %get-tuple-element.74), channel_id=1, source_target_pairs={{0,1},{1,2},{2,3},{3,4},{4,5},{5,6},{6,7},{7,8},{8,9},{9,10},{10,1... | collective-permute-start | bytes 344072 | tf_op jit(solution)/shard_map/ppermute | solution.py:18
  32.2 6.1 %collective-permute-start.5 = (f32[1,7,32,128]{3,2,1,0:T(8,128)S(1)}, f32[1,7,32,128]{3,2,1,0:T(8,128)S(1)}, u32[]{:S(2)}, u32[]{:S(2)}) collective-permute-start(f32[1,7,32,128]{3,2,1,0:T(8,128)S(1)} %get-tuple-element.75), channel_id=1, source_target_pairs={{1,0},{2,1},{3,2},{4,3},{5,4},{6,5},{7,6},{8,7},{9,8},{10,9},{11,1... | collective-permute-start | bytes 344072 | tf_op jit(solution)/shard_map/ppermute | solution.py:19
  39.5 6.3 %collective-permute-start.6 = (f32[1,7,32,128]{3,2,1,0:T(8,128)S(1)}, f32[1,7,32,128]{3,2,1,0:T(8,128)S(1)}, u32[]{:S(2)}, u32[]{:S(2)}) collective-permute-start(f32[1,7,32,128]{3,2,1,0:T(8,128)S(1)} %get-tuple-element.72), channel_id=1, source_target_pairs={{0,1},{1,2},{2,3},{3,4},{4,5},{5,6},{6,7},{7,8},{8,9},{9,10},{10,1... | collective-permute-start | bytes 344072 | tf_op jit(solution)/shard_map/ppermute | solution.py:18
  41.5 7.0 %collective-permute-start.7 = (f32[1,7,32,128]{3,2,1,0:T(8,128)S(1)}, f32[1,7,32,128]{3,2,1,0:T(8,128)S(1)}, u32[]{:S(2)}, u32[]{:S(2)}) collective-permute-start(f32[1,7,32,128]{3,2,1,0:T(8,128)S(1)} %get-tuple-element.73), channel_id=1, source_target_pairs={{1,0},{2,1},{3,2},{4,3},{5,4},{6,5},{7,6},{8,7},{9,8},{10,9},{11,1... | collective-permute-start | bytes 344072 | tf_op jit(solution)/shard_map/ppermute | solution.py:19
  49.3 1.7 %copy-start.8 = (f32[1,4,2048]{2,1,0:T(4,128)S(1)}, f32[1,4,2048]{2,1,0:T(4,128)}, u32[]{:S(2)}) copy-start(f32[1,4,2048]{2,1,0:T(4,128)} %param.19) | copy-start | bytes 98308
  50.9 2.6 %copy-start.2 = (f32[1,8,32,128]{3,2,1,0:T(8,128)S(1)}, f32[1,8,32,128]{3,2,1,0:T(8,128)}, u32[]{:S(2)}) copy-start(f32[1,8,32,128]{3,2,1,0:T(8,128)} %param.14) | copy-start | bytes 393220
  51.0 2.6 %copy-start.5 = (f32[1,8,32,128]{3,2,1,0:T(8,128)S(1)}, f32[1,8,32,128]{3,2,1,0:T(8,128)}, u32[]{:S(2)}) copy-start(f32[1,8,32,128]{3,2,1,0:T(8,128)} %param.15) | copy-start | bytes 393220
  54.3 8.9 %collective-permute-start.10 = (f32[1]{0:T(128)}, f32[1]{0:T(128)}, u32[]{:S(2)}, u32[]{:S(2)}) collective-permute-start(f32[1]{0:T(128)} %bitcast.30), channel_id=1, source_target_pairs={{0,2},{1,3},{2,0},{3,1},{4,6},{5,7},{6,4},{7,5},{8,10},{9,11},{10,... | collective-permute-start | bytes 20 | tf_op jit(solution)/shard_map/ppermute | solution.py:36
  57.3 6.6 %collective-permute-start.8 = (f32[1,7,32,128]{3,2,1,0:T(8,128)S(1)}, f32[1,7,32,128]{3,2,1,0:T(8,128)S(1)}, u32[]{:S(2)}, u32[]{:S(2)}) collective-permute-start(f32[1,7,32,128]{3,2,1,0:T(8,128)S(1)} %get-tuple-element.68), channel_id=1, source_target_pairs={{0,1},{1,2},{2,3},{3,4},{4,5},{5,6},{6,7},{7,8},{8,9},{9,10},{10,1... | collective-permute-start | bytes 344072 | tf_op jit(solution)/shard_map/ppermute | solution.py:18
  59.2 6.1 %collective-permute-start.9 = (f32[1,7,32,128]{3,2,1,0:T(8,128)S(1)}, f32[1,7,32,128]{3,2,1,0:T(8,128)S(1)}, u32[]{:S(2)}, u32[]{:S(2)}) collective-permute-start(f32[1,7,32,128]{3,2,1,0:T(8,128)S(1)} %get-tuple-element.69), channel_id=1, source_target_pairs={{1,0},{2,1},{3,2},{4,3},{5,4},{6,5},{7,6},{8,7},{9,8},{10,9},{11,1... | collective-permute-start | bytes 344072 | tf_op jit(solution)/shard_map/ppermute | solution.py:19
  65.9 8.4 %collective-permute-start.13 = (f32[1]{0:T(128)}, f32[1]{0:T(128)}, u32[]{:S(2)}, u32[]{:S(2)}) collective-permute-start(f32[1]{0:T(128)} %add.806), channel_id=1, source_target_pairs={{0,4},{1,5},{2,6},{3,7},{4,0},{5,1},{6,2},{7,3},{8,12},{9,13},{10,... | collective-permute-start | bytes 20 | tf_op jit(solution)/shard_map/ppermute | solution.py:36
  68.0 7.0 %collective-permute-start.11 = (f32[1,7,32,128]{3,2,1,0:T(8,128)S(1)}, f32[1,7,32,128]{3,2,1,0:T(8,128)S(1)}, u32[]{:S(2)}, u32[]{:S(2)}) collective-permute-start(f32[1,7,32,128]{3,2,1,0:T(8,128)S(1)} %get-tuple-element.66), channel_id=1, source_target_pairs={{0,1},{1,2},{2,3},{3,4},{4,5},{5,6},{6,7},{7,8},{8,9},{9,10},{10,1... | collective-permute-start | bytes 344072 | tf_op jit(solution)/shard_map/ppermute | solution.py:18
  70.8 6.1 %collective-permute-start.12 = (f32[1,7,32,128]{3,2,1,0:T(8,128)S(1)}, f32[1,7,32,128]{3,2,1,0:T(8,128)S(1)}, u32[]{:S(2)}, u32[]{:S(2)}) collective-permute-start(f32[1,7,32,128]{3,2,1,0:T(8,128)S(1)} %get-tuple-element.67), channel_id=1, source_target_pairs={{1,0},{2,1},{3,2},{4,3},{5,4},{6,5},{7,6},{8,7},{9,8},{10,9},{11,1... | collective-permute-start | bytes 344072 | tf_op jit(solution)/shard_map/ppermute | solution.py:19
  77.2 12.1 %copy-start.3 = (f32[1,8,32,128]{3,2,1,0:T(8,128)}, f32[1,8,32,128]{3,2,1,0:T(8,128)S(1)}, u32[]{:S(2)}) copy-start(f32[1,8,32,128]{3,2,1,0:T(8,128)S(1)} %fusion.531) | copy-start | bytes 393220
  77.6 9.0 %collective-permute-start.16 = (f32[1]{0:T(128)}, f32[1]{0:T(128)}, u32[]{:S(2)}, u32[]{:S(2)}) collective-permute-start(f32[1]{0:T(128)} %add.830), channel_id=1, source_target_pairs={{0,8},{1,9},{2,10},{3,11},{4,12},{5,13},{6,14},{7,15},{8,0},{9,1},... | collective-permute-start | bytes 20 | tf_op jit(solution)/shard_map/ppermute | solution.py:36
  80.4 8.7 %collective-permute-start.14 = (f32[1,7,32,128]{3,2,1,0:T(8,128)S(1)}, f32[1,7,32,128]{3,2,1,0:T(8,128)S(1)}, u32[]{:S(2)}, u32[]{:S(2)}) collective-permute-start(f32[1,7,32,128]{3,2,1,0:T(8,128)S(1)} %get-tuple-element.64), channel_id=1, source_target_pairs={{0,1},{1,2},{2,3},{3,4},{4,5},{5,6},{6,7},{7,8},{8,9},{9,10},{10,1... | collective-permute-start | bytes 344072 | tf_op jit(solution)/shard_map/ppermute | solution.py:18
  83.0 6.1 %collective-permute-start.15 = (f32[1,7,32,128]{3,2,1,0:T(8,128)S(1)}, f32[1,7,32,128]{3,2,1,0:T(8,128)S(1)}, u32[]{:S(2)}, u32[]{:S(2)}) collective-permute-start(f32[1,7,32,128]{3,2,1,0:T(8,128)S(1)} %get-tuple-element.65), channel_id=1, source_target_pairs={{1,0},{2,1},{3,2},{4,3},{5,4},{6,5},{7,6},{8,7},{9,8},{10,9},{11,1... | collective-permute-start | bytes 344072 | tf_op jit(solution)/shard_map/ppermute | solution.py:19
  87.2 1.2 %collective-permute-start.17 = (f32[1]{0:T(128)}, f32[1]{0:T(128)}, u32[]{:S(2)}, u32[]{:S(2)}) collective-permute-start(f32[1]{0:T(128)} %add.854), channel_id=1, source_target_pairs={{0,1},{1,0},{2,3},{3,2},{4,5},{5,4},{6,7},{7,6},{8,9},{9,8},{10,11... | collective-permute-start | bytes 20 | tf_op jit(solution)/shard_map/ppermute | solution.py:36

commit v18 on v17

--- a/solution.py
+++ b/solution.py
@@ -96,11 +96,10 @@
         flux = flux_buoyancy * forward_diff(wide, 1, planes + 7, start=HALO - 4)
         return backward_diff(flux, 1, planes) + cross_terms(values, buoyancy)
 
-    adjoint_operand = kappa * adjoint_next
-    first = extended(jnp.concatenate([buoyancy[None], wave_now, adjoint_operand], axis=0), 1, HALO)
+    first = extended(jnp.concatenate([buoyancy[None], wave_now], axis=0), 1, HALO)
     flux_buoyancy = first[0, HALO - 4 : HALO + planes + 3]
     first_lap = wide_operator(first[1 : 1 + shots], wave_now, flux_buoyancy)
-    adjoint_lap = wide_operator(first[1 + shots :], adjoint_operand, flux_buoyancy)
+    adjoint_operand = kappa * adjoint_next
 
     def operator(values, later=None):
         wide = extended(values, 1, HALO)
@@ -143,7 +142,8 @@
         if step == 0:
             lap = first_lap
         elif step == 1:
-            lap, scale = operator(current, 2.0 * velocity / buoyancy)
+            both, scale = operator(jnp.concatenate([current, adjoint_operand], axis=0), 2.0 * velocity / buoyancy)
+            lap, adjoint_lap = both[:shots], both[shots:]
         else:
             lap = operator(current)
         laps.append(lap)

time: 92.9 us -> 90.4 us (0.973)
  starting transfers between devices: 43.9 us -> 42 us
    ppermute x7, waiting for transfers between devices: 11 us -> 15.6 us  [extended(): after = lax.ppermute(first, 'mp', down)]
    ppermute x7, waiting for transfers between devices: 3.87 us -> 0.02 us  [extended(): before = lax.ppermute(last, 'mp', up)]
    ppermute x7, starting transfers between devices: 20.1 us -> 17.5 us  [extended(): before = lax.ppermute(last, 'mp', up)]
    mul x1, other arithmetic: 1.06 us -> 0.02 us  [local(): adjoint_operand = kappa * adjoint_next]
  transfers between devices with their start and end apart: 18 -> 18, of which waited for: 9 -> 8; matrix products, arithmetic and copies ran while one was open for 13% -> 14% of each run, Pallas kernels for 0% -> 0%
where the time goes in v18:
time: 90.4 us; the launch traced here: 88.9 us
  starting transfers between devices  42 us (46%)
  waiting for transfers between devices  15.9 us (18%)
  other arithmetic  12.1 us (13%)
  matrix products  11.4 us (13%)
  between operations  6.01 us (7%)
  local copies, waits for them, and re-layouts  1.51 us (2%)
    ppermute x7, starting transfers between devices, extended(): before = lax.ppermute(last, 'mp', up)  17.5 us
    ppermute x7, starting transfers between devices, extended(): after = lax.ppermute(first, 'mp', down)  15.6 us
    ppermute x7, waiting for transfers between devices, extended(): after = lax.ppermute(first, 'mp', down)  15.6 us
    ppermute x4, starting transfers between devices, butterfly_round(): return values + lax.ppermute(values, axis, pairs)  8.96 us
    dot_general x4, matrix products, sample(): jnp.einsum('srk,skz->srz', row_pick, field.reshape(shots, rows, cz), prec...  6.43 us
    dot_general x4, matrix products, injected(): jnp.einsum('srk,srz->skz', row_pick, spread, precision=lax.Precision.HIGH...  4.93 us
    add x4, other arithmetic, local(): following = following + jnp.where(source_hit, amount, 0.0)  3.25 us
    mul x7, other arithmetic, cross_terms(): flux = buoyancy * forward_diff(pad_axis(values, axis), axis, length)  2.4 us
  transfers between devices with their start and end apart: 18, of which 8 were waited for; matrix products, arithmetic and copies ran while one was open for 14% of the time, Pallas kernels for 0%

profile of v18, /device:TPU:1, one launch (start us, length us, event | category | flops | bytes accessed | tf_op | source)
XLA Modules:
  0.0 88.9 jit_solution(2686995483619448676)
XLA Ops:
  0.7 1.2 %pad_maximum_fusion.12 = (f32[2,7,32,128]{3,2,1,0:T(8,128)S(1)}, f32[2,7,32,128]{3,2,1,0:T(8,128)S(1)}) fusion(f32[1,8,32,128]{3,2,1,0:T(8,128)} %param.13, f32[1,8,32,128]{3,2,1,0:T(8,128)} %bitcast.121), kind=kLoop, calls=%fused_computation.331 | loop fusion | flops 114688 | bytes 720896 | tf_op jit(solution)/shard_map/concatenate | solution.py:99
  1.9 4.5 %collective-permute-start = (f32[2,7,32,128]{3,2,1,0:T(8,128)S(1)}, f32[2,7,32,128]{3,2,1,0:T(8,128)S(1)}, u32[]{:S(2)}, u32[]{:S(2)}) collective-permute-start(f32[2,7,32,128]{3,2,1,0:T(8,128)S(1)} %get-tuple-element.60), channel_id=1, source_target_pairs={{0,1},{1,2},{2,3},{3,4},{4,5},{5,6},{6,7},{7,8},{8,9},{9,10},{10,1... | collective-permute-start | bytes 688136 | tf_op jit(solution)/shard_map/ppermute | solution.py:18
  6.4 1.9 %collective-permute-start.1 = (f32[2,7,32,128]{3,2,1,0:T(8,128)S(1)}, f32[2,7,32,128]{3,2,1,0:T(8,128)S(1)}, u32[]{:S(2)}, u32[]{:S(2)}) collective-permute-start(f32[2,7,32,128]{3,2,1,0:T(8,128)S(1)} %get-tuple-element.59), channel_id=1, source_target_pairs={{1,0},{2,1},{3,2},{4,3},{5,4},{6,5},{7,6},{8,7},{9,8},{10,9},{11,1... | collective-permute-start | bytes 688136 | tf_op jit(solution)/shard_map/ppermute | solution.py:19
  8.4 0.3 fusion.189
  9.4 0.6 fusion.552
  10.1 3.6 %collective-permute-done.1 = f32[2,7,32,128]{3,2,1,0:T(8,128)S(1)} collective-permute-done((f32[2,7,32,128]{3,2,1,0:T(8,128)S(1)}, f32[2,7,32,128]{3,2,1,0:T(8,128)S(1)}, u32[]{:S(2)}, u32[]{:S(2)}) %collective-permute-start.1) | collective-permute-done | bytes 229408 | tf_op jit(solution)/shard_map/ppermute | solution.py:19
  13.8 0.1 slice_bitcast_fusion
  13.9 0.8 copy-done.5
  14.7 1.0 %fusion.526 = (f32[1,8,32,128]{3,2,1,0:T(8,128)S(1)}, f32[1,8,32,128]{3,2,1,0:T(8,128)S(1)}, f32[8,32,128]{2,1,0:T(8,128)S(1)}) fusion(f32[1,8,32,128]{3,2,1,0:T(8,128)S(1)} %copy-done.5, f32[1,8,32,128]{3,2,1,0:T(8,128)S(1)} %copy-done.1, f32[]{:T(128)} %bitcast.4, s32[]{:T(128)} %bitcast.3, s32[32]{0:T(128)S(1)} %iota_multiply_fusion, ...), kind=kLoop, calls=%fused_computation.793 | loop fusion | flops 1507328 | bytes 2228392 | tf_op jit(solution)/shard_map/add | solution.py:152
  15.8 1.9 %collective-permute-start.2 = (f32[2,7,32,128]{3,2,1,0:T(8,128)S(1)}, f32[2,7,32,128]{3,2,1,0:T(8,128)S(1)}, u32[]{:S(2)}, u32[]{:S(2)}) collective-permute-start(f32[2,7,32,128]{3,2,1,0:T(8,128)S(1)} %get-tuple-element.57), channel_id=1, source_target_pairs={{0,1},{1,2},{2,3},{3,4},{4,5},{5,6},{6,7},{7,8},{8,9},{9,10},{10,1... | collective-permute-start | bytes 688136 | tf_op jit(solution)/shard_map/ppermute | solution.py:18
  17.8 2.4 %collective-permute-start.3 = (f32[2,7,32,128]{3,2,1,0:T(8,128)S(1)}, f32[2,7,32,128]{3,2,1,0:T(8,128)S(1)}, u32[]{:S(2)}, u32[]{:S(2)}) collective-permute-start(f32[2,7,32,128]{3,2,1,0:T(8,128)S(1)} %get-tuple-element.58), channel_id=1, source_target_pairs={{1,0},{2,1},{3,2},{4,3},{5,4},{6,5},{7,6},{8,7},{9,8},{10,9},{11,1... | collective-permute-start | bytes 688136 | tf_op jit(solution)/shard_map/ppermute | solution.py:19
  20.2 0.5 fusion.106
  20.7 0.5 fusion.94
  21.3 1.6 %fusion.16 = f32[2048]{0:T(1024)S(1)} fusion(f32[256,128]{1,0:T(8,128)S(1)} %bitcast.125, s32[2048]{0:T(1024)S(1)} %bitcast.144, s32[2048]{0:T(1024)S(1)} %bitcast.136), kind=kOutput, calls=%fused_computation.15 | convolution fusion | flops 806615040 | bytes 155648 | tf_op jit(solution)/shard_map/srk,skz->srz/dot_general | solution.py:128
  22.9 3.0 %collective-permute-done.3 = f32[2,7,32,128]{3,2,1,0:T(8,128)S(1)} collective-permute-done((f32[2,7,32,128]{3,2,1,0:T(8,128)S(1)}, f32[2,7,32,128]{3,2,1,0:T(8,128)S(1)}, u32[]{:S(2)}, u32[]{:S(2)}) %collective-permute-start.3) | collective-permute-done | bytes 229408 | tf_op jit(solution)/shard_map/ppermute | solution.py:19
  25.9 0.2 fusion.72
  26.2 0.1 fusion.126
  26.3 0.7 fusion.528
  27.1 0.3 fusion.357
  27.4 1.9 %collective-permute-start.4 = (f32[1,7,32,128]{3,2,1,0:T(8,128)S(1)}, f32[1,7,32,128]{3,2,1,0:T(8,128)S(1)}, u32[]{:S(2)}, u32[]{:S(2)}) collective-permute-start(f32[1,7,32,128]{3,2,1,0:T(8,128)S(1)} %get-tuple-element.71), channel_id=1, source_target_pairs={{0,1},{1,2},{2,3},{3,4},{4,5},{5,6},{6,7},{7,8},{8,9},{9,10},{10,1... | collective-permute-start | bytes 344072 | tf_op jit(solution)/shard_map/ppermute | solution.py:18
  29.3 2.4 %collective-permute-start.5 = (f32[1,7,32,128]{3,2,1,0:T(8,128)S(1)}, f32[1,7,32,128]{3,2,1,0:T(8,128)S(1)}, u32[]{:S(2)}, u32[]{:S(2)}) collective-permute-start(f32[1,7,32,128]{3,2,1,0:T(8,128)S(1)} %get-tuple-element.72), channel_id=1, source_target_pairs={{1,0},{2,1},{3,2},{4,3},{5,4},{6,5},{7,6},{8,7},{9,8},{10,9},{11,1... | collective-permute-start | bytes 344072 | tf_op jit(solution)/shard_map/ppermute | solution.py:19
  31.7 0.3 fusion.226
  32.0 1.6 %fusion.19 = f32[2048]{0:T(1024)S(1)} fusion(f32[256,128]{1,0:T(8,128)S(1)} %bitcast.124, s32[2048]{0:T(1024)S(1)} %bitcast.145, s32[2048]{0:T(1024)S(1)} %bitcast.137), kind=kOutput, calls=%fused_computation.16 | convolution fusion | flops 806615040 | bytes 155648 | tf_op jit(solution)/shard_map/srk,skz->srz/dot_general | solution.py:128
  33.6 2.7 %collective-permute-done.5 = f32[1,7,32,128]{3,2,1,0:T(8,128)S(1)} collective-permute-done((f32[1,7,32,128]{3,2,1,0:T(8,128)S(1)}, f32[1,7,32,128]{3,2,1,0:T(8,128)S(1)}, u32[]{:S(2)}, u32[]{:S(2)}) %collective-permute-start.5) | collective-permute-done | bytes 114720 | tf_op jit(solution)/shard_map/ppermute | solution.py:19
  36.3 0.1 fusion.163
  36.5 0.7 fusion.530
  37.2 0.3 fusion.380
  37.5 1.9 %collective-permute-start.6 = (f32[1,7,32,128]{3,2,1,0:T(8,128)S(1)}, f32[1,7,32,128]{3,2,1,0:T(8,128)S(1)}, u32[]{:S(2)}, u32[]{:S(2)}) collective-permute-start(f32[1,7,32,128]{3,2,1,0:T(8,128)S(1)} %get-tuple-element.69), channel_id=1, source_target_pairs={{0,1},{1,2},{2,3},{3,4},{4,5},{5,6},{6,7},{7,8},{8,9},{9,10},{10,1... | collective-permute-start | bytes 344072 | tf_op jit(solution)/shard_map/ppermute | solution.py:18
  39.5 2.4 %collective-permute-start.7 = (f32[1,7,32,128]{3,2,1,0:T(8,128)S(1)}, f32[1,7,32,128]{3,2,1,0:T(8,128)S(1)}, u32[]{:S(2)}, u32[]{:S(2)}) collective-permute-start(f32[1,7,32,128]{3,2,1,0:T(8,128)S(1)} %get-tuple-element.70), channel_id=1, source_target_pairs={{1,0},{2,1},{3,2},{4,3},{5,4},{6,5},{7,6},{8,7},{9,8},{10,9},{11,1... | collective-permute-start | bytes 344072 | tf_op jit(solution)/shard_map/ppermute | solution.py:19
  41.9 0.3 fusion.250
  42.2 1.6 %fusion.22 = f32[2048]{0:T(1024)S(1)} fusion(f32[256,128]{1,0:T(8,128)S(1)} %bitcast.126, s32[2048]{0:T(1024)S(1)} %bitcast.146, s32[2048]{0:T(1024)S(1)} %bitcast.138), kind=kOutput, calls=%fused_computation.17 | convolution fusion | flops 806615040 | bytes 155648 | tf_op jit(solution)/shard_map/srk,skz->srz/dot_general | solution.py:128
  43.8 2.7 %collective-permute-done.7 = f32[1,7,32,128]{3,2,1,0:T(8,128)S(1)} collective-permute-done((f32[1,7,32,128]{3,2,1,0:T(8,128)S(1)}, f32[1,7,32,128]{3,2,1,0:T(8,128)S(1)}, u32[]{:S(2)}, u32[]{:S(2)}) %collective-permute-start.7) | collective-permute-done | bytes 114720 | tf_op jit(solution)/shard_map/ppermute | solution.py:19
  46.5 0.1 fusion.156
  46.6 0.7 fusion.532
  47.4 1.6 %fusion.13 = f32[2048]{0:T(1024)S(1)} fusion(f32[256,128]{1,0:T(8,128)S(1)} %bitcast.127, s32[2048]{0:T(1024)S(1)} %bitcast.147, s32[2048]{0:T(1024)S(1)} %bitcast.139), kind=kOutput, calls=%fused_computation.14 | convolution fusion | flops 806615040 | bytes 155648 | tf_op jit(solution)/shard_map/srk,skz->srz/dot_general | solution.py:128
  49.1 1.2 %fusion.25 = f32[1,8,32,128]{3,2,1,0:T(8,128)S(1)} fusion(s32[8,32]{1,0:T(8,128)S(1)} %multiply_add_fusion, s32[2048]{0:T(1024)S(1)} %bitcast.148, f32[2048]{0:T(1024)S(1)} %bitcast.134, s32[2048]{0:T(1024)S(1)} %bitcast.140), kind=kOutput, calls=%fused_computation.18 | convolution fusion | flops 806354944 | bytes 156672 | tf_op jit(solution)/shard_map/srk,srz->skz/dot_general | solution.py:135
  50.3 0.6 fusion.533
  51.7 0.3 fusion.403
  52.0 3.0 %collective-permute-start.10 = (f32[1]{0:T(128)}, f32[1]{0:T(128)}, u32[]{:S(2)}, u32[]{:S(2)}) collective-permute-start(f32[1]{0:T(128)} %bitcast.31), channel_id=1, source_target_pairs={{0,2},{1,3},{2,0},{3,1},{4,6},{5,7},{6,4},{7,5},{8,10},{9,11},{10,... | collective-permute-start | bytes 20 | tf_op jit(solution)/shard_map/ppermute | solution.py:36
  55.1 1.9 %collective-permute-start.8 = (f32[1,7,32,128]{3,2,1,0:T(8,128)S(1)}, f32[1,7,32,128]{3,2,1,0:T(8,128)S(1)}, u32[]{:S(2)}, u32[]{:S(2)}) collective-permute-start(f32[1,7,32,128]{3,2,1,0:T(8,128)S(1)} %get-tuple-element.67), channel_id=1, source_target_pairs={{0,1},{1,2},{2,3},{3,4},{4,5},{5,6},{6,7},{7,8},{8,9},{9,10},{10,1... | collective-permute-start | bytes 344072 | tf_op jit(solution)/shard_map/ppermute | solution.py:18
  57.0 2.6 %collective-permute-start.9 = (f32[1,7,32,128]{3,2,1,0:T(8,128)S(1)}, f32[1,7,32,128]{3,2,1,0:T(8,128)S(1)}, u32[]{:S(2)}, u32[]{:S(2)}) collective-permute-start(f32[1,7,32,128]{3,2,1,0:T(8,128)S(1)} %get-tuple-element.68), channel_id=1, source_target_pairs={{1,0},{2,1},{3,2},{4,3},{5,4},{6,5},{7,6},{8,7},{9,8},{10,9},{11,1... | collective-permute-start | bytes 344072 | tf_op jit(solution)/shard_map/ppermute | solution.py:19
  59.6 0.3 fusion.274
  59.9 1.2 %fusion.28 = f32[1,8,32,128]{3,2,1,0:T(8,128)S(1)} fusion(s32[8,32]{1,0:T(8,128)S(1)} %multiply_add_fusion, s32[2048]{0:T(1024)S(1)} %bitcast.149, f32[2048]{0:T(1024)S(1)} %bitcast.133, s32[2048]{0:T(1024)S(1)} %bitcast.141), kind=kOutput, calls=%fused_computation.19 | convolution fusion | flops 806354944 | bytes 156672 | tf_op jit(solution)/shard_map/srk,srz->skz/dot_general | solution.py:135
  61.7 1.4 %collective-permute-done.9 = f32[1,7,32,128]{3,2,1,0:T(8,128)S(1)} collective-permute-done((f32[1,7,32,128]{3,2,1,0:T(8,128)S(1)}, f32[1,7,32,128]{3,2,1,0:T(8,128)S(1)}, u32[]{:S(2)}, u32[]{:S(2)}) %collective-permute-start.9) | collective-permute-done | bytes 114720 | tf_op jit(solution)/shard_map/ppermute | solution.py:19
  63.1 0.1 fusion.149
  63.4 0.3 fusion.426
  63.7 2.1 %collective-permute-start.13 = (f32[1]{0:T(128)}, f32[1]{0:T(128)}, u32[]{:S(2)}, u32[]{:S(2)}) collective-permute-start(f32[1]{0:T(128)} %add.718), channel_id=1, source_target_pairs={{0,4},{1,5},{2,6},{3,7},{4,0},{5,1},{6,2},{7,3},{8,12},{9,13},{10,... | collective-permute-start | bytes 20 | tf_op jit(solution)/shard_map/ppermute | solution.py:36
  65.8 2.6 %collective-permute-start.11 = (f32[1,7,32,128]{3,2,1,0:T(8,128)S(1)}, f32[1,7,32,128]{3,2,1,0:T(8,128)S(1)}, u32[]{:S(2)}, u32[]{:S(2)}) collective-permute-start(f32[1,7,32,128]{3,2,1,0:T(8,128)S(1)} %get-tuple-element.65), channel_id=1, source_target_pairs={{0,1},{1,2},{2,3},{3,4},{4,5},{5,6},{6,7},{7,8},{8,9},{9,10},{10,1... | collective-permute-start | bytes 344072 | tf_op jit(solution)/shard_map/ppermute | solution.py:18
  68.4 1.9 %collective-permute-start.12 = (f32[1,7,32,128]{3,2,1,0:T(8,128)S(1)}, f32[1,7,32,128]{3,2,1,0:T(8,128)S(1)}, u32[]{:S(2)}, u32[]{:S(2)}) collective-permute-start(f32[1,7,32,128]{3,2,1,0:T(8,128)S(1)} %get-tuple-element.66), channel_id=1, source_target_pairs={{1,0},{2,1},{3,2},{4,3},{5,4},{6,5},{7,6},{8,7},{9,8},{10,9},{11,1... | collective-permute-start | bytes 344072 | tf_op jit(solution)/shard_map/ppermute | solution.py:19
  70.4 0.3 fusion.298
  70.7 1.2 %fusion.31 = f32[1,8,32,128]{3,2,1,0:T(8,128)S(1)} fusion(s32[8,32]{1,0:T(8,128)S(1)} %multiply_add_fusion, s32[2048]{0:T(1024)S(1)} %bitcast.150, f32[2048]{0:T(1024)S(1)} %bitcast.131, s32[2048]{0:T(1024)S(1)} %bitcast.142), kind=kOutput, calls=%fused_computation.20 | convolution fusion | flops 806354944 | bytes 156672 | tf_op jit(solution)/shard_map/srk,srz->skz/dot_general | solution.py:135
  72.5 2.1 %collective-permute-done.12 = f32[1,7,32,128]{3,2,1,0:T(8,128)S(1)} collective-permute-done((f32[1,7,32,128]{3,2,1,0:T(8,128)S(1)}, f32[1,7,32,128]{3,2,1,0:T(8,128)S(1)}, u32[]{:S(2)}, u32[]{:S(2)}) %collective-permute-start.12) | collective-permute-done | bytes 114720 | tf_op jit(solution)/shard_map/ppermute | solution.py:19
  74.6 0.1 fusion.142
  74.8 0.3 fusion.449
  75.1 2.8 %collective-permute-start.16 = (f32[1]{0:T(128)}, f32[1]{0:T(128)}, u32[]{:S(2)}, u32[]{:S(2)}) collective-permute-start(f32[1]{0:T(128)} %add.742), channel_id=1, source_target_pairs={{0,8},{1,9},{2,10},{3,11},{4,12},{5,13},{6,14},{7,15},{8,0},{9,1},... | collective-permute-start | bytes 20 | tf_op jit(solution)/shard_map/ppermute | solution.py:36
  78.0 2.6 %collective-permute-start.14 = (f32[1,7,32,128]{3,2,1,0:T(8,128)S(1)}, f32[1,7,32,128]{3,2,1,0:T(8,128)S(1)}, u32[]{:S(2)}, u32[]{:S(2)}) collective-permute-start(f32[1,7,32,128]{3,2,1,0:T(8,128)S(1)} %get-tuple-element.63), channel_id=1, source_target_pairs={{0,1},{1,2},{2,3},{3,4},{4,5},{5,6},{6,7},{7,8},{8,9},{9,10},{10,1... | collective-permute-start | bytes 344072 | tf_op jit(solution)/shard_map/ppermute | solution.py:18
  80.6 1.9 %collective-permute-start.15 = (f32[1,7,32,128]{3,2,1,0:T(8,128)S(1)}, f32[1,7,32,128]{3,2,1,0:T(8,128)S(1)}, u32[]{:S(2)}, u32[]{:S(2)}) collective-permute-start(f32[1,7,32,128]{3,2,1,0:T(8,128)S(1)} %get-tuple-element.64), channel_id=1, source_target_pairs={{1,0},{2,1},{3,2},{4,3},{5,4},{6,5},{7,6},{8,7},{9,8},{10,9},{11,1... | collective-permute-start | bytes 344072 | tf_op jit(solution)/shard_map/ppermute | solution.py:19
  82.5 0.3 fusion.322
  82.9 1.2 %fusion.34 = f32[1,8,32,128]{3,2,1,0:T(8,128)S(1)} fusion(s32[8,32]{1,0:T(8,128)S(1)} %multiply_add_fusion, s32[2048]{0:T(1024)S(1)} %bitcast.151, f32[2048]{0:T(1024)S(1)} %bitcast.129, s32[2048]{0:T(1024)S(1)} %bitcast.143), kind=kOutput, calls=%fused_computation.21 | convolution fusion | flops 806354944 | bytes 156672 | tf_op jit(solution)/shard_map/srk,srz->skz/dot_general | solution.py:135
  84.7 1.0 %collective-permute-start.17 = (f32[1]{0:T(128)}, f32[1]{0:T(128)}, u32[]{:S(2)}, u32[]{:S(2)}) collective-permute-start(f32[1]{0:T(128)} %add.766), channel_id=1, source_target_pairs={{0,1},{1,0},{2,3},{3,2},{4,5},{5,4},{6,7},{7,6},{8,9},{9,8},{10,11... | collective-permute-start | bytes 20 | tf_op jit(solution)/shard_map/ppermute | solution.py:36
  85.7 0.3 collective-permute-done.17
  86.6 0.2 collective-permute-done.15
  86.8 0.1 fusion.135
  86.9 0.9 bitcast_multiply_fusion
  (57 shorter events, 0.9 us)
Async XLA Ops:
  0.6 7.7 %copy-start = (f32[8,32,128]{2,1,0:T(8,128)S(1)}, f32[8,32,128]{2,1,0:T(8,128)}, u32[]{:S(2)}) copy-start(f32[8,32,128]{2,1,0:T(8,128)} %param.11) | copy-start | bytes 393220
  0.6 7.7 %copy-start.1 = (f32[1,8,32,128]{3,2,1,0:T(8,128)S(1)}, f32[1,8,32,128]{3,2,1,0:T(8,128)}, u32[]{:S(2)}) copy-start(f32[1,8,32,128]{3,2,1,0:T(8,128)} %param.13) | copy-start | bytes 393220
  0.7 8.7 %copy-start.9 = (f32[1,4]{1,0:T(1,128)S(1)}, f32[1,4]{1,0:T(1,128)}, u32[]{:S(2)}) copy-start(f32[1,4]{1,0:T(1,128)} %param.17) | copy-start | bytes 52
  0.7 9.3 %copy-start.7 = (s32[1,2048]{1,0:T(1,128)S(1)}, s32[1,2048]{1,0:T(1,128)}, u32[]{:S(2)}) copy-start(s32[1,2048]{1,0:T(1,128)} %param.18) | copy-start | bytes 24580
  0.7 9.4 %copy-start.4 = (f32[8,32,128]{2,1,0:T(8,128)S(1)}, f32[8,32,128]{2,1,0:T(8,128)}, u32[]{:S(2)}) copy-start(f32[8,32,128]{2,1,0:T(8,128)} %param.10) | copy-start | bytes 393220
  1.9 8.2 %collective-permute-start = (f32[2,7,32,128]{3,2,1,0:T(8,128)S(1)}, f32[2,7,32,128]{3,2,1,0:T(8,128)S(1)}, u32[]{:S(2)}, u32[]{:S(2)}) collective-permute-start(f32[2,7,32,128]{3,2,1,0:T(8,128)S(1)} %get-tuple-element.60), channel_id=1, source_target_pairs={{0,1},{1,2},{2,3},{3,4},{4,5},{5,6},{6,7},{7,8},{8,9},{9,10},{10,1... | collective-permute-start | bytes 688136 | tf_op jit(solution)/shard_map/ppermute | solution.py:18
  6.4 7.3 %collective-permute-start.1 = (f32[2,7,32,128]{3,2,1,0:T(8,128)S(1)}, f32[2,7,32,128]{3,2,1,0:T(8,128)S(1)}, u32[]{:S(2)}, u32[]{:S(2)}) collective-permute-start(f32[2,7,32,128]{3,2,1,0:T(8,128)S(1)} %get-tuple-element.59), channel_id=1, source_target_pairs={{1,0},{2,1},{3,2},{4,3},{5,4},{6,5},{7,6},{8,7},{9,8},{10,9},{11,1... | collective-permute-start | bytes 688136 | tf_op jit(solution)/shard_map/ppermute | solution.py:19
  13.8 0.9 %copy-start.5 = (f32[1,8,32,128]{3,2,1,0:T(8,128)S(1)}, f32[1,8,32,128]{3,2,1,0:T(8,128)}, u32[]{:S(2)}) copy-start(f32[1,8,32,128]{3,2,1,0:T(8,128)} %param.12) | copy-start | bytes 393220
  14.7 1.0 %copy-start.2 = (f32[1,8,32,128]{3,2,1,0:T(8,128)S(1)}, f32[1,8,32,128]{3,2,1,0:T(8,128)}, u32[]{:S(2)}) copy-start(f32[1,8,32,128]{3,2,1,0:T(8,128)} %param.14) | copy-start | bytes 393220
  15.8 7.1 %collective-permute-start.2 = (f32[2,7,32,128]{3,2,1,0:T(8,128)S(1)}, f32[2,7,32,128]{3,2,1,0:T(8,128)S(1)}, u32[]{:S(2)}, u32[]{:S(2)}) collective-permute-start(f32[2,7,32,128]{3,2,1,0:T(8,128)S(1)} %get-tuple-element.57), channel_id=1, source_target_pairs={{0,1},{1,2},{2,3},{3,4},{4,5},{5,6},{6,7},{7,8},{8,9},{9,10},{10,1... | collective-permute-start | bytes 688136 | tf_op jit(solution)/shard_map/ppermute | solution.py:18
  17.8 8.1 %collective-permute-start.3 = (f32[2,7,32,128]{3,2,1,0:T(8,128)S(1)}, f32[2,7,32,128]{3,2,1,0:T(8,128)S(1)}, u32[]{:S(2)}, u32[]{:S(2)}) collective-permute-start(f32[2,7,32,128]{3,2,1,0:T(8,128)S(1)} %get-tuple-element.58), channel_id=1, source_target_pairs={{1,0},{2,1},{3,2},{4,3},{5,4},{6,5},{7,6},{8,7},{9,8},{10,9},{11,1... | collective-permute-start | bytes 688136 | tf_op jit(solution)/shard_map/ppermute | solution.py:19
  27.4 6.3 %collective-permute-start.4 = (f32[1,7,32,128]{3,2,1,0:T(8,128)S(1)}, f32[1,7,32,128]{3,2,1,0:T(8,128)S(1)}, u32[]{:S(2)}, u32[]{:S(2)}) collective-permute-start(f32[1,7,32,128]{3,2,1,0:T(8,128)S(1)} %get-tuple-element.71), channel_id=1, source_target_pairs={{0,1},{1,2},{2,3},{3,4},{4,5},{5,6},{6,7},{7,8},{8,9},{9,10},{10,1... | collective-permute-start | bytes 344072 | tf_op jit(solution)/shard_map/ppermute | solution.py:18
  29.3 7.0 %collective-permute-start.5 = (f32[1,7,32,128]{3,2,1,0:T(8,128)S(1)}, f32[1,7,32,128]{3,2,1,0:T(8,128)S(1)}, u32[]{:S(2)}, u32[]{:S(2)}) collective-permute-start(f32[1,7,32,128]{3,2,1,0:T(8,128)S(1)} %get-tuple-element.72), channel_id=1, source_target_pairs={{1,0},{2,1},{3,2},{4,3},{5,4},{6,5},{7,6},{8,7},{9,8},{10,9},{11,1... | collective-permute-start | bytes 344072 | tf_op jit(solution)/shard_map/ppermute | solution.py:19
  37.5 6.3 %collective-permute-start.6 = (f32[1,7,32,128]{3,2,1,0:T(8,128)S(1)}, f32[1,7,32,128]{3,2,1,0:T(8,128)S(1)}, u32[]{:S(2)}, u32[]{:S(2)}) collective-permute-start(f32[1,7,32,128]{3,2,1,0:T(8,128)S(1)} %get-tuple-element.69), channel_id=1, source_target_pairs={{0,1},{1,2},{2,3},{3,4},{4,5},{5,6},{6,7},{7,8},{8,9},{9,10},{10,1... | collective-permute-start | bytes 344072 | tf_op jit(solution)/shard_map/ppermute | solution.py:18
  39.5 7.0 %collective-permute-start.7 = (f32[1,7,32,128]{3,2,1,0:T(8,128)S(1)}, f32[1,7,32,128]{3,2,1,0:T(8,128)S(1)}, u32[]{:S(2)}, u32[]{:S(2)}) collective-permute-start(f32[1,7,32,128]{3,2,1,0:T(8,128)S(1)} %get-tuple-element.70), channel_id=1, source_target_pairs={{1,0},{2,1},{3,2},{4,3},{5,4},{6,5},{7,6},{8,7},{9,8},{10,9},{11,1... | collective-permute-start | bytes 344072 | tf_op jit(solution)/shard_map/ppermute | solution.py:19
  47.4 1.6 %copy-start.8 = (f32[1,4,2048]{2,1,0:T(4,128)S(1)}, f32[1,4,2048]{2,1,0:T(4,128)}, u32[]{:S(2)}) copy-start(f32[1,4,2048]{2,1,0:T(4,128)} %param.19) | copy-start | bytes 98308
  49.1 2.5 %copy-start.6 = (f32[1,8,32,128]{3,2,1,0:T(8,128)S(1)}, f32[1,8,32,128]{3,2,1,0:T(8,128)}, u32[]{:S(2)}) copy-start(f32[1,8,32,128]{3,2,1,0:T(8,128)} %param.15) | copy-start | bytes 393220
  52.0 9.1 %collective-permute-start.10 = (f32[1]{0:T(128)}, f32[1]{0:T(128)}, u32[]{:S(2)}, u32[]{:S(2)}) collective-permute-start(f32[1]{0:T(128)} %bitcast.31), channel_id=1, source_target_pairs={{0,2},{1,3},{2,0},{3,1},{4,6},{5,7},{6,4},{7,5},{8,10},{9,11},{10,... | collective-permute-start | bytes 20 | tf_op jit(solution)/shard_map/ppermute | solution.py:36
  55.1 6.6 %collective-permute-start.8 = (f32[1,7,32,128]{3,2,1,0:T(8,128)S(1)}, f32[1,7,32,128]{3,2,1,0:T(8,128)S(1)}, u32[]{:S(2)}, u32[]{:S(2)}) collective-permute-start(f32[1,7,32,128]{3,2,1,0:T(8,128)S(1)} %get-tuple-element.67), channel_id=1, source_target_pairs={{0,1},{1,2},{2,3},{3,4},{4,5},{5,6},{6,7},{7,8},{8,9},{9,10},{10,1... | collective-permute-start | bytes 344072 | tf_op jit(solution)/shard_map/ppermute | solution.py:18
  57.0 6.1 %collective-permute-start.9 = (f32[1,7,32,128]{3,2,1,0:T(8,128)S(1)}, f32[1,7,32,128]{3,2,1,0:T(8,128)S(1)}, u32[]{:S(2)}, u32[]{:S(2)}) collective-permute-start(f32[1,7,32,128]{3,2,1,0:T(8,128)S(1)} %get-tuple-element.68), channel_id=1, source_target_pairs={{1,0},{2,1},{3,2},{4,3},{5,4},{6,5},{7,6},{8,7},{9,8},{10,9},{11,1... | collective-permute-start | bytes 344072 | tf_op jit(solution)/shard_map/ppermute | solution.py:19
  63.7 8.2 %collective-permute-start.13 = (f32[1]{0:T(128)}, f32[1]{0:T(128)}, u32[]{:S(2)}, u32[]{:S(2)}) collective-permute-start(f32[1]{0:T(128)} %add.718), channel_id=1, source_target_pairs={{0,4},{1,5},{2,6},{3,7},{4,0},{5,1},{6,2},{7,3},{8,12},{9,13},{10,... | collective-permute-start | bytes 20 | tf_op jit(solution)/shard_map/ppermute | solution.py:36
  65.8 6.7 %collective-permute-start.11 = (f32[1,7,32,128]{3,2,1,0:T(8,128)S(1)}, f32[1,7,32,128]{3,2,1,0:T(8,128)S(1)}, u32[]{:S(2)}, u32[]{:S(2)}) collective-permute-start(f32[1,7,32,128]{3,2,1,0:T(8,128)S(1)} %get-tuple-element.65), channel_id=1, source_target_pairs={{0,1},{1,2},{2,3},{3,4},{4,5},{5,6},{6,7},{7,8},{8,9},{9,10},{10,1... | collective-permute-start | bytes 344072 | tf_op jit(solution)/shard_map/ppermute | solution.py:18
  68.4 6.1 %collective-permute-start.12 = (f32[1,7,32,128]{3,2,1,0:T(8,128)S(1)}, f32[1,7,32,128]{3,2,1,0:T(8,128)S(1)}, u32[]{:S(2)}, u32[]{:S(2)}) collective-permute-start(f32[1,7,32,128]{3,2,1,0:T(8,128)S(1)} %get-tuple-element.66), channel_id=1, source_target_pairs={{1,0},{2,1},{3,2},{4,3},{5,4},{6,5},{7,6},{8,7},{9,8},{10,9},{11,1... | collective-permute-start | bytes 344072 | tf_op jit(solution)/shard_map/ppermute | solution.py:19
  74.8 12.1 %copy-start.3 = (f32[1,8,32,128]{3,2,1,0:T(8,128)}, f32[1,8,32,128]{3,2,1,0:T(8,128)S(1)}, u32[]{:S(2)}) copy-start(f32[1,8,32,128]{3,2,1,0:T(8,128)S(1)} %fusion.483) | copy-start | bytes 393220
  75.1 9.0 %collective-permute-start.16 = (f32[1]{0:T(128)}, f32[1]{0:T(128)}, u32[]{:S(2)}, u32[]{:S(2)}) collective-permute-start(f32[1]{0:T(128)} %add.742), channel_id=1, source_target_pairs={{0,8},{1,9},{2,10},{3,11},{4,12},{5,13},{6,14},{7,15},{8,0},{9,1},... | collective-permute-start | bytes 20 | tf_op jit(solution)/shard_map/ppermute | solution.py:36
  78.0 8.6 %collective-permute-start.14 = (f32[1,7,32,128]{3,2,1,0:T(8,128)S(1)}, f32[1,7,32,128]{3,2,1,0:T(8,128)S(1)}, u32[]{:S(2)}, u32[]{:S(2)}) collective-permute-start(f32[1,7,32,128]{3,2,1,0:T(8,128)S(1)} %get-tuple-element.63), channel_id=1, source_target_pairs={{0,1},{1,2},{2,3},{3,4},{4,5},{5,6},{6,7},{7,8},{8,9},{9,10},{10,1... | collective-permute-start | bytes 344072 | tf_op jit(solution)/shard_map/ppermute | solution.py:18
  80.6 6.1 %collective-permute-start.15 = (f32[1,7,32,128]{3,2,1,0:T(8,128)S(1)}, f32[1,7,32,128]{3,2,1,0:T(8,128)S(1)}, u32[]{:S(2)}, u32[]{:S(2)}) collective-permute-start(f32[1,7,32,128]{3,2,1,0:T(8,128)S(1)} %get-tuple-element.64), channel_id=1, source_target_pairs={{1,0},{2,1},{3,2},{4,3},{5,4},{6,5},{7,6},{8,7},{9,8},{10,9},{11,1... | collective-permute-start | bytes 344072 | tf_op jit(solution)/shard_map/ppermute | solution.py:19
  84.7 1.3 %collective-permute-start.17 = (f32[1]{0:T(128)}, f32[1]{0:T(128)}, u32[]{:S(2)}, u32[]{:S(2)}) collective-permute-start(f32[1]{0:T(128)} %add.766), channel_id=1, source_target_pairs={{0,1},{1,0},{2,3},{3,2},{4,5},{5,4},{6,7},{7,6},{8,9},{9,8},{10,11... | collective-permute-start | bytes 20 | tf_op jit(solution)/shard_map/ppermute | solution.py:36

commit v19 on v18

--- a/solution.py
+++ b/solution.py
@@ -98,7 +98,9 @@
 
     first = extended(jnp.concatenate([buoyancy[None], wave_now], axis=0), 1, HALO)
     flux_buoyancy = first[0, HALO - 4 : HALO + planes + 3]
-    first_lap = wide_operator(first[1 : 1 + shots], wave_now, flux_buoyancy)
+    first_cross, first_base = lax.optimization_barrier((cross_terms(wave_now, buoyancy), 2.0 * wave_now - wave_prev))
+    first_flux = flux_buoyancy * forward_diff(first[1 : 1 + shots], 1, planes + 7, start=HALO - 4)
+    first_lap = backward_diff(first_flux, 1, planes) + first_cross
     adjoint_operand = kappa * adjoint_next
 
     def operator(values, later=None):
@@ -147,7 +149,7 @@
         else:
             lap = operator(current)
         laps.append(lap)
-        following = 2.0 * current - before + kappa * lap
+        following = (first_base if step == 0 else 2.0 * current - before) + kappa * lap
         amount = wavelet[:, step].reshape(shots, 1, 1, 1)
         following = following + jnp.where(source_hit, amount, 0.0)
         sampled = sample(following)

time: 90.4 us -> 89.6 us (level)
    add x6 -> x7, other arithmetic: 2.08 us -> 2.39 us  [cross_terms(): total = total + backward_diff(pad_axis(flux, axis), axis, length)]
where the time goes in v19:
time: 89.6 us; the launch traced here: 88.1 us
  starting transfers between devices  42.2 us (47%)
  waiting for transfers between devices  15.5 us (17%)
  other arithmetic  12.1 us (14%)
  matrix products  11.4 us (13%)
  between operations  6.02 us (7%)
    ppermute x7, starting transfers between devices, extended(): before = lax.ppermute(last, 'mp', up)  17.6 us
    ppermute x7, starting transfers between devices, extended(): after = lax.ppermute(first, 'mp', down)  15.6 us
    ppermute x7, waiting for transfers between devices, extended(): after = lax.ppermute(first, 'mp', down)  15.2 us
    ppermute x4, starting transfers between devices, butterfly_round(): return values + lax.ppermute(values, axis, pairs)  8.96 us
    dot_general x4, matrix products, sample(): jnp.einsum('srk,skz->srz', row_pick, field.reshape(shots, rows, cz), prec...  6.43 us
    dot_general x4, matrix products, injected(): jnp.einsum('srk,srz->skz', row_pick, spread, precision=lax.Precision.HIGH...  4.93 us
    add x4, other arithmetic, local(): following = following + jnp.where(source_hit, amount, 0.0)  3.03 us
    mul x7, other arithmetic, cross_terms(): flux = buoyancy * forward_diff(pad_axis(values, axis), axis, length)  2.4 us
  transfers between devices with their start and end apart: 18, of which 8 were waited for; matrix products, arithmetic and copies ran while one was open for 14% of the time, Pallas kernels for 0%

profile of v19, /device:TPU:1, one launch (start us, length us, event | category | flops | bytes accessed | tf_op | source)
XLA Modules:
  0.0 88.1 jit_solution(12329464753027955406)
XLA Ops:
  0.7 1.1 %pad_maximum_fusion.12 = (f32[2,7,32,128]{3,2,1,0:T(8,128)S(1)}, f32[2,7,32,128]{3,2,1,0:T(8,128)S(1)}) fusion(f32[1,8,32,128]{3,2,1,0:T(8,128)} %param.13, f32[1,8,32,128]{3,2,1,0:T(8,128)} %bitcast.121), kind=kLoop, calls=%fused_computation.331 | loop fusion | flops 114688 | bytes 720896 | tf_op jit(solution)/shard_map/concatenate | solution.py:99
  1.9 4.7 %collective-permute-start = (f32[2,7,32,128]{3,2,1,0:T(8,128)S(1)}, f32[2,7,32,128]{3,2,1,0:T(8,128)S(1)}, u32[]{:S(2)}, u32[]{:S(2)}) collective-permute-start(f32[2,7,32,128]{3,2,1,0:T(8,128)S(1)} %get-tuple-element.64), channel_id=1, source_target_pairs={{0,1},{1,2},{2,3},{3,4},{4,5},{5,6},{6,7},{7,8},{8,9},{9,10},{10,1... | collective-permute-start | bytes 688136 | tf_op jit(solution)/shard_map/ppermute | solution.py:18
  6.5 1.9 %collective-permute-start.1 = (f32[2,7,32,128]{3,2,1,0:T(8,128)S(1)}, f32[2,7,32,128]{3,2,1,0:T(8,128)S(1)}, u32[]{:S(2)}, u32[]{:S(2)}) collective-permute-start(f32[2,7,32,128]{3,2,1,0:T(8,128)S(1)} %get-tuple-element.63), channel_id=1, source_target_pairs={{1,0},{2,1},{3,2},{4,3},{5,4},{6,5},{7,6},{8,7},{9,8},{10,9},{11,1... | collective-permute-start | bytes 688136 | tf_op jit(solution)/shard_map/ppermute | solution.py:19
  8.5 0.3 fusion.333
  8.8 0.3 fusion.201
  9.8 0.6 fusion.552
  10.6 3.3 %collective-permute-done.1 = f32[2,7,32,128]{3,2,1,0:T(8,128)S(1)} collective-permute-done((f32[2,7,32,128]{3,2,1,0:T(8,128)S(1)}, f32[2,7,32,128]{3,2,1,0:T(8,128)S(1)}, u32[]{:S(2)}, u32[]{:S(2)}) %collective-permute-start.1) | collective-permute-done | bytes 229408 | tf_op jit(solution)/shard_map/ppermute | solution.py:19
  13.9 0.1 slice_bitcast_fusion
  14.1 0.8 fusion.526
  14.8 0.1 copy-done.2
  15.1 1.9 %collective-permute-start.2 = (f32[2,7,32,128]{3,2,1,0:T(8,128)S(1)}, f32[2,7,32,128]{3,2,1,0:T(8,128)S(1)}, u32[]{:S(2)}, u32[]{:S(2)}) collective-permute-start(f32[2,7,32,128]{3,2,1,0:T(8,128)S(1)} %get-tuple-element.61), channel_id=1, source_target_pairs={{0,1},{1,2},{2,3},{3,4},{4,5},{5,6},{6,7},{7,8},{8,9},{9,10},{10,1... | collective-permute-start | bytes 688136 | tf_op jit(solution)/shard_map/ppermute | solution.py:18
  17.0 2.4 %collective-permute-start.3 = (f32[2,7,32,128]{3,2,1,0:T(8,128)S(1)}, f32[2,7,32,128]{3,2,1,0:T(8,128)S(1)}, u32[]{:S(2)}, u32[]{:S(2)}) collective-permute-start(f32[2,7,32,128]{3,2,1,0:T(8,128)S(1)} %get-tuple-element.62), channel_id=1, source_target_pairs={{1,0},{2,1},{3,2},{4,3},{5,4},{6,5},{7,6},{8,7},{9,8},{10,9},{11,1... | collective-permute-start | bytes 688136 | tf_op jit(solution)/shard_map/ppermute | solution.py:19
  19.4 0.5 fusion.106
  20.0 0.5 fusion.94
  20.5 1.6 %fusion.16 = f32[2048]{0:T(1024)S(1)} fusion(f32[256,128]{1,0:T(8,128)S(1)} %bitcast.125, s32[2048]{0:T(1024)S(1)} %bitcast.144, s32[2048]{0:T(1024)S(1)} %bitcast.136), kind=kOutput, calls=%fused_computation.15 | convolution fusion | flops 806615040 | bytes 155648 | tf_op jit(solution)/shard_map/srk,skz->srz/dot_general | solution.py:130
  22.1 3.0 %collective-permute-done.3 = f32[2,7,32,128]{3,2,1,0:T(8,128)S(1)} collective-permute-done((f32[2,7,32,128]{3,2,1,0:T(8,128)S(1)}, f32[2,7,32,128]{3,2,1,0:T(8,128)S(1)}, u32[]{:S(2)}, u32[]{:S(2)}) %collective-permute-start.3) | collective-permute-done | bytes 229408 | tf_op jit(solution)/shard_map/ppermute | solution.py:19
  25.2 0.2 fusion.72
  25.4 0.1 fusion.126
  25.5 0.7 fusion.528
  26.3 0.3 fusion.356
  26.6 1.9 %collective-permute-start.4 = (f32[1,7,32,128]{3,2,1,0:T(8,128)S(1)}, f32[1,7,32,128]{3,2,1,0:T(8,128)S(1)}, u32[]{:S(2)}, u32[]{:S(2)}) collective-permute-start(f32[1,7,32,128]{3,2,1,0:T(8,128)S(1)} %get-tuple-element.75), channel_id=1, source_target_pairs={{0,1},{1,2},{2,3},{3,4},{4,5},{5,6},{6,7},{7,8},{8,9},{9,10},{10,1... | collective-permute-start | bytes 344072 | tf_op jit(solution)/shard_map/ppermute | solution.py:18
  28.5 2.4 %collective-permute-start.5 = (f32[1,7,32,128]{3,2,1,0:T(8,128)S(1)}, f32[1,7,32,128]{3,2,1,0:T(8,128)S(1)}, u32[]{:S(2)}, u32[]{:S(2)}) collective-permute-start(f32[1,7,32,128]{3,2,1,0:T(8,128)S(1)} %get-tuple-element.76), channel_id=1, source_target_pairs={{1,0},{2,1},{3,2},{4,3},{5,4},{6,5},{7,6},{8,7},{9,8},{10,9},{11,1... | collective-permute-start | bytes 344072 | tf_op jit(solution)/shard_map/ppermute | solution.py:19
  30.9 0.3 fusion.225
  31.3 1.6 %fusion.19 = f32[2048]{0:T(1024)S(1)} fusion(f32[256,128]{1,0:T(8,128)S(1)} %bitcast.124, s32[2048]{0:T(1024)S(1)} %bitcast.145, s32[2048]{0:T(1024)S(1)} %bitcast.137), kind=kOutput, calls=%fused_computation.16 | convolution fusion | flops 806615040 | bytes 155648 | tf_op jit(solution)/shard_map/srk,skz->srz/dot_general | solution.py:130
  32.9 2.7 %collective-permute-done.5 = f32[1,7,32,128]{3,2,1,0:T(8,128)S(1)} collective-permute-done((f32[1,7,32,128]{3,2,1,0:T(8,128)S(1)}, f32[1,7,32,128]{3,2,1,0:T(8,128)S(1)}, u32[]{:S(2)}, u32[]{:S(2)}) %collective-permute-start.5) | collective-permute-done | bytes 114720 | tf_op jit(solution)/shard_map/ppermute | solution.py:19
  35.6 0.1 fusion.163
  35.7 0.7 fusion.530
  36.5 0.3 fusion.379
  36.8 1.9 %collective-permute-start.6 = (f32[1,7,32,128]{3,2,1,0:T(8,128)S(1)}, f32[1,7,32,128]{3,2,1,0:T(8,128)S(1)}, u32[]{:S(2)}, u32[]{:S(2)}) collective-permute-start(f32[1,7,32,128]{3,2,1,0:T(8,128)S(1)} %get-tuple-element.73), channel_id=1, source_target_pairs={{0,1},{1,2},{2,3},{3,4},{4,5},{5,6},{6,7},{7,8},{8,9},{9,10},{10,1... | collective-permute-start | bytes 344072 | tf_op jit(solution)/shard_map/ppermute | solution.py:18
  38.7 2.4 %collective-permute-start.7 = (f32[1,7,32,128]{3,2,1,0:T(8,128)S(1)}, f32[1,7,32,128]{3,2,1,0:T(8,128)S(1)}, u32[]{:S(2)}, u32[]{:S(2)}) collective-permute-start(f32[1,7,32,128]{3,2,1,0:T(8,128)S(1)} %get-tuple-element.74), channel_id=1, source_target_pairs={{1,0},{2,1},{3,2},{4,3},{5,4},{6,5},{7,6},{8,7},{9,8},{10,9},{11,1... | collective-permute-start | bytes 344072 | tf_op jit(solution)/shard_map/ppermute | solution.py:19
  41.1 0.3 fusion.249
  41.4 1.6 %fusion.22 = f32[2048]{0:T(1024)S(1)} fusion(f32[256,128]{1,0:T(8,128)S(1)} %bitcast.126, s32[2048]{0:T(1024)S(1)} %bitcast.146, s32[2048]{0:T(1024)S(1)} %bitcast.138), kind=kOutput, calls=%fused_computation.17 | convolution fusion | flops 806615040 | bytes 155648 | tf_op jit(solution)/shard_map/srk,skz->srz/dot_general | solution.py:130
  43.0 2.7 %collective-permute-done.7 = f32[1,7,32,128]{3,2,1,0:T(8,128)S(1)} collective-permute-done((f32[1,7,32,128]{3,2,1,0:T(8,128)S(1)}, f32[1,7,32,128]{3,2,1,0:T(8,128)S(1)}, u32[]{:S(2)}, u32[]{:S(2)}) %collective-permute-start.7) | collective-permute-done | bytes 114720 | tf_op jit(solution)/shard_map/ppermute | solution.py:19
  45.7 0.1 fusion.156
  45.8 0.7 fusion.532
  46.6 1.6 %fusion.13 = f32[2048]{0:T(1024)S(1)} fusion(f32[256,128]{1,0:T(8,128)S(1)} %bitcast.127, s32[2048]{0:T(1024)S(1)} %bitcast.147, s32[2048]{0:T(1024)S(1)} %bitcast.139), kind=kOutput, calls=%fused_computation.14 | convolution fusion | flops 806615040 | bytes 155648 | tf_op jit(solution)/shard_map/srk,skz->srz/dot_general | solution.py:130
  48.3 1.2 %fusion.25 = f32[1,8,32,128]{3,2,1,0:T(8,128)S(1)} fusion(s32[8,32]{1,0:T(8,128)S(1)} %multiply_add_fusion, s32[2048]{0:T(1024)S(1)} %bitcast.148, f32[2048]{0:T(1024)S(1)} %bitcast.134, s32[2048]{0:T(1024)S(1)} %bitcast.140), kind=kOutput, calls=%fused_computation.18 | convolution fusion | flops 806354944 | bytes 156672 | tf_op jit(solution)/shard_map/srk,srz->skz/dot_general | solution.py:137
  49.5 0.6 fusion.533
  50.9 0.3 fusion.402
  51.3 3.0 %collective-permute-start.10 = (f32[1]{0:T(128)}, f32[1]{0:T(128)}, u32[]{:S(2)}, u32[]{:S(2)}) collective-permute-start(f32[1]{0:T(128)} %bitcast.31), channel_id=1, source_target_pairs={{0,2},{1,3},{2,0},{3,1},{4,6},{5,7},{6,4},{7,5},{8,10},{9,11},{10,... | collective-permute-start | bytes 20 | tf_op jit(solution)/shard_map/ppermute | solution.py:36
  54.3 1.9 %collective-permute-start.8 = (f32[1,7,32,128]{3,2,1,0:T(8,128)S(1)}, f32[1,7,32,128]{3,2,1,0:T(8,128)S(1)}, u32[]{:S(2)}, u32[]{:S(2)}) collective-permute-start(f32[1,7,32,128]{3,2,1,0:T(8,128)S(1)} %get-tuple-element.71), channel_id=1, source_target_pairs={{0,1},{1,2},{2,3},{3,4},{4,5},{5,6},{6,7},{7,8},{8,9},{9,10},{10,1... | collective-permute-start | bytes 344072 | tf_op jit(solution)/shard_map/ppermute | solution.py:18
  56.2 2.6 %collective-permute-start.9 = (f32[1,7,32,128]{3,2,1,0:T(8,128)S(1)}, f32[1,7,32,128]{3,2,1,0:T(8,128)S(1)}, u32[]{:S(2)}, u32[]{:S(2)}) collective-permute-start(f32[1,7,32,128]{3,2,1,0:T(8,128)S(1)} %get-tuple-element.72), channel_id=1, source_target_pairs={{1,0},{2,1},{3,2},{4,3},{5,4},{6,5},{7,6},{8,7},{9,8},{10,9},{11,1... | collective-permute-start | bytes 344072 | tf_op jit(solution)/shard_map/ppermute | solution.py:19
  58.8 0.3 fusion.273
  59.1 1.2 %fusion.28 = f32[1,8,32,128]{3,2,1,0:T(8,128)S(1)} fusion(s32[8,32]{1,0:T(8,128)S(1)} %multiply_add_fusion, s32[2048]{0:T(1024)S(1)} %bitcast.149, f32[2048]{0:T(1024)S(1)} %bitcast.133, s32[2048]{0:T(1024)S(1)} %bitcast.141), kind=kOutput, calls=%fused_computation.19 | convolution fusion | flops 806354944 | bytes 156672 | tf_op jit(solution)/shard_map/srk,srz->skz/dot_general | solution.py:137
  60.9 1.4 %collective-permute-done.9 = f32[1,7,32,128]{3,2,1,0:T(8,128)S(1)} collective-permute-done((f32[1,7,32,128]{3,2,1,0:T(8,128)S(1)}, f32[1,7,32,128]{3,2,1,0:T(8,128)S(1)}, u32[]{:S(2)}, u32[]{:S(2)}) %collective-permute-start.9) | collective-permute-done | bytes 114720 | tf_op jit(solution)/shard_map/ppermute | solution.py:19
  62.4 0.1 fusion.149
  62.6 0.3 fusion.425
  62.9 2.1 %collective-permute-start.13 = (f32[1]{0:T(128)}, f32[1]{0:T(128)}, u32[]{:S(2)}, u32[]{:S(2)}) collective-permute-start(f32[1]{0:T(128)} %add.718), channel_id=1, source_target_pairs={{0,4},{1,5},{2,6},{3,7},{4,0},{5,1},{6,2},{7,3},{8,12},{9,13},{10,... | collective-permute-start | bytes 20 | tf_op jit(solution)/shard_map/ppermute | solution.py:36
  65.0 2.6 %collective-permute-start.11 = (f32[1,7,32,128]{3,2,1,0:T(8,128)S(1)}, f32[1,7,32,128]{3,2,1,0:T(8,128)S(1)}, u32[]{:S(2)}, u32[]{:S(2)}) collective-permute-start(f32[1,7,32,128]{3,2,1,0:T(8,128)S(1)} %get-tuple-element.69), channel_id=1, source_target_pairs={{0,1},{1,2},{2,3},{3,4},{4,5},{5,6},{6,7},{7,8},{8,9},{9,10},{10,1... | collective-permute-start | bytes 344072 | tf_op jit(solution)/shard_map/ppermute | solution.py:18
  67.7 1.9 %collective-permute-start.12 = (f32[1,7,32,128]{3,2,1,0:T(8,128)S(1)}, f32[1,7,32,128]{3,2,1,0:T(8,128)S(1)}, u32[]{:S(2)}, u32[]{:S(2)}) collective-permute-start(f32[1,7,32,128]{3,2,1,0:T(8,128)S(1)} %get-tuple-element.70), channel_id=1, source_target_pairs={{1,0},{2,1},{3,2},{4,3},{5,4},{6,5},{7,6},{8,7},{9,8},{10,9},{11,1... | collective-permute-start | bytes 344072 | tf_op jit(solution)/shard_map/ppermute | solution.py:19
  69.6 0.3 fusion.297
  69.9 1.2 %fusion.31 = f32[1,8,32,128]{3,2,1,0:T(8,128)S(1)} fusion(s32[8,32]{1,0:T(8,128)S(1)} %multiply_add_fusion, s32[2048]{0:T(1024)S(1)} %bitcast.150, f32[2048]{0:T(1024)S(1)} %bitcast.131, s32[2048]{0:T(1024)S(1)} %bitcast.142), kind=kOutput, calls=%fused_computation.20 | convolution fusion | flops 806354944 | bytes 156672 | tf_op jit(solution)/shard_map/srk,srz->skz/dot_general | solution.py:137
  71.7 2.1 %collective-permute-done.12 = f32[1,7,32,128]{3,2,1,0:T(8,128)S(1)} collective-permute-done((f32[1,7,32,128]{3,2,1,0:T(8,128)S(1)}, f32[1,7,32,128]{3,2,1,0:T(8,128)S(1)}, u32[]{:S(2)}, u32[]{:S(2)}) %collective-permute-start.12) | collective-permute-done | bytes 114720 | tf_op jit(solution)/shard_map/ppermute | solution.py:19
  74.1 0.3 fusion.448
  74.4 2.8 %collective-permute-start.16 = (f32[1]{0:T(128)}, f32[1]{0:T(128)}, u32[]{:S(2)}, u32[]{:S(2)}) collective-permute-start(f32[1]{0:T(128)} %add.742), channel_id=1, source_target_pairs={{0,8},{1,9},{2,10},{3,11},{4,12},{5,13},{6,14},{7,15},{8,0},{9,1},... | collective-permute-start | bytes 20 | tf_op jit(solution)/shard_map/ppermute | solution.py:36
  77.2 2.6 %collective-permute-start.14 = (f32[1,7,32,128]{3,2,1,0:T(8,128)S(1)}, f32[1,7,32,128]{3,2,1,0:T(8,128)S(1)}, u32[]{:S(2)}, u32[]{:S(2)}) collective-permute-start(f32[1,7,32,128]{3,2,1,0:T(8,128)S(1)} %get-tuple-element.67), channel_id=1, source_target_pairs={{0,1},{1,2},{2,3},{3,4},{4,5},{5,6},{6,7},{7,8},{8,9},{9,10},{10,1... | collective-permute-start | bytes 344072 | tf_op jit(solution)/shard_map/ppermute | solution.py:18
  79.8 1.9 %collective-permute-start.15 = (f32[1,7,32,128]{3,2,1,0:T(8,128)S(1)}, f32[1,7,32,128]{3,2,1,0:T(8,128)S(1)}, u32[]{:S(2)}, u32[]{:S(2)}) collective-permute-start(f32[1,7,32,128]{3,2,1,0:T(8,128)S(1)} %get-tuple-element.68), channel_id=1, source_target_pairs={{1,0},{2,1},{3,2},{4,3},{5,4},{6,5},{7,6},{8,7},{9,8},{10,9},{11,1... | collective-permute-start | bytes 344072 | tf_op jit(solution)/shard_map/ppermute | solution.py:19
  81.8 0.3 fusion.321
  82.1 1.2 %fusion.34 = f32[1,8,32,128]{3,2,1,0:T(8,128)S(1)} fusion(s32[8,32]{1,0:T(8,128)S(1)} %multiply_add_fusion, s32[2048]{0:T(1024)S(1)} %bitcast.151, f32[2048]{0:T(1024)S(1)} %bitcast.129, s32[2048]{0:T(1024)S(1)} %bitcast.143), kind=kOutput, calls=%fused_computation.21 | convolution fusion | flops 806354944 | bytes 156672 | tf_op jit(solution)/shard_map/srk,srz->skz/dot_general | solution.py:137
  83.9 1.0 %collective-permute-start.17 = (f32[1]{0:T(128)}, f32[1]{0:T(128)}, u32[]{:S(2)}, u32[]{:S(2)}) collective-permute-start(f32[1]{0:T(128)} %add.766), channel_id=1, source_target_pairs={{0,1},{1,0},{2,3},{3,2},{4,5},{5,4},{6,7},{7,6},{8,9},{9,8},{10,11... | collective-permute-start | bytes 20 | tf_op jit(solution)/shard_map/ppermute | solution.py:36
  84.9 0.3 collective-permute-done.17
  85.8 0.2 collective-permute-done.15
  86.0 0.1 fusion.135
  86.1 0.9 bitcast_multiply_fusion
  (58 shorter events, 1.0 us)
Async XLA Ops:
  0.6 7.9 %copy-start = (f32[8,32,128]{2,1,0:T(8,128)S(1)}, f32[8,32,128]{2,1,0:T(8,128)}, u32[]{:S(2)}) copy-start(f32[8,32,128]{2,1,0:T(8,128)} %param.11) | copy-start | bytes 393220
  0.6 7.9 %copy-start.1 = (f32[1,8,32,128]{3,2,1,0:T(8,128)S(1)}, f32[1,8,32,128]{3,2,1,0:T(8,128)}, u32[]{:S(2)}) copy-start(f32[1,8,32,128]{3,2,1,0:T(8,128)} %param.13) | copy-start | bytes 393220
  0.7 7.9 %copy-start.6 = (f32[1,8,32,128]{3,2,1,0:T(8,128)S(1)}, f32[1,8,32,128]{3,2,1,0:T(8,128)}, u32[]{:S(2)}) copy-start(f32[1,8,32,128]{3,2,1,0:T(8,128)} %param.12) | copy-start | bytes 393220
  1.8 8.0 %copy-start.9 = (f32[1,4]{1,0:T(1,128)S(1)}, f32[1,4]{1,0:T(1,128)}, u32[]{:S(2)}) copy-start(f32[1,4]{1,0:T(1,128)} %param.17) | copy-start | bytes 52
  1.8 8.6 %copy-start.7 = (s32[1,2048]{1,0:T(1,128)S(1)}, s32[1,2048]{1,0:T(1,128)}, u32[]{:S(2)}) copy-start(s32[1,2048]{1,0:T(1,128)} %param.18) | copy-start | bytes 24580
  1.8 8.7 %copy-start.4 = (f32[8,32,128]{2,1,0:T(8,128)S(1)}, f32[8,32,128]{2,1,0:T(8,128)}, u32[]{:S(2)}) copy-start(f32[8,32,128]{2,1,0:T(8,128)} %param.10) | copy-start | bytes 393220
  1.9 8.7 %collective-permute-start = (f32[2,7,32,128]{3,2,1,0:T(8,128)S(1)}, f32[2,7,32,128]{3,2,1,0:T(8,128)S(1)}, u32[]{:S(2)}, u32[]{:S(2)}) collective-permute-start(f32[2,7,32,128]{3,2,1,0:T(8,128)S(1)} %get-tuple-element.64), channel_id=1, source_target_pairs={{0,1},{1,2},{2,3},{3,4},{4,5},{5,6},{6,7},{7,8},{8,9},{9,10},{10,1... | collective-permute-start | bytes 688136 | tf_op jit(solution)/shard_map/ppermute | solution.py:18
  6.5 7.3 %collective-permute-start.1 = (f32[2,7,32,128]{3,2,1,0:T(8,128)S(1)}, f32[2,7,32,128]{3,2,1,0:T(8,128)S(1)}, u32[]{:S(2)}, u32[]{:S(2)}) collective-permute-start(f32[2,7,32,128]{3,2,1,0:T(8,128)S(1)} %get-tuple-element.63), channel_id=1, source_target_pairs={{1,0},{2,1},{3,2},{4,3},{5,4},{6,5},{7,6},{8,7},{9,8},{10,9},{11,1... | collective-permute-start | bytes 688136 | tf_op jit(solution)/shard_map/ppermute | solution.py:19
  14.0 0.9 %copy-start.2 = (f32[1,8,32,128]{3,2,1,0:T(8,128)S(1)}, f32[1,8,32,128]{3,2,1,0:T(8,128)}, u32[]{:S(2)}) copy-start(f32[1,8,32,128]{3,2,1,0:T(8,128)} %param.14) | copy-start | bytes 393220
  15.1 7.1 %collective-permute-start.2 = (f32[2,7,32,128]{3,2,1,0:T(8,128)S(1)}, f32[2,7,32,128]{3,2,1,0:T(8,128)S(1)}, u32[]{:S(2)}, u32[]{:S(2)}) collective-permute-start(f32[2,7,32,128]{3,2,1,0:T(8,128)S(1)} %get-tuple-element.61), channel_id=1, source_target_pairs={{0,1},{1,2},{2,3},{3,4},{4,5},{5,6},{6,7},{7,8},{8,9},{9,10},{10,1... | collective-permute-start | bytes 688136 | tf_op jit(solution)/shard_map/ppermute | solution.py:18
  17.0 8.1 %collective-permute-start.3 = (f32[2,7,32,128]{3,2,1,0:T(8,128)S(1)}, f32[2,7,32,128]{3,2,1,0:T(8,128)S(1)}, u32[]{:S(2)}, u32[]{:S(2)}) collective-permute-start(f32[2,7,32,128]{3,2,1,0:T(8,128)S(1)} %get-tuple-element.62), channel_id=1, source_target_pairs={{1,0},{2,1},{3,2},{4,3},{5,4},{6,5},{7,6},{8,7},{9,8},{10,9},{11,1... | collective-permute-start | bytes 688136 | tf_op jit(solution)/shard_map/ppermute | solution.py:19
  26.6 6.3 %collective-permute-start.4 = (f32[1,7,32,128]{3,2,1,0:T(8,128)S(1)}, f32[1,7,32,128]{3,2,1,0:T(8,128)S(1)}, u32[]{:S(2)}, u32[]{:S(2)}) collective-permute-start(f32[1,7,32,128]{3,2,1,0:T(8,128)S(1)} %get-tuple-element.75), channel_id=1, source_target_pairs={{0,1},{1,2},{2,3},{3,4},{4,5},{5,6},{6,7},{7,8},{8,9},{9,10},{10,1... | collective-permute-start | bytes 344072 | tf_op jit(solution)/shard_map/ppermute | solution.py:18
  28.5 7.0 %collective-permute-start.5 = (f32[1,7,32,128]{3,2,1,0:T(8,128)S(1)}, f32[1,7,32,128]{3,2,1,0:T(8,128)S(1)}, u32[]{:S(2)}, u32[]{:S(2)}) collective-permute-start(f32[1,7,32,128]{3,2,1,0:T(8,128)S(1)} %get-tuple-element.76), channel_id=1, source_target_pairs={{1,0},{2,1},{3,2},{4,3},{5,4},{6,5},{7,6},{8,7},{9,8},{10,9},{11,1... | collective-permute-start | bytes 344072 | tf_op jit(solution)/shard_map/ppermute | solution.py:19
  36.8 6.3 %collective-permute-start.6 = (f32[1,7,32,128]{3,2,1,0:T(8,128)S(1)}, f32[1,7,32,128]{3,2,1,0:T(8,128)S(1)}, u32[]{:S(2)}, u32[]{:S(2)}) collective-permute-start(f32[1,7,32,128]{3,2,1,0:T(8,128)S(1)} %get-tuple-element.73), channel_id=1, source_target_pairs={{0,1},{1,2},{2,3},{3,4},{4,5},{5,6},{6,7},{7,8},{8,9},{9,10},{10,1... | collective-permute-start | bytes 344072 | tf_op jit(solution)/shard_map/ppermute | solution.py:18
  38.7 7.0 %collective-permute-start.7 = (f32[1,7,32,128]{3,2,1,0:T(8,128)S(1)}, f32[1,7,32,128]{3,2,1,0:T(8,128)S(1)}, u32[]{:S(2)}, u32[]{:S(2)}) collective-permute-start(f32[1,7,32,128]{3,2,1,0:T(8,128)S(1)} %get-tuple-element.74), channel_id=1, source_target_pairs={{1,0},{2,1},{3,2},{4,3},{5,4},{6,5},{7,6},{8,7},{9,8},{10,9},{11,1... | collective-permute-start | bytes 344072 | tf_op jit(solution)/shard_map/ppermute | solution.py:19
  46.6 1.6 %copy-start.8 = (f32[1,4,2048]{2,1,0:T(4,128)S(1)}, f32[1,4,2048]{2,1,0:T(4,128)}, u32[]{:S(2)}) copy-start(f32[1,4,2048]{2,1,0:T(4,128)} %param.19) | copy-start | bytes 98308
  48.3 2.5 %copy-start.5 = (f32[1,8,32,128]{3,2,1,0:T(8,128)S(1)}, f32[1,8,32,128]{3,2,1,0:T(8,128)}, u32[]{:S(2)}) copy-start(f32[1,8,32,128]{3,2,1,0:T(8,128)} %param.15) | copy-start | bytes 393220
  51.3 9.1 %collective-permute-start.10 = (f32[1]{0:T(128)}, f32[1]{0:T(128)}, u32[]{:S(2)}, u32[]{:S(2)}) collective-permute-start(f32[1]{0:T(128)} %bitcast.31), channel_id=1, source_target_pairs={{0,2},{1,3},{2,0},{3,1},{4,6},{5,7},{6,4},{7,5},{8,10},{9,11},{10,... | collective-permute-start | bytes 20 | tf_op jit(solution)/shard_map/ppermute | solution.py:36
  54.3 6.6 %collective-permute-start.8 = (f32[1,7,32,128]{3,2,1,0:T(8,128)S(1)}, f32[1,7,32,128]{3,2,1,0:T(8,128)S(1)}, u32[]{:S(2)}, u32[]{:S(2)}) collective-permute-start(f32[1,7,32,128]{3,2,1,0:T(8,128)S(1)} %get-tuple-element.71), channel_id=1, source_target_pairs={{0,1},{1,2},{2,3},{3,4},{4,5},{5,6},{6,7},{7,8},{8,9},{9,10},{10,1... | collective-permute-start | bytes 344072 | tf_op jit(solution)/shard_map/ppermute | solution.py:18
  56.2 6.1 %collective-permute-start.9 = (f32[1,7,32,128]{3,2,1,0:T(8,128)S(1)}, f32[1,7,32,128]{3,2,1,0:T(8,128)S(1)}, u32[]{:S(2)}, u32[]{:S(2)}) collective-permute-start(f32[1,7,32,128]{3,2,1,0:T(8,128)S(1)} %get-tuple-element.72), channel_id=1, source_target_pairs={{1,0},{2,1},{3,2},{4,3},{5,4},{6,5},{7,6},{8,7},{9,8},{10,9},{11,1... | collective-permute-start | bytes 344072 | tf_op jit(solution)/shard_map/ppermute | solution.py:19
  62.9 8.2 %collective-permute-start.13 = (f32[1]{0:T(128)}, f32[1]{0:T(128)}, u32[]{:S(2)}, u32[]{:S(2)}) collective-permute-start(f32[1]{0:T(128)} %add.718), channel_id=1, source_target_pairs={{0,4},{1,5},{2,6},{3,7},{4,0},{5,1},{6,2},{7,3},{8,12},{9,13},{10,... | collective-permute-start | bytes 20 | tf_op jit(solution)/shard_map/ppermute | solution.py:36
  65.0 6.7 %collective-permute-start.11 = (f32[1,7,32,128]{3,2,1,0:T(8,128)S(1)}, f32[1,7,32,128]{3,2,1,0:T(8,128)S(1)}, u32[]{:S(2)}, u32[]{:S(2)}) collective-permute-start(f32[1,7,32,128]{3,2,1,0:T(8,128)S(1)} %get-tuple-element.69), channel_id=1, source_target_pairs={{0,1},{1,2},{2,3},{3,4},{4,5},{5,6},{6,7},{7,8},{8,9},{9,10},{10,1... | collective-permute-start | bytes 344072 | tf_op jit(solution)/shard_map/ppermute | solution.py:18
  67.7 6.1 %collective-permute-start.12 = (f32[1,7,32,128]{3,2,1,0:T(8,128)S(1)}, f32[1,7,32,128]{3,2,1,0:T(8,128)S(1)}, u32[]{:S(2)}, u32[]{:S(2)}) collective-permute-start(f32[1,7,32,128]{3,2,1,0:T(8,128)S(1)} %get-tuple-element.70), channel_id=1, source_target_pairs={{1,0},{2,1},{3,2},{4,3},{5,4},{6,5},{7,6},{8,7},{9,8},{10,9},{11,1... | collective-permute-start | bytes 344072 | tf_op jit(solution)/shard_map/ppermute | solution.py:19
  74.0 12.1 %copy-start.3 = (f32[1,8,32,128]{3,2,1,0:T(8,128)}, f32[1,8,32,128]{3,2,1,0:T(8,128)S(1)}, u32[]{:S(2)}) copy-start(f32[1,8,32,128]{3,2,1,0:T(8,128)S(1)} %fusion.482) | copy-start | bytes 393220
  74.4 9.0 %collective-permute-start.16 = (f32[1]{0:T(128)}, f32[1]{0:T(128)}, u32[]{:S(2)}, u32[]{:S(2)}) collective-permute-start(f32[1]{0:T(128)} %add.742), channel_id=1, source_target_pairs={{0,8},{1,9},{2,10},{3,11},{4,12},{5,13},{6,14},{7,15},{8,0},{9,1},... | collective-permute-start | bytes 20 | tf_op jit(solution)/shard_map/ppermute | solution.py:36
  77.2 8.6 %collective-permute-start.14 = (f32[1,7,32,128]{3,2,1,0:T(8,128)S(1)}, f32[1,7,32,128]{3,2,1,0:T(8,128)S(1)}, u32[]{:S(2)}, u32[]{:S(2)}) collective-permute-start(f32[1,7,32,128]{3,2,1,0:T(8,128)S(1)} %get-tuple-element.67), channel_id=1, source_target_pairs={{0,1},{1,2},{2,3},{3,4},{4,5},{5,6},{6,7},{7,8},{8,9},{9,10},{10,1... | collective-permute-start | bytes 344072 | tf_op jit(solution)/shard_map/ppermute | solution.py:18
  79.8 6.1 %collective-permute-start.15 = (f32[1,7,32,128]{3,2,1,0:T(8,128)S(1)}, f32[1,7,32,128]{3,2,1,0:T(8,128)S(1)}, u32[]{:S(2)}, u32[]{:S(2)}) collective-permute-start(f32[1,7,32,128]{3,2,1,0:T(8,128)S(1)} %get-tuple-element.68), channel_id=1, source_target_pairs={{1,0},{2,1},{3,2},{4,3},{5,4},{6,5},{7,6},{8,7},{9,8},{10,9},{11,1... | collective-permute-start | bytes 344072 | tf_op jit(solution)/shard_map/ppermute | solution.py:19
  83.9 1.3 %collective-permute-start.17 = (f32[1]{0:T(128)}, f32[1]{0:T(128)}, u32[]{:S(2)}, u32[]{:S(2)}) collective-permute-start(f32[1]{0:T(128)} %add.766), channel_id=1, source_target_pairs={{0,1},{1,0},{2,3},{3,2},{4,5},{5,4},{6,7},{7,6},{8,9},{9,8},{10,11... | collective-permute-start | bytes 20 | tf_op jit(solution)/shard_map/ppermute | solution.py:36

commit v20 on v19

--- a/solution.py
+++ b/solution.py
@@ -104,11 +104,11 @@
     adjoint_operand = kappa * adjoint_next
 
     def operator(values, later=None):
-        wide = extended(values, 1, HALO)
+        wide = extended(values, 1, planes)
         cross = lax.optimization_barrier(cross_terms(values, buoyancy))
         if later is not None:
             cross, later = lax.optimization_barrier((cross, later))
-        flux = flux_buoyancy * forward_diff(wide, 1, planes + 7, start=HALO - 4)
+        flux = flux_buoyancy * forward_diff(wide, 1, planes + 7, start=planes - 4)
         lap = backward_diff(flux, 1, planes) + cross
         return lap if later is None else (lap, later)
 

time: 89.6 us -> 92.2 us (1.029)
  starting transfers between devices: 42.2 us -> 49.1 us
  waiting for transfers between devices: 15.5 us -> 11.7 us
    ppermute x4, starting transfers between devices: 8.96 us -> 13.4 us  [butterfly_round(): return values + lax.ppermute(values, axis, pairs)]
    ppermute x7, waiting for transfers between devices: 15.2 us -> 11.7 us  [extended(): after = lax.ppermute(first, 'mp', down)]
    ppermute x7, starting transfers between devices: 17.6 us -> 20.1 us  [extended(): before = lax.ppermute(last, 'mp', up)]
  transfers between devices with their start and end apart: 18 -> 18, of which waited for: 8 -> 4; matrix products, arithmetic and copies ran while one was open for 14% -> 15% of each run, Pallas kernels for 0% -> 0%
where the time goes in v20:
time: 92.2 us; the launch traced here: 91.4 us
  starting transfers between devices  49.1 us (53%)
  other arithmetic  12.1 us (13%)
  waiting for transfers between devices  11.7 us (13%)
  matrix products  11.4 us (12%)
  between operations  6.3 us (7%)
    ppermute x7, starting transfers between devices, extended(): before = lax.ppermute(last, 'mp', up)  20.1 us
    ppermute x7, starting transfers between devices, extended(): after = lax.ppermute(first, 'mp', down)  15.6 us
    ppermute x4, starting transfers between devices, butterfly_round(): return values + lax.ppermute(values, axis, pairs)  13.4 us
    ppermute x7, waiting for transfers between devices, extended(): after = lax.ppermute(first, 'mp', down)  11.7 us
    dot_general x4, matrix products, sample(): jnp.einsum('srk,skz->srz', row_pick, field.reshape(shots, rows, cz), prec...  6.43 us
    dot_general x4, matrix products, injected(): jnp.einsum('srk,srz->skz', row_pick, spread, precision=lax.Precision.HIGH...  4.93 us
    add x4, other arithmetic, local(): following = following + jnp.where(source_hit, amount, 0.0)  3.03 us
    mul x7, other arithmetic, cross_terms(): flux = buoyancy * forward_diff(pad_axis(values, axis), axis, length)  2.4 us
  transfers between devices with their start and end apart: 18, of which 4 were waited for; matrix products, arithmetic and copies ran while one was open for 15% of the time, Pallas kernels for 0%

profile of v20, /device:TPU:1, one launch (start us, length us, event | category | flops | bytes accessed | tf_op | source)
XLA Modules:
  0.0 91.4 jit_solution(17356657655608070004)
XLA Ops:
  0.7 1.2 %pad_maximum_fusion.26 = (f32[2,7,32,128]{3,2,1,0:T(8,128)S(1)}, f32[2,7,32,128]{3,2,1,0:T(8,128)S(1)}) fusion(f32[1,8,32,128]{3,2,1,0:T(8,128)} %param.13, f32[1,8,32,128]{3,2,1,0:T(8,128)} %bitcast.121), kind=kLoop, calls=%fused_computation.339 | loop fusion | flops 114688 | bytes 720896 | tf_op jit(solution)/shard_map/concatenate | solution.py:99
  1.9 4.7 %collective-permute-start = (f32[2,7,32,128]{3,2,1,0:T(8,128)S(1)}, f32[2,7,32,128]{3,2,1,0:T(8,128)S(1)}, u32[]{:S(2)}, u32[]{:S(2)}) collective-permute-start(f32[2,7,32,128]{3,2,1,0:T(8,128)S(1)} %get-tuple-element.62), channel_id=1, source_target_pairs={{0,1},{1,2},{2,3},{3,4},{4,5},{5,6},{6,7},{7,8},{8,9},{9,10},{10,1... | collective-permute-start | bytes 688136 | tf_op jit(solution)/shard_map/ppermute | solution.py:18
  6.5 1.9 %collective-permute-start.1 = (f32[2,7,32,128]{3,2,1,0:T(8,128)S(1)}, f32[2,7,32,128]{3,2,1,0:T(8,128)S(1)}, u32[]{:S(2)}, u32[]{:S(2)}) collective-permute-start(f32[2,7,32,128]{3,2,1,0:T(8,128)S(1)} %get-tuple-element.61), channel_id=1, source_target_pairs={{1,0},{2,1},{3,2},{4,3},{5,4},{6,5},{7,6},{8,7},{9,8},{10,9},{11,1... | collective-permute-start | bytes 688136 | tf_op jit(solution)/shard_map/ppermute | solution.py:19
  8.5 0.3 fusion.337
  8.9 0.3 fusion.205
  9.8 0.6 fusion.551
  10.6 3.3 %collective-permute-done.1 = f32[2,7,32,128]{3,2,1,0:T(8,128)S(1)} collective-permute-done((f32[2,7,32,128]{3,2,1,0:T(8,128)S(1)}, f32[2,7,32,128]{3,2,1,0:T(8,128)S(1)}, u32[]{:S(2)}, u32[]{:S(2)}) %collective-permute-start.1) | collective-permute-done | bytes 229408 | tf_op jit(solution)/shard_map/ppermute | solution.py:19
  13.9 0.1 slice_bitcast_fusion
  14.1 0.8 fusion.530
  14.9 0.1 copy-done.2
  15.0 1.9 %collective-permute-start.2 = (f32[2,8,32,128]{3,2,1,0:T(8,128)S(1)}, f32[2,8,32,128]{3,2,1,0:T(8,128)S(1)}, u32[]{:S(2)}, u32[]{:S(2)}) collective-permute-start(f32[2,8,32,128]{3,2,1,0:T(8,128)S(1)} %pad_maximum_fusion.11), channel_id=1, source_target_pairs={{0,1},{1,2},{2,3},{3,4},{4,5},{5,6},{6,7},{7,8},{8,9},{9,10},{10,1... | collective-permute-start | bytes 786440 | tf_op jit(solution)/shard_map/ppermute | solution.py:18
  17.0 2.4 %collective-permute-start.3 = (f32[2,8,32,128]{3,2,1,0:T(8,128)S(1)}, f32[2,8,32,128]{3,2,1,0:T(8,128)S(1)}, u32[]{:S(2)}, u32[]{:S(2)}) collective-permute-start(f32[2,8,32,128]{3,2,1,0:T(8,128)S(1)} %pad_maximum_fusion.11), channel_id=1, source_target_pairs={{1,0},{2,1},{3,2},{4,3},{5,4},{6,5},{7,6},{8,7},{9,8},{10,9},{11,1... | collective-permute-start | bytes 786440 | tf_op jit(solution)/shard_map/ppermute | solution.py:19
  19.4 0.5 fusion.107
  19.9 0.5 fusion.95
  20.5 1.6 %fusion.16 = f32[2048]{0:T(1024)S(1)} fusion(f32[256,128]{1,0:T(8,128)S(1)} %bitcast.124, s32[2048]{0:T(1024)S(1)} %bitcast.144, s32[2048]{0:T(1024)S(1)} %bitcast.136), kind=kOutput, calls=%fused_computation.15 | convolution fusion | flops 806615040 | bytes 155648 | tf_op jit(solution)/shard_map/srk,skz->srz/dot_general | solution.py:130
  22.1 3.3 %collective-permute-done.3 = f32[2,8,32,128]{3,2,1,0:T(8,128)S(1)} collective-permute-done((f32[2,8,32,128]{3,2,1,0:T(8,128)S(1)}, f32[2,8,32,128]{3,2,1,0:T(8,128)S(1)}, u32[]{:S(2)}, u32[]{:S(2)}) %collective-permute-start.3) | collective-permute-done | bytes 262176 | tf_op jit(solution)/shard_map/ppermute | solution.py:19
  25.5 0.2 fusion.72
  25.7 0.1 fusion.127
  25.8 0.7 fusion.532
  26.6 1.9 %collective-permute-start.4 = (f32[1,8,32,128]{3,2,1,0:T(8,128)S(1)}, f32[1,8,32,128]{3,2,1,0:T(8,128)S(1)}, u32[]{:S(2)}, u32[]{:S(2)}) collective-permute-start(f32[1,8,32,128]{3,2,1,0:T(8,128)S(1)} %fusion.532), channel_id=1, source_target_pairs={{0,1},{1,2},{2,3},{3,4},{4,5},{5,6},{6,7},{7,8},{8,9},{9,10},{10,1... | collective-permute-start | bytes 393224 | tf_op jit(solution)/shard_map/ppermute | solution.py:18
  28.5 2.4 %collective-permute-start.5 = (f32[1,8,32,128]{3,2,1,0:T(8,128)S(1)}, f32[1,8,32,128]{3,2,1,0:T(8,128)S(1)}, u32[]{:S(2)}, u32[]{:S(2)}) collective-permute-start(f32[1,8,32,128]{3,2,1,0:T(8,128)S(1)} %fusion.532), channel_id=1, source_target_pairs={{1,0},{2,1},{3,2},{4,3},{5,4},{6,5},{7,6},{8,7},{9,8},{10,9},{11,1... | collective-permute-start | bytes 393224 | tf_op jit(solution)/shard_map/ppermute | solution.py:19
  30.9 0.3 fusion.360
  31.2 0.3 fusion.229
  31.5 1.6 %fusion.19 = f32[2048]{0:T(1024)S(1)} fusion(f32[256,128]{1,0:T(8,128)S(1)} %bitcast.125, s32[2048]{0:T(1024)S(1)} %bitcast.145, s32[2048]{0:T(1024)S(1)} %bitcast.137), kind=kOutput, calls=%fused_computation.16 | convolution fusion | flops 806615040 | bytes 155648 | tf_op jit(solution)/shard_map/srk,skz->srz/dot_general | solution.py:130
  33.2 2.5 %collective-permute-done.5 = f32[1,8,32,128]{3,2,1,0:T(8,128)S(1)} collective-permute-done((f32[1,8,32,128]{3,2,1,0:T(8,128)S(1)}, f32[1,8,32,128]{3,2,1,0:T(8,128)S(1)}, u32[]{:S(2)}, u32[]{:S(2)}) %collective-permute-start.5) | collective-permute-done | bytes 131104 | tf_op jit(solution)/shard_map/ppermute | solution.py:19
  35.7 0.1 fusion.172
  35.8 0.7 fusion.534
  36.6 1.9 %collective-permute-start.6 = (f32[1,8,32,128]{3,2,1,0:T(8,128)S(1)}, f32[1,8,32,128]{3,2,1,0:T(8,128)S(1)}, u32[]{:S(2)}, u32[]{:S(2)}) collective-permute-start(f32[1,8,32,128]{3,2,1,0:T(8,128)S(1)} %get-tuple-element.42), channel_id=1, source_target_pairs={{0,1},{1,2},{2,3},{3,4},{4,5},{5,6},{6,7},{7,8},{8,9},{9,10},{10,1... | collective-permute-start | bytes 393224 | tf_op jit(solution)/shard_map/ppermute | solution.py:18
  38.5 2.4 %collective-permute-start.7 = (f32[1,8,32,128]{3,2,1,0:T(8,128)S(1)}, f32[1,8,32,128]{3,2,1,0:T(8,128)S(1)}, u32[]{:S(2)}, u32[]{:S(2)}) collective-permute-start(f32[1,8,32,128]{3,2,1,0:T(8,128)S(1)} %get-tuple-element.42), channel_id=1, source_target_pairs={{1,0},{2,1},{3,2},{4,3},{5,4},{6,5},{7,6},{8,7},{9,8},{10,9},{11,1... | collective-permute-start | bytes 393224 | tf_op jit(solution)/shard_map/ppermute | solution.py:19
  40.9 0.3 fusion.383
  41.3 0.3 fusion.253
  41.6 1.6 %fusion.22 = f32[2048]{0:T(1024)S(1)} fusion(f32[256,128]{1,0:T(8,128)S(1)} %bitcast.126, s32[2048]{0:T(1024)S(1)} %bitcast.146, s32[2048]{0:T(1024)S(1)} %bitcast.138), kind=kOutput, calls=%fused_computation.17 | convolution fusion | flops 806615040 | bytes 155648 | tf_op jit(solution)/shard_map/srk,skz->srz/dot_general | solution.py:130
  43.2 2.5 %collective-permute-done.7 = f32[1,8,32,128]{3,2,1,0:T(8,128)S(1)} collective-permute-done((f32[1,8,32,128]{3,2,1,0:T(8,128)S(1)}, f32[1,8,32,128]{3,2,1,0:T(8,128)S(1)}, u32[]{:S(2)}, u32[]{:S(2)}) %collective-permute-start.7) | collective-permute-done | bytes 131104 | tf_op jit(solution)/shard_map/ppermute | solution.py:19
  45.7 0.1 fusion.163
  45.9 0.7 fusion.536
  46.6 1.6 %fusion.13 = f32[2048]{0:T(1024)S(1)} fusion(f32[256,128]{1,0:T(8,128)S(1)} %bitcast.127, s32[2048]{0:T(1024)S(1)} %bitcast.147, s32[2048]{0:T(1024)S(1)} %bitcast.139), kind=kOutput, calls=%fused_computation.14 | convolution fusion | flops 806615040 | bytes 155648 | tf_op jit(solution)/shard_map/srk,skz->srz/dot_general | solution.py:130
  48.2 0.1 fusion.540
  48.3 1.2 %fusion.25 = f32[1,8,32,128]{3,2,1,0:T(8,128)S(1)} fusion(s32[8,32]{1,0:T(8,128)S(1)} %multiply_add_fusion, s32[2048]{0:T(1024)S(1)} %bitcast.148, f32[2048]{0:T(1024)S(1)} %bitcast.134, s32[2048]{0:T(1024)S(1)} %bitcast.140), kind=kOutput, calls=%fused_computation.18 | convolution fusion | flops 806354944 | bytes 156672 | tf_op jit(solution)/shard_map/srk,srz->skz/dot_general | solution.py:137
  49.6 0.6 fusion.537
  50.9 1.9 %collective-permute-start.8 = (f32[1,8,32,128]{3,2,1,0:T(8,128)S(1)}, f32[1,8,32,128]{3,2,1,0:T(8,128)S(1)}, u32[]{:S(2)}, u32[]{:S(2)}) collective-permute-start(f32[1,8,32,128]{3,2,1,0:T(8,128)S(1)} %bitcast_multiply_fusion.3), channel_id=1, source_target_pairs={{0,1},{1,2},{2,3},{3,4},{4,5},{5,6},{6,7},{7,8},{8,9},{9,10},{10,1... | collective-permute-start | bytes 393224 | tf_op jit(solution)/shard_map/ppermute | solution.py:18
  52.9 2.4 %collective-permute-start.9 = (f32[1,8,32,128]{3,2,1,0:T(8,128)S(1)}, f32[1,8,32,128]{3,2,1,0:T(8,128)S(1)}, u32[]{:S(2)}, u32[]{:S(2)}) collective-permute-start(f32[1,8,32,128]{3,2,1,0:T(8,128)S(1)} %bitcast_multiply_fusion.3), channel_id=1, source_target_pairs={{1,0},{2,1},{3,2},{4,3},{5,4},{6,5},{7,6},{8,7},{9,8},{10,9},{11,1... | collective-permute-start | bytes 393224 | tf_op jit(solution)/shard_map/ppermute | solution.py:19
  55.3 0.3 fusion.406
  55.6 3.0 %collective-permute-start.10 = (f32[1]{0:T(128)}, f32[1]{0:T(128)}, u32[]{:S(2)}, u32[]{:S(2)}) collective-permute-start(f32[1]{0:T(128)} %bitcast.31), channel_id=1, source_target_pairs={{0,2},{1,3},{2,0},{3,1},{4,6},{5,7},{6,4},{7,5},{8,10},{9,11},{10,... | collective-permute-start | bytes 20 | tf_op jit(solution)/shard_map/ppermute | solution.py:36
  58.6 0.3 fusion.277
  58.9 1.2 %fusion.28 = f32[1,8,32,128]{3,2,1,0:T(8,128)S(1)} fusion(s32[8,32]{1,0:T(8,128)S(1)} %multiply_add_fusion, s32[2048]{0:T(1024)S(1)} %bitcast.149, f32[2048]{0:T(1024)S(1)} %bitcast.133, s32[2048]{0:T(1024)S(1)} %bitcast.141), kind=kOutput, calls=%fused_computation.19 | convolution fusion | flops 806354944 | bytes 156672 | tf_op jit(solution)/shard_map/srk,srz->skz/dot_general | solution.py:137
  60.9 0.1 fusion.154
  61.0 0.1 fusion.497
  61.1 3.2 %collective-permute-start.11 = (f32[1,8,32,128]{3,2,1,0:T(8,128)S(1)}, f32[1,8,32,128]{3,2,1,0:T(8,128)S(1)}, u32[]{:S(2)}, u32[]{:S(2)}) collective-permute-start(f32[1,8,32,128]{3,2,1,0:T(8,128)S(1)} %bitcast_multiply_fusion.2), channel_id=1, source_target_pairs={{0,1},{1,2},{2,3},{3,4},{4,5},{5,6},{6,7},{7,8},{8,9},{9,10},{10,1... | collective-permute-start | bytes 393224 | tf_op jit(solution)/shard_map/ppermute | solution.py:18
  64.4 2.1 %collective-permute-start.12 = (f32[1,8,32,128]{3,2,1,0:T(8,128)S(1)}, f32[1,8,32,128]{3,2,1,0:T(8,128)S(1)}, u32[]{:S(2)}, u32[]{:S(2)}) collective-permute-start(f32[1,8,32,128]{3,2,1,0:T(8,128)S(1)} %bitcast_multiply_fusion.2), channel_id=1, source_target_pairs={{1,0},{2,1},{3,2},{4,3},{5,4},{6,5},{7,6},{8,7},{9,8},{10,9},{11,1... | collective-permute-start | bytes 393224 | tf_op jit(solution)/shard_map/ppermute | solution.py:19
  66.5 0.3 fusion.429
  66.8 2.7 %collective-permute-start.13 = (f32[1]{0:T(128)}, f32[1]{0:T(128)}, u32[]{:S(2)}, u32[]{:S(2)}) collective-permute-start(f32[1]{0:T(128)} %add.718), channel_id=1, source_target_pairs={{0,4},{1,5},{2,6},{3,7},{4,0},{5,1},{6,2},{7,3},{8,12},{9,13},{10,... | collective-permute-start | bytes 20 | tf_op jit(solution)/shard_map/ppermute | solution.py:36
  69.5 0.3 fusion.301
  69.8 1.2 %fusion.31 = f32[1,8,32,128]{3,2,1,0:T(8,128)S(1)} fusion(s32[8,32]{1,0:T(8,128)S(1)} %multiply_add_fusion, s32[2048]{0:T(1024)S(1)} %bitcast.150, f32[2048]{0:T(1024)S(1)} %bitcast.131, s32[2048]{0:T(1024)S(1)} %bitcast.142), kind=kOutput, calls=%fused_computation.20 | convolution fusion | flops 806354944 | bytes 156672 | tf_op jit(solution)/shard_map/srk,srz->skz/dot_general | solution.py:137
  71.8 0.1 fusion.145
  71.9 0.1 fusion.486
  72.0 4.5 %collective-permute-start.14 = (f32[1,8,32,128]{3,2,1,0:T(8,128)S(1)}, f32[1,8,32,128]{3,2,1,0:T(8,128)S(1)}, u32[]{:S(2)}, u32[]{:S(2)}) collective-permute-start(f32[1,8,32,128]{3,2,1,0:T(8,128)S(1)} %bitcast_multiply_fusion.1), channel_id=1, source_target_pairs={{0,1},{1,2},{2,3},{3,4},{4,5},{5,6},{6,7},{7,8},{8,9},{9,10},{10,1... | collective-permute-start | bytes 393224 | tf_op jit(solution)/shard_map/ppermute | solution.py:18
  76.5 1.9 %collective-permute-start.15 = (f32[1,8,32,128]{3,2,1,0:T(8,128)S(1)}, f32[1,8,32,128]{3,2,1,0:T(8,128)S(1)}, u32[]{:S(2)}, u32[]{:S(2)}) collective-permute-start(f32[1,8,32,128]{3,2,1,0:T(8,128)S(1)} %bitcast_multiply_fusion.1), channel_id=1, source_target_pairs={{1,0},{2,1},{3,2},{4,3},{5,4},{6,5},{7,6},{8,7},{9,8},{10,9},{11,1... | collective-permute-start | bytes 393224 | tf_op jit(solution)/shard_map/ppermute | solution.py:19
  78.4 0.3 fusion.452
  78.7 3.2 %collective-permute-start.16 = (f32[1]{0:T(128)}, f32[1]{0:T(128)}, u32[]{:S(2)}, u32[]{:S(2)}) collective-permute-start(f32[1]{0:T(128)} %add.742), channel_id=1, source_target_pairs={{0,8},{1,9},{2,10},{3,11},{4,12},{5,13},{6,14},{7,15},{8,0},{9,1},... | collective-permute-start | bytes 20 | tf_op jit(solution)/shard_map/ppermute | solution.py:36
  81.9 0.3 fusion.325
  82.2 1.2 %fusion.34 = f32[1,8,32,128]{3,2,1,0:T(8,128)S(1)} fusion(s32[8,32]{1,0:T(8,128)S(1)} %multiply_add_fusion, s32[2048]{0:T(1024)S(1)} %bitcast.151, f32[2048]{0:T(1024)S(1)} %bitcast.129, s32[2048]{0:T(1024)S(1)} %bitcast.143), kind=kOutput, calls=%fused_computation.21 | convolution fusion | flops 806354944 | bytes 156672 | tf_op jit(solution)/shard_map/srk,srz->skz/dot_general | solution.py:137
  84.1 4.5 %collective-permute-start.17 = (f32[1]{0:T(128)}, f32[1]{0:T(128)}, u32[]{:S(2)}, u32[]{:S(2)}) collective-permute-start(f32[1]{0:T(128)} %add.766), channel_id=1, source_target_pairs={{0,1},{1,0},{2,3},{3,2},{4,5},{5,4},{6,7},{7,6},{8,9},{9,8},{10,11... | collective-permute-start | bytes 20 | tf_op jit(solution)/shard_map/ppermute | solution.py:36
  89.3 0.1 fusion.136
  89.4 0.9 bitcast_multiply_fusion
  (52 shorter events, 0.6 us)
Async XLA Ops:
  0.6 7.9 %copy-start = (f32[8,32,128]{2,1,0:T(8,128)S(1)}, f32[8,32,128]{2,1,0:T(8,128)}, u32[]{:S(2)}) copy-start(f32[8,32,128]{2,1,0:T(8,128)} %param.11) | copy-start | bytes 393220
  0.6 7.9 %copy-start.1 = (f32[1,8,32,128]{3,2,1,0:T(8,128)S(1)}, f32[1,8,32,128]{3,2,1,0:T(8,128)}, u32[]{:S(2)}) copy-start(f32[1,8,32,128]{3,2,1,0:T(8,128)} %param.13) | copy-start | bytes 393220
  0.7 7.9 %copy-start.6 = (f32[1,8,32,128]{3,2,1,0:T(8,128)S(1)}, f32[1,8,32,128]{3,2,1,0:T(8,128)}, u32[]{:S(2)}) copy-start(f32[1,8,32,128]{3,2,1,0:T(8,128)} %param.12) | copy-start | bytes 393220
  0.7 9.2 %copy-start.9 = (f32[1,4]{1,0:T(1,128)S(1)}, f32[1,4]{1,0:T(1,128)}, u32[]{:S(2)}) copy-start(f32[1,4]{1,0:T(1,128)} %param.17) | copy-start | bytes 52
  0.7 9.8 %copy-start.7 = (s32[1,2048]{1,0:T(1,128)S(1)}, s32[1,2048]{1,0:T(1,128)}, u32[]{:S(2)}) copy-start(s32[1,2048]{1,0:T(1,128)} %param.18) | copy-start | bytes 24580
  1.9 8.7 %copy-start.4 = (f32[8,32,128]{2,1,0:T(8,128)S(1)}, f32[8,32,128]{2,1,0:T(8,128)}, u32[]{:S(2)}) copy-start(f32[8,32,128]{2,1,0:T(8,128)} %param.10) | copy-start | bytes 393220
  1.9 8.7 %collective-permute-start = (f32[2,7,32,128]{3,2,1,0:T(8,128)S(1)}, f32[2,7,32,128]{3,2,1,0:T(8,128)S(1)}, u32[]{:S(2)}, u32[]{:S(2)}) collective-permute-start(f32[2,7,32,128]{3,2,1,0:T(8,128)S(1)} %get-tuple-element.62), channel_id=1, source_target_pairs={{0,1},{1,2},{2,3},{3,4},{4,5},{5,6},{6,7},{7,8},{8,9},{9,10},{10,1... | collective-permute-start | bytes 688136 | tf_op jit(solution)/shard_map/ppermute | solution.py:18
  6.5 7.3 %collective-permute-start.1 = (f32[2,7,32,128]{3,2,1,0:T(8,128)S(1)}, f32[2,7,32,128]{3,2,1,0:T(8,128)S(1)}, u32[]{:S(2)}, u32[]{:S(2)}) collective-permute-start(f32[2,7,32,128]{3,2,1,0:T(8,128)S(1)} %get-tuple-element.61), channel_id=1, source_target_pairs={{1,0},{2,1},{3,2},{4,3},{5,4},{6,5},{7,6},{8,7},{9,8},{10,9},{11,1... | collective-permute-start | bytes 688136 | tf_op jit(solution)/shard_map/ppermute | solution.py:19
  14.1 0.9 %copy-start.2 = (f32[1,8,32,128]{3,2,1,0:T(8,128)S(1)}, f32[1,8,32,128]{3,2,1,0:T(8,128)}, u32[]{:S(2)}) copy-start(f32[1,8,32,128]{3,2,1,0:T(8,128)} %param.14) | copy-start | bytes 393220
  15.0 7.1 %collective-permute-start.2 = (f32[2,8,32,128]{3,2,1,0:T(8,128)S(1)}, f32[2,8,32,128]{3,2,1,0:T(8,128)S(1)}, u32[]{:S(2)}, u32[]{:S(2)}) collective-permute-start(f32[2,8,32,128]{3,2,1,0:T(8,128)S(1)} %pad_maximum_fusion.11), channel_id=1, source_target_pairs={{0,1},{1,2},{2,3},{3,4},{4,5},{5,6},{6,7},{7,8},{8,9},{9,10},{10,1... | collective-permute-start | bytes 786440 | tf_op jit(solution)/shard_map/ppermute | solution.py:18
  17.0 8.5 %collective-permute-start.3 = (f32[2,8,32,128]{3,2,1,0:T(8,128)S(1)}, f32[2,8,32,128]{3,2,1,0:T(8,128)S(1)}, u32[]{:S(2)}, u32[]{:S(2)}) collective-permute-start(f32[2,8,32,128]{3,2,1,0:T(8,128)S(1)} %pad_maximum_fusion.11), channel_id=1, source_target_pairs={{1,0},{2,1},{3,2},{4,3},{5,4},{6,5},{7,6},{8,7},{9,8},{10,9},{11,1... | collective-permute-start | bytes 786440 | tf_op jit(solution)/shard_map/ppermute | solution.py:19
  26.6 6.6 %collective-permute-start.4 = (f32[1,8,32,128]{3,2,1,0:T(8,128)S(1)}, f32[1,8,32,128]{3,2,1,0:T(8,128)S(1)}, u32[]{:S(2)}, u32[]{:S(2)}) collective-permute-start(f32[1,8,32,128]{3,2,1,0:T(8,128)S(1)} %fusion.532), channel_id=1, source_target_pairs={{0,1},{1,2},{2,3},{3,4},{4,5},{5,6},{6,7},{7,8},{8,9},{9,10},{10,1... | collective-permute-start | bytes 393224 | tf_op jit(solution)/shard_map/ppermute | solution.py:18
  28.5 7.2 %collective-permute-start.5 = (f32[1,8,32,128]{3,2,1,0:T(8,128)S(1)}, f32[1,8,32,128]{3,2,1,0:T(8,128)S(1)}, u32[]{:S(2)}, u32[]{:S(2)}) collective-permute-start(f32[1,8,32,128]{3,2,1,0:T(8,128)S(1)} %fusion.532), channel_id=1, source_target_pairs={{1,0},{2,1},{3,2},{4,3},{5,4},{6,5},{7,6},{8,7},{9,8},{10,9},{11,1... | collective-permute-start | bytes 393224 | tf_op jit(solution)/shard_map/ppermute | solution.py:19
  36.6 6.6 %collective-permute-start.6 = (f32[1,8,32,128]{3,2,1,0:T(8,128)S(1)}, f32[1,8,32,128]{3,2,1,0:T(8,128)S(1)}, u32[]{:S(2)}, u32[]{:S(2)}) collective-permute-start(f32[1,8,32,128]{3,2,1,0:T(8,128)S(1)} %get-tuple-element.42), channel_id=1, source_target_pairs={{0,1},{1,2},{2,3},{3,4},{4,5},{5,6},{6,7},{7,8},{8,9},{9,10},{10,1... | collective-permute-start | bytes 393224 | tf_op jit(solution)/shard_map/ppermute | solution.py:18
  38.5 7.2 %collective-permute-start.7 = (f32[1,8,32,128]{3,2,1,0:T(8,128)S(1)}, f32[1,8,32,128]{3,2,1,0:T(8,128)S(1)}, u32[]{:S(2)}, u32[]{:S(2)}) collective-permute-start(f32[1,8,32,128]{3,2,1,0:T(8,128)S(1)} %get-tuple-element.42), channel_id=1, source_target_pairs={{1,0},{2,1},{3,2},{4,3},{5,4},{6,5},{7,6},{8,7},{9,8},{10,9},{11,1... | collective-permute-start | bytes 393224 | tf_op jit(solution)/shard_map/ppermute | solution.py:19
  46.6 1.6 %copy-start.8 = (f32[1,4,2048]{2,1,0:T(4,128)S(1)}, f32[1,4,2048]{2,1,0:T(4,128)}, u32[]{:S(2)}) copy-start(f32[1,4,2048]{2,1,0:T(4,128)} %param.19) | copy-start | bytes 98308
  48.3 2.5 %copy-start.5 = (f32[1,8,32,128]{3,2,1,0:T(8,128)S(1)}, f32[1,8,32,128]{3,2,1,0:T(8,128)}, u32[]{:S(2)}) copy-start(f32[1,8,32,128]{3,2,1,0:T(8,128)} %param.15) | copy-start | bytes 393220
  50.9 9.9 %collective-permute-start.8 = (f32[1,8,32,128]{3,2,1,0:T(8,128)S(1)}, f32[1,8,32,128]{3,2,1,0:T(8,128)S(1)}, u32[]{:S(2)}, u32[]{:S(2)}) collective-permute-start(f32[1,8,32,128]{3,2,1,0:T(8,128)S(1)} %bitcast_multiply_fusion.3), channel_id=1, source_target_pairs={{0,1},{1,2},{2,3},{3,4},{4,5},{5,6},{6,7},{7,8},{8,9},{9,10},{10,1... | collective-permute-start | bytes 393224 | tf_op jit(solution)/shard_map/ppermute | solution.py:18
  52.9 8.0 %collective-permute-start.9 = (f32[1,8,32,128]{3,2,1,0:T(8,128)S(1)}, f32[1,8,32,128]{3,2,1,0:T(8,128)S(1)}, u32[]{:S(2)}, u32[]{:S(2)}) collective-permute-start(f32[1,8,32,128]{3,2,1,0:T(8,128)S(1)} %bitcast_multiply_fusion.3), channel_id=1, source_target_pairs={{1,0},{2,1},{3,2},{4,3},{5,4},{6,5},{7,6},{8,7},{9,8},{10,9},{11,1... | collective-permute-start | bytes 393224 | tf_op jit(solution)/shard_map/ppermute | solution.py:19
  55.6 4.6 %collective-permute-start.10 = (f32[1]{0:T(128)}, f32[1]{0:T(128)}, u32[]{:S(2)}, u32[]{:S(2)}) collective-permute-start(f32[1]{0:T(128)} %bitcast.31), channel_id=1, source_target_pairs={{0,2},{1,3},{2,0},{3,1},{4,6},{5,7},{6,4},{7,5},{8,10},{9,11},{10,... | collective-permute-start | bytes 20 | tf_op jit(solution)/shard_map/ppermute | solution.py:36
  61.1 10.6 %collective-permute-start.11 = (f32[1,8,32,128]{3,2,1,0:T(8,128)S(1)}, f32[1,8,32,128]{3,2,1,0:T(8,128)S(1)}, u32[]{:S(2)}, u32[]{:S(2)}) collective-permute-start(f32[1,8,32,128]{3,2,1,0:T(8,128)S(1)} %bitcast_multiply_fusion.2), channel_id=1, source_target_pairs={{0,1},{1,2},{2,3},{3,4},{4,5},{5,6},{6,7},{7,8},{8,9},{9,10},{10,1... | collective-permute-start | bytes 393224 | tf_op jit(solution)/shard_map/ppermute | solution.py:18
  64.4 7.4 %collective-permute-start.12 = (f32[1,8,32,128]{3,2,1,0:T(8,128)S(1)}, f32[1,8,32,128]{3,2,1,0:T(8,128)S(1)}, u32[]{:S(2)}, u32[]{:S(2)}) collective-permute-start(f32[1,8,32,128]{3,2,1,0:T(8,128)S(1)} %bitcast_multiply_fusion.2), channel_id=1, source_target_pairs={{1,0},{2,1},{3,2},{4,3},{5,4},{6,5},{7,6},{8,7},{9,8},{10,9},{11,1... | collective-permute-start | bytes 393224 | tf_op jit(solution)/shard_map/ppermute | solution.py:19
  66.8 4.3 %collective-permute-start.13 = (f32[1]{0:T(128)}, f32[1]{0:T(128)}, u32[]{:S(2)}, u32[]{:S(2)}) collective-permute-start(f32[1]{0:T(128)} %add.718), channel_id=1, source_target_pairs={{0,4},{1,5},{2,6},{3,7},{4,0},{5,1},{6,2},{7,3},{8,12},{9,13},{10,... | collective-permute-start | bytes 20 | tf_op jit(solution)/shard_map/ppermute | solution.py:36
  72.0 17.4 %copy-start.3 = (f32[1,8,32,128]{3,2,1,0:T(8,128)}, f32[1,8,32,128]{3,2,1,0:T(8,128)S(1)}, u32[]{:S(2)}) copy-start(f32[1,8,32,128]{3,2,1,0:T(8,128)S(1)} %fusion.486) | copy-start | bytes 393220
  72.0 17.2 %collective-permute-start.14 = (f32[1,8,32,128]{3,2,1,0:T(8,128)S(1)}, f32[1,8,32,128]{3,2,1,0:T(8,128)S(1)}, u32[]{:S(2)}, u32[]{:S(2)}) collective-permute-start(f32[1,8,32,128]{3,2,1,0:T(8,128)S(1)} %bitcast_multiply_fusion.1), channel_id=1, source_target_pairs={{0,1},{1,2},{2,3},{3,4},{4,5},{5,6},{6,7},{7,8},{8,9},{9,10},{10,1... | collective-permute-start | bytes 393224 | tf_op jit(solution)/shard_map/ppermute | solution.py:18
  76.5 12.7 %collective-permute-start.15 = (f32[1,8,32,128]{3,2,1,0:T(8,128)S(1)}, f32[1,8,32,128]{3,2,1,0:T(8,128)S(1)}, u32[]{:S(2)}, u32[]{:S(2)}) collective-permute-start(f32[1,8,32,128]{3,2,1,0:T(8,128)S(1)} %bitcast_multiply_fusion.1), channel_id=1, source_target_pairs={{1,0},{2,1},{3,2},{4,3},{5,4},{6,5},{7,6},{8,7},{9,8},{10,9},{11,1... | collective-permute-start | bytes 393224 | tf_op jit(solution)/shard_map/ppermute | solution.py:19
  78.7 4.7 %collective-permute-start.16 = (f32[1]{0:T(128)}, f32[1]{0:T(128)}, u32[]{:S(2)}, u32[]{:S(2)}) collective-permute-start(f32[1]{0:T(128)} %add.742), channel_id=1, source_target_pairs={{0,8},{1,9},{2,10},{3,11},{4,12},{5,13},{6,14},{7,15},{8,0},{9,1},... | collective-permute-start | bytes 20 | tf_op jit(solution)/shard_map/ppermute | solution.py:36
  84.1 4.5 %collective-permute-start.17 = (f32[1]{0:T(128)}, f32[1]{0:T(128)}, u32[]{:S(2)}, u32[]{:S(2)}) collective-permute-start(f32[1]{0:T(128)} %add.766), channel_id=1, source_target_pairs={{0,1},{1,0},{2,3},{3,2},{4,5},{5,4},{6,7},{7,6},{8,9},{9,8},{10,11... | collective-permute-start | bytes 20 | tf_op jit(solution)/shard_map/ppermute | solution.py:36

commit v21 on v19

--- a/solution.py
+++ b/solution.py
@@ -96,10 +96,21 @@
         flux = flux_buoyancy * forward_diff(wide, 1, planes + 7, start=HALO - 4)
         return backward_diff(flux, 1, planes) + cross_terms(values, buoyancy)
 
-    first = extended(jnp.concatenate([buoyancy[None], wave_now], axis=0), 1, HALO)
-    flux_buoyancy = first[0, HALO - 4 : HALO + planes + 3]
+    devices = lax.axis_size("mp")
+    up = [(i, i + 1) for i in range(devices - 1)]
+    down = [(j, i) for i, j in up]
+    below = lax.ppermute(
+        jnp.concatenate([buoyancy[planes - 4 :], wave_now[:, planes - HALO :].reshape((shots * HALO, cy, cz))]), "mp", up
+    )
+    above = lax.ppermute(
+        jnp.concatenate([buoyancy[:3], wave_now[:, :HALO].reshape((shots * HALO, cy, cz))]), "mp", down
+    )
+    flux_buoyancy = jnp.concatenate([below[:4], buoyancy, above[:3]], axis=0)
+    first_wide = jnp.concatenate(
+        [below[4:].reshape((shots, HALO, cy, cz)), wave_now, above[3:].reshape((shots, HALO, cy, cz))], axis=1
+    )
     first_cross, first_base = lax.optimization_barrier((cross_terms(wave_now, buoyancy), 2.0 * wave_now - wave_prev))
-    first_flux = flux_buoyancy * forward_diff(first[1 : 1 + shots], 1, planes + 7, start=HALO - 4)
+    first_flux = flux_buoyancy * forward_diff(first_wide, 1, planes + 7, start=HALO - 4)
     first_lap = backward_diff(first_flux, 1, planes) + first_cross
     adjoint_operand = kappa * adjoint_next
 

time: 89.6 us -> 90 us (level)
  local copies, waits for them, and re-layouts: 0.86 us -> 2.77 us
  other arithmetic: 12.1 us -> 11 us
  waiting for transfers between devices: 15.5 us -> 14.5 us
    ppermute x0 -> x2, starting transfers between devices: none -> 6.59 us  [the longest x1 4.67 us: local(): lax.ppermute(jnp.concatenate([buoyancy[planes - 4:], wave_now[:, planes -...]
    ppermute x7 -> x6, starting transfers between devices: 17.6 us -> 13.1 us  [extended(): before = lax.ppermute(last, 'mp', up)]
    ppermute x7 -> x6, waiting for transfers between devices: 15.2 us -> 11.6 us  [extended(): after = lax.ppermute(first, 'mp', down)]
    ppermute x0 -> x2, waiting for transfers between devices: none -> 2.6 us  [the longest x1 2.6 us: local(): lax.ppermute(jnp.concatenate([buoyancy[:3], wave_now[:, :HALO].reshape((s...]
    ppermute x7 -> x6, starting transfers between devices: 15.6 us -> 13.7 us  [extended(): after = lax.ppermute(first, 'mp', down)]
    concatenate x1 -> x4, other arithmetic: 1.14 us -> 0.07 us  [the longest x1 0.03 us: local(): jnp.concatenate([below[4:].reshape((shots, HALO, cy, cz)), wave_now, abov...]
    reshape x0 -> x3, local copies, waits for them, and re-layouts: none -> 1.05 us  [the longest x1 1.03 us: local(): wave_now[:, planes - HALO:].reshape((shots * HALO, cy, cz))]
where the time goes in v21:
time: 90 us; the launch traced here: 88.3 us
  starting transfers between devices  42.1 us (47%)
  waiting for transfers between devices  14.5 us (16%)
  matrix products  11.4 us (13%)
  other arithmetic  11 us (12%)
  between operations  6.53 us (7%)
  local copies, waits for them, and re-layouts  2.77 us (3%)
    ppermute x6, starting transfers between devices, extended(): after = lax.ppermute(first, 'mp', down)  13.7 us
    ppermute x6, starting transfers between devices, extended(): before = lax.ppermute(last, 'mp', up)  13.1 us
    ppermute x6, waiting for transfers between devices, extended(): after = lax.ppermute(first, 'mp', down)  11.6 us
    ppermute x4, starting transfers between devices, butterfly_round(): return values + lax.ppermute(values, axis, pairs)  8.83 us
    dot_general x4, matrix products, sample(): jnp.einsum('srk,skz->srz', row_pick, field.reshape(shots, rows, cz), prec...  6.43 us
    dot_general x4, matrix products, injected(): jnp.einsum('srk,srz->skz', row_pick, spread, precision=lax.Precision.HIGH...  4.93 us
    ppermute x1, starting transfers between devices, local(): lax.ppermute(jnp.concatenate([buoyancy[planes - 4:], wave_now[:, planes -...  4.67 us
    add x4, other arithmetic, local(): following = following + jnp.where(source_hit, amount, 0.0)  3.02 us
  transfers between devices with their start and end apart: 18, of which 8 were waited for; matrix products, arithmetic and copies ran while one was open for 14% of the time, Pallas kernels for 0%

profile of v21, /device:TPU:1, one launch (start us, length us, event | category | flops | bytes accessed | tf_op | source)
XLA Modules:
  0.0 88.3 jit_solution(6880691488546697191)
XLA Ops:
  0.7 1.0 %slice_bitcast_fusion.3 = (f32[7,32,128]{2,1,0:T(8,128)S(1)}, f32[7,32,128]{2,1,0:T(8,128)S(1)}) fusion(f32[1,8,32,128]{3,2,1,0:T(8,128)} %param.13), kind=kLoop, calls=%fused_computation.801 | loop fusion | bytes 458752 | tf_op jit(solution)/shard_map/reshape | solution.py:103
  1.7 0.8 slice.1056
  2.6 4.7 %collective-permute-start = (f32[11,32,128]{2,1,0:T(8,128)S(1)}, f32[11,32,128]{2,1,0:T(8,128)S(1)}, u32[]{:S(2)}, u32[]{:S(2)}) collective-permute-start(f32[11,32,128]{2,1,0:T(8,128)S(1)} %pad_maximum_fusion.9), channel_id=1, source_target_pairs={{0,1},{1,2},{2,3},{3,4},{4,5},{5,6},{6,7},{7,8},{8,9},{9,10},{10,1... | collective-permute-start | bytes 540680 | tf_op jit(solution)/shard_map/ppermute | solution.py:102
  7.3 1.9 %collective-permute-start.1 = (f32[10,32,128]{2,1,0:T(8,128)S(1)}, f32[10,32,128]{2,1,0:T(8,128)S(1)}, u32[]{:S(2)}, u32[]{:S(2)}) collective-permute-start(f32[10,32,128]{2,1,0:T(8,128)S(1)} %pad_maximum_fusion.10), channel_id=1, source_target_pairs={{1,0},{2,1},{3,2},{4,3},{5,4},{6,5},{7,6},{8,7},{9,8},{10,9},{11,1... | collective-permute-start | bytes 491528 | tf_op jit(solution)/shard_map/ppermute | solution.py:105
  9.3 0.3 fusion.331
  9.8 0.3 fusion.199
  10.7 0.6 fusion.550
  11.3 2.6 %collective-permute-done.1 = f32[10,32,128]{2,1,0:T(8,128)S(1)} collective-permute-done((f32[10,32,128]{2,1,0:T(8,128)S(1)}, f32[10,32,128]{2,1,0:T(8,128)S(1)}, u32[]{:S(2)}, u32[]{:S(2)}) %collective-permute-start.1) | collective-permute-done | bytes 163872 | tf_op jit(solution)/shard_map/ppermute | solution.py:105
  14.0 0.1 fusion.170
  14.2 0.8 fusion.524
  14.9 0.1 copy-done.2
  15.2 1.9 %collective-permute-start.2 = (f32[2,7,32,128]{3,2,1,0:T(8,128)S(1)}, f32[2,7,32,128]{3,2,1,0:T(8,128)S(1)}, u32[]{:S(2)}, u32[]{:S(2)}) collective-permute-start(f32[2,7,32,128]{3,2,1,0:T(8,128)S(1)} %get-tuple-element.59), channel_id=1, source_target_pairs={{0,1},{1,2},{2,3},{3,4},{4,5},{5,6},{6,7},{7,8},{8,9},{9,10},{10,1... | collective-permute-start | bytes 688136 | tf_op jit(solution)/shard_map/ppermute | solution.py:18
  17.1 2.4 %collective-permute-start.3 = (f32[2,7,32,128]{3,2,1,0:T(8,128)S(1)}, f32[2,7,32,128]{3,2,1,0:T(8,128)S(1)}, u32[]{:S(2)}, u32[]{:S(2)}) collective-permute-start(f32[2,7,32,128]{3,2,1,0:T(8,128)S(1)} %get-tuple-element.60), channel_id=1, source_target_pairs={{1,0},{2,1},{3,2},{4,3},{5,4},{6,5},{7,6},{8,7},{9,8},{10,9},{11,1... | collective-permute-start | bytes 688136 | tf_op jit(solution)/shard_map/ppermute | solution.py:19
  19.5 0.5 fusion.106
  20.1 0.5 fusion.94
  20.6 1.6 %fusion.16 = f32[2048]{0:T(1024)S(1)} fusion(f32[256,128]{1,0:T(8,128)S(1)} %bitcast.135, s32[2048]{0:T(1024)S(1)} %bitcast.154, s32[2048]{0:T(1024)S(1)} %bitcast.146), kind=kOutput, calls=%fused_computation.15 | convolution fusion | flops 806615040 | bytes 155648 | tf_op jit(solution)/shard_map/srk,skz->srz/dot_general | solution.py:141
  22.3 3.0 %collective-permute-done.3 = f32[2,7,32,128]{3,2,1,0:T(8,128)S(1)} collective-permute-done((f32[2,7,32,128]{3,2,1,0:T(8,128)S(1)}, f32[2,7,32,128]{3,2,1,0:T(8,128)S(1)}, u32[]{:S(2)}, u32[]{:S(2)}) %collective-permute-start.3) | collective-permute-done | bytes 229408 | tf_op jit(solution)/shard_map/ppermute | solution.py:19
  25.3 0.2 fusion.72
  25.5 0.1 fusion.126
  25.6 0.7 fusion.526
  26.4 0.3 fusion.354
  26.7 1.9 %collective-permute-start.4 = (f32[1,7,32,128]{3,2,1,0:T(8,128)S(1)}, f32[1,7,32,128]{3,2,1,0:T(8,128)S(1)}, u32[]{:S(2)}, u32[]{:S(2)}) collective-permute-start(f32[1,7,32,128]{3,2,1,0:T(8,128)S(1)} %get-tuple-element.71), channel_id=1, source_target_pairs={{0,1},{1,2},{2,3},{3,4},{4,5},{5,6},{6,7},{7,8},{8,9},{9,10},{10,1... | collective-permute-start | bytes 344072 | tf_op jit(solution)/shard_map/ppermute | solution.py:18
  28.6 2.4 %collective-permute-start.5 = (f32[1,7,32,128]{3,2,1,0:T(8,128)S(1)}, f32[1,7,32,128]{3,2,1,0:T(8,128)S(1)}, u32[]{:S(2)}, u32[]{:S(2)}) collective-permute-start(f32[1,7,32,128]{3,2,1,0:T(8,128)S(1)} %get-tuple-element.72), channel_id=1, source_target_pairs={{1,0},{2,1},{3,2},{4,3},{5,4},{6,5},{7,6},{8,7},{9,8},{10,9},{11,1... | collective-permute-start | bytes 344072 | tf_op jit(solution)/shard_map/ppermute | solution.py:19
  31.0 0.3 fusion.223
  31.4 1.6 %fusion.19 = f32[2048]{0:T(1024)S(1)} fusion(f32[256,128]{1,0:T(8,128)S(1)} %bitcast.134, s32[2048]{0:T(1024)S(1)} %bitcast.155, s32[2048]{0:T(1024)S(1)} %bitcast.147), kind=kOutput, calls=%fused_computation.16 | convolution fusion | flops 806615040 | bytes 155648 | tf_op jit(solution)/shard_map/srk,skz->srz/dot_general | solution.py:141
  33.0 2.7 %collective-permute-done.5 = f32[1,7,32,128]{3,2,1,0:T(8,128)S(1)} collective-permute-done((f32[1,7,32,128]{3,2,1,0:T(8,128)S(1)}, f32[1,7,32,128]{3,2,1,0:T(8,128)S(1)}, u32[]{:S(2)}, u32[]{:S(2)}) %collective-permute-start.5) | collective-permute-done | bytes 114720 | tf_op jit(solution)/shard_map/ppermute | solution.py:19
  35.7 0.1 fusion.163
  35.8 0.7 fusion.528
  36.6 0.3 fusion.377
  36.9 1.9 %collective-permute-start.6 = (f32[1,7,32,128]{3,2,1,0:T(8,128)S(1)}, f32[1,7,32,128]{3,2,1,0:T(8,128)S(1)}, u32[]{:S(2)}, u32[]{:S(2)}) collective-permute-start(f32[1,7,32,128]{3,2,1,0:T(8,128)S(1)} %get-tuple-element.69), channel_id=1, source_target_pairs={{0,1},{1,2},{2,3},{3,4},{4,5},{5,6},{6,7},{7,8},{8,9},{9,10},{10,1... | collective-permute-start | bytes 344072 | tf_op jit(solution)/shard_map/ppermute | solution.py:18
  38.8 2.4 %collective-permute-start.7 = (f32[1,7,32,128]{3,2,1,0:T(8,128)S(1)}, f32[1,7,32,128]{3,2,1,0:T(8,128)S(1)}, u32[]{:S(2)}, u32[]{:S(2)}) collective-permute-start(f32[1,7,32,128]{3,2,1,0:T(8,128)S(1)} %get-tuple-element.70), channel_id=1, source_target_pairs={{1,0},{2,1},{3,2},{4,3},{5,4},{6,5},{7,6},{8,7},{9,8},{10,9},{11,1... | collective-permute-start | bytes 344072 | tf_op jit(solution)/shard_map/ppermute | solution.py:19
  41.2 0.3 fusion.247
  41.5 1.6 %fusion.22 = f32[2048]{0:T(1024)S(1)} fusion(f32[256,128]{1,0:T(8,128)S(1)} %bitcast.136, s32[2048]{0:T(1024)S(1)} %bitcast.156, s32[2048]{0:T(1024)S(1)} %bitcast.148), kind=kOutput, calls=%fused_computation.17 | convolution fusion | flops 806615040 | bytes 155648 | tf_op jit(solution)/shard_map/srk,skz->srz/dot_general | solution.py:141
  43.1 2.7 %collective-permute-done.7 = f32[1,7,32,128]{3,2,1,0:T(8,128)S(1)} collective-permute-done((f32[1,7,32,128]{3,2,1,0:T(8,128)S(1)}, f32[1,7,32,128]{3,2,1,0:T(8,128)S(1)}, u32[]{:S(2)}, u32[]{:S(2)}) %collective-permute-start.7) | collective-permute-done | bytes 114720 | tf_op jit(solution)/shard_map/ppermute | solution.py:19
  45.8 0.1 fusion.156
  45.9 0.7 fusion.530
  46.7 1.6 %fusion.13 = f32[2048]{0:T(1024)S(1)} fusion(f32[256,128]{1,0:T(8,128)S(1)} %bitcast.137, s32[2048]{0:T(1024)S(1)} %bitcast.157, s32[2048]{0:T(1024)S(1)} %bitcast.149), kind=kOutput, calls=%fused_computation.14 | convolution fusion | flops 806615040 | bytes 155648 | tf_op jit(solution)/shard_map/srk,skz->srz/dot_general | solution.py:141
  48.4 1.2 %fusion.25 = f32[1,8,32,128]{3,2,1,0:T(8,128)S(1)} fusion(s32[8,32]{1,0:T(8,128)S(1)} %multiply_add_fusion, s32[2048]{0:T(1024)S(1)} %bitcast.158, f32[2048]{0:T(1024)S(1)} %bitcast.144, s32[2048]{0:T(1024)S(1)} %bitcast.150), kind=kOutput, calls=%fused_computation.18 | convolution fusion | flops 806354944 | bytes 156672 | tf_op jit(solution)/shard_map/srk,srz->skz/dot_general | solution.py:148
  49.7 0.6 fusion.531
  51.1 0.3 fusion.400
  51.4 3.0 %collective-permute-start.10 = (f32[1]{0:T(128)}, f32[1]{0:T(128)}, u32[]{:S(2)}, u32[]{:S(2)}) collective-permute-start(f32[1]{0:T(128)} %bitcast.35), channel_id=1, source_target_pairs={{0,2},{1,3},{2,0},{3,1},{4,6},{5,7},{6,4},{7,5},{8,10},{9,11},{10,... | collective-permute-start | bytes 20 | tf_op jit(solution)/shard_map/ppermute | solution.py:36
  54.4 1.9 %collective-permute-start.8 = (f32[1,7,32,128]{3,2,1,0:T(8,128)S(1)}, f32[1,7,32,128]{3,2,1,0:T(8,128)S(1)}, u32[]{:S(2)}, u32[]{:S(2)}) collective-permute-start(f32[1,7,32,128]{3,2,1,0:T(8,128)S(1)} %get-tuple-element.67), channel_id=1, source_target_pairs={{0,1},{1,2},{2,3},{3,4},{4,5},{5,6},{6,7},{7,8},{8,9},{9,10},{10,1... | collective-permute-start | bytes 344072 | tf_op jit(solution)/shard_map/ppermute | solution.py:18
  56.3 2.6 %collective-permute-start.9 = (f32[1,7,32,128]{3,2,1,0:T(8,128)S(1)}, f32[1,7,32,128]{3,2,1,0:T(8,128)S(1)}, u32[]{:S(2)}, u32[]{:S(2)}) collective-permute-start(f32[1,7,32,128]{3,2,1,0:T(8,128)S(1)} %get-tuple-element.68), channel_id=1, source_target_pairs={{1,0},{2,1},{3,2},{4,3},{5,4},{6,5},{7,6},{8,7},{9,8},{10,9},{11,1... | collective-permute-start | bytes 344072 | tf_op jit(solution)/shard_map/ppermute | solution.py:19
  58.9 0.3 fusion.271
  59.2 1.2 %fusion.28 = f32[1,8,32,128]{3,2,1,0:T(8,128)S(1)} fusion(s32[8,32]{1,0:T(8,128)S(1)} %multiply_add_fusion, s32[2048]{0:T(1024)S(1)} %bitcast.159, f32[2048]{0:T(1024)S(1)} %bitcast.143, s32[2048]{0:T(1024)S(1)} %bitcast.151), kind=kOutput, calls=%fused_computation.19 | convolution fusion | flops 806354944 | bytes 156672 | tf_op jit(solution)/shard_map/srk,srz->skz/dot_general | solution.py:148
  61.2 1.3 %collective-permute-done.9 = f32[1,7,32,128]{3,2,1,0:T(8,128)S(1)} collective-permute-done((f32[1,7,32,128]{3,2,1,0:T(8,128)S(1)}, f32[1,7,32,128]{3,2,1,0:T(8,128)S(1)}, u32[]{:S(2)}, u32[]{:S(2)}) %collective-permute-start.9) | collective-permute-done | bytes 114720 | tf_op jit(solution)/shard_map/ppermute | solution.py:19
  62.5 0.1 fusion.149
  62.7 0.3 fusion.423
  63.0 2.1 %collective-permute-start.13 = (f32[1]{0:T(128)}, f32[1]{0:T(128)}, u32[]{:S(2)}, u32[]{:S(2)}) collective-permute-start(f32[1]{0:T(128)} %add.718), channel_id=1, source_target_pairs={{0,4},{1,5},{2,6},{3,7},{4,0},{5,1},{6,2},{7,3},{8,12},{9,13},{10,... | collective-permute-start | bytes 20 | tf_op jit(solution)/shard_map/ppermute | solution.py:36
  65.1 2.7 %collective-permute-start.11 = (f32[1,7,32,128]{3,2,1,0:T(8,128)S(1)}, f32[1,7,32,128]{3,2,1,0:T(8,128)S(1)}, u32[]{:S(2)}, u32[]{:S(2)}) collective-permute-start(f32[1,7,32,128]{3,2,1,0:T(8,128)S(1)} %get-tuple-element.65), channel_id=1, source_target_pairs={{0,1},{1,2},{2,3},{3,4},{4,5},{5,6},{6,7},{7,8},{8,9},{9,10},{10,1... | collective-permute-start | bytes 344072 | tf_op jit(solution)/shard_map/ppermute | solution.py:18
  67.9 1.9 %collective-permute-start.12 = (f32[1,7,32,128]{3,2,1,0:T(8,128)S(1)}, f32[1,7,32,128]{3,2,1,0:T(8,128)S(1)}, u32[]{:S(2)}, u32[]{:S(2)}) collective-permute-start(f32[1,7,32,128]{3,2,1,0:T(8,128)S(1)} %get-tuple-element.66), channel_id=1, source_target_pairs={{1,0},{2,1},{3,2},{4,3},{5,4},{6,5},{7,6},{8,7},{9,8},{10,9},{11,1... | collective-permute-start | bytes 344072 | tf_op jit(solution)/shard_map/ppermute | solution.py:19
  69.8 0.3 fusion.295
  70.1 1.2 %fusion.31 = f32[1,8,32,128]{3,2,1,0:T(8,128)S(1)} fusion(s32[8,32]{1,0:T(8,128)S(1)} %multiply_add_fusion, s32[2048]{0:T(1024)S(1)} %bitcast.160, f32[2048]{0:T(1024)S(1)} %bitcast.141, s32[2048]{0:T(1024)S(1)} %bitcast.152), kind=kOutput, calls=%fused_computation.20 | convolution fusion | flops 806354944 | bytes 156672 | tf_op jit(solution)/shard_map/srk,srz->skz/dot_general | solution.py:148
  72.0 1.9 %collective-permute-done.12 = f32[1,7,32,128]{3,2,1,0:T(8,128)S(1)} collective-permute-done((f32[1,7,32,128]{3,2,1,0:T(8,128)S(1)}, f32[1,7,32,128]{3,2,1,0:T(8,128)S(1)}, u32[]{:S(2)}, u32[]{:S(2)}) %collective-permute-start.12) | collective-permute-done | bytes 114720 | tf_op jit(solution)/shard_map/ppermute | solution.py:19
  74.0 0.1 fusion.142
  74.3 0.3 fusion.446
  74.6 2.8 %collective-permute-start.16 = (f32[1]{0:T(128)}, f32[1]{0:T(128)}, u32[]{:S(2)}, u32[]{:S(2)}) collective-permute-start(f32[1]{0:T(128)} %add.742), channel_id=1, source_target_pairs={{0,8},{1,9},{2,10},{3,11},{4,12},{5,13},{6,14},{7,15},{8,0},{9,1},... | collective-permute-start | bytes 20 | tf_op jit(solution)/shard_map/ppermute | solution.py:36
  77.4 2.6 %collective-permute-start.14 = (f32[1,7,32,128]{3,2,1,0:T(8,128)S(1)}, f32[1,7,32,128]{3,2,1,0:T(8,128)S(1)}, u32[]{:S(2)}, u32[]{:S(2)}) collective-permute-start(f32[1,7,32,128]{3,2,1,0:T(8,128)S(1)} %get-tuple-element.63), channel_id=1, source_target_pairs={{0,1},{1,2},{2,3},{3,4},{4,5},{5,6},{6,7},{7,8},{8,9},{9,10},{10,1... | collective-permute-start | bytes 344072 | tf_op jit(solution)/shard_map/ppermute | solution.py:18
  80.0 1.9 %collective-permute-start.15 = (f32[1,7,32,128]{3,2,1,0:T(8,128)S(1)}, f32[1,7,32,128]{3,2,1,0:T(8,128)S(1)}, u32[]{:S(2)}, u32[]{:S(2)}) collective-permute-start(f32[1,7,32,128]{3,2,1,0:T(8,128)S(1)} %get-tuple-element.64), channel_id=1, source_target_pairs={{1,0},{2,1},{3,2},{4,3},{5,4},{6,5},{7,6},{8,7},{9,8},{10,9},{11,1... | collective-permute-start | bytes 344072 | tf_op jit(solution)/shard_map/ppermute | solution.py:19
  82.0 0.3 fusion.319
  82.3 1.2 %fusion.34 = f32[1,8,32,128]{3,2,1,0:T(8,128)S(1)} fusion(s32[8,32]{1,0:T(8,128)S(1)} %multiply_add_fusion, s32[2048]{0:T(1024)S(1)} %bitcast.161, f32[2048]{0:T(1024)S(1)} %bitcast.139, s32[2048]{0:T(1024)S(1)} %bitcast.153), kind=kOutput, calls=%fused_computation.21 | convolution fusion | flops 806354944 | bytes 156672 | tf_op jit(solution)/shard_map/srk,srz->skz/dot_general | solution.py:148
  84.2 0.9 %collective-permute-start.17 = (f32[1]{0:T(128)}, f32[1]{0:T(128)}, u32[]{:S(2)}, u32[]{:S(2)}) collective-permute-start(f32[1]{0:T(128)} %add.766), channel_id=1, source_target_pairs={{0,1},{1,0},{2,3},{3,2},{4,5},{5,4},{6,7},{7,6},{8,9},{9,8},{10,11... | collective-permute-start | bytes 20 | tf_op jit(solution)/shard_map/ppermute | solution.py:36
  85.1 0.3 collective-permute-done.17
  86.3 0.9 bitcast_multiply_fusion
  (68 shorter events, 1.1 us)
Async XLA Ops:
  0.6 8.6 %copy-start.1 = (f32[1,8,32,128]{3,2,1,0:T(8,128)S(1)}, f32[1,8,32,128]{3,2,1,0:T(8,128)}, u32[]{:S(2)}) copy-start(f32[1,8,32,128]{3,2,1,0:T(8,128)} %param.13) | copy-start | bytes 393220
  0.6 6.6 %slice-start = ((f32[8,32,128]{2,1,0:T(8,128)}), f32[3,32,128]{2,1,0:T(8,128)S(1)}, s32[]{:S(2)}) async-start(f32[8,32,128]{2,1,0:T(8,128)} %param.11), calls=%async_computation | async-start | bytes 98304 | tf_op jit(solution)/shard_map/slice | solution.py:106
  0.7 8.6 %copy-start = (f32[8,32,128]{2,1,0:T(8,128)S(1)}, f32[8,32,128]{2,1,0:T(8,128)}, u32[]{:S(2)}) copy-start(f32[8,32,128]{2,1,0:T(8,128)} %param.11) | copy-start | bytes 393220
  0.7 8.6 %copy-start.6 = (f32[1,8,32,128]{3,2,1,0:T(8,128)S(1)}, f32[1,8,32,128]{3,2,1,0:T(8,128)}, u32[]{:S(2)}) copy-start(f32[1,8,32,128]{3,2,1,0:T(8,128)} %param.12) | copy-start | bytes 393220
  2.6 7.0 %copy-start.4 = (f32[8,32,128]{2,1,0:T(8,128)S(1)}, f32[8,32,128]{2,1,0:T(8,128)}, u32[]{:S(2)}) copy-start(f32[8,32,128]{2,1,0:T(8,128)} %param.10) | copy-start | bytes 393220
  2.6 11.4 %collective-permute-start = (f32[11,32,128]{2,1,0:T(8,128)S(1)}, f32[11,32,128]{2,1,0:T(8,128)S(1)}, u32[]{:S(2)}, u32[]{:S(2)}) collective-permute-start(f32[11,32,128]{2,1,0:T(8,128)S(1)} %pad_maximum_fusion.9), channel_id=1, source_target_pairs={{0,1},{1,2},{2,3},{3,4},{4,5},{5,6},{6,7},{7,8},{8,9},{9,10},{10,1... | collective-permute-start | bytes 540680 | tf_op jit(solution)/shard_map/ppermute | solution.py:102
  7.3 2.4 %copy-start.7 = (s32[1,2048]{1,0:T(1,128)S(1)}, s32[1,2048]{1,0:T(1,128)}, u32[]{:S(2)}) copy-start(s32[1,2048]{1,0:T(1,128)} %param.18) | copy-start | bytes 24580
  7.3 6.6 %collective-permute-start.1 = (f32[10,32,128]{2,1,0:T(8,128)S(1)}, f32[10,32,128]{2,1,0:T(8,128)S(1)}, u32[]{:S(2)}, u32[]{:S(2)}) collective-permute-start(f32[10,32,128]{2,1,0:T(8,128)S(1)} %pad_maximum_fusion.10), channel_id=1, source_target_pairs={{1,0},{2,1},{3,2},{4,3},{5,4},{6,5},{7,6},{8,7},{9,8},{10,9},{11,1... | collective-permute-start | bytes 491528 | tf_op jit(solution)/shard_map/ppermute | solution.py:105
  9.3 1.4 %copy-start.9 = (f32[1,4]{1,0:T(1,128)S(1)}, f32[1,4]{1,0:T(1,128)}, u32[]{:S(2)}) copy-start(f32[1,4]{1,0:T(1,128)} %param.17) | copy-start | bytes 52
  14.1 0.9 %copy-start.2 = (f32[1,8,32,128]{3,2,1,0:T(8,128)S(1)}, f32[1,8,32,128]{3,2,1,0:T(8,128)}, u32[]{:S(2)}) copy-start(f32[1,8,32,128]{3,2,1,0:T(8,128)} %param.14) | copy-start | bytes 393220
  15.2 7.1 %collective-permute-start.2 = (f32[2,7,32,128]{3,2,1,0:T(8,128)S(1)}, f32[2,7,32,128]{3,2,1,0:T(8,128)S(1)}, u32[]{:S(2)}, u32[]{:S(2)}) collective-permute-start(f32[2,7,32,128]{3,2,1,0:T(8,128)S(1)} %get-tuple-element.59), channel_id=1, source_target_pairs={{0,1},{1,2},{2,3},{3,4},{4,5},{5,6},{6,7},{7,8},{8,9},{9,10},{10,1... | collective-permute-start | bytes 688136 | tf_op jit(solution)/shard_map/ppermute | solution.py:18
  17.1 8.1 %collective-permute-start.3 = (f32[2,7,32,128]{3,2,1,0:T(8,128)S(1)}, f32[2,7,32,128]{3,2,1,0:T(8,128)S(1)}, u32[]{:S(2)}, u32[]{:S(2)}) collective-permute-start(f32[2,7,32,128]{3,2,1,0:T(8,128)S(1)} %get-tuple-element.60), channel_id=1, source_target_pairs={{1,0},{2,1},{3,2},{4,3},{5,4},{6,5},{7,6},{8,7},{9,8},{10,9},{11,1... | collective-permute-start | bytes 688136 | tf_op jit(solution)/shard_map/ppermute | solution.py:19
  26.7 6.3 %collective-permute-start.4 = (f32[1,7,32,128]{3,2,1,0:T(8,128)S(1)}, f32[1,7,32,128]{3,2,1,0:T(8,128)S(1)}, u32[]{:S(2)}, u32[]{:S(2)}) collective-permute-start(f32[1,7,32,128]{3,2,1,0:T(8,128)S(1)} %get-tuple-element.71), channel_id=1, source_target_pairs={{0,1},{1,2},{2,3},{3,4},{4,5},{5,6},{6,7},{7,8},{8,9},{9,10},{10,1... | collective-permute-start | bytes 344072 | tf_op jit(solution)/shard_map/ppermute | solution.py:18
  28.6 7.0 %collective-permute-start.5 = (f32[1,7,32,128]{3,2,1,0:T(8,128)S(1)}, f32[1,7,32,128]{3,2,1,0:T(8,128)S(1)}, u32[]{:S(2)}, u32[]{:S(2)}) collective-permute-start(f32[1,7,32,128]{3,2,1,0:T(8,128)S(1)} %get-tuple-element.72), channel_id=1, source_target_pairs={{1,0},{2,1},{3,2},{4,3},{5,4},{6,5},{7,6},{8,7},{9,8},{10,9},{11,1... | collective-permute-start | bytes 344072 | tf_op jit(solution)/shard_map/ppermute | solution.py:19
  36.9 6.3 %collective-permute-start.6 = (f32[1,7,32,128]{3,2,1,0:T(8,128)S(1)}, f32[1,7,32,128]{3,2,1,0:T(8,128)S(1)}, u32[]{:S(2)}, u32[]{:S(2)}) collective-permute-start(f32[1,7,32,128]{3,2,1,0:T(8,128)S(1)} %get-tuple-element.69), channel_id=1, source_target_pairs={{0,1},{1,2},{2,3},{3,4},{4,5},{5,6},{6,7},{7,8},{8,9},{9,10},{10,1... | collective-permute-start | bytes 344072 | tf_op jit(solution)/shard_map/ppermute | solution.py:18
  38.8 7.0 %collective-permute-start.7 = (f32[1,7,32,128]{3,2,1,0:T(8,128)S(1)}, f32[1,7,32,128]{3,2,1,0:T(8,128)S(1)}, u32[]{:S(2)}, u32[]{:S(2)}) collective-permute-start(f32[1,7,32,128]{3,2,1,0:T(8,128)S(1)} %get-tuple-element.70), channel_id=1, source_target_pairs={{1,0},{2,1},{3,2},{4,3},{5,4},{6,5},{7,6},{8,7},{9,8},{10,9},{11,1... | collective-permute-start | bytes 344072 | tf_op jit(solution)/shard_map/ppermute | solution.py:19
  46.7 1.6 %copy-start.8 = (f32[1,4,2048]{2,1,0:T(4,128)S(1)}, f32[1,4,2048]{2,1,0:T(4,128)}, u32[]{:S(2)}) copy-start(f32[1,4,2048]{2,1,0:T(4,128)} %param.19) | copy-start | bytes 98308
  48.4 2.5 %copy-start.5 = (f32[1,8,32,128]{3,2,1,0:T(8,128)S(1)}, f32[1,8,32,128]{3,2,1,0:T(8,128)}, u32[]{:S(2)}) copy-start(f32[1,8,32,128]{3,2,1,0:T(8,128)} %param.15) | copy-start | bytes 393220
  51.4 9.1 %collective-permute-start.10 = (f32[1]{0:T(128)}, f32[1]{0:T(128)}, u32[]{:S(2)}, u32[]{:S(2)}) collective-permute-start(f32[1]{0:T(128)} %bitcast.35), channel_id=1, source_target_pairs={{0,2},{1,3},{2,0},{3,1},{4,6},{5,7},{6,4},{7,5},{8,10},{9,11},{10,... | collective-permute-start | bytes 20 | tf_op jit(solution)/shard_map/ppermute | solution.py:36
  54.4 6.7 %collective-permute-start.8 = (f32[1,7,32,128]{3,2,1,0:T(8,128)S(1)}, f32[1,7,32,128]{3,2,1,0:T(8,128)S(1)}, u32[]{:S(2)}, u32[]{:S(2)}) collective-permute-start(f32[1,7,32,128]{3,2,1,0:T(8,128)S(1)} %get-tuple-element.67), channel_id=1, source_target_pairs={{0,1},{1,2},{2,3},{3,4},{4,5},{5,6},{6,7},{7,8},{8,9},{9,10},{10,1... | collective-permute-start | bytes 344072 | tf_op jit(solution)/shard_map/ppermute | solution.py:18
  56.3 6.1 %collective-permute-start.9 = (f32[1,7,32,128]{3,2,1,0:T(8,128)S(1)}, f32[1,7,32,128]{3,2,1,0:T(8,128)S(1)}, u32[]{:S(2)}, u32[]{:S(2)}) collective-permute-start(f32[1,7,32,128]{3,2,1,0:T(8,128)S(1)} %get-tuple-element.68), channel_id=1, source_target_pairs={{1,0},{2,1},{3,2},{4,3},{5,4},{6,5},{7,6},{8,7},{9,8},{10,9},{11,1... | collective-permute-start | bytes 344072 | tf_op jit(solution)/shard_map/ppermute | solution.py:19
  63.0 8.3 %collective-permute-start.13 = (f32[1]{0:T(128)}, f32[1]{0:T(128)}, u32[]{:S(2)}, u32[]{:S(2)}) collective-permute-start(f32[1]{0:T(128)} %add.718), channel_id=1, source_target_pairs={{0,4},{1,5},{2,6},{3,7},{4,0},{5,1},{6,2},{7,3},{8,12},{9,13},{10,... | collective-permute-start | bytes 20 | tf_op jit(solution)/shard_map/ppermute | solution.py:36
  65.1 6.9 %collective-permute-start.11 = (f32[1,7,32,128]{3,2,1,0:T(8,128)S(1)}, f32[1,7,32,128]{3,2,1,0:T(8,128)S(1)}, u32[]{:S(2)}, u32[]{:S(2)}) collective-permute-start(f32[1,7,32,128]{3,2,1,0:T(8,128)S(1)} %get-tuple-element.65), channel_id=1, source_target_pairs={{0,1},{1,2},{2,3},{3,4},{4,5},{5,6},{6,7},{7,8},{8,9},{9,10},{10,1... | collective-permute-start | bytes 344072 | tf_op jit(solution)/shard_map/ppermute | solution.py:18
  67.9 6.1 %collective-permute-start.12 = (f32[1,7,32,128]{3,2,1,0:T(8,128)S(1)}, f32[1,7,32,128]{3,2,1,0:T(8,128)S(1)}, u32[]{:S(2)}, u32[]{:S(2)}) collective-permute-start(f32[1,7,32,128]{3,2,1,0:T(8,128)S(1)} %get-tuple-element.66), channel_id=1, source_target_pairs={{1,0},{2,1},{3,2},{4,3},{5,4},{6,5},{7,6},{8,7},{9,8},{10,9},{11,1... | collective-permute-start | bytes 344072 | tf_op jit(solution)/shard_map/ppermute | solution.py:19
  74.2 12.1 %copy-start.3 = (f32[1,8,32,128]{3,2,1,0:T(8,128)}, f32[1,8,32,128]{3,2,1,0:T(8,128)S(1)}, u32[]{:S(2)}) copy-start(f32[1,8,32,128]{3,2,1,0:T(8,128)S(1)} %fusion.480) | copy-start | bytes 393220
  74.6 9.0 %collective-permute-start.16 = (f32[1]{0:T(128)}, f32[1]{0:T(128)}, u32[]{:S(2)}, u32[]{:S(2)}) collective-permute-start(f32[1]{0:T(128)} %add.742), channel_id=1, source_target_pairs={{0,8},{1,9},{2,10},{3,11},{4,12},{5,13},{6,14},{7,15},{8,0},{9,1},... | collective-permute-start | bytes 20 | tf_op jit(solution)/shard_map/ppermute | solution.py:36
  77.4 8.7 %collective-permute-start.14 = (f32[1,7,32,128]{3,2,1,0:T(8,128)S(1)}, f32[1,7,32,128]{3,2,1,0:T(8,128)S(1)}, u32[]{:S(2)}, u32[]{:S(2)}) collective-permute-start(f32[1,7,32,128]{3,2,1,0:T(8,128)S(1)} %get-tuple-element.63), channel_id=1, source_target_pairs={{0,1},{1,2},{2,3},{3,4},{4,5},{5,6},{6,7},{7,8},{8,9},{9,10},{10,1... | collective-permute-start | bytes 344072 | tf_op jit(solution)/shard_map/ppermute | solution.py:18
  80.0 6.1 %collective-permute-start.15 = (f32[1,7,32,128]{3,2,1,0:T(8,128)S(1)}, f32[1,7,32,128]{3,2,1,0:T(8,128)S(1)}, u32[]{:S(2)}, u32[]{:S(2)}) collective-permute-start(f32[1,7,32,128]{3,2,1,0:T(8,128)S(1)} %get-tuple-element.64), channel_id=1, source_target_pairs={{1,0},{2,1},{3,2},{4,3},{5,4},{6,5},{7,6},{8,7},{9,8},{10,9},{11,1... | collective-permute-start | bytes 344072 | tf_op jit(solution)/shard_map/ppermute | solution.py:19
  84.2 1.2 %collective-permute-start.17 = (f32[1]{0:T(128)}, f32[1]{0:T(128)}, u32[]{:S(2)}, u32[]{:S(2)}) collective-permute-start(f32[1]{0:T(128)} %add.766), channel_id=1, source_target_pairs={{0,1},{1,0},{2,3},{3,2},{4,5},{5,4},{6,7},{7,6},{8,9},{9,8},{10,11... | collective-permute-start | bytes 20 | tf_op jit(solution)/shard_map/ppermute | solution.py:36

commit v22 on v19

--- a/solution.py
+++ b/solution.py
@@ -165,10 +165,9 @@
             lap = adjoint_lap
             resid = resids[level - 1]
         else:
+            lap, (resid, misfit) = operator(kappa * mu_near, (resids[level - 1], misfit))
             if distances:
-                mu_near, misfit = lax.optimization_barrier((mu_near, misfit))
                 misfit = butterfly_round(misfit, "mp", distances.pop(0))
-            lap, resid = operator(kappa * mu_near, resids[level - 1])
         state = 2.0 * mu_near + lap - mu_far
         state = state + injected(resid)
         gradient = gradient + state * laps[level - 1]

time: 89.6 us -> 90.4 us (level)
  waiting for transfers between devices: 15.5 us -> 16.5 us
    ppermute x7, waiting for transfers between devices: 15.2 us -> 16.2 us  [extended(): after = lax.ppermute(first, 'mp', down)]
  transfers between devices with their start and end apart: 18 -> 18, of which waited for: 8 -> 8; matrix products, arithmetic and copies ran while one was open for 14% -> 13% of each run, Pallas kernels for 0% -> 0%
where the time goes in v22:
time: 90.4 us; the launch traced here: 89 us
  starting transfers between devices  42.2 us (47%)
  waiting for transfers between devices  16.5 us (18%)
  other arithmetic  12.1 us (13%)
  matrix products  11.4 us (13%)
  between operations  6.02 us (7%)
    ppermute x7, starting transfers between devices, extended(): before = lax.ppermute(last, 'mp', up)  17.6 us
    ppermute x7, waiting for transfers between devices, extended(): after = lax.ppermute(first, 'mp', down)  16.2 us
    ppermute x7, starting transfers between devices, extended(): after = lax.ppermute(first, 'mp', down)  15.6 us
    ppermute x4, starting transfers between devices, butterfly_round(): return values + lax.ppermute(values, axis, pairs)  8.96 us
    dot_general x4, matrix products, sample(): jnp.einsum('srk,skz->srz', row_pick, field.reshape(shots, rows, cz), prec...  6.43 us
    dot_general x4, matrix products, injected(): jnp.einsum('srk,srz->skz', row_pick, spread, precision=lax.Precision.HIGH...  4.93 us
    add x4, other arithmetic, local(): following = following + jnp.where(source_hit, amount, 0.0)  3.03 us
    mul x7, other arithmetic, cross_terms(): flux = buoyancy * forward_diff(pad_axis(values, axis), axis, length)  2.4 us
  transfers between devices with their start and end apart: 18, of which 8 were waited for; matrix products, arithmetic and copies ran while one was open for 13% of the time, Pallas kernels for 0%

profile of v22, /device:TPU:1, one launch (start us, length us, event | category | flops | bytes accessed | tf_op | source)
XLA Modules:
  0.0 89.0 jit_solution(2717503549924999218)
XLA Ops:
  0.7 1.1 %pad_maximum_fusion.12 = (f32[2,7,32,128]{3,2,1,0:T(8,128)S(1)}, f32[2,7,32,128]{3,2,1,0:T(8,128)S(1)}) fusion(f32[1,8,32,128]{3,2,1,0:T(8,128)} %param.13, f32[1,8,32,128]{3,2,1,0:T(8,128)} %bitcast.121), kind=kLoop, calls=%fused_computation.331 | loop fusion | flops 114688 | bytes 720896 | tf_op jit(solution)/shard_map/concatenate | solution.py:99
  1.9 4.7 %collective-permute-start = (f32[2,7,32,128]{3,2,1,0:T(8,128)S(1)}, f32[2,7,32,128]{3,2,1,0:T(8,128)S(1)}, u32[]{:S(2)}, u32[]{:S(2)}) collective-permute-start(f32[2,7,32,128]{3,2,1,0:T(8,128)S(1)} %get-tuple-element.70), channel_id=1, source_target_pairs={{0,1},{1,2},{2,3},{3,4},{4,5},{5,6},{6,7},{7,8},{8,9},{9,10},{10,1... | collective-permute-start | bytes 688136 | tf_op jit(solution)/shard_map/ppermute | solution.py:18
  6.5 1.9 %collective-permute-start.1 = (f32[2,7,32,128]{3,2,1,0:T(8,128)S(1)}, f32[2,7,32,128]{3,2,1,0:T(8,128)S(1)}, u32[]{:S(2)}, u32[]{:S(2)}) collective-permute-start(f32[2,7,32,128]{3,2,1,0:T(8,128)S(1)} %get-tuple-element.69), channel_id=1, source_target_pairs={{1,0},{2,1},{3,2},{4,3},{5,4},{6,5},{7,6},{8,7},{9,8},{10,9},{11,1... | collective-permute-start | bytes 688136 | tf_op jit(solution)/shard_map/ppermute | solution.py:19
  8.5 0.3 fusion.333
  8.8 0.3 fusion.201
  9.8 0.6 fusion.552
  10.6 3.3 %collective-permute-done.1 = f32[2,7,32,128]{3,2,1,0:T(8,128)S(1)} collective-permute-done((f32[2,7,32,128]{3,2,1,0:T(8,128)S(1)}, f32[2,7,32,128]{3,2,1,0:T(8,128)S(1)}, u32[]{:S(2)}, u32[]{:S(2)}) %collective-permute-start.1) | collective-permute-done | bytes 229408 | tf_op jit(solution)/shard_map/ppermute | solution.py:19
  13.9 0.1 slice_bitcast_fusion
  14.1 0.8 fusion.526
  14.8 0.1 copy-done.2
  15.1 1.9 %collective-permute-start.2 = (f32[2,7,32,128]{3,2,1,0:T(8,128)S(1)}, f32[2,7,32,128]{3,2,1,0:T(8,128)S(1)}, u32[]{:S(2)}, u32[]{:S(2)}) collective-permute-start(f32[2,7,32,128]{3,2,1,0:T(8,128)S(1)} %get-tuple-element.67), channel_id=1, source_target_pairs={{0,1},{1,2},{2,3},{3,4},{4,5},{5,6},{6,7},{7,8},{8,9},{9,10},{10,1... | collective-permute-start | bytes 688136 | tf_op jit(solution)/shard_map/ppermute | solution.py:18
  17.0 2.4 %collective-permute-start.3 = (f32[2,7,32,128]{3,2,1,0:T(8,128)S(1)}, f32[2,7,32,128]{3,2,1,0:T(8,128)S(1)}, u32[]{:S(2)}, u32[]{:S(2)}) collective-permute-start(f32[2,7,32,128]{3,2,1,0:T(8,128)S(1)} %get-tuple-element.68), channel_id=1, source_target_pairs={{1,0},{2,1},{3,2},{4,3},{5,4},{6,5},{7,6},{8,7},{9,8},{10,9},{11,1... | collective-permute-start | bytes 688136 | tf_op jit(solution)/shard_map/ppermute | solution.py:19
  19.4 0.5 fusion.106
  20.0 0.5 fusion.94
  20.5 1.6 %fusion.16 = f32[2048]{0:T(1024)S(1)} fusion(f32[256,128]{1,0:T(8,128)S(1)} %bitcast.125, s32[2048]{0:T(1024)S(1)} %bitcast.144, s32[2048]{0:T(1024)S(1)} %bitcast.136), kind=kOutput, calls=%fused_computation.15 | convolution fusion | flops 806615040 | bytes 155648 | tf_op jit(solution)/shard_map/srk,skz->srz/dot_general | solution.py:130
  22.1 3.0 %collective-permute-done.3 = f32[2,7,32,128]{3,2,1,0:T(8,128)S(1)} collective-permute-done((f32[2,7,32,128]{3,2,1,0:T(8,128)S(1)}, f32[2,7,32,128]{3,2,1,0:T(8,128)S(1)}, u32[]{:S(2)}, u32[]{:S(2)}) %collective-permute-start.3) | collective-permute-done | bytes 229408 | tf_op jit(solution)/shard_map/ppermute | solution.py:19
  25.2 0.2 fusion.72
  25.4 0.1 fusion.126
  25.5 0.7 fusion.528
  26.3 0.3 fusion.356
  26.6 1.9 %collective-permute-start.4 = (f32[1,7,32,128]{3,2,1,0:T(8,128)S(1)}, f32[1,7,32,128]{3,2,1,0:T(8,128)S(1)}, u32[]{:S(2)}, u32[]{:S(2)}) collective-permute-start(f32[1,7,32,128]{3,2,1,0:T(8,128)S(1)} %get-tuple-element.81), channel_id=1, source_target_pairs={{0,1},{1,2},{2,3},{3,4},{4,5},{5,6},{6,7},{7,8},{8,9},{9,10},{10,1... | collective-permute-start | bytes 344072 | tf_op jit(solution)/shard_map/ppermute | solution.py:18
  28.5 2.4 %collective-permute-start.5 = (f32[1,7,32,128]{3,2,1,0:T(8,128)S(1)}, f32[1,7,32,128]{3,2,1,0:T(8,128)S(1)}, u32[]{:S(2)}, u32[]{:S(2)}) collective-permute-start(f32[1,7,32,128]{3,2,1,0:T(8,128)S(1)} %get-tuple-element.82), channel_id=1, source_target_pairs={{1,0},{2,1},{3,2},{4,3},{5,4},{6,5},{7,6},{8,7},{9,8},{10,9},{11,1... | collective-permute-start | bytes 344072 | tf_op jit(solution)/shard_map/ppermute | solution.py:19
  30.9 0.3 fusion.225
  31.3 1.6 %fusion.19 = f32[2048]{0:T(1024)S(1)} fusion(f32[256,128]{1,0:T(8,128)S(1)} %bitcast.124, s32[2048]{0:T(1024)S(1)} %bitcast.145, s32[2048]{0:T(1024)S(1)} %bitcast.137), kind=kOutput, calls=%fused_computation.16 | convolution fusion | flops 806615040 | bytes 155648 | tf_op jit(solution)/shard_map/srk,skz->srz/dot_general | solution.py:130
  32.9 2.7 %collective-permute-done.5 = f32[1,7,32,128]{3,2,1,0:T(8,128)S(1)} collective-permute-done((f32[1,7,32,128]{3,2,1,0:T(8,128)S(1)}, f32[1,7,32,128]{3,2,1,0:T(8,128)S(1)}, u32[]{:S(2)}, u32[]{:S(2)}) %collective-permute-start.5) | collective-permute-done | bytes 114720 | tf_op jit(solution)/shard_map/ppermute | solution.py:19
  35.6 0.1 fusion.163
  35.7 0.7 fusion.530
  36.5 0.3 fusion.379
  36.8 1.9 %collective-permute-start.6 = (f32[1,7,32,128]{3,2,1,0:T(8,128)S(1)}, f32[1,7,32,128]{3,2,1,0:T(8,128)S(1)}, u32[]{:S(2)}, u32[]{:S(2)}) collective-permute-start(f32[1,7,32,128]{3,2,1,0:T(8,128)S(1)} %get-tuple-element.79), channel_id=1, source_target_pairs={{0,1},{1,2},{2,3},{3,4},{4,5},{5,6},{6,7},{7,8},{8,9},{9,10},{10,1... | collective-permute-start | bytes 344072 | tf_op jit(solution)/shard_map/ppermute | solution.py:18
  38.7 2.4 %collective-permute-start.7 = (f32[1,7,32,128]{3,2,1,0:T(8,128)S(1)}, f32[1,7,32,128]{3,2,1,0:T(8,128)S(1)}, u32[]{:S(2)}, u32[]{:S(2)}) collective-permute-start(f32[1,7,32,128]{3,2,1,0:T(8,128)S(1)} %get-tuple-element.80), channel_id=1, source_target_pairs={{1,0},{2,1},{3,2},{4,3},{5,4},{6,5},{7,6},{8,7},{9,8},{10,9},{11,1... | collective-permute-start | bytes 344072 | tf_op jit(solution)/shard_map/ppermute | solution.py:19
  41.1 0.3 fusion.249
  41.4 1.6 %fusion.22 = f32[2048]{0:T(1024)S(1)} fusion(f32[256,128]{1,0:T(8,128)S(1)} %bitcast.126, s32[2048]{0:T(1024)S(1)} %bitcast.146, s32[2048]{0:T(1024)S(1)} %bitcast.138), kind=kOutput, calls=%fused_computation.17 | convolution fusion | flops 806615040 | bytes 155648 | tf_op jit(solution)/shard_map/srk,skz->srz/dot_general | solution.py:130
  43.0 2.7 %collective-permute-done.7 = f32[1,7,32,128]{3,2,1,0:T(8,128)S(1)} collective-permute-done((f32[1,7,32,128]{3,2,1,0:T(8,128)S(1)}, f32[1,7,32,128]{3,2,1,0:T(8,128)S(1)}, u32[]{:S(2)}, u32[]{:S(2)}) %collective-permute-start.7) | collective-permute-done | bytes 114720 | tf_op jit(solution)/shard_map/ppermute | solution.py:19
  45.7 0.1 fusion.156
  45.8 0.7 fusion.532
  46.6 1.6 %fusion.13 = f32[2048]{0:T(1024)S(1)} fusion(f32[256,128]{1,0:T(8,128)S(1)} %bitcast.127, s32[2048]{0:T(1024)S(1)} %bitcast.147, s32[2048]{0:T(1024)S(1)} %bitcast.139), kind=kOutput, calls=%fused_computation.14 | convolution fusion | flops 806615040 | bytes 155648 | tf_op jit(solution)/shard_map/srk,skz->srz/dot_general | solution.py:130
  48.3 1.2 %fusion.25 = f32[1,8,32,128]{3,2,1,0:T(8,128)S(1)} fusion(s32[8,32]{1,0:T(8,128)S(1)} %multiply_add_fusion, s32[2048]{0:T(1024)S(1)} %bitcast.148, f32[2048]{0:T(1024)S(1)} %bitcast.134, s32[2048]{0:T(1024)S(1)} %bitcast.140), kind=kOutput, calls=%fused_computation.18 | convolution fusion | flops 806354944 | bytes 156672 | tf_op jit(solution)/shard_map/srk,srz->skz/dot_general | solution.py:137
  49.5 0.6 fusion.533
  50.9 0.3 fusion.402
  51.3 0.3 fusion.273
  51.6 3.0 %collective-permute-start.10 = (f32[1]{0:T(128)}, f32[1]{0:T(128)}, u32[]{:S(2)}, u32[]{:S(2)}) collective-permute-start(f32[1]{0:T(128)} %bitcast.31), channel_id=1, source_target_pairs={{0,2},{1,3},{2,0},{3,1},{4,6},{5,7},{6,4},{7,5},{8,10},{9,11},{10,... | collective-permute-start | bytes 20 | tf_op jit(solution)/shard_map/ppermute | solution.py:36
  54.6 1.9 %collective-permute-start.8 = (f32[1,7,32,128]{3,2,1,0:T(8,128)S(1)}, f32[1,7,32,128]{3,2,1,0:T(8,128)S(1)}, u32[]{:S(2)}, u32[]{:S(2)}) collective-permute-start(f32[1,7,32,128]{3,2,1,0:T(8,128)S(1)} %get-tuple-element.77), channel_id=1, source_target_pairs={{0,1},{1,2},{2,3},{3,4},{4,5},{5,6},{6,7},{7,8},{8,9},{9,10},{10,1... | collective-permute-start | bytes 344072 | tf_op jit(solution)/shard_map/ppermute | solution.py:18
  56.5 2.6 %collective-permute-start.9 = (f32[1,7,32,128]{3,2,1,0:T(8,128)S(1)}, f32[1,7,32,128]{3,2,1,0:T(8,128)S(1)}, u32[]{:S(2)}, u32[]{:S(2)}) collective-permute-start(f32[1,7,32,128]{3,2,1,0:T(8,128)S(1)} %get-tuple-element.78), channel_id=1, source_target_pairs={{1,0},{2,1},{3,2},{4,3},{5,4},{6,5},{7,6},{8,7},{9,8},{10,9},{11,1... | collective-permute-start | bytes 344072 | tf_op jit(solution)/shard_map/ppermute | solution.py:19
  59.1 1.2 %fusion.28 = f32[1,8,32,128]{3,2,1,0:T(8,128)S(1)} fusion(s32[8,32]{1,0:T(8,128)S(1)} %multiply_add_fusion, s32[2048]{0:T(1024)S(1)} %bitcast.149, f32[2048]{0:T(1024)S(1)} %bitcast.133, s32[2048]{0:T(1024)S(1)} %bitcast.141), kind=kOutput, calls=%fused_computation.19 | convolution fusion | flops 806354944 | bytes 156672 | tf_op jit(solution)/shard_map/srk,srz->skz/dot_general | solution.py:137
  60.9 1.7 %collective-permute-done.9 = f32[1,7,32,128]{3,2,1,0:T(8,128)S(1)} collective-permute-done((f32[1,7,32,128]{3,2,1,0:T(8,128)S(1)}, f32[1,7,32,128]{3,2,1,0:T(8,128)S(1)}, u32[]{:S(2)}, u32[]{:S(2)}) %collective-permute-start.9) | collective-permute-done | bytes 114720 | tf_op jit(solution)/shard_map/ppermute | solution.py:19
  62.7 0.1 fusion.149
  62.9 0.3 fusion.425
  63.2 0.3 fusion.297
  63.5 2.1 %collective-permute-start.13 = (f32[1]{0:T(128)}, f32[1]{0:T(128)}, u32[]{:S(2)}, u32[]{:S(2)}) collective-permute-start(f32[1]{0:T(128)} %add.718), channel_id=1, source_target_pairs={{0,4},{1,5},{2,6},{3,7},{4,0},{5,1},{6,2},{7,3},{8,12},{9,13},{10,... | collective-permute-start | bytes 20 | tf_op jit(solution)/shard_map/ppermute | solution.py:36
  65.6 2.6 %collective-permute-start.11 = (f32[1,7,32,128]{3,2,1,0:T(8,128)S(1)}, f32[1,7,32,128]{3,2,1,0:T(8,128)S(1)}, u32[]{:S(2)}, u32[]{:S(2)}) collective-permute-start(f32[1,7,32,128]{3,2,1,0:T(8,128)S(1)} %get-tuple-element.75), channel_id=1, source_target_pairs={{0,1},{1,2},{2,3},{3,4},{4,5},{5,6},{6,7},{7,8},{8,9},{9,10},{10,1... | collective-permute-start | bytes 344072 | tf_op jit(solution)/shard_map/ppermute | solution.py:18
  68.3 1.9 %collective-permute-start.12 = (f32[1,7,32,128]{3,2,1,0:T(8,128)S(1)}, f32[1,7,32,128]{3,2,1,0:T(8,128)S(1)}, u32[]{:S(2)}, u32[]{:S(2)}) collective-permute-start(f32[1,7,32,128]{3,2,1,0:T(8,128)S(1)} %get-tuple-element.76), channel_id=1, source_target_pairs={{1,0},{2,1},{3,2},{4,3},{5,4},{6,5},{7,6},{8,7},{9,8},{10,9},{11,1... | collective-permute-start | bytes 344072 | tf_op jit(solution)/shard_map/ppermute | solution.py:19
  70.2 1.2 %fusion.31 = f32[1,8,32,128]{3,2,1,0:T(8,128)S(1)} fusion(s32[8,32]{1,0:T(8,128)S(1)} %multiply_add_fusion, s32[2048]{0:T(1024)S(1)} %bitcast.150, f32[2048]{0:T(1024)S(1)} %bitcast.131, s32[2048]{0:T(1024)S(1)} %bitcast.142), kind=kOutput, calls=%fused_computation.20 | convolution fusion | flops 806354944 | bytes 156672 | tf_op jit(solution)/shard_map/srk,srz->skz/dot_general | solution.py:137
  72.0 2.4 %collective-permute-done.12 = f32[1,7,32,128]{3,2,1,0:T(8,128)S(1)} collective-permute-done((f32[1,7,32,128]{3,2,1,0:T(8,128)S(1)}, f32[1,7,32,128]{3,2,1,0:T(8,128)S(1)}, u32[]{:S(2)}, u32[]{:S(2)}) %collective-permute-start.12) | collective-permute-done | bytes 114720 | tf_op jit(solution)/shard_map/ppermute | solution.py:19
  74.4 0.1 fusion.142
  74.7 0.3 fusion.448
  75.0 0.3 fusion.321
  75.3 2.8 %collective-permute-start.16 = (f32[1]{0:T(128)}, f32[1]{0:T(128)}, u32[]{:S(2)}, u32[]{:S(2)}) collective-permute-start(f32[1]{0:T(128)} %add.742), channel_id=1, source_target_pairs={{0,8},{1,9},{2,10},{3,11},{4,12},{5,13},{6,14},{7,15},{8,0},{9,1},... | collective-permute-start | bytes 20 | tf_op jit(solution)/shard_map/ppermute | solution.py:36
  78.1 2.6 %collective-permute-start.14 = (f32[1,7,32,128]{3,2,1,0:T(8,128)S(1)}, f32[1,7,32,128]{3,2,1,0:T(8,128)S(1)}, u32[]{:S(2)}, u32[]{:S(2)}) collective-permute-start(f32[1,7,32,128]{3,2,1,0:T(8,128)S(1)} %get-tuple-element.73), channel_id=1, source_target_pairs={{0,1},{1,2},{2,3},{3,4},{4,5},{5,6},{6,7},{7,8},{8,9},{9,10},{10,1... | collective-permute-start | bytes 344072 | tf_op jit(solution)/shard_map/ppermute | solution.py:18
  80.8 1.9 %collective-permute-start.15 = (f32[1,7,32,128]{3,2,1,0:T(8,128)S(1)}, f32[1,7,32,128]{3,2,1,0:T(8,128)S(1)}, u32[]{:S(2)}, u32[]{:S(2)}) collective-permute-start(f32[1,7,32,128]{3,2,1,0:T(8,128)S(1)} %get-tuple-element.74), channel_id=1, source_target_pairs={{1,0},{2,1},{3,2},{4,3},{5,4},{6,5},{7,6},{8,7},{9,8},{10,9},{11,1... | collective-permute-start | bytes 344072 | tf_op jit(solution)/shard_map/ppermute | solution.py:19
  82.7 1.2 %fusion.34 = f32[1,8,32,128]{3,2,1,0:T(8,128)S(1)} fusion(s32[8,32]{1,0:T(8,128)S(1)} %multiply_add_fusion, s32[2048]{0:T(1024)S(1)} %bitcast.151, f32[2048]{0:T(1024)S(1)} %bitcast.129, s32[2048]{0:T(1024)S(1)} %bitcast.143), kind=kOutput, calls=%fused_computation.21 | convolution fusion | flops 806354944 | bytes 156672 | tf_op jit(solution)/shard_map/srk,srz->skz/dot_general | solution.py:137
  84.5 1.0 %collective-permute-start.17 = (f32[1]{0:T(128)}, f32[1]{0:T(128)}, u32[]{:S(2)}, u32[]{:S(2)}) collective-permute-start(f32[1]{0:T(128)} %add.766), channel_id=1, source_target_pairs={{0,1},{1,0},{2,3},{3,2},{4,5},{5,4},{6,7},{7,6},{8,9},{9,8},{10,11... | collective-permute-start | bytes 20 | tf_op jit(solution)/shard_map/ppermute | solution.py:36
  85.5 0.3 collective-permute-done.17
  86.4 0.5 collective-permute-done.15
  87.0 0.9 bitcast_multiply_fusion
  (58 shorter events, 1.0 us)
Async XLA Ops:
  0.6 7.9 %copy-start = (f32[8,32,128]{2,1,0:T(8,128)S(1)}, f32[8,32,128]{2,1,0:T(8,128)}, u32[]{:S(2)}) copy-start(f32[8,32,128]{2,1,0:T(8,128)} %param.11) | copy-start | bytes 393220
  0.6 7.9 %copy-start.1 = (f32[1,8,32,128]{3,2,1,0:T(8,128)S(1)}, f32[1,8,32,128]{3,2,1,0:T(8,128)}, u32[]{:S(2)}) copy-start(f32[1,8,32,128]{3,2,1,0:T(8,128)} %param.13) | copy-start | bytes 393220
  0.7 7.9 %copy-start.6 = (f32[1,8,32,128]{3,2,1,0:T(8,128)S(1)}, f32[1,8,32,128]{3,2,1,0:T(8,128)}, u32[]{:S(2)}) copy-start(f32[1,8,32,128]{3,2,1,0:T(8,128)} %param.12) | copy-start | bytes 393220
  1.8 8.0 %copy-start.9 = (f32[1,4]{1,0:T(1,128)S(1)}, f32[1,4]{1,0:T(1,128)}, u32[]{:S(2)}) copy-start(f32[1,4]{1,0:T(1,128)} %param.17) | copy-start | bytes 52
  1.8 8.6 %copy-start.7 = (s32[1,2048]{1,0:T(1,128)S(1)}, s32[1,2048]{1,0:T(1,128)}, u32[]{:S(2)}) copy-start(s32[1,2048]{1,0:T(1,128)} %param.18) | copy-start | bytes 24580
  1.8 8.7 %copy-start.4 = (f32[8,32,128]{2,1,0:T(8,128)S(1)}, f32[8,32,128]{2,1,0:T(8,128)}, u32[]{:S(2)}) copy-start(f32[8,32,128]{2,1,0:T(8,128)} %param.10) | copy-start | bytes 393220
  1.9 8.7 %collective-permute-start = (f32[2,7,32,128]{3,2,1,0:T(8,128)S(1)}, f32[2,7,32,128]{3,2,1,0:T(8,128)S(1)}, u32[]{:S(2)}, u32[]{:S(2)}) collective-permute-start(f32[2,7,32,128]{3,2,1,0:T(8,128)S(1)} %get-tuple-element.70), channel_id=1, source_target_pairs={{0,1},{1,2},{2,3},{3,4},{4,5},{5,6},{6,7},{7,8},{8,9},{9,10},{10,1... | collective-permute-start | bytes 688136 | tf_op jit(solution)/shard_map/ppermute | solution.py:18
  6.5 7.3 %collective-permute-start.1 = (f32[2,7,32,128]{3,2,1,0:T(8,128)S(1)}, f32[2,7,32,128]{3,2,1,0:T(8,128)S(1)}, u32[]{:S(2)}, u32[]{:S(2)}) collective-permute-start(f32[2,7,32,128]{3,2,1,0:T(8,128)S(1)} %get-tuple-element.69), channel_id=1, source_target_pairs={{1,0},{2,1},{3,2},{4,3},{5,4},{6,5},{7,6},{8,7},{9,8},{10,9},{11,1... | collective-permute-start | bytes 688136 | tf_op jit(solution)/shard_map/ppermute | solution.py:19
  14.0 0.9 %copy-start.2 = (f32[1,8,32,128]{3,2,1,0:T(8,128)S(1)}, f32[1,8,32,128]{3,2,1,0:T(8,128)}, u32[]{:S(2)}) copy-start(f32[1,8,32,128]{3,2,1,0:T(8,128)} %param.14) | copy-start | bytes 393220
  15.1 7.1 %collective-permute-start.2 = (f32[2,7,32,128]{3,2,1,0:T(8,128)S(1)}, f32[2,7,32,128]{3,2,1,0:T(8,128)S(1)}, u32[]{:S(2)}, u32[]{:S(2)}) collective-permute-start(f32[2,7,32,128]{3,2,1,0:T(8,128)S(1)} %get-tuple-element.67), channel_id=1, source_target_pairs={{0,1},{1,2},{2,3},{3,4},{4,5},{5,6},{6,7},{7,8},{8,9},{9,10},{10,1... | collective-permute-start | bytes 688136 | tf_op jit(solution)/shard_map/ppermute | solution.py:18
  17.0 8.1 %collective-permute-start.3 = (f32[2,7,32,128]{3,2,1,0:T(8,128)S(1)}, f32[2,7,32,128]{3,2,1,0:T(8,128)S(1)}, u32[]{:S(2)}, u32[]{:S(2)}) collective-permute-start(f32[2,7,32,128]{3,2,1,0:T(8,128)S(1)} %get-tuple-element.68), channel_id=1, source_target_pairs={{1,0},{2,1},{3,2},{4,3},{5,4},{6,5},{7,6},{8,7},{9,8},{10,9},{11,1... | collective-permute-start | bytes 688136 | tf_op jit(solution)/shard_map/ppermute | solution.py:19
  26.6 6.3 %collective-permute-start.4 = (f32[1,7,32,128]{3,2,1,0:T(8,128)S(1)}, f32[1,7,32,128]{3,2,1,0:T(8,128)S(1)}, u32[]{:S(2)}, u32[]{:S(2)}) collective-permute-start(f32[1,7,32,128]{3,2,1,0:T(8,128)S(1)} %get-tuple-element.81), channel_id=1, source_target_pairs={{0,1},{1,2},{2,3},{3,4},{4,5},{5,6},{6,7},{7,8},{8,9},{9,10},{10,1... | collective-permute-start | bytes 344072 | tf_op jit(solution)/shard_map/ppermute | solution.py:18
  28.5 7.0 %collective-permute-start.5 = (f32[1,7,32,128]{3,2,1,0:T(8,128)S(1)}, f32[1,7,32,128]{3,2,1,0:T(8,128)S(1)}, u32[]{:S(2)}, u32[]{:S(2)}) collective-permute-start(f32[1,7,32,128]{3,2,1,0:T(8,128)S(1)} %get-tuple-element.82), channel_id=1, source_target_pairs={{1,0},{2,1},{3,2},{4,3},{5,4},{6,5},{7,6},{8,7},{9,8},{10,9},{11,1... | collective-permute-start | bytes 344072 | tf_op jit(solution)/shard_map/ppermute | solution.py:19
  36.8 6.3 %collective-permute-start.6 = (f32[1,7,32,128]{3,2,1,0:T(8,128)S(1)}, f32[1,7,32,128]{3,2,1,0:T(8,128)S(1)}, u32[]{:S(2)}, u32[]{:S(2)}) collective-permute-start(f32[1,7,32,128]{3,2,1,0:T(8,128)S(1)} %get-tuple-element.79), channel_id=1, source_target_pairs={{0,1},{1,2},{2,3},{3,4},{4,5},{5,6},{6,7},{7,8},{8,9},{9,10},{10,1... | collective-permute-start | bytes 344072 | tf_op jit(solution)/shard_map/ppermute | solution.py:18
  38.7 7.0 %collective-permute-start.7 = (f32[1,7,32,128]{3,2,1,0:T(8,128)S(1)}, f32[1,7,32,128]{3,2,1,0:T(8,128)S(1)}, u32[]{:S(2)}, u32[]{:S(2)}) collective-permute-start(f32[1,7,32,128]{3,2,1,0:T(8,128)S(1)} %get-tuple-element.80), channel_id=1, source_target_pairs={{1,0},{2,1},{3,2},{4,3},{5,4},{6,5},{7,6},{8,7},{9,8},{10,9},{11,1... | collective-permute-start | bytes 344072 | tf_op jit(solution)/shard_map/ppermute | solution.py:19
  46.6 1.6 %copy-start.8 = (f32[1,4,2048]{2,1,0:T(4,128)S(1)}, f32[1,4,2048]{2,1,0:T(4,128)}, u32[]{:S(2)}) copy-start(f32[1,4,2048]{2,1,0:T(4,128)} %param.19) | copy-start | bytes 98308
  48.3 2.5 %copy-start.5 = (f32[1,8,32,128]{3,2,1,0:T(8,128)S(1)}, f32[1,8,32,128]{3,2,1,0:T(8,128)}, u32[]{:S(2)}) copy-start(f32[1,8,32,128]{3,2,1,0:T(8,128)} %param.15) | copy-start | bytes 393220
  51.6 8.8 %collective-permute-start.10 = (f32[1]{0:T(128)}, f32[1]{0:T(128)}, u32[]{:S(2)}, u32[]{:S(2)}) collective-permute-start(f32[1]{0:T(128)} %bitcast.31), channel_id=1, source_target_pairs={{0,2},{1,3},{2,0},{3,1},{4,6},{5,7},{6,4},{7,5},{8,10},{9,11},{10,... | collective-permute-start | bytes 20 | tf_op jit(solution)/shard_map/ppermute | solution.py:36
  54.6 6.3 %collective-permute-start.8 = (f32[1,7,32,128]{3,2,1,0:T(8,128)S(1)}, f32[1,7,32,128]{3,2,1,0:T(8,128)S(1)}, u32[]{:S(2)}, u32[]{:S(2)}) collective-permute-start(f32[1,7,32,128]{3,2,1,0:T(8,128)S(1)} %get-tuple-element.77), channel_id=1, source_target_pairs={{0,1},{1,2},{2,3},{3,4},{4,5},{5,6},{6,7},{7,8},{8,9},{9,10},{10,1... | collective-permute-start | bytes 344072 | tf_op jit(solution)/shard_map/ppermute | solution.py:18
  56.5 6.1 %collective-permute-start.9 = (f32[1,7,32,128]{3,2,1,0:T(8,128)S(1)}, f32[1,7,32,128]{3,2,1,0:T(8,128)S(1)}, u32[]{:S(2)}, u32[]{:S(2)}) collective-permute-start(f32[1,7,32,128]{3,2,1,0:T(8,128)S(1)} %get-tuple-element.78), channel_id=1, source_target_pairs={{1,0},{2,1},{3,2},{4,3},{5,4},{6,5},{7,6},{8,7},{9,8},{10,9},{11,1... | collective-permute-start | bytes 344072 | tf_op jit(solution)/shard_map/ppermute | solution.py:19
  63.5 7.9 %collective-permute-start.13 = (f32[1]{0:T(128)}, f32[1]{0:T(128)}, u32[]{:S(2)}, u32[]{:S(2)}) collective-permute-start(f32[1]{0:T(128)} %add.718), channel_id=1, source_target_pairs={{0,4},{1,5},{2,6},{3,7},{4,0},{5,1},{6,2},{7,3},{8,12},{9,13},{10,... | collective-permute-start | bytes 20 | tf_op jit(solution)/shard_map/ppermute | solution.py:36
  65.6 6.4 %collective-permute-start.11 = (f32[1,7,32,128]{3,2,1,0:T(8,128)S(1)}, f32[1,7,32,128]{3,2,1,0:T(8,128)S(1)}, u32[]{:S(2)}, u32[]{:S(2)}) collective-permute-start(f32[1,7,32,128]{3,2,1,0:T(8,128)S(1)} %get-tuple-element.75), channel_id=1, source_target_pairs={{0,1},{1,2},{2,3},{3,4},{4,5},{5,6},{6,7},{7,8},{8,9},{9,10},{10,1... | collective-permute-start | bytes 344072 | tf_op jit(solution)/shard_map/ppermute | solution.py:18
  68.3 6.1 %collective-permute-start.12 = (f32[1,7,32,128]{3,2,1,0:T(8,128)S(1)}, f32[1,7,32,128]{3,2,1,0:T(8,128)S(1)}, u32[]{:S(2)}, u32[]{:S(2)}) collective-permute-start(f32[1,7,32,128]{3,2,1,0:T(8,128)S(1)} %get-tuple-element.76), channel_id=1, source_target_pairs={{1,0},{2,1},{3,2},{4,3},{5,4},{6,5},{7,6},{8,7},{9,8},{10,9},{11,1... | collective-permute-start | bytes 344072 | tf_op jit(solution)/shard_map/ppermute | solution.py:19
  74.6 12.4 %copy-start.3 = (f32[1,8,32,128]{3,2,1,0:T(8,128)}, f32[1,8,32,128]{3,2,1,0:T(8,128)S(1)}, u32[]{:S(2)}) copy-start(f32[1,8,32,128]{3,2,1,0:T(8,128)S(1)} %fusion.482) | copy-start | bytes 393220
  75.3 8.6 %collective-permute-start.16 = (f32[1]{0:T(128)}, f32[1]{0:T(128)}, u32[]{:S(2)}, u32[]{:S(2)}) collective-permute-start(f32[1]{0:T(128)} %add.742), channel_id=1, source_target_pairs={{0,8},{1,9},{2,10},{3,11},{4,12},{5,13},{6,14},{7,15},{8,0},{9,1},... | collective-permute-start | bytes 20 | tf_op jit(solution)/shard_map/ppermute | solution.py:36
  78.1 8.3 %collective-permute-start.14 = (f32[1,7,32,128]{3,2,1,0:T(8,128)S(1)}, f32[1,7,32,128]{3,2,1,0:T(8,128)S(1)}, u32[]{:S(2)}, u32[]{:S(2)}) collective-permute-start(f32[1,7,32,128]{3,2,1,0:T(8,128)S(1)} %get-tuple-element.73), channel_id=1, source_target_pairs={{0,1},{1,2},{2,3},{3,4},{4,5},{5,6},{6,7},{7,8},{8,9},{9,10},{10,1... | collective-permute-start | bytes 344072 | tf_op jit(solution)/shard_map/ppermute | solution.py:18
  80.8 6.1 %collective-permute-start.15 = (f32[1,7,32,128]{3,2,1,0:T(8,128)S(1)}, f32[1,7,32,128]{3,2,1,0:T(8,128)S(1)}, u32[]{:S(2)}, u32[]{:S(2)}) collective-permute-start(f32[1,7,32,128]{3,2,1,0:T(8,128)S(1)} %get-tuple-element.74), channel_id=1, source_target_pairs={{1,0},{2,1},{3,2},{4,3},{5,4},{6,5},{7,6},{8,7},{9,8},{10,9},{11,1... | collective-permute-start | bytes 344072 | tf_op jit(solution)/shard_map/ppermute | solution.py:19
  84.5 1.3 %collective-permute-start.17 = (f32[1]{0:T(128)}, f32[1]{0:T(128)}, u32[]{:S(2)}, u32[]{:S(2)}) collective-permute-start(f32[1]{0:T(128)} %add.766), channel_id=1, source_target_pairs={{0,1},{1,0},{2,3},{3,2},{4,5},{5,4},{6,7},{7,6},{8,9},{9,8},{10,11... | collective-permute-start | bytes 20 | tf_op jit(solution)/shard_map/ppermute | solution.py:36

commit v23 on v19

--- a/solution.py
+++ b/solution.py
@@ -144,12 +144,14 @@
         if step == 0:
             lap = first_lap
         elif step == 1:
-            both, scale = operator(jnp.concatenate([current, adjoint_operand], axis=0), 2.0 * velocity / buoyancy)
+            both, (scale, base) = operator(
+                jnp.concatenate([current, adjoint_operand], axis=0), (2.0 * velocity / buoyancy, 2.0 * current - before)
+            )
             lap, adjoint_lap = both[:shots], both[shots:]
         else:
-            lap = operator(current)
+            lap, base = operator(current, 2.0 * current - before)
         laps.append(lap)
-        following = (first_base if step == 0 else 2.0 * current - before) + kappa * lap
+        following = (first_base if step == 0 else base) + kappa * lap
         amount = wavelet[:, step].reshape(shots, 1, 1, 1)
         following = following + jnp.where(source_hit, amount, 0.0)
         sampled = sample(following)

time: 89.6 us -> 89.8 us (level)
    sub x0 -> x3, other arithmetic: none -> 2.3 us  [the longest x2 1.51 us: local(): lap, base = operator(current, 2.0 * current - before)]
    add x4 -> x1, other arithmetic: 3.03 us -> 0.74 us  [local(): following = following + jnp.where(source_hit, amount, 0.0)]
where the time goes in v23:
time: 89.8 us; the launch traced here: 88.2 us
  starting transfers between devices  42.1 us (47%)
  waiting for transfers between devices  15.2 us (17%)
  other arithmetic  12.2 us (14%)
  matrix products  11.4 us (13%)
  between operations  6.48 us (7%)
    ppermute x7, starting transfers between devices, extended(): before = lax.ppermute(last, 'mp', up)  17.7 us
    ppermute x7, starting transfers between devices, extended(): after = lax.ppermute(first, 'mp', down)  15.6 us
    ppermute x7, waiting for transfers between devices, extended(): after = lax.ppermute(first, 'mp', down)  14.9 us
    ppermute x4, starting transfers between devices, butterfly_round(): return values + lax.ppermute(values, axis, pairs)  8.83 us
    dot_general x4, matrix products, sample(): jnp.einsum('srk,skz->srz', row_pick, field.reshape(shots, rows, cz), prec...  6.43 us
    dot_general x4, matrix products, injected(): jnp.einsum('srk,srz->skz', row_pick, spread, precision=lax.Precision.HIGH...  4.93 us
    mul x7, other arithmetic, cross_terms(): flux = buoyancy * forward_diff(pad_axis(values, axis), axis, length)  2.4 us
    add x7, other arithmetic, cross_terms(): total = total + backward_diff(pad_axis(flux, axis), axis, length)  2.39 us
  transfers between devices with their start and end apart: 18, of which 8 were waited for; matrix products, arithmetic and copies ran while one was open for 14% of the time, Pallas kernels for 0%

profile of v23, /device:TPU:1, one launch (start us, length us, event | category | flops | bytes accessed | tf_op | source)
XLA Modules:
  0.0 88.2 jit_solution(11095655776404228201)
XLA Ops:
  0.7 1.1 %pad_maximum_fusion.12 = (f32[2,7,32,128]{3,2,1,0:T(8,128)S(1)}, f32[2,7,32,128]{3,2,1,0:T(8,128)S(1)}) fusion(f32[1,8,32,128]{3,2,1,0:T(8,128)} %param.13, f32[1,8,32,128]{3,2,1,0:T(8,128)} %bitcast.124), kind=kLoop, calls=%fused_computation.331 | loop fusion | flops 114688 | bytes 720896 | tf_op jit(solution)/shard_map/concatenate | solution.py:99
  1.9 4.7 %collective-permute-start = (f32[2,7,32,128]{3,2,1,0:T(8,128)S(1)}, f32[2,7,32,128]{3,2,1,0:T(8,128)S(1)}, u32[]{:S(2)}, u32[]{:S(2)}) collective-permute-start(f32[2,7,32,128]{3,2,1,0:T(8,128)S(1)} %get-tuple-element.78), channel_id=1, source_target_pairs={{0,1},{1,2},{2,3},{3,4},{4,5},{5,6},{6,7},{7,8},{8,9},{9,10},{10,1... | collective-permute-start | bytes 688136 | tf_op jit(solution)/shard_map/ppermute | solution.py:18
  6.5 1.9 %collective-permute-start.1 = (f32[2,7,32,128]{3,2,1,0:T(8,128)S(1)}, f32[2,7,32,128]{3,2,1,0:T(8,128)S(1)}, u32[]{:S(2)}, u32[]{:S(2)}) collective-permute-start(f32[2,7,32,128]{3,2,1,0:T(8,128)S(1)} %get-tuple-element.77), channel_id=1, source_target_pairs={{1,0},{2,1},{3,2},{4,3},{5,4},{6,5},{7,6},{8,7},{9,8},{10,9},{11,1... | collective-permute-start | bytes 688136 | tf_op jit(solution)/shard_map/ppermute | solution.py:19
  8.5 0.3 fusion.333
  8.8 0.3 fusion.201
  9.8 0.6 fusion.555
  10.6 3.3 %collective-permute-done.1 = f32[2,7,32,128]{3,2,1,0:T(8,128)S(1)} collective-permute-done((f32[2,7,32,128]{3,2,1,0:T(8,128)S(1)}, f32[2,7,32,128]{3,2,1,0:T(8,128)S(1)}, u32[]{:S(2)}, u32[]{:S(2)}) %collective-permute-start.1) | collective-permute-done | bytes 229408 | tf_op jit(solution)/shard_map/ppermute | solution.py:19
  13.9 0.1 slice_bitcast_fusion
  14.1 0.8 multiply_subtract_fusion.2
  14.9 0.1 copy-done.2
  15.1 1.9 %collective-permute-start.2 = (f32[2,7,32,128]{3,2,1,0:T(8,128)S(1)}, f32[2,7,32,128]{3,2,1,0:T(8,128)S(1)}, u32[]{:S(2)}, u32[]{:S(2)}) collective-permute-start(f32[2,7,32,128]{3,2,1,0:T(8,128)S(1)} %get-tuple-element.75), channel_id=1, source_target_pairs={{0,1},{1,2},{2,3},{3,4},{4,5},{5,6},{6,7},{7,8},{8,9},{9,10},{10,1... | collective-permute-start | bytes 688136 | tf_op jit(solution)/shard_map/ppermute | solution.py:18
  17.0 2.4 %collective-permute-start.3 = (f32[2,7,32,128]{3,2,1,0:T(8,128)S(1)}, f32[2,7,32,128]{3,2,1,0:T(8,128)S(1)}, u32[]{:S(2)}, u32[]{:S(2)}) collective-permute-start(f32[2,7,32,128]{3,2,1,0:T(8,128)S(1)} %get-tuple-element.76), channel_id=1, source_target_pairs={{1,0},{2,1},{3,2},{4,3},{5,4},{6,5},{7,6},{8,7},{9,8},{10,9},{11,1... | collective-permute-start | bytes 688136 | tf_op jit(solution)/shard_map/ppermute | solution.py:19
  19.4 0.5 fusion.106
  20.0 0.5 fusion.94
  20.5 1.6 %fusion.16 = f32[2048]{0:T(1024)S(1)} fusion(f32[256,128]{1,0:T(8,128)S(1)} %bitcast.128, s32[2048]{0:T(1024)S(1)} %bitcast.147, s32[2048]{0:T(1024)S(1)} %bitcast.139), kind=kOutput, calls=%fused_computation.15 | convolution fusion | flops 806615040 | bytes 155648 | tf_op jit(solution)/shard_map/srk,skz->srz/dot_general | solution.py:130
  22.1 3.0 %collective-permute-done.3 = f32[2,7,32,128]{3,2,1,0:T(8,128)S(1)} collective-permute-done((f32[2,7,32,128]{3,2,1,0:T(8,128)S(1)}, f32[2,7,32,128]{3,2,1,0:T(8,128)S(1)}, u32[]{:S(2)}, u32[]{:S(2)}) %collective-permute-start.3) | collective-permute-done | bytes 229408 | tf_op jit(solution)/shard_map/ppermute | solution.py:19
  25.2 0.2 fusion.72
  25.4 0.1 fusion.126
  25.5 0.8 multiply_subtract_fusion.1
  26.3 0.3 fusion.356
  26.6 1.9 %collective-permute-start.4 = (f32[1,7,32,128]{3,2,1,0:T(8,128)S(1)}, f32[1,7,32,128]{3,2,1,0:T(8,128)S(1)}, u32[]{:S(2)}, u32[]{:S(2)}) collective-permute-start(f32[1,7,32,128]{3,2,1,0:T(8,128)S(1)} %get-tuple-element.89), channel_id=1, source_target_pairs={{0,1},{1,2},{2,3},{3,4},{4,5},{5,6},{6,7},{7,8},{8,9},{9,10},{10,1... | collective-permute-start | bytes 344072 | tf_op jit(solution)/shard_map/ppermute | solution.py:18
  28.5 2.4 %collective-permute-start.5 = (f32[1,7,32,128]{3,2,1,0:T(8,128)S(1)}, f32[1,7,32,128]{3,2,1,0:T(8,128)S(1)}, u32[]{:S(2)}, u32[]{:S(2)}) collective-permute-start(f32[1,7,32,128]{3,2,1,0:T(8,128)S(1)} %get-tuple-element.90), channel_id=1, source_target_pairs={{1,0},{2,1},{3,2},{4,3},{5,4},{6,5},{7,6},{8,7},{9,8},{10,9},{11,1... | collective-permute-start | bytes 344072 | tf_op jit(solution)/shard_map/ppermute | solution.py:19
  31.0 0.3 fusion.225
  31.3 1.6 %fusion.19 = f32[2048]{0:T(1024)S(1)} fusion(f32[256,128]{1,0:T(8,128)S(1)} %bitcast.127, s32[2048]{0:T(1024)S(1)} %bitcast.148, s32[2048]{0:T(1024)S(1)} %bitcast.140), kind=kOutput, calls=%fused_computation.16 | convolution fusion | flops 806615040 | bytes 155648 | tf_op jit(solution)/shard_map/srk,skz->srz/dot_general | solution.py:130
  32.9 2.7 %collective-permute-done.5 = f32[1,7,32,128]{3,2,1,0:T(8,128)S(1)} collective-permute-done((f32[1,7,32,128]{3,2,1,0:T(8,128)S(1)}, f32[1,7,32,128]{3,2,1,0:T(8,128)S(1)}, u32[]{:S(2)}, u32[]{:S(2)}) %collective-permute-start.5) | collective-permute-done | bytes 114720 | tf_op jit(solution)/shard_map/ppermute | solution.py:19
  35.6 0.1 fusion.163
  35.7 0.8 multiply_subtract_fusion
  36.5 0.3 fusion.379
  36.8 1.9 %collective-permute-start.6 = (f32[1,7,32,128]{3,2,1,0:T(8,128)S(1)}, f32[1,7,32,128]{3,2,1,0:T(8,128)S(1)}, u32[]{:S(2)}, u32[]{:S(2)}) collective-permute-start(f32[1,7,32,128]{3,2,1,0:T(8,128)S(1)} %get-tuple-element.87), channel_id=1, source_target_pairs={{0,1},{1,2},{2,3},{3,4},{4,5},{5,6},{6,7},{7,8},{8,9},{9,10},{10,1... | collective-permute-start | bytes 344072 | tf_op jit(solution)/shard_map/ppermute | solution.py:18
  38.7 2.4 %collective-permute-start.7 = (f32[1,7,32,128]{3,2,1,0:T(8,128)S(1)}, f32[1,7,32,128]{3,2,1,0:T(8,128)S(1)}, u32[]{:S(2)}, u32[]{:S(2)}) collective-permute-start(f32[1,7,32,128]{3,2,1,0:T(8,128)S(1)} %get-tuple-element.88), channel_id=1, source_target_pairs={{1,0},{2,1},{3,2},{4,3},{5,4},{6,5},{7,6},{8,7},{9,8},{10,9},{11,1... | collective-permute-start | bytes 344072 | tf_op jit(solution)/shard_map/ppermute | solution.py:19
  41.1 0.3 fusion.249
  41.4 1.6 %fusion.22 = f32[2048]{0:T(1024)S(1)} fusion(f32[256,128]{1,0:T(8,128)S(1)} %bitcast.129, s32[2048]{0:T(1024)S(1)} %bitcast.149, s32[2048]{0:T(1024)S(1)} %bitcast.141), kind=kOutput, calls=%fused_computation.17 | convolution fusion | flops 806615040 | bytes 155648 | tf_op jit(solution)/shard_map/srk,skz->srz/dot_general | solution.py:130
  43.1 2.7 %collective-permute-done.7 = f32[1,7,32,128]{3,2,1,0:T(8,128)S(1)} collective-permute-done((f32[1,7,32,128]{3,2,1,0:T(8,128)S(1)}, f32[1,7,32,128]{3,2,1,0:T(8,128)S(1)}, u32[]{:S(2)}, u32[]{:S(2)}) %collective-permute-start.7) | collective-permute-done | bytes 114720 | tf_op jit(solution)/shard_map/ppermute | solution.py:19
  45.8 0.1 fusion.156
  45.9 0.7 fusion.532
  46.6 1.6 %fusion.13 = f32[2048]{0:T(1024)S(1)} fusion(f32[256,128]{1,0:T(8,128)S(1)} %bitcast.130, s32[2048]{0:T(1024)S(1)} %bitcast.150, s32[2048]{0:T(1024)S(1)} %bitcast.142), kind=kOutput, calls=%fused_computation.14 | convolution fusion | flops 806615040 | bytes 155648 | tf_op jit(solution)/shard_map/srk,skz->srz/dot_general | solution.py:130
  48.3 1.2 %fusion.25 = f32[1,8,32,128]{3,2,1,0:T(8,128)S(1)} fusion(s32[8,32]{1,0:T(8,128)S(1)} %multiply_add_fusion, s32[2048]{0:T(1024)S(1)} %bitcast.151, f32[2048]{0:T(1024)S(1)} %bitcast.137, s32[2048]{0:T(1024)S(1)} %bitcast.143), kind=kOutput, calls=%fused_computation.18 | convolution fusion | flops 806354944 | bytes 156672 | tf_op jit(solution)/shard_map/srk,srz->skz/dot_general | solution.py:137
  49.6 0.6 fusion.533
  51.0 0.3 fusion.402
  51.3 3.0 %collective-permute-start.10 = (f32[1]{0:T(128)}, f32[1]{0:T(128)}, u32[]{:S(2)}, u32[]{:S(2)}) collective-permute-start(f32[1]{0:T(128)} %bitcast.31), channel_id=1, source_target_pairs={{0,2},{1,3},{2,0},{3,1},{4,6},{5,7},{6,4},{7,5},{8,10},{9,11},{10,... | collective-permute-start | bytes 20 | tf_op jit(solution)/shard_map/ppermute | solution.py:36
  54.3 1.9 %collective-permute-start.8 = (f32[1,7,32,128]{3,2,1,0:T(8,128)S(1)}, f32[1,7,32,128]{3,2,1,0:T(8,128)S(1)}, u32[]{:S(2)}, u32[]{:S(2)}) collective-permute-start(f32[1,7,32,128]{3,2,1,0:T(8,128)S(1)} %get-tuple-element.85), channel_id=1, source_target_pairs={{0,1},{1,2},{2,3},{3,4},{4,5},{5,6},{6,7},{7,8},{8,9},{9,10},{10,1... | collective-permute-start | bytes 344072 | tf_op jit(solution)/shard_map/ppermute | solution.py:18
  56.2 2.6 %collective-permute-start.9 = (f32[1,7,32,128]{3,2,1,0:T(8,128)S(1)}, f32[1,7,32,128]{3,2,1,0:T(8,128)S(1)}, u32[]{:S(2)}, u32[]{:S(2)}) collective-permute-start(f32[1,7,32,128]{3,2,1,0:T(8,128)S(1)} %get-tuple-element.86), channel_id=1, source_target_pairs={{1,0},{2,1},{3,2},{4,3},{5,4},{6,5},{7,6},{8,7},{9,8},{10,9},{11,1... | collective-permute-start | bytes 344072 | tf_op jit(solution)/shard_map/ppermute | solution.py:19
  58.8 0.3 fusion.273
  59.1 1.2 %fusion.28 = f32[1,8,32,128]{3,2,1,0:T(8,128)S(1)} fusion(s32[8,32]{1,0:T(8,128)S(1)} %multiply_add_fusion, s32[2048]{0:T(1024)S(1)} %bitcast.152, f32[2048]{0:T(1024)S(1)} %bitcast.136, s32[2048]{0:T(1024)S(1)} %bitcast.144), kind=kOutput, calls=%fused_computation.19 | convolution fusion | flops 806354944 | bytes 156672 | tf_op jit(solution)/shard_map/srk,srz->skz/dot_general | solution.py:137
  61.1 1.3 %collective-permute-done.9 = f32[1,7,32,128]{3,2,1,0:T(8,128)S(1)} collective-permute-done((f32[1,7,32,128]{3,2,1,0:T(8,128)S(1)}, f32[1,7,32,128]{3,2,1,0:T(8,128)S(1)}, u32[]{:S(2)}, u32[]{:S(2)}) %collective-permute-start.9) | collective-permute-done | bytes 114720 | tf_op jit(solution)/shard_map/ppermute | solution.py:19
  62.4 0.1 fusion.149
  62.6 0.3 fusion.425
  62.9 2.1 %collective-permute-start.13 = (f32[1]{0:T(128)}, f32[1]{0:T(128)}, u32[]{:S(2)}, u32[]{:S(2)}) collective-permute-start(f32[1]{0:T(128)} %add.718), channel_id=1, source_target_pairs={{0,4},{1,5},{2,6},{3,7},{4,0},{5,1},{6,2},{7,3},{8,12},{9,13},{10,... | collective-permute-start | bytes 20 | tf_op jit(solution)/shard_map/ppermute | solution.py:36
  65.0 2.7 %collective-permute-start.11 = (f32[1,7,32,128]{3,2,1,0:T(8,128)S(1)}, f32[1,7,32,128]{3,2,1,0:T(8,128)S(1)}, u32[]{:S(2)}, u32[]{:S(2)}) collective-permute-start(f32[1,7,32,128]{3,2,1,0:T(8,128)S(1)} %get-tuple-element.83), channel_id=1, source_target_pairs={{0,1},{1,2},{2,3},{3,4},{4,5},{5,6},{6,7},{7,8},{8,9},{9,10},{10,1... | collective-permute-start | bytes 344072 | tf_op jit(solution)/shard_map/ppermute | solution.py:18
  67.8 1.9 %collective-permute-start.12 = (f32[1,7,32,128]{3,2,1,0:T(8,128)S(1)}, f32[1,7,32,128]{3,2,1,0:T(8,128)S(1)}, u32[]{:S(2)}, u32[]{:S(2)}) collective-permute-start(f32[1,7,32,128]{3,2,1,0:T(8,128)S(1)} %get-tuple-element.84), channel_id=1, source_target_pairs={{1,0},{2,1},{3,2},{4,3},{5,4},{6,5},{7,6},{8,7},{9,8},{10,9},{11,1... | collective-permute-start | bytes 344072 | tf_op jit(solution)/shard_map/ppermute | solution.py:19
  69.7 0.3 fusion.297
  70.0 1.2 %fusion.31 = f32[1,8,32,128]{3,2,1,0:T(8,128)S(1)} fusion(s32[8,32]{1,0:T(8,128)S(1)} %multiply_add_fusion, s32[2048]{0:T(1024)S(1)} %bitcast.153, f32[2048]{0:T(1024)S(1)} %bitcast.134, s32[2048]{0:T(1024)S(1)} %bitcast.145), kind=kOutput, calls=%fused_computation.20 | convolution fusion | flops 806354944 | bytes 156672 | tf_op jit(solution)/shard_map/srk,srz->skz/dot_general | solution.py:137
  71.9 1.9 %collective-permute-done.12 = f32[1,7,32,128]{3,2,1,0:T(8,128)S(1)} collective-permute-done((f32[1,7,32,128]{3,2,1,0:T(8,128)S(1)}, f32[1,7,32,128]{3,2,1,0:T(8,128)S(1)}, u32[]{:S(2)}, u32[]{:S(2)}) %collective-permute-start.12) | collective-permute-done | bytes 114720 | tf_op jit(solution)/shard_map/ppermute | solution.py:19
  73.9 0.1 fusion.142
  74.2 0.3 fusion.448
  74.5 2.8 %collective-permute-start.16 = (f32[1]{0:T(128)}, f32[1]{0:T(128)}, u32[]{:S(2)}, u32[]{:S(2)}) collective-permute-start(f32[1]{0:T(128)} %add.742), channel_id=1, source_target_pairs={{0,8},{1,9},{2,10},{3,11},{4,12},{5,13},{6,14},{7,15},{8,0},{9,1},... | collective-permute-start | bytes 20 | tf_op jit(solution)/shard_map/ppermute | solution.py:36
  77.3 2.6 %collective-permute-start.14 = (f32[1,7,32,128]{3,2,1,0:T(8,128)S(1)}, f32[1,7,32,128]{3,2,1,0:T(8,128)S(1)}, u32[]{:S(2)}, u32[]{:S(2)}) collective-permute-start(f32[1,7,32,128]{3,2,1,0:T(8,128)S(1)} %get-tuple-element.81), channel_id=1, source_target_pairs={{0,1},{1,2},{2,3},{3,4},{4,5},{5,6},{6,7},{7,8},{8,9},{9,10},{10,1... | collective-permute-start | bytes 344072 | tf_op jit(solution)/shard_map/ppermute | solution.py:18
  80.0 1.9 %collective-permute-start.15 = (f32[1,7,32,128]{3,2,1,0:T(8,128)S(1)}, f32[1,7,32,128]{3,2,1,0:T(8,128)S(1)}, u32[]{:S(2)}, u32[]{:S(2)}) collective-permute-start(f32[1,7,32,128]{3,2,1,0:T(8,128)S(1)} %get-tuple-element.82), channel_id=1, source_target_pairs={{1,0},{2,1},{3,2},{4,3},{5,4},{6,5},{7,6},{8,7},{9,8},{10,9},{11,1... | collective-permute-start | bytes 344072 | tf_op jit(solution)/shard_map/ppermute | solution.py:19
  81.9 0.3 fusion.321
  82.2 1.2 %fusion.34 = f32[1,8,32,128]{3,2,1,0:T(8,128)S(1)} fusion(s32[8,32]{1,0:T(8,128)S(1)} %multiply_add_fusion, s32[2048]{0:T(1024)S(1)} %bitcast.154, f32[2048]{0:T(1024)S(1)} %bitcast.132, s32[2048]{0:T(1024)S(1)} %bitcast.146), kind=kOutput, calls=%fused_computation.21 | convolution fusion | flops 806354944 | bytes 156672 | tf_op jit(solution)/shard_map/srk,srz->skz/dot_general | solution.py:137
  84.1 0.9 %collective-permute-start.17 = (f32[1]{0:T(128)}, f32[1]{0:T(128)}, u32[]{:S(2)}, u32[]{:S(2)}) collective-permute-start(f32[1]{0:T(128)} %add.766), channel_id=1, source_target_pairs={{0,1},{1,0},{2,3},{3,2},{4,5},{5,4},{6,7},{7,6},{8,9},{9,8},{10,11... | collective-permute-start | bytes 20 | tf_op jit(solution)/shard_map/ppermute | solution.py:36
  85.0 0.3 collective-permute-done.17
  86.1 0.1 fusion.135
  86.2 0.9 bitcast_multiply_fusion
  (58 shorter events, 1.0 us)
Async XLA Ops:
  0.6 7.9 %copy-start = (f32[8,32,128]{2,1,0:T(8,128)S(1)}, f32[8,32,128]{2,1,0:T(8,128)}, u32[]{:S(2)}) copy-start(f32[8,32,128]{2,1,0:T(8,128)} %param.11) | copy-start | bytes 393220
  0.6 7.9 %copy-start.1 = (f32[1,8,32,128]{3,2,1,0:T(8,128)S(1)}, f32[1,8,32,128]{3,2,1,0:T(8,128)}, u32[]{:S(2)}) copy-start(f32[1,8,32,128]{3,2,1,0:T(8,128)} %param.13) | copy-start | bytes 393220
  0.7 7.9 %copy-start.6 = (f32[1,8,32,128]{3,2,1,0:T(8,128)S(1)}, f32[1,8,32,128]{3,2,1,0:T(8,128)}, u32[]{:S(2)}) copy-start(f32[1,8,32,128]{3,2,1,0:T(8,128)} %param.12) | copy-start | bytes 393220
  1.8 8.0 %copy-start.9 = (f32[1,4]{1,0:T(1,128)S(1)}, f32[1,4]{1,0:T(1,128)}, u32[]{:S(2)}) copy-start(f32[1,4]{1,0:T(1,128)} %param.17) | copy-start | bytes 52
  1.8 8.6 %copy-start.7 = (s32[1,2048]{1,0:T(1,128)S(1)}, s32[1,2048]{1,0:T(1,128)}, u32[]{:S(2)}) copy-start(s32[1,2048]{1,0:T(1,128)} %param.18) | copy-start | bytes 24580
  1.8 8.7 %copy-start.4 = (f32[8,32,128]{2,1,0:T(8,128)S(1)}, f32[8,32,128]{2,1,0:T(8,128)}, u32[]{:S(2)}) copy-start(f32[8,32,128]{2,1,0:T(8,128)} %param.10) | copy-start | bytes 393220
  1.9 8.7 %collective-permute-start = (f32[2,7,32,128]{3,2,1,0:T(8,128)S(1)}, f32[2,7,32,128]{3,2,1,0:T(8,128)S(1)}, u32[]{:S(2)}, u32[]{:S(2)}) collective-permute-start(f32[2,7,32,128]{3,2,1,0:T(8,128)S(1)} %get-tuple-element.78), channel_id=1, source_target_pairs={{0,1},{1,2},{2,3},{3,4},{4,5},{5,6},{6,7},{7,8},{8,9},{9,10},{10,1... | collective-permute-start | bytes 688136 | tf_op jit(solution)/shard_map/ppermute | solution.py:18
  6.5 7.3 %collective-permute-start.1 = (f32[2,7,32,128]{3,2,1,0:T(8,128)S(1)}, f32[2,7,32,128]{3,2,1,0:T(8,128)S(1)}, u32[]{:S(2)}, u32[]{:S(2)}) collective-permute-start(f32[2,7,32,128]{3,2,1,0:T(8,128)S(1)} %get-tuple-element.77), channel_id=1, source_target_pairs={{1,0},{2,1},{3,2},{4,3},{5,4},{6,5},{7,6},{8,7},{9,8},{10,9},{11,1... | collective-permute-start | bytes 688136 | tf_op jit(solution)/shard_map/ppermute | solution.py:19
  14.0 0.9 %copy-start.2 = (f32[1,8,32,128]{3,2,1,0:T(8,128)S(1)}, f32[1,8,32,128]{3,2,1,0:T(8,128)}, u32[]{:S(2)}) copy-start(f32[1,8,32,128]{3,2,1,0:T(8,128)} %param.14) | copy-start | bytes 393220
  15.1 7.1 %collective-permute-start.2 = (f32[2,7,32,128]{3,2,1,0:T(8,128)S(1)}, f32[2,7,32,128]{3,2,1,0:T(8,128)S(1)}, u32[]{:S(2)}, u32[]{:S(2)}) collective-permute-start(f32[2,7,32,128]{3,2,1,0:T(8,128)S(1)} %get-tuple-element.75), channel_id=1, source_target_pairs={{0,1},{1,2},{2,3},{3,4},{4,5},{5,6},{6,7},{7,8},{8,9},{9,10},{10,1... | collective-permute-start | bytes 688136 | tf_op jit(solution)/shard_map/ppermute | solution.py:18
  17.0 8.1 %collective-permute-start.3 = (f32[2,7,32,128]{3,2,1,0:T(8,128)S(1)}, f32[2,7,32,128]{3,2,1,0:T(8,128)S(1)}, u32[]{:S(2)}, u32[]{:S(2)}) collective-permute-start(f32[2,7,32,128]{3,2,1,0:T(8,128)S(1)} %get-tuple-element.76), channel_id=1, source_target_pairs={{1,0},{2,1},{3,2},{4,3},{5,4},{6,5},{7,6},{8,7},{9,8},{10,9},{11,1... | collective-permute-start | bytes 688136 | tf_op jit(solution)/shard_map/ppermute | solution.py:19
  26.6 6.3 %collective-permute-start.4 = (f32[1,7,32,128]{3,2,1,0:T(8,128)S(1)}, f32[1,7,32,128]{3,2,1,0:T(8,128)S(1)}, u32[]{:S(2)}, u32[]{:S(2)}) collective-permute-start(f32[1,7,32,128]{3,2,1,0:T(8,128)S(1)} %get-tuple-element.89), channel_id=1, source_target_pairs={{0,1},{1,2},{2,3},{3,4},{4,5},{5,6},{6,7},{7,8},{8,9},{9,10},{10,1... | collective-permute-start | bytes 344072 | tf_op jit(solution)/shard_map/ppermute | solution.py:18
  28.5 7.0 %collective-permute-start.5 = (f32[1,7,32,128]{3,2,1,0:T(8,128)S(1)}, f32[1,7,32,128]{3,2,1,0:T(8,128)S(1)}, u32[]{:S(2)}, u32[]{:S(2)}) collective-permute-start(f32[1,7,32,128]{3,2,1,0:T(8,128)S(1)} %get-tuple-element.90), channel_id=1, source_target_pairs={{1,0},{2,1},{3,2},{4,3},{5,4},{6,5},{7,6},{8,7},{9,8},{10,9},{11,1... | collective-permute-start | bytes 344072 | tf_op jit(solution)/shard_map/ppermute | solution.py:19
  36.8 6.3 %collective-permute-start.6 = (f32[1,7,32,128]{3,2,1,0:T(8,128)S(1)}, f32[1,7,32,128]{3,2,1,0:T(8,128)S(1)}, u32[]{:S(2)}, u32[]{:S(2)}) collective-permute-start(f32[1,7,32,128]{3,2,1,0:T(8,128)S(1)} %get-tuple-element.87), channel_id=1, source_target_pairs={{0,1},{1,2},{2,3},{3,4},{4,5},{5,6},{6,7},{7,8},{8,9},{9,10},{10,1... | collective-permute-start | bytes 344072 | tf_op jit(solution)/shard_map/ppermute | solution.py:18
  38.7 7.0 %collective-permute-start.7 = (f32[1,7,32,128]{3,2,1,0:T(8,128)S(1)}, f32[1,7,32,128]{3,2,1,0:T(8,128)S(1)}, u32[]{:S(2)}, u32[]{:S(2)}) collective-permute-start(f32[1,7,32,128]{3,2,1,0:T(8,128)S(1)} %get-tuple-element.88), channel_id=1, source_target_pairs={{1,0},{2,1},{3,2},{4,3},{5,4},{6,5},{7,6},{8,7},{9,8},{10,9},{11,1... | collective-permute-start | bytes 344072 | tf_op jit(solution)/shard_map/ppermute | solution.py:19
  46.6 1.6 %copy-start.8 = (f32[1,4,2048]{2,1,0:T(4,128)S(1)}, f32[1,4,2048]{2,1,0:T(4,128)}, u32[]{:S(2)}) copy-start(f32[1,4,2048]{2,1,0:T(4,128)} %param.19) | copy-start | bytes 98308
  48.3 2.5 %copy-start.5 = (f32[1,8,32,128]{3,2,1,0:T(8,128)S(1)}, f32[1,8,32,128]{3,2,1,0:T(8,128)}, u32[]{:S(2)}) copy-start(f32[1,8,32,128]{3,2,1,0:T(8,128)} %param.15) | copy-start | bytes 393220
  51.3 9.1 %collective-permute-start.10 = (f32[1]{0:T(128)}, f32[1]{0:T(128)}, u32[]{:S(2)}, u32[]{:S(2)}) collective-permute-start(f32[1]{0:T(128)} %bitcast.31), channel_id=1, source_target_pairs={{0,2},{1,3},{2,0},{3,1},{4,6},{5,7},{6,4},{7,5},{8,10},{9,11},{10,... | collective-permute-start | bytes 20 | tf_op jit(solution)/shard_map/ppermute | solution.py:36
  54.3 6.7 %collective-permute-start.8 = (f32[1,7,32,128]{3,2,1,0:T(8,128)S(1)}, f32[1,7,32,128]{3,2,1,0:T(8,128)S(1)}, u32[]{:S(2)}, u32[]{:S(2)}) collective-permute-start(f32[1,7,32,128]{3,2,1,0:T(8,128)S(1)} %get-tuple-element.85), channel_id=1, source_target_pairs={{0,1},{1,2},{2,3},{3,4},{4,5},{5,6},{6,7},{7,8},{8,9},{9,10},{10,1... | collective-permute-start | bytes 344072 | tf_op jit(solution)/shard_map/ppermute | solution.py:18
  56.2 6.1 %collective-permute-start.9 = (f32[1,7,32,128]{3,2,1,0:T(8,128)S(1)}, f32[1,7,32,128]{3,2,1,0:T(8,128)S(1)}, u32[]{:S(2)}, u32[]{:S(2)}) collective-permute-start(f32[1,7,32,128]{3,2,1,0:T(8,128)S(1)} %get-tuple-element.86), channel_id=1, source_target_pairs={{1,0},{2,1},{3,2},{4,3},{5,4},{6,5},{7,6},{8,7},{9,8},{10,9},{11,1... | collective-permute-start | bytes 344072 | tf_op jit(solution)/shard_map/ppermute | solution.py:19
  62.9 8.3 %collective-permute-start.13 = (f32[1]{0:T(128)}, f32[1]{0:T(128)}, u32[]{:S(2)}, u32[]{:S(2)}) collective-permute-start(f32[1]{0:T(128)} %add.718), channel_id=1, source_target_pairs={{0,4},{1,5},{2,6},{3,7},{4,0},{5,1},{6,2},{7,3},{8,12},{9,13},{10,... | collective-permute-start | bytes 20 | tf_op jit(solution)/shard_map/ppermute | solution.py:36
  65.0 6.9 %collective-permute-start.11 = (f32[1,7,32,128]{3,2,1,0:T(8,128)S(1)}, f32[1,7,32,128]{3,2,1,0:T(8,128)S(1)}, u32[]{:S(2)}, u32[]{:S(2)}) collective-permute-start(f32[1,7,32,128]{3,2,1,0:T(8,128)S(1)} %get-tuple-element.83), channel_id=1, source_target_pairs={{0,1},{1,2},{2,3},{3,4},{4,5},{5,6},{6,7},{7,8},{8,9},{9,10},{10,1... | collective-permute-start | bytes 344072 | tf_op jit(solution)/shard_map/ppermute | solution.py:18
  67.8 6.1 %collective-permute-start.12 = (f32[1,7,32,128]{3,2,1,0:T(8,128)S(1)}, f32[1,7,32,128]{3,2,1,0:T(8,128)S(1)}, u32[]{:S(2)}, u32[]{:S(2)}) collective-permute-start(f32[1,7,32,128]{3,2,1,0:T(8,128)S(1)} %get-tuple-element.84), channel_id=1, source_target_pairs={{1,0},{2,1},{3,2},{4,3},{5,4},{6,5},{7,6},{8,7},{9,8},{10,9},{11,1... | collective-permute-start | bytes 344072 | tf_op jit(solution)/shard_map/ppermute | solution.py:19
  74.1 12.1 %copy-start.3 = (f32[1,8,32,128]{3,2,1,0:T(8,128)}, f32[1,8,32,128]{3,2,1,0:T(8,128)S(1)}, u32[]{:S(2)}) copy-start(f32[1,8,32,128]{3,2,1,0:T(8,128)S(1)} %fusion.482) | copy-start | bytes 393220
  74.5 9.0 %collective-permute-start.16 = (f32[1]{0:T(128)}, f32[1]{0:T(128)}, u32[]{:S(2)}, u32[]{:S(2)}) collective-permute-start(f32[1]{0:T(128)} %add.742), channel_id=1, source_target_pairs={{0,8},{1,9},{2,10},{3,11},{4,12},{5,13},{6,14},{7,15},{8,0},{9,1},... | collective-permute-start | bytes 20 | tf_op jit(solution)/shard_map/ppermute | solution.py:36
  77.3 8.7 %collective-permute-start.14 = (f32[1,7,32,128]{3,2,1,0:T(8,128)S(1)}, f32[1,7,32,128]{3,2,1,0:T(8,128)S(1)}, u32[]{:S(2)}, u32[]{:S(2)}) collective-permute-start(f32[1,7,32,128]{3,2,1,0:T(8,128)S(1)} %get-tuple-element.81), channel_id=1, source_target_pairs={{0,1},{1,2},{2,3},{3,4},{4,5},{5,6},{6,7},{7,8},{8,9},{9,10},{10,1... | collective-permute-start | bytes 344072 | tf_op jit(solution)/shard_map/ppermute | solution.py:18
  80.0 6.1 %collective-permute-start.15 = (f32[1,7,32,128]{3,2,1,0:T(8,128)S(1)}, f32[1,7,32,128]{3,2,1,0:T(8,128)S(1)}, u32[]{:S(2)}, u32[]{:S(2)}) collective-permute-start(f32[1,7,32,128]{3,2,1,0:T(8,128)S(1)} %get-tuple-element.82), channel_id=1, source_target_pairs={{1,0},{2,1},{3,2},{4,3},{5,4},{6,5},{7,6},{8,7},{9,8},{10,9},{11,1... | collective-permute-start | bytes 344072 | tf_op jit(solution)/shard_map/ppermute | solution.py:19
  84.1 1.2 %collective-permute-start.17 = (f32[1]{0:T(128)}, f32[1]{0:T(128)}, u32[]{:S(2)}, u32[]{:S(2)}) collective-permute-start(f32[1]{0:T(128)} %add.766), channel_id=1, source_target_pairs={{0,1},{1,0},{2,3},{3,2},{4,5},{5,4},{6,7},{7,6},{8,9},{9,8},{10,11... | collective-permute-start | bytes 20 | tf_op jit(solution)/shard_map/ppermute | solution.py:36

commit v24 on v19

--- a/solution.py
+++ b/solution.py
@@ -23,12 +23,12 @@
 def butterfly_distances(axis):
     devices = lax.axis_size(axis)
     assert devices & (devices - 1) == 0
-    far = []
-    distance = 2
+    distances = []
+    distance = 1
     while distance < devices:
-        far.append(distance)
+        distances.append(distance)
         distance *= 2
-    return far + [1] if devices > 1 else []
+    return distances
 
 
 def butterfly_round(values, axis, distance):

time: 89.6 us -> 92.1 us (1.028)
  the two profiles are of different devices: /device:TPU:1 before, /device:TPU:0 now
where the time goes in v24:
time: 92.1 us; the launch traced here: 91.5 us
  starting transfers between devices  56.8 us (62%)
  other arithmetic  12.2 us (13%)
  matrix products  11.4 us (12%)
  between operations  6.07 us (7%)
  waiting for transfers between devices  4.22 us (5%)
    ppermute x7, starting transfers between devices, extended(): before = lax.ppermute(last, 'mp', up)  26.4 us
    ppermute x4, starting transfers between devices, butterfly_round(): return values + lax.ppermute(values, axis, pairs)  21.2 us
    ppermute x7, starting transfers between devices, extended(): after = lax.ppermute(first, 'mp', down)  9.23 us
    dot_general x4, matrix products, sample(): jnp.einsum('srk,skz->srz', row_pick, field.reshape(shots, rows, cz), prec...  6.43 us
    dot_general x4, matrix products, injected(): jnp.einsum('srk,srz->skz', row_pick, spread, precision=lax.Precision.HIGH...  4.93 us
    ppermute x7, waiting for transfers between devices, extended(): after = lax.ppermute(first, 'mp', down)  3.87 us
    add x4, other arithmetic, local(): following = following + jnp.where(source_hit, amount, 0.0)  3.03 us
    mul x7, other arithmetic, cross_terms(): flux = buoyancy * forward_diff(pad_axis(values, axis), axis, length)  2.4 us
  transfers between devices with their start and end apart: 18, of which 3 were waited for; matrix products, arithmetic and copies ran while one was open for 14% of the time, Pallas kernels for 0%

profile of v24, /device:TPU:0, one launch (start us, length us, event | category | flops | bytes accessed | tf_op | source)
XLA Modules:
  0.0 91.5 jit_solution(1550618083990531832)
XLA Ops:
  0.7 1.1 %pad_maximum_fusion.12 = (f32[2,7,32,128]{3,2,1,0:T(8,128)S(1)}, f32[2,7,32,128]{3,2,1,0:T(8,128)S(1)}) fusion(f32[1,8,32,128]{3,2,1,0:T(8,128)} %param.13, f32[1,8,32,128]{3,2,1,0:T(8,128)} %bitcast.121), kind=kLoop, calls=%fused_computation.331 | loop fusion | flops 114688 | bytes 720896 | tf_op jit(solution)/shard_map/concatenate | solution.py:99
  1.8 0.0 copy-start.4
  1.9 2.5 %collective-permute-start = (f32[2,7,32,128]{3,2,1,0:T(8,128)S(1)}, f32[2,7,32,128]{3,2,1,0:T(8,128)S(1)}, u32[]{:S(2)}, u32[]{:S(2)}) collective-permute-start(f32[2,7,32,128]{3,2,1,0:T(8,128)S(1)} %get-tuple-element.64), channel_id=1, source_target_pairs={{0,1},{1,2},{2,3},{3,4},{4,5},{5,6},{6,7},{7,8},{8,9},{9,10},{10,1... | collective-permute-start | bytes 688136 | tf_op jit(solution)/shard_map/ppermute | solution.py:18
  4.4 1.3 %collective-permute-start.1 = (f32[2,7,32,128]{3,2,1,0:T(8,128)S(1)}, f32[2,7,32,128]{3,2,1,0:T(8,128)S(1)}, u32[]{:S(2)}, u32[]{:S(2)}) collective-permute-start(f32[2,7,32,128]{3,2,1,0:T(8,128)S(1)} %get-tuple-element.63), channel_id=1, source_target_pairs={{1,0},{2,1},{3,2},{4,3},{5,4},{6,5},{7,6},{8,7},{9,8},{10,9},{11,1... | collective-permute-start | bytes 688136 | tf_op jit(solution)/shard_map/ppermute | solution.py:19
  5.7 0.3 fusion.333
  6.0 0.3 fusion.201
  7.0 0.6 fusion.552
  7.8 2.1 %collective-permute-done.1 = f32[2,7,32,128]{3,2,1,0:T(8,128)S(1)} collective-permute-done((f32[2,7,32,128]{3,2,1,0:T(8,128)S(1)}, f32[2,7,32,128]{3,2,1,0:T(8,128)S(1)}, u32[]{:S(2)}, u32[]{:S(2)}) %collective-permute-start.1) | collective-permute-done | bytes 229408 | tf_op jit(solution)/shard_map/ppermute | solution.py:19
  9.9 0.1 slice_bitcast_fusion
  10.1 0.8 fusion.526
  10.8 0.1 copy-done.2
  11.1 6.4 %collective-permute-start.2 = (f32[2,7,32,128]{3,2,1,0:T(8,128)S(1)}, f32[2,7,32,128]{3,2,1,0:T(8,128)S(1)}, u32[]{:S(2)}, u32[]{:S(2)}) collective-permute-start(f32[2,7,32,128]{3,2,1,0:T(8,128)S(1)} %get-tuple-element.61), channel_id=1, source_target_pairs={{0,1},{1,2},{2,3},{3,4},{4,5},{5,6},{6,7},{7,8},{8,9},{9,10},{10,1... | collective-permute-start | bytes 688136 | tf_op jit(solution)/shard_map/ppermute | solution.py:18
  17.4 1.3 %collective-permute-start.3 = (f32[2,7,32,128]{3,2,1,0:T(8,128)S(1)}, f32[2,7,32,128]{3,2,1,0:T(8,128)S(1)}, u32[]{:S(2)}, u32[]{:S(2)}) collective-permute-start(f32[2,7,32,128]{3,2,1,0:T(8,128)S(1)} %get-tuple-element.62), channel_id=1, source_target_pairs={{1,0},{2,1},{3,2},{4,3},{5,4},{6,5},{7,6},{8,7},{9,8},{10,9},{11,1... | collective-permute-start | bytes 688136 | tf_op jit(solution)/shard_map/ppermute | solution.py:19
  18.7 0.5 fusion.106
  19.3 0.5 fusion.94
  19.8 1.6 %fusion.16 = f32[2048]{0:T(1024)S(1)} fusion(f32[256,128]{1,0:T(8,128)S(1)} %bitcast.125, s32[2048]{0:T(1024)S(1)} %bitcast.144, s32[2048]{0:T(1024)S(1)} %bitcast.136), kind=kOutput, calls=%fused_computation.15 | convolution fusion | flops 806615040 | bytes 155648 | tf_op jit(solution)/shard_map/srk,skz->srz/dot_general | solution.py:130
  21.5 0.2 fusion.72
  21.7 0.1 fusion.126
  21.9 0.7 fusion.528
  22.6 0.3 fusion.356
  23.0 6.0 %collective-permute-start.4 = (f32[1,7,32,128]{3,2,1,0:T(8,128)S(1)}, f32[1,7,32,128]{3,2,1,0:T(8,128)S(1)}, u32[]{:S(2)}, u32[]{:S(2)}) collective-permute-start(f32[1,7,32,128]{3,2,1,0:T(8,128)S(1)} %get-tuple-element.75), channel_id=1, source_target_pairs={{0,1},{1,2},{2,3},{3,4},{4,5},{5,6},{6,7},{7,8},{8,9},{9,10},{10,1... | collective-permute-start | bytes 344072 | tf_op jit(solution)/shard_map/ppermute | solution.py:18
  29.0 1.3 %collective-permute-start.5 = (f32[1,7,32,128]{3,2,1,0:T(8,128)S(1)}, f32[1,7,32,128]{3,2,1,0:T(8,128)S(1)}, u32[]{:S(2)}, u32[]{:S(2)}) collective-permute-start(f32[1,7,32,128]{3,2,1,0:T(8,128)S(1)} %get-tuple-element.76), channel_id=1, source_target_pairs={{1,0},{2,1},{3,2},{4,3},{5,4},{6,5},{7,6},{8,7},{9,8},{10,9},{11,1... | collective-permute-start | bytes 344072 | tf_op jit(solution)/shard_map/ppermute | solution.py:19
  30.3 0.3 fusion.225
  30.6 1.6 %fusion.19 = f32[2048]{0:T(1024)S(1)} fusion(f32[256,128]{1,0:T(8,128)S(1)} %bitcast.124, s32[2048]{0:T(1024)S(1)} %bitcast.145, s32[2048]{0:T(1024)S(1)} %bitcast.137), kind=kOutput, calls=%fused_computation.16 | convolution fusion | flops 806615040 | bytes 155648 | tf_op jit(solution)/shard_map/srk,skz->srz/dot_general | solution.py:130
  32.2 0.1 fusion.163
  32.4 0.7 fusion.530
  33.1 0.3 fusion.379
  33.5 5.7 %collective-permute-start.6 = (f32[1,7,32,128]{3,2,1,0:T(8,128)S(1)}, f32[1,7,32,128]{3,2,1,0:T(8,128)S(1)}, u32[]{:S(2)}, u32[]{:S(2)}) collective-permute-start(f32[1,7,32,128]{3,2,1,0:T(8,128)S(1)} %get-tuple-element.73), channel_id=1, source_target_pairs={{0,1},{1,2},{2,3},{3,4},{4,5},{5,6},{6,7},{7,8},{8,9},{9,10},{10,1... | collective-permute-start | bytes 344072 | tf_op jit(solution)/shard_map/ppermute | solution.py:18
  39.1 1.3 %collective-permute-start.7 = (f32[1,7,32,128]{3,2,1,0:T(8,128)S(1)}, f32[1,7,32,128]{3,2,1,0:T(8,128)S(1)}, u32[]{:S(2)}, u32[]{:S(2)}) collective-permute-start(f32[1,7,32,128]{3,2,1,0:T(8,128)S(1)} %get-tuple-element.74), channel_id=1, source_target_pairs={{1,0},{2,1},{3,2},{4,3},{5,4},{6,5},{7,6},{8,7},{9,8},{10,9},{11,1... | collective-permute-start | bytes 344072 | tf_op jit(solution)/shard_map/ppermute | solution.py:19
  40.4 0.3 fusion.249
  40.7 1.6 %fusion.22 = f32[2048]{0:T(1024)S(1)} fusion(f32[256,128]{1,0:T(8,128)S(1)} %bitcast.126, s32[2048]{0:T(1024)S(1)} %bitcast.146, s32[2048]{0:T(1024)S(1)} %bitcast.138), kind=kOutput, calls=%fused_computation.17 | convolution fusion | flops 806615040 | bytes 155648 | tf_op jit(solution)/shard_map/srk,skz->srz/dot_general | solution.py:130
  42.4 0.1 fusion.156
  42.5 0.7 fusion.532
  43.3 1.6 %fusion.13 = f32[2048]{0:T(1024)S(1)} fusion(f32[256,128]{1,0:T(8,128)S(1)} %bitcast.127, s32[2048]{0:T(1024)S(1)} %bitcast.147, s32[2048]{0:T(1024)S(1)} %bitcast.139), kind=kOutput, calls=%fused_computation.14 | convolution fusion | flops 806615040 | bytes 155648 | tf_op jit(solution)/shard_map/srk,skz->srz/dot_general | solution.py:130
  44.9 0.1 fusion.536
  45.0 1.2 %fusion.25 = f32[1,8,32,128]{3,2,1,0:T(8,128)S(1)} fusion(s32[8,32]{1,0:T(8,128)S(1)} %multiply_add_fusion, s32[2048]{0:T(1024)S(1)} %bitcast.148, f32[2048]{0:T(1024)S(1)} %bitcast.134, s32[2048]{0:T(1024)S(1)} %bitcast.140), kind=kOutput, calls=%fused_computation.18 | convolution fusion | flops 806354944 | bytes 156672 | tf_op jit(solution)/shard_map/srk,srz->skz/dot_general | solution.py:137
  46.2 0.6 fusion.533
  47.6 0.3 fusion.402
  47.9 4.8 %collective-permute-start.10 = (f32[1]{0:T(128)}, f32[1]{0:T(128)}, u32[]{:S(2)}, u32[]{:S(2)}) collective-permute-start(f32[1]{0:T(128)} %bitcast.31), channel_id=1, source_target_pairs={{0,1},{1,0},{2,3},{3,2},{4,5},{5,4},{6,7},{7,6},{8,9},{9,8},{10,11... | collective-permute-start | bytes 20 | tf_op jit(solution)/shard_map/ppermute | solution.py:36
  52.7 1.9 %collective-permute-start.8 = (f32[1,7,32,128]{3,2,1,0:T(8,128)S(1)}, f32[1,7,32,128]{3,2,1,0:T(8,128)S(1)}, u32[]{:S(2)}, u32[]{:S(2)}) collective-permute-start(f32[1,7,32,128]{3,2,1,0:T(8,128)S(1)} %get-tuple-element.71), channel_id=1, source_target_pairs={{0,1},{1,2},{2,3},{3,4},{4,5},{5,6},{6,7},{7,8},{8,9},{9,10},{10,1... | collective-permute-start | bytes 344072 | tf_op jit(solution)/shard_map/ppermute | solution.py:18
  54.6 1.5 %collective-permute-start.9 = (f32[1,7,32,128]{3,2,1,0:T(8,128)S(1)}, f32[1,7,32,128]{3,2,1,0:T(8,128)S(1)}, u32[]{:S(2)}, u32[]{:S(2)}) collective-permute-start(f32[1,7,32,128]{3,2,1,0:T(8,128)S(1)} %get-tuple-element.72), channel_id=1, source_target_pairs={{1,0},{2,1},{3,2},{4,3},{5,4},{6,5},{7,6},{8,7},{9,8},{10,9},{11,1... | collective-permute-start | bytes 344072 | tf_op jit(solution)/shard_map/ppermute | solution.py:19
  56.1 0.3 fusion.273
  56.4 1.2 %fusion.28 = f32[1,8,32,128]{3,2,1,0:T(8,128)S(1)} fusion(s32[8,32]{1,0:T(8,128)S(1)} %multiply_add_fusion, s32[2048]{0:T(1024)S(1)} %bitcast.149, f32[2048]{0:T(1024)S(1)} %bitcast.133, s32[2048]{0:T(1024)S(1)} %bitcast.141), kind=kOutput, calls=%fused_computation.19 | convolution fusion | flops 806354944 | bytes 156672 | tf_op jit(solution)/shard_map/srk,srz->skz/dot_general | solution.py:137
  58.3 1.7 %collective-permute-done.9 = f32[1,7,32,128]{3,2,1,0:T(8,128)S(1)} collective-permute-done((f32[1,7,32,128]{3,2,1,0:T(8,128)S(1)}, f32[1,7,32,128]{3,2,1,0:T(8,128)S(1)}, u32[]{:S(2)}, u32[]{:S(2)}) %collective-permute-start.9) | collective-permute-done | bytes 114720 | tf_op jit(solution)/shard_map/ppermute | solution.py:19
  60.0 0.1 fusion.149
  60.1 0.1 fusion.493
  60.3 0.3 fusion.425
  60.6 4.5 %collective-permute-start.13 = (f32[1]{0:T(128)}, f32[1]{0:T(128)}, u32[]{:S(2)}, u32[]{:S(2)}) collective-permute-start(f32[1]{0:T(128)} %add.718), channel_id=1, source_target_pairs={{0,2},{1,3},{2,0},{3,1},{4,6},{5,7},{6,4},{7,5},{8,10},{9,11},{10,... | collective-permute-start | bytes 20 | tf_op jit(solution)/shard_map/ppermute | solution.py:36
  65.1 2.7 %collective-permute-start.11 = (f32[1,7,32,128]{3,2,1,0:T(8,128)S(1)}, f32[1,7,32,128]{3,2,1,0:T(8,128)S(1)}, u32[]{:S(2)}, u32[]{:S(2)}) collective-permute-start(f32[1,7,32,128]{3,2,1,0:T(8,128)S(1)} %get-tuple-element.69), channel_id=1, source_target_pairs={{0,1},{1,2},{2,3},{3,4},{4,5},{5,6},{6,7},{7,8},{8,9},{9,10},{10,1... | collective-permute-start | bytes 344072 | tf_op jit(solution)/shard_map/ppermute | solution.py:18
  67.8 1.3 %collective-permute-start.12 = (f32[1,7,32,128]{3,2,1,0:T(8,128)S(1)}, f32[1,7,32,128]{3,2,1,0:T(8,128)S(1)}, u32[]{:S(2)}, u32[]{:S(2)}) collective-permute-start(f32[1,7,32,128]{3,2,1,0:T(8,128)S(1)} %get-tuple-element.70), channel_id=1, source_target_pairs={{1,0},{2,1},{3,2},{4,3},{5,4},{6,5},{7,6},{8,7},{9,8},{10,9},{11,1... | collective-permute-start | bytes 344072 | tf_op jit(solution)/shard_map/ppermute | solution.py:19
  69.1 0.3 fusion.297
  69.4 1.2 %fusion.31 = f32[1,8,32,128]{3,2,1,0:T(8,128)S(1)} fusion(s32[8,32]{1,0:T(8,128)S(1)} %multiply_add_fusion, s32[2048]{0:T(1024)S(1)} %bitcast.150, f32[2048]{0:T(1024)S(1)} %bitcast.131, s32[2048]{0:T(1024)S(1)} %bitcast.142), kind=kOutput, calls=%fused_computation.20 | convolution fusion | flops 806354944 | bytes 156672 | tf_op jit(solution)/shard_map/srk,srz->skz/dot_general | solution.py:137
  71.3 0.1 fusion.142
  71.4 0.1 fusion.482
  71.5 0.3 fusion.448
  71.9 5.6 %collective-permute-start.16 = (f32[1]{0:T(128)}, f32[1]{0:T(128)}, u32[]{:S(2)}, u32[]{:S(2)}) collective-permute-start(f32[1]{0:T(128)} %add.742), channel_id=1, source_target_pairs={{0,4},{1,5},{2,6},{3,7},{4,0},{5,1},{6,2},{7,3},{8,12},{9,13},{10,... | collective-permute-start | bytes 20 | tf_op jit(solution)/shard_map/ppermute | solution.py:36
  77.5 1.3 %collective-permute-start.14 = (f32[1,7,32,128]{3,2,1,0:T(8,128)S(1)}, f32[1,7,32,128]{3,2,1,0:T(8,128)S(1)}, u32[]{:S(2)}, u32[]{:S(2)}) collective-permute-start(f32[1,7,32,128]{3,2,1,0:T(8,128)S(1)} %get-tuple-element.67), channel_id=1, source_target_pairs={{0,1},{1,2},{2,3},{3,4},{4,5},{5,6},{6,7},{7,8},{8,9},{9,10},{10,1... | collective-permute-start | bytes 344072 | tf_op jit(solution)/shard_map/ppermute | solution.py:18
  78.8 1.3 %collective-permute-start.15 = (f32[1,7,32,128]{3,2,1,0:T(8,128)S(1)}, f32[1,7,32,128]{3,2,1,0:T(8,128)S(1)}, u32[]{:S(2)}, u32[]{:S(2)}) collective-permute-start(f32[1,7,32,128]{3,2,1,0:T(8,128)S(1)} %get-tuple-element.68), channel_id=1, source_target_pairs={{1,0},{2,1},{3,2},{4,3},{5,4},{6,5},{7,6},{8,7},{9,8},{10,9},{11,1... | collective-permute-start | bytes 344072 | tf_op jit(solution)/shard_map/ppermute | solution.py:19
  80.1 0.3 fusion.321
  80.4 1.2 %fusion.34 = f32[1,8,32,128]{3,2,1,0:T(8,128)S(1)} fusion(s32[8,32]{1,0:T(8,128)S(1)} %multiply_add_fusion, s32[2048]{0:T(1024)S(1)} %bitcast.151, f32[2048]{0:T(1024)S(1)} %bitcast.129, s32[2048]{0:T(1024)S(1)} %bitcast.143), kind=kOutput, calls=%fused_computation.21 | convolution fusion | flops 806354944 | bytes 156672 | tf_op jit(solution)/shard_map/srk,srz->skz/dot_general | solution.py:137
  82.2 6.3 %collective-permute-start.17 = (f32[1]{0:T(128)}, f32[1]{0:T(128)}, u32[]{:S(2)}, u32[]{:S(2)}) collective-permute-start(f32[1]{0:T(128)} %add.766), channel_id=1, source_target_pairs={{0,8},{1,9},{2,10},{3,11},{4,12},{5,13},{6,14},{7,15},{8,0},{9,1},... | collective-permute-start | bytes 20 | tf_op jit(solution)/shard_map/ppermute | solution.py:36
  88.4 0.3 collective-permute-done.17
  89.4 0.1 fusion.135
  89.5 0.9 bitcast_multiply_fusion
  (58 shorter events, 0.7 us)
Async XLA Ops:
  0.6 5.1 %copy-start = (f32[8,32,128]{2,1,0:T(8,128)S(1)}, f32[8,32,128]{2,1,0:T(8,128)}, u32[]{:S(2)}) copy-start(f32[8,32,128]{2,1,0:T(8,128)} %param.11) | copy-start | bytes 393220
  0.6 5.1 %copy-start.1 = (f32[1,8,32,128]{3,2,1,0:T(8,128)S(1)}, f32[1,8,32,128]{3,2,1,0:T(8,128)}, u32[]{:S(2)}) copy-start(f32[1,8,32,128]{3,2,1,0:T(8,128)} %param.13) | copy-start | bytes 393220
  0.7 5.1 %copy-start.6 = (f32[1,8,32,128]{3,2,1,0:T(8,128)S(1)}, f32[1,8,32,128]{3,2,1,0:T(8,128)}, u32[]{:S(2)}) copy-start(f32[1,8,32,128]{3,2,1,0:T(8,128)} %param.12) | copy-start | bytes 393220
  1.8 5.2 %copy-start.9 = (f32[1,4]{1,0:T(1,128)S(1)}, f32[1,4]{1,0:T(1,128)}, u32[]{:S(2)}) copy-start(f32[1,4]{1,0:T(1,128)} %param.17) | copy-start | bytes 52
  1.8 5.8 %copy-start.7 = (s32[1,2048]{1,0:T(1,128)S(1)}, s32[1,2048]{1,0:T(1,128)}, u32[]{:S(2)}) copy-start(s32[1,2048]{1,0:T(1,128)} %param.18) | copy-start | bytes 24580
  1.8 5.9 %copy-start.4 = (f32[8,32,128]{2,1,0:T(8,128)S(1)}, f32[8,32,128]{2,1,0:T(8,128)}, u32[]{:S(2)}) copy-start(f32[8,32,128]{2,1,0:T(8,128)} %param.10) | copy-start | bytes 393220
  1.9 5.9 %collective-permute-start = (f32[2,7,32,128]{3,2,1,0:T(8,128)S(1)}, f32[2,7,32,128]{3,2,1,0:T(8,128)S(1)}, u32[]{:S(2)}, u32[]{:S(2)}) collective-permute-start(f32[2,7,32,128]{3,2,1,0:T(8,128)S(1)} %get-tuple-element.64), channel_id=1, source_target_pairs={{0,1},{1,2},{2,3},{3,4},{4,5},{5,6},{6,7},{7,8},{8,9},{9,10},{10,1... | collective-permute-start | bytes 688136 | tf_op jit(solution)/shard_map/ppermute | solution.py:18
  4.4 5.5 %collective-permute-start.1 = (f32[2,7,32,128]{3,2,1,0:T(8,128)S(1)}, f32[2,7,32,128]{3,2,1,0:T(8,128)S(1)}, u32[]{:S(2)}, u32[]{:S(2)}) collective-permute-start(f32[2,7,32,128]{3,2,1,0:T(8,128)S(1)} %get-tuple-element.63), channel_id=1, source_target_pairs={{1,0},{2,1},{3,2},{4,3},{5,4},{6,5},{7,6},{8,7},{9,8},{10,9},{11,1... | collective-permute-start | bytes 688136 | tf_op jit(solution)/shard_map/ppermute | solution.py:19
  10.0 0.9 %copy-start.2 = (f32[1,8,32,128]{3,2,1,0:T(8,128)S(1)}, f32[1,8,32,128]{3,2,1,0:T(8,128)}, u32[]{:S(2)}) copy-start(f32[1,8,32,128]{3,2,1,0:T(8,128)} %param.14) | copy-start | bytes 393220
  11.1 10.4 %collective-permute-start.2 = (f32[2,7,32,128]{3,2,1,0:T(8,128)S(1)}, f32[2,7,32,128]{3,2,1,0:T(8,128)S(1)}, u32[]{:S(2)}, u32[]{:S(2)}) collective-permute-start(f32[2,7,32,128]{3,2,1,0:T(8,128)S(1)} %get-tuple-element.61), channel_id=1, source_target_pairs={{0,1},{1,2},{2,3},{3,4},{4,5},{5,6},{6,7},{7,8},{8,9},{9,10},{10,1... | collective-permute-start | bytes 688136 | tf_op jit(solution)/shard_map/ppermute | solution.py:18
  17.4 4.0 %collective-permute-start.3 = (f32[2,7,32,128]{3,2,1,0:T(8,128)S(1)}, f32[2,7,32,128]{3,2,1,0:T(8,128)S(1)}, u32[]{:S(2)}, u32[]{:S(2)}) collective-permute-start(f32[2,7,32,128]{3,2,1,0:T(8,128)S(1)} %get-tuple-element.62), channel_id=1, source_target_pairs={{1,0},{2,1},{3,2},{4,3},{5,4},{6,5},{7,6},{8,7},{9,8},{10,9},{11,1... | collective-permute-start | bytes 688136 | tf_op jit(solution)/shard_map/ppermute | solution.py:19
  23.0 9.2 %collective-permute-start.4 = (f32[1,7,32,128]{3,2,1,0:T(8,128)S(1)}, f32[1,7,32,128]{3,2,1,0:T(8,128)S(1)}, u32[]{:S(2)}, u32[]{:S(2)}) collective-permute-start(f32[1,7,32,128]{3,2,1,0:T(8,128)S(1)} %get-tuple-element.75), channel_id=1, source_target_pairs={{0,1},{1,2},{2,3},{3,4},{4,5},{5,6},{6,7},{7,8},{8,9},{9,10},{10,1... | collective-permute-start | bytes 344072 | tf_op jit(solution)/shard_map/ppermute | solution.py:18
  29.0 3.2 %collective-permute-start.5 = (f32[1,7,32,128]{3,2,1,0:T(8,128)S(1)}, f32[1,7,32,128]{3,2,1,0:T(8,128)S(1)}, u32[]{:S(2)}, u32[]{:S(2)}) collective-permute-start(f32[1,7,32,128]{3,2,1,0:T(8,128)S(1)} %get-tuple-element.76), channel_id=1, source_target_pairs={{1,0},{2,1},{3,2},{4,3},{5,4},{6,5},{7,6},{8,7},{9,8},{10,9},{11,1... | collective-permute-start | bytes 344072 | tf_op jit(solution)/shard_map/ppermute | solution.py:19
  33.5 8.9 %collective-permute-start.6 = (f32[1,7,32,128]{3,2,1,0:T(8,128)S(1)}, f32[1,7,32,128]{3,2,1,0:T(8,128)S(1)}, u32[]{:S(2)}, u32[]{:S(2)}) collective-permute-start(f32[1,7,32,128]{3,2,1,0:T(8,128)S(1)} %get-tuple-element.73), channel_id=1, source_target_pairs={{0,1},{1,2},{2,3},{3,4},{4,5},{5,6},{6,7},{7,8},{8,9},{9,10},{10,1... | collective-permute-start | bytes 344072 | tf_op jit(solution)/shard_map/ppermute | solution.py:18
  39.1 3.2 %collective-permute-start.7 = (f32[1,7,32,128]{3,2,1,0:T(8,128)S(1)}, f32[1,7,32,128]{3,2,1,0:T(8,128)S(1)}, u32[]{:S(2)}, u32[]{:S(2)}) collective-permute-start(f32[1,7,32,128]{3,2,1,0:T(8,128)S(1)} %get-tuple-element.74), channel_id=1, source_target_pairs={{1,0},{2,1},{3,2},{4,3},{5,4},{6,5},{7,6},{8,7},{9,8},{10,9},{11,1... | collective-permute-start | bytes 344072 | tf_op jit(solution)/shard_map/ppermute | solution.py:19
  43.3 1.6 %copy-start.8 = (f32[1,4,2048]{2,1,0:T(4,128)S(1)}, f32[1,4,2048]{2,1,0:T(4,128)}, u32[]{:S(2)}) copy-start(f32[1,4,2048]{2,1,0:T(4,128)} %param.19) | copy-start | bytes 98308
  45.0 2.5 %copy-start.5 = (f32[1,8,32,128]{3,2,1,0:T(8,128)S(1)}, f32[1,8,32,128]{3,2,1,0:T(8,128)}, u32[]{:S(2)}) copy-start(f32[1,8,32,128]{3,2,1,0:T(8,128)} %param.15) | copy-start | bytes 393220
  47.9 9.7 %collective-permute-start.10 = (f32[1]{0:T(128)}, f32[1]{0:T(128)}, u32[]{:S(2)}, u32[]{:S(2)}) collective-permute-start(f32[1]{0:T(128)} %bitcast.31), channel_id=1, source_target_pairs={{0,1},{1,0},{2,3},{3,2},{4,5},{5,4},{6,7},{7,6},{8,9},{9,8},{10,11... | collective-permute-start | bytes 20 | tf_op jit(solution)/shard_map/ppermute | solution.py:36
  52.7 5.5 %collective-permute-start.8 = (f32[1,7,32,128]{3,2,1,0:T(8,128)S(1)}, f32[1,7,32,128]{3,2,1,0:T(8,128)S(1)}, u32[]{:S(2)}, u32[]{:S(2)}) collective-permute-start(f32[1,7,32,128]{3,2,1,0:T(8,128)S(1)} %get-tuple-element.71), channel_id=1, source_target_pairs={{0,1},{1,2},{2,3},{3,4},{4,5},{5,6},{6,7},{7,8},{8,9},{9,10},{10,1... | collective-permute-start | bytes 344072 | tf_op jit(solution)/shard_map/ppermute | solution.py:18
  54.6 5.4 %collective-permute-start.9 = (f32[1,7,32,128]{3,2,1,0:T(8,128)S(1)}, f32[1,7,32,128]{3,2,1,0:T(8,128)S(1)}, u32[]{:S(2)}, u32[]{:S(2)}) collective-permute-start(f32[1,7,32,128]{3,2,1,0:T(8,128)S(1)} %get-tuple-element.72), channel_id=1, source_target_pairs={{1,0},{2,1},{3,2},{4,3},{5,4},{6,5},{7,6},{8,7},{9,8},{10,9},{11,1... | collective-permute-start | bytes 344072 | tf_op jit(solution)/shard_map/ppermute | solution.py:19
  60.6 10.1 %collective-permute-start.13 = (f32[1]{0:T(128)}, f32[1]{0:T(128)}, u32[]{:S(2)}, u32[]{:S(2)}) collective-permute-start(f32[1]{0:T(128)} %add.718), channel_id=1, source_target_pairs={{0,2},{1,3},{2,0},{3,1},{4,6},{5,7},{6,4},{7,5},{8,10},{9,11},{10,... | collective-permute-start | bytes 20 | tf_op jit(solution)/shard_map/ppermute | solution.py:36
  65.1 6.1 %collective-permute-start.11 = (f32[1,7,32,128]{3,2,1,0:T(8,128)S(1)}, f32[1,7,32,128]{3,2,1,0:T(8,128)S(1)}, u32[]{:S(2)}, u32[]{:S(2)}) collective-permute-start(f32[1,7,32,128]{3,2,1,0:T(8,128)S(1)} %get-tuple-element.69), channel_id=1, source_target_pairs={{0,1},{1,2},{2,3},{3,4},{4,5},{5,6},{6,7},{7,8},{8,9},{9,10},{10,1... | collective-permute-start | bytes 344072 | tf_op jit(solution)/shard_map/ppermute | solution.py:18
  67.8 3.4 %collective-permute-start.12 = (f32[1,7,32,128]{3,2,1,0:T(8,128)S(1)}, f32[1,7,32,128]{3,2,1,0:T(8,128)S(1)}, u32[]{:S(2)}, u32[]{:S(2)}) collective-permute-start(f32[1,7,32,128]{3,2,1,0:T(8,128)S(1)} %get-tuple-element.70), channel_id=1, source_target_pairs={{1,0},{2,1},{3,2},{4,3},{5,4},{6,5},{7,6},{8,7},{9,8},{10,9},{11,1... | collective-permute-start | bytes 344072 | tf_op jit(solution)/shard_map/ppermute | solution.py:19
  71.5 18.0 %copy-start.3 = (f32[1,8,32,128]{3,2,1,0:T(8,128)}, f32[1,8,32,128]{3,2,1,0:T(8,128)S(1)}, u32[]{:S(2)}) copy-start(f32[1,8,32,128]{3,2,1,0:T(8,128)S(1)} %fusion.482) | copy-start | bytes 393220
  71.9 9.8 %collective-permute-start.16 = (f32[1]{0:T(128)}, f32[1]{0:T(128)}, u32[]{:S(2)}, u32[]{:S(2)}) collective-permute-start(f32[1]{0:T(128)} %add.742), channel_id=1, source_target_pairs={{0,4},{1,5},{2,6},{3,7},{4,0},{5,1},{6,2},{7,3},{8,12},{9,13},{10,... | collective-permute-start | bytes 20 | tf_op jit(solution)/shard_map/ppermute | solution.py:36
  77.5 11.9 %collective-permute-start.14 = (f32[1,7,32,128]{3,2,1,0:T(8,128)S(1)}, f32[1,7,32,128]{3,2,1,0:T(8,128)S(1)}, u32[]{:S(2)}, u32[]{:S(2)}) collective-permute-start(f32[1,7,32,128]{3,2,1,0:T(8,128)S(1)} %get-tuple-element.67), channel_id=1, source_target_pairs={{0,1},{1,2},{2,3},{3,4},{4,5},{5,6},{6,7},{7,8},{8,9},{9,10},{10,1... | collective-permute-start | bytes 344072 | tf_op jit(solution)/shard_map/ppermute | solution.py:18
  78.8 10.6 %collective-permute-start.15 = (f32[1,7,32,128]{3,2,1,0:T(8,128)S(1)}, f32[1,7,32,128]{3,2,1,0:T(8,128)S(1)}, u32[]{:S(2)}, u32[]{:S(2)}) collective-permute-start(f32[1,7,32,128]{3,2,1,0:T(8,128)S(1)} %get-tuple-element.68), channel_id=1, source_target_pairs={{1,0},{2,1},{3,2},{4,3},{5,4},{6,5},{7,6},{8,7},{9,8},{10,9},{11,1... | collective-permute-start | bytes 344072 | tf_op jit(solution)/shard_map/ppermute | solution.py:19
  82.2 6.6 %collective-permute-start.17 = (f32[1]{0:T(128)}, f32[1]{0:T(128)}, u32[]{:S(2)}, u32[]{:S(2)}) collective-permute-start(f32[1]{0:T(128)} %add.766), channel_id=1, source_target_pairs={{0,8},{1,9},{2,10},{3,11},{4,12},{5,13},{6,14},{7,15},{8,0},{9,1},... | collective-permute-start | bytes 20 | tf_op jit(solution)/shard_map/ppermute | solution.py:36

commit v25 on v19

--- a/solution.py
+++ b/solution.py
@@ -28,7 +28,7 @@
     while distance < devices:
         far.append(distance)
         distance *= 2
-    return far + [1] if devices > 1 else []
+    return far[::-1] + [1] if devices > 1 else []
 
 
 def butterfly_round(values, axis, distance):

time: 89.6 us -> 89.7 us (level)
  transfers between devices with their start and end apart: 18 -> 18, of which waited for: 8 -> 7; matrix products, arithmetic and copies ran while one was open for 14% -> 14% of each run, Pallas kernels for 0% -> 0%
where the time goes in v25:
time: 89.7 us; the launch traced here: 88.9 us
  starting transfers between devices  42.9 us (48%)
  waiting for transfers between devices  15.6 us (17%)
  other arithmetic  12.1 us (13%)
  matrix products  11.4 us (13%)
  between operations  6.03 us (7%)
    ppermute x7, starting transfers between devices, extended(): before = lax.ppermute(last, 'mp', up)  17.6 us
    ppermute x7, starting transfers between devices, extended(): after = lax.ppermute(first, 'mp', down)  16.4 us
    ppermute x7, waiting for transfers between devices, extended(): after = lax.ppermute(first, 'mp', down)  15.3 us
    ppermute x4, starting transfers between devices, butterfly_round(): return values + lax.ppermute(values, axis, pairs)  8.94 us
    dot_general x4, matrix products, sample(): jnp.einsum('srk,skz->srz', row_pick, field.reshape(shots, rows, cz), prec...  6.43 us
    dot_general x4, matrix products, injected(): jnp.einsum('srk,srz->skz', row_pick, spread, precision=lax.Precision.HIGH...  4.93 us
    add x4, other arithmetic, local(): following = following + jnp.where(source_hit, amount, 0.0)  3.03 us
    mul x7, other arithmetic, cross_terms(): flux = buoyancy * forward_diff(pad_axis(values, axis), axis, length)  2.4 us
  transfers between devices with their start and end apart: 18, of which 7 were waited for; matrix products, arithmetic and copies ran while one was open for 14% of the time, Pallas kernels for 0%

profile of v25, /device:TPU:1, one launch (start us, length us, event | category | flops | bytes accessed | tf_op | source)
XLA Modules:
  0.0 88.9 jit_solution(11320330188276983486)
XLA Ops:
  0.7 1.1 %pad_maximum_fusion.12 = (f32[2,7,32,128]{3,2,1,0:T(8,128)S(1)}, f32[2,7,32,128]{3,2,1,0:T(8,128)S(1)}) fusion(f32[1,8,32,128]{3,2,1,0:T(8,128)} %param.13, f32[1,8,32,128]{3,2,1,0:T(8,128)} %bitcast.121), kind=kLoop, calls=%fused_computation.331 | loop fusion | flops 114688 | bytes 720896 | tf_op jit(solution)/shard_map/concatenate | solution.py:99
  1.9 4.7 %collective-permute-start = (f32[2,7,32,128]{3,2,1,0:T(8,128)S(1)}, f32[2,7,32,128]{3,2,1,0:T(8,128)S(1)}, u32[]{:S(2)}, u32[]{:S(2)}) collective-permute-start(f32[2,7,32,128]{3,2,1,0:T(8,128)S(1)} %get-tuple-element.64), channel_id=1, source_target_pairs={{0,1},{1,2},{2,3},{3,4},{4,5},{5,6},{6,7},{7,8},{8,9},{9,10},{10,1... | collective-permute-start | bytes 688136 | tf_op jit(solution)/shard_map/ppermute | solution.py:18
  6.5 1.9 %collective-permute-start.1 = (f32[2,7,32,128]{3,2,1,0:T(8,128)S(1)}, f32[2,7,32,128]{3,2,1,0:T(8,128)S(1)}, u32[]{:S(2)}, u32[]{:S(2)}) collective-permute-start(f32[2,7,32,128]{3,2,1,0:T(8,128)S(1)} %get-tuple-element.63), channel_id=1, source_target_pairs={{1,0},{2,1},{3,2},{4,3},{5,4},{6,5},{7,6},{8,7},{9,8},{10,9},{11,1... | collective-permute-start | bytes 688136 | tf_op jit(solution)/shard_map/ppermute | solution.py:19
  8.5 0.3 fusion.333
  8.8 0.3 fusion.201
  9.8 0.6 fusion.552
  10.6 3.3 %collective-permute-done.1 = f32[2,7,32,128]{3,2,1,0:T(8,128)S(1)} collective-permute-done((f32[2,7,32,128]{3,2,1,0:T(8,128)S(1)}, f32[2,7,32,128]{3,2,1,0:T(8,128)S(1)}, u32[]{:S(2)}, u32[]{:S(2)}) %collective-permute-start.1) | collective-permute-done | bytes 229408 | tf_op jit(solution)/shard_map/ppermute | solution.py:19
  13.9 0.1 slice_bitcast_fusion
  14.1 0.8 fusion.526
  14.8 0.1 copy-done.2
  15.1 1.9 %collective-permute-start.2 = (f32[2,7,32,128]{3,2,1,0:T(8,128)S(1)}, f32[2,7,32,128]{3,2,1,0:T(8,128)S(1)}, u32[]{:S(2)}, u32[]{:S(2)}) collective-permute-start(f32[2,7,32,128]{3,2,1,0:T(8,128)S(1)} %get-tuple-element.61), channel_id=1, source_target_pairs={{0,1},{1,2},{2,3},{3,4},{4,5},{5,6},{6,7},{7,8},{8,9},{9,10},{10,1... | collective-permute-start | bytes 688136 | tf_op jit(solution)/shard_map/ppermute | solution.py:18
  17.0 2.4 %collective-permute-start.3 = (f32[2,7,32,128]{3,2,1,0:T(8,128)S(1)}, f32[2,7,32,128]{3,2,1,0:T(8,128)S(1)}, u32[]{:S(2)}, u32[]{:S(2)}) collective-permute-start(f32[2,7,32,128]{3,2,1,0:T(8,128)S(1)} %get-tuple-element.62), channel_id=1, source_target_pairs={{1,0},{2,1},{3,2},{4,3},{5,4},{6,5},{7,6},{8,7},{9,8},{10,9},{11,1... | collective-permute-start | bytes 688136 | tf_op jit(solution)/shard_map/ppermute | solution.py:19
  19.4 0.5 fusion.106
  20.0 0.5 fusion.94
  20.5 1.6 %fusion.16 = f32[2048]{0:T(1024)S(1)} fusion(f32[256,128]{1,0:T(8,128)S(1)} %bitcast.125, s32[2048]{0:T(1024)S(1)} %bitcast.144, s32[2048]{0:T(1024)S(1)} %bitcast.136), kind=kOutput, calls=%fused_computation.15 | convolution fusion | flops 806615040 | bytes 155648 | tf_op jit(solution)/shard_map/srk,skz->srz/dot_general | solution.py:130
  22.1 3.0 %collective-permute-done.3 = f32[2,7,32,128]{3,2,1,0:T(8,128)S(1)} collective-permute-done((f32[2,7,32,128]{3,2,1,0:T(8,128)S(1)}, f32[2,7,32,128]{3,2,1,0:T(8,128)S(1)}, u32[]{:S(2)}, u32[]{:S(2)}) %collective-permute-start.3) | collective-permute-done | bytes 229408 | tf_op jit(solution)/shard_map/ppermute | solution.py:19
  25.2 0.2 fusion.72
  25.4 0.1 fusion.126
  25.5 0.7 fusion.528
  26.3 0.3 fusion.356
  26.6 1.9 %collective-permute-start.4 = (f32[1,7,32,128]{3,2,1,0:T(8,128)S(1)}, f32[1,7,32,128]{3,2,1,0:T(8,128)S(1)}, u32[]{:S(2)}, u32[]{:S(2)}) collective-permute-start(f32[1,7,32,128]{3,2,1,0:T(8,128)S(1)} %get-tuple-element.75), channel_id=1, source_target_pairs={{0,1},{1,2},{2,3},{3,4},{4,5},{5,6},{6,7},{7,8},{8,9},{9,10},{10,1... | collective-permute-start | bytes 344072 | tf_op jit(solution)/shard_map/ppermute | solution.py:18
  28.5 2.4 %collective-permute-start.5 = (f32[1,7,32,128]{3,2,1,0:T(8,128)S(1)}, f32[1,7,32,128]{3,2,1,0:T(8,128)S(1)}, u32[]{:S(2)}, u32[]{:S(2)}) collective-permute-start(f32[1,7,32,128]{3,2,1,0:T(8,128)S(1)} %get-tuple-element.76), channel_id=1, source_target_pairs={{1,0},{2,1},{3,2},{4,3},{5,4},{6,5},{7,6},{8,7},{9,8},{10,9},{11,1... | collective-permute-start | bytes 344072 | tf_op jit(solution)/shard_map/ppermute | solution.py:19
  30.9 0.3 fusion.225
  31.3 1.6 %fusion.19 = f32[2048]{0:T(1024)S(1)} fusion(f32[256,128]{1,0:T(8,128)S(1)} %bitcast.124, s32[2048]{0:T(1024)S(1)} %bitcast.145, s32[2048]{0:T(1024)S(1)} %bitcast.137), kind=kOutput, calls=%fused_computation.16 | convolution fusion | flops 806615040 | bytes 155648 | tf_op jit(solution)/shard_map/srk,skz->srz/dot_general | solution.py:130
  32.9 2.7 %collective-permute-done.5 = f32[1,7,32,128]{3,2,1,0:T(8,128)S(1)} collective-permute-done((f32[1,7,32,128]{3,2,1,0:T(8,128)S(1)}, f32[1,7,32,128]{3,2,1,0:T(8,128)S(1)}, u32[]{:S(2)}, u32[]{:S(2)}) %collective-permute-start.5) | collective-permute-done | bytes 114720 | tf_op jit(solution)/shard_map/ppermute | solution.py:19
  35.6 0.1 fusion.163
  35.7 0.7 fusion.530
  36.5 0.3 fusion.379
  36.8 1.9 %collective-permute-start.6 = (f32[1,7,32,128]{3,2,1,0:T(8,128)S(1)}, f32[1,7,32,128]{3,2,1,0:T(8,128)S(1)}, u32[]{:S(2)}, u32[]{:S(2)}) collective-permute-start(f32[1,7,32,128]{3,2,1,0:T(8,128)S(1)} %get-tuple-element.73), channel_id=1, source_target_pairs={{0,1},{1,2},{2,3},{3,4},{4,5},{5,6},{6,7},{7,8},{8,9},{9,10},{10,1... | collective-permute-start | bytes 344072 | tf_op jit(solution)/shard_map/ppermute | solution.py:18
  38.7 2.4 %collective-permute-start.7 = (f32[1,7,32,128]{3,2,1,0:T(8,128)S(1)}, f32[1,7,32,128]{3,2,1,0:T(8,128)S(1)}, u32[]{:S(2)}, u32[]{:S(2)}) collective-permute-start(f32[1,7,32,128]{3,2,1,0:T(8,128)S(1)} %get-tuple-element.74), channel_id=1, source_target_pairs={{1,0},{2,1},{3,2},{4,3},{5,4},{6,5},{7,6},{8,7},{9,8},{10,9},{11,1... | collective-permute-start | bytes 344072 | tf_op jit(solution)/shard_map/ppermute | solution.py:19
  41.1 0.3 fusion.249
  41.4 1.6 %fusion.22 = f32[2048]{0:T(1024)S(1)} fusion(f32[256,128]{1,0:T(8,128)S(1)} %bitcast.126, s32[2048]{0:T(1024)S(1)} %bitcast.146, s32[2048]{0:T(1024)S(1)} %bitcast.138), kind=kOutput, calls=%fused_computation.17 | convolution fusion | flops 806615040 | bytes 155648 | tf_op jit(solution)/shard_map/srk,skz->srz/dot_general | solution.py:130
  43.0 2.7 %collective-permute-done.7 = f32[1,7,32,128]{3,2,1,0:T(8,128)S(1)} collective-permute-done((f32[1,7,32,128]{3,2,1,0:T(8,128)S(1)}, f32[1,7,32,128]{3,2,1,0:T(8,128)S(1)}, u32[]{:S(2)}, u32[]{:S(2)}) %collective-permute-start.7) | collective-permute-done | bytes 114720 | tf_op jit(solution)/shard_map/ppermute | solution.py:19
  45.7 0.1 fusion.156
  45.8 0.7 fusion.532
  46.6 1.6 %fusion.13 = f32[2048]{0:T(1024)S(1)} fusion(f32[256,128]{1,0:T(8,128)S(1)} %bitcast.127, s32[2048]{0:T(1024)S(1)} %bitcast.147, s32[2048]{0:T(1024)S(1)} %bitcast.139), kind=kOutput, calls=%fused_computation.14 | convolution fusion | flops 806615040 | bytes 155648 | tf_op jit(solution)/shard_map/srk,skz->srz/dot_general | solution.py:130
  48.3 1.2 %fusion.25 = f32[1,8,32,128]{3,2,1,0:T(8,128)S(1)} fusion(s32[8,32]{1,0:T(8,128)S(1)} %multiply_add_fusion, s32[2048]{0:T(1024)S(1)} %bitcast.148, f32[2048]{0:T(1024)S(1)} %bitcast.134, s32[2048]{0:T(1024)S(1)} %bitcast.140), kind=kOutput, calls=%fused_computation.18 | convolution fusion | flops 806354944 | bytes 156672 | tf_op jit(solution)/shard_map/srk,srz->skz/dot_general | solution.py:137
  49.5 0.6 fusion.533
  50.9 0.3 fusion.402
  51.3 3.1 %collective-permute-start.10 = (f32[1]{0:T(128)}, f32[1]{0:T(128)}, u32[]{:S(2)}, u32[]{:S(2)}) collective-permute-start(f32[1]{0:T(128)} %bitcast.31), channel_id=1, source_target_pairs={{0,8},{1,9},{2,10},{3,11},{4,12},{5,13},{6,14},{7,15},{8,0},{9,1},... | collective-permute-start | bytes 20 | tf_op jit(solution)/shard_map/ppermute | solution.py:36
  54.4 2.6 %collective-permute-start.8 = (f32[1,7,32,128]{3,2,1,0:T(8,128)S(1)}, f32[1,7,32,128]{3,2,1,0:T(8,128)S(1)}, u32[]{:S(2)}, u32[]{:S(2)}) collective-permute-start(f32[1,7,32,128]{3,2,1,0:T(8,128)S(1)} %get-tuple-element.71), channel_id=1, source_target_pairs={{0,1},{1,2},{2,3},{3,4},{4,5},{5,6},{6,7},{7,8},{8,9},{9,10},{10,1... | collective-permute-start | bytes 344072 | tf_op jit(solution)/shard_map/ppermute | solution.py:18
  57.0 2.1 %collective-permute-start.9 = (f32[1,7,32,128]{3,2,1,0:T(8,128)S(1)}, f32[1,7,32,128]{3,2,1,0:T(8,128)S(1)}, u32[]{:S(2)}, u32[]{:S(2)}) collective-permute-start(f32[1,7,32,128]{3,2,1,0:T(8,128)S(1)} %get-tuple-element.72), channel_id=1, source_target_pairs={{1,0},{2,1},{3,2},{4,3},{5,4},{6,5},{7,6},{8,7},{9,8},{10,9},{11,1... | collective-permute-start | bytes 344072 | tf_op jit(solution)/shard_map/ppermute | solution.py:19
  59.1 0.3 fusion.273
  59.4 1.2 %fusion.28 = f32[1,8,32,128]{3,2,1,0:T(8,128)S(1)} fusion(s32[8,32]{1,0:T(8,128)S(1)} %multiply_add_fusion, s32[2048]{0:T(1024)S(1)} %bitcast.149, f32[2048]{0:T(1024)S(1)} %bitcast.133, s32[2048]{0:T(1024)S(1)} %bitcast.141), kind=kOutput, calls=%fused_computation.19 | convolution fusion | flops 806354944 | bytes 156672 | tf_op jit(solution)/shard_map/srk,srz->skz/dot_general | solution.py:137
  61.2 2.0 %collective-permute-done.9 = f32[1,7,32,128]{3,2,1,0:T(8,128)S(1)} collective-permute-done((f32[1,7,32,128]{3,2,1,0:T(8,128)S(1)}, f32[1,7,32,128]{3,2,1,0:T(8,128)S(1)}, u32[]{:S(2)}, u32[]{:S(2)}) %collective-permute-start.9) | collective-permute-done | bytes 114720 | tf_op jit(solution)/shard_map/ppermute | solution.py:19
  63.3 0.1 fusion.149
  63.6 0.3 fusion.425
  63.9 1.3 %collective-permute-start.13 = (f32[1]{0:T(128)}, f32[1]{0:T(128)}, u32[]{:S(2)}, u32[]{:S(2)}) collective-permute-start(f32[1]{0:T(128)} %add.718), channel_id=1, source_target_pairs={{0,4},{1,5},{2,6},{3,7},{4,0},{5,1},{6,2},{7,3},{8,12},{9,13},{10,... | collective-permute-start | bytes 20 | tf_op jit(solution)/shard_map/ppermute | solution.py:36
  65.2 2.6 %collective-permute-start.11 = (f32[1,7,32,128]{3,2,1,0:T(8,128)S(1)}, f32[1,7,32,128]{3,2,1,0:T(8,128)S(1)}, u32[]{:S(2)}, u32[]{:S(2)}) collective-permute-start(f32[1,7,32,128]{3,2,1,0:T(8,128)S(1)} %get-tuple-element.69), channel_id=1, source_target_pairs={{0,1},{1,2},{2,3},{3,4},{4,5},{5,6},{6,7},{7,8},{8,9},{9,10},{10,1... | collective-permute-start | bytes 344072 | tf_op jit(solution)/shard_map/ppermute | solution.py:18
  67.8 2.7 %collective-permute-start.12 = (f32[1,7,32,128]{3,2,1,0:T(8,128)S(1)}, f32[1,7,32,128]{3,2,1,0:T(8,128)S(1)}, u32[]{:S(2)}, u32[]{:S(2)}) collective-permute-start(f32[1,7,32,128]{3,2,1,0:T(8,128)S(1)} %get-tuple-element.70), channel_id=1, source_target_pairs={{1,0},{2,1},{3,2},{4,3},{5,4},{6,5},{7,6},{8,7},{9,8},{10,9},{11,1... | collective-permute-start | bytes 344072 | tf_op jit(solution)/shard_map/ppermute | solution.py:19
  70.5 0.3 fusion.297
  70.8 1.2 %fusion.31 = f32[1,8,32,128]{3,2,1,0:T(8,128)S(1)} fusion(s32[8,32]{1,0:T(8,128)S(1)} %multiply_add_fusion, s32[2048]{0:T(1024)S(1)} %bitcast.150, f32[2048]{0:T(1024)S(1)} %bitcast.131, s32[2048]{0:T(1024)S(1)} %bitcast.142), kind=kOutput, calls=%fused_computation.20 | convolution fusion | flops 806354944 | bytes 156672 | tf_op jit(solution)/shard_map/srk,srz->skz/dot_general | solution.py:137
  72.7 1.7 %collective-permute-done.12 = f32[1,7,32,128]{3,2,1,0:T(8,128)S(1)} collective-permute-done((f32[1,7,32,128]{3,2,1,0:T(8,128)S(1)}, f32[1,7,32,128]{3,2,1,0:T(8,128)S(1)}, u32[]{:S(2)}, u32[]{:S(2)}) %collective-permute-start.12) | collective-permute-done | bytes 114720 | tf_op jit(solution)/shard_map/ppermute | solution.py:19
  74.4 0.1 fusion.142
  74.6 0.3 fusion.448
  74.9 3.5 %collective-permute-start.16 = (f32[1]{0:T(128)}, f32[1]{0:T(128)}, u32[]{:S(2)}, u32[]{:S(2)}) collective-permute-start(f32[1]{0:T(128)} %add.742), channel_id=1, source_target_pairs={{0,2},{1,3},{2,0},{3,1},{4,6},{5,7},{6,4},{7,5},{8,10},{9,11},{10,... | collective-permute-start | bytes 20 | tf_op jit(solution)/shard_map/ppermute | solution.py:36
  78.4 1.9 %collective-permute-start.14 = (f32[1,7,32,128]{3,2,1,0:T(8,128)S(1)}, f32[1,7,32,128]{3,2,1,0:T(8,128)S(1)}, u32[]{:S(2)}, u32[]{:S(2)}) collective-permute-start(f32[1,7,32,128]{3,2,1,0:T(8,128)S(1)} %get-tuple-element.67), channel_id=1, source_target_pairs={{0,1},{1,2},{2,3},{3,4},{4,5},{5,6},{6,7},{7,8},{8,9},{9,10},{10,1... | collective-permute-start | bytes 344072 | tf_op jit(solution)/shard_map/ppermute | solution.py:18
  80.3 2.4 %collective-permute-start.15 = (f32[1,7,32,128]{3,2,1,0:T(8,128)S(1)}, f32[1,7,32,128]{3,2,1,0:T(8,128)S(1)}, u32[]{:S(2)}, u32[]{:S(2)}) collective-permute-start(f32[1,7,32,128]{3,2,1,0:T(8,128)S(1)} %get-tuple-element.68), channel_id=1, source_target_pairs={{1,0},{2,1},{3,2},{4,3},{5,4},{6,5},{7,6},{8,7},{9,8},{10,9},{11,1... | collective-permute-start | bytes 344072 | tf_op jit(solution)/shard_map/ppermute | solution.py:19
  82.8 0.3 fusion.321
  83.1 1.2 %fusion.34 = f32[1,8,32,128]{3,2,1,0:T(8,128)S(1)} fusion(s32[8,32]{1,0:T(8,128)S(1)} %multiply_add_fusion, s32[2048]{0:T(1024)S(1)} %bitcast.151, f32[2048]{0:T(1024)S(1)} %bitcast.129, s32[2048]{0:T(1024)S(1)} %bitcast.143), kind=kOutput, calls=%fused_computation.21 | convolution fusion | flops 806354944 | bytes 156672 | tf_op jit(solution)/shard_map/srk,srz->skz/dot_general | solution.py:137
  84.9 1.0 %collective-permute-start.17 = (f32[1]{0:T(128)}, f32[1]{0:T(128)}, u32[]{:S(2)}, u32[]{:S(2)}) collective-permute-start(f32[1]{0:T(128)} %add.766), channel_id=1, source_target_pairs={{0,1},{1,0},{2,3},{3,2},{4,5},{5,4},{6,7},{7,6},{8,9},{9,8},{10,11... | collective-permute-start | bytes 20 | tf_op jit(solution)/shard_map/ppermute | solution.py:36
  85.9 0.3 collective-permute-done.17
  86.8 0.1 fusion.135
  86.9 0.9 bitcast_multiply_fusion
  (58 shorter events, 0.9 us)
Async XLA Ops:
  0.6 7.9 %copy-start = (f32[8,32,128]{2,1,0:T(8,128)S(1)}, f32[8,32,128]{2,1,0:T(8,128)}, u32[]{:S(2)}) copy-start(f32[8,32,128]{2,1,0:T(8,128)} %param.11) | copy-start | bytes 393220
  0.6 7.9 %copy-start.1 = (f32[1,8,32,128]{3,2,1,0:T(8,128)S(1)}, f32[1,8,32,128]{3,2,1,0:T(8,128)}, u32[]{:S(2)}) copy-start(f32[1,8,32,128]{3,2,1,0:T(8,128)} %param.13) | copy-start | bytes 393220
  0.7 7.9 %copy-start.6 = (f32[1,8,32,128]{3,2,1,0:T(8,128)S(1)}, f32[1,8,32,128]{3,2,1,0:T(8,128)}, u32[]{:S(2)}) copy-start(f32[1,8,32,128]{3,2,1,0:T(8,128)} %param.12) | copy-start | bytes 393220
  1.8 8.0 %copy-start.9 = (f32[1,4]{1,0:T(1,128)S(1)}, f32[1,4]{1,0:T(1,128)}, u32[]{:S(2)}) copy-start(f32[1,4]{1,0:T(1,128)} %param.17) | copy-start | bytes 52
  1.8 8.6 %copy-start.7 = (s32[1,2048]{1,0:T(1,128)S(1)}, s32[1,2048]{1,0:T(1,128)}, u32[]{:S(2)}) copy-start(s32[1,2048]{1,0:T(1,128)} %param.18) | copy-start | bytes 24580
  1.8 8.7 %copy-start.4 = (f32[8,32,128]{2,1,0:T(8,128)S(1)}, f32[8,32,128]{2,1,0:T(8,128)}, u32[]{:S(2)}) copy-start(f32[8,32,128]{2,1,0:T(8,128)} %param.10) | copy-start | bytes 393220
  1.9 8.7 %collective-permute-start = (f32[2,7,32,128]{3,2,1,0:T(8,128)S(1)}, f32[2,7,32,128]{3,2,1,0:T(8,128)S(1)}, u32[]{:S(2)}, u32[]{:S(2)}) collective-permute-start(f32[2,7,32,128]{3,2,1,0:T(8,128)S(1)} %get-tuple-element.64), channel_id=1, source_target_pairs={{0,1},{1,2},{2,3},{3,4},{4,5},{5,6},{6,7},{7,8},{8,9},{9,10},{10,1... | collective-permute-start | bytes 688136 | tf_op jit(solution)/shard_map/ppermute | solution.py:18
  6.5 7.3 %collective-permute-start.1 = (f32[2,7,32,128]{3,2,1,0:T(8,128)S(1)}, f32[2,7,32,128]{3,2,1,0:T(8,128)S(1)}, u32[]{:S(2)}, u32[]{:S(2)}) collective-permute-start(f32[2,7,32,128]{3,2,1,0:T(8,128)S(1)} %get-tuple-element.63), channel_id=1, source_target_pairs={{1,0},{2,1},{3,2},{4,3},{5,4},{6,5},{7,6},{8,7},{9,8},{10,9},{11,1... | collective-permute-start | bytes 688136 | tf_op jit(solution)/shard_map/ppermute | solution.py:19
  14.0 0.9 %copy-start.2 = (f32[1,8,32,128]{3,2,1,0:T(8,128)S(1)}, f32[1,8,32,128]{3,2,1,0:T(8,128)}, u32[]{:S(2)}) copy-start(f32[1,8,32,128]{3,2,1,0:T(8,128)} %param.14) | copy-start | bytes 393220
  15.1 7.1 %collective-permute-start.2 = (f32[2,7,32,128]{3,2,1,0:T(8,128)S(1)}, f32[2,7,32,128]{3,2,1,0:T(8,128)S(1)}, u32[]{:S(2)}, u32[]{:S(2)}) collective-permute-start(f32[2,7,32,128]{3,2,1,0:T(8,128)S(1)} %get-tuple-element.61), channel_id=1, source_target_pairs={{0,1},{1,2},{2,3},{3,4},{4,5},{5,6},{6,7},{7,8},{8,9},{9,10},{10,1... | collective-permute-start | bytes 688136 | tf_op jit(solution)/shard_map/ppermute | solution.py:18
  17.0 8.1 %collective-permute-start.3 = (f32[2,7,32,128]{3,2,1,0:T(8,128)S(1)}, f32[2,7,32,128]{3,2,1,0:T(8,128)S(1)}, u32[]{:S(2)}, u32[]{:S(2)}) collective-permute-start(f32[2,7,32,128]{3,2,1,0:T(8,128)S(1)} %get-tuple-element.62), channel_id=1, source_target_pairs={{1,0},{2,1},{3,2},{4,3},{5,4},{6,5},{7,6},{8,7},{9,8},{10,9},{11,1... | collective-permute-start | bytes 688136 | tf_op jit(solution)/shard_map/ppermute | solution.py:19
  26.6 6.3 %collective-permute-start.4 = (f32[1,7,32,128]{3,2,1,0:T(8,128)S(1)}, f32[1,7,32,128]{3,2,1,0:T(8,128)S(1)}, u32[]{:S(2)}, u32[]{:S(2)}) collective-permute-start(f32[1,7,32,128]{3,2,1,0:T(8,128)S(1)} %get-tuple-element.75), channel_id=1, source_target_pairs={{0,1},{1,2},{2,3},{3,4},{4,5},{5,6},{6,7},{7,8},{8,9},{9,10},{10,1... | collective-permute-start | bytes 344072 | tf_op jit(solution)/shard_map/ppermute | solution.py:18
  28.5 7.0 %collective-permute-start.5 = (f32[1,7,32,128]{3,2,1,0:T(8,128)S(1)}, f32[1,7,32,128]{3,2,1,0:T(8,128)S(1)}, u32[]{:S(2)}, u32[]{:S(2)}) collective-permute-start(f32[1,7,32,128]{3,2,1,0:T(8,128)S(1)} %get-tuple-element.76), channel_id=1, source_target_pairs={{1,0},{2,1},{3,2},{4,3},{5,4},{6,5},{7,6},{8,7},{9,8},{10,9},{11,1... | collective-permute-start | bytes 344072 | tf_op jit(solution)/shard_map/ppermute | solution.py:19
  36.8 6.3 %collective-permute-start.6 = (f32[1,7,32,128]{3,2,1,0:T(8,128)S(1)}, f32[1,7,32,128]{3,2,1,0:T(8,128)S(1)}, u32[]{:S(2)}, u32[]{:S(2)}) collective-permute-start(f32[1,7,32,128]{3,2,1,0:T(8,128)S(1)} %get-tuple-element.73), channel_id=1, source_target_pairs={{0,1},{1,2},{2,3},{3,4},{4,5},{5,6},{6,7},{7,8},{8,9},{9,10},{10,1... | collective-permute-start | bytes 344072 | tf_op jit(solution)/shard_map/ppermute | solution.py:18
  38.7 7.0 %collective-permute-start.7 = (f32[1,7,32,128]{3,2,1,0:T(8,128)S(1)}, f32[1,7,32,128]{3,2,1,0:T(8,128)S(1)}, u32[]{:S(2)}, u32[]{:S(2)}) collective-permute-start(f32[1,7,32,128]{3,2,1,0:T(8,128)S(1)} %get-tuple-element.74), channel_id=1, source_target_pairs={{1,0},{2,1},{3,2},{4,3},{5,4},{6,5},{7,6},{8,7},{9,8},{10,9},{11,1... | collective-permute-start | bytes 344072 | tf_op jit(solution)/shard_map/ppermute | solution.py:19
  46.6 1.6 %copy-start.8 = (f32[1,4,2048]{2,1,0:T(4,128)S(1)}, f32[1,4,2048]{2,1,0:T(4,128)}, u32[]{:S(2)}) copy-start(f32[1,4,2048]{2,1,0:T(4,128)} %param.19) | copy-start | bytes 98308
  48.3 2.5 %copy-start.5 = (f32[1,8,32,128]{3,2,1,0:T(8,128)S(1)}, f32[1,8,32,128]{3,2,1,0:T(8,128)}, u32[]{:S(2)}) copy-start(f32[1,8,32,128]{3,2,1,0:T(8,128)} %param.15) | copy-start | bytes 393220
  51.3 9.4 %collective-permute-start.10 = (f32[1]{0:T(128)}, f32[1]{0:T(128)}, u32[]{:S(2)}, u32[]{:S(2)}) collective-permute-start(f32[1]{0:T(128)} %bitcast.31), channel_id=1, source_target_pairs={{0,8},{1,9},{2,10},{3,11},{4,12},{5,13},{6,14},{7,15},{8,0},{9,1},... | collective-permute-start | bytes 20 | tf_op jit(solution)/shard_map/ppermute | solution.py:36
  54.4 6.9 %collective-permute-start.8 = (f32[1,7,32,128]{3,2,1,0:T(8,128)S(1)}, f32[1,7,32,128]{3,2,1,0:T(8,128)S(1)}, u32[]{:S(2)}, u32[]{:S(2)}) collective-permute-start(f32[1,7,32,128]{3,2,1,0:T(8,128)S(1)} %get-tuple-element.71), channel_id=1, source_target_pairs={{0,1},{1,2},{2,3},{3,4},{4,5},{5,6},{6,7},{7,8},{8,9},{9,10},{10,1... | collective-permute-start | bytes 344072 | tf_op jit(solution)/shard_map/ppermute | solution.py:18
  57.0 6.3 %collective-permute-start.9 = (f32[1,7,32,128]{3,2,1,0:T(8,128)S(1)}, f32[1,7,32,128]{3,2,1,0:T(8,128)S(1)}, u32[]{:S(2)}, u32[]{:S(2)}) collective-permute-start(f32[1,7,32,128]{3,2,1,0:T(8,128)S(1)} %get-tuple-element.72), channel_id=1, source_target_pairs={{1,0},{2,1},{3,2},{4,3},{5,4},{6,5},{7,6},{8,7},{9,8},{10,9},{11,1... | collective-permute-start | bytes 344072 | tf_op jit(solution)/shard_map/ppermute | solution.py:19
  63.9 8.2 %collective-permute-start.13 = (f32[1]{0:T(128)}, f32[1]{0:T(128)}, u32[]{:S(2)}, u32[]{:S(2)}) collective-permute-start(f32[1]{0:T(128)} %add.718), channel_id=1, source_target_pairs={{0,4},{1,5},{2,6},{3,7},{4,0},{5,1},{6,2},{7,3},{8,12},{9,13},{10,... | collective-permute-start | bytes 20 | tf_op jit(solution)/shard_map/ppermute | solution.py:36
  65.2 7.5 %collective-permute-start.11 = (f32[1,7,32,128]{3,2,1,0:T(8,128)S(1)}, f32[1,7,32,128]{3,2,1,0:T(8,128)S(1)}, u32[]{:S(2)}, u32[]{:S(2)}) collective-permute-start(f32[1,7,32,128]{3,2,1,0:T(8,128)S(1)} %get-tuple-element.69), channel_id=1, source_target_pairs={{0,1},{1,2},{2,3},{3,4},{4,5},{5,6},{6,7},{7,8},{8,9},{9,10},{10,1... | collective-permute-start | bytes 344072 | tf_op jit(solution)/shard_map/ppermute | solution.py:18
  67.8 6.5 %collective-permute-start.12 = (f32[1,7,32,128]{3,2,1,0:T(8,128)S(1)}, f32[1,7,32,128]{3,2,1,0:T(8,128)S(1)}, u32[]{:S(2)}, u32[]{:S(2)}) collective-permute-start(f32[1,7,32,128]{3,2,1,0:T(8,128)S(1)} %get-tuple-element.70), channel_id=1, source_target_pairs={{1,0},{2,1},{3,2},{4,3},{5,4},{6,5},{7,6},{8,7},{9,8},{10,9},{11,1... | collective-permute-start | bytes 344072 | tf_op jit(solution)/shard_map/ppermute | solution.py:19
  74.6 12.4 %copy-start.3 = (f32[1,8,32,128]{3,2,1,0:T(8,128)}, f32[1,8,32,128]{3,2,1,0:T(8,128)S(1)}, u32[]{:S(2)}) copy-start(f32[1,8,32,128]{3,2,1,0:T(8,128)S(1)} %fusion.482) | copy-start | bytes 393220
  74.9 9.4 %collective-permute-start.16 = (f32[1]{0:T(128)}, f32[1]{0:T(128)}, u32[]{:S(2)}, u32[]{:S(2)}) collective-permute-start(f32[1]{0:T(128)} %add.742), channel_id=1, source_target_pairs={{0,2},{1,3},{2,0},{3,1},{4,6},{5,7},{6,4},{7,5},{8,10},{9,11},{10,... | collective-permute-start | bytes 20 | tf_op jit(solution)/shard_map/ppermute | solution.py:36
  78.4 8.3 %collective-permute-start.14 = (f32[1,7,32,128]{3,2,1,0:T(8,128)S(1)}, f32[1,7,32,128]{3,2,1,0:T(8,128)S(1)}, u32[]{:S(2)}, u32[]{:S(2)}) collective-permute-start(f32[1,7,32,128]{3,2,1,0:T(8,128)S(1)} %get-tuple-element.67), channel_id=1, source_target_pairs={{0,1},{1,2},{2,3},{3,4},{4,5},{5,6},{6,7},{7,8},{8,9},{9,10},{10,1... | collective-permute-start | bytes 344072 | tf_op jit(solution)/shard_map/ppermute | solution.py:18
  80.3 6.4 %collective-permute-start.15 = (f32[1,7,32,128]{3,2,1,0:T(8,128)S(1)}, f32[1,7,32,128]{3,2,1,0:T(8,128)S(1)}, u32[]{:S(2)}, u32[]{:S(2)}) collective-permute-start(f32[1,7,32,128]{3,2,1,0:T(8,128)S(1)} %get-tuple-element.68), channel_id=1, source_target_pairs={{1,0},{2,1},{3,2},{4,3},{5,4},{6,5},{7,6},{8,7},{9,8},{10,9},{11,1... | collective-permute-start | bytes 344072 | tf_op jit(solution)/shard_map/ppermute | solution.py:19
  84.9 1.3 %collective-permute-start.17 = (f32[1]{0:T(128)}, f32[1]{0:T(128)}, u32[]{:S(2)}, u32[]{:S(2)}) collective-permute-start(f32[1]{0:T(128)} %add.766), channel_id=1, source_target_pairs={{0,1},{1,0},{2,3},{3,2},{4,5},{5,4},{6,7},{7,6},{8,9},{9,8},{10,11... | collective-permute-start | bytes 20 | tf_op jit(solution)/shard_map/ppermute | solution.py:36

commit v26 on v19

--- a/solution.py
+++ b/solution.py
@@ -135,7 +135,7 @@
     def injected(amounts):
         spread = jnp.where(col_pick, amounts[:, :, None], 0.0)
         added = jnp.einsum("srk,srz->skz", row_pick, spread, precision=lax.Precision.HIGHEST)
-        return lax.optimization_barrier(added.reshape(shape))
+        return added.reshape(shape)
 
     before, current = (wave_prev, wave_now)
     laps = []

time: 89.6 us -> 92.9 us (1.037)
  waiting for transfers between devices: 15.5 us -> 19.3 us
    ppermute x7, waiting for transfers between devices: 15.2 us -> 18.9 us  [extended(): after = lax.ppermute(first, 'mp', down)]
  transfers between devices with their start and end apart: 18 -> 18, of which waited for: 8 -> 8; matrix products, arithmetic and copies ran while one was open for 14% -> 10% of each run, Pallas kernels for 0% -> 0%
where the time goes in v26:
time: 92.9 us; the launch traced here: 91.5 us
  starting transfers between devices  42.2 us (45%)
  waiting for transfers between devices  19.3 us (21%)
  other arithmetic  11.7 us (13%)
  matrix products  11.5 us (12%)
  between operations  6.01 us (6%)
    ppermute x7, waiting for transfers between devices, extended(): after = lax.ppermute(first, 'mp', down)  18.9 us
    ppermute x7, starting transfers between devices, extended(): before = lax.ppermute(last, 'mp', up)  17.6 us
    ppermute x7, starting transfers between devices, extended(): after = lax.ppermute(first, 'mp', down)  15.6 us
    ppermute x4, starting transfers between devices, butterfly_round(): return values + lax.ppermute(values, axis, pairs)  8.97 us
    dot_general x4, matrix products, sample(): jnp.einsum('srk,skz->srz', row_pick, field.reshape(shots, rows, cz), prec...  6.43 us
    dot_general x4, matrix products, injected(): jnp.einsum('srk,srz->skz', row_pick, spread, precision=lax.Precision.HIGH...  5.04 us
    add x4, other arithmetic, local(): following = following + jnp.where(source_hit, amount, 0.0)  2.94 us
    mul x7, other arithmetic, cross_terms(): flux = buoyancy * forward_diff(pad_axis(values, axis), axis, length)  2.4 us
  transfers between devices with their start and end apart: 18, of which 8 were waited for; matrix products, arithmetic and copies ran while one was open for 10% of the time, Pallas kernels for 0%

profile of v26, /device:TPU:1, one launch (start us, length us, event | category | flops | bytes accessed | tf_op | source)
XLA Modules:
  0.0 91.5 jit_solution(3276933964993812926)
XLA Ops:
  0.7 1.1 %pad_maximum_fusion.12 = (f32[2,7,32,128]{3,2,1,0:T(8,128)S(1)}, f32[2,7,32,128]{3,2,1,0:T(8,128)S(1)}) fusion(f32[1,8,32,128]{3,2,1,0:T(8,128)} %param.13, f32[1,8,32,128]{3,2,1,0:T(8,128)} %bitcast.129), kind=kLoop, calls=%fused_computation.335 | loop fusion | flops 114688 | bytes 720896 | tf_op jit(solution)/shard_map/concatenate | solution.py:99
  1.9 4.7 %collective-permute-start = (f32[2,7,32,128]{3,2,1,0:T(8,128)S(1)}, f32[2,7,32,128]{3,2,1,0:T(8,128)S(1)}, u32[]{:S(2)}, u32[]{:S(2)}) collective-permute-start(f32[2,7,32,128]{3,2,1,0:T(8,128)S(1)} %get-tuple-element.62), channel_id=1, source_target_pairs={{0,1},{1,2},{2,3},{3,4},{4,5},{5,6},{6,7},{7,8},{8,9},{9,10},{10,1... | collective-permute-start | bytes 688136 | tf_op jit(solution)/shard_map/ppermute | solution.py:18
  6.5 1.9 %collective-permute-start.1 = (f32[2,7,32,128]{3,2,1,0:T(8,128)S(1)}, f32[2,7,32,128]{3,2,1,0:T(8,128)S(1)}, u32[]{:S(2)}, u32[]{:S(2)}) collective-permute-start(f32[2,7,32,128]{3,2,1,0:T(8,128)S(1)} %get-tuple-element.61), channel_id=1, source_target_pairs={{1,0},{2,1},{3,2},{4,3},{5,4},{6,5},{7,6},{8,7},{9,8},{10,9},{11,1... | collective-permute-start | bytes 688136 | tf_op jit(solution)/shard_map/ppermute | solution.py:19
  8.5 0.3 fusion.345
  8.8 0.3 fusion.213
  9.8 0.6 fusion.559
  10.6 3.3 %collective-permute-done.1 = f32[2,7,32,128]{3,2,1,0:T(8,128)S(1)} collective-permute-done((f32[2,7,32,128]{3,2,1,0:T(8,128)S(1)}, f32[2,7,32,128]{3,2,1,0:T(8,128)S(1)}, u32[]{:S(2)}, u32[]{:S(2)}) %collective-permute-start.1) | collective-permute-done | bytes 229408 | tf_op jit(solution)/shard_map/ppermute | solution.py:19
  13.9 0.1 slice_bitcast_fusion
  14.1 0.8 fusion.534
  14.8 0.1 copy-done.4
  15.1 1.9 %collective-permute-start.2 = (f32[2,7,32,128]{3,2,1,0:T(8,128)S(1)}, f32[2,7,32,128]{3,2,1,0:T(8,128)S(1)}, u32[]{:S(2)}, u32[]{:S(2)}) collective-permute-start(f32[2,7,32,128]{3,2,1,0:T(8,128)S(1)} %get-tuple-element.59), channel_id=1, source_target_pairs={{0,1},{1,2},{2,3},{3,4},{4,5},{5,6},{6,7},{7,8},{8,9},{9,10},{10,1... | collective-permute-start | bytes 688136 | tf_op jit(solution)/shard_map/ppermute | solution.py:18
  17.0 2.4 %collective-permute-start.3 = (f32[2,7,32,128]{3,2,1,0:T(8,128)S(1)}, f32[2,7,32,128]{3,2,1,0:T(8,128)S(1)}, u32[]{:S(2)}, u32[]{:S(2)}) collective-permute-start(f32[2,7,32,128]{3,2,1,0:T(8,128)S(1)} %get-tuple-element.60), channel_id=1, source_target_pairs={{1,0},{2,1},{3,2},{4,3},{5,4},{6,5},{7,6},{8,7},{9,8},{10,9},{11,1... | collective-permute-start | bytes 688136 | tf_op jit(solution)/shard_map/ppermute | solution.py:19
  19.4 0.5 fusion.118
  20.0 0.5 fusion.106
  20.5 1.6 %fusion.16 = f32[2048]{0:T(1024)S(1)} fusion(f32[256,128]{1,0:T(8,128)S(1)} %bitcast.133, s32[2048]{0:T(1024)S(1)} %bitcast.152, s32[2048]{0:T(1024)S(1)} %bitcast.144), kind=kOutput, calls=%fused_computation.15 | convolution fusion | flops 806615040 | bytes 155648 | tf_op jit(solution)/shard_map/srk,skz->srz/dot_general | solution.py:130
  22.1 3.0 %collective-permute-done.3 = f32[2,7,32,128]{3,2,1,0:T(8,128)S(1)} collective-permute-done((f32[2,7,32,128]{3,2,1,0:T(8,128)S(1)}, f32[2,7,32,128]{3,2,1,0:T(8,128)S(1)}, u32[]{:S(2)}, u32[]{:S(2)}) %collective-permute-start.3) | collective-permute-done | bytes 229408 | tf_op jit(solution)/shard_map/ppermute | solution.py:19
  25.2 0.2 fusion.84
  25.4 0.1 fusion.138
  25.5 0.7 fusion.536
  26.3 0.3 fusion.368
  26.6 1.9 %collective-permute-start.4 = (f32[1,7,32,128]{3,2,1,0:T(8,128)S(1)}, f32[1,7,32,128]{3,2,1,0:T(8,128)S(1)}, u32[]{:S(2)}, u32[]{:S(2)}) collective-permute-start(f32[1,7,32,128]{3,2,1,0:T(8,128)S(1)} %get-tuple-element.73), channel_id=1, source_target_pairs={{0,1},{1,2},{2,3},{3,4},{4,5},{5,6},{6,7},{7,8},{8,9},{9,10},{10,1... | collective-permute-start | bytes 344072 | tf_op jit(solution)/shard_map/ppermute | solution.py:18
  28.5 2.4 %collective-permute-start.5 = (f32[1,7,32,128]{3,2,1,0:T(8,128)S(1)}, f32[1,7,32,128]{3,2,1,0:T(8,128)S(1)}, u32[]{:S(2)}, u32[]{:S(2)}) collective-permute-start(f32[1,7,32,128]{3,2,1,0:T(8,128)S(1)} %get-tuple-element.74), channel_id=1, source_target_pairs={{1,0},{2,1},{3,2},{4,3},{5,4},{6,5},{7,6},{8,7},{9,8},{10,9},{11,1... | collective-permute-start | bytes 344072 | tf_op jit(solution)/shard_map/ppermute | solution.py:19
  30.9 0.3 fusion.237
  31.2 1.6 %fusion.19 = f32[2048]{0:T(1024)S(1)} fusion(f32[256,128]{1,0:T(8,128)S(1)} %bitcast.132, s32[2048]{0:T(1024)S(1)} %bitcast.153, s32[2048]{0:T(1024)S(1)} %bitcast.145), kind=kOutput, calls=%fused_computation.16 | convolution fusion | flops 806615040 | bytes 155648 | tf_op jit(solution)/shard_map/srk,skz->srz/dot_general | solution.py:130
  32.9 2.7 %collective-permute-done.5 = f32[1,7,32,128]{3,2,1,0:T(8,128)S(1)} collective-permute-done((f32[1,7,32,128]{3,2,1,0:T(8,128)S(1)}, f32[1,7,32,128]{3,2,1,0:T(8,128)S(1)}, u32[]{:S(2)}, u32[]{:S(2)}) %collective-permute-start.5) | collective-permute-done | bytes 114720 | tf_op jit(solution)/shard_map/ppermute | solution.py:19
  35.6 0.1 fusion.175
  35.7 0.7 fusion.538
  36.4 0.3 fusion.391
  36.7 1.9 %collective-permute-start.6 = (f32[1,7,32,128]{3,2,1,0:T(8,128)S(1)}, f32[1,7,32,128]{3,2,1,0:T(8,128)S(1)}, u32[]{:S(2)}, u32[]{:S(2)}) collective-permute-start(f32[1,7,32,128]{3,2,1,0:T(8,128)S(1)} %get-tuple-element.71), channel_id=1, source_target_pairs={{0,1},{1,2},{2,3},{3,4},{4,5},{5,6},{6,7},{7,8},{8,9},{9,10},{10,1... | collective-permute-start | bytes 344072 | tf_op jit(solution)/shard_map/ppermute | solution.py:18
  38.6 2.4 %collective-permute-start.7 = (f32[1,7,32,128]{3,2,1,0:T(8,128)S(1)}, f32[1,7,32,128]{3,2,1,0:T(8,128)S(1)}, u32[]{:S(2)}, u32[]{:S(2)}) collective-permute-start(f32[1,7,32,128]{3,2,1,0:T(8,128)S(1)} %get-tuple-element.72), channel_id=1, source_target_pairs={{1,0},{2,1},{3,2},{4,3},{5,4},{6,5},{7,6},{8,7},{9,8},{10,9},{11,1... | collective-permute-start | bytes 344072 | tf_op jit(solution)/shard_map/ppermute | solution.py:19
  41.0 0.3 fusion.261
  41.3 1.6 %fusion.22 = f32[2048]{0:T(1024)S(1)} fusion(f32[256,128]{1,0:T(8,128)S(1)} %bitcast.134, s32[2048]{0:T(1024)S(1)} %bitcast.154, s32[2048]{0:T(1024)S(1)} %bitcast.146), kind=kOutput, calls=%fused_computation.17 | convolution fusion | flops 806615040 | bytes 155648 | tf_op jit(solution)/shard_map/srk,skz->srz/dot_general | solution.py:130
  42.9 2.7 %collective-permute-done.7 = f32[1,7,32,128]{3,2,1,0:T(8,128)S(1)} collective-permute-done((f32[1,7,32,128]{3,2,1,0:T(8,128)S(1)}, f32[1,7,32,128]{3,2,1,0:T(8,128)S(1)}, u32[]{:S(2)}, u32[]{:S(2)}) %collective-permute-start.7) | collective-permute-done | bytes 114720 | tf_op jit(solution)/shard_map/ppermute | solution.py:19
  45.6 0.1 fusion.168
  45.7 0.7 fusion.540
  46.5 1.6 %fusion.13 = f32[2048]{0:T(1024)S(1)} fusion(f32[256,128]{1,0:T(8,128)S(1)} %bitcast.135, s32[2048]{0:T(1024)S(1)} %bitcast.155, s32[2048]{0:T(1024)S(1)} %bitcast.147), kind=kOutput, calls=%fused_computation.14 | convolution fusion | flops 806615040 | bytes 155648 | tf_op jit(solution)/shard_map/srk,skz->srz/dot_general | solution.py:130
  48.2 0.6 fusion.541
  49.5 1.3 %fusion.46 = f32[1,8,32,128]{3,2,1,0:T(8,128)S(1)} fusion(s32[8,32]{1,0:T(8,128)S(1)} %multiply_add_fusion, s32[2048]{0:T(1024)S(1)} %bitcast.156, f32[2048]{0:T(1024)S(1)} %bitcast.143, s32[2048]{0:T(1024)S(1)} %bitcast.148, f32[1,8,32,128]{3,2,1,0:T(8,128)S(1)} %copy-done.10, f32[2,8,32,128]{3,2,1,0:T(8,128)S(1)} %fusion.138, ...), kind=kOutput, calls=%fused_computation.25 | convolution fusion | flops 806486016 | bytes 549888 | tf_op jit(solution)/shard_map/srk,srz->skz/dot_general | solution.py:137
  50.8 0.3 fusion.414
  51.1 3.0 %collective-permute-start.10 = (f32[1]{0:T(128)}, f32[1]{0:T(128)}, u32[]{:S(2)}, u32[]{:S(2)}) collective-permute-start(f32[1]{0:T(128)} %bitcast.31), channel_id=1, source_target_pairs={{0,2},{1,3},{2,0},{3,1},{4,6},{5,7},{6,4},{7,5},{8,10},{9,11},{10,... | collective-permute-start | bytes 20 | tf_op jit(solution)/shard_map/ppermute | solution.py:36
  54.2 1.9 %collective-permute-start.8 = (f32[1,7,32,128]{3,2,1,0:T(8,128)S(1)}, f32[1,7,32,128]{3,2,1,0:T(8,128)S(1)}, u32[]{:S(2)}, u32[]{:S(2)}) collective-permute-start(f32[1,7,32,128]{3,2,1,0:T(8,128)S(1)} %get-tuple-element.69), channel_id=1, source_target_pairs={{0,1},{1,2},{2,3},{3,4},{4,5},{5,6},{6,7},{7,8},{8,9},{9,10},{10,1... | collective-permute-start | bytes 344072 | tf_op jit(solution)/shard_map/ppermute | solution.py:18
  56.1 2.6 %collective-permute-start.9 = (f32[1,7,32,128]{3,2,1,0:T(8,128)S(1)}, f32[1,7,32,128]{3,2,1,0:T(8,128)S(1)}, u32[]{:S(2)}, u32[]{:S(2)}) collective-permute-start(f32[1,7,32,128]{3,2,1,0:T(8,128)S(1)} %get-tuple-element.70), channel_id=1, source_target_pairs={{1,0},{2,1},{3,2},{4,3},{5,4},{6,5},{7,6},{8,7},{9,8},{10,9},{11,1... | collective-permute-start | bytes 344072 | tf_op jit(solution)/shard_map/ppermute | solution.py:19
  58.7 0.3 fusion.285
  59.6 2.6 %collective-permute-done.9 = f32[1,7,32,128]{3,2,1,0:T(8,128)S(1)} collective-permute-done((f32[1,7,32,128]{3,2,1,0:T(8,128)S(1)}, f32[1,7,32,128]{3,2,1,0:T(8,128)S(1)}, u32[]{:S(2)}, u32[]{:S(2)}) %collective-permute-start.9) | collective-permute-done | bytes 114720 | tf_op jit(solution)/shard_map/ppermute | solution.py:19
  62.3 1.3 %fusion.43 = f32[1,8,32,128]{3,2,1,0:T(8,128)S(1)} fusion(s32[8,32]{1,0:T(8,128)S(1)} %multiply_add_fusion, s32[2048]{0:T(1024)S(1)} %bitcast.157, f32[2048]{0:T(1024)S(1)} %bitcast.141, s32[2048]{0:T(1024)S(1)} %bitcast.149, f32[1,8,32,128]{3,2,1,0:T(8,128)S(1)} %copy-done.4, f32[1,8,32,128]{3,2,1,0:T(8,128)S(1)} %fusion.285, ...), kind=kOutput, calls=%fused_computation.24 | convolution fusion | flops 806879232 | bytes 1598464 | tf_op jit(solution)/shard_map/srk,srz->skz/dot_general | solution.py:137
  63.7 0.3 fusion.437
  64.0 2.1 %collective-permute-start.13 = (f32[1]{0:T(128)}, f32[1]{0:T(128)}, u32[]{:S(2)}, u32[]{:S(2)}) collective-permute-start(f32[1]{0:T(128)} %add.718), channel_id=1, source_target_pairs={{0,4},{1,5},{2,6},{3,7},{4,0},{5,1},{6,2},{7,3},{8,12},{9,13},{10,... | collective-permute-start | bytes 20 | tf_op jit(solution)/shard_map/ppermute | solution.py:36
  66.1 2.6 %collective-permute-start.11 = (f32[1,7,32,128]{3,2,1,0:T(8,128)S(1)}, f32[1,7,32,128]{3,2,1,0:T(8,128)S(1)}, u32[]{:S(2)}, u32[]{:S(2)}) collective-permute-start(f32[1,7,32,128]{3,2,1,0:T(8,128)S(1)} %get-tuple-element.67), channel_id=1, source_target_pairs={{0,1},{1,2},{2,3},{3,4},{4,5},{5,6},{6,7},{7,8},{8,9},{9,10},{10,1... | collective-permute-start | bytes 344072 | tf_op jit(solution)/shard_map/ppermute | solution.py:18
  68.7 1.9 %collective-permute-start.12 = (f32[1,7,32,128]{3,2,1,0:T(8,128)S(1)}, f32[1,7,32,128]{3,2,1,0:T(8,128)S(1)}, u32[]{:S(2)}, u32[]{:S(2)}) collective-permute-start(f32[1,7,32,128]{3,2,1,0:T(8,128)S(1)} %get-tuple-element.68), channel_id=1, source_target_pairs={{1,0},{2,1},{3,2},{4,3},{5,4},{6,5},{7,6},{8,7},{9,8},{10,9},{11,1... | collective-permute-start | bytes 344072 | tf_op jit(solution)/shard_map/ppermute | solution.py:19
  70.6 0.3 fusion.309
  71.5 3.3 %collective-permute-done.12 = f32[1,7,32,128]{3,2,1,0:T(8,128)S(1)} collective-permute-done((f32[1,7,32,128]{3,2,1,0:T(8,128)S(1)}, f32[1,7,32,128]{3,2,1,0:T(8,128)S(1)}, u32[]{:S(2)}, u32[]{:S(2)}) %collective-permute-start.12) | collective-permute-done | bytes 114720 | tf_op jit(solution)/shard_map/ppermute | solution.py:19
  74.9 0.1 fusion.154
  75.0 1.3 %fusion.40 = f32[1,8,32,128]{3,2,1,0:T(8,128)S(1)} fusion(s32[8,32]{1,0:T(8,128)S(1)} %multiply_add_fusion, s32[2048]{0:T(1024)S(1)} %bitcast.158, f32[2048]{0:T(1024)S(1)} %bitcast.139, s32[2048]{0:T(1024)S(1)} %bitcast.150, f32[1,8,32,128]{3,2,1,0:T(8,128)S(1)} %fusion.46, f32[1,8,32,128]{3,2,1,0:T(8,128)S(1)} %fusion.309, ...), kind=kOutput, calls=%fused_computation.23 | convolution fusion | flops 806879232 | bytes 1598464 | tf_op jit(solution)/shard_map/srk,srz->skz/dot_general | solution.py:137
  76.3 0.3 fusion.460
  76.6 2.8 %collective-permute-start.16 = (f32[1]{0:T(128)}, f32[1]{0:T(128)}, u32[]{:S(2)}, u32[]{:S(2)}) collective-permute-start(f32[1]{0:T(128)} %add.742), channel_id=1, source_target_pairs={{0,8},{1,9},{2,10},{3,11},{4,12},{5,13},{6,14},{7,15},{8,0},{9,1},... | collective-permute-start | bytes 20 | tf_op jit(solution)/shard_map/ppermute | solution.py:36
  79.4 2.6 %collective-permute-start.14 = (f32[1,7,32,128]{3,2,1,0:T(8,128)S(1)}, f32[1,7,32,128]{3,2,1,0:T(8,128)S(1)}, u32[]{:S(2)}, u32[]{:S(2)}) collective-permute-start(f32[1,7,32,128]{3,2,1,0:T(8,128)S(1)} %get-tuple-element.65), channel_id=1, source_target_pairs={{0,1},{1,2},{2,3},{3,4},{4,5},{5,6},{6,7},{7,8},{8,9},{9,10},{10,1... | collective-permute-start | bytes 344072 | tf_op jit(solution)/shard_map/ppermute | solution.py:18
  82.1 1.9 %collective-permute-start.15 = (f32[1,7,32,128]{3,2,1,0:T(8,128)S(1)}, f32[1,7,32,128]{3,2,1,0:T(8,128)S(1)}, u32[]{:S(2)}, u32[]{:S(2)}) collective-permute-start(f32[1,7,32,128]{3,2,1,0:T(8,128)S(1)} %get-tuple-element.66), channel_id=1, source_target_pairs={{1,0},{2,1},{3,2},{4,3},{5,4},{6,5},{7,6},{8,7},{9,8},{10,9},{11,1... | collective-permute-start | bytes 344072 | tf_op jit(solution)/shard_map/ppermute | solution.py:19
  84.0 0.3 fusion.333
  84.9 1.0 %collective-permute-start.17 = (f32[1]{0:T(128)}, f32[1]{0:T(128)}, u32[]{:S(2)}, u32[]{:S(2)}) collective-permute-start(f32[1]{0:T(128)} %add.766), channel_id=1, source_target_pairs={{0,1},{1,0},{2,3},{3,2},{4,5},{5,4},{6,7},{7,6},{8,9},{9,8},{10,11... | collective-permute-start | bytes 20 | tf_op jit(solution)/shard_map/ppermute | solution.py:36
  85.9 0.3 collective-permute-done.17
  86.8 1.4 %collective-permute-done.15 = f32[1,7,32,128]{3,2,1,0:T(8,128)S(1)} collective-permute-done((f32[1,7,32,128]{3,2,1,0:T(8,128)S(1)}, f32[1,7,32,128]{3,2,1,0:T(8,128)S(1)}, u32[]{:S(2)}, u32[]{:S(2)}) %collective-permute-start.15) | collective-permute-done | bytes 114720 | tf_op jit(solution)/shard_map/ppermute | solution.py:19
  88.2 0.1 fusion.147
  88.3 1.3 %fusion.37 = f32[1,8,32,128]{3,2,1,0:T(8,128)S(1)} fusion(s32[8,32]{1,0:T(8,128)S(1)} %multiply_add_fusion, s32[2048]{0:T(1024)S(1)} %bitcast.159, f32[2048]{0:T(1024)S(1)} %bitcast.137, s32[2048]{0:T(1024)S(1)} %bitcast.151, f32[1,8,32,128]{3,2,1,0:T(8,128)S(1)} %fusion.43, f32[1,8,32,128]{3,2,1,0:T(8,128)S(1)} %fusion.333, ...), kind=kOutput, calls=%fused_computation.22 | convolution fusion | flops 806879232 | bytes 1598464 | tf_op jit(solution)/shard_map/srk,srz->skz/dot_general | solution.py:137
  89.6 0.8 bitcast_multiply_fusion
  (57 shorter events, 0.8 us)
Async XLA Ops:
  0.6 7.9 %copy-start = (f32[8,32,128]{2,1,0:T(8,128)S(1)}, f32[8,32,128]{2,1,0:T(8,128)}, u32[]{:S(2)}) copy-start(f32[8,32,128]{2,1,0:T(8,128)} %param.11) | copy-start | bytes 393220
  0.6 7.9 %copy-start.1 = (f32[1,8,32,128]{3,2,1,0:T(8,128)S(1)}, f32[1,8,32,128]{3,2,1,0:T(8,128)}, u32[]{:S(2)}) copy-start(f32[1,8,32,128]{3,2,1,0:T(8,128)} %param.13) | copy-start | bytes 393220
  0.7 7.9 %copy-start.6 = (f32[1,8,32,128]{3,2,1,0:T(8,128)S(1)}, f32[1,8,32,128]{3,2,1,0:T(8,128)}, u32[]{:S(2)}) copy-start(f32[1,8,32,128]{3,2,1,0:T(8,128)} %param.12) | copy-start | bytes 393220
  1.8 8.0 %copy-start.9 = (f32[1,4]{1,0:T(1,128)S(1)}, f32[1,4]{1,0:T(1,128)}, u32[]{:S(2)}) copy-start(f32[1,4]{1,0:T(1,128)} %param.17) | copy-start | bytes 52
  1.8 8.6 %copy-start.7 = (s32[1,2048]{1,0:T(1,128)S(1)}, s32[1,2048]{1,0:T(1,128)}, u32[]{:S(2)}) copy-start(s32[1,2048]{1,0:T(1,128)} %param.18) | copy-start | bytes 24580
  1.8 8.7 %copy-start.2 = (f32[8,32,128]{2,1,0:T(8,128)S(1)}, f32[8,32,128]{2,1,0:T(8,128)}, u32[]{:S(2)}) copy-start(f32[8,32,128]{2,1,0:T(8,128)} %param.10) | copy-start | bytes 393220
  1.9 8.7 %collective-permute-start = (f32[2,7,32,128]{3,2,1,0:T(8,128)S(1)}, f32[2,7,32,128]{3,2,1,0:T(8,128)S(1)}, u32[]{:S(2)}, u32[]{:S(2)}) collective-permute-start(f32[2,7,32,128]{3,2,1,0:T(8,128)S(1)} %get-tuple-element.62), channel_id=1, source_target_pairs={{0,1},{1,2},{2,3},{3,4},{4,5},{5,6},{6,7},{7,8},{8,9},{9,10},{10,1... | collective-permute-start | bytes 688136 | tf_op jit(solution)/shard_map/ppermute | solution.py:18
  6.5 7.3 %collective-permute-start.1 = (f32[2,7,32,128]{3,2,1,0:T(8,128)S(1)}, f32[2,7,32,128]{3,2,1,0:T(8,128)S(1)}, u32[]{:S(2)}, u32[]{:S(2)}) collective-permute-start(f32[2,7,32,128]{3,2,1,0:T(8,128)S(1)} %get-tuple-element.61), channel_id=1, source_target_pairs={{1,0},{2,1},{3,2},{4,3},{5,4},{6,5},{7,6},{8,7},{9,8},{10,9},{11,1... | collective-permute-start | bytes 688136 | tf_op jit(solution)/shard_map/ppermute | solution.py:19
  14.0 0.9 %copy-start.4 = (f32[1,8,32,128]{3,2,1,0:T(8,128)S(1)}, f32[1,8,32,128]{3,2,1,0:T(8,128)}, u32[]{:S(2)}) copy-start(f32[1,8,32,128]{3,2,1,0:T(8,128)} %param.14) | copy-start | bytes 393220
  15.1 7.1 %collective-permute-start.2 = (f32[2,7,32,128]{3,2,1,0:T(8,128)S(1)}, f32[2,7,32,128]{3,2,1,0:T(8,128)S(1)}, u32[]{:S(2)}, u32[]{:S(2)}) collective-permute-start(f32[2,7,32,128]{3,2,1,0:T(8,128)S(1)} %get-tuple-element.59), channel_id=1, source_target_pairs={{0,1},{1,2},{2,3},{3,4},{4,5},{5,6},{6,7},{7,8},{8,9},{9,10},{10,1... | collective-permute-start | bytes 688136 | tf_op jit(solution)/shard_map/ppermute | solution.py:18
  17.0 8.1 %collective-permute-start.3 = (f32[2,7,32,128]{3,2,1,0:T(8,128)S(1)}, f32[2,7,32,128]{3,2,1,0:T(8,128)S(1)}, u32[]{:S(2)}, u32[]{:S(2)}) collective-permute-start(f32[2,7,32,128]{3,2,1,0:T(8,128)S(1)} %get-tuple-element.60), channel_id=1, source_target_pairs={{1,0},{2,1},{3,2},{4,3},{5,4},{6,5},{7,6},{8,7},{9,8},{10,9},{11,1... | collective-permute-start | bytes 688136 | tf_op jit(solution)/shard_map/ppermute | solution.py:19
  26.6 6.3 %collective-permute-start.4 = (f32[1,7,32,128]{3,2,1,0:T(8,128)S(1)}, f32[1,7,32,128]{3,2,1,0:T(8,128)S(1)}, u32[]{:S(2)}, u32[]{:S(2)}) collective-permute-start(f32[1,7,32,128]{3,2,1,0:T(8,128)S(1)} %get-tuple-element.73), channel_id=1, source_target_pairs={{0,1},{1,2},{2,3},{3,4},{4,5},{5,6},{6,7},{7,8},{8,9},{9,10},{10,1... | collective-permute-start | bytes 344072 | tf_op jit(solution)/shard_map/ppermute | solution.py:18
  28.5 7.0 %collective-permute-start.5 = (f32[1,7,32,128]{3,2,1,0:T(8,128)S(1)}, f32[1,7,32,128]{3,2,1,0:T(8,128)S(1)}, u32[]{:S(2)}, u32[]{:S(2)}) collective-permute-start(f32[1,7,32,128]{3,2,1,0:T(8,128)S(1)} %get-tuple-element.74), channel_id=1, source_target_pairs={{1,0},{2,1},{3,2},{4,3},{5,4},{6,5},{7,6},{8,7},{9,8},{10,9},{11,1... | collective-permute-start | bytes 344072 | tf_op jit(solution)/shard_map/ppermute | solution.py:19
  36.7 6.3 %collective-permute-start.6 = (f32[1,7,32,128]{3,2,1,0:T(8,128)S(1)}, f32[1,7,32,128]{3,2,1,0:T(8,128)S(1)}, u32[]{:S(2)}, u32[]{:S(2)}) collective-permute-start(f32[1,7,32,128]{3,2,1,0:T(8,128)S(1)} %get-tuple-element.71), channel_id=1, source_target_pairs={{0,1},{1,2},{2,3},{3,4},{4,5},{5,6},{6,7},{7,8},{8,9},{9,10},{10,1... | collective-permute-start | bytes 344072 | tf_op jit(solution)/shard_map/ppermute | solution.py:18
  38.6 7.0 %collective-permute-start.7 = (f32[1,7,32,128]{3,2,1,0:T(8,128)S(1)}, f32[1,7,32,128]{3,2,1,0:T(8,128)S(1)}, u32[]{:S(2)}, u32[]{:S(2)}) collective-permute-start(f32[1,7,32,128]{3,2,1,0:T(8,128)S(1)} %get-tuple-element.72), channel_id=1, source_target_pairs={{1,0},{2,1},{3,2},{4,3},{5,4},{6,5},{7,6},{8,7},{9,8},{10,9},{11,1... | collective-permute-start | bytes 344072 | tf_op jit(solution)/shard_map/ppermute | solution.py:19
  46.5 1.6 %copy-start.8 = (f32[1,4,2048]{2,1,0:T(4,128)S(1)}, f32[1,4,2048]{2,1,0:T(4,128)}, u32[]{:S(2)}) copy-start(f32[1,4,2048]{2,1,0:T(4,128)} %param.19) | copy-start | bytes 98308
  46.5 3.0 %copy-start.10 = (f32[1,8,32,128]{3,2,1,0:T(8,128)S(1)}, f32[1,8,32,128]{3,2,1,0:T(8,128)}, u32[]{:S(2)}) copy-start(f32[1,8,32,128]{3,2,1,0:T(8,128)} %param.15) | copy-start | bytes 393220
  51.1 7.9 %collective-permute-start.10 = (f32[1]{0:T(128)}, f32[1]{0:T(128)}, u32[]{:S(2)}, u32[]{:S(2)}) collective-permute-start(f32[1]{0:T(128)} %bitcast.31), channel_id=1, source_target_pairs={{0,2},{1,3},{2,0},{3,1},{4,6},{5,7},{6,4},{7,5},{8,10},{9,11},{10,... | collective-permute-start | bytes 20 | tf_op jit(solution)/shard_map/ppermute | solution.py:36
  54.2 5.4 %collective-permute-start.8 = (f32[1,7,32,128]{3,2,1,0:T(8,128)S(1)}, f32[1,7,32,128]{3,2,1,0:T(8,128)S(1)}, u32[]{:S(2)}, u32[]{:S(2)}) collective-permute-start(f32[1,7,32,128]{3,2,1,0:T(8,128)S(1)} %get-tuple-element.69), channel_id=1, source_target_pairs={{0,1},{1,2},{2,3},{3,4},{4,5},{5,6},{6,7},{7,8},{8,9},{9,10},{10,1... | collective-permute-start | bytes 344072 | tf_op jit(solution)/shard_map/ppermute | solution.py:18
  56.1 6.1 %collective-permute-start.9 = (f32[1,7,32,128]{3,2,1,0:T(8,128)S(1)}, f32[1,7,32,128]{3,2,1,0:T(8,128)S(1)}, u32[]{:S(2)}, u32[]{:S(2)}) collective-permute-start(f32[1,7,32,128]{3,2,1,0:T(8,128)S(1)} %get-tuple-element.70), channel_id=1, source_target_pairs={{1,0},{2,1},{3,2},{4,3},{5,4},{6,5},{7,6},{8,7},{9,8},{10,9},{11,1... | collective-permute-start | bytes 344072 | tf_op jit(solution)/shard_map/ppermute | solution.py:19
  64.0 7.0 %collective-permute-start.13 = (f32[1]{0:T(128)}, f32[1]{0:T(128)}, u32[]{:S(2)}, u32[]{:S(2)}) collective-permute-start(f32[1]{0:T(128)} %add.718), channel_id=1, source_target_pairs={{0,4},{1,5},{2,6},{3,7},{4,0},{5,1},{6,2},{7,3},{8,12},{9,13},{10,... | collective-permute-start | bytes 20 | tf_op jit(solution)/shard_map/ppermute | solution.py:36
  66.1 5.5 %collective-permute-start.11 = (f32[1,7,32,128]{3,2,1,0:T(8,128)S(1)}, f32[1,7,32,128]{3,2,1,0:T(8,128)S(1)}, u32[]{:S(2)}, u32[]{:S(2)}) collective-permute-start(f32[1,7,32,128]{3,2,1,0:T(8,128)S(1)} %get-tuple-element.67), channel_id=1, source_target_pairs={{0,1},{1,2},{2,3},{3,4},{4,5},{5,6},{6,7},{7,8},{8,9},{9,10},{10,1... | collective-permute-start | bytes 344072 | tf_op jit(solution)/shard_map/ppermute | solution.py:18
  68.7 6.1 %collective-permute-start.12 = (f32[1,7,32,128]{3,2,1,0:T(8,128)S(1)}, f32[1,7,32,128]{3,2,1,0:T(8,128)S(1)}, u32[]{:S(2)}, u32[]{:S(2)}) collective-permute-start(f32[1,7,32,128]{3,2,1,0:T(8,128)S(1)} %get-tuple-element.68), channel_id=1, source_target_pairs={{1,0},{2,1},{3,2},{4,3},{5,4},{6,5},{7,6},{8,7},{9,8},{10,9},{11,1... | collective-permute-start | bytes 344072 | tf_op jit(solution)/shard_map/ppermute | solution.py:19
  76.2 13.4 %copy-start.3 = (f32[1,8,32,128]{3,2,1,0:T(8,128)}, f32[1,8,32,128]{3,2,1,0:T(8,128)S(1)}, u32[]{:S(2)}) copy-start(f32[1,8,32,128]{3,2,1,0:T(8,128)S(1)} %fusion.40) | copy-start | bytes 393220
  76.6 7.7 %collective-permute-start.16 = (f32[1]{0:T(128)}, f32[1]{0:T(128)}, u32[]{:S(2)}, u32[]{:S(2)}) collective-permute-start(f32[1]{0:T(128)} %add.742), channel_id=1, source_target_pairs={{0,8},{1,9},{2,10},{3,11},{4,12},{5,13},{6,14},{7,15},{8,0},{9,1},... | collective-permute-start | bytes 20 | tf_op jit(solution)/shard_map/ppermute | solution.py:36
  79.4 7.3 %collective-permute-start.14 = (f32[1,7,32,128]{3,2,1,0:T(8,128)S(1)}, f32[1,7,32,128]{3,2,1,0:T(8,128)S(1)}, u32[]{:S(2)}, u32[]{:S(2)}) collective-permute-start(f32[1,7,32,128]{3,2,1,0:T(8,128)S(1)} %get-tuple-element.65), channel_id=1, source_target_pairs={{0,1},{1,2},{2,3},{3,4},{4,5},{5,6},{6,7},{7,8},{8,9},{9,10},{10,1... | collective-permute-start | bytes 344072 | tf_op jit(solution)/shard_map/ppermute | solution.py:18
  82.1 6.1 %collective-permute-start.15 = (f32[1,7,32,128]{3,2,1,0:T(8,128)S(1)}, f32[1,7,32,128]{3,2,1,0:T(8,128)S(1)}, u32[]{:S(2)}, u32[]{:S(2)}) collective-permute-start(f32[1,7,32,128]{3,2,1,0:T(8,128)S(1)} %get-tuple-element.66), channel_id=1, source_target_pairs={{1,0},{2,1},{3,2},{4,3},{5,4},{6,5},{7,6},{8,7},{9,8},{10,9},{11,1... | collective-permute-start | bytes 344072 | tf_op jit(solution)/shard_map/ppermute | solution.py:19
  84.9 1.3 %collective-permute-start.17 = (f32[1]{0:T(128)}, f32[1]{0:T(128)}, u32[]{:S(2)}, u32[]{:S(2)}) collective-permute-start(f32[1]{0:T(128)} %add.766), channel_id=1, source_target_pairs={{0,1},{1,0},{2,3},{3,2},{4,5},{5,4},{6,7},{7,6},{8,9},{9,8},{10,11... | collective-permute-start | bytes 20 | tf_op jit(solution)/shard_map/ppermute | solution.py:36
  89.6 0.8 copy-start.5

commit v27 on v19

--- a/solution.py
+++ b/solution.py
@@ -132,6 +132,19 @@
         )
         return jnp.sum(jnp.where(col_pick, picked, 0.0), axis=2)
 
+    def sample_split(field):
+        values = field.reshape(shots, rows, cz)
+        high = lax.reduce_precision(values, exponent_bits=8, mantissa_bits=7)
+        rest = values - high
+        middle = lax.reduce_precision(rest, exponent_bits=8, mantissa_bits=7)
+        low = lax.reduce_precision(rest - middle, exponent_bits=8, mantissa_bits=7)
+        pieces = jnp.concatenate([high, middle, low], axis=-1).astype(jnp.bfloat16)
+        picked = jnp.einsum(
+            "srk,skz->srz", row_pick.astype(jnp.bfloat16), pieces, preferred_element_type=jnp.float32
+        )
+        picked = (picked[..., :cz] + picked[..., cz : 2 * cz]) + picked[..., 2 * cz :]
+        return jnp.sum(jnp.where(col_pick, picked, 0.0), axis=2)
+
     def injected(amounts):
         spread = jnp.where(col_pick, amounts[:, :, None], 0.0)
         added = jnp.einsum("srk,srz->skz", row_pick, spread, precision=lax.Precision.HIGHEST)
@@ -152,7 +165,7 @@
         following = (first_base if step == 0 else 2.0 * current - before) + kappa * lap
         amount = wavelet[:, step].reshape(shots, 1, 1, 1)
         following = following + jnp.where(source_hit, amount, 0.0)
-        sampled = sample(following)
+        sampled = sample_split(following) if step == STEPS - 1 else sample(following)
         resids.append(jnp.where(receiver_owned, sampled - observed[:, step, :], 0.0))
         before, current = (current, following)
     stacked = jnp.stack(resids, axis=1)

time: 89.6 us -> 93.3 us (1.041)
  other arithmetic: 12.1 us -> 17.8 us
  waiting for transfers between devices: 15.5 us -> 12.6 us
  local copies, waits for them, and re-layouts: 0.86 us -> 2.65 us
    mul x7, other arithmetic: 2.4 us -> 5.37 us  [cross_terms(): flux = buoyancy * forward_diff(pad_axis(values, axis), axis, length)]
    ppermute x7, waiting for transfers between devices: 15.2 us -> 12.3 us  [extended(): after = lax.ppermute(first, 'mp', down)]
    dot_general x4 -> x3, matrix products: 6.43 us -> 4.82 us  [sample(): jnp.einsum('srk,skz->srz', row_pick, field.reshape(shots, rows, cz), prec...]
    unnamed x20 -> x16, local copies, waits for them, and re-layouts: 0.17 us -> 1.16 us
    div x1, other arithmetic: 0.03 us -> 1 us  [local(): 2.0 * velocity / buoyancy]
  transfers between devices with their start and end apart: 18 -> 18, of which waited for: 8 -> 7; matrix products, arithmetic and copies ran while one was open for 14% -> 20% of each run, Pallas kernels for 0% -> 0%
where the time goes in v27:
time: 93.3 us; the launch traced here: 91.7 us
  starting transfers between devices  41.9 us (45%)
  other arithmetic  17.8 us (19%)
  waiting for transfers between devices  12.6 us (14%)
  matrix products  10.5 us (11%)
  between operations  6.18 us (7%)
  local copies, waits for them, and re-layouts  2.65 us (3%)
    ppermute x7, starting transfers between devices, extended(): before = lax.ppermute(last, 'mp', up)  18 us
    ppermute x7, starting transfers between devices, extended(): after = lax.ppermute(first, 'mp', down)  15.1 us
    ppermute x7, waiting for transfers between devices, extended(): after = lax.ppermute(first, 'mp', down)  12.3 us
    ppermute x4, starting transfers between devices, butterfly_round(): return values + lax.ppermute(values, axis, pairs)  8.83 us
    mul x7, other arithmetic, cross_terms(): flux = buoyancy * forward_diff(pad_axis(values, axis), axis, length)  5.37 us
    dot_general x4, matrix products, injected(): jnp.einsum('srk,srz->skz', row_pick, spread, precision=lax.Precision.HIGH...  4.93 us
    dot_general x3, matrix products, sample(): jnp.einsum('srk,skz->srz', row_pick, field.reshape(shots, rows, cz), prec...  4.82 us
    add x4, other arithmetic, local(): following = following + jnp.where(source_hit, amount, 0.0)  3 us
  transfers between devices with their start and end apart: 18, of which 7 were waited for; matrix products, arithmetic and copies ran while one was open for 20% of the time, Pallas kernels for 0%

profile of v27, /device:TPU:1, one launch (start us, length us, event | category | flops | bytes accessed | tf_op | source)
XLA Modules:
  0.0 91.7 jit_solution(6002455569823138232)
XLA Ops:
  0.7 1.1 %pad_maximum_fusion.12 = (f32[2,7,32,128]{3,2,1,0:T(8,128)S(1)}, f32[2,7,32,128]{3,2,1,0:T(8,128)S(1)}) fusion(f32[1,8,32,128]{3,2,1,0:T(8,128)} %param.13, f32[1,8,32,128]{3,2,1,0:T(8,128)} %bitcast.125), kind=kLoop, calls=%fused_computation.337 | loop fusion | flops 114688 | bytes 720896 | tf_op jit(solution)/shard_map/concatenate | solution.py:99
  1.8 2.0 %collective-permute-start.1 = (f32[2,7,32,128]{3,2,1,0:T(8,128)S(1)}, f32[2,7,32,128]{3,2,1,0:T(8,128)S(1)}, u32[]{:S(2)}, u32[]{:S(2)}) collective-permute-start(f32[2,7,32,128]{3,2,1,0:T(8,128)S(1)} %get-tuple-element.63), channel_id=1, source_target_pairs={{1,0},{2,1},{3,2},{4,3},{5,4},{6,5},{7,6},{8,7},{9,8},{10,9},{11,1... | collective-permute-start | bytes 688136 | tf_op jit(solution)/shard_map/ppermute | solution.py:19
  3.8 4.5 %collective-permute-start = (f32[2,7,32,128]{3,2,1,0:T(8,128)S(1)}, f32[2,7,32,128]{3,2,1,0:T(8,128)S(1)}, u32[]{:S(2)}, u32[]{:S(2)}) collective-permute-start(f32[2,7,32,128]{3,2,1,0:T(8,128)S(1)} %get-tuple-element.64), channel_id=1, source_target_pairs={{0,1},{1,2},{2,3},{3,4},{4,5},{5,6},{6,7},{7,8},{8,9},{9,10},{10,1... | collective-permute-start | bytes 688136 | tf_op jit(solution)/shard_map/ppermute | solution.py:18
  9.0 1.4 %fusion.558 = (f32[1,1]{1,0:T(1,128)}, f32[1,1]{1,0:T(1,128)}, f32[1,1]{1,0:T(1,128)}, f32[1,1]{1,0:T(1,128)}) fusion(f32[1,4]{1,0:T(1,128)} %param.17), kind=kLoop, calls=%fused_computation.852 | loop fusion | bytes 32 | tf_op jit(solution)/shard_map/slice | solution.py:166
  10.4 0.7 and_select_fusion
  11.1 0.7 fusion.543
  11.8 3.3 %fusion.338 = (f32[1,8,32,128]{3,2,1,0:T(8,128)S(1)}, f32[1,8,32,128]{3,2,1,0:T(8,128)S(1)}, f32[1,8,32,128]{3,2,1,0:T(8,128)S(1)}) fusion(f32[1,8,32,128]{3,2,1,0:T(8,128)} %param.13, f32[8,32,128]{2,1,0:T(8,128)} %param.11, f32[1,8,32,128]{3,2,1,0:T(8,128)} %param.12), kind=kLoop, calls=%fused_computation.583 | loop fusion | flops 851968 | bytes 786432 | tf_op jit(solution)/shard_map/mul | solution.py:69
  15.1 0.3 fusion.206
  15.4 1.0 %multiply_divide_fusion = f32[8,32,128]{2,1,0:T(8,128)S(1)} fusion(f32[8,32,128]{2,1,0:T(8,128)} %param.11, f32[8,32,128]{2,1,0:T(8,128)} %param.10), kind=kLoop, calls=%fused_computation.817 | loop fusion | flops 65536 | bytes 393216 | tf_op jit(solution)/shard_map/div | solution.py:160
  16.6 0.1 slice_bitcast_fusion
  16.7 0.7 copy-done.4
  17.3 0.8 fusion.531
  18.2 0.5 fusion.104
  18.8 2.4 %collective-permute-start.2 = (f32[2,7,32,128]{3,2,1,0:T(8,128)S(1)}, f32[2,7,32,128]{3,2,1,0:T(8,128)S(1)}, u32[]{:S(2)}, u32[]{:S(2)}) collective-permute-start(f32[2,7,32,128]{3,2,1,0:T(8,128)S(1)} %get-tuple-element.61), channel_id=1, source_target_pairs={{0,1},{1,2},{2,3},{3,4},{4,5},{5,6},{6,7},{7,8},{8,9},{9,10},{10,1... | collective-permute-start | bytes 688136 | tf_op jit(solution)/shard_map/ppermute | solution.py:18
  21.2 1.9 %collective-permute-start.3 = (f32[2,7,32,128]{3,2,1,0:T(8,128)S(1)}, f32[2,7,32,128]{3,2,1,0:T(8,128)S(1)}, u32[]{:S(2)}, u32[]{:S(2)}) collective-permute-start(f32[2,7,32,128]{3,2,1,0:T(8,128)S(1)} %get-tuple-element.62), channel_id=1, source_target_pairs={{1,0},{2,1},{3,2},{4,3},{5,4},{6,5},{7,6},{8,7},{9,8},{10,9},{11,1... | collective-permute-start | bytes 688136 | tf_op jit(solution)/shard_map/ppermute | solution.py:19
  23.1 0.5 fusion.92
  23.7 1.6 %fusion.12 = f32[2048]{0:T(1024)S(1)} fusion(f32[256,128]{1,0:T(8,128)S(1)} %bitcast.129, s32[2048]{0:T(1024)S(1)} %bitcast.139, s32[2048]{0:T(1024)S(1)} %bitcast.131), kind=kOutput, calls=%fused_computation.16 | convolution fusion | flops 806615040 | bytes 155648 | tf_op jit(solution)/shard_map/srk,skz->srz/dot_general | solution.py:130
  25.3 3.5 %collective-permute-done.3 = f32[2,7,32,128]{3,2,1,0:T(8,128)S(1)} collective-permute-done((f32[2,7,32,128]{3,2,1,0:T(8,128)S(1)}, f32[2,7,32,128]{3,2,1,0:T(8,128)S(1)}, u32[]{:S(2)}, u32[]{:S(2)}) %collective-permute-start.3) | collective-permute-done | bytes 229408 | tf_op jit(solution)/shard_map/ppermute | solution.py:19
  28.8 0.2 fusion.70
  29.0 0.1 fusion.124
  29.2 0.7 fusion.533
  29.9 0.3 fusion.361
  30.2 1.9 %collective-permute-start.4 = (f32[1,7,32,128]{3,2,1,0:T(8,128)S(1)}, f32[1,7,32,128]{3,2,1,0:T(8,128)S(1)}, u32[]{:S(2)}, u32[]{:S(2)}) collective-permute-start(f32[1,7,32,128]{3,2,1,0:T(8,128)S(1)} %get-tuple-element.78), channel_id=1, source_target_pairs={{0,1},{1,2},{2,3},{3,4},{4,5},{5,6},{6,7},{7,8},{8,9},{9,10},{10,1... | collective-permute-start | bytes 344072 | tf_op jit(solution)/shard_map/ppermute | solution.py:18
  32.2 2.4 %collective-permute-start.5 = (f32[1,7,32,128]{3,2,1,0:T(8,128)S(1)}, f32[1,7,32,128]{3,2,1,0:T(8,128)S(1)}, u32[]{:S(2)}, u32[]{:S(2)}) collective-permute-start(f32[1,7,32,128]{3,2,1,0:T(8,128)S(1)} %get-tuple-element.79), channel_id=1, source_target_pairs={{1,0},{2,1},{3,2},{4,3},{5,4},{6,5},{7,6},{8,7},{9,8},{10,9},{11,1... | collective-permute-start | bytes 344072 | tf_op jit(solution)/shard_map/ppermute | solution.py:19
  34.6 0.3 fusion.230
  34.9 1.6 %fusion.15 = f32[2048]{0:T(1024)S(1)} fusion(f32[256,128]{1,0:T(8,128)S(1)} %bitcast.128, s32[2048]{0:T(1024)S(1)} %bitcast.140, s32[2048]{0:T(1024)S(1)} %bitcast.132), kind=kOutput, calls=%fused_computation.17 | convolution fusion | flops 806615040 | bytes 155648 | tf_op jit(solution)/shard_map/srk,skz->srz/dot_general | solution.py:130
  36.5 2.7 %collective-permute-done.5 = f32[1,7,32,128]{3,2,1,0:T(8,128)S(1)} collective-permute-done((f32[1,7,32,128]{3,2,1,0:T(8,128)S(1)}, f32[1,7,32,128]{3,2,1,0:T(8,128)S(1)}, u32[]{:S(2)}, u32[]{:S(2)}) %collective-permute-start.5) | collective-permute-done | bytes 114720 | tf_op jit(solution)/shard_map/ppermute | solution.py:19
  39.3 0.7 fusion.535
  40.1 0.3 fusion.384
  40.4 1.9 %collective-permute-start.6 = (f32[1,7,32,128]{3,2,1,0:T(8,128)S(1)}, f32[1,7,32,128]{3,2,1,0:T(8,128)S(1)}, u32[]{:S(2)}, u32[]{:S(2)}) collective-permute-start(f32[1,7,32,128]{3,2,1,0:T(8,128)S(1)} %get-tuple-element.76), channel_id=1, source_target_pairs={{0,1},{1,2},{2,3},{3,4},{4,5},{5,6},{6,7},{7,8},{8,9},{9,10},{10,1... | collective-permute-start | bytes 344072 | tf_op jit(solution)/shard_map/ppermute | solution.py:18
  42.3 2.4 %collective-permute-start.7 = (f32[1,7,32,128]{3,2,1,0:T(8,128)S(1)}, f32[1,7,32,128]{3,2,1,0:T(8,128)S(1)}, u32[]{:S(2)}, u32[]{:S(2)}) collective-permute-start(f32[1,7,32,128]{3,2,1,0:T(8,128)S(1)} %get-tuple-element.77), channel_id=1, source_target_pairs={{1,0},{2,1},{3,2},{4,3},{5,4},{6,5},{7,6},{8,7},{9,8},{10,9},{11,1... | collective-permute-start | bytes 344072 | tf_op jit(solution)/shard_map/ppermute | solution.py:19
  44.8 0.3 fusion.254
  45.1 1.6 %fusion.18 = f32[2048]{0:T(1024)S(1)} fusion(f32[256,128]{1,0:T(8,128)S(1)} %bitcast.130, s32[2048]{0:T(1024)S(1)} %bitcast.141, s32[2048]{0:T(1024)S(1)} %bitcast.133), kind=kOutput, calls=%fused_computation.18 | convolution fusion | flops 806615040 | bytes 155648 | tf_op jit(solution)/shard_map/srk,skz->srz/dot_general | solution.py:130
  46.7 2.7 %collective-permute-done.7 = f32[1,7,32,128]{3,2,1,0:T(8,128)S(1)} collective-permute-done((f32[1,7,32,128]{3,2,1,0:T(8,128)S(1)}, f32[1,7,32,128]{3,2,1,0:T(8,128)S(1)}, u32[]{:S(2)}, u32[]{:S(2)}) %collective-permute-start.7) | collective-permute-done | bytes 114720 | tf_op jit(solution)/shard_map/ppermute | solution.py:19
  49.5 0.7 fusion.537
  50.3 0.7 convolution_bitcast_fusion
  51.1 0.3 fusion.34
  51.4 0.4 copy-done.6
  51.9 1.2 %fusion.21 = f32[1,8,32,128]{3,2,1,0:T(8,128)S(1)} fusion(s32[8,32]{1,0:T(8,128)S(1)} %multiply_add_fusion, s32[2048]{0:T(1024)S(1)} %bitcast.143, f32[2048]{0:T(1024)S(1)} %bitcast.154, s32[2048]{0:T(1024)S(1)} %bitcast.135), kind=kOutput, calls=%fused_computation.19 | convolution fusion | flops 806354944 | bytes 156672 | tf_op jit(solution)/shard_map/srk,srz->skz/dot_general | solution.py:150
  53.1 0.6 fusion.538
  54.5 0.3 fusion.407
  54.8 3.0 %collective-permute-start.10 = (f32[1]{0:T(128)}, f32[1]{0:T(128)}, u32[]{:S(2)}, u32[]{:S(2)}) collective-permute-start(f32[1]{0:T(128)} %bitcast.32), channel_id=1, source_target_pairs={{0,2},{1,3},{2,0},{3,1},{4,6},{5,7},{6,4},{7,5},{8,10},{9,11},{10,... | collective-permute-start | bytes 20 | tf_op jit(solution)/shard_map/ppermute | solution.py:36
  57.9 1.9 %collective-permute-start.8 = (f32[1,7,32,128]{3,2,1,0:T(8,128)S(1)}, f32[1,7,32,128]{3,2,1,0:T(8,128)S(1)}, u32[]{:S(2)}, u32[]{:S(2)}) collective-permute-start(f32[1,7,32,128]{3,2,1,0:T(8,128)S(1)} %get-tuple-element.71), channel_id=1, source_target_pairs={{0,1},{1,2},{2,3},{3,4},{4,5},{5,6},{6,7},{7,8},{8,9},{9,10},{10,1... | collective-permute-start | bytes 344072 | tf_op jit(solution)/shard_map/ppermute | solution.py:18
  59.8 2.6 %collective-permute-start.9 = (f32[1,7,32,128]{3,2,1,0:T(8,128)S(1)}, f32[1,7,32,128]{3,2,1,0:T(8,128)S(1)}, u32[]{:S(2)}, u32[]{:S(2)}) collective-permute-start(f32[1,7,32,128]{3,2,1,0:T(8,128)S(1)} %get-tuple-element.72), channel_id=1, source_target_pairs={{1,0},{2,1},{3,2},{4,3},{5,4},{6,5},{7,6},{8,7},{9,8},{10,9},{11,1... | collective-permute-start | bytes 344072 | tf_op jit(solution)/shard_map/ppermute | solution.py:19
  62.4 0.3 fusion.278
  62.7 1.2 %fusion.24 = f32[1,8,32,128]{3,2,1,0:T(8,128)S(1)} fusion(s32[8,32]{1,0:T(8,128)S(1)} %multiply_add_fusion, s32[2048]{0:T(1024)S(1)} %bitcast.144, f32[2048]{0:T(1024)S(1)} %bitcast.153, s32[2048]{0:T(1024)S(1)} %bitcast.136), kind=kOutput, calls=%fused_computation.20 | convolution fusion | flops 806354944 | bytes 156672 | tf_op jit(solution)/shard_map/srk,srz->skz/dot_general | solution.py:150
  64.6 1.3 %collective-permute-done.9 = f32[1,7,32,128]{3,2,1,0:T(8,128)S(1)} collective-permute-done((f32[1,7,32,128]{3,2,1,0:T(8,128)S(1)}, f32[1,7,32,128]{3,2,1,0:T(8,128)S(1)}, u32[]{:S(2)}, u32[]{:S(2)}) %collective-permute-start.9) | collective-permute-done | bytes 114720 | tf_op jit(solution)/shard_map/ppermute | solution.py:19
  66.2 0.3 fusion.430
  66.5 2.1 %collective-permute-start.13 = (f32[1]{0:T(128)}, f32[1]{0:T(128)}, u32[]{:S(2)}, u32[]{:S(2)}) collective-permute-start(f32[1]{0:T(128)} %add.726), channel_id=1, source_target_pairs={{0,4},{1,5},{2,6},{3,7},{4,0},{5,1},{6,2},{7,3},{8,12},{9,13},{10,... | collective-permute-start | bytes 20 | tf_op jit(solution)/shard_map/ppermute | solution.py:36
  68.6 2.7 %collective-permute-start.11 = (f32[1,7,32,128]{3,2,1,0:T(8,128)S(1)}, f32[1,7,32,128]{3,2,1,0:T(8,128)S(1)}, u32[]{:S(2)}, u32[]{:S(2)}) collective-permute-start(f32[1,7,32,128]{3,2,1,0:T(8,128)S(1)} %get-tuple-element.69), channel_id=1, source_target_pairs={{0,1},{1,2},{2,3},{3,4},{4,5},{5,6},{6,7},{7,8},{8,9},{9,10},{10,1... | collective-permute-start | bytes 344072 | tf_op jit(solution)/shard_map/ppermute | solution.py:18
  71.2 1.9 %collective-permute-start.12 = (f32[1,7,32,128]{3,2,1,0:T(8,128)S(1)}, f32[1,7,32,128]{3,2,1,0:T(8,128)S(1)}, u32[]{:S(2)}, u32[]{:S(2)}) collective-permute-start(f32[1,7,32,128]{3,2,1,0:T(8,128)S(1)} %get-tuple-element.70), channel_id=1, source_target_pairs={{1,0},{2,1},{3,2},{4,3},{5,4},{6,5},{7,6},{8,7},{9,8},{10,9},{11,1... | collective-permute-start | bytes 344072 | tf_op jit(solution)/shard_map/ppermute | solution.py:19
  73.2 0.3 fusion.302
  73.5 1.2 %fusion.27 = f32[1,8,32,128]{3,2,1,0:T(8,128)S(1)} fusion(s32[8,32]{1,0:T(8,128)S(1)} %multiply_add_fusion, s32[2048]{0:T(1024)S(1)} %bitcast.145, f32[2048]{0:T(1024)S(1)} %bitcast.151, s32[2048]{0:T(1024)S(1)} %bitcast.137), kind=kOutput, calls=%fused_computation.21 | convolution fusion | flops 806354944 | bytes 156672 | tf_op jit(solution)/shard_map/srk,srz->skz/dot_general | solution.py:150
  75.4 2.0 %collective-permute-done.12 = f32[1,7,32,128]{3,2,1,0:T(8,128)S(1)} collective-permute-done((f32[1,7,32,128]{3,2,1,0:T(8,128)S(1)}, f32[1,7,32,128]{3,2,1,0:T(8,128)S(1)}, u32[]{:S(2)}, u32[]{:S(2)}) %collective-permute-start.12) | collective-permute-done | bytes 114720 | tf_op jit(solution)/shard_map/ppermute | solution.py:19
  77.7 0.3 fusion.453
  78.0 2.8 %collective-permute-start.16 = (f32[1]{0:T(128)}, f32[1]{0:T(128)}, u32[]{:S(2)}, u32[]{:S(2)}) collective-permute-start(f32[1]{0:T(128)} %add.750), channel_id=1, source_target_pairs={{0,8},{1,9},{2,10},{3,11},{4,12},{5,13},{6,14},{7,15},{8,0},{9,1},... | collective-permute-start | bytes 20 | tf_op jit(solution)/shard_map/ppermute | solution.py:36
  80.8 2.6 %collective-permute-start.14 = (f32[1,7,32,128]{3,2,1,0:T(8,128)S(1)}, f32[1,7,32,128]{3,2,1,0:T(8,128)S(1)}, u32[]{:S(2)}, u32[]{:S(2)}) collective-permute-start(f32[1,7,32,128]{3,2,1,0:T(8,128)S(1)} %get-tuple-element.67), channel_id=1, source_target_pairs={{0,1},{1,2},{2,3},{3,4},{4,5},{5,6},{6,7},{7,8},{8,9},{9,10},{10,1... | collective-permute-start | bytes 344072 | tf_op jit(solution)/shard_map/ppermute | solution.py:18
  83.4 1.9 %collective-permute-start.15 = (f32[1,7,32,128]{3,2,1,0:T(8,128)S(1)}, f32[1,7,32,128]{3,2,1,0:T(8,128)S(1)}, u32[]{:S(2)}, u32[]{:S(2)}) collective-permute-start(f32[1,7,32,128]{3,2,1,0:T(8,128)S(1)} %get-tuple-element.68), channel_id=1, source_target_pairs={{1,0},{2,1},{3,2},{4,3},{5,4},{6,5},{7,6},{8,7},{9,8},{10,9},{11,1... | collective-permute-start | bytes 344072 | tf_op jit(solution)/shard_map/ppermute | solution.py:19
  85.4 0.3 fusion.326
  85.7 1.2 %fusion.30 = f32[1,8,32,128]{3,2,1,0:T(8,128)S(1)} fusion(s32[8,32]{1,0:T(8,128)S(1)} %multiply_add_fusion, s32[2048]{0:T(1024)S(1)} %bitcast.146, f32[2048]{0:T(1024)S(1)} %bitcast.149, s32[2048]{0:T(1024)S(1)} %bitcast.138), kind=kOutput, calls=%fused_computation.22 | convolution fusion | flops 806354944 | bytes 156672 | tf_op jit(solution)/shard_map/srk,srz->skz/dot_general | solution.py:150
  87.5 0.9 collective-permute-start.17
  88.4 0.3 collective-permute-done.17
  89.3 0.2 collective-permute-done.15
  89.7 0.9 bitcast_multiply_fusion
  (56 shorter events, 1.4 us)
Async XLA Ops:
  0.6 15.8 %copy-start.1 = (f32[1,8,32,128]{3,2,1,0:T(8,128)S(1)}, f32[1,8,32,128]{3,2,1,0:T(8,128)}, u32[]{:S(2)}) copy-start(f32[1,8,32,128]{3,2,1,0:T(8,128)} %param.13) | copy-start | bytes 393220
  0.6 15.8 %copy-start = (f32[8,32,128]{2,1,0:T(8,128)S(1)}, f32[8,32,128]{2,1,0:T(8,128)}, u32[]{:S(2)}) copy-start(f32[8,32,128]{2,1,0:T(8,128)} %param.11) | copy-start | bytes 393220
  1.8 14.6 %collective-permute-start.1 = (f32[2,7,32,128]{3,2,1,0:T(8,128)S(1)}, f32[2,7,32,128]{3,2,1,0:T(8,128)S(1)}, u32[]{:S(2)}, u32[]{:S(2)}) collective-permute-start(f32[2,7,32,128]{3,2,1,0:T(8,128)S(1)} %get-tuple-element.63), channel_id=1, source_target_pairs={{1,0},{2,1},{3,2},{4,3},{5,4},{6,5},{7,6},{8,7},{9,8},{10,9},{11,1... | collective-permute-start | bytes 688136 | tf_op jit(solution)/shard_map/ppermute | solution.py:19
  3.8 12.7 %collective-permute-start = (f32[2,7,32,128]{3,2,1,0:T(8,128)S(1)}, f32[2,7,32,128]{3,2,1,0:T(8,128)S(1)}, u32[]{:S(2)}, u32[]{:S(2)}) collective-permute-start(f32[2,7,32,128]{3,2,1,0:T(8,128)S(1)} %get-tuple-element.64), channel_id=1, source_target_pairs={{0,1},{1,2},{2,3},{3,4},{4,5},{5,6},{6,7},{7,8},{8,9},{9,10},{10,1... | collective-permute-start | bytes 688136 | tf_op jit(solution)/shard_map/ppermute | solution.py:18
  16.4 0.9 copy-start.4
  16.5 1.6 %copy-start.2 = (f32[1,8,32,128]{3,2,1,0:T(8,128)S(1)}, f32[1,8,32,128]{3,2,1,0:T(8,128)}, u32[]{:S(2)}) copy-start(f32[1,8,32,128]{3,2,1,0:T(8,128)} %param.14) | copy-start | bytes 393220
  18.8 6.5 %collective-permute-start.2 = (f32[2,7,32,128]{3,2,1,0:T(8,128)S(1)}, f32[2,7,32,128]{3,2,1,0:T(8,128)S(1)}, u32[]{:S(2)}, u32[]{:S(2)}) collective-permute-start(f32[2,7,32,128]{3,2,1,0:T(8,128)S(1)} %get-tuple-element.61), channel_id=1, source_target_pairs={{0,1},{1,2},{2,3},{3,4},{4,5},{5,6},{6,7},{7,8},{8,9},{9,10},{10,1... | collective-permute-start | bytes 688136 | tf_op jit(solution)/shard_map/ppermute | solution.py:18
  21.2 7.6 %collective-permute-start.3 = (f32[2,7,32,128]{3,2,1,0:T(8,128)S(1)}, f32[2,7,32,128]{3,2,1,0:T(8,128)S(1)}, u32[]{:S(2)}, u32[]{:S(2)}) collective-permute-start(f32[2,7,32,128]{3,2,1,0:T(8,128)S(1)} %get-tuple-element.62), channel_id=1, source_target_pairs={{1,0},{2,1},{3,2},{4,3},{5,4},{6,5},{7,6},{8,7},{9,8},{10,9},{11,1... | collective-permute-start | bytes 688136 | tf_op jit(solution)/shard_map/ppermute | solution.py:19
  30.2 6.3 %collective-permute-start.4 = (f32[1,7,32,128]{3,2,1,0:T(8,128)S(1)}, f32[1,7,32,128]{3,2,1,0:T(8,128)S(1)}, u32[]{:S(2)}, u32[]{:S(2)}) collective-permute-start(f32[1,7,32,128]{3,2,1,0:T(8,128)S(1)} %get-tuple-element.78), channel_id=1, source_target_pairs={{0,1},{1,2},{2,3},{3,4},{4,5},{5,6},{6,7},{7,8},{8,9},{9,10},{10,1... | collective-permute-start | bytes 344072 | tf_op jit(solution)/shard_map/ppermute | solution.py:18
  32.2 7.0 %collective-permute-start.5 = (f32[1,7,32,128]{3,2,1,0:T(8,128)S(1)}, f32[1,7,32,128]{3,2,1,0:T(8,128)S(1)}, u32[]{:S(2)}, u32[]{:S(2)}) collective-permute-start(f32[1,7,32,128]{3,2,1,0:T(8,128)S(1)} %get-tuple-element.79), channel_id=1, source_target_pairs={{1,0},{2,1},{3,2},{4,3},{5,4},{6,5},{7,6},{8,7},{9,8},{10,9},{11,1... | collective-permute-start | bytes 344072 | tf_op jit(solution)/shard_map/ppermute | solution.py:19
  40.4 6.3 %collective-permute-start.6 = (f32[1,7,32,128]{3,2,1,0:T(8,128)S(1)}, f32[1,7,32,128]{3,2,1,0:T(8,128)S(1)}, u32[]{:S(2)}, u32[]{:S(2)}) collective-permute-start(f32[1,7,32,128]{3,2,1,0:T(8,128)S(1)} %get-tuple-element.76), channel_id=1, source_target_pairs={{0,1},{1,2},{2,3},{3,4},{4,5},{5,6},{6,7},{7,8},{8,9},{9,10},{10,1... | collective-permute-start | bytes 344072 | tf_op jit(solution)/shard_map/ppermute | solution.py:18
  42.3 7.0 %collective-permute-start.7 = (f32[1,7,32,128]{3,2,1,0:T(8,128)S(1)}, f32[1,7,32,128]{3,2,1,0:T(8,128)S(1)}, u32[]{:S(2)}, u32[]{:S(2)}) collective-permute-start(f32[1,7,32,128]{3,2,1,0:T(8,128)S(1)} %get-tuple-element.77), channel_id=1, source_target_pairs={{1,0},{2,1},{3,2},{4,3},{5,4},{6,5},{7,6},{8,7},{9,8},{10,9},{11,1... | collective-permute-start | bytes 344072 | tf_op jit(solution)/shard_map/ppermute | solution.py:19
  51.0 0.7 copy-start.6
  51.1 0.8 copy-start.7
  51.1 3.3 %copy-start.5 = (f32[1,8,32,128]{3,2,1,0:T(8,128)S(1)}, f32[1,8,32,128]{3,2,1,0:T(8,128)}, u32[]{:S(2)}) copy-start(f32[1,8,32,128]{3,2,1,0:T(8,128)} %param.15) | copy-start | bytes 393220
  54.8 9.1 %collective-permute-start.10 = (f32[1]{0:T(128)}, f32[1]{0:T(128)}, u32[]{:S(2)}, u32[]{:S(2)}) collective-permute-start(f32[1]{0:T(128)} %bitcast.32), channel_id=1, source_target_pairs={{0,2},{1,3},{2,0},{3,1},{4,6},{5,7},{6,4},{7,5},{8,10},{9,11},{10,... | collective-permute-start | bytes 20 | tf_op jit(solution)/shard_map/ppermute | solution.py:36
  57.9 6.7 %collective-permute-start.8 = (f32[1,7,32,128]{3,2,1,0:T(8,128)S(1)}, f32[1,7,32,128]{3,2,1,0:T(8,128)S(1)}, u32[]{:S(2)}, u32[]{:S(2)}) collective-permute-start(f32[1,7,32,128]{3,2,1,0:T(8,128)S(1)} %get-tuple-element.71), channel_id=1, source_target_pairs={{0,1},{1,2},{2,3},{3,4},{4,5},{5,6},{6,7},{7,8},{8,9},{9,10},{10,1... | collective-permute-start | bytes 344072 | tf_op jit(solution)/shard_map/ppermute | solution.py:18
  59.8 6.1 %collective-permute-start.9 = (f32[1,7,32,128]{3,2,1,0:T(8,128)S(1)}, f32[1,7,32,128]{3,2,1,0:T(8,128)S(1)}, u32[]{:S(2)}, u32[]{:S(2)}) collective-permute-start(f32[1,7,32,128]{3,2,1,0:T(8,128)S(1)} %get-tuple-element.72), channel_id=1, source_target_pairs={{1,0},{2,1},{3,2},{4,3},{5,4},{6,5},{7,6},{8,7},{9,8},{10,9},{11,1... | collective-permute-start | bytes 344072 | tf_op jit(solution)/shard_map/ppermute | solution.py:19
  66.5 8.2 %collective-permute-start.13 = (f32[1]{0:T(128)}, f32[1]{0:T(128)}, u32[]{:S(2)}, u32[]{:S(2)}) collective-permute-start(f32[1]{0:T(128)} %add.726), channel_id=1, source_target_pairs={{0,4},{1,5},{2,6},{3,7},{4,0},{5,1},{6,2},{7,3},{8,12},{9,13},{10,... | collective-permute-start | bytes 20 | tf_op jit(solution)/shard_map/ppermute | solution.py:36
  68.6 6.8 %collective-permute-start.11 = (f32[1,7,32,128]{3,2,1,0:T(8,128)S(1)}, f32[1,7,32,128]{3,2,1,0:T(8,128)S(1)}, u32[]{:S(2)}, u32[]{:S(2)}) collective-permute-start(f32[1,7,32,128]{3,2,1,0:T(8,128)S(1)} %get-tuple-element.69), channel_id=1, source_target_pairs={{0,1},{1,2},{2,3},{3,4},{4,5},{5,6},{6,7},{7,8},{8,9},{9,10},{10,1... | collective-permute-start | bytes 344072 | tf_op jit(solution)/shard_map/ppermute | solution.py:18
  71.2 6.1 %collective-permute-start.12 = (f32[1,7,32,128]{3,2,1,0:T(8,128)S(1)}, f32[1,7,32,128]{3,2,1,0:T(8,128)S(1)}, u32[]{:S(2)}, u32[]{:S(2)}) collective-permute-start(f32[1,7,32,128]{3,2,1,0:T(8,128)S(1)} %get-tuple-element.70), channel_id=1, source_target_pairs={{1,0},{2,1},{3,2},{4,3},{5,4},{6,5},{7,6},{8,7},{9,8},{10,9},{11,1... | collective-permute-start | bytes 344072 | tf_op jit(solution)/shard_map/ppermute | solution.py:19
  77.6 12.1 %copy-start.3 = (f32[1,8,32,128]{3,2,1,0:T(8,128)}, f32[1,8,32,128]{3,2,1,0:T(8,128)S(1)}, u32[]{:S(2)}) copy-start(f32[1,8,32,128]{3,2,1,0:T(8,128)S(1)} %fusion.487) | copy-start | bytes 393220
  78.0 9.0 %collective-permute-start.16 = (f32[1]{0:T(128)}, f32[1]{0:T(128)}, u32[]{:S(2)}, u32[]{:S(2)}) collective-permute-start(f32[1]{0:T(128)} %add.750), channel_id=1, source_target_pairs={{0,8},{1,9},{2,10},{3,11},{4,12},{5,13},{6,14},{7,15},{8,0},{9,1},... | collective-permute-start | bytes 20 | tf_op jit(solution)/shard_map/ppermute | solution.py:36
  80.8 8.5 %collective-permute-start.14 = (f32[1,7,32,128]{3,2,1,0:T(8,128)S(1)}, f32[1,7,32,128]{3,2,1,0:T(8,128)S(1)}, u32[]{:S(2)}, u32[]{:S(2)}) collective-permute-start(f32[1,7,32,128]{3,2,1,0:T(8,128)S(1)} %get-tuple-element.67), channel_id=1, source_target_pairs={{0,1},{1,2},{2,3},{3,4},{4,5},{5,6},{6,7},{7,8},{8,9},{9,10},{10,1... | collective-permute-start | bytes 344072 | tf_op jit(solution)/shard_map/ppermute | solution.py:18
  83.4 6.1 %collective-permute-start.15 = (f32[1,7,32,128]{3,2,1,0:T(8,128)S(1)}, f32[1,7,32,128]{3,2,1,0:T(8,128)S(1)}, u32[]{:S(2)}, u32[]{:S(2)}) collective-permute-start(f32[1,7,32,128]{3,2,1,0:T(8,128)S(1)} %get-tuple-element.68), channel_id=1, source_target_pairs={{1,0},{2,1},{3,2},{4,3},{5,4},{6,5},{7,6},{8,7},{9,8},{10,9},{11,1... | collective-permute-start | bytes 344072 | tf_op jit(solution)/shard_map/ppermute | solution.py:19
  87.5 1.2 %collective-permute-start.17 = (f32[1]{0:T(128)}, f32[1]{0:T(128)}, u32[]{:S(2)}, u32[]{:S(2)}) collective-permute-start(f32[1]{0:T(128)} %add.774), channel_id=1, source_target_pairs={{0,1},{1,0},{2,3},{3,2},{4,5},{5,4},{6,7},{7,6},{8,9},{9,8},{10,11... | collective-permute-start | bytes 20 | tf_op jit(solution)/shard_map/ppermute | solution.py:36
